TPU v7x, 32 devices: a whole 2x2x4 slice. The times are simulated.
32 devices in a mesh: seq: 16 (over z, y, core), tp: 2 (over x).
Axes of the slice: x: 2, y: 2, z: 4, core: 2. Of those that a mesh axis runs over, the one named last changes fastest.
Arguments:
- hidden: bfloat16 [1920, 5120], P(('seq', 'tp')), may hold values from -6 to 6
- queries: bfloat16 [1920, 2560], P('seq', 'tp'), may hold values from -10 to 10
- key_rows: bfloat16 [1920, 2560], P('seq', 'tp'), may hold values from -10 to 10
- value_rows: bfloat16 [1920, 2560], P('seq', 'tp'), may hold values from -6 to 6
- gate_scale: float32 [5120], replicated, may hold values from 0.5 to 2
- out_weight: bfloat16 [2560, 5120], P('tp'), may hold values from -0.125 to 0.125
- valid_count: int32 [16], P('seq'), may hold values from 1 to 120, 1200 in all
- assignment: int32 [16], P('seq'), may hold values from 0 to 15, each once
Outputs:
- mixed: bfloat16 [1920, 5120], P(('seq', 'tp'))
All inputs are finite; a program needn't handle non-finite values. No bound on the sum of `valid_count` on one device may be relied on, other than what follows from the above.
Results may differ from a plain program's by a relative error of at most 0.0075.
Values may be sent and summed in bfloat16 or wider, within the bound.
No kernel may reach another device: no remote copies, remote signals or barrier semaphores. Data moves between devices by JAX's collectives and lax.ppermute only.
A program may use at most 192 MiB of HBM per device.

v0:
```python
import math

import jax
import jax.numpy as jnp
from jax import lax
from jax.sharding import PartitionSpec as P

HEAD = 128


key_span = 1024
neg_large = -1e30


def lookup(table, wanted):
    columns = jnp.arange(table.shape[0], dtype=jnp.int32)
    matches = wanted[:, None] == columns[None, :]
    return jnp.sum(jnp.where(matches, table[None, :], 0), axis=1)


def attend(state, queries_3d, key_block, value_block, keeping, scale_factor):
    maxima, totals, sums = state
    key_count = key_block.shape[0]
    heads_used = queries_3d.shape[1]
    keys_3d = key_block.reshape(key_count, heads_used, -1)
    values_3d = value_block.reshape(key_count, heads_used, -1)
    scores = (
        jnp.einsum("qhd,khd->hqk", queries_3d, keys_3d, preferred_element_type=jnp.float32)
        * scale_factor
    )
    masked = jnp.where(keeping[None, None, :], scores, neg_large)
    new_max = jnp.maximum(maxima, jnp.max(masked, axis=2))
    weights = jnp.where(keeping[None, None, :], jnp.exp(masked - new_max[:, :, None]), 0.0)
    factor = jnp.exp(maxima - new_max)
    new_totals = totals * factor + jnp.sum(weights, axis=2)
    product = jnp.einsum(
        "hqk,khd->hqd", weights.astype(jnp.bfloat16), values_3d, preferred_element_type=jnp.float32
    )
    new_sums = sums * factor[:, :, None] + product
    return (new_max, new_totals, new_sums)


def build_fold(queries_3d, dev_counts, rows_dev, scale_factor):

    def keyed(state, key_block, value_block, first_index):
        indices = first_index + jnp.arange(key_block.shape[0], dtype=jnp.int32)
        keeping = indices % rows_dev < lookup(dev_counts, indices // rows_dev)
        return attend(state, queries_3d, key_block, value_block, keeping, scale_factor)

    def folding(state, piece, start):
        key_piece, value_piece = piece
        piece_rows = key_piece.shape[0]
        start_row = jnp.asarray(start, jnp.int32)
        blocks_full = piece_rows // key_span
        covered = blocks_full * key_span
        key_stack = key_piece[:covered].reshape(blocks_full, key_span, key_piece.shape[1])
        value_stack = value_piece[:covered].reshape(blocks_full, key_span, value_piece.shape[1])
        offsets = key_span * jnp.arange(blocks_full, dtype=jnp.int32)

        def stepper(carried, operands):
            return (keyed(carried, operands[0], operands[1], operands[2]), None)

        state, ignored = lax.scan(stepper, state, (key_stack, value_stack, offsets))
        state = keyed(state, key_piece[covered:], value_piece[covered:], start_row + covered)
        return state

    return folding


def start_state(heads_used, rows_dev):
    maxima = jnp.full((heads_used, rows_dev), neg_large, jnp.float32)
    totals = jnp.zeros((heads_used, rows_dev), jnp.float32)
    sums = jnp.zeros((heads_used, rows_dev, HEAD), jnp.float32)
    return (maxima, totals, sums)


def finish(state, heads_used, rows_dev):
    maxima, totals, sums = state
    result = (sums / totals[:, :, None]).astype(jnp.bfloat16)
    return result.transpose(1, 0, 2).reshape(rows_dev, heads_used * HEAD)


def make_projection(attention, weight_part):
    return jnp.dot(attention, weight_part, preferred_element_type=jnp.float32)


def on_device(
    hidden, queries, key_rows, value_rows, gate_scale, out_weight, valid_count, assignment
):
    rows_dev = queries.shape[0]
    heads_here = queries.shape[1] // HEAD
    scale_factor = 1.0 / math.sqrt(HEAD)
    counts_all, blocks_all = (
        lax.all_gather(valid_count, "seq", axis=0, tiled=True),
        lax.all_gather(assignment, "seq", axis=0, tiled=True),
    )
    dev_counts = lookup(counts_all, blocks_all)
    queries_3d = queries.reshape(rows_dev, heads_here, HEAD)
    folding = build_fold(queries_3d, dev_counts, rows_dev, scale_factor)
    state = folding(
        start_state(heads_here, rows_dev),
        (
            lax.all_gather(key_rows, "seq", axis=0, tiled=True),
            lax.all_gather(value_rows, "seq", axis=0, tiled=True),
        ),
        jnp.int32(0),
    )
    attention = finish(state, heads_here, rows_dev)
    summed = lax.psum_scatter(
        make_projection(attention, out_weight).astype(jnp.bfloat16),
        "tp",
        scatter_dimension=0,
        tiled=True,
    ).astype(jnp.float32)
    return (hidden.astype(jnp.float32) + gate_scale * summed).astype(jnp.bfloat16)


def solution(mesh):
    placed = (
        P(("seq", "tp"), None),
        P("seq", "tp"),
        P("seq", "tp"),
        P("seq", "tp"),
        P(),
        P("tp", None),
        P("seq"),
        P("seq"),
    )
    return jax.shard_map(
        on_device, mesh=mesh, in_specs=placed, out_specs=P(("seq", "tp"), None), check_vma=False
    )
```

profile of v0, /device:TPU:0, one launch (start us, length us, event | category | flops | bytes accessed | tf_op | source)
XLA Modules:
  0.0 186.3 jit_solution(9780263855048498722)
XLA Ops:
  6.5 0.0 all-gather.5.cloned.1.call-start
  6.5 0.7 all-gather.5.cloned.1.call-update
  7.3 0.0 all-gather.3.cloned.1.call-start
  7.3 0.7 all-gather.3.cloned.1.call-update
  9.3 1.2 dynamic-slice.2
  10.5 0.8 dynamic-update-slice.1
  11.3 0.8 dynamic-update-slice
  12.1 13.8 %all-reduce.4 = (s32[16]{0:T(128)S(1)}, s32[16]{0:T(128)S(1)}) all-reduce(s32[16]{0:T(128)S(1)} %dynamic-update-slice.1, s32[16]{0:T(128)S(1)} %dynamic-update-slice), channel_id=1, replica_groups=mesh['seq'=16,'tp'=2] {'seq'}, use_global_device_ids=true, to_apply=%add.1 | all-reduce | flops 32 | bytes 256
  25.8 1.2 copy.33
  27.1 0.2 select_reduce_fusion.2
  27.3 0.1 select_reduce_fusion.1
  27.3 0.1 select_reduce_fusion
  27.5 39.1 %all-gather.5.cloned.1.call-done = bf16[1920,1280]{1,0:T(8,128)(2,1)} async-done(((bf16[120,1280]{1,0:T(8,128)(2,1)}), bf16[1920,1280]{1,0:T(8,128)(2,1)}) %all-gather.5.cloned.1.call-update) | async-done | bytes 4915216 | tf_op jit(solution)/shard_map/all_gather | solution.py:104
  66.5 0.0 slice-start
  66.5 1.7 slice-done
  68.3 2.7 %copy.52 = bf16[1024,1280]{0,1:T(8,128)(2,1)} copy(bf16[1024,1280]{1,0:T(8,128)(2,1)S(1)} %slice-done) | data formatting | bytes 5242880
  70.9 0.0 slice-start.1
  71.0 1.6 slice-done.1
  72.6 3.3 %copy.54 = bf16[896,1280]{0,1:T(8,128)(2,1)} copy(bf16[896,1280]{1,0:T(8,128)(2,1)S(1)} %slice-done.1) | data formatting | bytes 4587520
  75.9 45.8 %all-gather.3.cloned.1.call-done = bf16[1920,1280]{1,0:T(8,128)(2,1)} async-done(((bf16[120,1280]{1,0:T(8,128)(2,1)}), bf16[1920,1280]{1,0:T(8,128)(2,1)}) %all-gather.3.cloned.1.call-update) | async-done | bytes 4915216 | tf_op jit(solution)/shard_map/all_gather | solution.py:103
  121.8 3.4 %slice.16 = bf16[1024,1280]{1,0:T(8,128)(2,1)} slice(bf16[1920,1280]{1,0:T(8,128)(2,1)} %all-gather.3.cloned.1.call-done), slice={[0:1024], [0:1280]} | slice | bytes 5242880 | tf_op jit(solution)/shard_map/slice | solution.py:56
  125.2 3.0 %copy.51 = bf16[1024,1280]{0,1:T(8,128)(2,1)S(1)} copy(bf16[1024,1280]{1,0:T(8,128)(2,1)} %slice.16) | data formatting | bytes 5242880
  128.2 3.2 %slice.18 = bf16[896,1280]{1,0:T(8,128)(2,1)} slice(bf16[1920,1280]{1,0:T(8,128)(2,1)} %all-gather.3.cloned.1.call-done), slice={[1024:1920], [0:1280]} | slice | bytes 4587520 | tf_op jit(solution)/shard_map/slice | solution.py:64
  131.4 4.4 %copy.53 = bf16[896,1280]{0,1:T(8,128)(2,1)} copy(bf16[896,1280]{1,0:T(8,128)(2,1)} %slice.18) | data formatting | bytes 4587520
  135.8 2.6 %fusion.2 = (f32[10,120]{1,0:T(8,128)S(1)}, f32[10,120,896]{2,1,0:T(8,128)S(1)}) fusion(pred[896]{0:T(1024)(128)(4,1)S(1)} %fusion.48, bf16[120,10,128]{0,2,1:T(8,128)(2,1)S(1)} %bitcast.55, bf16[896,10,128]{0,2,1:T(8,128)(2,1)} %bitcast.54), kind=kOutput, calls=%fused_computation.6 | convolution fusion | flops 278475584 | bytes 6907456 | tf_op jit(solution)/shard_map/qhd,khd->hqk/dot_general | solution.py:28
  138.4 1.1 fusion.1
  139.6 0.0 copy-start
  139.6 1.3 fusion.5
  140.8 1.4 fusion.3
  142.3 0.0 copy-done
  142.3 0.0 copy-start.1
  142.3 1.9 %fusion.30 = f32[120,10,128]{2,0,1:T(8,128)S(1)} fusion(bf16[1024,10,128]{0,2,1:T(8,128)(2,1)S(1)} %bitcast.57, f32[10,120,1024]{2,1,0:T(8,128)S(1)} %get-tuple-element.39, f32[10,120]{1,0:T(8,128)S(1)} %get-tuple-element.34, pred[1024]{0:T(1024)(128)(4,1)S(1)} %fusion.46, f32[120,10]{0,1:T(8,128)S(1)} %get-tuple-element.22, ...), kind=kOutput, calls=%fused_computation.27 | convolution fusion | flops 321024000 | bytes 8166464 | tf_op jit(solution)/shard_map/while/body/eval_jaxpr/hqk,khd->hqd/dot_general | solution.py:36
  144.2 0.0 copy-done.1
  144.2 1.8 fusion.39
  146.0 0.2 copy.44
  146.3 0.0 copy-start.4
  146.3 0.0 copy-start.2
  146.3 0.0 copy-start.3
  146.3 6.7 %convolution_convert_fusion = bf16[120,5120]{1,0:T(8,128)(2,1)S(1)} fusion(bf16[120,1280]{0,1:T(8,128)(2,1)S(1)} %bitcast.59, bf16[1280,5120]{1,0:T(8,128)(2,1)} %param.13), kind=kOutput, calls=%fused_computation | convolution fusion | flops 1573478400 | bytes 14643200 | tf_op jit(solution)/shard_map/dot_general | solution.py:84
  153.0 20.0 %fusion = bf16[64,5120]{1,0:T(8,128)(2,1)S(1)} fusion(bf16[120,5120]{1,0:T(8,128)(2,1)S(1)} %convolution_convert_fusion), kind=kCustom, calls=%all-reduce-scatter | all-reduce-scatter fusion | flops 655361 | bytes 1884672
  173.1 2.5 %collective-permute-start = (bf16[4,5120]{1,0:T(4,128)(2,1)S(1)}, bf16[4,5120]{1,0:T(4,128)(2,1)S(1)}, u32[]{:S(2)}, u32[]{:S(2)}) collective-permute-start(bf16[4,5120]{1,0:T(4,128)(2,1)S(1)} %slice.20), channel_id=1, source_target_pairs={{0,1},{2,3},{4,5},{6,7},{8,9},{10,11},{12,13},{14,15},{16,17},{18,... | collective-permute-start | bytes 122888
  175.6 0.0 copy-done.4
  175.6 0.6 dynamic-slice.8
  176.8 0.4 collective-permute-done
  177.2 1.1 concatenate
  178.3 0.0 copy-done.2
  178.4 0.0 copy-done.3
  178.4 1.1 add_convert_fusion
  (9 shorter events, 0.1 us)
Async XLA Ops:
  6.5 60.0 %all-gather.5.cloned.1.call-start = ((), (), s32[]{:S(2)}) async-start(), calls=%async_computation.1 | async-start | bytes 5222400 | tf_op jit(solution)/shard_map/all_gather | solution.py:104
  7.3 114.5 %all-gather.3.cloned.1.call-start = ((), (), s32[]{:S(2)}) async-start(), calls=%async_computation | async-start | bytes 5222400 | tf_op jit(solution)/shard_map/all_gather | solution.py:103
  66.5 1.7 slice-start
  70.9 1.6 slice-start.1
  139.6 2.7 %copy-start = (bf16[1024,1280]{0,1:T(8,128)(2,1)S(1)}, bf16[1024,1280]{0,1:T(8,128)(2,1)}, u32[]{:S(2)}) copy-start(bf16[1024,1280]{0,1:T(8,128)(2,1)} %copy.52) | copy-start | bytes 7864324
  142.3 1.9 %copy-start.1 = (bf16[896,1280]{0,1:T(8,128)(2,1)S(1)}, bf16[896,1280]{0,1:T(8,128)(2,1)}, u32[]{:S(2)}) copy-start(bf16[896,1280]{0,1:T(8,128)(2,1)} %copy.54) | copy-start | bytes 6881284
  146.3 29.3 %copy-start.4 = (u32[32]{0:T(128)S(1)}, u32[32]{0:T(128)}, u32[]{:S(2)}) copy-start(u32[32]{0:T(128)} %constant.86) | copy-start | bytes 388
  146.3 32.1 %copy-start.2 = (bf16[60,5120]{1,0:T(8,128)(2,1)S(1)}, bf16[60,5120]{1,0:T(8,128)(2,1)}, u32[]{:S(2)}) copy-start(bf16[60,5120]{1,0:T(8,128)(2,1)} %param.8) | copy-start | bytes 1843204
  146.3 32.1 %copy-start.3 = (f32[5120]{0:T(1024)S(1)}, f32[5120]{0:T(1024)}, u32[]{:S(2)}) copy-start(f32[5120]{0:T(1024)} %param.12) | copy-start | bytes 61444
  173.1 4.1 %collective-permute-start = (bf16[4,5120]{1,0:T(4,128)(2,1)S(1)}, bf16[4,5120]{1,0:T(4,128)(2,1)S(1)}, u32[]{:S(2)}, u32[]{:S(2)}) collective-permute-start(bf16[4,5120]{1,0:T(4,128)(2,1)S(1)} %slice.20), channel_id=1, source_target_pairs={{0,1},{2,3},{4,5},{6,7},{8,9},{10,11},{12,13},{14,15},{16,17},{18,... | collective-permute-start | bytes 122888
Sparse Core Ops, SparseCore 0:
  9.5 56.9 all-gather.4
  68.7 53.0 all-gather.2
where the time goes:
time: 187 us; the launch traced here: 186 us
  waiting for transfers between devices  86.7 us (46%)
  blocking collectives  33.8 us (18%)
  local copies, waits for them, and re-layouts  29.4 us (16%)
  between operations  15.6 us (8%)
  matrix products  14.1 us (8%)
  other arithmetic  4.22 us (2%)
  starting transfers between devices  2.51 us (1%)
    all_gather x1, waiting for transfers between devices, on_device(): lax.all_gather(key_rows, 'seq', axis=0, tiled=True)  45.8 us
    all_gather x1, waiting for transfers between devices, on_device(): lax.all_gather(value_rows, 'seq', axis=0, tiled=True)  39.1 us
    unnamed x2, blocking collectives  33.8 us
    unnamed x23, local copies, waits for them, and re-layouts  19.1 us
    dot_general x1, matrix products, make_projection(): return jnp.dot(attention, weight_part, preferred_element_type=jnp.float32)  6.7 us
  transfers between devices with their start and end apart: 3, of which 3 were waited for; matrix products, arithmetic and copies ran while one was open for 6% of the time, Pallas kernels for 0%

commit v1 on v0

v1 whole, which is shorter than its diff:
```python
import math

import jax
import jax.numpy as jnp
from jax import lax
from jax.sharding import PartitionSpec as P

HEAD = 128
neg_large = -1e30


def snake_ring(chips):
    half = chips // 2
    return [2 * a for a in range(half)] + [2 * a + 1 for a in reversed(range(half))]


def build(n_seq):
    chips = n_seq // 2
    ring = snake_ring(chips)
    place = [0] * chips
    for pos, chip in enumerate(ring):
        place[chip] = pos
    forward = [(ring[p] * 2 + c, ring[(p + 1) % chips] * 2 + c) for p in range(chips) for c in range(2)]
    backward = [(ring[(p + 1) % chips] * 2 + c, ring[p] * 2 + c) for p in range(chips) for c in range(2)]
    swap = [(i, i ^ 1) for i in range(n_seq)]
    ring_arr = jnp.asarray(ring, jnp.int32)
    place_arr = jnp.asarray(place, jnp.int32)

    def gather_ring(packet_a, packet_b, me):
        chip = me // 2
        core = me % 2
        pos = place_arr[chip]
        got_a, got_b, ids_a, ids_b = [], [], [], []
        cur_a, cur_b = packet_a, packet_b
        for step in range(chips):
            if step > 0:
                cur_a = lax.ppermute(cur_a, "seq", forward)
                cur_b = lax.ppermute(cur_b, "seq", backward)
            src_a = ring_arr[(pos - step) % chips] * 2 + core
            src_b = ring_arr[(pos + step) % chips] * 2 + core
            mate_a = lax.ppermute(cur_a, "seq", swap)
            mate_b = lax.ppermute(cur_b, "seq", swap)
            got_a += [cur_a, mate_a]
            got_b += [cur_b, mate_b]
            ids_a += [src_a, src_a ^ 1]
            ids_b += [src_b, src_b ^ 1]
        return got_a, got_b, jnp.stack(ids_a), jnp.stack(ids_b)

    return gather_ring


def attend_all(queries_3d, keys, values, keeping, scale_factor):
    scores = (
        jnp.einsum("qhd,khd->hqk", queries_3d, keys, preferred_element_type=jnp.float32)
        * scale_factor
    )
    masked = jnp.where(keeping[None, None, :], scores, neg_large)
    peak = jnp.max(masked, axis=2, keepdims=True)
    weights = jnp.where(keeping[None, None, :], jnp.exp(masked - peak), 0.0)
    totals = jnp.sum(weights, axis=2, keepdims=True)
    summed = jnp.einsum(
        "hqk,khd->hqd", weights.astype(jnp.bfloat16), values, preferred_element_type=jnp.float32
    )
    result = (summed / totals).astype(jnp.bfloat16)
    return result.transpose(1, 0, 2).reshape(queries_3d.shape[0], -1)


def solution(mesh):
    n_seq = mesh.shape["seq"]
    gather_ring = build(n_seq)

    def on_device(
        hidden, queries, key_rows, value_rows, gate_scale, out_weight, valid_count, assignment
    ):
        rows_dev = queries.shape[0]
        heads_here = queries.shape[1] // HEAD
        heads_a = heads_here // 2
        cut = heads_a * HEAD
        scale_factor = 1.0 / math.sqrt(HEAD)
        me = lax.axis_index("seq")
        pairs = lax.all_gather(jnp.concatenate([valid_count, assignment]), "seq", axis=0, tiled=False)
        counts_all, blocks_all = pairs[:, 0], pairs[:, 1]
        columns = jnp.arange(n_seq, dtype=jnp.int32)
        dev_counts = jnp.sum(
            jnp.where(blocks_all[:, None] == columns[None, :], counts_all[None, :], 0), axis=1
        )

        packet_a = jnp.concatenate([key_rows[:, :cut], value_rows[:, :cut]], axis=1)
        packet_b = jnp.concatenate([key_rows[:, cut:], value_rows[:, cut:]], axis=1)
        got_a, got_b, ids_a, ids_b = gather_ring(packet_a, packet_b, me)
        within = jnp.arange(rows_dev, dtype=jnp.int32)

        def half(got, ids, lo, hi):
            width = (hi - lo) * HEAD
            stack = jnp.concatenate(got, axis=0)
            keys = stack[:, :width].reshape(-1, hi - lo, HEAD)
            values = stack[:, width:].reshape(-1, hi - lo, HEAD)
            limits = jnp.sum(
                jnp.where(ids[:, None] == columns[None, :], dev_counts[None, :], 0), axis=1
            )
            keeping = (within[None, :] < limits[:, None]).reshape(-1)
            q3 = queries[:, lo * HEAD : hi * HEAD].reshape(rows_dev, hi - lo, HEAD)
            return attend_all(q3, keys, values, keeping, scale_factor)

        attention = jnp.concatenate(
            [half(got_a, ids_a, 0, heads_a), half(got_b, ids_b, heads_a, heads_here)], axis=1
        )
        partial = jnp.dot(attention, out_weight, preferred_element_type=jnp.float32)
        rows_out = hidden.shape[0]
        side = lax.axis_index("tp")
        n_tp = rows_dev // rows_out
        pieces = partial.reshape(n_tp, rows_out, partial.shape[1])
        own = jnp.take(pieces, side, axis=0)
        other = jnp.take(pieces, 1 - side, axis=0).astype(jnp.bfloat16)
        came = lax.ppermute(other, "tp", [(0, 1), (1, 0)])
        summed = own + came.astype(jnp.float32)
        return (hidden.astype(jnp.float32) + gate_scale * summed).astype(jnp.bfloat16)

    placed = (
        P(("seq", "tp"), None),
        P("seq", "tp"),
        P("seq", "tp"),
        P("seq", "tp"),
        P(),
        P("tp", None),
        P("seq"),
        P("seq"),
    )
    return jax.shard_map(
        on_device, mesh=mesh, in_specs=placed, out_specs=P(("seq", "tp"), None), check_vma=False
    )
```

time: 187 us -> 182 us (0.973)
  waiting for transfers between devices: 86.7 us -> 60.1 us
  blocking collectives: 33.8 us -> 11.4 us
  starting transfers between devices: 2.51 us -> 23 us
  matrix products: 14.1 us -> 22.2 us
  between operations: 15.6 us -> 22.9 us
  local copies, waits for them, and re-layouts: 29.4 us -> 36 us
    all_gather x2 -> x0, waiting for transfers between devices: 84.9 us -> none  [the longest x1 45.8 us: on_device(): lax.all_gather(key_rows, 'seq', axis=0, tiled=True)]
    ppermute x0 -> x31, waiting for transfers between devices: none -> 60.1 us  [the longest x7 32.3 us: gather_ring(): cur_a = lax.ppermute(cur_a, 'seq', forward)]
    ppermute x0 -> x31, starting transfers between devices: none -> 23 us  [the longest x7 12.8 us: gather_ring(): cur_a = lax.ppermute(cur_a, 'seq', forward)]
    unnamed x2 -> x1, blocking collectives: 33.8 us -> 11.4 us
    unnamed x23 -> x24, local copies, waits for them, and re-layouts: 19.1 us -> 1.93 us
    concatenate x0 -> x2, local copies, waits for them, and re-layouts: none -> 17.1 us  [half(): stack = jnp.concatenate(got, axis=0)]
    sub x0 -> x2, matrix products: none -> 9.92 us  [attend_all(): weights = jnp.where(keeping[None, None, :], jnp.exp(masked - peak), 0.0)]
    reduce_sum x5 -> x2, other arithmetic: 3.03 us -> 0.37 us  [the longest x1 0.18 us: half(): jnp.sum(jnp.where(ids[:, None] == columns[None, :], dev_counts[None, :],...]
  transfers between devices with their start and end apart: 3 -> 31, of which waited for: 3 -> 9; matrix products, arithmetic and copies ran while one was open for 6% -> 15% of each run, Pallas kernels for 0% -> 0%
where the time goes in v1:
time: 182 us; the launch traced here: 180 us
  waiting for transfers between devices  60.1 us (33%)
  local copies, waits for them, and re-layouts  36 us (20%)
  starting transfers between devices  23 us (13%)
  between operations  22.9 us (13%)
  matrix products  22.2 us (12%)
  blocking collectives  11.4 us (6%)
  other arithmetic  4.58 us (3%)
    ppermute x7, waiting for transfers between devices, gather_ring(): cur_a = lax.ppermute(cur_a, 'seq', forward)  32.3 us
    concatenate x2, local copies, waits for them, and re-layouts, half(): stack = jnp.concatenate(got, axis=0)  17.1 us
    ppermute x1, waiting for transfers between devices, on_device(): came = lax.ppermute(other, 'tp', [(0, 1), (1, 0)])  15.2 us
    ppermute x7, starting transfers between devices, gather_ring(): cur_a = lax.ppermute(cur_a, 'seq', forward)  12.8 us
    ppermute x7, waiting for transfers between devices, gather_ring(): cur_b = lax.ppermute(cur_b, 'seq', backward)  12.5 us
    unnamed x1, blocking collectives  11.4 us
    sub x2, matrix products, attend_all(): weights = jnp.where(keeping[None, None, :], jnp.exp(masked - peak), 0.0)  9.92 us
    slice x2, local copies, waits for them, and re-layouts, half(): keys = stack[:, :width].reshape(-1, hi - lo, HEAD)  8.53 us
  transfers between devices with their start and end apart: 31, of which 9 were waited for; matrix products, arithmetic and copies ran while one was open for 15% of the time, Pallas kernels for 0%

profile of v1, /device:TPU:0, one launch (start us, length us, event | category | flops | bytes accessed | tf_op | source)
XLA Modules:
  0.0 180.0 jit_solution(3369681548424540454)
XLA Ops:
  0.0 1.1 fusion.59
  1.1 0.2 copy.45
  1.2 1.0 fusion.60
  2.3 0.2 copy.46
  2.5 3.1 %collective-permute-start.1 = (bf16[120,1280]{0,1:T(8,128)(2,1)S(1)}, bf16[120,1280]{0,1:T(8,128)(2,1)S(1)}, u32[]{:S(2)}, u32[]{:S(2)}) collective-permute-start(bf16[120,1280]{0,1:T(8,128)(2,1)S(1)} %pad_maximum_fusion), channel_id=1, source_target_pairs={{0,8},{2,10},{8,16},{10,18},{16,24},{18,26},{24,28},{26,30},{28,20... | collective-permute-start | bytes 921608 | tf_op jit(solution)/shard_map/ppermute | solution.py:37
  5.6 7.7 %collective-permute-done.1 = bf16[120,1280]{0,1:T(8,128)(2,1)S(1)} collective-permute-done((bf16[120,1280]{0,1:T(8,128)(2,1)S(1)}, bf16[120,1280]{0,1:T(8,128)(2,1)S(1)}, u32[]{:S(2)}, u32[]{:S(2)}) %collective-permute-start.1) | collective-permute-done | bytes 307232 | tf_op jit(solution)/shard_map/ppermute | solution.py:37
  13.2 1.8 collective-permute-start.3
  15.0 0.2 copy.47
  15.2 0.2 copy.48
  15.4 0.3 collective-permute-start.16
  15.7 6.4 %collective-permute-done.3 = bf16[120,1280]{0,1:T(8,128)(2,1)S(1)} collective-permute-done((bf16[120,1280]{0,1:T(8,128)(2,1)S(1)}, bf16[120,1280]{0,1:T(8,128)(2,1)S(1)}, u32[]{:S(2)}, u32[]{:S(2)}) %collective-permute-start.3) | collective-permute-done | bytes 307232 | tf_op jit(solution)/shard_map/ppermute | solution.py:37
  22.1 1.5 collective-permute-start.5
  23.6 0.2 collective-permute-done.16
  23.8 0.5 collective-permute-start.18
  24.3 5.8 %collective-permute-done.5 = bf16[120,1280]{0,1:T(8,128)(2,1)S(1)} collective-permute-done((bf16[120,1280]{0,1:T(8,128)(2,1)S(1)}, bf16[120,1280]{0,1:T(8,128)(2,1)S(1)}, u32[]{:S(2)}, u32[]{:S(2)}) %collective-permute-start.5) | collective-permute-done | bytes 307232 | tf_op jit(solution)/shard_map/ppermute | solution.py:37
  30.1 1.4 collective-permute-start.7
  31.5 0.7 collective-permute-start.20
  32.1 5.8 %collective-permute-done.7 = bf16[120,1280]{0,1:T(8,128)(2,1)S(1)} collective-permute-done((bf16[120,1280]{0,1:T(8,128)(2,1)S(1)}, bf16[120,1280]{0,1:T(8,128)(2,1)S(1)}, u32[]{:S(2)}, u32[]{:S(2)}) %collective-permute-start.7) | collective-permute-done | bytes 307232 | tf_op jit(solution)/shard_map/ppermute | solution.py:37
  38.0 1.9 %collective-permute-start.9 = (bf16[120,1280]{0,1:T(8,128)(2,1)S(1)}, bf16[120,1280]{0,1:T(8,128)(2,1)}, u32[]{:S(2)}, u32[]{:S(2)}) collective-permute-start(bf16[120,1280]{0,1:T(8,128)(2,1)S(1)} %collective-permute-done.7), channel_id=1, source_target_pairs={{0,8},{2,10},{8,16},{10,18},{16,24},{18,26},{24,28},{26,30},{28,20... | collective-permute-start | bytes 921608 | tf_op jit(solution)/shard_map/ppermute | solution.py:37
  39.9 0.1 collective-permute-start.22
  40.0 6.6 %collective-permute-done.9 = bf16[120,1280]{0,1:T(8,128)(2,1)} collective-permute-done((bf16[120,1280]{0,1:T(8,128)(2,1)S(1)}, bf16[120,1280]{0,1:T(8,128)(2,1)}, u32[]{:S(2)}, u32[]{:S(2)}) %collective-permute-start.9) | collective-permute-done | bytes 307232 | tf_op jit(solution)/shard_map/ppermute | solution.py:37
  46.6 2.3 %collective-permute-start.11 = (bf16[120,1280]{0,1:T(8,128)(2,1)}, bf16[120,1280]{0,1:T(8,128)(2,1)}, u32[]{:S(2)}, u32[]{:S(2)}) collective-permute-start(bf16[120,1280]{0,1:T(8,128)(2,1)} %collective-permute-done.9), channel_id=1, source_target_pairs={{0,8},{2,10},{8,16},{10,18},{16,24},{18,26},{24,28},{26,30},{28,20... | collective-permute-start | bytes 921608 | tf_op jit(solution)/shard_map/ppermute | solution.py:37
  49.0 0.6 dynamic_slice.49
  60.9 0.8 fusion.61
  72.3 0.6 dynamic-slice.5
  73.5 0.2 add_dynamic-update-slice_fusion
  73.7 11.4 %all-reduce = s32[32]{0:T(128)S(1)} all-reduce(s32[32]{0:T(128)S(1)} %add_dynamic-update-slice_fusion), channel_id=2, replica_groups=mesh['seq'=16,'tp'=2] {'seq'}, use_global_device_ids=true, to_apply=%add | all-reduce | flops 32 | bytes 256
  85.1 0.1 stack.129
  85.4 0.5 collective-permute-start.4
  86.0 1.2 collective-permute-start.24
  87.2 0.8 collective-permute-start.13
  88.0 0.2 slice_reduce_fusion.1
  88.2 0.2 select_reduce_fusion.2
  88.4 0.2 select_reduce_fusion.1
  88.7 0.5 collective-permute-start.10
  89.2 7.0 %collective-permute-done.24 = bf16[120,1280]{0,1:T(8,128)(2,1)} collective-permute-done((bf16[120,1280]{0,1:T(8,128)(2,1)S(1)}, bf16[120,1280]{0,1:T(8,128)(2,1)}, u32[]{:S(2)}, u32[]{:S(2)}) %collective-permute-start.24) | collective-permute-done | bytes 307232 | tf_op jit(solution)/shard_map/ppermute | solution.py:38
  96.2 1.2 collective-permute-start.26
  97.5 0.6 copy-done.4
  98.3 1.0 fusion.58
  99.3 0.2 copy.27
  99.5 0.1 lt.199
  99.6 0.2 copy.34
  99.7 0.6 collective-permute-start.15
  100.4 5.4 %collective-permute-done.26 = bf16[120,1280]{0,1:T(8,128)(2,1)} collective-permute-done((bf16[120,1280]{0,1:T(8,128)(2,1)}, bf16[120,1280]{0,1:T(8,128)(2,1)}, u32[]{:S(2)}, u32[]{:S(2)}) %collective-permute-start.26) | collective-permute-done | bytes 307232 | tf_op jit(solution)/shard_map/ppermute | solution.py:38
  105.8 0.5 collective-permute-start.21
  106.3 1.2 collective-permute-start.28
  107.5 8.4 %concatenate.20 = bf16[1920,1280]{0,1:T(8,128)(2,1)} concatenate(bf16[120,1280]{0,1:T(8,128)(2,1)S(1)} %pad_maximum_fusion, bf16[120,1280]{0,1:T(8,128)(2,1)} %collective-permute-done, bf16[120,1280]{0,1:T(8,128)(2,1)S(1)} %collective-permute-done.1, bf16[120,1280]{0,1:T(8,128)(2,1)} %copy-done.2, bf16[120,1280]{0,1:T(8,128)(2,1)S(1)} %collective-permute-done.3, ...), dimensions={0} | concatenate | bytes 9830400 | tf_op jit(solution)/shard_map/concatenate | solution.py:95
  115.9 4.3 %fusion.56 = (bf16[1920,640]{0,1:T(8,128)(2,1)}, bf16[1920,640]{0,1:T(8,128)(2,1)S(1)}) fusion(bf16[1920,1280]{0,1:T(8,128)(2,1)} %concatenate.20), kind=kLoop, calls=%fused_computation.59 | loop fusion | bytes 9830400 | tf_op jit(solution)/shard_map/slice | solution.py:96
  120.2 5.0 %fusion.63 = (f32[5,120]{1,0:T(8,128)S(1)}, bf16[5,120,1920]{2,1,0:T(8,128)(2,1)}) fusion(pred[1920]{0:T(1024)(128)(4,1)S(1)} %lt.181, bf16[1920,5,128]{0,2,1:T(8,128)(2,1)} %bitcast.120, bf16[120,5,128]{0,2,1:T(8,128)(2,1)S(1)} %bitcast.125), kind=kOutput, calls=%fused_computation.66 | convolution fusion | flops 301825920 | bytes 4919520 | tf_op jit(solution)/shard_map/sub | solution.py:59
  125.1 0.5 collective-permute-start.25
  125.7 0.4 collective-permute-start.29
  126.2 3.2 %fusion.37 = bf16[120,5,128]{2,0,1:T(8,128)(2,1)} fusion(bf16[1920,5,128]{0,2,1:T(8,128)(2,1)S(1)} %bitcast.118, bf16[5,120,1920]{2,1,0:T(8,128)(2,1)} %get-tuple-element.49, f32[120,5]{0,1:T(8,128)S(1)} %bitcast.126), kind=kOutput, calls=%fused_computation.33 | convolution fusion | flops 295065600 | bytes 4917600 | tf_op jit(solution)/shard_map/hqk,khd->hqd/dot_general | solution.py:61
  129.3 1.1 copy.31
  130.5 8.7 %concatenate.22 = bf16[1920,1280]{0,1:T(8,128)(2,1)} concatenate(bf16[120,1280]{0,1:T(8,128)(2,1)S(1)} %pad_maximum_fusion.1, bf16[120,1280]{0,1:T(8,128)(2,1)} %collective-permute-done.15, bf16[120,1280]{0,1:T(8,128)(2,1)S(1)} %collective-permute-done.16, bf16[120,1280]{0,1:T(8,128)(2,1)} %collective-permute-done.17, bf16[120,1280]{0,1:T(8,128)(2,1)} %collective-permute-done.18, ...), dimensions={0} | concatenate | bytes 9830400 | tf_op jit(solution)/shard_map/concatenate | solution.py:95
  139.1 4.3 %fusion.57 = (bf16[1920,640]{0,1:T(8,128)(2,1)}, bf16[1920,640]{0,1:T(8,128)(2,1)S(1)}) fusion(bf16[1920,1280]{0,1:T(8,128)(2,1)} %concatenate.22), kind=kLoop, calls=%fused_computation.60 | loop fusion | bytes 9830400 | tf_op jit(solution)/shard_map/slice | solution.py:96
  143.4 5.0 %fusion.62 = (f32[5,120]{1,0:T(8,128)S(1)}, bf16[5,120,1920]{2,1,0:T(8,128)(2,1)}) fusion(pred[1920]{0:T(1024)(128)(4,1)S(1)} %lt.199, bf16[1920,5,128]{0,2,1:T(8,128)(2,1)} %bitcast.121, bf16[120,5,128]{0,2,1:T(8,128)(2,1)S(1)} %bitcast.124), kind=kOutput, calls=%fused_computation.65 | convolution fusion | flops 301825920 | bytes 4919520 | tf_op jit(solution)/shard_map/sub | solution.py:59
  148.3 2.5 %fusion.40 = bf16[120,5,128]{2,0,1:T(8,128)(2,1)S(1)} fusion(bf16[1920,5,128]{0,2,1:T(8,128)(2,1)S(1)} %bitcast.119, bf16[5,120,1920]{2,1,0:T(8,128)(2,1)} %get-tuple-element.47, f32[120,5]{0,1:T(8,128)S(1)} %bitcast.127), kind=kOutput, calls=%fused_computation.34 | convolution fusion | flops 295065600 | bytes 4917600 | tf_op jit(solution)/shard_map/hqk,khd->hqd/dot_general | solution.py:61
  150.9 0.2 copy.38
  151.0 6.6 %fusion.43 = f32[120,5120]{1,0:T(8,128)S(1)} fusion(bf16[1280,5120]{1,0:T(8,128)(2,1)} %param.17, bf16[120,640]{0,1:T(8,128)(2,1)S(1)} %bitcast.123, bf16[120,640]{0,1:T(8,128)(2,1)S(1)} %bitcast.122), kind=kOutput, calls=%fused_computation.37 | convolution fusion | flops 1573478400 | bytes 15872000 | tf_op jit(solution)/shard_map/dot_general | solution.py:108
  157.7 1.7 reshape.105
  159.4 1.4 bitcast_convert_fusion
  160.8 1.5 collective-permute-start.30
  162.4 15.2 %collective-permute-done.30 = bf16[60,5120]{1,0:T(8,128)(2,1)S(1)} collective-permute-done((bf16[60,5120]{1,0:T(8,128)(2,1)S(1)}, bf16[60,5120]{1,0:T(8,128)(2,1)S(1)}, u32[]{:S(2)}, u32[]{:S(2)}) %collective-permute-start.30) | collective-permute-done | bytes 614432 | tf_op jit(solution)/shard_map/ppermute | solution.py:115
  177.6 2.4 %fusion.24 = bf16[60,5120]{1,0:T(8,128)(2,1)} fusion(f32[2,60,5120]{2,1,0:T(8,128)} %reshape.105, s32[]{:T(128)S(6)} %select_n.203, bf16[60,5120]{1,0:T(8,128)(2,1)S(1)} %collective-permute-done.30, bf16[60,5120]{1,0:T(8,128)(2,1)S(1)} %copy-done, f32[5120]{0:T(1024)S(1)} %copy-done.6, pred[]{:T(512)S(6)} %and.96), kind=kLoop, calls=%fused_computation.28 | loop fusion | flops 2150400 | bytes 3092485 | tf_op jit(solution)/shard_map/convert_element_type | solution.py:117
  (56 shorter events, 1.0 us)
Async XLA Ops:
  0.0 49.0 %copy-start.8 = (s32[8]{0:T(128)S(1)}, s32[8]{0:T(128)}, u32[]{:S(2)}) copy-start(s32[8]{0:T(128)} %constant.163.clone) | copy-start | bytes 100
  0.0 60.9 %copy-start.5 = (s32[8]{0:T(128)S(1)}, s32[8]{0:T(128)}, u32[]{:S(2)}) copy-start(s32[8]{0:T(128)} %constant.164.clone) | copy-start | bytes 100
  0.0 72.3 %copy-start.7 = (u32[32]{0:T(128)S(1)}, u32[32]{0:T(128)}, u32[]{:S(2)}) copy-start(u32[32]{0:T(128)} %constant.196) | copy-start | bytes 388
  2.5 10.7 %collective-permute-start.1 = (bf16[120,1280]{0,1:T(8,128)(2,1)S(1)}, bf16[120,1280]{0,1:T(8,128)(2,1)S(1)}, u32[]{:S(2)}, u32[]{:S(2)}) collective-permute-start(bf16[120,1280]{0,1:T(8,128)(2,1)S(1)} %pad_maximum_fusion), channel_id=1, source_target_pairs={{0,8},{2,10},{8,16},{10,18},{16,24},{18,26},{24,28},{26,30},{28,20... | collective-permute-start | bytes 921608 | tf_op jit(solution)/shard_map/ppermute | solution.py:37
  13.2 8.9 %collective-permute-start.3 = (bf16[120,1280]{0,1:T(8,128)(2,1)S(1)}, bf16[120,1280]{0,1:T(8,128)(2,1)S(1)}, u32[]{:S(2)}, u32[]{:S(2)}) collective-permute-start(bf16[120,1280]{0,1:T(8,128)(2,1)S(1)} %collective-permute-done.1), channel_id=1, source_target_pairs={{0,8},{2,10},{8,16},{10,18},{16,24},{18,26},{24,28},{26,30},{28,20... | collective-permute-start | bytes 921608 | tf_op jit(solution)/shard_map/ppermute | solution.py:37
  15.4 8.4 %collective-permute-start.16 = (bf16[120,1280]{0,1:T(8,128)(2,1)S(1)}, bf16[120,1280]{0,1:T(8,128)(2,1)S(1)}, u32[]{:S(2)}, u32[]{:S(2)}) collective-permute-start(bf16[120,1280]{0,1:T(8,128)(2,1)S(1)} %pad_maximum_fusion.1), channel_id=1, source_target_pairs={{8,0},{10,2},{16,8},{18,10},{24,16},{26,18},{28,24},{30,26},{20,28... | collective-permute-start | bytes 921608 | tf_op jit(solution)/shard_map/ppermute | solution.py:38
  22.1 8.0 %collective-permute-start.5 = (bf16[120,1280]{0,1:T(8,128)(2,1)S(1)}, bf16[120,1280]{0,1:T(8,128)(2,1)S(1)}, u32[]{:S(2)}, u32[]{:S(2)}) collective-permute-start(bf16[120,1280]{0,1:T(8,128)(2,1)S(1)} %collective-permute-done.3), channel_id=1, source_target_pairs={{0,8},{2,10},{8,16},{10,18},{16,24},{18,26},{24,28},{26,30},{28,20... | collective-permute-start | bytes 921608 | tf_op jit(solution)/shard_map/ppermute | solution.py:37
  23.8 7.7 %collective-permute-start.18 = (bf16[120,1280]{0,1:T(8,128)(2,1)S(1)}, bf16[120,1280]{0,1:T(8,128)(2,1)}, u32[]{:S(2)}, u32[]{:S(2)}) collective-permute-start(bf16[120,1280]{0,1:T(8,128)(2,1)S(1)} %collective-permute-done.16), channel_id=1, source_target_pairs={{8,0},{10,2},{16,8},{18,10},{24,16},{26,18},{28,24},{30,26},{20,28... | collective-permute-start | bytes 921608 | tf_op jit(solution)/shard_map/ppermute | solution.py:38
  30.1 7.9 %collective-permute-start.7 = (bf16[120,1280]{0,1:T(8,128)(2,1)S(1)}, bf16[120,1280]{0,1:T(8,128)(2,1)S(1)}, u32[]{:S(2)}, u32[]{:S(2)}) collective-permute-start(bf16[120,1280]{0,1:T(8,128)(2,1)S(1)} %collective-permute-done.5), channel_id=1, source_target_pairs={{0,8},{2,10},{8,16},{10,18},{16,24},{18,26},{24,28},{26,30},{28,20... | collective-permute-start | bytes 921608 | tf_op jit(solution)/shard_map/ppermute | solution.py:37
  31.5 8.4 %collective-permute-start.20 = (bf16[120,1280]{0,1:T(8,128)(2,1)}, bf16[120,1280]{0,1:T(8,128)(2,1)}, u32[]{:S(2)}, u32[]{:S(2)}) collective-permute-start(bf16[120,1280]{0,1:T(8,128)(2,1)} %collective-permute-done.18), channel_id=1, source_target_pairs={{8,0},{10,2},{16,8},{18,10},{24,16},{26,18},{28,24},{30,26},{20,28... | collective-permute-start | bytes 921608 | tf_op jit(solution)/shard_map/ppermute | solution.py:38
  38.0 8.7 %collective-permute-start.9 = (bf16[120,1280]{0,1:T(8,128)(2,1)S(1)}, bf16[120,1280]{0,1:T(8,128)(2,1)}, u32[]{:S(2)}, u32[]{:S(2)}) collective-permute-start(bf16[120,1280]{0,1:T(8,128)(2,1)S(1)} %collective-permute-done.7), channel_id=1, source_target_pairs={{0,8},{2,10},{8,16},{10,18},{16,24},{18,26},{24,28},{26,30},{28,20... | collective-permute-start | bytes 921608 | tf_op jit(solution)/shard_map/ppermute | solution.py:37
  39.9 46.1 %collective-permute-start = (bf16[120,1280]{0,1:T(8,128)(2,1)S(1)}, bf16[120,1280]{0,1:T(8,128)(2,1)}, u32[]{:S(2)}, u32[]{:S(2)}) collective-permute-start(bf16[120,1280]{0,1:T(8,128)(2,1)S(1)} %pad_maximum_fusion), channel_id=1, source_target_pairs={{0,2},{2,0},{4,6},{6,4},{8,10},{10,8},{12,14},{14,12},{16,18},{18,... | collective-permute-start | bytes 921608 | tf_op jit(solution)/shard_map/ppermute | solution.py:41
  39.9 46.1 %collective-permute-start.22 = (bf16[120,1280]{0,1:T(8,128)(2,1)}, bf16[120,1280]{0,1:T(8,128)(2,1)S(1)}, u32[]{:S(2)}, u32[]{:S(2)}) collective-permute-start(bf16[120,1280]{0,1:T(8,128)(2,1)} %collective-permute-done.20), channel_id=1, source_target_pairs={{8,0},{10,2},{16,8},{18,10},{24,16},{26,18},{28,24},{30,26},{20,28... | collective-permute-start | bytes 921608 | tf_op jit(solution)/shard_map/ppermute | solution.py:38
  46.6 40.5 %collective-permute-start.11 = (bf16[120,1280]{0,1:T(8,128)(2,1)}, bf16[120,1280]{0,1:T(8,128)(2,1)}, u32[]{:S(2)}, u32[]{:S(2)}) collective-permute-start(bf16[120,1280]{0,1:T(8,128)(2,1)} %collective-permute-done.9), channel_id=1, source_target_pairs={{0,8},{2,10},{8,16},{10,18},{16,24},{18,26},{24,28},{26,30},{28,20... | collective-permute-start | bytes 921608 | tf_op jit(solution)/shard_map/ppermute | solution.py:37
  85.3 3.2 %collective-permute-start.2 = (bf16[120,1280]{0,1:T(8,128)(2,1)S(1)}, bf16[120,1280]{0,1:T(8,128)(2,1)S(1)}, u32[]{:S(2)}, u32[]{:S(2)}) collective-permute-start(bf16[120,1280]{0,1:T(8,128)(2,1)S(1)} %collective-permute-done.1), channel_id=1, source_target_pairs={{0,2},{2,0},{4,6},{6,4},{8,10},{10,8},{12,14},{14,12},{16,18},{18,... | collective-permute-start | bytes 921608 | tf_op jit(solution)/shard_map/ppermute | solution.py:41
  85.4 3.3 %collective-permute-start.4 = (bf16[120,1280]{0,1:T(8,128)(2,1)S(1)}, bf16[120,1280]{0,1:T(8,128)(2,1)S(1)}, u32[]{:S(2)}, u32[]{:S(2)}) collective-permute-start(bf16[120,1280]{0,1:T(8,128)(2,1)S(1)} %collective-permute-done.3), channel_id=1, source_target_pairs={{0,2},{2,0},{4,6},{6,4},{8,10},{10,8},{12,14},{14,12},{16,18},{18,... | collective-permute-start | bytes 921608 | tf_op jit(solution)/shard_map/ppermute | solution.py:41
  85.9 11.4 %collective-permute-start.6 = (bf16[120,1280]{0,1:T(8,128)(2,1)S(1)}, bf16[120,1280]{0,1:T(8,128)(2,1)S(1)}, u32[]{:S(2)}, u32[]{:S(2)}) collective-permute-start(bf16[120,1280]{0,1:T(8,128)(2,1)S(1)} %collective-permute-done.5), channel_id=1, source_target_pairs={{0,2},{2,0},{4,6},{6,4},{8,10},{10,8},{12,14},{14,12},{16,18},{18,... | collective-permute-start | bytes 921608 | tf_op jit(solution)/shard_map/ppermute | solution.py:41
  86.0 12.2 %copy-start.1 = (bf16[120,1280]{0,1:T(8,128)(2,1)}, bf16[120,1280]{0,1:T(8,128)(2,1)S(1)}, u32[]{:S(2)}) copy-start(bf16[120,1280]{0,1:T(8,128)(2,1)S(1)} %collective-permute-done.22) | copy-start | bytes 921604
  86.0 10.2 %collective-permute-start.24 = (bf16[120,1280]{0,1:T(8,128)(2,1)S(1)}, bf16[120,1280]{0,1:T(8,128)(2,1)}, u32[]{:S(2)}, u32[]{:S(2)}) collective-permute-start(bf16[120,1280]{0,1:T(8,128)(2,1)S(1)} %collective-permute-done.22), channel_id=1, source_target_pairs={{8,0},{10,2},{16,8},{18,10},{24,16},{26,18},{28,24},{30,26},{20,28... | collective-permute-start | bytes 921608 | tf_op jit(solution)/shard_map/ppermute | solution.py:38
  87.2 10.3 %collective-permute-start.13 = (bf16[120,1280]{0,1:T(8,128)(2,1)}, bf16[120,1280]{0,1:T(8,128)(2,1)}, u32[]{:S(2)}, u32[]{:S(2)}) collective-permute-start(bf16[120,1280]{0,1:T(8,128)(2,1)} %collective-permute-done.11), channel_id=1, source_target_pairs={{0,8},{2,10},{8,16},{10,18},{16,24},{18,26},{24,28},{26,30},{28,20... | collective-permute-start | bytes 921608 | tf_op jit(solution)/shard_map/ppermute | solution.py:37
  88.6 8.8 %copy-start.2 = (bf16[120,1280]{0,1:T(8,128)(2,1)}, bf16[120,1280]{0,1:T(8,128)(2,1)S(1)}, u32[]{:S(2)}) copy-start(bf16[120,1280]{0,1:T(8,128)(2,1)S(1)} %collective-permute-done.2) | copy-start | bytes 921604
  88.6 11.1 %collective-permute-start.8 = (bf16[120,1280]{0,1:T(8,128)(2,1)S(1)}, bf16[120,1280]{0,1:T(8,128)(2,1)}, u32[]{:S(2)}, u32[]{:S(2)}) collective-permute-start(bf16[120,1280]{0,1:T(8,128)(2,1)S(1)} %collective-permute-done.7), channel_id=1, source_target_pairs={{0,2},{2,0},{4,6},{6,4},{8,10},{10,8},{12,14},{14,12},{16,18},{18,... | collective-permute-start | bytes 921608 | tf_op jit(solution)/shard_map/ppermute | solution.py:41
  88.7 8.7 %copy-start.3 = (bf16[120,1280]{0,1:T(8,128)(2,1)}, bf16[120,1280]{0,1:T(8,128)(2,1)S(1)}, u32[]{:S(2)}) copy-start(bf16[120,1280]{0,1:T(8,128)(2,1)S(1)} %collective-permute-done.4) | copy-start | bytes 921604
  88.7 11.6 %collective-permute-start.10 = (bf16[120,1280]{0,1:T(8,128)(2,1)}, bf16[120,1280]{0,1:T(8,128)(2,1)}, u32[]{:S(2)}, u32[]{:S(2)}) collective-permute-start(bf16[120,1280]{0,1:T(8,128)(2,1)} %collective-permute-done.9), channel_id=1, source_target_pairs={{0,2},{2,0},{4,6},{6,4},{8,10},{10,8},{12,14},{14,12},{16,18},{18,... | collective-permute-start | bytes 921608 | tf_op jit(solution)/shard_map/ppermute | solution.py:41
  96.2 9.6 %collective-permute-start.26 = (bf16[120,1280]{0,1:T(8,128)(2,1)}, bf16[120,1280]{0,1:T(8,128)(2,1)}, u32[]{:S(2)}, u32[]{:S(2)}) collective-permute-start(bf16[120,1280]{0,1:T(8,128)(2,1)} %collective-permute-done.24), channel_id=1, source_target_pairs={{8,0},{10,2},{16,8},{18,10},{24,16},{26,18},{28,24},{30,26},{20,28... | collective-permute-start | bytes 921608 | tf_op jit(solution)/shard_map/ppermute | solution.py:38
  97.4 0.7 copy-start.4
  97.4 8.4 %collective-permute-start.12 = (bf16[120,1280]{0,1:T(8,128)(2,1)}, bf16[120,1280]{0,1:T(8,128)(2,1)}, u32[]{:S(2)}, u32[]{:S(2)}) collective-permute-start(bf16[120,1280]{0,1:T(8,128)(2,1)} %collective-permute-done.11), channel_id=1, source_target_pairs={{0,2},{2,0},{4,6},{6,4},{8,10},{10,8},{12,14},{14,12},{16,18},{18,... | collective-permute-start | bytes 921608 | tf_op jit(solution)/shard_map/ppermute | solution.py:41
  98.1 8.2 %collective-permute-start.14 = (bf16[120,1280]{0,1:T(8,128)(2,1)}, bf16[120,1280]{0,1:T(8,128)(2,1)}, u32[]{:S(2)}, u32[]{:S(2)}) collective-permute-start(bf16[120,1280]{0,1:T(8,128)(2,1)} %collective-permute-done.13), channel_id=1, source_target_pairs={{0,2},{2,0},{4,6},{6,4},{8,10},{10,8},{12,14},{14,12},{16,18},{18,... | collective-permute-start | bytes 921608 | tf_op jit(solution)/shard_map/ppermute | solution.py:41
  99.7 25.4 %collective-permute-start.15 = (bf16[120,1280]{0,1:T(8,128)(2,1)S(1)}, bf16[120,1280]{0,1:T(8,128)(2,1)}, u32[]{:S(2)}, u32[]{:S(2)}) collective-permute-start(bf16[120,1280]{0,1:T(8,128)(2,1)S(1)} %pad_maximum_fusion.1), channel_id=1, source_target_pairs={{0,2},{2,0},{4,6},{6,4},{8,10},{10,8},{12,14},{14,12},{16,18},{18,... | collective-permute-start | bytes 921608 | tf_op jit(solution)/shard_map/ppermute | solution.py:42
  100.3 24.8 %collective-permute-start.17 = (bf16[120,1280]{0,1:T(8,128)(2,1)S(1)}, bf16[120,1280]{0,1:T(8,128)(2,1)}, u32[]{:S(2)}, u32[]{:S(2)}) collective-permute-start(bf16[120,1280]{0,1:T(8,128)(2,1)S(1)} %collective-permute-done.16), channel_id=1, source_target_pairs={{0,2},{2,0},{4,6},{6,4},{8,10},{10,8},{12,14},{14,12},{16,18},{18,... | collective-permute-start | bytes 921608 | tf_op jit(solution)/shard_map/ppermute | solution.py:42
  105.8 19.9 %collective-permute-start.19 = (bf16[120,1280]{0,1:T(8,128)(2,1)}, bf16[120,1280]{0,1:T(8,128)(2,1)}, u32[]{:S(2)}, u32[]{:S(2)}) collective-permute-start(bf16[120,1280]{0,1:T(8,128)(2,1)} %collective-permute-done.18), channel_id=1, source_target_pairs={{0,2},{2,0},{4,6},{6,4},{8,10},{10,8},{12,14},{14,12},{16,18},{18,... | collective-permute-start | bytes 921608 | tf_op jit(solution)/shard_map/ppermute | solution.py:42
  105.8 24.6 %collective-permute-start.21 = (bf16[120,1280]{0,1:T(8,128)(2,1)}, bf16[120,1280]{0,1:T(8,128)(2,1)}, u32[]{:S(2)}, u32[]{:S(2)}) collective-permute-start(bf16[120,1280]{0,1:T(8,128)(2,1)} %collective-permute-done.20), channel_id=1, source_target_pairs={{0,2},{2,0},{4,6},{6,4},{8,10},{10,8},{12,14},{14,12},{16,18},{18,... | collective-permute-start | bytes 921608 | tf_op jit(solution)/shard_map/ppermute | solution.py:42
  106.3 19.4 %collective-permute-start.28 = (bf16[120,1280]{0,1:T(8,128)(2,1)}, bf16[120,1280]{0,1:T(8,128)(2,1)}, u32[]{:S(2)}, u32[]{:S(2)}) collective-permute-start(bf16[120,1280]{0,1:T(8,128)(2,1)} %collective-permute-done.26), channel_id=1, source_target_pairs={{8,0},{10,2},{16,8},{18,10},{24,16},{26,18},{28,24},{30,26},{20,28... | collective-permute-start | bytes 921608 | tf_op jit(solution)/shard_map/ppermute | solution.py:38
  125.1 5.3 %collective-permute-start.23 = (bf16[120,1280]{0,1:T(8,128)(2,1)}, bf16[120,1280]{0,1:T(8,128)(2,1)}, u32[]{:S(2)}, u32[]{:S(2)}) collective-permute-start(bf16[120,1280]{0,1:T(8,128)(2,1)} %copy-done.1), channel_id=1, source_target_pairs={{0,2},{2,0},{4,6},{6,4},{8,10},{10,8},{12,14},{14,12},{16,18},{18,... | collective-permute-start | bytes 921608 | tf_op jit(solution)/shard_map/ppermute | solution.py:42
  125.1 5.3 %collective-permute-start.25 = (bf16[120,1280]{0,1:T(8,128)(2,1)}, bf16[120,1280]{0,1:T(8,128)(2,1)}, u32[]{:S(2)}, u32[]{:S(2)}) collective-permute-start(bf16[120,1280]{0,1:T(8,128)(2,1)} %collective-permute-done.24), channel_id=1, source_target_pairs={{0,2},{2,0},{4,6},{6,4},{8,10},{10,8},{12,14},{14,12},{16,18},{18,... | collective-permute-start | bytes 921608 | tf_op jit(solution)/shard_map/ppermute | solution.py:42
  125.7 4.8 %collective-permute-start.27 = (bf16[120,1280]{0,1:T(8,128)(2,1)}, bf16[120,1280]{0,1:T(8,128)(2,1)}, u32[]{:S(2)}, u32[]{:S(2)}) collective-permute-start(bf16[120,1280]{0,1:T(8,128)(2,1)} %collective-permute-done.26), channel_id=1, source_target_pairs={{0,2},{2,0},{4,6},{6,4},{8,10},{10,8},{12,14},{14,12},{16,18},{18,... | collective-permute-start | bytes 921608 | tf_op jit(solution)/shard_map/ppermute | solution.py:42
  125.7 4.7 %collective-permute-start.29 = (bf16[120,1280]{0,1:T(8,128)(2,1)}, bf16[120,1280]{0,1:T(8,128)(2,1)}, u32[]{:S(2)}, u32[]{:S(2)}) collective-permute-start(bf16[120,1280]{0,1:T(8,128)(2,1)} %collective-permute-done.28), channel_id=1, source_target_pairs={{0,2},{2,0},{4,6},{6,4},{8,10},{10,8},{12,14},{14,12},{16,18},{18,... | collective-permute-start | bytes 921608 | tf_op jit(solution)/shard_map/ppermute | solution.py:42
  157.7 19.9 %copy-start = (bf16[60,5120]{1,0:T(8,128)(2,1)S(1)}, bf16[60,5120]{1,0:T(8,128)(2,1)}, u32[]{:S(2)}) copy-start(bf16[60,5120]{1,0:T(8,128)(2,1)} %param.12) | copy-start | bytes 1843204
  157.7 19.9 %copy-start.6 = (f32[5120]{0:T(1024)S(1)}, f32[5120]{0:T(1024)}, u32[]{:S(2)}) copy-start(f32[5120]{0:T(1024)} %param.16) | copy-start | bytes 61444
  160.8 16.8 %collective-permute-start.30 = (bf16[60,5120]{1,0:T(8,128)(2,1)S(1)}, bf16[60,5120]{1,0:T(8,128)(2,1)S(1)}, u32[]{:S(2)}, u32[]{:S(2)}) collective-permute-start(bf16[60,5120]{1,0:T(8,128)(2,1)S(1)} %bitcast_convert_fusion), channel_id=1, source_target_pairs={{0,1},{1,0},{2,3},{3,2},{4,5},{5,4},{6,7},{7,6},{8,9},{9,8},{10,11... | collective-permute-start | bytes 1843208 | tf_op jit(solution)/shard_map/ppermute | solution.py:115

commit v2 on v1

--- a/solution.py
+++ b/solution.py
@@ -17,27 +17,26 @@
 def build(n_seq):
     chips = n_seq // 2
     ring = snake_ring(chips)
-    place = [0] * chips
-    for pos, chip in enumerate(ring):
-        place[chip] = pos
+    half = chips // 2
     forward = [(ring[p] * 2 + c, ring[(p + 1) % chips] * 2 + c) for p in range(chips) for c in range(2)]
     backward = [(ring[(p + 1) % chips] * 2 + c, ring[p] * 2 + c) for p in range(chips) for c in range(2)]
     swap = [(i, i ^ 1) for i in range(n_seq)]
-    ring_arr = jnp.asarray(ring, jnp.int32)
-    place_arr = jnp.asarray(place, jnp.int32)
+
+    def chip_at(pos):
+        return jnp.where(pos < half, 2 * pos, 2 * (chips - 1 - pos) + 1)
 
     def gather_ring(packet_a, packet_b, me):
         chip = me // 2
         core = me % 2
-        pos = place_arr[chip]
+        pos = jnp.where(chip % 2 == 0, chip // 2, chips - 1 - chip // 2)
         got_a, got_b, ids_a, ids_b = [], [], [], []
         cur_a, cur_b = packet_a, packet_b
         for step in range(chips):
             if step > 0:
                 cur_a = lax.ppermute(cur_a, "seq", forward)
                 cur_b = lax.ppermute(cur_b, "seq", backward)
-            src_a = ring_arr[(pos - step) % chips] * 2 + core
-            src_b = ring_arr[(pos + step) % chips] * 2 + core
+            src_a = chip_at((pos - step) % chips) * 2 + core
+            src_b = chip_at((pos + step) % chips) * 2 + core
             mate_a = lax.ppermute(cur_a, "seq", swap)
             mate_b = lax.ppermute(cur_b, "seq", swap)
             got_a += [cur_a, mate_a]
@@ -78,32 +77,34 @@
         cut = heads_a * HEAD
         scale_factor = 1.0 / math.sqrt(HEAD)
         me = lax.axis_index("seq")
-        pairs = lax.all_gather(jnp.concatenate([valid_count, assignment]), "seq", axis=0, tiled=False)
-        counts_all, blocks_all = pairs[:, 0], pairs[:, 1]
-        columns = jnp.arange(n_seq, dtype=jnp.int32)
-        dev_counts = jnp.sum(
-            jnp.where(blocks_all[:, None] == columns[None, :], counts_all[None, :], 0), axis=1
+        info = jnp.zeros((1, 2 * cut), jnp.float32)
+        info = info.at[0, 0].set(valid_count[0].astype(jnp.float32))
+        info = info.at[0, 1].set(assignment[0].astype(jnp.float32))
+        packet_a = jnp.concatenate(
+            [jnp.concatenate([key_rows[:, :cut], value_rows[:, :cut]], axis=1), info.astype(jnp.bfloat16)],
+            axis=0,
         )
-
-        packet_a = jnp.concatenate([key_rows[:, :cut], value_rows[:, :cut]], axis=1)
         packet_b = jnp.concatenate([key_rows[:, cut:], value_rows[:, cut:]], axis=1)
         got_a, got_b, ids_a, ids_b = gather_ring(packet_a, packet_b, me)
+        extra = jnp.stack([g[rows_dev, :2] for g in got_a]).astype(jnp.float32).astype(jnp.int32)
+        counts_of, blocks_of = extra[:, 0], extra[:, 1]
+        limit_a = jnp.sum(
+            jnp.where(blocks_of[:, None] == ids_a[None, :], counts_of[None, :], 0), axis=1
+        )
+        limit_b = jnp.sum(jnp.where(ids_b[:, None] == ids_a[None, :], limit_a[None, :], 0), axis=1)
         within = jnp.arange(rows_dev, dtype=jnp.int32)
 
-        def half(got, ids, lo, hi):
+        def half(got, limits, lo, hi):
             width = (hi - lo) * HEAD
-            stack = jnp.concatenate(got, axis=0)
+            stack = jnp.concatenate([g[:rows_dev] for g in got], axis=0)
             keys = stack[:, :width].reshape(-1, hi - lo, HEAD)
             values = stack[:, width:].reshape(-1, hi - lo, HEAD)
-            limits = jnp.sum(
-                jnp.where(ids[:, None] == columns[None, :], dev_counts[None, :], 0), axis=1
-            )
             keeping = (within[None, :] < limits[:, None]).reshape(-1)
             q3 = queries[:, lo * HEAD : hi * HEAD].reshape(rows_dev, hi - lo, HEAD)
             return attend_all(q3, keys, values, keeping, scale_factor)
 
         attention = jnp.concatenate(
-            [half(got_a, ids_a, 0, heads_a), half(got_b, ids_b, heads_a, heads_here)], axis=1
+            [half(got_a, limit_a, 0, heads_a), half(got_b, limit_b, heads_a, heads_here)], axis=1
         )
         partial = jnp.dot(attention, out_weight, preferred_element_type=jnp.float32)
         rows_out = hidden.shape[0]

time: 182 us -> 164 us (0.901)
  between operations: 22.9 us -> 2.77 us
  blocking collectives: 11.4 us -> 0 us
  local copies, waits for them, and re-layouts: 36 us -> 45.1 us
  other arithmetic: 4.58 us -> 8.35 us
  waiting for transfers between devices: 60.1 us -> 62.4 us
  starting transfers between devices: 23 us -> 21.1 us
    unnamed x1 -> x0, blocking collectives: 11.4 us -> none
    slice x3 -> x18, local copies, waits for them, and re-layouts: 2.24 us -> 9.76 us  [the longest x16 7.73 us: on_device(): g[rows_dev, :2]]
    ppermute x7, waiting for transfers between devices: 12.5 us -> 18.6 us  [gather_ring(): cur_b = lax.ppermute(cur_b, 'seq', backward)]
    ppermute x7, waiting for transfers between devices: 32.3 us -> 28.2 us  [gather_ring(): cur_a = lax.ppermute(cur_a, 'seq', forward)]
    another operation x0 -> x3, other arithmetic: none -> 2.96 us
  transfers between devices with their start and end apart: 31 -> 31, of which waited for: 9 -> 10; matrix products, arithmetic and copies ran while one was open for 15% -> 14% of each run, Pallas kernels for 0% -> 0%
where the time goes in v2:
time: 164 us; the launch traced here: 162 us
  waiting for transfers between devices  62.4 us (38%)
  local copies, waits for them, and re-layouts  45.1 us (28%)
  matrix products  22.3 us (14%)
  starting transfers between devices  21.1 us (13%)
  other arithmetic  8.35 us (5%)
  between operations  2.77 us (2%)
    ppermute x7, waiting for transfers between devices, gather_ring(): cur_a = lax.ppermute(cur_a, 'seq', forward)  28.2 us
    ppermute x7, waiting for transfers between devices, gather_ring(): cur_b = lax.ppermute(cur_b, 'seq', backward)  18.6 us
    concatenate x2, local copies, waits for them, and re-layouts, half(): stack = jnp.concatenate([g[:rows_dev] for g in got], axis=0)  17.3 us
    ppermute x1, waiting for transfers between devices, on_device(): came = lax.ppermute(other, 'tp', [(0, 1), (1, 0)])  15.6 us
    ppermute x7, starting transfers between devices, gather_ring(): cur_a = lax.ppermute(cur_a, 'seq', forward)  12.8 us
    sub x2, matrix products, attend_all(): weights = jnp.where(keeping[None, None, :], jnp.exp(masked - peak), 0.0)  9.9 us
    slice x2, local copies, waits for them, and re-layouts, half(): keys = stack[:, :width].reshape(-1, hi - lo, HEAD)  9.24 us
    slice x16, local copies, waits for them, and re-layouts, on_device(): g[rows_dev, :2]  7.73 us
  transfers between devices with their start and end apart: 31, of which 10 were waited for; matrix products, arithmetic and copies ran while one was open for 14% of the time, Pallas kernels for 0%

profile of v2, /device:TPU:0, one launch (start us, length us, event | category | flops | bytes accessed | tf_op | source)
XLA Modules:
  0.0 162.1 jit_solution(11498063145289746004)
XLA Ops:
  0.0 0.6 compare_reduce_fusion.1
  0.6 0.6 compare_reduce_fusion
  1.9 0.6 slice.164
  3.9 1.0 fusion.59
  5.1 1.0 fusion.60
  6.3 1.7 %fusion.61 = bf16[1,1]{0,1:T(2,128)(2,1)} fusion(pred[1,1]{0,1:T(4,128)(4,1)} %bitcast.2, bf16[1,1]{0,1:T(2,128)(2,1)} %bitcast.3, s32[]{:T(128)} %bitcast.4, bf16[1,1]{0,1:T(2,128)(2,1)} %bitcast.1), kind=kLoop, calls=%fused_computation.65 | loop fusion | flops 1 | bytes 11 | tf_op jit(solution)/shard_map/select.3
  8.0 1.3 scatter.9
  9.3 0.9 pad_maximum_fusion.1
  10.2 3.0 %collective-permute-start.1 = (bf16[121,1280]{0,1:T(8,128)(2,1)}, bf16[121,1280]{0,1:T(8,128)(2,1)S(1)}, u32[]{:S(2)}, u32[]{:S(2)}) collective-permute-start(bf16[121,1280]{0,1:T(8,128)(2,1)} %pad_maximum_fusion.1), channel_id=1, source_target_pairs={{0,8},{2,10},{8,16},{10,18},{16,24},{18,26},{24,28},{26,30},{28,20... | collective-permute-start | bytes 929288 | tf_op jit(solution)/shard_map/ppermute | solution.py:36
  13.7 7.4 %collective-permute-done.1 = bf16[121,1280]{0,1:T(8,128)(2,1)S(1)} collective-permute-done((bf16[121,1280]{0,1:T(8,128)(2,1)}, bf16[121,1280]{0,1:T(8,128)(2,1)S(1)}, u32[]{:S(2)}, u32[]{:S(2)}) %collective-permute-start.1) | collective-permute-done | bytes 309792 | tf_op jit(solution)/shard_map/ppermute | solution.py:36
  21.1 1.8 %collective-permute-start.3 = (bf16[121,1280]{0,1:T(8,128)(2,1)S(1)}, bf16[121,1280]{0,1:T(8,128)(2,1)S(1)}, u32[]{:S(2)}, u32[]{:S(2)}) collective-permute-start(bf16[121,1280]{0,1:T(8,128)(2,1)S(1)} %collective-permute-done.1), channel_id=1, source_target_pairs={{0,8},{2,10},{8,16},{10,18},{16,24},{18,26},{24,28},{26,30},{28,20... | collective-permute-start | bytes 929288 | tf_op jit(solution)/shard_map/ppermute | solution.py:36
  22.9 0.3 collective-permute-start.18
  23.1 6.8 %collective-permute-done.3 = bf16[121,1280]{0,1:T(8,128)(2,1)S(1)} collective-permute-done((bf16[121,1280]{0,1:T(8,128)(2,1)S(1)}, bf16[121,1280]{0,1:T(8,128)(2,1)S(1)}, u32[]{:S(2)}, u32[]{:S(2)}) %collective-permute-start.3) | collective-permute-done | bytes 309792 | tf_op jit(solution)/shard_map/ppermute | solution.py:36
  29.9 1.5 collective-permute-start.5
  31.4 0.5 collective-permute-start.20
  32.0 5.9 %collective-permute-done.5 = bf16[121,1280]{0,1:T(8,128)(2,1)S(1)} collective-permute-done((bf16[121,1280]{0,1:T(8,128)(2,1)S(1)}, bf16[121,1280]{0,1:T(8,128)(2,1)S(1)}, u32[]{:S(2)}, u32[]{:S(2)}) %collective-permute-start.5) | collective-permute-done | bytes 309792 | tf_op jit(solution)/shard_map/ppermute | solution.py:36
  37.9 1.4 collective-permute-start.7
  39.3 0.6 collective-permute-start.22
  40.2 5.6 %collective-permute-done.7 = bf16[121,1280]{0,1:T(8,128)(2,1)S(1)} collective-permute-done((bf16[121,1280]{0,1:T(8,128)(2,1)S(1)}, bf16[121,1280]{0,1:T(8,128)(2,1)S(1)}, u32[]{:S(2)}, u32[]{:S(2)}) %collective-permute-start.7) | collective-permute-done | bytes 309792 | tf_op jit(solution)/shard_map/ppermute | solution.py:36
  45.8 1.9 %collective-permute-start.9 = (bf16[121,1280]{0,1:T(8,128)(2,1)S(1)}, bf16[121,1280]{0,1:T(8,128)(2,1)S(1)}, u32[]{:S(2)}, u32[]{:S(2)}) collective-permute-start(bf16[121,1280]{0,1:T(8,128)(2,1)S(1)} %collective-permute-done.7), channel_id=1, source_target_pairs={{0,8},{2,10},{8,16},{10,18},{16,24},{18,26},{24,28},{26,30},{28,20... | collective-permute-start | bytes 929288 | tf_op jit(solution)/shard_map/ppermute | solution.py:36
  47.7 0.5 collective-permute-start.17
  48.2 1.6 collective-permute-done.22
  49.8 0.6 collective-permute-start.24
  50.5 2.4 %collective-permute-done.9 = bf16[121,1280]{0,1:T(8,128)(2,1)S(1)} collective-permute-done((bf16[121,1280]{0,1:T(8,128)(2,1)S(1)}, bf16[121,1280]{0,1:T(8,128)(2,1)S(1)}, u32[]{:S(2)}, u32[]{:S(2)}) %collective-permute-start.9) | collective-permute-done | bytes 309792 | tf_op jit(solution)/shard_map/ppermute | solution.py:36
  52.9 1.9 %collective-permute-start.11 = (bf16[121,1280]{0,1:T(8,128)(2,1)S(1)}, bf16[121,1280]{0,1:T(8,128)(2,1)S(1)}, u32[]{:S(2)}, u32[]{:S(2)}) collective-permute-start(bf16[121,1280]{0,1:T(8,128)(2,1)S(1)} %collective-permute-done.9), channel_id=1, source_target_pairs={{0,8},{2,10},{8,16},{10,18},{16,24},{18,26},{24,28},{26,30},{28,20... | collective-permute-start | bytes 929288 | tf_op jit(solution)/shard_map/ppermute | solution.py:36
  54.8 0.5 collective-permute-start.19
  55.3 4.1 %collective-permute-done.24 = bf16[120,1280]{0,1:T(8,128)(2,1)} collective-permute-done((bf16[120,1280]{0,1:T(8,128)(2,1)}, bf16[120,1280]{0,1:T(8,128)(2,1)}, u32[]{:S(2)}, u32[]{:S(2)}) %collective-permute-start.24) | collective-permute-done | bytes 307232 | tf_op jit(solution)/shard_map/ppermute | solution.py:37
  59.4 0.6 collective-permute-start.26
  60.1 0.5 collective-permute-start.10
  60.6 1.4 collective-permute-start.13
  62.0 6.2 %collective-permute-done.26 = bf16[120,1280]{0,1:T(8,128)(2,1)} collective-permute-done((bf16[120,1280]{0,1:T(8,128)(2,1)}, bf16[120,1280]{0,1:T(8,128)(2,1)}, u32[]{:S(2)}, u32[]{:S(2)}) %collective-permute-start.26) | collective-permute-done | bytes 307232 | tf_op jit(solution)/shard_map/ppermute | solution.py:37
  68.2 0.6 collective-permute-start.28
  68.9 0.5 collective-permute-start.23
  69.4 6.7 %collective-permute-done.28 = bf16[120,1280]{0,1:T(8,128)(2,1)} collective-permute-done((bf16[120,1280]{0,1:T(8,128)(2,1)}, bf16[120,1280]{0,1:T(8,128)(2,1)}, u32[]{:S(2)}, u32[]{:S(2)}) %collective-permute-start.28) | collective-permute-done | bytes 307232 | tf_op jit(solution)/shard_map/ppermute | solution.py:37
  76.0 0.5 collective-permute-start.27
  76.8 0.7 copy-done.15
  77.5 0.5 collective-permute-start.29
  78.0 1.0 fusion.58
  79.5 0.8 copy.25
  80.3 0.8 copy.32
  81.6 0.7 slice.220
  82.4 0.8 slice.222
  83.2 0.8 slice.224
  84.0 0.7 slice.227
  84.7 0.8 slice.226
  85.5 0.7 slice.229
  86.2 0.7 slice.228
  86.9 0.7 slice.231
  87.6 0.8 slice.230
  88.4 8.7 %concatenate.26 = bf16[1920,1280]{0,1:T(8,128)(2,1)} concatenate(bf16[120,1280]{0,1:T(8,128)(2,1)S(1)} %pad_maximum_fusion.2, bf16[120,1280]{0,1:T(8,128)(2,1)} %copy-done.11, bf16[120,1280]{0,1:T(8,128)(2,1)} %copy-done.5, bf16[120,1280]{0,1:T(8,128)(2,1)} %collective-permute-done.17, bf16[120,1280]{0,1:T(8,128)(2,1)} %copy-done.7, bf16[120,1280]{0,1:T(8,128)(2,1)} %collective-permute-done.19, ...), dimensions={0} | concatenate | bytes 9830400 | tf_op jit(solution)/shard_map/concatenate | solution.py:99
  97.2 4.2 %fusion.57 = (bf16[1920,640]{0,1:T(8,128)(2,1)}, bf16[1920,640]{0,1:T(8,128)(2,1)S(1)}) fusion(bf16[1920,1280]{0,1:T(8,128)(2,1)} %concatenate.26), kind=kLoop, calls=%fused_computation.61 | loop fusion | bytes 9830400 | tf_op jit(solution)/shard_map/slice | solution.py:100
  101.4 0.7 slice.232
  102.6 8.5 %concatenate.24 = bf16[1920,1280]{0,1:T(8,128)(2,1)} concatenate(bf16[120,1280]{0,1:T(8,128)(2,1)S(1)} %pad_maximum_fusion, bf16[120,1280]{0,1:T(8,128)(2,1)} %bitcast.135, bf16[120,1280]{0,1:T(8,128)(2,1)S(1)} %bitcast.131, bf16[120,1280]{0,1:T(8,128)(2,1)} %bitcast.137, bf16[120,1280]{0,1:T(8,128)(2,1)S(1)} %bitcast.132, bf16[120,1280]{0,1:T(8,128)(2,1)} %bitcast.138, ...), dimensions={0} | concatenate | bytes 9830400 | tf_op jit(solution)/shard_map/concatenate | solution.py:99
  111.2 5.0 %fusion.56 = (bf16[1920,640]{0,1:T(8,128)(2,1)}, bf16[1920,640]{0,1:T(8,128)(2,1)}) fusion(bf16[1920,1280]{0,1:T(8,128)(2,1)} %concatenate.24), kind=kLoop, calls=%fused_computation.60 | loop fusion | bytes 9830400 | tf_op jit(solution)/shard_map/slice | solution.py:100
  116.2 5.0 %fusion.63 = (f32[5,120]{1,0:T(8,128)S(1)}, bf16[5,120,1920]{2,1,0:T(8,128)(2,1)}) fusion(pred[1920]{0:T(1024)(128)(4,1)S(1)} %lt.182, bf16[1920,5,128]{0,2,1:T(8,128)(2,1)} %bitcast.128, bf16[120,5,128]{0,2,1:T(8,128)(2,1)S(1)} %bitcast.145), kind=kOutput, calls=%fused_computation.67 | convolution fusion | flops 301825920 | bytes 4919520 | tf_op jit(solution)/shard_map/sub | solution.py:58
  121.2 3.3 %fusion.37 = bf16[120,5,128]{2,0,1:T(8,128)(2,1)S(1)} fusion(bf16[1920,5,128]{0,2,1:T(8,128)(2,1)} %bitcast.127, bf16[5,120,1920]{2,1,0:T(8,128)(2,1)} %get-tuple-element.56, f32[120,5]{0,1:T(8,128)S(1)} %bitcast.147), kind=kOutput, calls=%fused_computation.33 | convolution fusion | flops 295065600 | bytes 4917600 | tf_op jit(solution)/shard_map/hqk,khd->hqd/dot_general | solution.py:60
  125.0 5.0 %fusion.62 = (f32[5,120]{1,0:T(8,128)S(1)}, bf16[5,120,1920]{2,1,0:T(8,128)(2,1)}) fusion(pred[1920]{0:T(1024)(128)(4,1)S(1)} %lt.200, bf16[1920,5,128]{0,2,1:T(8,128)(2,1)} %bitcast.126, bf16[120,5,128]{0,2,1:T(8,128)(2,1)S(1)} %bitcast.146), kind=kOutput, calls=%fused_computation.66 | convolution fusion | flops 301825920 | bytes 4919520 | tf_op jit(solution)/shard_map/sub | solution.py:58
  129.9 2.5 %fusion.40 = bf16[120,5,128]{2,0,1:T(8,128)(2,1)S(1)} fusion(bf16[1920,5,128]{0,2,1:T(8,128)(2,1)S(1)} %bitcast.125, bf16[5,120,1920]{2,1,0:T(8,128)(2,1)} %get-tuple-element.54, f32[120,5]{0,1:T(8,128)S(1)} %bitcast.148), kind=kOutput, calls=%fused_computation.34 | convolution fusion | flops 295065600 | bytes 4917600 | tf_op jit(solution)/shard_map/hqk,khd->hqd/dot_general | solution.py:60
  132.6 6.6 %fusion.43 = f32[120,5120]{1,0:T(8,128)S(1)} fusion(bf16[1280,5120]{1,0:T(8,128)(2,1)} %param.19, bf16[120,640]{0,1:T(8,128)(2,1)S(1)} %bitcast.130, bf16[120,640]{0,1:T(8,128)(2,1)S(1)} %bitcast.129), kind=kOutput, calls=%fused_computation.38 | convolution fusion | flops 1573478400 | bytes 15872000 | tf_op jit(solution)/shard_map/dot_general | solution.py:109
  139.3 1.7 %reshape.146 = f32[2,60,5120]{2,1,0:T(8,128)} reshape(f32[120,5120]{1,0:T(8,128)S(1)} %fusion.43) | data formatting | bytes 4915200 | tf_op jit(solution)/shard_map/reshape | solution.py:113
  141.0 1.4 bitcast_convert_fusion
  142.4 1.6 collective-permute-start.30
  144.0 15.6 %collective-permute-done.30 = bf16[60,5120]{1,0:T(8,128)(2,1)S(1)} collective-permute-done((bf16[60,5120]{1,0:T(8,128)(2,1)S(1)}, bf16[60,5120]{1,0:T(8,128)(2,1)S(1)}, u32[]{:S(2)}, u32[]{:S(2)}) %collective-permute-start.30) | collective-permute-done | bytes 614432 | tf_op jit(solution)/shard_map/ppermute | solution.py:116
  159.6 2.4 %fusion.24 = bf16[60,5120]{1,0:T(8,128)(2,1)} fusion(f32[2,60,5120]{2,1,0:T(8,128)} %reshape.146, s32[]{:T(128)S(6)} %select_n.209, bf16[60,5120]{1,0:T(8,128)(2,1)S(1)} %collective-permute-done.30, bf16[60,5120]{1,0:T(8,128)(2,1)S(1)} %copy-done, f32[5120]{0:T(1024)S(1)} %copy-done.18, pred[]{:T(512)S(6)} %and.115), kind=kLoop, calls=%fused_computation.28 | loop fusion | flops 2150400 | bytes 3092485 | tf_op jit(solution)/shard_map/convert_element_type | solution.py:118
  (96 shorter events, 3.3 us)
Async XLA Ops:
  10.2 10.9 %collective-permute-start.1 = (bf16[121,1280]{0,1:T(8,128)(2,1)}, bf16[121,1280]{0,1:T(8,128)(2,1)S(1)}, u32[]{:S(2)}, u32[]{:S(2)}) collective-permute-start(bf16[121,1280]{0,1:T(8,128)(2,1)} %pad_maximum_fusion.1), channel_id=1, source_target_pairs={{0,8},{2,10},{8,16},{10,18},{16,24},{18,26},{24,28},{26,30},{28,20... | collective-permute-start | bytes 929288 | tf_op jit(solution)/shard_map/ppermute | solution.py:36
  13.6 9.2 %collective-permute-start.16 = (bf16[120,1280]{0,1:T(8,128)(2,1)S(1)}, bf16[120,1280]{0,1:T(8,128)(2,1)S(1)}, u32[]{:S(2)}, u32[]{:S(2)}) collective-permute-start(bf16[120,1280]{0,1:T(8,128)(2,1)S(1)} %pad_maximum_fusion.2), channel_id=1, source_target_pairs={{8,0},{10,2},{16,8},{18,10},{24,16},{26,18},{28,24},{30,26},{20,28... | collective-permute-start | bytes 921608 | tf_op jit(solution)/shard_map/ppermute | solution.py:37
  21.1 8.9 %collective-permute-start.3 = (bf16[121,1280]{0,1:T(8,128)(2,1)S(1)}, bf16[121,1280]{0,1:T(8,128)(2,1)S(1)}, u32[]{:S(2)}, u32[]{:S(2)}) collective-permute-start(bf16[121,1280]{0,1:T(8,128)(2,1)S(1)} %collective-permute-done.1), channel_id=1, source_target_pairs={{0,8},{2,10},{8,16},{10,18},{16,24},{18,26},{24,28},{26,30},{28,20... | collective-permute-start | bytes 929288 | tf_op jit(solution)/shard_map/ppermute | solution.py:36
  22.9 53.7 %copy-start.5 = (bf16[120,1280]{0,1:T(8,128)(2,1)}, bf16[120,1280]{0,1:T(8,128)(2,1)S(1)}, u32[]{:S(2)}) copy-start(bf16[120,1280]{0,1:T(8,128)(2,1)S(1)} %collective-permute-done.16) | copy-start | bytes 921604
  22.9 8.6 %collective-permute-start.18 = (bf16[120,1280]{0,1:T(8,128)(2,1)S(1)}, bf16[120,1280]{0,1:T(8,128)(2,1)S(1)}, u32[]{:S(2)}, u32[]{:S(2)}) collective-permute-start(bf16[120,1280]{0,1:T(8,128)(2,1)S(1)} %collective-permute-done.16), channel_id=1, source_target_pairs={{8,0},{10,2},{16,8},{18,10},{24,16},{26,18},{28,24},{30,26},{20,28... | collective-permute-start | bytes 921608 | tf_op jit(solution)/shard_map/ppermute | solution.py:37
  29.9 8.0 %collective-permute-start.5 = (bf16[121,1280]{0,1:T(8,128)(2,1)S(1)}, bf16[121,1280]{0,1:T(8,128)(2,1)S(1)}, u32[]{:S(2)}, u32[]{:S(2)}) collective-permute-start(bf16[121,1280]{0,1:T(8,128)(2,1)S(1)} %collective-permute-done.3), channel_id=1, source_target_pairs={{0,8},{2,10},{8,16},{10,18},{16,24},{18,26},{24,28},{26,30},{28,20... | collective-permute-start | bytes 929288 | tf_op jit(solution)/shard_map/ppermute | solution.py:36
  31.4 45.1 %copy-start.7 = (bf16[120,1280]{0,1:T(8,128)(2,1)}, bf16[120,1280]{0,1:T(8,128)(2,1)S(1)}, u32[]{:S(2)}) copy-start(bf16[120,1280]{0,1:T(8,128)(2,1)S(1)} %collective-permute-done.18) | copy-start | bytes 921604
  31.4 7.9 %collective-permute-start.20 = (bf16[120,1280]{0,1:T(8,128)(2,1)S(1)}, bf16[120,1280]{0,1:T(8,128)(2,1)}, u32[]{:S(2)}, u32[]{:S(2)}) collective-permute-start(bf16[120,1280]{0,1:T(8,128)(2,1)S(1)} %collective-permute-done.18), channel_id=1, source_target_pairs={{8,0},{10,2},{16,8},{18,10},{24,16},{26,18},{28,24},{30,26},{20,28... | collective-permute-start | bytes 921608 | tf_op jit(solution)/shard_map/ppermute | solution.py:37
  37.9 50.5 %copy-start.1 = (bf16[121,1280]{0,1:T(8,128)(2,1)}, bf16[121,1280]{0,1:T(8,128)(2,1)S(1)}, u32[]{:S(2)}) copy-start(bf16[121,1280]{0,1:T(8,128)(2,1)S(1)} %collective-permute-done.5) | copy-start | bytes 929284
  37.9 7.9 %collective-permute-start.7 = (bf16[121,1280]{0,1:T(8,128)(2,1)S(1)}, bf16[121,1280]{0,1:T(8,128)(2,1)S(1)}, u32[]{:S(2)}, u32[]{:S(2)}) collective-permute-start(bf16[121,1280]{0,1:T(8,128)(2,1)S(1)} %collective-permute-done.5), channel_id=1, source_target_pairs={{0,8},{2,10},{8,16},{10,18},{16,24},{18,26},{24,28},{26,30},{28,20... | collective-permute-start | bytes 929288 | tf_op jit(solution)/shard_map/ppermute | solution.py:36
  39.3 8.4 %collective-permute-start.15 = (bf16[120,1280]{0,1:T(8,128)(2,1)S(1)}, bf16[120,1280]{0,1:T(8,128)(2,1)S(1)}, u32[]{:S(2)}, u32[]{:S(2)}) collective-permute-start(bf16[120,1280]{0,1:T(8,128)(2,1)S(1)} %pad_maximum_fusion.2), channel_id=1, source_target_pairs={{0,2},{2,0},{4,6},{6,4},{8,10},{10,8},{12,14},{14,12},{16,18},{18,... | collective-permute-start | bytes 921608 | tf_op jit(solution)/shard_map/ppermute | solution.py:41
  39.3 10.4 %collective-permute-start.22 = (bf16[120,1280]{0,1:T(8,128)(2,1)}, bf16[120,1280]{0,1:T(8,128)(2,1)}, u32[]{:S(2)}, u32[]{:S(2)}) collective-permute-start(bf16[120,1280]{0,1:T(8,128)(2,1)} %collective-permute-done.20), channel_id=1, source_target_pairs={{8,0},{10,2},{16,8},{18,10},{24,16},{26,18},{28,24},{30,26},{20,28... | collective-permute-start | bytes 921608 | tf_op jit(solution)/shard_map/ppermute | solution.py:37
  40.0 10.4 %collective-permute-start = (bf16[121,1280]{0,1:T(8,128)(2,1)}, bf16[121,1280]{0,1:T(8,128)(2,1)S(1)}, u32[]{:S(2)}, u32[]{:S(2)}) collective-permute-start(bf16[121,1280]{0,1:T(8,128)(2,1)} %pad_maximum_fusion.1), channel_id=1, source_target_pairs={{0,2},{2,0},{4,6},{6,4},{8,10},{10,8},{12,14},{14,12},{16,18},{18,... | collective-permute-start | bytes 929288 | tf_op jit(solution)/shard_map/ppermute | solution.py:40
  45.8 42.6 %copy-start.2 = (bf16[121,1280]{0,1:T(8,128)(2,1)}, bf16[121,1280]{0,1:T(8,128)(2,1)S(1)}, u32[]{:S(2)}) copy-start(bf16[121,1280]{0,1:T(8,128)(2,1)S(1)} %collective-permute-done.7) | copy-start | bytes 929284
  45.8 7.1 %collective-permute-start.9 = (bf16[121,1280]{0,1:T(8,128)(2,1)S(1)}, bf16[121,1280]{0,1:T(8,128)(2,1)S(1)}, u32[]{:S(2)}, u32[]{:S(2)}) collective-permute-start(bf16[121,1280]{0,1:T(8,128)(2,1)S(1)} %collective-permute-done.7), channel_id=1, source_target_pairs={{0,8},{2,10},{8,16},{10,18},{16,24},{18,26},{24,28},{26,30},{28,20... | collective-permute-start | bytes 929288 | tf_op jit(solution)/shard_map/ppermute | solution.py:36
  47.7 7.1 %collective-permute-start.2 = (bf16[121,1280]{0,1:T(8,128)(2,1)S(1)}, bf16[121,1280]{0,1:T(8,128)(2,1)S(1)}, u32[]{:S(2)}, u32[]{:S(2)}) collective-permute-start(bf16[121,1280]{0,1:T(8,128)(2,1)S(1)} %collective-permute-done.1), channel_id=1, source_target_pairs={{0,2},{2,0},{4,6},{6,4},{8,10},{10,8},{12,14},{14,12},{16,18},{18,... | collective-permute-start | bytes 929288 | tf_op jit(solution)/shard_map/ppermute | solution.py:40
  47.7 2.7 %copy-start.11 = (bf16[120,1280]{0,1:T(8,128)(2,1)}, bf16[120,1280]{0,1:T(8,128)(2,1)S(1)}, u32[]{:S(2)}) copy-start(bf16[120,1280]{0,1:T(8,128)(2,1)S(1)} %collective-permute-done.15) | copy-start | bytes 921604
  47.7 7.1 %collective-permute-start.17 = (bf16[120,1280]{0,1:T(8,128)(2,1)S(1)}, bf16[120,1280]{0,1:T(8,128)(2,1)}, u32[]{:S(2)}, u32[]{:S(2)}) collective-permute-start(bf16[120,1280]{0,1:T(8,128)(2,1)S(1)} %collective-permute-done.16), channel_id=1, source_target_pairs={{0,2},{2,0},{4,6},{6,4},{8,10},{10,8},{12,14},{14,12},{16,18},{18,... | collective-permute-start | bytes 921608 | tf_op jit(solution)/shard_map/ppermute | solution.py:41
  49.8 9.7 %collective-permute-start.24 = (bf16[120,1280]{0,1:T(8,128)(2,1)}, bf16[120,1280]{0,1:T(8,128)(2,1)}, u32[]{:S(2)}, u32[]{:S(2)}) collective-permute-start(bf16[120,1280]{0,1:T(8,128)(2,1)} %collective-permute-done.22), channel_id=1, source_target_pairs={{8,0},{10,2},{16,8},{18,10},{24,16},{26,18},{28,24},{30,26},{20,28... | collective-permute-start | bytes 921608 | tf_op jit(solution)/shard_map/ppermute | solution.py:37
  50.4 38.0 %copy-start.3 = (bf16[121,1280]{0,1:T(8,128)(2,1)}, bf16[121,1280]{0,1:T(8,128)(2,1)S(1)}, u32[]{:S(2)}) copy-start(bf16[121,1280]{0,1:T(8,128)(2,1)S(1)} %collective-permute-done) | copy-start | bytes 929284
  50.4 9.7 %collective-permute-start.4 = (bf16[121,1280]{0,1:T(8,128)(2,1)S(1)}, bf16[121,1280]{0,1:T(8,128)(2,1)S(1)}, u32[]{:S(2)}, u32[]{:S(2)}) collective-permute-start(bf16[121,1280]{0,1:T(8,128)(2,1)S(1)} %collective-permute-done.3), channel_id=1, source_target_pairs={{0,2},{2,0},{4,6},{6,4},{8,10},{10,8},{12,14},{14,12},{16,18},{18,... | collective-permute-start | bytes 929288 | tf_op jit(solution)/shard_map/ppermute | solution.py:40
  52.9 28.3 %copy-start.4 = (bf16[121,1280]{0,1:T(8,128)(2,1)}, bf16[121,1280]{0,1:T(8,128)(2,1)S(1)}, u32[]{:S(2)}) copy-start(bf16[121,1280]{0,1:T(8,128)(2,1)S(1)} %collective-permute-done.9) | copy-start | bytes 929284
  52.9 7.7 %collective-permute-start.11 = (bf16[121,1280]{0,1:T(8,128)(2,1)S(1)}, bf16[121,1280]{0,1:T(8,128)(2,1)S(1)}, u32[]{:S(2)}, u32[]{:S(2)}) collective-permute-start(bf16[121,1280]{0,1:T(8,128)(2,1)S(1)} %collective-permute-done.9), channel_id=1, source_target_pairs={{0,8},{2,10},{8,16},{10,18},{16,24},{18,26},{24,28},{26,30},{28,20... | collective-permute-start | bytes 929288 | tf_op jit(solution)/shard_map/ppermute | solution.py:36
  54.8 7.2 %collective-permute-start.6 = (bf16[121,1280]{0,1:T(8,128)(2,1)S(1)}, bf16[121,1280]{0,1:T(8,128)(2,1)S(1)}, u32[]{:S(2)}, u32[]{:S(2)}) collective-permute-start(bf16[121,1280]{0,1:T(8,128)(2,1)S(1)} %collective-permute-done.5), channel_id=1, source_target_pairs={{0,2},{2,0},{4,6},{6,4},{8,10},{10,8},{12,14},{14,12},{16,18},{18,... | collective-permute-start | bytes 929288 | tf_op jit(solution)/shard_map/ppermute | solution.py:40
  54.8 21.8 %copy-start.6 = (bf16[121,1280]{0,1:T(8,128)(2,1)}, bf16[121,1280]{0,1:T(8,128)(2,1)S(1)}, u32[]{:S(2)}) copy-start(bf16[121,1280]{0,1:T(8,128)(2,1)S(1)} %collective-permute-done.2) | copy-start | bytes 929284
  54.8 5.3 %collective-permute-start.19 = (bf16[120,1280]{0,1:T(8,128)(2,1)S(1)}, bf16[120,1280]{0,1:T(8,128)(2,1)}, u32[]{:S(2)}, u32[]{:S(2)}) collective-permute-start(bf16[120,1280]{0,1:T(8,128)(2,1)S(1)} %collective-permute-done.18), channel_id=1, source_target_pairs={{0,2},{2,0},{4,6},{6,4},{8,10},{10,8},{12,14},{14,12},{16,18},{18,... | collective-permute-start | bytes 921608 | tf_op jit(solution)/shard_map/ppermute | solution.py:41
  59.4 8.8 %collective-permute-start.26 = (bf16[120,1280]{0,1:T(8,128)(2,1)}, bf16[120,1280]{0,1:T(8,128)(2,1)}, u32[]{:S(2)}, u32[]{:S(2)}) collective-permute-start(bf16[120,1280]{0,1:T(8,128)(2,1)} %collective-permute-done.24), channel_id=1, source_target_pairs={{8,0},{10,2},{16,8},{18,10},{24,16},{26,18},{28,24},{30,26},{20,28... | collective-permute-start | bytes 921608 | tf_op jit(solution)/shard_map/ppermute | solution.py:37
  60.1 8.8 %collective-permute-start.8 = (bf16[121,1280]{0,1:T(8,128)(2,1)S(1)}, bf16[121,1280]{0,1:T(8,128)(2,1)S(1)}, u32[]{:S(2)}, u32[]{:S(2)}) collective-permute-start(bf16[121,1280]{0,1:T(8,128)(2,1)S(1)} %collective-permute-done.7), channel_id=1, source_target_pairs={{0,2},{2,0},{4,6},{6,4},{8,10},{10,8},{12,14},{14,12},{16,18},{18,... | collective-permute-start | bytes 929288 | tf_op jit(solution)/shard_map/ppermute | solution.py:40
  60.1 16.5 %copy-start.8 = (bf16[121,1280]{0,1:T(8,128)(2,1)}, bf16[121,1280]{0,1:T(8,128)(2,1)S(1)}, u32[]{:S(2)}) copy-start(bf16[121,1280]{0,1:T(8,128)(2,1)S(1)} %collective-permute-done.4) | copy-start | bytes 929284
  60.1 8.8 %collective-permute-start.10 = (bf16[121,1280]{0,1:T(8,128)(2,1)S(1)}, bf16[121,1280]{0,1:T(8,128)(2,1)S(1)}, u32[]{:S(2)}, u32[]{:S(2)}) collective-permute-start(bf16[121,1280]{0,1:T(8,128)(2,1)S(1)} %collective-permute-done.9), channel_id=1, source_target_pairs={{0,2},{2,0},{4,6},{6,4},{8,10},{10,8},{12,14},{14,12},{16,18},{18,... | collective-permute-start | bytes 929288 | tf_op jit(solution)/shard_map/ppermute | solution.py:40
  60.6 16.0 %copy-start.9 = (bf16[121,1280]{0,1:T(8,128)(2,1)}, bf16[121,1280]{0,1:T(8,128)(2,1)S(1)}, u32[]{:S(2)}) copy-start(bf16[121,1280]{0,1:T(8,128)(2,1)S(1)} %collective-permute-done.11) | copy-start | bytes 929284
  60.6 15.4 %collective-permute-start.13 = (bf16[121,1280]{0,1:T(8,128)(2,1)S(1)}, bf16[121,1280]{0,1:T(8,128)(2,1)S(1)}, u32[]{:S(2)}, u32[]{:S(2)}) collective-permute-start(bf16[121,1280]{0,1:T(8,128)(2,1)S(1)} %collective-permute-done.11), channel_id=1, source_target_pairs={{0,8},{2,10},{8,16},{10,18},{16,24},{18,26},{24,28},{26,30},{28,20... | collective-permute-start | bytes 929288 | tf_op jit(solution)/shard_map/ppermute | solution.py:36
  62.0 14.6 %copy-start.10 = (bf16[121,1280]{0,1:T(8,128)(2,1)}, bf16[121,1280]{0,1:T(8,128)(2,1)S(1)}, u32[]{:S(2)}) copy-start(bf16[121,1280]{0,1:T(8,128)(2,1)S(1)} %collective-permute-done.6) | copy-start | bytes 929284
  62.0 14.6 %collective-permute-start.12 = (bf16[121,1280]{0,1:T(8,128)(2,1)S(1)}, bf16[121,1280]{0,1:T(8,128)(2,1)S(1)}, u32[]{:S(2)}, u32[]{:S(2)}) collective-permute-start(bf16[121,1280]{0,1:T(8,128)(2,1)S(1)} %collective-permute-done.11), channel_id=1, source_target_pairs={{0,2},{2,0},{4,6},{6,4},{8,10},{10,8},{12,14},{14,12},{16,18},{18,... | collective-permute-start | bytes 929288 | tf_op jit(solution)/shard_map/ppermute | solution.py:40
  68.2 7.8 %collective-permute-start.28 = (bf16[120,1280]{0,1:T(8,128)(2,1)}, bf16[120,1280]{0,1:T(8,128)(2,1)}, u32[]{:S(2)}, u32[]{:S(2)}) collective-permute-start(bf16[120,1280]{0,1:T(8,128)(2,1)} %collective-permute-done.26), channel_id=1, source_target_pairs={{8,0},{10,2},{16,8},{18,10},{24,16},{26,18},{28,24},{30,26},{20,28... | collective-permute-start | bytes 921608 | tf_op jit(solution)/shard_map/ppermute | solution.py:37
  68.8 7.8 %copy-start.12 = (bf16[121,1280]{0,1:T(8,128)(2,1)}, bf16[121,1280]{0,1:T(8,128)(2,1)S(1)}, u32[]{:S(2)}) copy-start(bf16[121,1280]{0,1:T(8,128)(2,1)S(1)} %collective-permute-done.8) | copy-start | bytes 929284
  68.8 19.5 %collective-permute-start.21 = (bf16[120,1280]{0,1:T(8,128)(2,1)}, bf16[120,1280]{0,1:T(8,128)(2,1)}, u32[]{:S(2)}, u32[]{:S(2)}) collective-permute-start(bf16[120,1280]{0,1:T(8,128)(2,1)} %collective-permute-done.20), channel_id=1, source_target_pairs={{0,2},{2,0},{4,6},{6,4},{8,10},{10,8},{12,14},{14,12},{16,18},{18,... | collective-permute-start | bytes 921608 | tf_op jit(solution)/shard_map/ppermute | solution.py:41
  68.8 7.8 %copy-start.13 = (bf16[121,1280]{0,1:T(8,128)(2,1)}, bf16[121,1280]{0,1:T(8,128)(2,1)S(1)}, u32[]{:S(2)}) copy-start(bf16[121,1280]{0,1:T(8,128)(2,1)S(1)} %collective-permute-done.10) | copy-start | bytes 929284
  68.9 19.5 %collective-permute-start.23 = (bf16[120,1280]{0,1:T(8,128)(2,1)}, bf16[120,1280]{0,1:T(8,128)(2,1)}, u32[]{:S(2)}, u32[]{:S(2)}) collective-permute-start(bf16[120,1280]{0,1:T(8,128)(2,1)} %collective-permute-done.22), channel_id=1, source_target_pairs={{0,2},{2,0},{4,6},{6,4},{8,10},{10,8},{12,14},{14,12},{16,18},{18,... | collective-permute-start | bytes 921608 | tf_op jit(solution)/shard_map/ppermute | solution.py:41
  76.0 12.4 %collective-permute-start.25 = (bf16[120,1280]{0,1:T(8,128)(2,1)}, bf16[120,1280]{0,1:T(8,128)(2,1)}, u32[]{:S(2)}, u32[]{:S(2)}) collective-permute-start(bf16[120,1280]{0,1:T(8,128)(2,1)} %collective-permute-done.24), channel_id=1, source_target_pairs={{0,2},{2,0},{4,6},{6,4},{8,10},{10,8},{12,14},{14,12},{16,18},{18,... | collective-permute-start | bytes 921608 | tf_op jit(solution)/shard_map/ppermute | solution.py:41
  76.0 0.7 copy-start.14
  76.0 12.4 %collective-permute-start.27 = (bf16[120,1280]{0,1:T(8,128)(2,1)}, bf16[120,1280]{0,1:T(8,128)(2,1)}, u32[]{:S(2)}, u32[]{:S(2)}) collective-permute-start(bf16[120,1280]{0,1:T(8,128)(2,1)} %collective-permute-done.26), channel_id=1, source_target_pairs={{0,2},{2,0},{4,6},{6,4},{8,10},{10,8},{12,14},{14,12},{16,18},{18,... | collective-permute-start | bytes 921608 | tf_op jit(solution)/shard_map/ppermute | solution.py:41
  76.8 0.7 copy-start.15
  77.5 10.9 %collective-permute-start.29 = (bf16[120,1280]{0,1:T(8,128)(2,1)}, bf16[120,1280]{0,1:T(8,128)(2,1)}, u32[]{:S(2)}, u32[]{:S(2)}) collective-permute-start(bf16[120,1280]{0,1:T(8,128)(2,1)} %collective-permute-done.28), channel_id=1, source_target_pairs={{0,2},{2,0},{4,6},{6,4},{8,10},{10,8},{12,14},{14,12},{16,18},{18,... | collective-permute-start | bytes 921608 | tf_op jit(solution)/shard_map/ppermute | solution.py:41
  88.4 13.0 %collective-permute-start.14 = (bf16[121,1280]{0,1:T(8,128)(2,1)}, bf16[121,1280]{0,1:T(8,128)(2,1)}, u32[]{:S(2)}, u32[]{:S(2)}) collective-permute-start(bf16[121,1280]{0,1:T(8,128)(2,1)} %copy-done.14), channel_id=1, source_target_pairs={{0,2},{2,0},{4,6},{6,4},{8,10},{10,8},{12,14},{14,12},{16,18},{18,... | collective-permute-start | bytes 929288 | tf_op jit(solution)/shard_map/ppermute | solution.py:40
  111.2 5.0 %copy-start.16 = (bf16[120,640]{0,1:T(8,128)(2,1)S(1)}, bf16[120,640]{0,1:T(8,128)(2,1)}, u32[]{:S(2)}) copy-start(bf16[120,640]{0,1:T(8,128)(2,1)} %copy.25) | copy-start | bytes 460804
  121.2 3.8 %copy-start.17 = (bf16[120,640]{0,1:T(8,128)(2,1)S(1)}, bf16[120,640]{0,1:T(8,128)(2,1)}, u32[]{:S(2)}) copy-start(bf16[120,640]{0,1:T(8,128)(2,1)} %copy.32) | copy-start | bytes 460804
  139.3 20.4 %copy-start = (bf16[60,5120]{1,0:T(8,128)(2,1)S(1)}, bf16[60,5120]{1,0:T(8,128)(2,1)}, u32[]{:S(2)}) copy-start(bf16[60,5120]{1,0:T(8,128)(2,1)} %param.14) | copy-start | bytes 1843204
  139.3 20.3 %copy-start.18 = (f32[5120]{0:T(1024)S(1)}, f32[5120]{0:T(1024)}, u32[]{:S(2)}) copy-start(f32[5120]{0:T(1024)} %param.18) | copy-start | bytes 61444
  142.4 17.2 %collective-permute-start.30 = (bf16[60,5120]{1,0:T(8,128)(2,1)S(1)}, bf16[60,5120]{1,0:T(8,128)(2,1)S(1)}, u32[]{:S(2)}, u32[]{:S(2)}) collective-permute-start(bf16[60,5120]{1,0:T(8,128)(2,1)S(1)} %bitcast_convert_fusion), channel_id=1, source_target_pairs={{0,1},{1,0},{2,3},{3,2},{4,5},{5,4},{6,7},{7,6},{8,9},{9,8},{10,11... | collective-permute-start | bytes 1843208 | tf_op jit(solution)/shard_map/ppermute | solution.py:116

commit v3 on v2

--- a/solution.py
+++ b/solution.py
@@ -48,7 +48,7 @@
     return gather_ring
 
 
-def attend_all(queries_3d, keys, values, keeping, scale_factor):
+def attend_part(queries_3d, keys, values, keeping, scale_factor):
     scores = (
         jnp.einsum("qhd,khd->hqk", queries_3d, keys, preferred_element_type=jnp.float32)
         * scale_factor
@@ -60,8 +60,21 @@
     summed = jnp.einsum(
         "hqk,khd->hqd", weights.astype(jnp.bfloat16), values, preferred_element_type=jnp.float32
     )
+    return peak, totals, summed
+
+
+def combine(parts, rows_dev):
+    peak = parts[0][0]
+    for part in parts[1:]:
+        peak = jnp.maximum(peak, part[0])
+    totals = 0.0
+    summed = 0.0
+    for part_peak, part_totals, part_summed in parts:
+        factor = jnp.exp(part_peak - peak)
+        totals = totals + factor * part_totals
+        summed = summed + factor * part_summed
     result = (summed / totals).astype(jnp.bfloat16)
-    return result.transpose(1, 0, 2).reshape(queries_3d.shape[0], -1)
+    return result.transpose(1, 0, 2).reshape(rows_dev, -1)
 
 
 def solution(mesh):
@@ -80,28 +93,43 @@
         info = jnp.zeros((1, 2 * cut), jnp.float32)
         info = info.at[0, 0].set(valid_count[0].astype(jnp.float32))
         info = info.at[0, 1].set(assignment[0].astype(jnp.float32))
+        info = info.astype(jnp.bfloat16)
         packet_a = jnp.concatenate(
-            [jnp.concatenate([key_rows[:, :cut], value_rows[:, :cut]], axis=1), info.astype(jnp.bfloat16)],
-            axis=0,
+            [jnp.concatenate([key_rows[:, :cut], value_rows[:, :cut]], axis=1), info], axis=0
         )
-        packet_b = jnp.concatenate([key_rows[:, cut:], value_rows[:, cut:]], axis=1)
+        packet_b = jnp.concatenate(
+            [jnp.concatenate([key_rows[:, cut:], value_rows[:, cut:]], axis=1), info], axis=0
+        )
         got_a, got_b, ids_a, ids_b = gather_ring(packet_a, packet_b, me)
-        extra = jnp.stack([g[rows_dev, :2] for g in got_a]).astype(jnp.float32).astype(jnp.int32)
+        chips = n_seq // 2
+        known = chips // 2
+        seen = 2 * (known + 1)
+        heard = got_a[:seen] + got_b[:seen]
+        heard_ids = jnp.concatenate([ids_a[:seen], ids_b[:seen]])
+        extra = jnp.stack([g[rows_dev, :2] for g in heard]).astype(jnp.float32).astype(jnp.int32)
         counts_of, blocks_of = extra[:, 0], extra[:, 1]
-        limit_a = jnp.sum(
-            jnp.where(blocks_of[:, None] == ids_a[None, :], counts_of[None, :], 0), axis=1
-        )
-        limit_b = jnp.sum(jnp.where(ids_b[:, None] == ids_a[None, :], limit_a[None, :], 0), axis=1)
+
+        def limits_for(ids):
+            clip = jnp.max(jnp.where(ids[:, None] == heard_ids[None, :], blocks_of[None, :], -1), axis=1)
+            return jnp.max(jnp.where(clip[:, None] == heard_ids[None, :], counts_of[None, :], -1), axis=1)
+
+        limit_a = limits_for(ids_a)
+        limit_b = limits_for(ids_b)
         within = jnp.arange(rows_dev, dtype=jnp.int32)
+        phases = [(0, known + 1), (known + 1, chips - 1), (chips - 1, chips)]
+        phases = [(2 * lo, 2 * hi) for lo, hi in phases if hi > lo]
 
         def half(got, limits, lo, hi):
             width = (hi - lo) * HEAD
-            stack = jnp.concatenate([g[:rows_dev] for g in got], axis=0)
-            keys = stack[:, :width].reshape(-1, hi - lo, HEAD)
-            values = stack[:, width:].reshape(-1, hi - lo, HEAD)
-            keeping = (within[None, :] < limits[:, None]).reshape(-1)
             q3 = queries[:, lo * HEAD : hi * HEAD].reshape(rows_dev, hi - lo, HEAD)
-            return attend_all(q3, keys, values, keeping, scale_factor)
+            parts = []
+            for first, last in phases:
+                stack = jnp.concatenate([g[:rows_dev] for g in got[first:last]], axis=0)
+                keys = stack[:, :width].reshape(-1, hi - lo, HEAD)
+                values = stack[:, width:].reshape(-1, hi - lo, HEAD)
+                keeping = (within[None, :] < limits[first:last, None]).reshape(-1)
+                parts.append(attend_part(q3, keys, values, keeping, scale_factor))
+            return combine(parts, rows_dev)
 
         attention = jnp.concatenate(
             [half(got_a, limit_a, 0, heads_a), half(got_b, limit_b, heads_a, heads_here)], axis=1

time: 164 us -> 144 us (0.88)
  waiting for transfers between devices: 62.4 us -> 50.9 us
  other arithmetic: 8.35 us -> 17.4 us
  local copies, waits for them, and re-layouts: 45.1 us -> 36.8 us
  matrix products: 22.3 us -> 15.5 us
  starting transfers between devices: 21.1 us -> 19.3 us
    ppermute x7, waiting for transfers between devices: 18.6 us -> 2.64 us  [gather_ring(): cur_b = lax.ppermute(cur_b, 'seq', backward)]
    sub x2 -> x0, matrix products: 9.9 us -> none  [attend_all(): weights = jnp.where(keeping[None, None, :], jnp.exp(masked - peak), 0.0)]
    concatenate x1 -> x5, other arithmetic: 0.07 us -> 6.47 us  [the longest x4 5.68 us: half(): stack = jnp.concatenate([g[:rows_dev] for g in got[first:last]], axis=0)]
    concatenate x2 -> x3, local copies, waits for them, and re-layouts: 17.3 us -> 10.9 us  [the longest x2 10.8 us: half(): stack = jnp.concatenate([g[:rows_dev] for g in got[first:last]], axis=0)]
    slice x2, local copies, waits for them, and re-layouts: 9.24 us -> 3.34 us  [half(): keys = stack[:, :width].reshape(-1, hi - lo, HEAD)]
    ppermute x7, waiting for transfers between devices: 28.2 us -> 32.6 us  [gather_ring(): cur_a = lax.ppermute(cur_a, 'seq', forward)]
    dot_general x2 -> x12, matrix products: 5.76 us -> 8.82 us  [the longest x6 4.95 us: attend_part(): jnp.einsum('hqk,khd->hqd', weights.astype(jnp.bfloat16), values, preferre...]
    reduce_sum x2 -> x6, other arithmetic: 0.36 us -> 2.16 us  [attend_part(): totals = jnp.sum(weights, axis=2, keepdims=True)]
  transfers between devices with their start and end apart: 31 -> 31, of which waited for: 10 -> 9; matrix products, arithmetic and copies ran while one was open for 14% -> 30% of each run, Pallas kernels for 0% -> 0%
where the time goes in v3:
time: 144 us; the launch traced here: 143 us
  waiting for transfers between devices  50.9 us (35%)
  local copies, waits for them, and re-layouts  36.8 us (26%)
  starting transfers between devices  19.3 us (13%)
  other arithmetic  17.4 us (12%)
  matrix products  15.5 us (11%)
  between operations  2.92 us (2%)
    ppermute x7, waiting for transfers between devices, gather_ring(): cur_a = lax.ppermute(cur_a, 'seq', forward)  32.6 us
    ppermute x1, waiting for transfers between devices, on_device(): came = lax.ppermute(other, 'tp', [(0, 1), (1, 0)])  15.7 us
    ppermute x7, starting transfers between devices, gather_ring(): cur_a = lax.ppermute(cur_a, 'seq', forward)  12.3 us
    concatenate x2, local copies, waits for them, and re-layouts, half(): stack = jnp.concatenate([g[:rows_dev] for g in got[first:last]], axis=0)  10.8 us
    slice x19, local copies, waits for them, and re-layouts, on_device(): g[rows_dev, :2]  8.62 us
    dot_general x1, matrix products, on_device(): partial = jnp.dot(attention, out_weight, preferred_element_type=jnp.float32)  6.65 us
    concatenate x4, other arithmetic, half(): stack = jnp.concatenate([g[:rows_dev] for g in got[first:last]], axis=0)  5.68 us
    dot_general x6, matrix products, attend_part(): jnp.einsum('hqk,khd->hqd', weights.astype(jnp.bfloat16), values, preferre...  4.95 us
  transfers between devices with their start and end apart: 31, of which 9 were waited for; matrix products, arithmetic and copies ran while one was open for 30% of the time, Pallas kernels for 0%

profile of v3, /device:TPU:0, one launch (start us, length us, event | category | flops | bytes accessed | tf_op | source)
XLA Modules:
  0.0 142.8 jit_solution(610524204851194261)
XLA Ops:
  0.0 0.6 compare_reduce_fusion.1
  0.6 0.7 compare_reduce_fusion
  2.0 0.6 slice.265
  3.9 1.0 fusion.111
  5.1 1.0 fusion.112
  6.6 1.7 %fusion.113 = bf16[1,1]{0,1:T(2,128)(2,1)} fusion(pred[1,1]{0,1:T(4,128)(4,1)} %bitcast.26, bf16[1,1]{0,1:T(2,128)(2,1)} %bitcast.27, s32[]{:T(128)} %bitcast.28, bf16[1,1]{0,1:T(2,128)(2,1)} %bitcast.25), kind=kLoop, calls=%fused_computation.156 | loop fusion | flops 1 | bytes 11 | tf_op jit(solution)/shard_map/select.3
  8.3 1.2 scatter.9
  9.8 3.1 %collective-permute-start.1 = (bf16[121,1280]{0,1:T(8,128)(2,1)S(1)}, bf16[121,1280]{0,1:T(8,128)(2,1)S(1)}, u32[]{:S(2)}, u32[]{:S(2)}) collective-permute-start(bf16[121,1280]{0,1:T(8,128)(2,1)S(1)} %get-tuple-element.65), channel_id=1, source_target_pairs={{0,8},{2,10},{8,16},{10,18},{16,24},{18,26},{24,28},{26,30},{28,20... | collective-permute-start | bytes 929288 | tf_op jit(solution)/shard_map/ppermute | solution.py:36
  12.9 7.6 %collective-permute-done.1 = bf16[121,1280]{0,1:T(8,128)(2,1)S(1)} collective-permute-done((bf16[121,1280]{0,1:T(8,128)(2,1)S(1)}, bf16[121,1280]{0,1:T(8,128)(2,1)S(1)}, u32[]{:S(2)}, u32[]{:S(2)}) %collective-permute-start.1) | collective-permute-done | bytes 309792 | tf_op jit(solution)/shard_map/ppermute | solution.py:36
  20.6 1.8 %collective-permute-start.3 = (bf16[121,1280]{0,1:T(8,128)(2,1)S(1)}, bf16[121,1280]{0,1:T(8,128)(2,1)S(1)}, u32[]{:S(2)}, u32[]{:S(2)}) collective-permute-start(bf16[121,1280]{0,1:T(8,128)(2,1)S(1)} %collective-permute-done.1), channel_id=1, source_target_pairs={{0,8},{2,10},{8,16},{10,18},{16,24},{18,26},{24,28},{26,30},{28,20... | collective-permute-start | bytes 929288 | tf_op jit(solution)/shard_map/ppermute | solution.py:36
  23.1 6.4 %collective-permute-done.3 = bf16[121,1280]{0,1:T(8,128)(2,1)S(1)} collective-permute-done((bf16[121,1280]{0,1:T(8,128)(2,1)S(1)}, bf16[121,1280]{0,1:T(8,128)(2,1)S(1)}, u32[]{:S(2)}, u32[]{:S(2)}) %collective-permute-start.3) | collective-permute-done | bytes 309792 | tf_op jit(solution)/shard_map/ppermute | solution.py:36
  29.5 1.5 %collective-permute-start.5 = (bf16[121,1280]{0,1:T(8,128)(2,1)S(1)}, bf16[121,1280]{0,1:T(8,128)(2,1)}, u32[]{:S(2)}, u32[]{:S(2)}) collective-permute-start(bf16[121,1280]{0,1:T(8,128)(2,1)S(1)} %collective-permute-done.3), channel_id=1, source_target_pairs={{0,8},{2,10},{8,16},{10,18},{16,24},{18,26},{24,28},{26,30},{28,20... | collective-permute-start | bytes 929288 | tf_op jit(solution)/shard_map/ppermute | solution.py:36
  31.0 0.5 collective-permute-start.14
  32.1 5.4 %collective-permute-done.5 = bf16[121,1280]{0,1:T(8,128)(2,1)} collective-permute-done((bf16[121,1280]{0,1:T(8,128)(2,1)S(1)}, bf16[121,1280]{0,1:T(8,128)(2,1)}, u32[]{:S(2)}, u32[]{:S(2)}) %collective-permute-start.5) | collective-permute-done | bytes 309792 | tf_op jit(solution)/shard_map/ppermute | solution.py:36
  37.6 1.2 collective-permute-start.7
  38.7 0.9 collective-permute-start.16
  39.6 0.8 pad_maximum_fusion.4
  41.0 4.0 %collective-permute-done.7 = bf16[121,1280]{0,1:T(8,128)(2,1)} collective-permute-done((bf16[121,1280]{0,1:T(8,128)(2,1)}, bf16[121,1280]{0,1:T(8,128)(2,1)}, u32[]{:S(2)}, u32[]{:S(2)}) %collective-permute-start.7) | collective-permute-done | bytes 309792 | tf_op jit(solution)/shard_map/ppermute | solution.py:36
  45.0 1.0 collective-permute-done.16
  45.9 1.0 fusion.110
  47.5 0.8 copy.91
  48.8 0.8 pad_maximum_fusion.5
  50.0 0.7 slice.353
  50.8 0.7 slice.362
  51.5 0.8 slice.356
  52.3 0.7 slice.355
  53.1 0.8 slice.364
  53.8 0.7 slice.358
  54.6 0.7 slice.367
  55.3 1.6 %collective-permute-start.18 = (bf16[121,1280]{0,1:T(8,128)(2,1)}, bf16[121,1280]{0,1:T(8,128)(2,1)}, u32[]{:S(2)}, u32[]{:S(2)}) collective-permute-start(bf16[121,1280]{0,1:T(8,128)(2,1)} %collective-permute-done.7), channel_id=1, source_target_pairs={{0,8},{2,10},{8,16},{10,18},{16,24},{18,26},{24,28},{26,30},{28,20... | collective-permute-start | bytes 929288 | tf_op jit(solution)/shard_map/ppermute | solution.py:36
  57.3 0.7 slice.357
  58.1 0.7 slice.366
  58.8 0.7 slice.359
  59.5 0.7 slice.368
  61.0 5.4 %concatenate.48 = bf16[1200,1280]{0,1:T(8,128)(2,1)S(1)} concatenate(bf16[120,1280]{0,1:T(8,128)(2,1)} %pad_maximum_fusion.4, bf16[120,1280]{0,1:T(8,128)(2,1)} %bitcast.308, bf16[120,1280]{0,1:T(8,128)(2,1)} %bitcast.303, bf16[120,1280]{0,1:T(8,128)(2,1)} %bitcast.310, bf16[120,1280]{0,1:T(8,128)(2,1)} %bitcast.306, bf16[120,1280]{0,1:T(8,128)(2,1)} %bitcast.311, ...), dimensions={0} | concatenate | bytes 6144000 | tf_op jit(solution)/shard_map/concatenate | solution.py:127
  66.5 1.9 %fusion.106 = (bf16[1200,640]{0,1:T(8,128)(2,1)}, bf16[1200,640]{0,1:T(8,128)(2,1)}) fusion(bf16[1200,1280]{0,1:T(8,128)(2,1)S(1)} %concatenate.48), kind=kLoop, calls=%fused_computation.149 | loop fusion | bytes 6144000 | tf_op jit(solution)/shard_map/slice | solution.py:128
  68.6 5.4 %concatenate.51 = bf16[1200,1280]{0,1:T(8,128)(2,1)S(1)} concatenate(bf16[120,1280]{0,1:T(8,128)(2,1)} %pad_maximum_fusion.5, bf16[120,1280]{0,1:T(8,128)(2,1)} %bitcast.305, bf16[120,1280]{0,1:T(8,128)(2,1)} %bitcast.302, bf16[120,1280]{0,1:T(8,128)(2,1)} %bitcast.309, bf16[120,1280]{0,1:T(8,128)(2,1)} %bitcast.304, bf16[120,1280]{0,1:T(8,128)(2,1)} %bitcast.256, ...), dimensions={0} | concatenate | bytes 6144000 | tf_op jit(solution)/shard_map/concatenate | solution.py:127
  74.0 1.4 fusion.107
  75.4 0.6 copy-done.4
  76.0 1.1 fusion.117
  77.1 1.1 fusion.114
  78.5 1.6 %collective-permute-start.20 = (bf16[121,1280]{0,1:T(8,128)(2,1)}, bf16[121,1280]{0,1:T(8,128)(2,1)}, u32[]{:S(2)}, u32[]{:S(2)}) collective-permute-start(bf16[121,1280]{0,1:T(8,128)(2,1)} %collective-permute-done.18), channel_id=1, source_target_pairs={{0,8},{2,10},{8,16},{10,18},{16,24},{18,26},{24,28},{26,30},{28,20... | collective-permute-start | bytes 929288 | tf_op jit(solution)/shard_map/ppermute | solution.py:36
  80.8 0.7 fusion.4
  81.4 7.0 %collective-permute-done.20 = bf16[121,1280]{0,1:T(8,128)(2,1)} collective-permute-done((bf16[121,1280]{0,1:T(8,128)(2,1)}, bf16[121,1280]{0,1:T(8,128)(2,1)}, u32[]{:S(2)}, u32[]{:S(2)}) %collective-permute-start.20) | collective-permute-done | bytes 309792 | tf_op jit(solution)/shard_map/ppermute | solution.py:36
  89.3 0.6 fusion.6
  90.0 1.6 %collective-permute-start.22 = (bf16[121,1280]{0,1:T(8,128)(2,1)}, bf16[121,1280]{0,1:T(8,128)(2,1)S(1)}, u32[]{:S(2)}, u32[]{:S(2)}) collective-permute-start(bf16[121,1280]{0,1:T(8,128)(2,1)} %collective-permute-done.20), channel_id=1, source_target_pairs={{0,8},{2,10},{8,16},{10,18},{16,24},{18,26},{24,28},{26,30},{28,20... | collective-permute-start | bytes 929288 | tf_op jit(solution)/shard_map/ppermute | solution.py:36
  91.6 0.7 collective-permute-start.28
  92.3 2.0 %pad_maximum_fusion = bf16[480,1280]{0,1:T(8,128)(2,1)S(1)} fusion(bf16[120,1280]{0,1:T(8,128)(2,1)} %bitcast.280, bf16[120,1280]{0,1:T(8,128)(2,1)} %bitcast.281, bf16[120,1280]{0,1:T(8,128)(2,1)} %bitcast.282, bf16[120,1280]{0,1:T(8,128)(2,1)} %bitcast.283), kind=kLoop, calls=%fused_computation.26 | loop fusion | flops 4915200 | bytes 2457600 | tf_op jit(solution)/shard_map/concatenate | solution.py:127
  94.4 1.8 %pad_maximum_fusion.1 = bf16[480,1280]{0,1:T(8,128)(2,1)S(1)} fusion(bf16[120,1280]{0,1:T(8,128)(2,1)S(1)} %bitcast.316, bf16[120,1280]{0,1:T(8,128)(2,1)} %bitcast.265, bf16[120,1280]{0,1:T(8,128)(2,1)S(1)} %bitcast.313, bf16[120,1280]{0,1:T(8,128)(2,1)} %bitcast.267), kind=kLoop, calls=%fused_computation.27 | loop fusion | flops 4915200 | bytes 2457600 | tf_op jit(solution)/shard_map/concatenate | solution.py:127
  96.8 0.9 fusion.109
  97.7 2.2 %collective-permute-done.22 = bf16[121,1280]{0,1:T(8,128)(2,1)S(1)} collective-permute-done((bf16[121,1280]{0,1:T(8,128)(2,1)}, bf16[121,1280]{0,1:T(8,128)(2,1)S(1)}, u32[]{:S(2)}, u32[]{:S(2)}) %collective-permute-start.22) | collective-permute-done | bytes 309792 | tf_op jit(solution)/shard_map/ppermute | solution.py:36
  100.4 1.7 %collective-permute-done.28 = bf16[121,1280]{0,1:T(8,128)(2,1)} collective-permute-done((bf16[121,1280]{0,1:T(8,128)(2,1)}, bf16[121,1280]{0,1:T(8,128)(2,1)}, u32[]{:S(2)}, u32[]{:S(2)}) %collective-permute-start.28) | collective-permute-done | bytes 309792 | tf_op jit(solution)/shard_map/ppermute | solution.py:37
  103.5 1.1 copy-done.1
  104.6 1.2 fusion.42
  106.3 1.1 fusion.51
  107.5 1.1 copy.104
  108.6 1.6 %pad_maximum_fusion.2 = (bf16[240,640]{0,1:T(8,128)(2,1)S(1)}, bf16[240,640]{0,1:T(8,128)(2,1)S(1)}) fusion(bf16[120,1280]{0,1:T(8,128)(2,1)} %bitcast.262, bf16[120,1280]{0,1:T(8,128)(2,1)} %bitcast.263), kind=kLoop, calls=%fused_computation.83 | loop fusion | flops 1228800 | bytes 1228800 | tf_op jit(solution)/shard_map/concatenate | solution.py:127
  110.7 1.1 fusion.48
  113.3 6.6 %fusion.71 = f32[120,5120]{1,0:T(8,128)S(1)} fusion(bf16[1280,5120]{1,0:T(8,128)(2,1)} %param.19, bf16[120,640]{0,1:T(8,128)(2,1)S(1)} %bitcast.301, bf16[120,640]{0,1:T(8,128)(2,1)S(1)} %bitcast.300), kind=kOutput, calls=%fused_computation.89 | convolution fusion | flops 1573478400 | bytes 15872000 | tf_op jit(solution)/shard_map/dot_general | solution.py:137
  120.0 1.7 %reshape.355 = f32[2,60,5120]{2,1,0:T(8,128)} reshape(f32[120,5120]{1,0:T(8,128)S(1)} %fusion.71) | data formatting | bytes 4915200 | tf_op jit(solution)/shard_map/reshape | solution.py:141
  121.7 1.5 %bitcast_convert_fusion = bf16[60,5120]{1,0:T(8,128)(2,1)S(1)} fusion(f32[2,60,5120]{2,1,0:T(8,128)} %reshape.355, s32[]{:T(128)S(6)} %select_n.269, pred[]{:T(512)S(6)} %and.116), kind=kLoop, calls=%fused_computation.28 | loop fusion | flops 307200 | bytes 1228805 | tf_op jit(solution)/shard_map/convert_element_type | solution.py:143
  123.2 1.6 %collective-permute-start.30 = (bf16[60,5120]{1,0:T(8,128)(2,1)S(1)}, bf16[60,5120]{1,0:T(8,128)(2,1)S(1)}, u32[]{:S(2)}, u32[]{:S(2)}) collective-permute-start(bf16[60,5120]{1,0:T(8,128)(2,1)S(1)} %bitcast_convert_fusion), channel_id=1, source_target_pairs={{0,1},{1,0},{2,3},{3,2},{4,5},{5,4},{6,7},{7,6},{8,9},{9,8},{10,11... | collective-permute-start | bytes 1843208 | tf_op jit(solution)/shard_map/ppermute | solution.py:144
  124.7 15.7 %collective-permute-done.30 = bf16[60,5120]{1,0:T(8,128)(2,1)S(1)} collective-permute-done((bf16[60,5120]{1,0:T(8,128)(2,1)S(1)}, bf16[60,5120]{1,0:T(8,128)(2,1)S(1)}, u32[]{:S(2)}, u32[]{:S(2)}) %collective-permute-start.30) | collective-permute-done | bytes 614432 | tf_op jit(solution)/shard_map/ppermute | solution.py:144
  140.4 2.4 %fusion.24 = bf16[60,5120]{1,0:T(8,128)(2,1)} fusion(f32[2,60,5120]{2,1,0:T(8,128)} %reshape.355, s32[]{:T(128)S(6)} %select_n.267, bf16[60,5120]{1,0:T(8,128)(2,1)S(1)} %collective-permute-done.30, bf16[60,5120]{1,0:T(8,128)(2,1)S(1)} %copy-done.10, f32[5120]{0:T(1024)S(1)} %copy-done.21, pred[]{:T(512)S(6)} %and.115), kind=kLoop, calls=%fused_computation.32 | loop fusion | flops 2150400 | bytes 3092485 | tf_op jit(solution)/shard_map/convert_element_type | solution.py:146
  (140 shorter events, 12.3 us)
Async XLA Ops:
  9.8 10.7 %collective-permute-start.1 = (bf16[121,1280]{0,1:T(8,128)(2,1)S(1)}, bf16[121,1280]{0,1:T(8,128)(2,1)S(1)}, u32[]{:S(2)}, u32[]{:S(2)}) collective-permute-start(bf16[121,1280]{0,1:T(8,128)(2,1)S(1)} %get-tuple-element.65), channel_id=1, source_target_pairs={{0,8},{2,10},{8,16},{10,18},{16,24},{18,26},{24,28},{26,30},{28,20... | collective-permute-start | bytes 929288 | tf_op jit(solution)/shard_map/ppermute | solution.py:36
  12.9 9.5 %collective-permute-start.10 = (bf16[121,1280]{0,1:T(8,128)(2,1)S(1)}, bf16[121,1280]{0,1:T(8,128)(2,1)S(1)}, u32[]{:S(2)}, u32[]{:S(2)}) collective-permute-start(bf16[121,1280]{0,1:T(8,128)(2,1)S(1)} %get-tuple-element.66), channel_id=1, source_target_pairs={{8,0},{10,2},{16,8},{18,10},{24,16},{26,18},{28,24},{30,26},{20,28... | collective-permute-start | bytes 929288 | tf_op jit(solution)/shard_map/ppermute | solution.py:37
  20.6 29.0 %copy-start.12 = (bf16[121,1280]{0,1:T(8,128)(2,1)}, bf16[121,1280]{0,1:T(8,128)(2,1)S(1)}, u32[]{:S(2)}) copy-start(bf16[121,1280]{0,1:T(8,128)(2,1)S(1)} %collective-permute-done.1) | copy-start | bytes 929284
  20.6 8.9 %collective-permute-start.3 = (bf16[121,1280]{0,1:T(8,128)(2,1)S(1)}, bf16[121,1280]{0,1:T(8,128)(2,1)S(1)}, u32[]{:S(2)}, u32[]{:S(2)}) collective-permute-start(bf16[121,1280]{0,1:T(8,128)(2,1)S(1)} %collective-permute-done.1), channel_id=1, source_target_pairs={{0,8},{2,10},{8,16},{10,18},{16,24},{18,26},{24,28},{26,30},{28,20... | collective-permute-start | bytes 929288 | tf_op jit(solution)/shard_map/ppermute | solution.py:36
  22.4 27.3 %copy-start.11 = (bf16[121,1280]{0,1:T(8,128)(2,1)}, bf16[121,1280]{0,1:T(8,128)(2,1)S(1)}, u32[]{:S(2)}) copy-start(bf16[121,1280]{0,1:T(8,128)(2,1)S(1)} %collective-permute-done.10) | copy-start | bytes 929284
  22.4 8.6 %collective-permute-start.12 = (bf16[121,1280]{0,1:T(8,128)(2,1)S(1)}, bf16[121,1280]{0,1:T(8,128)(2,1)S(1)}, u32[]{:S(2)}, u32[]{:S(2)}) collective-permute-start(bf16[121,1280]{0,1:T(8,128)(2,1)S(1)} %collective-permute-done.10), channel_id=1, source_target_pairs={{8,0},{10,2},{16,8},{18,10},{24,16},{26,18},{28,24},{30,26},{20,28... | collective-permute-start | bytes 929288 | tf_op jit(solution)/shard_map/ppermute | solution.py:37
  22.6 8.9 %collective-permute-start = (bf16[121,1280]{0,1:T(8,128)(2,1)S(1)}, bf16[121,1280]{0,1:T(8,128)(2,1)S(1)}, u32[]{:S(2)}, u32[]{:S(2)}) collective-permute-start(bf16[121,1280]{0,1:T(8,128)(2,1)S(1)} %get-tuple-element.65), channel_id=1, source_target_pairs={{0,2},{2,0},{4,6},{6,4},{8,10},{10,8},{12,14},{14,12},{16,18},{18,... | collective-permute-start | bytes 929288 | tf_op jit(solution)/shard_map/ppermute | solution.py:40
  22.6 9.4 %collective-permute-start.9 = (bf16[121,1280]{0,1:T(8,128)(2,1)S(1)}, bf16[121,1280]{0,1:T(8,128)(2,1)S(1)}, u32[]{:S(2)}, u32[]{:S(2)}) collective-permute-start(bf16[121,1280]{0,1:T(8,128)(2,1)S(1)} %get-tuple-element.66), channel_id=1, source_target_pairs={{0,2},{2,0},{4,6},{6,4},{8,10},{10,8},{12,14},{14,12},{16,18},{18,... | collective-permute-start | bytes 929288 | tf_op jit(solution)/shard_map/ppermute | solution.py:41
  29.5 20.4 %copy-start.15 = (bf16[121,1280]{0,1:T(8,128)(2,1)}, bf16[121,1280]{0,1:T(8,128)(2,1)S(1)}, u32[]{:S(2)}) copy-start(bf16[121,1280]{0,1:T(8,128)(2,1)S(1)} %collective-permute-done.3) | copy-start | bytes 929284
  29.5 8.1 %collective-permute-start.5 = (bf16[121,1280]{0,1:T(8,128)(2,1)S(1)}, bf16[121,1280]{0,1:T(8,128)(2,1)}, u32[]{:S(2)}, u32[]{:S(2)}) collective-permute-start(bf16[121,1280]{0,1:T(8,128)(2,1)S(1)} %collective-permute-done.3), channel_id=1, source_target_pairs={{0,8},{2,10},{8,16},{10,18},{16,24},{18,26},{24,28},{26,30},{28,20... | collective-permute-start | bytes 929288 | tf_op jit(solution)/shard_map/ppermute | solution.py:36
  31.0 19.0 %copy-start.13 = (bf16[121,1280]{0,1:T(8,128)(2,1)}, bf16[121,1280]{0,1:T(8,128)(2,1)S(1)}, u32[]{:S(2)}) copy-start(bf16[121,1280]{0,1:T(8,128)(2,1)S(1)} %collective-permute-done.12) | copy-start | bytes 929284
  31.0 7.8 %collective-permute-start.14 = (bf16[121,1280]{0,1:T(8,128)(2,1)S(1)}, bf16[121,1280]{0,1:T(8,128)(2,1)S(1)}, u32[]{:S(2)}, u32[]{:S(2)}) collective-permute-start(bf16[121,1280]{0,1:T(8,128)(2,1)S(1)} %collective-permute-done.12), channel_id=1, source_target_pairs={{8,0},{10,2},{16,8},{18,10},{24,16},{26,18},{28,24},{30,26},{20,28... | collective-permute-start | bytes 929288 | tf_op jit(solution)/shard_map/ppermute | solution.py:37
  31.5 8.9 %collective-permute-start.2 = (bf16[121,1280]{0,1:T(8,128)(2,1)S(1)}, bf16[121,1280]{0,1:T(8,128)(2,1)S(1)}, u32[]{:S(2)}, u32[]{:S(2)}) collective-permute-start(bf16[121,1280]{0,1:T(8,128)(2,1)S(1)} %collective-permute-done.1), channel_id=1, source_target_pairs={{0,2},{2,0},{4,6},{6,4},{8,10},{10,8},{12,14},{14,12},{16,18},{18,... | collective-permute-start | bytes 929288 | tf_op jit(solution)/shard_map/ppermute | solution.py:40
  31.5 18.2 %copy-start.17 = (bf16[121,1280]{0,1:T(8,128)(2,1)}, bf16[121,1280]{0,1:T(8,128)(2,1)S(1)}, u32[]{:S(2)}) copy-start(bf16[121,1280]{0,1:T(8,128)(2,1)S(1)} %collective-permute-done) | copy-start | bytes 929284
  31.5 8.9 %collective-permute-start.11 = (bf16[121,1280]{0,1:T(8,128)(2,1)S(1)}, bf16[121,1280]{0,1:T(8,128)(2,1)S(1)}, u32[]{:S(2)}, u32[]{:S(2)}) collective-permute-start(bf16[121,1280]{0,1:T(8,128)(2,1)S(1)} %collective-permute-done.10), channel_id=1, source_target_pairs={{0,2},{2,0},{4,6},{6,4},{8,10},{10,8},{12,14},{14,12},{16,18},{18,... | collective-permute-start | bytes 929288 | tf_op jit(solution)/shard_map/ppermute | solution.py:41
  32.0 17.8 %copy-start.14 = (bf16[121,1280]{0,1:T(8,128)(2,1)}, bf16[121,1280]{0,1:T(8,128)(2,1)S(1)}, u32[]{:S(2)}) copy-start(bf16[121,1280]{0,1:T(8,128)(2,1)S(1)} %collective-permute-done.9) | copy-start | bytes 929284
  32.0 8.9 %collective-permute-start.4 = (bf16[121,1280]{0,1:T(8,128)(2,1)S(1)}, bf16[121,1280]{0,1:T(8,128)(2,1)S(1)}, u32[]{:S(2)}, u32[]{:S(2)}) collective-permute-start(bf16[121,1280]{0,1:T(8,128)(2,1)S(1)} %collective-permute-done.3), channel_id=1, source_target_pairs={{0,2},{2,0},{4,6},{6,4},{8,10},{10,8},{12,14},{14,12},{16,18},{18,... | collective-permute-start | bytes 929288 | tf_op jit(solution)/shard_map/ppermute | solution.py:40
  37.6 7.4 %collective-permute-start.7 = (bf16[121,1280]{0,1:T(8,128)(2,1)}, bf16[121,1280]{0,1:T(8,128)(2,1)}, u32[]{:S(2)}, u32[]{:S(2)}) collective-permute-start(bf16[121,1280]{0,1:T(8,128)(2,1)} %collective-permute-done.5), channel_id=1, source_target_pairs={{0,8},{2,10},{8,16},{10,18},{16,24},{18,26},{24,28},{26,30},{28,20... | collective-permute-start | bytes 929288 | tf_op jit(solution)/shard_map/ppermute | solution.py:36
  38.7 13.6 %copy-start.16 = (bf16[121,1280]{0,1:T(8,128)(2,1)}, bf16[121,1280]{0,1:T(8,128)(2,1)S(1)}, u32[]{:S(2)}) copy-start(bf16[121,1280]{0,1:T(8,128)(2,1)S(1)} %collective-permute-done.14) | copy-start | bytes 929284
  38.7 7.2 %collective-permute-start.16 = (bf16[121,1280]{0,1:T(8,128)(2,1)S(1)}, bf16[121,1280]{0,1:T(8,128)(2,1)}, u32[]{:S(2)}, u32[]{:S(2)}) collective-permute-start(bf16[121,1280]{0,1:T(8,128)(2,1)S(1)} %collective-permute-done.14), channel_id=1, source_target_pairs={{8,0},{10,2},{16,8},{18,10},{24,16},{26,18},{28,24},{30,26},{20,28... | collective-permute-start | bytes 929288 | tf_op jit(solution)/shard_map/ppermute | solution.py:37
  40.4 5.5 %copy-start.19 = (bf16[121,1280]{0,1:T(8,128)(2,1)}, bf16[121,1280]{0,1:T(8,128)(2,1)S(1)}, u32[]{:S(2)}) copy-start(bf16[121,1280]{0,1:T(8,128)(2,1)S(1)} %collective-permute-done.2) | copy-start | bytes 929284
  40.4 12.7 %collective-permute-start.13 = (bf16[121,1280]{0,1:T(8,128)(2,1)S(1)}, bf16[121,1280]{0,1:T(8,128)(2,1)}, u32[]{:S(2)}, u32[]{:S(2)}) collective-permute-start(bf16[121,1280]{0,1:T(8,128)(2,1)S(1)} %collective-permute-done.12), channel_id=1, source_target_pairs={{0,2},{2,0},{4,6},{6,4},{8,10},{10,8},{12,14},{14,12},{16,18},{18,... | collective-permute-start | bytes 929288 | tf_op jit(solution)/shard_map/ppermute | solution.py:41
  40.4 5.5 %copy-start.18 = (bf16[121,1280]{0,1:T(8,128)(2,1)}, bf16[121,1280]{0,1:T(8,128)(2,1)S(1)}, u32[]{:S(2)}) copy-start(bf16[121,1280]{0,1:T(8,128)(2,1)S(1)} %collective-permute-done.11) | copy-start | bytes 929284
  40.4 16.5 %collective-permute-start.6 = (bf16[121,1280]{0,1:T(8,128)(2,1)}, bf16[121,1280]{0,1:T(8,128)(2,1)}, u32[]{:S(2)}, u32[]{:S(2)}) collective-permute-start(bf16[121,1280]{0,1:T(8,128)(2,1)} %collective-permute-done.5), channel_id=1, source_target_pairs={{0,2},{2,0},{4,6},{6,4},{8,10},{10,8},{12,14},{14,12},{16,18},{18,... | collective-permute-start | bytes 929288 | tf_op jit(solution)/shard_map/ppermute | solution.py:40
  40.9 6.0 %copy-start.20 = (bf16[121,1280]{0,1:T(8,128)(2,1)}, bf16[121,1280]{0,1:T(8,128)(2,1)S(1)}, u32[]{:S(2)}) copy-start(bf16[121,1280]{0,1:T(8,128)(2,1)S(1)} %collective-permute-done.4) | copy-start | bytes 929284
  40.9 17.2 %collective-permute-start.15 = (bf16[121,1280]{0,1:T(8,128)(2,1)S(1)}, bf16[121,1280]{0,1:T(8,128)(2,1)}, u32[]{:S(2)}, u32[]{:S(2)}) collective-permute-start(bf16[121,1280]{0,1:T(8,128)(2,1)S(1)} %collective-permute-done.14), channel_id=1, source_target_pairs={{0,2},{2,0},{4,6},{6,4},{8,10},{10,8},{12,14},{14,12},{16,18},{18,... | collective-permute-start | bytes 929288 | tf_op jit(solution)/shard_map/ppermute | solution.py:41
  45.0 13.9 %collective-permute-start.8 = (bf16[121,1280]{0,1:T(8,128)(2,1)}, bf16[121,1280]{0,1:T(8,128)(2,1)}, u32[]{:S(2)}, u32[]{:S(2)}) collective-permute-start(bf16[121,1280]{0,1:T(8,128)(2,1)} %collective-permute-done.7), channel_id=1, source_target_pairs={{0,2},{2,0},{4,6},{6,4},{8,10},{10,8},{12,14},{14,12},{16,18},{18,... | collective-permute-start | bytes 929288 | tf_op jit(solution)/shard_map/ppermute | solution.py:40
  45.9 13.6 %collective-permute-start.17 = (bf16[121,1280]{0,1:T(8,128)(2,1)}, bf16[121,1280]{0,1:T(8,128)(2,1)}, u32[]{:S(2)}, u32[]{:S(2)}) collective-permute-start(bf16[121,1280]{0,1:T(8,128)(2,1)} %collective-permute-done.16), channel_id=1, source_target_pairs={{0,2},{2,0},{4,6},{6,4},{8,10},{10,8},{12,14},{14,12},{16,18},{18,... | collective-permute-start | bytes 929288 | tf_op jit(solution)/shard_map/ppermute | solution.py:41
  55.3 23.2 %collective-permute-start.18 = (bf16[121,1280]{0,1:T(8,128)(2,1)}, bf16[121,1280]{0,1:T(8,128)(2,1)}, u32[]{:S(2)}, u32[]{:S(2)}) collective-permute-start(bf16[121,1280]{0,1:T(8,128)(2,1)} %collective-permute-done.7), channel_id=1, source_target_pairs={{0,8},{2,10},{8,16},{10,18},{16,24},{18,26},{24,28},{26,30},{28,20... | collective-permute-start | bytes 929288 | tf_op jit(solution)/shard_map/ppermute | solution.py:36
  56.9 23.4 %collective-permute-start.24 = (bf16[121,1280]{0,1:T(8,128)(2,1)}, bf16[121,1280]{0,1:T(8,128)(2,1)}, u32[]{:S(2)}, u32[]{:S(2)}) collective-permute-start(bf16[121,1280]{0,1:T(8,128)(2,1)} %collective-permute-done.16), channel_id=1, source_target_pairs={{8,0},{10,2},{16,8},{18,10},{24,16},{26,18},{28,24},{30,26},{20,28... | collective-permute-start | bytes 929288 | tf_op jit(solution)/shard_map/ppermute | solution.py:37
  74.0 2.0 %copy-start.4 = (bf16[1200,640]{0,1:T(8,128)(2,1)S(1)}, bf16[1200,640]{0,1:T(8,128)(2,1)}, u32[]{:S(2)}) copy-start(bf16[1200,640]{0,1:T(8,128)(2,1)} %get-tuple-element.53) | copy-start | bytes 4608004
  74.0 2.0 %copy-start.5 = (bf16[120,640]{0,1:T(8,128)(2,1)S(1)}, bf16[120,640]{0,1:T(8,128)(2,1)}, u32[]{:S(2)}) copy-start(bf16[120,640]{0,1:T(8,128)(2,1)} %copy.91) | copy-start | bytes 460804
  77.1 3.6 %copy-start = (f32[5,120,1200]{1,2,0:T(8,128)}, f32[5,120,1200]{1,2,0:T(8,128)S(1)}, u32[]{:S(2)}) copy-start(f32[5,120,1200]{1,2,0:T(8,128)S(1)} %get-tuple-element.82) | copy-start | bytes 8640004
  78.5 9.9 %collective-permute-start.20 = (bf16[121,1280]{0,1:T(8,128)(2,1)}, bf16[121,1280]{0,1:T(8,128)(2,1)}, u32[]{:S(2)}, u32[]{:S(2)}) collective-permute-start(bf16[121,1280]{0,1:T(8,128)(2,1)} %collective-permute-done.18), channel_id=1, source_target_pairs={{0,8},{2,10},{8,16},{10,18},{16,24},{18,26},{24,28},{26,30},{28,20... | collective-permute-start | bytes 929288 | tf_op jit(solution)/shard_map/ppermute | solution.py:36
  80.2 11.4 %collective-permute-start.19 = (bf16[121,1280]{0,1:T(8,128)(2,1)}, bf16[121,1280]{0,1:T(8,128)(2,1)}, u32[]{:S(2)}, u32[]{:S(2)}) collective-permute-start(bf16[121,1280]{0,1:T(8,128)(2,1)} %collective-permute-done.18), channel_id=1, source_target_pairs={{0,2},{2,0},{4,6},{6,4},{8,10},{10,8},{12,14},{14,12},{16,18},{18,... | collective-permute-start | bytes 929288 | tf_op jit(solution)/shard_map/ppermute | solution.py:40
  80.3 11.4 %collective-permute-start.26 = (bf16[121,1280]{0,1:T(8,128)(2,1)}, bf16[121,1280]{0,1:T(8,128)(2,1)}, u32[]{:S(2)}, u32[]{:S(2)}) collective-permute-start(bf16[121,1280]{0,1:T(8,128)(2,1)} %collective-permute-done.24), channel_id=1, source_target_pairs={{8,0},{10,2},{16,8},{18,10},{24,16},{26,18},{28,24},{30,26},{20,28... | collective-permute-start | bytes 929288 | tf_op jit(solution)/shard_map/ppermute | solution.py:37
  88.4 3.9 %collective-permute-start.21 = (bf16[121,1280]{0,1:T(8,128)(2,1)}, bf16[121,1280]{0,1:T(8,128)(2,1)}, u32[]{:S(2)}, u32[]{:S(2)}) collective-permute-start(bf16[121,1280]{0,1:T(8,128)(2,1)} %collective-permute-done.20), channel_id=1, source_target_pairs={{0,2},{2,0},{4,6},{6,4},{8,10},{10,8},{12,14},{14,12},{16,18},{18,... | collective-permute-start | bytes 929288 | tf_op jit(solution)/shard_map/ppermute | solution.py:40
  88.8 5.6 %collective-permute-start.25 = (bf16[121,1280]{0,1:T(8,128)(2,1)}, bf16[121,1280]{0,1:T(8,128)(2,1)S(1)}, u32[]{:S(2)}, u32[]{:S(2)}) collective-permute-start(bf16[121,1280]{0,1:T(8,128)(2,1)} %collective-permute-done.24), channel_id=1, source_target_pairs={{0,2},{2,0},{4,6},{6,4},{8,10},{10,8},{12,14},{14,12},{16,18},{18,... | collective-permute-start | bytes 929288 | tf_op jit(solution)/shard_map/ppermute | solution.py:41
  90.0 9.9 %collective-permute-start.22 = (bf16[121,1280]{0,1:T(8,128)(2,1)}, bf16[121,1280]{0,1:T(8,128)(2,1)S(1)}, u32[]{:S(2)}, u32[]{:S(2)}) collective-permute-start(bf16[121,1280]{0,1:T(8,128)(2,1)} %collective-permute-done.20), channel_id=1, source_target_pairs={{0,8},{2,10},{8,16},{10,18},{16,24},{18,26},{24,28},{26,30},{28,20... | collective-permute-start | bytes 929288 | tf_op jit(solution)/shard_map/ppermute | solution.py:36
  91.6 2.8 %collective-permute-start.27 = (bf16[121,1280]{0,1:T(8,128)(2,1)}, bf16[121,1280]{0,1:T(8,128)(2,1)S(1)}, u32[]{:S(2)}, u32[]{:S(2)}) collective-permute-start(bf16[121,1280]{0,1:T(8,128)(2,1)} %collective-permute-done.26), channel_id=1, source_target_pairs={{0,2},{2,0},{4,6},{6,4},{8,10},{10,8},{12,14},{14,12},{16,18},{18,... | collective-permute-start | bytes 929288 | tf_op jit(solution)/shard_map/ppermute | solution.py:41
  91.6 10.4 %collective-permute-start.28 = (bf16[121,1280]{0,1:T(8,128)(2,1)}, bf16[121,1280]{0,1:T(8,128)(2,1)}, u32[]{:S(2)}, u32[]{:S(2)}) collective-permute-start(bf16[121,1280]{0,1:T(8,128)(2,1)} %collective-permute-done.26), channel_id=1, source_target_pairs={{8,0},{10,2},{16,8},{18,10},{24,16},{26,18},{28,24},{30,26},{20,28... | collective-permute-start | bytes 929288 | tf_op jit(solution)/shard_map/ppermute | solution.py:37
  94.4 1.9 %copy-start.6 = (bf16[120,640]{0,1:T(8,128)(2,1)S(1)}, bf16[120,640]{0,1:T(8,128)(2,1)}, u32[]{:S(2)}) copy-start(bf16[120,640]{0,1:T(8,128)(2,1)} %copy.91) | copy-start | bytes 460804
  99.9 2.8 %collective-permute-start.23 = (bf16[121,1280]{0,1:T(8,128)(2,1)S(1)}, bf16[121,1280]{0,1:T(8,128)(2,1)S(1)}, u32[]{:S(2)}, u32[]{:S(2)}) collective-permute-start(bf16[121,1280]{0,1:T(8,128)(2,1)S(1)} %collective-permute-done.22), channel_id=1, source_target_pairs={{0,2},{2,0},{4,6},{6,4},{8,10},{10,8},{12,14},{14,12},{16,18},{18,... | collective-permute-start | bytes 929288 | tf_op jit(solution)/shard_map/ppermute | solution.py:40
  100.4 2.6 %copy-start.2 = (f32[5,120,480]{1,2,0:T(8,128)}, f32[5,120,480]{1,2,0:T(8,128)S(1)}, u32[]{:S(2)}) copy-start(f32[5,120,480]{1,2,0:T(8,128)S(1)} %get-tuple-element.80) | copy-start | bytes 3456004
  102.1 6.5 %collective-permute-start.29 = (bf16[121,1280]{0,1:T(8,128)(2,1)}, bf16[121,1280]{0,1:T(8,128)(2,1)}, u32[]{:S(2)}, u32[]{:S(2)}) collective-permute-start(bf16[121,1280]{0,1:T(8,128)(2,1)} %collective-permute-done.28), channel_id=1, source_target_pairs={{0,2},{2,0},{4,6},{6,4},{8,10},{10,8},{12,14},{14,12},{16,18},{18,... | collective-permute-start | bytes 929288 | tf_op jit(solution)/shard_map/ppermute | solution.py:41
  102.1 1.4 %copy-start.9 = (bf16[1200,640]{0,1:T(8,128)(2,1)S(1)}, bf16[1200,640]{0,1:T(8,128)(2,1)}, u32[]{:S(2)}) copy-start(bf16[1200,640]{0,1:T(8,128)(2,1)} %get-tuple-element.54) | copy-start | bytes 4608004
  102.6 2.0 %copy-start.1 = (f32[5,120,1200]{1,2,0:T(8,128)S(1)}, f32[5,120,1200]{1,2,0:T(8,128)}, u32[]{:S(2)}) copy-start(f32[5,120,1200]{1,2,0:T(8,128)} %copy-done) | copy-start | bytes 8640004
  108.5 2.1 %copy-start.8 = (bf16[1200,640]{0,1:T(8,128)(2,1)S(1)}, bf16[1200,640]{0,1:T(8,128)(2,1)}, u32[]{:S(2)}) copy-start(bf16[1200,640]{0,1:T(8,128)(2,1)} %get-tuple-element.56) | copy-start | bytes 4608004
  110.6 1.3 copy-start.3
  110.7 1.4 %copy-start.7 = (bf16[480,640]{0,1:T(8,128)(2,1)S(1)}, bf16[480,640]{0,1:T(8,128)(2,1)}, u32[]{:S(2)}) copy-start(bf16[480,640]{0,1:T(8,128)(2,1)} %get-tuple-element.59) | copy-start | bytes 1843204
  119.9 20.4 %copy-start.21 = (f32[5120]{0:T(1024)S(1)}, f32[5120]{0:T(1024)}, u32[]{:S(2)}) copy-start(f32[5120]{0:T(1024)} %param.18) | copy-start | bytes 61444
  121.7 18.7 %copy-start.10 = (bf16[60,5120]{1,0:T(8,128)(2,1)S(1)}, bf16[60,5120]{1,0:T(8,128)(2,1)}, u32[]{:S(2)}) copy-start(bf16[60,5120]{1,0:T(8,128)(2,1)} %param.14) | copy-start | bytes 1843204
  123.2 17.2 %collective-permute-start.30 = (bf16[60,5120]{1,0:T(8,128)(2,1)S(1)}, bf16[60,5120]{1,0:T(8,128)(2,1)S(1)}, u32[]{:S(2)}, u32[]{:S(2)}) collective-permute-start(bf16[60,5120]{1,0:T(8,128)(2,1)S(1)} %bitcast_convert_fusion), channel_id=1, source_target_pairs={{0,1},{1,0},{2,3},{3,2},{4,5},{5,4},{6,7},{7,6},{8,9},{9,8},{10,11... | collective-permute-start | bytes 1843208 | tf_op jit(solution)/shard_map/ppermute | solution.py:144

commit v4 on v3

--- a/solution.py
+++ b/solution.py
@@ -90,10 +90,14 @@
         cut = heads_a * HEAD
         scale_factor = 1.0 / math.sqrt(HEAD)
         me = lax.axis_index("seq")
-        info = jnp.zeros((1, 2 * cut), jnp.float32)
-        info = info.at[0, 0].set(valid_count[0].astype(jnp.float32))
-        info = info.at[0, 1].set(assignment[0].astype(jnp.float32))
-        info = info.astype(jnp.bfloat16)
+        rows_pad = (rows_dev + 1 + 7) // 8 * 8
+        row_id = lax.broadcasted_iota(jnp.int32, (rows_pad - rows_dev, 2 * cut), 0)
+        col_id = lax.broadcasted_iota(jnp.int32, (rows_pad - rows_dev, 2 * cut), 1)
+        info = jnp.where(
+            (row_id == 0) & (col_id == 0),
+            valid_count[0],
+            jnp.where((row_id == 0) & (col_id == 1), assignment[0], 0),
+        ).astype(jnp.bfloat16)
         packet_a = jnp.concatenate(
             [jnp.concatenate([key_rows[:, :cut], value_rows[:, :cut]], axis=1), info], axis=0
         )
@@ -115,7 +119,7 @@
 
         limit_a = limits_for(ids_a)
         limit_b = limits_for(ids_b)
-        within = jnp.arange(rows_dev, dtype=jnp.int32)
+        within = jnp.arange(rows_pad, dtype=jnp.int32)
         phases = [(0, known + 1), (known + 1, chips - 1), (chips - 1, chips)]
         phases = [(2 * lo, 2 * hi) for lo, hi in phases if hi > lo]
 
@@ -124,9 +128,9 @@
             q3 = queries[:, lo * HEAD : hi * HEAD].reshape(rows_dev, hi - lo, HEAD)
             parts = []
             for first, last in phases:
-                stack = jnp.concatenate([g[:rows_dev] for g in got[first:last]], axis=0)
-                keys = stack[:, :width].reshape(-1, hi - lo, HEAD)
-                values = stack[:, width:].reshape(-1, hi - lo, HEAD)
+                stack = jnp.stack(got[first:last])
+                keys = stack[:, :, :width].reshape(-1, hi - lo, HEAD)
+                values = stack[:, :, width:].reshape(-1, hi - lo, HEAD)
                 keeping = (within[None, :] < limits[first:last, None]).reshape(-1)
                 parts.append(attend_part(q3, keys, values, keeping, scale_factor))
             return combine(parts, rows_dev)

time: 144 us -> 187 us (1.30)
  local copies, waits for them, and re-layouts: 36.8 us -> 81.4 us
  waiting for transfers between devices: 50.9 us -> 35.8 us
  matrix products: 15.5 us -> 27.2 us
  other arithmetic: 17.4 us -> 19.9 us
    reshape x0 -> x12, local copies, waits for them, and re-layouts: none -> 24.3 us  [the longest x6 13.5 us: half(): keys = stack[:, :, :width].reshape(-1, hi - lo, HEAD)]
    ppermute x7, waiting for transfers between devices: 32.6 us -> 10.2 us  [gather_ring(): cur_a = lax.ppermute(cur_a, 'seq', forward)]
    slice x4 -> x16, local copies, waits for them, and re-layouts: 4.35 us -> 22.7 us  [the longest x8 15.2 us: half(): keys = stack[:, :, :width].reshape(-1, hi - lo, HEAD)]
    unnamed x48 -> x46, local copies, waits for them, and re-layouts: 2.82 us -> 17.1 us
    concatenate x2 -> x0, local copies, waits for them, and re-layouts: 10.8 us -> none  [half(): stack = jnp.concatenate([g[:rows_dev] for g in got[first:last]], axis=0)]
    ppermute x7, starting transfers between devices: 12.3 us -> 2.67 us  [gather_ring(): cur_a = lax.ppermute(cur_a, 'seq', forward)]
    ppermute x7, starting transfers between devices: 3.28 us -> 12.9 us  [gather_ring(): cur_b = lax.ppermute(cur_b, 'seq', backward)]
    concatenate x7 -> x0, other arithmetic: 7.52 us -> none  [the longest x4 5.68 us: half(): stack = jnp.concatenate([g[:rows_dev] for g in got[first:last]], axis=0)]
  transfers between devices with their start and end apart: 31 -> 31, of which waited for: 9 -> 7; matrix products, arithmetic and copies ran while one was open for 30% -> 52% of each run, Pallas kernels for 0% -> 0%
where the time goes in v4:
time: 187 us; the launch traced here: 186 us
  local copies, waits for them, and re-layouts  81.4 us (44%)
  waiting for transfers between devices  35.8 us (19%)
  matrix products  27.2 us (15%)
  other arithmetic  19.9 us (11%)
  starting transfers between devices  19.6 us (10%)
  between operations  1.91 us (1%)
    unnamed x46, local copies, waits for them, and re-layouts  17.1 us
    ppermute x1, waiting for transfers between devices, on_device(): came = lax.ppermute(other, 'tp', [(0, 1), (1, 0)])  15.6 us
    slice x8, local copies, waits for them, and re-layouts, half(): keys = stack[:, :, :width].reshape(-1, hi - lo, HEAD)  15.2 us
    reshape x6, local copies, waits for them, and re-layouts, half(): keys = stack[:, :, :width].reshape(-1, hi - lo, HEAD)  13.5 us
    ppermute x7, starting transfers between devices, gather_ring(): cur_b = lax.ppermute(cur_b, 'seq', backward)  12.9 us
    dot_general x6, matrix products, attend_part(): jnp.einsum('hqk,khd->hqd', weights.astype(jnp.bfloat16), values, preferre...  11 us
    reshape x6, local copies, waits for them, and re-layouts, half(): values = stack[:, :, width:].reshape(-1, hi - lo, HEAD)  10.8 us
    ppermute x7, waiting for transfers between devices, gather_ring(): cur_a = lax.ppermute(cur_a, 'seq', forward)  10.2 us
  transfers between devices with their start and end apart: 31, of which 7 were waited for; matrix products, arithmetic and copies ran while one was open for 52% of the time, Pallas kernels for 0%

profile of v4, /device:TPU:0, one launch (start us, length us, event | category | flops | bytes accessed | tf_op | source)
XLA Modules:
  0.0 185.8 jit_solution(11320110598904999976)
XLA Ops:
  1.3 1.0 fusion.128
  2.5 1.0 fusion.127
  6.9 2.3 %bitcast_dynamic-update-slice_fusion.19 = (bf16[10,128,1280]{1,2,0:T(8,128)(2,1)S(1)}, bf16[128,1280]{0,1:T(8,128)(2,1)}, bf16[10,128,1280]{1,2,0:T(8,128)(2,1)}, bf16[128,1280]{0,1:T(8,128)(2,1)}) fusion(bf16[8,1280]{0,1:T(8,128)(2,1)S(1)} %select_convert_fusion, bf16[120,640]{0,1:T(8,128)(2,1)S(1)} %copy.130, bf16[120,640]{0,1:T(8,128)(2,1)} %copy.129, ...), kind=kLoop, calls=%fused_computation.115 | loop fusion | flops 1802238 | bytes 1945600
  9.1 3.0 %collective-permute-start.10 = (bf16[128,1280]{0,1:T(8,128)(2,1)}, bf16[128,1280]{0,1:T(8,128)(2,1)}, u32[]{:S(2)}, u32[]{:S(2)}) collective-permute-start(bf16[128,1280]{0,1:T(8,128)(2,1)} %get-tuple-element.46), channel_id=1, source_target_pairs={{8,0},{10,2},{16,8},{18,10},{24,16},{26,18},{28,24},{30,26},{20,28... | collective-permute-start | bytes 983048 | tf_op jit(solution)/shard_map/ppermute | solution.py:37
  12.7 1.8 fusion.126
  14.4 1.1 copy.99
  15.7 1.7 copy.82
  17.7 2.5 %collective-permute-done.10 = bf16[128,1280]{0,1:T(8,128)(2,1)} collective-permute-done((bf16[128,1280]{0,1:T(8,128)(2,1)}, bf16[128,1280]{0,1:T(8,128)(2,1)}, u32[]{:S(2)}, u32[]{:S(2)}) %collective-permute-start.10) | collective-permute-done | bytes 327712 | tf_op jit(solution)/shard_map/ppermute | solution.py:37
  20.2 1.7 collective-permute-start.12
  24.7 1.7 bitcast_dynamic-update-slice_fusion.8
  26.4 1.7 bitcast_dynamic-update-slice_fusion.7
  28.9 1.0 bitcast_dynamic-update-slice_fusion.18
  29.9 1.0 bitcast_dynamic-update-slice_fusion.17
  31.0 1.7 collective-permute-start.14
  32.8 1.0 collective-permute-done.3
  36.0 5.2 %collective-permute-done.14 = bf16[128,1280]{0,1:T(8,128)(2,1)S(1)} collective-permute-done((bf16[128,1280]{0,1:T(8,128)(2,1)S(1)}, bf16[128,1280]{0,1:T(8,128)(2,1)S(1)}, u32[]{:S(2)}, u32[]{:S(2)}) %collective-permute-start.14) | collective-permute-done | bytes 327712 | tf_op jit(solution)/shard_map/ppermute | solution.py:37
  41.2 1.7 collective-permute-start.16
  42.8 1.2 collective-permute-done.5
  46.3 8.1 %collective-permute-done.7 = bf16[128,1280]{0,1:T(8,128)(2,1)} collective-permute-done((bf16[128,1280]{0,1:T(8,128)(2,1)S(1)}, bf16[128,1280]{0,1:T(8,128)(2,1)}, u32[]{:S(2)}, u32[]{:S(2)}) %collective-permute-start.7) | collective-permute-done | bytes 327712 | tf_op jit(solution)/shard_map/ppermute | solution.py:36
  56.4 1.6 collective-permute-start.24
  59.2 1.7 bitcast_dynamic-update-slice_fusion.1
  61.1 1.0 bitcast_dynamic-update-slice_fusion.11
  63.0 1.0 copy-done.11
  64.7 1.7 bitcast_dynamic-update-slice_fusion
  66.5 2.2 %fusion.123 = (bf16[10,128,640]{1,2,0:T(8,128)(2,1)S(1)}, bf16[10,128,640]{1,2,0:T(8,128)(2,1)S(1)}) fusion(bf16[10,128,1280]{1,2,0:T(8,128)(2,1)} %bitcast_dynamic-update-slice_fusion), kind=kLoop, calls=%fused_computation.176 | loop fusion | bytes 6553600 | tf_op jit(solution)/shard_map/slice | solution.py:132
  68.6 2.4 %copy.98 = bf16[10,128,640]{2,1,0:T(8,128)(2,1)} copy(bf16[10,128,640]{1,2,0:T(8,128)(2,1)S(1)} %get-tuple-element.35) | data formatting | bytes 3276800 | tf_op jit(solution)/shard_map/slice | solution.py:132
  71.0 4.7 %reshape.276 = bf16[1280,5,128]{2,1,0:T(8,128)(2,1)} reshape(bf16[10,128,640]{2,1,0:T(8,128)(2,1)} %copy.98) | data formatting | bytes 3276800 | tf_op jit(solution)/shard_map/reshape | solution.py:132
  76.6 3.5 %fusion.122 = (bf16[10,128,640]{1,2,0:T(8,128)(2,1)}, bf16[10,128,640]{1,2,0:T(8,128)(2,1)S(1)}) fusion(bf16[10,128,1280]{1,2,0:T(8,128)(2,1)} %bitcast_dynamic-update-slice_fusion.10), kind=kLoop, calls=%fused_computation.175 | loop fusion | bytes 6553600 | tf_op jit(solution)/shard_map/slice | solution.py:132
  80.3 2.4 %fusion.129 = (f32[5,120]{1,0:T(8,128)S(1)}, f32[5,120,1280]{2,1,0:T(8,128)}) fusion(bf16[120,5,128]{0,2,1:T(8,128)(2,1)S(1)} %bitcast.317, bf16[1280,5,128]{2,1,0:T(8,128)(2,1)S(1)} %copy-done.2, pred[1280]{0:T(1024)(128)(4,1)S(1)} %fusion.96), kind=kOutput, calls=%fused_computation.182 | convolution fusion | flops 198911392 | bytes 4867680 | tf_op jit(solution)/shard_map/qhd,khd->hqk/dot_general | solution.py:53
  82.9 3.5 %copy.81 = bf16[10,128,640]{2,1,0:T(8,128)(2,1)} copy(bf16[10,128,640]{1,2,0:T(8,128)(2,1)} %get-tuple-element.33) | data formatting | bytes 3276800 | tf_op jit(solution)/shard_map/slice | solution.py:132
  86.5 4.7 %reshape.268 = bf16[1280,5,128]{2,1,0:T(8,128)(2,1)} reshape(bf16[10,128,640]{2,1,0:T(8,128)(2,1)} %copy.81) | data formatting | bytes 3276800 | tf_op jit(solution)/shard_map/reshape | solution.py:132
  91.2 1.6 collective-permute-start.26
  92.8 2.5 %fusion.6 = f32[5,120]{1,0:T(8,128)S(1)} fusion(f32[5,120,1280]{2,1,0:T(8,128)} %get-tuple-element.56, f32[5,120]{1,0:T(8,128)S(1)} %get-tuple-element.55, pred[1280]{0:T(1024)(128)(4,1)S(1)} %fusion.96), kind=kLoop, calls=%fused_computation.10 | loop fusion | flops 2303400 | bytes 3078080 | tf_op jit(solution)/shard_map/reduce_sum | solution.py:59
  96.0 2.4 %fusion.132 = (f32[5,120]{1,0:T(8,128)S(1)}, f32[5,120,1280]{2,1,0:T(8,128)}) fusion(bf16[120,5,128]{0,2,1:T(8,128)(2,1)S(1)} %bitcast.320, bf16[1280,5,128]{2,1,0:T(8,128)(2,1)S(1)} %copy-done.1, pred[1280]{0:T(1024)(128)(4,1)S(1)} %fusion.95), kind=kOutput, calls=%fused_computation.185 | convolution fusion | flops 198911392 | bytes 4867680 | tf_op jit(solution)/shard_map/qhd,khd->hqk/dot_general | solution.py:53
  98.4 2.2 %collective-permute-done.26 = bf16[128,1280]{0,1:T(8,128)(2,1)} collective-permute-done((bf16[128,1280]{0,1:T(8,128)(2,1)}, bf16[128,1280]{0,1:T(8,128)(2,1)}, u32[]{:S(2)}, u32[]{:S(2)}) %collective-permute-start.26) | collective-permute-done | bytes 327712 | tf_op jit(solution)/shard_map/ppermute | solution.py:37
  100.7 2.4 %copy.108 = bf16[10,128,640]{2,1,0:T(8,128)(2,1)} copy(bf16[10,128,640]{1,2,0:T(8,128)(2,1)S(1)} %get-tuple-element.36) | data formatting | bytes 3276800 | tf_op jit(solution)/shard_map/slice | solution.py:133
  103.0 4.7 %reshape.280 = bf16[1280,5,128]{2,1,0:T(8,128)(2,1)} reshape(bf16[10,128,640]{2,1,0:T(8,128)(2,1)} %copy.108) | data formatting | bytes 3276800 | tf_op jit(solution)/shard_map/reshape | solution.py:133
  107.7 1.7 copy.91
  109.4 3.1 %reshape.272 = bf16[1280,5,128]{2,1,0:T(8,128)(2,1)} reshape(bf16[10,128,640]{2,1,0:T(8,128)(2,1)S(1)} %copy.91) | data formatting | bytes 3276800 | tf_op jit(solution)/shard_map/reshape | solution.py:133
  113.0 2.5 %fusion.4 = f32[5,120]{1,0:T(8,128)S(1)} fusion(f32[5,120,1280]{2,1,0:T(8,128)} %get-tuple-element.62, f32[5,120]{1,0:T(8,128)S(1)} %get-tuple-element.61, pred[1280]{0:T(1024)(128)(4,1)S(1)} %fusion.95), kind=kLoop, calls=%fused_computation.8 | loop fusion | flops 2303400 | bytes 3078080 | tf_op jit(solution)/shard_map/reduce_sum | solution.py:59
  115.5 1.6 collective-permute-start.28
  117.6 1.4 pad_maximum_fusion.1
  120.0 1.2 pad_maximum_fusion
  122.6 1.3 copy.110
  123.9 2.3 %reshape.281 = bf16[512,5,128]{0,2,1:T(8,128)(2,1)} reshape(bf16[4,128,640]{1,0,2:T(4,128)(2,1)} %copy.110) | data formatting | bytes 1310720 | tf_op jit(solution)/shard_map/reshape | solution.py:133
  126.2 1.6 copy.85
  127.8 1.1 reshape.270
  130.3 1.5 fusion.134
  132.7 1.8 pad_maximum_fusion.2
  134.4 1.1 copy.105
  135.5 1.9 %reshape.279 = bf16[256,5,128]{0,2,1:T(8,128)(2,1)} reshape(bf16[2,128,640]{1,0,2:T(2,128)(2,1)} %copy.105) | data formatting | bytes 655360 | tf_op jit(solution)/shard_map/reshape | solution.py:132
  137.4 1.3 fusion.130
  139.6 3.8 %fusion.53 = f32[120,5,128]{2,0,1:T(8,128)S(1)} fusion(bf16[1280,5,128]{2,1,0:T(8,128)(2,1)} %reshape.280, f32[5,120,1280]{2,1,0:T(8,128)} %get-tuple-element.56, f32[5,120]{1,0:T(8,128)S(1)} %get-tuple-element.55, pred[1280]{0:T(1024)(128)(4,1)S(1)} %fusion.96, f32[120,5]{0,1:T(8,128)S(1)} %get-tuple-element.30), kind=kOutput, calls=%fused_computation.61 | convolution fusion | flops 198988800 | bytes 5023680 | tf_op jit(solution)/shard_map/hqk,khd->hqd/dot_general | solution.py:60
  143.4 1.2 fusion.40
  145.2 1.5 fusion.64
  146.9 1.2 pad_maximum_fusion.3
  149.9 1.3 fusion.133
  151.6 3.8 %fusion.58 = f32[120,5,128]{2,0,1:T(8,128)S(1)} fusion(bf16[1280,5,128]{2,1,0:T(8,128)(2,1)} %reshape.272, f32[5,120,1280]{2,1,0:T(8,128)} %get-tuple-element.62, f32[5,120]{1,0:T(8,128)S(1)} %get-tuple-element.61, pred[1280]{0:T(1024)(128)(4,1)S(1)} %fusion.95, f32[120,5]{0,1:T(8,128)S(1)} %get-tuple-element.24), kind=kOutput, calls=%fused_computation.62 | convolution fusion | flops 198988800 | bytes 5023680 | tf_op jit(solution)/shard_map/hqk,khd->hqd/dot_general | solution.py:60
  156.3 6.6 %fusion.83 = f32[120,5120]{1,0:T(8,128)S(1)} fusion(bf16[1280,5120]{1,0:T(8,128)(2,1)} %param.15, bf16[120,640]{0,1:T(8,128)(2,1)S(1)} %bitcast.323, bf16[120,640]{0,1:T(8,128)(2,1)S(1)} %bitcast.324), kind=kOutput, calls=%fused_computation.92 | convolution fusion | flops 1573478400 | bytes 15872000 | tf_op jit(solution)/shard_map/dot_general | solution.py:141
  163.0 1.7 reshape.284
  164.7 1.4 bitcast_convert_fusion
  166.1 1.6 collective-permute-start.30
  167.7 15.6 %collective-permute-done.30 = bf16[60,5120]{1,0:T(8,128)(2,1)S(1)} collective-permute-done((bf16[60,5120]{1,0:T(8,128)(2,1)S(1)}, bf16[60,5120]{1,0:T(8,128)(2,1)S(1)}, u32[]{:S(2)}, u32[]{:S(2)}) %collective-permute-start.30) | collective-permute-done | bytes 614432 | tf_op jit(solution)/shard_map/ppermute | solution.py:148
  183.3 2.4 %fusion.28 = bf16[60,5120]{1,0:T(8,128)(2,1)} fusion(f32[2,60,5120]{2,1,0:T(8,128)} %reshape.284, s32[]{:T(128)S(6)} %select_n.277, bf16[60,5120]{1,0:T(8,128)(2,1)S(1)} %collective-permute-done.30, bf16[60,5120]{1,0:T(8,128)(2,1)S(1)} %copy-done.8, f32[5120]{0:T(1024)S(1)} %copy-done.12, pred[]{:T(512)S(6)} %and.115), kind=kLoop, calls=%fused_computation.36 | loop fusion | flops 2150400 | bytes 3092485 | tf_op jit(solution)/shard_map/convert_element_type | solution.py:150
  (150 shorter events, 29.5 us)
Async XLA Ops:
  9.1 11.0 %collective-permute-start.10 = (bf16[128,1280]{0,1:T(8,128)(2,1)}, bf16[128,1280]{0,1:T(8,128)(2,1)}, u32[]{:S(2)}, u32[]{:S(2)}) collective-permute-start(bf16[128,1280]{0,1:T(8,128)(2,1)} %get-tuple-element.46), channel_id=1, source_target_pairs={{8,0},{10,2},{16,8},{18,10},{24,16},{26,18},{28,24},{30,26},{20,28... | collective-permute-start | bytes 983048 | tf_op jit(solution)/shard_map/ppermute | solution.py:37
  12.1 9.8 %collective-permute-start.1 = (bf16[128,1280]{0,1:T(8,128)(2,1)}, bf16[128,1280]{0,1:T(8,128)(2,1)}, u32[]{:S(2)}, u32[]{:S(2)}) collective-permute-start(bf16[128,1280]{0,1:T(8,128)(2,1)} %get-tuple-element.26), channel_id=1, source_target_pairs={{0,8},{2,10},{8,16},{10,18},{16,24},{18,26},{24,28},{26,30},{28,20... | collective-permute-start | bytes 983048 | tf_op jit(solution)/shard_map/ppermute | solution.py:36
  12.2 11.4 %collective-permute-start.9 = (bf16[128,1280]{0,1:T(8,128)(2,1)}, bf16[128,1280]{0,1:T(8,128)(2,1)}, u32[]{:S(2)}, u32[]{:S(2)}) collective-permute-start(bf16[128,1280]{0,1:T(8,128)(2,1)} %get-tuple-element.46), channel_id=1, source_target_pairs={{0,2},{2,0},{4,6},{6,4},{8,10},{10,8},{12,14},{14,12},{16,18},{18,... | collective-permute-start | bytes 983048 | tf_op jit(solution)/shard_map/ppermute | solution.py:41
  12.2 16.0 %collective-permute-start = (bf16[128,1280]{0,1:T(8,128)(2,1)}, bf16[128,1280]{0,1:T(8,128)(2,1)}, u32[]{:S(2)}, u32[]{:S(2)}) collective-permute-start(bf16[128,1280]{0,1:T(8,128)(2,1)} %get-tuple-element.26), channel_id=1, source_target_pairs={{0,2},{2,0},{4,6},{6,4},{8,10},{10,8},{12,14},{14,12},{16,18},{18,... | collective-permute-start | bytes 983048 | tf_op jit(solution)/shard_map/ppermute | solution.py:40
  20.2 13.7 %collective-permute-start.11 = (bf16[128,1280]{0,1:T(8,128)(2,1)}, bf16[128,1280]{0,1:T(8,128)(2,1)S(1)}, u32[]{:S(2)}, u32[]{:S(2)}) collective-permute-start(bf16[128,1280]{0,1:T(8,128)(2,1)} %collective-permute-done.10), channel_id=1, source_target_pairs={{0,2},{2,0},{4,6},{6,4},{8,10},{10,8},{12,14},{14,12},{16,18},{18,... | collective-permute-start | bytes 983048 | tf_op jit(solution)/shard_map/ppermute | solution.py:41
  20.2 10.8 %collective-permute-start.12 = (bf16[128,1280]{0,1:T(8,128)(2,1)}, bf16[128,1280]{0,1:T(8,128)(2,1)S(1)}, u32[]{:S(2)}, u32[]{:S(2)}) collective-permute-start(bf16[128,1280]{0,1:T(8,128)(2,1)} %collective-permute-done.10), channel_id=1, source_target_pairs={{8,0},{10,2},{16,8},{18,10},{24,16},{26,18},{28,24},{30,26},{20,28... | collective-permute-start | bytes 983048 | tf_op jit(solution)/shard_map/ppermute | solution.py:37
  22.6 13.2 %collective-permute-start.2 = (bf16[128,1280]{0,1:T(8,128)(2,1)}, bf16[128,1280]{0,1:T(8,128)(2,1)S(1)}, u32[]{:S(2)}, u32[]{:S(2)}) collective-permute-start(bf16[128,1280]{0,1:T(8,128)(2,1)} %collective-permute-done.1), channel_id=1, source_target_pairs={{0,2},{2,0},{4,6},{6,4},{8,10},{10,8},{12,14},{14,12},{16,18},{18,... | collective-permute-start | bytes 983048 | tf_op jit(solution)/shard_map/ppermute | solution.py:40
  23.6 10.1 %collective-permute-start.3 = (bf16[128,1280]{0,1:T(8,128)(2,1)}, bf16[128,1280]{0,1:T(8,128)(2,1)S(1)}, u32[]{:S(2)}, u32[]{:S(2)}) collective-permute-start(bf16[128,1280]{0,1:T(8,128)(2,1)} %collective-permute-done.1), channel_id=1, source_target_pairs={{0,8},{2,10},{8,16},{10,18},{16,24},{18,26},{24,28},{26,30},{28,20... | collective-permute-start | bytes 983048 | tf_op jit(solution)/shard_map/ppermute | solution.py:36
  31.0 13.2 %collective-permute-start.13 = (bf16[128,1280]{0,1:T(8,128)(2,1)S(1)}, bf16[128,1280]{0,1:T(8,128)(2,1)S(1)}, u32[]{:S(2)}, u32[]{:S(2)}) collective-permute-start(bf16[128,1280]{0,1:T(8,128)(2,1)S(1)} %collective-permute-done.12), channel_id=1, source_target_pairs={{0,2},{2,0},{4,6},{6,4},{8,10},{10,8},{12,14},{14,12},{16,18},{18,... | collective-permute-start | bytes 983048 | tf_op jit(solution)/shard_map/ppermute | solution.py:41
  31.0 10.1 %collective-permute-start.14 = (bf16[128,1280]{0,1:T(8,128)(2,1)S(1)}, bf16[128,1280]{0,1:T(8,128)(2,1)S(1)}, u32[]{:S(2)}, u32[]{:S(2)}) collective-permute-start(bf16[128,1280]{0,1:T(8,128)(2,1)S(1)} %collective-permute-done.12), channel_id=1, source_target_pairs={{8,0},{10,2},{16,8},{18,10},{24,16},{26,18},{28,24},{30,26},{20,28... | collective-permute-start | bytes 983048 | tf_op jit(solution)/shard_map/ppermute | solution.py:37
  33.8 12.3 %collective-permute-start.4 = (bf16[128,1280]{0,1:T(8,128)(2,1)S(1)}, bf16[128,1280]{0,1:T(8,128)(2,1)S(1)}, u32[]{:S(2)}, u32[]{:S(2)}) collective-permute-start(bf16[128,1280]{0,1:T(8,128)(2,1)S(1)} %collective-permute-done.3), channel_id=1, source_target_pairs={{0,2},{2,0},{4,6},{6,4},{8,10},{10,8},{12,14},{14,12},{16,18},{18,... | collective-permute-start | bytes 983048 | tf_op jit(solution)/shard_map/ppermute | solution.py:40
  33.9 10.1 %collective-permute-start.5 = (bf16[128,1280]{0,1:T(8,128)(2,1)S(1)}, bf16[128,1280]{0,1:T(8,128)(2,1)S(1)}, u32[]{:S(2)}, u32[]{:S(2)}) collective-permute-start(bf16[128,1280]{0,1:T(8,128)(2,1)S(1)} %collective-permute-done.3), channel_id=1, source_target_pairs={{0,8},{2,10},{8,16},{10,18},{16,24},{18,26},{24,28},{26,30},{28,20... | collective-permute-start | bytes 983048 | tf_op jit(solution)/shard_map/ppermute | solution.py:36
  41.2 16.8 %collective-permute-start.15 = (bf16[128,1280]{0,1:T(8,128)(2,1)S(1)}, bf16[128,1280]{0,1:T(8,128)(2,1)S(1)}, u32[]{:S(2)}, u32[]{:S(2)}) collective-permute-start(bf16[128,1280]{0,1:T(8,128)(2,1)S(1)} %collective-permute-done.14), channel_id=1, source_target_pairs={{0,2},{2,0},{4,6},{6,4},{8,10},{10,8},{12,14},{14,12},{16,18},{18,... | collective-permute-start | bytes 983048 | tf_op jit(solution)/shard_map/ppermute | solution.py:41
  41.2 13.9 %collective-permute-start.16 = (bf16[128,1280]{0,1:T(8,128)(2,1)S(1)}, bf16[128,1280]{0,1:T(8,128)(2,1)}, u32[]{:S(2)}, u32[]{:S(2)}) collective-permute-start(bf16[128,1280]{0,1:T(8,128)(2,1)S(1)} %collective-permute-done.14), channel_id=1, source_target_pairs={{8,0},{10,2},{16,8},{18,10},{24,16},{26,18},{28,24},{30,26},{20,28... | collective-permute-start | bytes 983048 | tf_op jit(solution)/shard_map/ppermute | solution.py:37
  44.1 16.9 %collective-permute-start.6 = (bf16[128,1280]{0,1:T(8,128)(2,1)S(1)}, bf16[128,1280]{0,1:T(8,128)(2,1)S(1)}, u32[]{:S(2)}, u32[]{:S(2)}) collective-permute-start(bf16[128,1280]{0,1:T(8,128)(2,1)S(1)} %collective-permute-done.5), channel_id=1, source_target_pairs={{0,2},{2,0},{4,6},{6,4},{8,10},{10,8},{12,14},{14,12},{16,18},{18,... | collective-permute-start | bytes 983048 | tf_op jit(solution)/shard_map/ppermute | solution.py:40
  44.2 10.2 %collective-permute-start.7 = (bf16[128,1280]{0,1:T(8,128)(2,1)S(1)}, bf16[128,1280]{0,1:T(8,128)(2,1)}, u32[]{:S(2)}, u32[]{:S(2)}) collective-permute-start(bf16[128,1280]{0,1:T(8,128)(2,1)S(1)} %collective-permute-done.5), channel_id=1, source_target_pairs={{0,8},{2,10},{8,16},{10,18},{16,24},{18,26},{24,28},{26,30},{28,20... | collective-permute-start | bytes 983048 | tf_op jit(solution)/shard_map/ppermute | solution.py:36
  55.1 7.0 %collective-permute-start.8 = (bf16[128,1280]{0,1:T(8,128)(2,1)}, bf16[128,1280]{0,1:T(8,128)(2,1)S(1)}, u32[]{:S(2)}, u32[]{:S(2)}) collective-permute-start(bf16[128,1280]{0,1:T(8,128)(2,1)} %collective-permute-done.7), channel_id=1, source_target_pairs={{0,2},{2,0},{4,6},{6,4},{8,10},{10,8},{12,14},{14,12},{16,18},{18,... | collective-permute-start | bytes 983048 | tf_op jit(solution)/shard_map/ppermute | solution.py:40
  55.1 7.9 %collective-permute-start.17 = (bf16[128,1280]{0,1:T(8,128)(2,1)}, bf16[128,1280]{0,1:T(8,128)(2,1)S(1)}, u32[]{:S(2)}, u32[]{:S(2)}) collective-permute-start(bf16[128,1280]{0,1:T(8,128)(2,1)} %collective-permute-done.16), channel_id=1, source_target_pairs={{0,2},{2,0},{4,6},{6,4},{8,10},{10,8},{12,14},{14,12},{16,18},{18,... | collective-permute-start | bytes 983048 | tf_op jit(solution)/shard_map/ppermute | solution.py:41
  56.4 34.8 %collective-permute-start.24 = (bf16[128,1280]{0,1:T(8,128)(2,1)}, bf16[128,1280]{0,1:T(8,128)(2,1)}, u32[]{:S(2)}, u32[]{:S(2)}) collective-permute-start(bf16[128,1280]{0,1:T(8,128)(2,1)} %collective-permute-done.16), channel_id=1, source_target_pairs={{8,0},{10,2},{16,8},{18,10},{24,16},{26,18},{28,24},{30,26},{20,28... | collective-permute-start | bytes 983048 | tf_op jit(solution)/shard_map/ppermute | solution.py:37
  57.9 37.4 %collective-permute-start.18 = (bf16[128,1280]{0,1:T(8,128)(2,1)}, bf16[128,1280]{0,1:T(8,128)(2,1)}, u32[]{:S(2)}, u32[]{:S(2)}) collective-permute-start(bf16[128,1280]{0,1:T(8,128)(2,1)} %collective-permute-done.7), channel_id=1, source_target_pairs={{0,8},{2,10},{8,16},{10,18},{16,24},{18,26},{24,28},{26,30},{28,20... | collective-permute-start | bytes 983048 | tf_op jit(solution)/shard_map/ppermute | solution.py:36
  62.1 2.6 %copy-start = (bf16[10,128,1280]{1,2,0:T(8,128)(2,1)}, bf16[10,128,1280]{1,2,0:T(8,128)(2,1)S(1)}, u32[]{:S(2)}) copy-start(bf16[10,128,1280]{1,2,0:T(8,128)(2,1)S(1)} %bitcast_dynamic-update-slice_fusion.11) | copy-start | bytes 9830404
  62.1 0.8 copy-start.9
  63.0 1.0 copy-start.11
  71.0 4.8 %copy-start.10 = (bf16[128,1280]{0,1:T(8,128)(2,1)S(1)}, bf16[128,1280]{0,1:T(8,128)(2,1)}, u32[]{:S(2)}) copy-start(bf16[128,1280]{0,1:T(8,128)(2,1)} %copy-done.9) | copy-start | bytes 983044
  76.6 3.6 %copy-start.2 = (bf16[1280,5,128]{2,1,0:T(8,128)(2,1)S(1)}, bf16[1280,5,128]{2,1,0:T(8,128)(2,1)}, u32[]{:S(2)}) copy-start(bf16[1280,5,128]{2,1,0:T(8,128)(2,1)} %reshape.276) | copy-start | bytes 4915204
  91.1 4.8 %copy-start.1 = (bf16[1280,5,128]{2,1,0:T(8,128)(2,1)S(1)}, bf16[1280,5,128]{2,1,0:T(8,128)(2,1)}, u32[]{:S(2)}) copy-start(bf16[1280,5,128]{2,1,0:T(8,128)(2,1)} %reshape.268) | copy-start | bytes 4915204
  91.1 4.8 %copy-start.5 = (bf16[120,640]{0,1:T(8,128)(2,1)S(1)}, bf16[120,640]{0,1:T(8,128)(2,1)}, u32[]{:S(2)}) copy-start(bf16[120,640]{0,1:T(8,128)(2,1)} %copy.82) | copy-start | bytes 460804
  91.2 9.5 %collective-permute-start.26 = (bf16[128,1280]{0,1:T(8,128)(2,1)}, bf16[128,1280]{0,1:T(8,128)(2,1)}, u32[]{:S(2)}, u32[]{:S(2)}) collective-permute-start(bf16[128,1280]{0,1:T(8,128)(2,1)} %collective-permute-done.24), channel_id=1, source_target_pairs={{8,0},{10,2},{16,8},{18,10},{24,16},{26,18},{28,24},{30,26},{20,28... | collective-permute-start | bytes 983048 | tf_op jit(solution)/shard_map/ppermute | solution.py:37
  92.8 24.8 %collective-permute-start.25 = (bf16[128,1280]{0,1:T(8,128)(2,1)}, bf16[128,1280]{0,1:T(8,128)(2,1)}, u32[]{:S(2)}, u32[]{:S(2)}) collective-permute-start(bf16[128,1280]{0,1:T(8,128)(2,1)} %collective-permute-done.24), channel_id=1, source_target_pairs={{0,2},{2,0},{4,6},{6,4},{8,10},{10,8},{12,14},{14,12},{16,18},{18,... | collective-permute-start | bytes 983048 | tf_op jit(solution)/shard_map/ppermute | solution.py:41
  95.3 21.9 %collective-permute-start.20 = (bf16[128,1280]{0,1:T(8,128)(2,1)}, bf16[128,1280]{0,1:T(8,128)(2,1)}, u32[]{:S(2)}, u32[]{:S(2)}) collective-permute-start(bf16[128,1280]{0,1:T(8,128)(2,1)} %collective-permute-done.18), channel_id=1, source_target_pairs={{0,8},{2,10},{8,16},{10,18},{16,24},{18,26},{24,28},{26,30},{28,20... | collective-permute-start | bytes 983048 | tf_op jit(solution)/shard_map/ppermute | solution.py:36
  100.6 17.0 %collective-permute-start.27 = (bf16[128,1280]{0,1:T(8,128)(2,1)}, bf16[128,1280]{0,1:T(8,128)(2,1)}, u32[]{:S(2)}, u32[]{:S(2)}) collective-permute-start(bf16[128,1280]{0,1:T(8,128)(2,1)} %collective-permute-done.26), channel_id=1, source_target_pairs={{0,2},{2,0},{4,6},{6,4},{8,10},{10,8},{12,14},{14,12},{16,18},{18,... | collective-permute-start | bytes 983048 | tf_op jit(solution)/shard_map/ppermute | solution.py:41
  112.5 7.4 %collective-permute-start.19 = (bf16[128,1280]{0,1:T(8,128)(2,1)}, bf16[128,1280]{0,1:T(8,128)(2,1)S(1)}, u32[]{:S(2)}, u32[]{:S(2)}) collective-permute-start(bf16[128,1280]{0,1:T(8,128)(2,1)} %collective-permute-done.18), channel_id=1, source_target_pairs={{0,2},{2,0},{4,6},{6,4},{8,10},{10,8},{12,14},{14,12},{16,18},{18,... | collective-permute-start | bytes 983048 | tf_op jit(solution)/shard_map/ppermute | solution.py:40
  115.5 14.1 %collective-permute-start.28 = (bf16[128,1280]{0,1:T(8,128)(2,1)}, bf16[128,1280]{0,1:T(8,128)(2,1)}, u32[]{:S(2)}, u32[]{:S(2)}) collective-permute-start(bf16[128,1280]{0,1:T(8,128)(2,1)} %collective-permute-done.26), channel_id=1, source_target_pairs={{8,0},{10,2},{16,8},{18,10},{24,16},{26,18},{28,24},{30,26},{20,28... | collective-permute-start | bytes 983048 | tf_op jit(solution)/shard_map/ppermute | solution.py:37
  117.2 14.6 %collective-permute-start.22 = (bf16[128,1280]{0,1:T(8,128)(2,1)}, bf16[128,1280]{0,1:T(8,128)(2,1)}, u32[]{:S(2)}, u32[]{:S(2)}) collective-permute-start(bf16[128,1280]{0,1:T(8,128)(2,1)} %collective-permute-done.20), channel_id=1, source_target_pairs={{0,8},{2,10},{8,16},{10,18},{16,24},{18,26},{24,28},{26,30},{28,20... | collective-permute-start | bytes 983048 | tf_op jit(solution)/shard_map/ppermute | solution.py:36
  117.6 2.3 %collective-permute-start.21 = (bf16[128,1280]{0,1:T(8,128)(2,1)}, bf16[128,1280]{0,1:T(8,128)(2,1)S(1)}, u32[]{:S(2)}, u32[]{:S(2)}) collective-permute-start(bf16[128,1280]{0,1:T(8,128)(2,1)} %collective-permute-done.20), channel_id=1, source_target_pairs={{0,2},{2,0},{4,6},{6,4},{8,10},{10,8},{12,14},{14,12},{16,18},{18,... | collective-permute-start | bytes 983048 | tf_op jit(solution)/shard_map/ppermute | solution.py:40
  126.2 4.1 %copy-start.6 = (bf16[120,640]{0,1:T(8,128)(2,1)S(1)}, bf16[120,640]{0,1:T(8,128)(2,1)}, u32[]{:S(2)}) copy-start(bf16[120,640]{0,1:T(8,128)(2,1)} %copy.82) | copy-start | bytes 460804
  129.7 3.0 %collective-permute-start.29 = (bf16[128,1280]{0,1:T(8,128)(2,1)}, bf16[128,1280]{0,1:T(8,128)(2,1)S(1)}, u32[]{:S(2)}, u32[]{:S(2)}) collective-permute-start(bf16[128,1280]{0,1:T(8,128)(2,1)} %collective-permute-done.28), channel_id=1, source_target_pairs={{0,2},{2,0},{4,6},{6,4},{8,10},{10,8},{12,14},{14,12},{16,18},{18,... | collective-permute-start | bytes 983048 | tf_op jit(solution)/shard_map/ppermute | solution.py:41
  131.8 15.0 %collective-permute-start.23 = (bf16[128,1280]{0,1:T(8,128)(2,1)}, bf16[128,1280]{0,1:T(8,128)(2,1)}, u32[]{:S(2)}, u32[]{:S(2)}) collective-permute-start(bf16[128,1280]{0,1:T(8,128)(2,1)} %collective-permute-done.22), channel_id=1, source_target_pairs={{0,2},{2,0},{4,6},{6,4},{8,10},{10,8},{12,14},{14,12},{16,18},{18,... | collective-permute-start | bytes 983048 | tf_op jit(solution)/shard_map/ppermute | solution.py:40
  138.8 0.8 copy-start.4
  139.6 3.8 %copy-start.3 = (bf16[512,5,128]{0,2,1:T(8,128)(2,1)S(1)}, bf16[512,5,128]{0,2,1:T(8,128)(2,1)}, u32[]{:S(2)}) copy-start(bf16[512,5,128]{0,2,1:T(8,128)(2,1)} %reshape.281) | copy-start | bytes 1966084
  143.4 1.2 copy-start.7
  163.0 20.4 %copy-start.8 = (bf16[60,5120]{1,0:T(8,128)(2,1)S(1)}, bf16[60,5120]{1,0:T(8,128)(2,1)}, u32[]{:S(2)}) copy-start(bf16[60,5120]{1,0:T(8,128)(2,1)} %param.10) | copy-start | bytes 1843204
  163.0 20.3 %copy-start.12 = (f32[5120]{0:T(1024)S(1)}, f32[5120]{0:T(1024)}, u32[]{:S(2)}) copy-start(f32[5120]{0:T(1024)} %param.14) | copy-start | bytes 61444
  166.1 17.2 %collective-permute-start.30 = (bf16[60,5120]{1,0:T(8,128)(2,1)S(1)}, bf16[60,5120]{1,0:T(8,128)(2,1)S(1)}, u32[]{:S(2)}, u32[]{:S(2)}) collective-permute-start(bf16[60,5120]{1,0:T(8,128)(2,1)S(1)} %bitcast_convert_fusion), channel_id=1, source_target_pairs={{0,1},{1,0},{2,3},{3,2},{4,5},{5,4},{6,7},{7,6},{8,9},{9,8},{10,11... | collective-permute-start | bytes 1843208 | tf_op jit(solution)/shard_map/ppermute | solution.py:148

commit v5 on v4

v5 whole, which is shorter than its diff:
```python
import math

import jax
import jax.numpy as jnp
from jax import lax
from jax.sharding import PartitionSpec as P

HEAD = 128
neg_large = -1e30


def snake_ring(chips):
    half = chips // 2
    return [2 * a for a in range(half)] + [2 * a + 1 for a in reversed(range(half))]


def attend_part(queries_3d, keys, values, keeping, scale_factor):
    scores = (
        jnp.einsum("qhd,khd->hqk", queries_3d, keys, preferred_element_type=jnp.float32)
        * scale_factor
    )
    masked = jnp.where(keeping[None, None, :], scores, neg_large)
    peak = jnp.max(masked, axis=2, keepdims=True)
    weights = jnp.where(keeping[None, None, :], jnp.exp(masked - peak), 0.0)
    totals = jnp.sum(weights, axis=2, keepdims=True)
    summed = jnp.einsum(
        "hqk,khd->hqd", weights.astype(jnp.bfloat16), values, preferred_element_type=jnp.float32
    )
    return peak, totals, summed


def combine(parts, rows_dev):
    peak = parts[0][0]
    for part in parts[1:]:
        peak = jnp.maximum(peak, part[0])
    totals = 0.0
    summed = 0.0
    for part_peak, part_totals, part_summed in parts:
        factor = jnp.exp(part_peak - peak)
        totals = totals + factor * part_totals
        summed = summed + factor * part_summed
    result = (summed / totals).astype(jnp.bfloat16)
    return result.transpose(1, 0, 2).reshape(rows_dev, -1)


def solution(mesh):
    n_seq = mesh.shape["seq"]
    chips = n_seq // 2
    ring = snake_ring(chips)
    half = chips // 2
    ring_pairs = [(ring[p] * 2, ring[(p + 1) % chips] * 2) for p in range(chips)] + [
        (ring[(p + 1) % chips] * 2 + 1, ring[p] * 2 + 1) for p in range(chips)
    ]
    swap = [(i, i ^ 1) for i in range(n_seq)]

    def chip_at(pos):
        return jnp.where(pos < half, 2 * pos, 2 * (chips - 1 - pos) + 1)

    def on_device(
        hidden, queries, key_rows, value_rows, gate_scale, out_weight, valid_count, assignment
    ):
        rows_dev = queries.shape[0]
        heads_here = queries.shape[1] // HEAD
        heads_g = heads_here // 2
        cut = heads_g * HEAD
        scale_factor = 1.0 / math.sqrt(HEAD)
        me = lax.axis_index("seq")
        chip = me // 2
        core = me % 2
        first_core = core == 0
        pos = jnp.where(chip % 2 == 0, chip // 2, chips - 1 - chip // 2)
        step_dir = 1 - 2 * core

        rows_pad = (rows_dev + 1 + 7) // 8 * 8
        row_id = lax.broadcasted_iota(jnp.int32, (rows_pad - rows_dev, 2 * cut), 0)
        col_id = lax.broadcasted_iota(jnp.int32, (rows_pad - rows_dev, 2 * cut), 1)
        info = jnp.where(
            (row_id == 0) & (col_id == 0),
            valid_count[0],
            jnp.where((row_id == 0) & (col_id == 1), assignment[0], 0),
        ).astype(jnp.bfloat16)
        block_a = jnp.concatenate(
            [jnp.concatenate([key_rows[:, :cut], value_rows[:, :cut]], axis=1), info], axis=0
        )
        block_b = jnp.concatenate(
            [jnp.concatenate([key_rows[:, cut:], value_rows[:, cut:]], axis=1), info], axis=0
        )
        kept_here = jnp.where(first_core, block_a, block_b)
        given = jnp.where(first_core, block_b, block_a)
        from_mate = lax.ppermute(given, "seq", swap)
        packet = jnp.concatenate(
            [jnp.where(first_core, kept_here, from_mate), jnp.where(first_core, from_mate, kept_here)],
            axis=0,
        )

        ring_got, mate_got, ring_src, mate_src = [], [], [], []
        cur = packet
        for step in range(chips):
            if step > 0:
                cur = lax.ppermute(cur, "seq", ring_pairs)
            ring_got.append(cur)
            mate_got.append(lax.ppermute(cur, "seq", swap))
            ring_src.append(chip_at((pos - step * step_dir) % chips))
            mate_src.append(chip_at((pos + step * step_dir) % chips))
        ring_src = jnp.stack(ring_src)
        mate_src = jnp.stack(mate_src)

        known = chips // 2
        heard = ring_got[: known + 1] + mate_got[: known + 1]
        heard_chips = jnp.concatenate([ring_src[: known + 1], mate_src[: known + 1]])
        heard_ids = jnp.concatenate([heard_chips * 2, heard_chips * 2 + 1])
        extra = jnp.concatenate(
            [jnp.stack([g[rows_dev, :2] for g in heard]), jnp.stack([g[rows_pad + rows_dev, :2] for g in heard])]
        )
        extra = extra.astype(jnp.float32).astype(jnp.int32)
        counts_of, blocks_of = extra[:, 0], extra[:, 1]

        def limits_for(src):
            ids = jnp.stack([src * 2, src * 2 + 1], axis=1).reshape(-1)
            clip = jnp.max(jnp.where(ids[:, None] == heard_ids[None, :], blocks_of[None, :], -1), axis=1)
            found = jnp.max(jnp.where(clip[:, None] == heard_ids[None, :], counts_of[None, :], -1), axis=1)
            return found.reshape(-1, 2)

        limit_ring = limits_for(ring_src)
        limit_mate = limits_for(mate_src)
        within = jnp.arange(2 * rows_pad, dtype=jnp.int32)
        local = within % rows_pad
        which = within // rows_pad
        phases = [(0, known + 1), (known + 1, chips - 1), (chips - 1, chips)]
        phases = [(lo, hi) for lo, hi in phases if hi > lo]
        q_a = queries[:, :cut].reshape(rows_dev, heads_g, HEAD)
        q_b = queries[:, cut:].reshape(rows_dev, heads_g, HEAD)
        q_ring = jnp.where(first_core, q_a, q_b)
        q_mate = jnp.where(first_core, q_b, q_a)

        def group(got, limits, q3):
            parts = []
            for lo, hi in phases:
                stack = jnp.concatenate(got[lo:hi], axis=0)
                keys = stack[:, :cut].reshape(-1, heads_g, HEAD)
                values = stack[:, cut:].reshape(-1, heads_g, HEAD)
                bound = jnp.take_along_axis(limits[lo:hi], jnp.broadcast_to(which[None, :], (hi - lo, 2 * rows_pad)), axis=1)
                keeping = (local[None, :] < bound).reshape(-1)
                parts.append(attend_part(q3, keys, values, keeping, scale_factor))
            return combine(parts, rows_dev)

        out_ring = group(ring_got, limit_ring, q_ring)
        out_mate = group(mate_got, limit_mate, q_mate)
        attention = jnp.concatenate(
            [jnp.where(first_core, out_ring, out_mate), jnp.where(first_core, out_mate, out_ring)], axis=1
        )
        partial = jnp.dot(attention, out_weight, preferred_element_type=jnp.float32)
        rows_out = hidden.shape[0]
        side = lax.axis_index("tp")
        n_tp = rows_dev // rows_out
        pieces = partial.reshape(n_tp, rows_out, partial.shape[1])
        own = jnp.take(pieces, side, axis=0)
        other = jnp.take(pieces, 1 - side, axis=0).astype(jnp.bfloat16)
        came = lax.ppermute(other, "tp", [(0, 1), (1, 0)])
        summed = own + came.astype(jnp.float32)
        return (hidden.astype(jnp.float32) + gate_scale * summed).astype(jnp.bfloat16)

    placed = (
        P(("seq", "tp"), None),
        P("seq", "tp"),
        P("seq", "tp"),
        P("seq", "tp"),
        P(),
        P("tp", None),
        P("seq"),
        P("seq"),
    )
    return jax.shard_map(
        on_device, mesh=mesh, in_specs=placed, out_specs=P(("seq", "tp"), None), check_vma=False
    )
```

time: 187 us -> 152 us (0.81)
  local copies, waits for them, and re-layouts: 81.4 us -> 52 us
  waiting for transfers between devices: 35.8 us -> 54.1 us
  matrix products: 27.2 us -> 13.2 us
  other arithmetic: 19.9 us -> 13.8 us
  starting transfers between devices: 19.6 us -> 16.8 us
    reshape x12 -> x0, local copies, waits for them, and re-layouts: 24.3 us -> none  [the longest x6 13.5 us: half(): keys = stack[:, :, :width].reshape(-1, hi - lo, HEAD)]
    gather x0 -> x11, local copies, waits for them, and re-layouts: none -> 21.7 us  [group(): jnp.take_along_axis(limits[lo:hi], jnp.broadcast_to(which[None, :], (hi -...]
    ppermute x30 -> x16, waiting for transfers between devices: 20.1 us -> 38.6 us  [the longest x7 37.3 us: on_device(): cur = lax.ppermute(cur, 'seq', ring_pairs)]
    slice x23 -> x24, local copies, waits for them, and re-layouts: 27.6 us -> 10.1 us  [the longest x2 5.81 us: group(): keys = stack[:, :cut].reshape(-1, heads_g, HEAD)]
    unnamed x46 -> x34, local copies, waits for them, and re-layouts: 17.1 us -> 8.12 us
    dot_general x6, matrix products: 11 us -> 3.37 us  [attend_part(): jnp.einsum('hqk,khd->hqd', weights.astype(jnp.bfloat16), values, preferre...]
    dot_general x6, matrix products: 9.5 us -> 3.17 us  [attend_part(): jnp.einsum('qhd,khd->hqk', queries_3d, keys, preferred_element_type=jnp.f...]
    concatenate x1 -> x6, local copies, waits for them, and re-layouts: 0.11 us -> 5.77 us  [the longest x4 4.36 us: group(): stack = jnp.concatenate(got[lo:hi], axis=0)]
  transfers between devices with their start and end apart: 31 -> 17, of which waited for: 7 -> 10; matrix products, arithmetic and copies ran while one was open for 52% -> 35% of each run, Pallas kernels for 0% -> 0%
where the time goes in v5:
time: 152 us
  waiting for transfers between devices  54.1 us (36%)
  local copies, waits for them, and re-layouts  52 us (34%)
  starting transfers between devices  16.8 us (11%)
  other arithmetic  13.8 us (9%)
  matrix products  13.2 us (9%)
  between operations  1.87 us (1%)
    ppermute x7, waiting for transfers between devices, on_device(): cur = lax.ppermute(cur, 'seq', ring_pairs)  37.3 us
    gather x11, local copies, waits for them, and re-layouts, group(): jnp.take_along_axis(limits[lo:hi], jnp.broadcast_to(which[None, :], (hi -...  21.7 us
    ppermute x1, waiting for transfers between devices, on_device(): came = lax.ppermute(other, 'tp', [(0, 1), (1, 0)])  15.4 us
    ppermute x7, starting transfers between devices, on_device(): cur = lax.ppermute(cur, 'seq', ring_pairs)  14.5 us
    unnamed x34, local copies, waits for them, and re-layouts  8.12 us
    dot_general x1, matrix products, on_device(): partial = jnp.dot(attention, out_weight, preferred_element_type=jnp.float32)  6.65 us
    slice x2, local copies, waits for them, and re-layouts, group(): keys = stack[:, :cut].reshape(-1, heads_g, HEAD)  5.81 us
    concatenate x4, local copies, waits for them, and re-layouts, group(): stack = jnp.concatenate(got[lo:hi], axis=0)  4.36 us
  transfers between devices with their start and end apart: 17, of which 10 were waited for; matrix products, arithmetic and copies ran while one was open for 35% of the time, Pallas kernels for 0%

profile of v5, /device:TPU:0, one launch (start us, length us, event | category | flops | bytes accessed | tf_op | source)
XLA Modules:
  0.0 151.7 jit_solution(16290924282180412719)
XLA Ops:
  1.3 1.0 fusion.125
  2.5 1.0 fusion.124
  4.1 0.9 select_convert_fusion
  5.3 0.5 collective-permute-start
  7.1 1.1 constant_dynamic-update-slice_fusion.5
  8.2 1.1 constant_dynamic-update-slice_fusion.4
  9.3 3.0 %collective-permute-start.1 = (bf16[256,1280]{0,1:T(8,128)(2,1)S(1)}, bf16[256,1280]{0,1:T(8,128)(2,1)}, u32[]{:S(2)}, u32[]{:S(2)}) collective-permute-start(bf16[256,1280]{0,1:T(8,128)(2,1)S(1)} %pad_maximum_fusion), channel_id=1, source_target_pairs={{0,8},{8,16},{16,24},{24,28},{28,20},{20,12},{12,4},{4,0},{10,2},{... | collective-permute-start | bytes 1966088 | tf_op jit(solution)/shard_map/ppermute | solution.py:100
  12.3 0.8 copy.85
  13.4 0.6 slice.277
  14.0 0.7 slice.287
  14.7 6.3 %collective-permute-done.1 = bf16[256,1280]{0,1:T(8,128)(2,1)} collective-permute-done((bf16[256,1280]{0,1:T(8,128)(2,1)S(1)}, bf16[256,1280]{0,1:T(8,128)(2,1)}, u32[]{:S(2)}, u32[]{:S(2)}) %collective-permute-start.1) | collective-permute-done | bytes 655392 | tf_op jit(solution)/shard_map/ppermute | solution.py:100
  20.9 2.1 %collective-permute-start.2 = (bf16[256,1280]{0,1:T(8,128)(2,1)}, bf16[256,1280]{0,1:T(8,128)(2,1)S(1)}, u32[]{:S(2)}, u32[]{:S(2)}) collective-permute-start(bf16[256,1280]{0,1:T(8,128)(2,1)} %collective-permute-done.1), channel_id=1, source_target_pairs={{0,8},{8,16},{16,24},{24,28},{28,20},{20,12},{12,4},{4,0},{10,2},{... | collective-permute-start | bytes 1966088 | tf_op jit(solution)/shard_map/ppermute | solution.py:100
  23.0 2.1 %constant_dynamic-update-slice_fusion.3 = bf16[1280,1280]{0,1:T(8,128)(2,1)} fusion(bf16[1280,1280]{0,1:T(8,128)(2,1)} %get-tuple-element.28, bf16[256,1280]{0,1:T(8,128)(2,1)} %collective-permute-done.1), kind=kLoop, calls=%fused_computation.98 | loop fusion | bytes 1310720
  25.1 0.8 fusion.123
  26.0 5.7 %collective-permute-done.2 = bf16[256,1280]{0,1:T(8,128)(2,1)S(1)} collective-permute-done((bf16[256,1280]{0,1:T(8,128)(2,1)}, bf16[256,1280]{0,1:T(8,128)(2,1)S(1)}, u32[]{:S(2)}, u32[]{:S(2)}) %collective-permute-start.2) | collective-permute-done | bytes 655392 | tf_op jit(solution)/shard_map/ppermute | solution.py:100
  31.7 2.1 %collective-permute-start.3 = (bf16[256,1280]{0,1:T(8,128)(2,1)S(1)}, bf16[256,1280]{0,1:T(8,128)(2,1)S(1)}, u32[]{:S(2)}, u32[]{:S(2)}) collective-permute-start(bf16[256,1280]{0,1:T(8,128)(2,1)S(1)} %collective-permute-done.2), channel_id=1, source_target_pairs={{0,8},{8,16},{16,24},{24,28},{28,20},{20,12},{12,4},{4,0},{10,2},{... | collective-permute-start | bytes 1966088 | tf_op jit(solution)/shard_map/ppermute | solution.py:100
  33.8 0.9 constant_dynamic-update-slice_fusion.2
  35.0 7.4 %collective-permute-done.3 = bf16[256,1280]{0,1:T(8,128)(2,1)S(1)} collective-permute-done((bf16[256,1280]{0,1:T(8,128)(2,1)S(1)}, bf16[256,1280]{0,1:T(8,128)(2,1)S(1)}, u32[]{:S(2)}, u32[]{:S(2)}) %collective-permute-start.3) | collective-permute-done | bytes 655392 | tf_op jit(solution)/shard_map/ppermute | solution.py:100
  42.3 2.1 %collective-permute-start.4 = (bf16[256,1280]{0,1:T(8,128)(2,1)S(1)}, bf16[256,1280]{0,1:T(8,128)(2,1)}, u32[]{:S(2)}, u32[]{:S(2)}) collective-permute-start(bf16[256,1280]{0,1:T(8,128)(2,1)S(1)} %collective-permute-done.3), channel_id=1, source_target_pairs={{0,8},{8,16},{16,24},{24,28},{28,20},{20,12},{12,4},{4,0},{10,2},{... | collective-permute-start | bytes 1966088 | tf_op jit(solution)/shard_map/ppermute | solution.py:100
  44.4 0.9 constant_dynamic-update-slice_fusion.1
  45.5 7.5 %collective-permute-done.4 = bf16[256,1280]{0,1:T(8,128)(2,1)} collective-permute-done((bf16[256,1280]{0,1:T(8,128)(2,1)S(1)}, bf16[256,1280]{0,1:T(8,128)(2,1)}, u32[]{:S(2)}, u32[]{:S(2)}) %collective-permute-start.4) | collective-permute-done | bytes 655392 | tf_op jit(solution)/shard_map/ppermute | solution.py:100
  53.0 2.1 %collective-permute-start.10 = (bf16[256,1280]{0,1:T(8,128)(2,1)}, bf16[256,1280]{0,1:T(8,128)(2,1)}, u32[]{:S(2)}, u32[]{:S(2)}) collective-permute-start(bf16[256,1280]{0,1:T(8,128)(2,1)} %collective-permute-done.4), channel_id=1, source_target_pairs={{0,8},{8,16},{16,24},{24,28},{28,20},{20,12},{12,4},{4,0},{10,2},{... | collective-permute-start | bytes 1966088 | tf_op jit(solution)/shard_map/ppermute | solution.py:100
  55.1 0.8 fusion.120
  55.9 2.0 %constant_dynamic-update-slice_fusion = bf16[1280,1280]{0,1:T(8,128)(2,1)} fusion(bf16[1280,1280]{0,1:T(8,128)(2,1)} %constant_dynamic-update-slice_fusion.1, bf16[256,1280]{0,1:T(8,128)(2,1)} %collective-permute-done.4), kind=kLoop, calls=%fused_computation.95 | loop fusion | bytes 1310720 | tf_op jit(solution)/shard_map/concatenate | solution.py:139
  58.0 3.9 %fusion.109 = (bf16[1280,640]{0,1:T(8,128)(2,1)}, bf16[1280,640]{0,1:T(8,128)(2,1)}) fusion(bf16[1280,1280]{0,1:T(8,128)(2,1)} %constant_dynamic-update-slice_fusion), kind=kLoop, calls=%fused_computation.202 | loop fusion | bytes 6553600 | tf_op jit(solution)/shard_map/slice | solution.py:140
  61.9 0.8 fusion.115
  62.7 1.3 concatenate.72
  64.0 0.6 convert_convert_fusion
  65.3 5.5 %gather_fusion = s32[1280]{0:T(1024)S(1)} fusion(s32[5,2]{1,0:T(8,128)S(1)} %slice.219, s32[1280]{0:T(1024)S(1)} %reshape.831), kind=kCustom, calls=%fused_computation.clone | custom fusion | bytes 20480 | tf_op jit(solution)/shard_map/jit(take_along_axis)/gather | solution.py:142
  71.0 5.5 %gather_fusion.2 = s32[1280]{0:T(1024)S(1)} fusion(s32[5,2]{1,0:T(8,128)S(1)} %slice.233, s32[1280]{0:T(1024)S(1)} %reshape.831), kind=kCustom, calls=%fused_computation.2.clone | custom fusion | bytes 20480 | tf_op jit(solution)/shard_map/jit(take_along_axis)/gather | solution.py:142
  76.6 4.7 %gather_fusion.1 = s32[512]{0:T(512)S(1)} fusion(s32[2,2]{1,0:T(2,128)S(1)} %slice.224, s32[512]{0:T(512)S(1)} %bitcast.261), kind=kCustom, calls=%fused_computation.1.clone | custom fusion | bytes 8192 | tf_op jit(solution)/shard_map/jit(take_along_axis)/gather | solution.py:142
  81.4 4.7 %gather_fusion.3 = s32[512]{0:T(512)S(1)} fusion(s32[2,2]{1,0:T(2,128)S(1)} %slice.236, s32[512]{0:T(512)S(1)} %bitcast.262), kind=kCustom, calls=%fused_computation.3.clone | custom fusion | bytes 8192 | tf_op jit(solution)/shard_map/jit(take_along_axis)/gather | solution.py:142
  86.2 1.1 constant_dynamic-update-slice_fusion.8
  87.4 1.9 %fusion.110 = (bf16[1280,640]{0,1:T(8,128)(2,1)}, bf16[1280,640]{0,1:T(8,128)(2,1)}) fusion(bf16[1280,1280]{0,1:T(8,128)(2,1)S(1)} %constant_dynamic-update-slice_fusion.8), kind=kLoop, calls=%fused_computation.203 | loop fusion | bytes 6553600 | tf_op jit(solution)/shard_map/slice | solution.py:140
  89.4 0.7 fusion.128
  90.3 0.6 fusion.2
  90.9 0.9 copy-done
  91.9 0.9 copy-done.3
  92.8 0.8 fusion.131
  93.6 1.6 %collective-permute-start.11 = (bf16[256,1280]{0,1:T(8,128)(2,1)}, bf16[256,1280]{0,1:T(8,128)(2,1)}, u32[]{:S(2)}, u32[]{:S(2)}) collective-permute-start(bf16[256,1280]{0,1:T(8,128)(2,1)} %collective-permute-done.10), channel_id=1, source_target_pairs={{0,8},{8,16},{16,24},{24,28},{28,20},{20,12},{12,4},{4,0},{10,2},{... | collective-permute-start | bytes 1966088 | tf_op jit(solution)/shard_map/ppermute | solution.py:100
  95.2 0.6 fusion.126
  95.9 1.3 compare_reduce_fusion.1
  97.2 0.6 fusion.127
  97.8 1.3 compare_reduce_fusion
  99.1 0.6 fusion.4
  99.7 1.1 constant_dynamic-update-slice_fusion.7
  100.8 3.7 %collective-permute-done.11 = bf16[256,1280]{0,1:T(8,128)(2,1)} collective-permute-done((bf16[256,1280]{0,1:T(8,128)(2,1)}, bf16[256,1280]{0,1:T(8,128)(2,1)}, u32[]{:S(2)}, u32[]{:S(2)}) %collective-permute-start.11) | collective-permute-done | bytes 655392 | tf_op jit(solution)/shard_map/ppermute | solution.py:100
  104.5 1.6 %collective-permute-start.12 = (bf16[256,1280]{0,1:T(8,128)(2,1)}, bf16[256,1280]{0,1:T(8,128)(2,1)S(1)}, u32[]{:S(2)}, u32[]{:S(2)}) collective-permute-start(bf16[256,1280]{0,1:T(8,128)(2,1)} %collective-permute-done.11), channel_id=1, source_target_pairs={{0,8},{8,16},{16,24},{24,28},{28,20},{20,12},{12,4},{4,0},{10,2},{... | collective-permute-start | bytes 1966088 | tf_op jit(solution)/shard_map/ppermute | solution.py:100
  106.1 1.2 constant_dynamic-update-slice_fusion.6
  107.4 0.5 fusion.130
  107.9 0.4 fusion.47
  108.6 6.7 %collective-permute-done.12 = bf16[256,1280]{0,1:T(8,128)(2,1)S(1)} collective-permute-done((bf16[256,1280]{0,1:T(8,128)(2,1)}, bf16[256,1280]{0,1:T(8,128)(2,1)S(1)}, u32[]{:S(2)}, u32[]{:S(2)}) %collective-permute-start.12) | collective-permute-done | bytes 655392 | tf_op jit(solution)/shard_map/ppermute | solution.py:100
  116.1 0.9 fusion.36
  117.0 0.5 fusion.133
  117.9 0.5 fusion.28
  118.7 0.9 collective-permute-done.15
  120.4 0.9 fusion.42
  121.2 0.5 fusion.30
  122.4 6.6 %fusion.63 = f32[120,5120]{1,0:T(8,128)S(1)} fusion(bf16[1280,5120]{1,0:T(8,128)(2,1)} %param.21, bf16[120,640]{0,1:T(8,128)(2,1)S(1)} %bitcast.279, bf16[120,640]{0,1:T(8,128)(2,1)S(1)} %bitcast.280), kind=kOutput, calls=%fused_computation.77 | convolution fusion | flops 1573478400 | bytes 15872000 | tf_op jit(solution)/shard_map/dot_general | solution.py:152
  129.1 1.7 %reshape.685 = f32[2,60,5120]{2,1,0:T(8,128)} reshape(f32[120,5120]{1,0:T(8,128)S(1)} %fusion.63) | data formatting | bytes 4915200 | tf_op jit(solution)/shard_map/reshape | solution.py:156
  130.8 1.5 bitcast_convert_fusion
  132.3 1.6 %collective-permute-start.16 = (bf16[60,5120]{1,0:T(8,128)(2,1)S(1)}, bf16[60,5120]{1,0:T(8,128)(2,1)S(1)}, u32[]{:S(2)}, u32[]{:S(2)}) collective-permute-start(bf16[60,5120]{1,0:T(8,128)(2,1)S(1)} %bitcast_convert_fusion), channel_id=1, source_target_pairs={{0,1},{1,0},{2,3},{3,2},{4,5},{5,4},{6,7},{7,6},{8,9},{9,8},{10,11... | collective-permute-start | bytes 1843208 | tf_op jit(solution)/shard_map/ppermute | solution.py:159
  133.8 15.4 %collective-permute-done.16 = bf16[60,5120]{1,0:T(8,128)(2,1)S(1)} collective-permute-done((bf16[60,5120]{1,0:T(8,128)(2,1)S(1)}, bf16[60,5120]{1,0:T(8,128)(2,1)S(1)}, u32[]{:S(2)}, u32[]{:S(2)}) %collective-permute-start.16) | collective-permute-done | bytes 614432 | tf_op jit(solution)/shard_map/ppermute | solution.py:159
  149.3 2.4 %fusion.20 = bf16[60,5120]{1,0:T(8,128)(2,1)} fusion(f32[2,60,5120]{2,1,0:T(8,128)} %reshape.685, s32[]{:T(128)S(6)} %select_n.413, bf16[60,5120]{1,0:T(8,128)(2,1)S(1)} %collective-permute-done.16, bf16[60,5120]{1,0:T(8,128)(2,1)S(1)} %copy-done.7, f32[5120]{0:T(1024)S(1)} %copy-done.9, pred[]{:T(512)S(6)} %and.226), kind=kLoop, calls=%fused_computation.30 | loop fusion | flops 2150400 | bytes 3092485 | tf_op jit(solution)/shard_map/convert_element_type | solution.py:161
  (113 shorter events, 7.8 us)
Async XLA Ops:
  3.5 2.3 %copy-start.8 = (bf16[120,1280]{1,0:T(8,128)(2,1)S(1)}, bf16[120,1280]{1,0:T(8,128)(2,1)}, u32[]{:S(2)}) copy-start(bf16[120,1280]{1,0:T(8,128)(2,1)} %param.17) | copy-start | bytes 921604
  5.3 1.8 %collective-permute-start = (bf16[128,1280]{0,1:T(8,128)(2,1)S(1)}, bf16[128,1280]{0,1:T(8,128)(2,1)S(1)}, u32[]{:S(2)}, u32[]{:S(2)}) collective-permute-start(bf16[128,1280]{0,1:T(8,128)(2,1)S(1)} %broadcast_select_fusion.2), channel_id=1, source_target_pairs={{0,2},{2,0},{4,6},{6,4},{8,10},{10,8},{12,14},{14,12},{16,18},{18,... | collective-permute-start | bytes 983048 | tf_op jit(solution)/shard_map/ppermute | solution.py:90
  9.3 11.6 %collective-permute-start.1 = (bf16[256,1280]{0,1:T(8,128)(2,1)S(1)}, bf16[256,1280]{0,1:T(8,128)(2,1)}, u32[]{:S(2)}, u32[]{:S(2)}) collective-permute-start(bf16[256,1280]{0,1:T(8,128)(2,1)S(1)} %pad_maximum_fusion), channel_id=1, source_target_pairs={{0,8},{8,16},{16,24},{24,28},{28,20},{20,12},{12,4},{4,0},{10,2},{... | collective-permute-start | bytes 1966088 | tf_op jit(solution)/shard_map/ppermute | solution.py:100
  13.2 12.7 %collective-permute-start.5 = (bf16[256,1280]{0,1:T(8,128)(2,1)S(1)}, bf16[256,1280]{0,1:T(8,128)(2,1)S(1)}, u32[]{:S(2)}, u32[]{:S(2)}) collective-permute-start(bf16[256,1280]{0,1:T(8,128)(2,1)S(1)} %pad_maximum_fusion), channel_id=1, source_target_pairs={{0,2},{2,0},{4,6},{6,4},{8,10},{10,8},{12,14},{14,12},{16,18},{18,... | collective-permute-start | bytes 1966088 | tf_op jit(solution)/shard_map/ppermute | solution.py:102
  20.9 10.8 %collective-permute-start.2 = (bf16[256,1280]{0,1:T(8,128)(2,1)}, bf16[256,1280]{0,1:T(8,128)(2,1)S(1)}, u32[]{:S(2)}, u32[]{:S(2)}) collective-permute-start(bf16[256,1280]{0,1:T(8,128)(2,1)} %collective-permute-done.1), channel_id=1, source_target_pairs={{0,8},{8,16},{16,24},{24,28},{28,20},{20,12},{12,4},{4,0},{10,2},{... | collective-permute-start | bytes 1966088 | tf_op jit(solution)/shard_map/ppermute | solution.py:100
  23.0 11.8 %collective-permute-start.6 = (bf16[256,1280]{0,1:T(8,128)(2,1)}, bf16[256,1280]{0,1:T(8,128)(2,1)S(1)}, u32[]{:S(2)}, u32[]{:S(2)}) collective-permute-start(bf16[256,1280]{0,1:T(8,128)(2,1)} %collective-permute-done.1), channel_id=1, source_target_pairs={{0,2},{2,0},{4,6},{6,4},{8,10},{10,8},{12,14},{14,12},{16,18},{18,... | collective-permute-start | bytes 1966088 | tf_op jit(solution)/shard_map/ppermute | solution.py:102
  31.7 10.6 %collective-permute-start.3 = (bf16[256,1280]{0,1:T(8,128)(2,1)S(1)}, bf16[256,1280]{0,1:T(8,128)(2,1)S(1)}, u32[]{:S(2)}, u32[]{:S(2)}) collective-permute-start(bf16[256,1280]{0,1:T(8,128)(2,1)S(1)} %collective-permute-done.2), channel_id=1, source_target_pairs={{0,8},{8,16},{16,24},{24,28},{28,20},{20,12},{12,4},{4,0},{10,2},{... | collective-permute-start | bytes 1966088 | tf_op jit(solution)/shard_map/ppermute | solution.py:100
  33.8 11.6 %collective-permute-start.7 = (bf16[256,1280]{0,1:T(8,128)(2,1)S(1)}, bf16[256,1280]{0,1:T(8,128)(2,1)S(1)}, u32[]{:S(2)}, u32[]{:S(2)}) collective-permute-start(bf16[256,1280]{0,1:T(8,128)(2,1)S(1)} %collective-permute-done.2), channel_id=1, source_target_pairs={{0,2},{2,0},{4,6},{6,4},{8,10},{10,8},{12,14},{14,12},{16,18},{18,... | collective-permute-start | bytes 1966088 | tf_op jit(solution)/shard_map/ppermute | solution.py:102
  42.3 10.7 %collective-permute-start.4 = (bf16[256,1280]{0,1:T(8,128)(2,1)S(1)}, bf16[256,1280]{0,1:T(8,128)(2,1)}, u32[]{:S(2)}, u32[]{:S(2)}) collective-permute-start(bf16[256,1280]{0,1:T(8,128)(2,1)S(1)} %collective-permute-done.3), channel_id=1, source_target_pairs={{0,8},{8,16},{16,24},{24,28},{28,20},{20,12},{12,4},{4,0},{10,2},{... | collective-permute-start | bytes 1966088 | tf_op jit(solution)/shard_map/ppermute | solution.py:100
  44.4 13.5 %collective-permute-start.8 = (bf16[256,1280]{0,1:T(8,128)(2,1)S(1)}, bf16[256,1280]{0,1:T(8,128)(2,1)S(1)}, u32[]{:S(2)}, u32[]{:S(2)}) collective-permute-start(bf16[256,1280]{0,1:T(8,128)(2,1)S(1)} %collective-permute-done.3), channel_id=1, source_target_pairs={{0,2},{2,0},{4,6},{6,4},{8,10},{10,8},{12,14},{14,12},{16,18},{18,... | collective-permute-start | bytes 1966088 | tf_op jit(solution)/shard_map/ppermute | solution.py:102
  53.0 8.9 %collective-permute-start.9 = (bf16[256,1280]{0,1:T(8,128)(2,1)}, bf16[256,1280]{0,1:T(8,128)(2,1)}, u32[]{:S(2)}, u32[]{:S(2)}) collective-permute-start(bf16[256,1280]{0,1:T(8,128)(2,1)} %collective-permute-done.4), channel_id=1, source_target_pairs={{0,2},{2,0},{4,6},{6,4},{8,10},{10,8},{12,14},{14,12},{16,18},{18,... | collective-permute-start | bytes 1966088 | tf_op jit(solution)/shard_map/ppermute | solution.py:102
  53.0 40.6 %collective-permute-start.10 = (bf16[256,1280]{0,1:T(8,128)(2,1)}, bf16[256,1280]{0,1:T(8,128)(2,1)}, u32[]{:S(2)}, u32[]{:S(2)}) collective-permute-start(bf16[256,1280]{0,1:T(8,128)(2,1)} %collective-permute-done.4), channel_id=1, source_target_pairs={{0,8},{8,16},{16,24},{24,28},{28,20},{20,12},{12,4},{4,0},{10,2},{... | collective-permute-start | bytes 1966088 | tf_op jit(solution)/shard_map/ppermute | solution.py:100
  87.3 2.1 %copy-start.2 = (bf16[1280,640]{0,1:T(8,128)(2,1)S(1)}, bf16[1280,640]{0,1:T(8,128)(2,1)}, u32[]{:S(2)}) copy-start(bf16[1280,640]{0,1:T(8,128)(2,1)} %get-tuple-element.36) | copy-start | bytes 4915204
  90.2 1.7 %copy-start = (f32[5,120,1280]{2,1,0:T(8,128)}, f32[5,120,1280]{2,1,0:T(8,128)S(1)}, u32[]{:S(2)}) copy-start(f32[5,120,1280]{2,1,0:T(8,128)S(1)} %get-tuple-element.91) | copy-start | bytes 9216004
  90.2 1.7 %copy-start.4 = (bf16[120,640]{0,1:T(8,128)(2,1)S(1)}, bf16[120,640]{0,1:T(8,128)(2,1)}, u32[]{:S(2)}) copy-start(bf16[120,640]{0,1:T(8,128)(2,1)} %copy.85) | copy-start | bytes 460804
  90.3 2.5 %copy-start.3 = (bf16[1280,640]{0,1:T(8,128)(2,1)S(1)}, bf16[1280,640]{0,1:T(8,128)(2,1)}, u32[]{:S(2)}) copy-start(bf16[1280,640]{0,1:T(8,128)(2,1)} %get-tuple-element.38) | copy-start | bytes 4915204
  93.6 11.0 %collective-permute-start.11 = (bf16[256,1280]{0,1:T(8,128)(2,1)}, bf16[256,1280]{0,1:T(8,128)(2,1)}, u32[]{:S(2)}, u32[]{:S(2)}) collective-permute-start(bf16[256,1280]{0,1:T(8,128)(2,1)} %collective-permute-done.10), channel_id=1, source_target_pairs={{0,8},{8,16},{16,24},{24,28},{28,20},{20,12},{12,4},{4,0},{10,2},{... | collective-permute-start | bytes 1966088 | tf_op jit(solution)/shard_map/ppermute | solution.py:100
  95.8 11.6 %collective-permute-start.13 = (bf16[256,1280]{0,1:T(8,128)(2,1)}, bf16[256,1280]{0,1:T(8,128)(2,1)S(1)}, u32[]{:S(2)}, u32[]{:S(2)}) collective-permute-start(bf16[256,1280]{0,1:T(8,128)(2,1)} %collective-permute-done.10), channel_id=1, source_target_pairs={{0,2},{2,0},{4,6},{6,4},{8,10},{10,8},{12,14},{14,12},{16,18},{18,... | collective-permute-start | bytes 1966088 | tf_op jit(solution)/shard_map/ppermute | solution.py:102
  104.5 10.8 %collective-permute-start.12 = (bf16[256,1280]{0,1:T(8,128)(2,1)}, bf16[256,1280]{0,1:T(8,128)(2,1)S(1)}, u32[]{:S(2)}, u32[]{:S(2)}) collective-permute-start(bf16[256,1280]{0,1:T(8,128)(2,1)} %collective-permute-done.11), channel_id=1, source_target_pairs={{0,8},{8,16},{16,24},{24,28},{28,20},{20,12},{12,4},{4,0},{10,2},{... | collective-permute-start | bytes 1966088 | tf_op jit(solution)/shard_map/ppermute | solution.py:100
  106.1 2.3 %collective-permute-start.14 = (bf16[256,1280]{0,1:T(8,128)(2,1)}, bf16[256,1280]{0,1:T(8,128)(2,1)S(1)}, u32[]{:S(2)}, u32[]{:S(2)}) collective-permute-start(bf16[256,1280]{0,1:T(8,128)(2,1)} %collective-permute-done.11), channel_id=1, source_target_pairs={{0,2},{2,0},{4,6},{6,4},{8,10},{10,8},{12,14},{14,12},{16,18},{18,... | collective-permute-start | bytes 1966088 | tf_op jit(solution)/shard_map/ppermute | solution.py:102
  108.5 7.6 %copy-start.5 = (bf16[1280,640]{0,1:T(8,128)(2,1)S(1)}, bf16[1280,640]{0,1:T(8,128)(2,1)}, u32[]{:S(2)}) copy-start(bf16[1280,640]{0,1:T(8,128)(2,1)} %get-tuple-element.37) | copy-start | bytes 4915204
  108.6 7.5 %copy-start.1 = (f32[5,120,1280]{2,1,0:T(8,128)S(1)}, f32[5,120,1280]{2,1,0:T(8,128)}, u32[]{:S(2)}) copy-start(f32[5,120,1280]{2,1,0:T(8,128)} %copy-done) | copy-start | bytes 9216004
  117.4 2.2 %collective-permute-start.15 = (bf16[256,1280]{0,1:T(8,128)(2,1)S(1)}, bf16[256,1280]{0,1:T(8,128)(2,1)S(1)}, u32[]{:S(2)}, u32[]{:S(2)}) collective-permute-start(bf16[256,1280]{0,1:T(8,128)(2,1)S(1)} %collective-permute-done.12), channel_id=1, source_target_pairs={{0,2},{2,0},{4,6},{6,4},{8,10},{10,8},{12,14},{14,12},{16,18},{18,... | collective-permute-start | bytes 1966088 | tf_op jit(solution)/shard_map/ppermute | solution.py:102
  118.7 1.6 %copy-start.6 = (bf16[1280,640]{0,1:T(8,128)(2,1)S(1)}, bf16[1280,640]{0,1:T(8,128)(2,1)}, u32[]{:S(2)}) copy-start(bf16[1280,640]{0,1:T(8,128)(2,1)} %get-tuple-element.39) | copy-start | bytes 4915204
  129.1 20.2 %copy-start.9 = (f32[5120]{0:T(1024)S(1)}, f32[5120]{0:T(1024)}, u32[]{:S(2)}) copy-start(f32[5120]{0:T(1024)} %param.20) | copy-start | bytes 61444
  130.8 18.5 %copy-start.7 = (bf16[60,5120]{1,0:T(8,128)(2,1)S(1)}, bf16[60,5120]{1,0:T(8,128)(2,1)}, u32[]{:S(2)}) copy-start(bf16[60,5120]{1,0:T(8,128)(2,1)} %param.16) | copy-start | bytes 1843204
  132.3 17.0 %collective-permute-start.16 = (bf16[60,5120]{1,0:T(8,128)(2,1)S(1)}, bf16[60,5120]{1,0:T(8,128)(2,1)S(1)}, u32[]{:S(2)}, u32[]{:S(2)}) collective-permute-start(bf16[60,5120]{1,0:T(8,128)(2,1)S(1)} %bitcast_convert_fusion), channel_id=1, source_target_pairs={{0,1},{1,0},{2,3},{3,2},{4,5},{5,4},{6,7},{7,6},{8,9},{9,8},{10,11... | collective-permute-start | bytes 1843208 | tf_op jit(solution)/shard_map/ppermute | solution.py:159

commit v6 on v4

--- a/solution.py
+++ b/solution.py
@@ -128,9 +128,9 @@
             q3 = queries[:, lo * HEAD : hi * HEAD].reshape(rows_dev, hi - lo, HEAD)
             parts = []
             for first, last in phases:
-                stack = jnp.stack(got[first:last])
-                keys = stack[:, :, :width].reshape(-1, hi - lo, HEAD)
-                values = stack[:, :, width:].reshape(-1, hi - lo, HEAD)
+                stack = jnp.concatenate(got[first:last], axis=0)
+                keys = stack[:, :width].reshape(-1, hi - lo, HEAD)
+                values = stack[:, width:].reshape(-1, hi - lo, HEAD)
                 keeping = (within[None, :] < limits[first:last, None]).reshape(-1)
                 parts.append(attend_part(q3, keys, values, keeping, scale_factor))
             return combine(parts, rows_dev)

time: 187 us -> 141 us (0.75)
  local copies, waits for them, and re-layouts: 81.4 us -> 40.4 us
  waiting for transfers between devices: 35.8 us -> 54.1 us
  matrix products: 27.2 us -> 13.8 us
  other arithmetic: 19.9 us -> 10.2 us
    reshape x12 -> x0, local copies, waits for them, and re-layouts: 24.3 us -> none  [the longest x6 13.5 us: half(): keys = stack[:, :, :width].reshape(-1, hi - lo, HEAD)]
    ppermute x7, waiting for transfers between devices: 10.2 us -> 33 us  [gather_ring(): cur_a = lax.ppermute(cur_a, 'seq', forward)]
    slice x16 -> x6, local copies, waits for them, and re-layouts: 22.7 us -> 5.58 us  [the longest x2 3.28 us: half(): keys = stack[:, :width].reshape(-1, hi - lo, HEAD)]
    concatenate x0 -> x6, local copies, waits for them, and re-layouts: none -> 11.6 us  [half(): stack = jnp.concatenate(got[first:last], axis=0)]
    unnamed x46 -> x52, local copies, waits for them, and re-layouts: 17.1 us -> 6.75 us
    ppermute x7, starting transfers between devices: 12.9 us -> 3.05 us  [gather_ring(): cur_b = lax.ppermute(cur_b, 'seq', backward)]
    ppermute x7, starting transfers between devices: 2.67 us -> 12.3 us  [gather_ring(): cur_a = lax.ppermute(cur_a, 'seq', forward)]
    dot_general x6, matrix products: 11 us -> 4.02 us  [attend_part(): jnp.einsum('hqk,khd->hqd', weights.astype(jnp.bfloat16), values, preferre...]
  transfers between devices with their start and end apart: 31 -> 31, of which waited for: 7 -> 11; matrix products, arithmetic and copies ran while one was open for 52% -> 29% of each run, Pallas kernels for 0% -> 0%
where the time goes in v6:
time: 141 us; the launch traced here: 139 us
  waiting for transfers between devices  54.1 us (38%)
  local copies, waits for them, and re-layouts  40.4 us (29%)
  starting transfers between devices  18.7 us (13%)
  matrix products  13.8 us (10%)
  other arithmetic  10.2 us (7%)
  between operations  2.27 us (2%)
    ppermute x7, waiting for transfers between devices, gather_ring(): cur_a = lax.ppermute(cur_a, 'seq', forward)  33 us
    ppermute x1, waiting for transfers between devices, on_device(): came = lax.ppermute(other, 'tp', [(0, 1), (1, 0)])  15.7 us
    ppermute x7, starting transfers between devices, gather_ring(): cur_a = lax.ppermute(cur_a, 'seq', forward)  12.3 us
    concatenate x6, local copies, waits for them, and re-layouts, half(): stack = jnp.concatenate(got[first:last], axis=0)  11.6 us
    slice x19, local copies, waits for them, and re-layouts, on_device(): g[rows_dev, :2]  8.72 us
    unnamed x52, local copies, waits for them, and re-layouts  6.75 us
    dot_general x1, matrix products, on_device(): partial = jnp.dot(attention, out_weight, preferred_element_type=jnp.float32)  6.65 us
    ppermute x7, waiting for transfers between devices, gather_ring(): cur_b = lax.ppermute(cur_b, 'seq', backward)  4.78 us
  transfers between devices with their start and end apart: 31, of which 11 were waited for; matrix products, arithmetic and copies ran while one was open for 29% of the time, Pallas kernels for 0%

profile of v6, /device:TPU:0, one launch (start us, length us, event | category | flops | bytes accessed | tf_op | source)
XLA Modules:
  0.0 139.4 jit_solution(14543554675550595637)
XLA Ops:
  1.3 1.0 fusion.115
  2.5 1.0 fusion.116
  4.0 0.9 select_convert_fusion
  5.3 3.1 %collective-permute-start.1 = (bf16[128,1280]{0,1:T(8,128)(2,1)S(1)}, bf16[128,1280]{0,1:T(8,128)(2,1)S(1)}, u32[]{:S(2)}, u32[]{:S(2)}) collective-permute-start(bf16[128,1280]{0,1:T(8,128)(2,1)S(1)} %get-tuple-element.41), channel_id=1, source_target_pairs={{0,8},{2,10},{8,16},{10,18},{16,24},{18,26},{24,28},{26,30},{28,20... | collective-permute-start | bytes 983048 | tf_op jit(solution)/shard_map/ppermute | solution.py:36
  8.4 7.6 %collective-permute-done.1 = bf16[128,1280]{0,1:T(8,128)(2,1)S(1)} collective-permute-done((bf16[128,1280]{0,1:T(8,128)(2,1)S(1)}, bf16[128,1280]{0,1:T(8,128)(2,1)S(1)}, u32[]{:S(2)}, u32[]{:S(2)}) %collective-permute-start.1) | collective-permute-done | bytes 327712 | tf_op jit(solution)/shard_map/ppermute | solution.py:36
  16.0 1.8 %collective-permute-start.3 = (bf16[128,1280]{0,1:T(8,128)(2,1)S(1)}, bf16[128,1280]{0,1:T(8,128)(2,1)S(1)}, u32[]{:S(2)}, u32[]{:S(2)}) collective-permute-start(bf16[128,1280]{0,1:T(8,128)(2,1)S(1)} %collective-permute-done.1), channel_id=1, source_target_pairs={{0,8},{2,10},{8,16},{10,18},{16,24},{18,26},{24,28},{26,30},{28,20... | collective-permute-start | bytes 983048 | tf_op jit(solution)/shard_map/ppermute | solution.py:36
  18.0 0.5 collective-permute-start.9
  18.5 6.4 %collective-permute-done.3 = bf16[128,1280]{0,1:T(8,128)(2,1)S(1)} collective-permute-done((bf16[128,1280]{0,1:T(8,128)(2,1)S(1)}, bf16[128,1280]{0,1:T(8,128)(2,1)S(1)}, u32[]{:S(2)}, u32[]{:S(2)}) %collective-permute-start.3) | collective-permute-done | bytes 327712 | tf_op jit(solution)/shard_map/ppermute | solution.py:36
  24.9 1.5 %collective-permute-start.5 = (bf16[128,1280]{0,1:T(8,128)(2,1)S(1)}, bf16[128,1280]{0,1:T(8,128)(2,1)}, u32[]{:S(2)}, u32[]{:S(2)}) collective-permute-start(bf16[128,1280]{0,1:T(8,128)(2,1)S(1)} %collective-permute-done.3), channel_id=1, source_target_pairs={{0,8},{2,10},{8,16},{10,18},{16,24},{18,26},{24,28},{26,30},{28,20... | collective-permute-start | bytes 983048 | tf_op jit(solution)/shard_map/ppermute | solution.py:36
  26.4 0.5 collective-permute-start.14
  27.5 5.4 %collective-permute-done.5 = bf16[128,1280]{0,1:T(8,128)(2,1)} collective-permute-done((bf16[128,1280]{0,1:T(8,128)(2,1)S(1)}, bf16[128,1280]{0,1:T(8,128)(2,1)}, u32[]{:S(2)}, u32[]{:S(2)}) %collective-permute-start.5) | collective-permute-done | bytes 327712 | tf_op jit(solution)/shard_map/ppermute | solution.py:36
  33.0 1.2 collective-permute-start.7
  34.1 0.9 collective-permute-start.16
  35.0 0.8 pad_maximum_fusion
  36.4 4.0 %collective-permute-done.7 = bf16[128,1280]{0,1:T(8,128)(2,1)} collective-permute-done((bf16[128,1280]{0,1:T(8,128)(2,1)}, bf16[128,1280]{0,1:T(8,128)(2,1)}, u32[]{:S(2)}, u32[]{:S(2)}) %collective-permute-start.7) | collective-permute-done | bytes 327712 | tf_op jit(solution)/shard_map/ppermute | solution.py:36
  40.4 1.0 collective-permute-done.16
  41.3 1.0 fusion.114
  42.9 0.8 copy.39
  44.2 0.8 pad_maximum_fusion.1
  45.5 0.8 slice.197
  46.2 0.7 slice.206
  46.9 0.7 slice.200
  47.8 0.7 slice.199
  48.5 0.7 slice.208
  49.2 0.7 slice.202
  50.0 0.7 slice.211
  50.7 1.6 %collective-permute-start.18 = (bf16[128,1280]{0,1:T(8,128)(2,1)}, bf16[128,1280]{0,1:T(8,128)(2,1)}, u32[]{:S(2)}, u32[]{:S(2)}) collective-permute-start(bf16[128,1280]{0,1:T(8,128)(2,1)} %collective-permute-done.7), channel_id=1, source_target_pairs={{0,8},{2,10},{8,16},{10,18},{16,24},{18,26},{24,28},{26,30},{28,20... | collective-permute-start | bytes 983048 | tf_op jit(solution)/shard_map/ppermute | solution.py:36
  52.8 0.8 slice.201
  53.5 0.8 slice.210
  54.3 0.8 slice.203
  55.0 0.7 slice.212
  56.5 4.8 %concatenate.46 = bf16[1280,1280]{0,1:T(8,128)(2,1)S(1)} concatenate(bf16[120,1280]{0,1:T(8,128)(2,1)} %pad_maximum_fusion, bf16[8,1280]{0,1:T(8,128)(2,1)} %copy-done.3, bf16[128,1280]{0,1:T(8,128)(2,1)} %copy-done.15, bf16[128,1280]{0,1:T(8,128)(2,1)} %copy-done.11, bf16[128,1280]{0,1:T(8,128)(2,1)} %copy-done.17, bf16[128,1280]{0,1:T(8,128)(2,1)} %copy-done.13, ...), dimensions={0} | concatenate | bytes 6553600 | tf_op jit(solution)/shard_map/concatenate | solution.py:131
  61.3 1.9 %fusion.108 = (bf16[1280,640]{0,1:T(8,128)(2,1)}, bf16[1280,640]{0,1:T(8,128)(2,1)}) fusion(bf16[1280,1280]{0,1:T(8,128)(2,1)S(1)} %concatenate.46), kind=kLoop, calls=%fused_computation.155 | loop fusion | bytes 6553600 | tf_op jit(solution)/shard_map/slice | solution.py:132
  63.5 4.8 %concatenate.49 = bf16[1280,1280]{0,1:T(8,128)(2,1)S(1)} concatenate(bf16[120,1280]{0,1:T(8,128)(2,1)} %pad_maximum_fusion.1, bf16[8,1280]{0,1:T(8,128)(2,1)} %copy-done.3, bf16[128,1280]{0,1:T(8,128)(2,1)} %copy-done.12, bf16[128,1280]{0,1:T(8,128)(2,1)} %copy-done.9, bf16[128,1280]{0,1:T(8,128)(2,1)} %copy-done.16, bf16[128,1280]{0,1:T(8,128)(2,1)} %copy-done.10, ...), dimensions={0} | concatenate | bytes 6553600 | tf_op jit(solution)/shard_map/concatenate | solution.py:131
  68.4 1.4 fusion.109
  69.7 0.6 copy-done.2
  70.4 0.7 fusion.120
  71.3 0.7 fusion.4
  71.9 1.0 constant_dynamic-update-slice_fusion.3
  73.0 1.6 %collective-permute-start.20 = (bf16[128,1280]{0,1:T(8,128)(2,1)}, bf16[128,1280]{0,1:T(8,128)(2,1)S(1)}, u32[]{:S(2)}, u32[]{:S(2)}) collective-permute-start(bf16[128,1280]{0,1:T(8,128)(2,1)} %collective-permute-done.18), channel_id=1, source_target_pairs={{0,8},{2,10},{8,16},{10,18},{16,24},{18,26},{24,28},{26,30},{28,20... | collective-permute-start | bytes 983048 | tf_op jit(solution)/shard_map/ppermute | solution.py:36
  74.7 0.7 fusion.117
  75.4 1.0 constant_dynamic-update-slice_fusion.9
  77.0 0.6 fusion.6
  77.7 5.7 %collective-permute-done.20 = bf16[128,1280]{0,1:T(8,128)(2,1)S(1)} collective-permute-done((bf16[128,1280]{0,1:T(8,128)(2,1)}, bf16[128,1280]{0,1:T(8,128)(2,1)S(1)}, u32[]{:S(2)}, u32[]{:S(2)}) %collective-permute-start.20) | collective-permute-done | bytes 327712 | tf_op jit(solution)/shard_map/ppermute | solution.py:36
  83.4 1.6 %collective-permute-start.22 = (bf16[128,1280]{0,1:T(8,128)(2,1)S(1)}, bf16[128,1280]{0,1:T(8,128)(2,1)S(1)}, u32[]{:S(2)}, u32[]{:S(2)}) collective-permute-start(bf16[128,1280]{0,1:T(8,128)(2,1)S(1)} %collective-permute-done.20), channel_id=1, source_target_pairs={{0,8},{2,10},{8,16},{10,18},{16,24},{18,26},{24,28},{26,30},{28,20... | collective-permute-start | bytes 983048 | tf_op jit(solution)/shard_map/ppermute | solution.py:36
  85.0 1.6 %collective-permute-done.26 = bf16[128,1280]{0,1:T(8,128)(2,1)S(1)} collective-permute-done((bf16[128,1280]{0,1:T(8,128)(2,1)}, bf16[128,1280]{0,1:T(8,128)(2,1)S(1)}, u32[]{:S(2)}, u32[]{:S(2)}) %collective-permute-start.26) | collective-permute-done | bytes 327712 | tf_op jit(solution)/shard_map/ppermute | solution.py:37
  87.5 0.6 collective-permute-done.27
  88.2 0.9 fusion.111
  89.6 3.9 %collective-permute-done.22 = bf16[128,1280]{0,1:T(8,128)(2,1)S(1)} collective-permute-done((bf16[128,1280]{0,1:T(8,128)(2,1)S(1)}, bf16[128,1280]{0,1:T(8,128)(2,1)S(1)}, u32[]{:S(2)}, u32[]{:S(2)}) %collective-permute-start.22) | collective-permute-done | bytes 327712 | tf_op jit(solution)/shard_map/ppermute | solution.py:36
  94.5 2.3 %collective-permute-done.28 = bf16[128,1280]{0,1:T(8,128)(2,1)} collective-permute-done((bf16[128,1280]{0,1:T(8,128)(2,1)S(1)}, bf16[128,1280]{0,1:T(8,128)(2,1)}, u32[]{:S(2)}, u32[]{:S(2)}) %collective-permute-start.28) | collective-permute-done | bytes 327712 | tf_op jit(solution)/shard_map/ppermute | solution.py:37
  97.1 1.7 %constant_dynamic-update-slice_fusion.11 = bf16[256,1280]{0,1:T(8,128)(2,1)} fusion(bf16[128,1280]{0,1:T(8,128)(2,1)} %collective-permute-done.28), kind=kLoop, calls=%fused_computation.101 | loop fusion | bytes 655360
  99.7 0.7 copy-done.7
  100.4 0.9 fusion.42
  101.7 1.0 fusion.51
  102.7 1.1 copy.49
  103.8 1.7 %constant_dynamic-update-slice_fusion.10 = bf16[256,1280]{0,1:T(8,128)(2,1)} fusion(bf16[256,1280]{0,1:T(8,128)(2,1)} %constant_dynamic-update-slice_fusion.11, bf16[128,1280]{0,1:T(8,128)(2,1)} %collective-permute-done.29), kind=kLoop, calls=%fused_computation.100 | loop fusion | bytes 655360 | tf_op jit(solution)/shard_map/concatenate | solution.py:131
  105.5 1.2 fusion.113
  107.5 0.9 fusion.48
  109.9 6.6 %fusion.69 = f32[120,5120]{1,0:T(8,128)S(1)} fusion(bf16[1280,5120]{1,0:T(8,128)(2,1)} %param.15, bf16[120,640]{0,1:T(8,128)(2,1)S(1)} %bitcast.282, bf16[120,640]{0,1:T(8,128)(2,1)S(1)} %bitcast.281), kind=kOutput, calls=%fused_computation.80 | convolution fusion | flops 1573478400 | bytes 15872000 | tf_op jit(solution)/shard_map/dot_general | solution.py:141
  116.6 1.7 %reshape.284 = f32[2,60,5120]{2,1,0:T(8,128)} reshape(f32[120,5120]{1,0:T(8,128)S(1)} %fusion.69) | data formatting | bytes 4915200 | tf_op jit(solution)/shard_map/reshape | solution.py:145
  118.3 1.5 %bitcast_convert_fusion = bf16[60,5120]{1,0:T(8,128)(2,1)S(1)} fusion(f32[2,60,5120]{2,1,0:T(8,128)} %reshape.284, s32[]{:T(128)S(6)} %select_n.279, pred[]{:T(512)S(6)} %and.116), kind=kLoop, calls=%fused_computation.26 | loop fusion | flops 307200 | bytes 1228805 | tf_op jit(solution)/shard_map/convert_element_type | solution.py:147
  119.8 1.6 %collective-permute-start.30 = (bf16[60,5120]{1,0:T(8,128)(2,1)S(1)}, bf16[60,5120]{1,0:T(8,128)(2,1)S(1)}, u32[]{:S(2)}, u32[]{:S(2)}) collective-permute-start(bf16[60,5120]{1,0:T(8,128)(2,1)S(1)} %bitcast_convert_fusion), channel_id=1, source_target_pairs={{0,1},{1,0},{2,3},{3,2},{4,5},{5,4},{6,7},{7,6},{8,9},{9,8},{10,11... | collective-permute-start | bytes 1843208 | tf_op jit(solution)/shard_map/ppermute | solution.py:148
  121.4 15.7 %collective-permute-done.30 = bf16[60,5120]{1,0:T(8,128)(2,1)S(1)} collective-permute-done((bf16[60,5120]{1,0:T(8,128)(2,1)S(1)}, bf16[60,5120]{1,0:T(8,128)(2,1)S(1)}, u32[]{:S(2)}, u32[]{:S(2)}) %collective-permute-start.30) | collective-permute-done | bytes 614432 | tf_op jit(solution)/shard_map/ppermute | solution.py:148
  137.0 2.4 %fusion.24 = bf16[60,5120]{1,0:T(8,128)(2,1)} fusion(f32[2,60,5120]{2,1,0:T(8,128)} %reshape.284, s32[]{:T(128)S(6)} %select_n.277, bf16[60,5120]{1,0:T(8,128)(2,1)S(1)} %collective-permute-done.30, bf16[60,5120]{1,0:T(8,128)(2,1)S(1)} %copy-done.8, f32[5120]{0:T(1024)S(1)} %copy-done.19, pred[]{:T(512)S(6)} %and.115), kind=kLoop, calls=%fused_computation.30 | loop fusion | flops 2150400 | bytes 3092485 | tf_op jit(solution)/shard_map/convert_element_type | solution.py:150
  (136 shorter events, 12.0 us)
Async XLA Ops:
  5.0 37.7 %copy-start.3 = (bf16[8,1280]{0,1:T(8,128)(2,1)}, bf16[8,1280]{0,1:T(8,128)(2,1)S(1)}, u32[]{:S(2)}) copy-start(bf16[8,1280]{0,1:T(8,128)(2,1)S(1)} %select_convert_fusion) | copy-start | bytes 61444
  5.3 10.7 %collective-permute-start.1 = (bf16[128,1280]{0,1:T(8,128)(2,1)S(1)}, bf16[128,1280]{0,1:T(8,128)(2,1)S(1)}, u32[]{:S(2)}, u32[]{:S(2)}) collective-permute-start(bf16[128,1280]{0,1:T(8,128)(2,1)S(1)} %get-tuple-element.41), channel_id=1, source_target_pairs={{0,8},{2,10},{8,16},{10,18},{16,24},{18,26},{24,28},{26,30},{28,20... | collective-permute-start | bytes 983048 | tf_op jit(solution)/shard_map/ppermute | solution.py:36
  8.3 9.5 %collective-permute-start.10 = (bf16[128,1280]{0,1:T(8,128)(2,1)S(1)}, bf16[128,1280]{0,1:T(8,128)(2,1)S(1)}, u32[]{:S(2)}, u32[]{:S(2)}) collective-permute-start(bf16[128,1280]{0,1:T(8,128)(2,1)S(1)} %get-tuple-element.42), channel_id=1, source_target_pairs={{8,0},{10,2},{16,8},{18,10},{24,16},{26,18},{28,24},{30,26},{20,28... | collective-permute-start | bytes 983048 | tf_op jit(solution)/shard_map/ppermute | solution.py:37
  16.0 29.0 %copy-start.11 = (bf16[128,1280]{0,1:T(8,128)(2,1)}, bf16[128,1280]{0,1:T(8,128)(2,1)S(1)}, u32[]{:S(2)}) copy-start(bf16[128,1280]{0,1:T(8,128)(2,1)S(1)} %collective-permute-done.1) | copy-start | bytes 983044
  16.0 8.9 %collective-permute-start.3 = (bf16[128,1280]{0,1:T(8,128)(2,1)S(1)}, bf16[128,1280]{0,1:T(8,128)(2,1)S(1)}, u32[]{:S(2)}, u32[]{:S(2)}) collective-permute-start(bf16[128,1280]{0,1:T(8,128)(2,1)S(1)} %collective-permute-done.1), channel_id=1, source_target_pairs={{0,8},{2,10},{8,16},{10,18},{16,24},{18,26},{24,28},{26,30},{28,20... | collective-permute-start | bytes 983048 | tf_op jit(solution)/shard_map/ppermute | solution.py:36
  17.8 27.3 %copy-start.9 = (bf16[128,1280]{0,1:T(8,128)(2,1)}, bf16[128,1280]{0,1:T(8,128)(2,1)S(1)}, u32[]{:S(2)}) copy-start(bf16[128,1280]{0,1:T(8,128)(2,1)S(1)} %collective-permute-done.10) | copy-start | bytes 983044
  17.8 8.6 %collective-permute-start.12 = (bf16[128,1280]{0,1:T(8,128)(2,1)S(1)}, bf16[128,1280]{0,1:T(8,128)(2,1)S(1)}, u32[]{:S(2)}, u32[]{:S(2)}) collective-permute-start(bf16[128,1280]{0,1:T(8,128)(2,1)S(1)} %collective-permute-done.10), channel_id=1, source_target_pairs={{8,0},{10,2},{16,8},{18,10},{24,16},{26,18},{28,24},{30,26},{20,28... | collective-permute-start | bytes 983048 | tf_op jit(solution)/shard_map/ppermute | solution.py:37
  18.0 8.9 %collective-permute-start = (bf16[128,1280]{0,1:T(8,128)(2,1)S(1)}, bf16[128,1280]{0,1:T(8,128)(2,1)S(1)}, u32[]{:S(2)}, u32[]{:S(2)}) collective-permute-start(bf16[128,1280]{0,1:T(8,128)(2,1)S(1)} %get-tuple-element.41), channel_id=1, source_target_pairs={{0,2},{2,0},{4,6},{6,4},{8,10},{10,8},{12,14},{14,12},{16,18},{18,... | collective-permute-start | bytes 983048 | tf_op jit(solution)/shard_map/ppermute | solution.py:40
  18.0 9.4 %collective-permute-start.9 = (bf16[128,1280]{0,1:T(8,128)(2,1)S(1)}, bf16[128,1280]{0,1:T(8,128)(2,1)S(1)}, u32[]{:S(2)}, u32[]{:S(2)}) collective-permute-start(bf16[128,1280]{0,1:T(8,128)(2,1)S(1)} %get-tuple-element.42), channel_id=1, source_target_pairs={{0,2},{2,0},{4,6},{6,4},{8,10},{10,8},{12,14},{14,12},{16,18},{18,... | collective-permute-start | bytes 983048 | tf_op jit(solution)/shard_map/ppermute | solution.py:41
  24.9 20.4 %copy-start.13 = (bf16[128,1280]{0,1:T(8,128)(2,1)}, bf16[128,1280]{0,1:T(8,128)(2,1)S(1)}, u32[]{:S(2)}) copy-start(bf16[128,1280]{0,1:T(8,128)(2,1)S(1)} %collective-permute-done.3) | copy-start | bytes 983044
  24.9 8.1 %collective-permute-start.5 = (bf16[128,1280]{0,1:T(8,128)(2,1)S(1)}, bf16[128,1280]{0,1:T(8,128)(2,1)}, u32[]{:S(2)}, u32[]{:S(2)}) collective-permute-start(bf16[128,1280]{0,1:T(8,128)(2,1)S(1)} %collective-permute-done.3), channel_id=1, source_target_pairs={{0,8},{2,10},{8,16},{10,18},{16,24},{18,26},{24,28},{26,30},{28,20... | collective-permute-start | bytes 983048 | tf_op jit(solution)/shard_map/ppermute | solution.py:36
  26.4 19.0 %copy-start.10 = (bf16[128,1280]{0,1:T(8,128)(2,1)}, bf16[128,1280]{0,1:T(8,128)(2,1)S(1)}, u32[]{:S(2)}) copy-start(bf16[128,1280]{0,1:T(8,128)(2,1)S(1)} %collective-permute-done.12) | copy-start | bytes 983044
  26.4 7.8 %collective-permute-start.14 = (bf16[128,1280]{0,1:T(8,128)(2,1)S(1)}, bf16[128,1280]{0,1:T(8,128)(2,1)S(1)}, u32[]{:S(2)}, u32[]{:S(2)}) collective-permute-start(bf16[128,1280]{0,1:T(8,128)(2,1)S(1)} %collective-permute-done.12), channel_id=1, source_target_pairs={{8,0},{10,2},{16,8},{18,10},{24,16},{26,18},{28,24},{30,26},{20,28... | collective-permute-start | bytes 983048 | tf_op jit(solution)/shard_map/ppermute | solution.py:37
  26.9 8.9 %collective-permute-start.2 = (bf16[128,1280]{0,1:T(8,128)(2,1)S(1)}, bf16[128,1280]{0,1:T(8,128)(2,1)S(1)}, u32[]{:S(2)}, u32[]{:S(2)}) collective-permute-start(bf16[128,1280]{0,1:T(8,128)(2,1)S(1)} %collective-permute-done.1), channel_id=1, source_target_pairs={{0,2},{2,0},{4,6},{6,4},{8,10},{10,8},{12,14},{14,12},{16,18},{18,... | collective-permute-start | bytes 983048 | tf_op jit(solution)/shard_map/ppermute | solution.py:40
  26.9 18.2 %copy-start.15 = (bf16[128,1280]{0,1:T(8,128)(2,1)}, bf16[128,1280]{0,1:T(8,128)(2,1)S(1)}, u32[]{:S(2)}) copy-start(bf16[128,1280]{0,1:T(8,128)(2,1)S(1)} %collective-permute-done) | copy-start | bytes 983044
  26.9 8.9 %collective-permute-start.11 = (bf16[128,1280]{0,1:T(8,128)(2,1)S(1)}, bf16[128,1280]{0,1:T(8,128)(2,1)S(1)}, u32[]{:S(2)}, u32[]{:S(2)}) collective-permute-start(bf16[128,1280]{0,1:T(8,128)(2,1)S(1)} %collective-permute-done.10), channel_id=1, source_target_pairs={{0,2},{2,0},{4,6},{6,4},{8,10},{10,8},{12,14},{14,12},{16,18},{18,... | collective-permute-start | bytes 983048 | tf_op jit(solution)/shard_map/ppermute | solution.py:41
  27.5 17.8 %copy-start.12 = (bf16[128,1280]{0,1:T(8,128)(2,1)}, bf16[128,1280]{0,1:T(8,128)(2,1)S(1)}, u32[]{:S(2)}) copy-start(bf16[128,1280]{0,1:T(8,128)(2,1)S(1)} %collective-permute-done.9) | copy-start | bytes 983044
  27.5 8.9 %collective-permute-start.4 = (bf16[128,1280]{0,1:T(8,128)(2,1)S(1)}, bf16[128,1280]{0,1:T(8,128)(2,1)S(1)}, u32[]{:S(2)}, u32[]{:S(2)}) collective-permute-start(bf16[128,1280]{0,1:T(8,128)(2,1)S(1)} %collective-permute-done.3), channel_id=1, source_target_pairs={{0,2},{2,0},{4,6},{6,4},{8,10},{10,8},{12,14},{14,12},{16,18},{18,... | collective-permute-start | bytes 983048 | tf_op jit(solution)/shard_map/ppermute | solution.py:40
  33.0 7.4 %collective-permute-start.7 = (bf16[128,1280]{0,1:T(8,128)(2,1)}, bf16[128,1280]{0,1:T(8,128)(2,1)}, u32[]{:S(2)}, u32[]{:S(2)}) collective-permute-start(bf16[128,1280]{0,1:T(8,128)(2,1)} %collective-permute-done.5), channel_id=1, source_target_pairs={{0,8},{2,10},{8,16},{10,18},{16,24},{18,26},{24,28},{26,30},{28,20... | collective-permute-start | bytes 983048 | tf_op jit(solution)/shard_map/ppermute | solution.py:36
  34.1 13.5 %copy-start.14 = (bf16[128,1280]{0,1:T(8,128)(2,1)}, bf16[128,1280]{0,1:T(8,128)(2,1)S(1)}, u32[]{:S(2)}) copy-start(bf16[128,1280]{0,1:T(8,128)(2,1)S(1)} %collective-permute-done.14) | copy-start | bytes 983044
  34.1 7.2 %collective-permute-start.16 = (bf16[128,1280]{0,1:T(8,128)(2,1)S(1)}, bf16[128,1280]{0,1:T(8,128)(2,1)}, u32[]{:S(2)}, u32[]{:S(2)}) collective-permute-start(bf16[128,1280]{0,1:T(8,128)(2,1)S(1)} %collective-permute-done.14), channel_id=1, source_target_pairs={{8,0},{10,2},{16,8},{18,10},{24,16},{26,18},{28,24},{30,26},{20,28... | collective-permute-start | bytes 983048 | tf_op jit(solution)/shard_map/ppermute | solution.py:37
  35.8 5.5 %copy-start.17 = (bf16[128,1280]{0,1:T(8,128)(2,1)}, bf16[128,1280]{0,1:T(8,128)(2,1)S(1)}, u32[]{:S(2)}) copy-start(bf16[128,1280]{0,1:T(8,128)(2,1)S(1)} %collective-permute-done.2) | copy-start | bytes 983044
  35.8 12.7 %collective-permute-start.13 = (bf16[128,1280]{0,1:T(8,128)(2,1)S(1)}, bf16[128,1280]{0,1:T(8,128)(2,1)}, u32[]{:S(2)}, u32[]{:S(2)}) collective-permute-start(bf16[128,1280]{0,1:T(8,128)(2,1)S(1)} %collective-permute-done.12), channel_id=1, source_target_pairs={{0,2},{2,0},{4,6},{6,4},{8,10},{10,8},{12,14},{14,12},{16,18},{18,... | collective-permute-start | bytes 983048 | tf_op jit(solution)/shard_map/ppermute | solution.py:41
  35.8 5.5 %copy-start.16 = (bf16[128,1280]{0,1:T(8,128)(2,1)}, bf16[128,1280]{0,1:T(8,128)(2,1)S(1)}, u32[]{:S(2)}) copy-start(bf16[128,1280]{0,1:T(8,128)(2,1)S(1)} %collective-permute-done.11) | copy-start | bytes 983044
  35.8 16.5 %collective-permute-start.6 = (bf16[128,1280]{0,1:T(8,128)(2,1)}, bf16[128,1280]{0,1:T(8,128)(2,1)}, u32[]{:S(2)}, u32[]{:S(2)}) collective-permute-start(bf16[128,1280]{0,1:T(8,128)(2,1)} %collective-permute-done.5), channel_id=1, source_target_pairs={{0,2},{2,0},{4,6},{6,4},{8,10},{10,8},{12,14},{14,12},{16,18},{18,... | collective-permute-start | bytes 983048 | tf_op jit(solution)/shard_map/ppermute | solution.py:40
  36.3 6.0 %copy-start.18 = (bf16[128,1280]{0,1:T(8,128)(2,1)}, bf16[128,1280]{0,1:T(8,128)(2,1)S(1)}, u32[]{:S(2)}) copy-start(bf16[128,1280]{0,1:T(8,128)(2,1)S(1)} %collective-permute-done.4) | copy-start | bytes 983044
  36.3 17.2 %collective-permute-start.15 = (bf16[128,1280]{0,1:T(8,128)(2,1)S(1)}, bf16[128,1280]{0,1:T(8,128)(2,1)}, u32[]{:S(2)}, u32[]{:S(2)}) collective-permute-start(bf16[128,1280]{0,1:T(8,128)(2,1)S(1)} %collective-permute-done.14), channel_id=1, source_target_pairs={{0,2},{2,0},{4,6},{6,4},{8,10},{10,8},{12,14},{14,12},{16,18},{18,... | collective-permute-start | bytes 983048 | tf_op jit(solution)/shard_map/ppermute | solution.py:41
  40.4 13.9 %collective-permute-start.8 = (bf16[128,1280]{0,1:T(8,128)(2,1)}, bf16[128,1280]{0,1:T(8,128)(2,1)}, u32[]{:S(2)}, u32[]{:S(2)}) collective-permute-start(bf16[128,1280]{0,1:T(8,128)(2,1)} %collective-permute-done.7), channel_id=1, source_target_pairs={{0,2},{2,0},{4,6},{6,4},{8,10},{10,8},{12,14},{14,12},{16,18},{18,... | collective-permute-start | bytes 983048 | tf_op jit(solution)/shard_map/ppermute | solution.py:40
  41.3 13.7 %collective-permute-start.17 = (bf16[128,1280]{0,1:T(8,128)(2,1)}, bf16[128,1280]{0,1:T(8,128)(2,1)}, u32[]{:S(2)}, u32[]{:S(2)}) collective-permute-start(bf16[128,1280]{0,1:T(8,128)(2,1)} %collective-permute-done.16), channel_id=1, source_target_pairs={{0,2},{2,0},{4,6},{6,4},{8,10},{10,8},{12,14},{14,12},{16,18},{18,... | collective-permute-start | bytes 983048 | tf_op jit(solution)/shard_map/ppermute | solution.py:41
  50.7 21.2 %collective-permute-start.18 = (bf16[128,1280]{0,1:T(8,128)(2,1)}, bf16[128,1280]{0,1:T(8,128)(2,1)}, u32[]{:S(2)}, u32[]{:S(2)}) collective-permute-start(bf16[128,1280]{0,1:T(8,128)(2,1)} %collective-permute-done.7), channel_id=1, source_target_pairs={{0,8},{2,10},{8,16},{10,18},{16,24},{18,26},{24,28},{26,30},{28,20... | collective-permute-start | bytes 983048 | tf_op jit(solution)/shard_map/ppermute | solution.py:36
  52.3 23.1 %collective-permute-start.24 = (bf16[128,1280]{0,1:T(8,128)(2,1)}, bf16[128,1280]{0,1:T(8,128)(2,1)}, u32[]{:S(2)}, u32[]{:S(2)}) collective-permute-start(bf16[128,1280]{0,1:T(8,128)(2,1)} %collective-permute-done.16), channel_id=1, source_target_pairs={{8,0},{10,2},{16,8},{18,10},{24,16},{26,18},{28,24},{30,26},{20,28... | collective-permute-start | bytes 983048 | tf_op jit(solution)/shard_map/ppermute | solution.py:37
  68.3 2.0 %copy-start.2 = (bf16[1280,640]{0,1:T(8,128)(2,1)S(1)}, bf16[1280,640]{0,1:T(8,128)(2,1)}, u32[]{:S(2)}) copy-start(bf16[1280,640]{0,1:T(8,128)(2,1)} %get-tuple-element.29) | copy-start | bytes 4915204
  68.4 2.0 %copy-start.4 = (bf16[120,640]{0,1:T(8,128)(2,1)S(1)}, bf16[120,640]{0,1:T(8,128)(2,1)}, u32[]{:S(2)}) copy-start(bf16[120,640]{0,1:T(8,128)(2,1)} %copy.39) | copy-start | bytes 460804
  73.0 13.6 %collective-permute-start.19 = (bf16[128,1280]{0,1:T(8,128)(2,1)}, bf16[128,1280]{0,1:T(8,128)(2,1)S(1)}, u32[]{:S(2)}, u32[]{:S(2)}) collective-permute-start(bf16[128,1280]{0,1:T(8,128)(2,1)} %collective-permute-done.18), channel_id=1, source_target_pairs={{0,2},{2,0},{4,6},{6,4},{8,10},{10,8},{12,14},{14,12},{16,18},{18,... | collective-permute-start | bytes 983048 | tf_op jit(solution)/shard_map/ppermute | solution.py:40
  73.0 10.3 %collective-permute-start.20 = (bf16[128,1280]{0,1:T(8,128)(2,1)}, bf16[128,1280]{0,1:T(8,128)(2,1)S(1)}, u32[]{:S(2)}, u32[]{:S(2)}) collective-permute-start(bf16[128,1280]{0,1:T(8,128)(2,1)} %collective-permute-done.18), channel_id=1, source_target_pairs={{0,8},{2,10},{8,16},{10,18},{16,24},{18,26},{24,28},{26,30},{28,20... | collective-permute-start | bytes 983048 | tf_op jit(solution)/shard_map/ppermute | solution.py:36
  76.5 10.0 %collective-permute-start.26 = (bf16[128,1280]{0,1:T(8,128)(2,1)}, bf16[128,1280]{0,1:T(8,128)(2,1)S(1)}, u32[]{:S(2)}, u32[]{:S(2)}) collective-permute-start(bf16[128,1280]{0,1:T(8,128)(2,1)} %collective-permute-done.24), channel_id=1, source_target_pairs={{8,0},{10,2},{16,8},{18,10},{24,16},{26,18},{28,24},{30,26},{20,28... | collective-permute-start | bytes 983048 | tf_op jit(solution)/shard_map/ppermute | solution.py:37
  77.0 10.1 %collective-permute-start.25 = (bf16[128,1280]{0,1:T(8,128)(2,1)}, bf16[128,1280]{0,1:T(8,128)(2,1)S(1)}, u32[]{:S(2)}, u32[]{:S(2)}) collective-permute-start(bf16[128,1280]{0,1:T(8,128)(2,1)} %collective-permute-done.24), channel_id=1, source_target_pairs={{0,2},{2,0},{4,6},{6,4},{8,10},{10,8},{12,14},{14,12},{16,18},{18,... | collective-permute-start | bytes 983048 | tf_op jit(solution)/shard_map/ppermute | solution.py:41
  83.4 4.0 %collective-permute-start.21 = (bf16[128,1280]{0,1:T(8,128)(2,1)S(1)}, bf16[128,1280]{0,1:T(8,128)(2,1)S(1)}, u32[]{:S(2)}, u32[]{:S(2)}) collective-permute-start(bf16[128,1280]{0,1:T(8,128)(2,1)S(1)} %collective-permute-done.20), channel_id=1, source_target_pairs={{0,2},{2,0},{4,6},{6,4},{8,10},{10,8},{12,14},{14,12},{16,18},{18,... | collective-permute-start | bytes 983048 | tf_op jit(solution)/shard_map/ppermute | solution.py:40
  83.4 10.1 %collective-permute-start.22 = (bf16[128,1280]{0,1:T(8,128)(2,1)S(1)}, bf16[128,1280]{0,1:T(8,128)(2,1)S(1)}, u32[]{:S(2)}, u32[]{:S(2)}) collective-permute-start(bf16[128,1280]{0,1:T(8,128)(2,1)S(1)} %collective-permute-done.20), channel_id=1, source_target_pairs={{0,8},{2,10},{8,16},{10,18},{16,24},{18,26},{24,28},{26,30},{28,20... | collective-permute-start | bytes 983048 | tf_op jit(solution)/shard_map/ppermute | solution.py:36
  86.5 1.6 %collective-permute-start.27 = (bf16[128,1280]{0,1:T(8,128)(2,1)S(1)}, bf16[128,1280]{0,1:T(8,128)(2,1)S(1)}, u32[]{:S(2)}, u32[]{:S(2)}) collective-permute-start(bf16[128,1280]{0,1:T(8,128)(2,1)S(1)} %collective-permute-done.26), channel_id=1, source_target_pairs={{0,2},{2,0},{4,6},{6,4},{8,10},{10,8},{12,14},{14,12},{16,18},{18,... | collective-permute-start | bytes 983048 | tf_op jit(solution)/shard_map/ppermute | solution.py:41
  86.5 10.2 %collective-permute-start.28 = (bf16[128,1280]{0,1:T(8,128)(2,1)S(1)}, bf16[128,1280]{0,1:T(8,128)(2,1)}, u32[]{:S(2)}, u32[]{:S(2)}) collective-permute-start(bf16[128,1280]{0,1:T(8,128)(2,1)S(1)} %collective-permute-done.26), channel_id=1, source_target_pairs={{8,0},{10,2},{16,8},{18,10},{24,16},{26,18},{28,24},{30,26},{20,28... | collective-permute-start | bytes 983048 | tf_op jit(solution)/shard_map/ppermute | solution.py:37
  93.9 4.9 %collective-permute-start.23 = (bf16[128,1280]{0,1:T(8,128)(2,1)S(1)}, bf16[128,1280]{0,1:T(8,128)(2,1)S(1)}, u32[]{:S(2)}, u32[]{:S(2)}) collective-permute-start(bf16[128,1280]{0,1:T(8,128)(2,1)S(1)} %collective-permute-done.22), channel_id=1, source_target_pairs={{0,2},{2,0},{4,6},{6,4},{8,10},{10,8},{12,14},{14,12},{16,18},{18,... | collective-permute-start | bytes 983048 | tf_op jit(solution)/shard_map/ppermute | solution.py:40
  94.5 4.5 %copy-start = (f32[5,120,512]{2,1,0:T(8,128)}, f32[5,120,512]{2,1,0:T(8,128)S(1)}, u32[]{:S(2)}) copy-start(f32[5,120,512]{2,1,0:T(8,128)S(1)} %get-tuple-element.56) | copy-start | bytes 3686404
  96.8 7.1 %collective-permute-start.29 = (bf16[128,1280]{0,1:T(8,128)(2,1)}, bf16[128,1280]{0,1:T(8,128)(2,1)}, u32[]{:S(2)}, u32[]{:S(2)}) collective-permute-start(bf16[128,1280]{0,1:T(8,128)(2,1)} %collective-permute-done.28), channel_id=1, source_target_pairs={{0,2},{2,0},{4,6},{6,4},{8,10},{10,8},{12,14},{14,12},{16,18},{18,... | collective-permute-start | bytes 983048 | tf_op jit(solution)/shard_map/ppermute | solution.py:41
  98.9 1.4 %copy-start.7 = (bf16[1280,640]{0,1:T(8,128)(2,1)S(1)}, bf16[1280,640]{0,1:T(8,128)(2,1)}, u32[]{:S(2)}) copy-start(bf16[1280,640]{0,1:T(8,128)(2,1)} %get-tuple-element.30) | copy-start | bytes 4915204
  105.5 1.9 %copy-start.6 = (bf16[1280,640]{0,1:T(8,128)(2,1)S(1)}, bf16[1280,640]{0,1:T(8,128)(2,1)}, u32[]{:S(2)}) copy-start(bf16[1280,640]{0,1:T(8,128)(2,1)} %get-tuple-element.32) | copy-start | bytes 4915204
  107.5 1.3 copy-start.1
  107.5 1.4 %copy-start.5 = (bf16[512,640]{0,1:T(8,128)(2,1)S(1)}, bf16[512,640]{0,1:T(8,128)(2,1)}, u32[]{:S(2)}) copy-start(bf16[512,640]{0,1:T(8,128)(2,1)} %get-tuple-element.35) | copy-start | bytes 1966084
  116.6 20.4 %copy-start.19 = (f32[5120]{0:T(1024)S(1)}, f32[5120]{0:T(1024)}, u32[]{:S(2)}) copy-start(f32[5120]{0:T(1024)} %param.14) | copy-start | bytes 61444
  118.3 18.7 %copy-start.8 = (bf16[60,5120]{1,0:T(8,128)(2,1)S(1)}, bf16[60,5120]{1,0:T(8,128)(2,1)}, u32[]{:S(2)}) copy-start(bf16[60,5120]{1,0:T(8,128)(2,1)} %param.10) | copy-start | bytes 1843204
  119.8 17.2 %collective-permute-start.30 = (bf16[60,5120]{1,0:T(8,128)(2,1)S(1)}, bf16[60,5120]{1,0:T(8,128)(2,1)S(1)}, u32[]{:S(2)}, u32[]{:S(2)}) collective-permute-start(bf16[60,5120]{1,0:T(8,128)(2,1)S(1)} %bitcast_convert_fusion), channel_id=1, source_target_pairs={{0,1},{1,0},{2,3},{3,2},{4,5},{5,4},{6,7},{7,6},{8,9},{9,8},{10,11... | collective-permute-start | bytes 1843208 | tf_op jit(solution)/shard_map/ppermute | solution.py:148

commit v7 on v6

--- a/solution.py
+++ b/solution.py
@@ -138,16 +138,25 @@
         attention = jnp.concatenate(
             [half(got_a, limit_a, 0, heads_a), half(got_b, limit_b, heads_a, heads_here)], axis=1
         )
-        partial = jnp.dot(attention, out_weight, preferred_element_type=jnp.float32)
         rows_out = hidden.shape[0]
         side = lax.axis_index("tp")
         n_tp = rows_dev // rows_out
-        pieces = partial.reshape(n_tp, rows_out, partial.shape[1])
-        own = jnp.take(pieces, side, axis=0)
-        other = jnp.take(pieces, 1 - side, axis=0).astype(jnp.bfloat16)
-        came = lax.ppermute(other, "tp", [(0, 1), (1, 0)])
-        summed = own + came.astype(jnp.float32)
-        return (hidden.astype(jnp.float32) + gate_scale * summed).astype(jnp.bfloat16)
+        width_all = out_weight.shape[1]
+        n_chunks = 4 if width_all % (4 * HEAD) == 0 else 1
+        width = width_all // n_chunks
+        mixed = []
+        for i in range(n_chunks):
+            cols = slice(i * width, (i + 1) * width)
+            partial = jnp.dot(attention, out_weight[:, cols], preferred_element_type=jnp.float32)
+            pieces = partial.reshape(n_tp, rows_out, width)
+            own = jnp.take(pieces, side, axis=0)
+            other = jnp.take(pieces, 1 - side, axis=0).astype(jnp.bfloat16)
+            came = lax.ppermute(other, "tp", [(0, 1), (1, 0)])
+            summed = own + came.astype(jnp.float32)
+            mixed.append(
+                (hidden[:, cols].astype(jnp.float32) + gate_scale[cols] * summed).astype(jnp.bfloat16)
+            )
+        return jnp.concatenate(mixed, axis=1)
 
     placed = (
         P(("seq", "tp"), None),

time: 141 us -> 143 us (1.014)
  waiting for transfers between devices: 54.1 us -> 48.9 us
  matrix products: 13.8 us -> 18.2 us
  starting transfers between devices: 18.7 us -> 21.3 us
    ppermute x1 -> x4, waiting for transfers between devices: 15.7 us -> 10.5 us  [on_device(): came = lax.ppermute(other, 'tp', [(0, 1), (1, 0)])]
    dot_general x1 -> x4, matrix products: 6.65 us -> 11.1 us  [on_device(): jnp.dot(attention, out_weight[:, cols], preferred_element_type=jnp.float32)]
    ppermute x1 -> x4, starting transfers between devices: 1.55 us -> 4.12 us  [on_device(): came = lax.ppermute(other, 'tp', [(0, 1), (1, 0)])]
  transfers between devices with their start and end apart: 31 -> 34, of which waited for: 11 -> 14; matrix products, arithmetic and copies ran while one was open for 29% -> 31% of each run, Pallas kernels for 0% -> 0%
where the time goes in v7:
time: 143 us; the launch traced here: 141 us
  waiting for transfers between devices  48.9 us (34%)
  local copies, waits for them, and re-layouts  39.9 us (28%)
  starting transfers between devices  21.3 us (15%)
  matrix products  18.2 us (13%)
  other arithmetic  10.6 us (7%)
  between operations  2.32 us (2%)
    ppermute x7, waiting for transfers between devices, gather_ring(): cur_a = lax.ppermute(cur_a, 'seq', forward)  32.9 us
    ppermute x7, starting transfers between devices, gather_ring(): cur_a = lax.ppermute(cur_a, 'seq', forward)  12.3 us
    concatenate x6, local copies, waits for them, and re-layouts, half(): stack = jnp.concatenate(got[first:last], axis=0)  11.6 us
    dot_general x4, matrix products, on_device(): jnp.dot(attention, out_weight[:, cols], preferred_element_type=jnp.float32)  11.1 us
    ppermute x4, waiting for transfers between devices, on_device(): came = lax.ppermute(other, 'tp', [(0, 1), (1, 0)])  10.5 us
    slice x19, local copies, waits for them, and re-layouts, on_device(): g[rows_dev, :2]  8.68 us
    unnamed x52, local copies, waits for them, and re-layouts  6.73 us
    ppermute x7, waiting for transfers between devices, gather_ring(): cur_b = lax.ppermute(cur_b, 'seq', backward)  4.78 us
  transfers between devices with their start and end apart: 34, of which 14 were waited for; matrix products, arithmetic and copies ran while one was open for 31% of the time, Pallas kernels for 0%

profile of v7, /device:TPU:0, one launch (start us, length us, event | category | flops | bytes accessed | tf_op | source)
XLA Modules:
  0.0 141.3 jit_solution(2903483917133237720)
XLA Ops:
  1.3 1.0 fusion.127
  2.5 1.0 fusion.128
  4.0 0.9 select_convert_fusion
  5.3 3.1 %collective-permute-start.1 = (bf16[128,1280]{0,1:T(8,128)(2,1)S(1)}, bf16[128,1280]{0,1:T(8,128)(2,1)S(1)}, u32[]{:S(2)}, u32[]{:S(2)}) collective-permute-start(bf16[128,1280]{0,1:T(8,128)(2,1)S(1)} %get-tuple-element.45), channel_id=1, source_target_pairs={{0,8},{2,10},{8,16},{10,18},{16,24},{18,26},{24,28},{26,30},{28,20... | collective-permute-start | bytes 983048 | tf_op jit(solution)/shard_map/ppermute | solution.py:36
  8.4 7.6 %collective-permute-done.1 = bf16[128,1280]{0,1:T(8,128)(2,1)S(1)} collective-permute-done((bf16[128,1280]{0,1:T(8,128)(2,1)S(1)}, bf16[128,1280]{0,1:T(8,128)(2,1)S(1)}, u32[]{:S(2)}, u32[]{:S(2)}) %collective-permute-start.1) | collective-permute-done | bytes 327712 | tf_op jit(solution)/shard_map/ppermute | solution.py:36
  16.0 1.8 %collective-permute-start.3 = (bf16[128,1280]{0,1:T(8,128)(2,1)S(1)}, bf16[128,1280]{0,1:T(8,128)(2,1)S(1)}, u32[]{:S(2)}, u32[]{:S(2)}) collective-permute-start(bf16[128,1280]{0,1:T(8,128)(2,1)S(1)} %collective-permute-done.1), channel_id=1, source_target_pairs={{0,8},{2,10},{8,16},{10,18},{16,24},{18,26},{24,28},{26,30},{28,20... | collective-permute-start | bytes 983048 | tf_op jit(solution)/shard_map/ppermute | solution.py:36
  18.5 6.4 %collective-permute-done.3 = bf16[128,1280]{0,1:T(8,128)(2,1)S(1)} collective-permute-done((bf16[128,1280]{0,1:T(8,128)(2,1)S(1)}, bf16[128,1280]{0,1:T(8,128)(2,1)S(1)}, u32[]{:S(2)}, u32[]{:S(2)}) %collective-permute-start.3) | collective-permute-done | bytes 327712 | tf_op jit(solution)/shard_map/ppermute | solution.py:36
  24.9 1.5 %collective-permute-start.5 = (bf16[128,1280]{0,1:T(8,128)(2,1)S(1)}, bf16[128,1280]{0,1:T(8,128)(2,1)}, u32[]{:S(2)}, u32[]{:S(2)}) collective-permute-start(bf16[128,1280]{0,1:T(8,128)(2,1)S(1)} %collective-permute-done.3), channel_id=1, source_target_pairs={{0,8},{2,10},{8,16},{10,18},{16,24},{18,26},{24,28},{26,30},{28,20... | collective-permute-start | bytes 983048 | tf_op jit(solution)/shard_map/ppermute | solution.py:36
  27.5 5.4 %collective-permute-done.5 = bf16[128,1280]{0,1:T(8,128)(2,1)} collective-permute-done((bf16[128,1280]{0,1:T(8,128)(2,1)S(1)}, bf16[128,1280]{0,1:T(8,128)(2,1)}, u32[]{:S(2)}, u32[]{:S(2)}) %collective-permute-start.5) | collective-permute-done | bytes 327712 | tf_op jit(solution)/shard_map/ppermute | solution.py:36
  33.0 1.2 collective-permute-start.7
  34.1 0.9 collective-permute-start.16
  35.0 0.8 pad_maximum_fusion.1
  36.4 3.9 %collective-permute-done.7 = bf16[128,1280]{0,1:T(8,128)(2,1)} collective-permute-done((bf16[128,1280]{0,1:T(8,128)(2,1)}, bf16[128,1280]{0,1:T(8,128)(2,1)}, u32[]{:S(2)}, u32[]{:S(2)}) %collective-permute-start.7) | collective-permute-done | bytes 327712 | tf_op jit(solution)/shard_map/ppermute | solution.py:36
  40.4 1.0 collective-permute-done.16
  41.3 1.0 fusion.126
  42.9 0.8 copy.39
  44.2 0.8 pad_maximum_fusion.2
  45.5 0.8 slice.245
  46.2 0.8 slice.254
  47.0 0.7 slice.248
  47.8 0.8 slice.247
  48.5 0.7 slice.256
  49.2 0.7 slice.250
  50.0 0.7 slice.259
  50.7 1.6 %collective-permute-start.18 = (bf16[128,1280]{0,1:T(8,128)(2,1)}, bf16[128,1280]{0,1:T(8,128)(2,1)}, u32[]{:S(2)}, u32[]{:S(2)}) collective-permute-start(bf16[128,1280]{0,1:T(8,128)(2,1)} %collective-permute-done.7), channel_id=1, source_target_pairs={{0,8},{2,10},{8,16},{10,18},{16,24},{18,26},{24,28},{26,30},{28,20... | collective-permute-start | bytes 983048 | tf_op jit(solution)/shard_map/ppermute | solution.py:36
  52.8 0.7 slice.249
  53.5 0.8 slice.258
  54.2 0.7 slice.251
  55.0 0.8 slice.260
  56.5 4.8 %concatenate.49 = bf16[1280,1280]{0,1:T(8,128)(2,1)S(1)} concatenate(bf16[120,1280]{0,1:T(8,128)(2,1)} %pad_maximum_fusion.1, bf16[8,1280]{0,1:T(8,128)(2,1)} %copy-done.3, bf16[128,1280]{0,1:T(8,128)(2,1)} %copy-done.15, bf16[128,1280]{0,1:T(8,128)(2,1)} %copy-done.11, bf16[128,1280]{0,1:T(8,128)(2,1)} %copy-done.17, bf16[128,1280]{0,1:T(8,128)(2,1)} %copy-done.13, ...), dimensions={0} | concatenate | bytes 6553600 | tf_op jit(solution)/shard_map/concatenate | solution.py:131
  61.3 1.9 %fusion.120 = (bf16[1280,640]{0,1:T(8,128)(2,1)}, bf16[1280,640]{0,1:T(8,128)(2,1)}) fusion(bf16[1280,1280]{0,1:T(8,128)(2,1)S(1)} %concatenate.49), kind=kLoop, calls=%fused_computation.175 | loop fusion | bytes 6553600 | tf_op jit(solution)/shard_map/slice | solution.py:132
  63.5 4.8 %concatenate.52 = bf16[1280,1280]{0,1:T(8,128)(2,1)S(1)} concatenate(bf16[120,1280]{0,1:T(8,128)(2,1)} %pad_maximum_fusion.2, bf16[8,1280]{0,1:T(8,128)(2,1)} %copy-done.3, bf16[128,1280]{0,1:T(8,128)(2,1)} %copy-done.12, bf16[128,1280]{0,1:T(8,128)(2,1)} %copy-done.9, bf16[128,1280]{0,1:T(8,128)(2,1)} %copy-done.16, bf16[128,1280]{0,1:T(8,128)(2,1)} %copy-done.10, ...), dimensions={0} | concatenate | bytes 6553600 | tf_op jit(solution)/shard_map/concatenate | solution.py:131
  68.3 1.4 fusion.121
  70.3 0.8 fusion.133
  71.9 1.0 constant_dynamic-update-slice_fusion.3
  73.0 1.6 %collective-permute-start.20 = (bf16[128,1280]{0,1:T(8,128)(2,1)}, bf16[128,1280]{0,1:T(8,128)(2,1)S(1)}, u32[]{:S(2)}, u32[]{:S(2)}) collective-permute-start(bf16[128,1280]{0,1:T(8,128)(2,1)} %collective-permute-done.18), channel_id=1, source_target_pairs={{0,8},{2,10},{8,16},{10,18},{16,24},{18,26},{24,28},{26,30},{28,20... | collective-permute-start | bytes 983048 | tf_op jit(solution)/shard_map/ppermute | solution.py:36
  74.6 0.8 fusion.130
  75.4 1.0 constant_dynamic-update-slice_fusion.9
  77.6 5.7 %collective-permute-done.20 = bf16[128,1280]{0,1:T(8,128)(2,1)S(1)} collective-permute-done((bf16[128,1280]{0,1:T(8,128)(2,1)}, bf16[128,1280]{0,1:T(8,128)(2,1)S(1)}, u32[]{:S(2)}, u32[]{:S(2)}) %collective-permute-start.20) | collective-permute-done | bytes 327712 | tf_op jit(solution)/shard_map/ppermute | solution.py:36
  83.3 1.6 %collective-permute-start.22 = (bf16[128,1280]{0,1:T(8,128)(2,1)S(1)}, bf16[128,1280]{0,1:T(8,128)(2,1)S(1)}, u32[]{:S(2)}, u32[]{:S(2)}) collective-permute-start(bf16[128,1280]{0,1:T(8,128)(2,1)S(1)} %collective-permute-done.20), channel_id=1, source_target_pairs={{0,8},{2,10},{8,16},{10,18},{16,24},{18,26},{24,28},{26,30},{28,20... | collective-permute-start | bytes 983048 | tf_op jit(solution)/shard_map/ppermute | solution.py:36
  84.9 1.6 %collective-permute-done.26 = bf16[128,1280]{0,1:T(8,128)(2,1)S(1)} collective-permute-done((bf16[128,1280]{0,1:T(8,128)(2,1)}, bf16[128,1280]{0,1:T(8,128)(2,1)S(1)}, u32[]{:S(2)}, u32[]{:S(2)}) %collective-permute-start.26) | collective-permute-done | bytes 327712 | tf_op jit(solution)/shard_map/ppermute | solution.py:37
  88.2 1.0 fusion.123
  89.6 3.9 %collective-permute-done.22 = bf16[128,1280]{0,1:T(8,128)(2,1)S(1)} collective-permute-done((bf16[128,1280]{0,1:T(8,128)(2,1)S(1)}, bf16[128,1280]{0,1:T(8,128)(2,1)S(1)}, u32[]{:S(2)}, u32[]{:S(2)}) %collective-permute-start.22) | collective-permute-done | bytes 327712 | tf_op jit(solution)/shard_map/ppermute | solution.py:36
  94.5 2.3 %collective-permute-done.28 = bf16[128,1280]{0,1:T(8,128)(2,1)} collective-permute-done((bf16[128,1280]{0,1:T(8,128)(2,1)S(1)}, bf16[128,1280]{0,1:T(8,128)(2,1)}, u32[]{:S(2)}, u32[]{:S(2)}) %collective-permute-start.28) | collective-permute-done | bytes 327712 | tf_op jit(solution)/shard_map/ppermute | solution.py:37
  97.1 1.7 %constant_dynamic-update-slice_fusion.11 = bf16[256,1280]{0,1:T(8,128)(2,1)} fusion(bf16[128,1280]{0,1:T(8,128)(2,1)} %collective-permute-done.28), kind=kLoop, calls=%fused_computation.122 | loop fusion | bytes 655360
  100.3 0.9 fusion.47
  101.7 1.0 fusion.56
  102.7 1.1 copy.49
  103.8 1.7 %constant_dynamic-update-slice_fusion.10 = bf16[256,1280]{0,1:T(8,128)(2,1)} fusion(bf16[256,1280]{0,1:T(8,128)(2,1)} %constant_dynamic-update-slice_fusion.11, bf16[128,1280]{0,1:T(8,128)(2,1)} %collective-permute-done.29), kind=kLoop, calls=%fused_computation.121 | loop fusion | bytes 655360 | tf_op jit(solution)/shard_map/concatenate | solution.py:131
  105.5 1.2 fusion.125
  107.5 0.9 fusion.53
  109.9 2.6 %fusion.8 = f32[120,1280]{1,0:T(8,128)S(1)} fusion(bf16[1280,5120]{1,0:T(8,128)(2,1)} %param.15, bf16[120,640]{0,1:T(8,128)(2,1)S(1)} %bitcast.316, bf16[120,640]{0,1:T(8,128)(2,1)S(1)} %bitcast.312), kind=kOutput, calls=%fused_computation.10 | convolution fusion | flops 393830400 | bytes 4198400 | tf_op jit(solution)/shard_map/dot_general | solution.py:150
  112.5 2.6 %fusion.6 = f32[120,1280]{1,0:T(8,128)S(1)} fusion(bf16[1280,5120]{1,0:T(8,128)(2,1)} %param.15, bf16[120,640]{0,1:T(8,128)(2,1)S(1)} %bitcast.317, bf16[120,640]{0,1:T(8,128)(2,1)S(1)} %bitcast.313), kind=kOutput, calls=%fused_computation.8 | convolution fusion | flops 393830400 | bytes 4198400 | tf_op jit(solution)/shard_map/dot_general | solution.py:150
  115.0 2.6 %fusion.4 = f32[120,1280]{1,0:T(8,128)S(1)} fusion(bf16[1280,5120]{1,0:T(8,128)(2,1)} %param.15, bf16[120,640]{0,1:T(8,128)(2,1)S(1)} %bitcast.318, bf16[120,640]{0,1:T(8,128)(2,1)S(1)} %bitcast.314), kind=kOutput, calls=%fused_computation.6 | convolution fusion | flops 393830400 | bytes 4198400 | tf_op jit(solution)/shard_map/dot_general | solution.py:150
  117.6 3.4 %fusion.10 = f32[120,1280]{1,0:T(8,128)} fusion(bf16[1280,5120]{1,0:T(8,128)(2,1)} %param.15, bf16[120,640]{0,1:T(8,128)(2,1)S(1)} %bitcast.319, bf16[120,640]{0,1:T(8,128)(2,1)S(1)} %bitcast.315), kind=kOutput, calls=%fused_computation.12 | convolution fusion | flops 393830400 | bytes 4198400 | tf_op jit(solution)/shard_map/dot_general | solution.py:150
  121.7 1.5 %collective-permute-start.31 = (bf16[60,1280]{1,0:T(8,128)(2,1)}, bf16[60,1280]{1,0:T(8,128)(2,1)S(1)}, u32[]{:S(2)}, u32[]{:S(2)}) collective-permute-start(bf16[60,1280]{1,0:T(8,128)(2,1)} %bitcast_convert_fusion.2), channel_id=1, source_target_pairs={{0,1},{1,0},{2,3},{3,2},{4,5},{5,4},{6,7},{7,6},{8,9},{9,8},{10,11... | collective-permute-start | bytes 460808 | tf_op jit(solution)/shard_map/ppermute | solution.py:154
  124.6 0.7 bitcast_convert_fusion
  125.3 1.5 %collective-permute-start.33 = (bf16[60,1280]{1,0:T(8,128)(2,1)}, bf16[60,1280]{1,0:T(8,128)(2,1)}, u32[]{:S(2)}, u32[]{:S(2)}) collective-permute-start(bf16[60,1280]{1,0:T(8,128)(2,1)} %bitcast_convert_fusion), channel_id=1, source_target_pairs={{0,1},{1,0},{2,3},{3,2},{4,5},{5,4},{6,7},{7,6},{8,9},{9,8},{10,11... | collective-permute-start | bytes 460808 | tf_op jit(solution)/shard_map/ppermute | solution.py:154
  126.8 1.1 reshape.296
  128.9 3.6 %collective-permute-done.32 = bf16[60,1280]{1,0:T(8,128)(2,1)} collective-permute-done((bf16[60,1280]{1,0:T(8,128)(2,1)}, bf16[60,1280]{1,0:T(8,128)(2,1)}, u32[]{:S(2)}, u32[]{:S(2)}) %collective-permute-start.32) | collective-permute-done | bytes 153632 | tf_op jit(solution)/shard_map/ppermute | solution.py:154
  132.6 3.5 %collective-permute-done.33 = bf16[60,1280]{1,0:T(8,128)(2,1)} collective-permute-done((bf16[60,1280]{1,0:T(8,128)(2,1)}, bf16[60,1280]{1,0:T(8,128)(2,1)}, u32[]{:S(2)}, u32[]{:S(2)}) %collective-permute-start.33) | collective-permute-done | bytes 153632 | tf_op jit(solution)/shard_map/ppermute | solution.py:154
  136.1 3.0 %collective-permute-done.30 = bf16[60,1280]{1,0:T(8,128)(2,1)S(1)} collective-permute-done((bf16[60,1280]{1,0:T(8,128)(2,1)S(1)}, bf16[60,1280]{1,0:T(8,128)(2,1)S(1)}, u32[]{:S(2)}, u32[]{:S(2)}) %collective-permute-start.30) | collective-permute-done | bytes 153632 | tf_op jit(solution)/shard_map/ppermute | solution.py:154
  139.1 1.3 fusion.85
  140.4 0.9 pad_maximum_fusion
  (153 shorter events, 19.4 us)
Async XLA Ops:
  5.0 37.7 %copy-start.3 = (bf16[8,1280]{0,1:T(8,128)(2,1)}, bf16[8,1280]{0,1:T(8,128)(2,1)S(1)}, u32[]{:S(2)}) copy-start(bf16[8,1280]{0,1:T(8,128)(2,1)S(1)} %select_convert_fusion) | copy-start | bytes 61444
  5.3 10.7 %collective-permute-start.1 = (bf16[128,1280]{0,1:T(8,128)(2,1)S(1)}, bf16[128,1280]{0,1:T(8,128)(2,1)S(1)}, u32[]{:S(2)}, u32[]{:S(2)}) collective-permute-start(bf16[128,1280]{0,1:T(8,128)(2,1)S(1)} %get-tuple-element.45), channel_id=1, source_target_pairs={{0,8},{2,10},{8,16},{10,18},{16,24},{18,26},{24,28},{26,30},{28,20... | collective-permute-start | bytes 983048 | tf_op jit(solution)/shard_map/ppermute | solution.py:36
  8.3 9.5 %collective-permute-start.10 = (bf16[128,1280]{0,1:T(8,128)(2,1)S(1)}, bf16[128,1280]{0,1:T(8,128)(2,1)S(1)}, u32[]{:S(2)}, u32[]{:S(2)}) collective-permute-start(bf16[128,1280]{0,1:T(8,128)(2,1)S(1)} %get-tuple-element.46), channel_id=1, source_target_pairs={{8,0},{10,2},{16,8},{18,10},{24,16},{26,18},{28,24},{30,26},{20,28... | collective-permute-start | bytes 983048 | tf_op jit(solution)/shard_map/ppermute | solution.py:37
  16.0 29.0 %copy-start.11 = (bf16[128,1280]{0,1:T(8,128)(2,1)}, bf16[128,1280]{0,1:T(8,128)(2,1)S(1)}, u32[]{:S(2)}) copy-start(bf16[128,1280]{0,1:T(8,128)(2,1)S(1)} %collective-permute-done.1) | copy-start | bytes 983044
  16.0 8.9 %collective-permute-start.3 = (bf16[128,1280]{0,1:T(8,128)(2,1)S(1)}, bf16[128,1280]{0,1:T(8,128)(2,1)S(1)}, u32[]{:S(2)}, u32[]{:S(2)}) collective-permute-start(bf16[128,1280]{0,1:T(8,128)(2,1)S(1)} %collective-permute-done.1), channel_id=1, source_target_pairs={{0,8},{2,10},{8,16},{10,18},{16,24},{18,26},{24,28},{26,30},{28,20... | collective-permute-start | bytes 983048 | tf_op jit(solution)/shard_map/ppermute | solution.py:36
  17.8 27.3 %copy-start.9 = (bf16[128,1280]{0,1:T(8,128)(2,1)}, bf16[128,1280]{0,1:T(8,128)(2,1)S(1)}, u32[]{:S(2)}) copy-start(bf16[128,1280]{0,1:T(8,128)(2,1)S(1)} %collective-permute-done.10) | copy-start | bytes 983044
  17.8 8.6 %collective-permute-start.12 = (bf16[128,1280]{0,1:T(8,128)(2,1)S(1)}, bf16[128,1280]{0,1:T(8,128)(2,1)S(1)}, u32[]{:S(2)}, u32[]{:S(2)}) collective-permute-start(bf16[128,1280]{0,1:T(8,128)(2,1)S(1)} %collective-permute-done.10), channel_id=1, source_target_pairs={{8,0},{10,2},{16,8},{18,10},{24,16},{26,18},{28,24},{30,26},{20,28... | collective-permute-start | bytes 983048 | tf_op jit(solution)/shard_map/ppermute | solution.py:37
  18.0 8.9 %collective-permute-start = (bf16[128,1280]{0,1:T(8,128)(2,1)S(1)}, bf16[128,1280]{0,1:T(8,128)(2,1)S(1)}, u32[]{:S(2)}, u32[]{:S(2)}) collective-permute-start(bf16[128,1280]{0,1:T(8,128)(2,1)S(1)} %get-tuple-element.45), channel_id=1, source_target_pairs={{0,2},{2,0},{4,6},{6,4},{8,10},{10,8},{12,14},{14,12},{16,18},{18,... | collective-permute-start | bytes 983048 | tf_op jit(solution)/shard_map/ppermute | solution.py:40
  18.0 9.4 %collective-permute-start.9 = (bf16[128,1280]{0,1:T(8,128)(2,1)S(1)}, bf16[128,1280]{0,1:T(8,128)(2,1)S(1)}, u32[]{:S(2)}, u32[]{:S(2)}) collective-permute-start(bf16[128,1280]{0,1:T(8,128)(2,1)S(1)} %get-tuple-element.46), channel_id=1, source_target_pairs={{0,2},{2,0},{4,6},{6,4},{8,10},{10,8},{12,14},{14,12},{16,18},{18,... | collective-permute-start | bytes 983048 | tf_op jit(solution)/shard_map/ppermute | solution.py:41
  24.9 20.4 %copy-start.13 = (bf16[128,1280]{0,1:T(8,128)(2,1)}, bf16[128,1280]{0,1:T(8,128)(2,1)S(1)}, u32[]{:S(2)}) copy-start(bf16[128,1280]{0,1:T(8,128)(2,1)S(1)} %collective-permute-done.3) | copy-start | bytes 983044
  24.9 8.1 %collective-permute-start.5 = (bf16[128,1280]{0,1:T(8,128)(2,1)S(1)}, bf16[128,1280]{0,1:T(8,128)(2,1)}, u32[]{:S(2)}, u32[]{:S(2)}) collective-permute-start(bf16[128,1280]{0,1:T(8,128)(2,1)S(1)} %collective-permute-done.3), channel_id=1, source_target_pairs={{0,8},{2,10},{8,16},{10,18},{16,24},{18,26},{24,28},{26,30},{28,20... | collective-permute-start | bytes 983048 | tf_op jit(solution)/shard_map/ppermute | solution.py:36
  26.4 19.0 %copy-start.10 = (bf16[128,1280]{0,1:T(8,128)(2,1)}, bf16[128,1280]{0,1:T(8,128)(2,1)S(1)}, u32[]{:S(2)}) copy-start(bf16[128,1280]{0,1:T(8,128)(2,1)S(1)} %collective-permute-done.12) | copy-start | bytes 983044
  26.4 7.8 %collective-permute-start.14 = (bf16[128,1280]{0,1:T(8,128)(2,1)S(1)}, bf16[128,1280]{0,1:T(8,128)(2,1)S(1)}, u32[]{:S(2)}, u32[]{:S(2)}) collective-permute-start(bf16[128,1280]{0,1:T(8,128)(2,1)S(1)} %collective-permute-done.12), channel_id=1, source_target_pairs={{8,0},{10,2},{16,8},{18,10},{24,16},{26,18},{28,24},{30,26},{20,28... | collective-permute-start | bytes 983048 | tf_op jit(solution)/shard_map/ppermute | solution.py:37
  26.9 8.9 %collective-permute-start.2 = (bf16[128,1280]{0,1:T(8,128)(2,1)S(1)}, bf16[128,1280]{0,1:T(8,128)(2,1)S(1)}, u32[]{:S(2)}, u32[]{:S(2)}) collective-permute-start(bf16[128,1280]{0,1:T(8,128)(2,1)S(1)} %collective-permute-done.1), channel_id=1, source_target_pairs={{0,2},{2,0},{4,6},{6,4},{8,10},{10,8},{12,14},{14,12},{16,18},{18,... | collective-permute-start | bytes 983048 | tf_op jit(solution)/shard_map/ppermute | solution.py:40
  26.9 18.2 %copy-start.15 = (bf16[128,1280]{0,1:T(8,128)(2,1)}, bf16[128,1280]{0,1:T(8,128)(2,1)S(1)}, u32[]{:S(2)}) copy-start(bf16[128,1280]{0,1:T(8,128)(2,1)S(1)} %collective-permute-done) | copy-start | bytes 983044
  26.9 8.9 %collective-permute-start.11 = (bf16[128,1280]{0,1:T(8,128)(2,1)S(1)}, bf16[128,1280]{0,1:T(8,128)(2,1)S(1)}, u32[]{:S(2)}, u32[]{:S(2)}) collective-permute-start(bf16[128,1280]{0,1:T(8,128)(2,1)S(1)} %collective-permute-done.10), channel_id=1, source_target_pairs={{0,2},{2,0},{4,6},{6,4},{8,10},{10,8},{12,14},{14,12},{16,18},{18,... | collective-permute-start | bytes 983048 | tf_op jit(solution)/shard_map/ppermute | solution.py:41
  27.5 17.8 %copy-start.12 = (bf16[128,1280]{0,1:T(8,128)(2,1)}, bf16[128,1280]{0,1:T(8,128)(2,1)S(1)}, u32[]{:S(2)}) copy-start(bf16[128,1280]{0,1:T(8,128)(2,1)S(1)} %collective-permute-done.9) | copy-start | bytes 983044
  27.5 8.9 %collective-permute-start.4 = (bf16[128,1280]{0,1:T(8,128)(2,1)S(1)}, bf16[128,1280]{0,1:T(8,128)(2,1)S(1)}, u32[]{:S(2)}, u32[]{:S(2)}) collective-permute-start(bf16[128,1280]{0,1:T(8,128)(2,1)S(1)} %collective-permute-done.3), channel_id=1, source_target_pairs={{0,2},{2,0},{4,6},{6,4},{8,10},{10,8},{12,14},{14,12},{16,18},{18,... | collective-permute-start | bytes 983048 | tf_op jit(solution)/shard_map/ppermute | solution.py:40
  33.0 7.4 %collective-permute-start.7 = (bf16[128,1280]{0,1:T(8,128)(2,1)}, bf16[128,1280]{0,1:T(8,128)(2,1)}, u32[]{:S(2)}, u32[]{:S(2)}) collective-permute-start(bf16[128,1280]{0,1:T(8,128)(2,1)} %collective-permute-done.5), channel_id=1, source_target_pairs={{0,8},{2,10},{8,16},{10,18},{16,24},{18,26},{24,28},{26,30},{28,20... | collective-permute-start | bytes 983048 | tf_op jit(solution)/shard_map/ppermute | solution.py:36
  34.1 13.6 %copy-start.14 = (bf16[128,1280]{0,1:T(8,128)(2,1)}, bf16[128,1280]{0,1:T(8,128)(2,1)S(1)}, u32[]{:S(2)}) copy-start(bf16[128,1280]{0,1:T(8,128)(2,1)S(1)} %collective-permute-done.14) | copy-start | bytes 983044
  34.1 7.2 %collective-permute-start.16 = (bf16[128,1280]{0,1:T(8,128)(2,1)S(1)}, bf16[128,1280]{0,1:T(8,128)(2,1)}, u32[]{:S(2)}, u32[]{:S(2)}) collective-permute-start(bf16[128,1280]{0,1:T(8,128)(2,1)S(1)} %collective-permute-done.14), channel_id=1, source_target_pairs={{8,0},{10,2},{16,8},{18,10},{24,16},{26,18},{28,24},{30,26},{20,28... | collective-permute-start | bytes 983048 | tf_op jit(solution)/shard_map/ppermute | solution.py:37
  35.8 5.5 %copy-start.17 = (bf16[128,1280]{0,1:T(8,128)(2,1)}, bf16[128,1280]{0,1:T(8,128)(2,1)S(1)}, u32[]{:S(2)}) copy-start(bf16[128,1280]{0,1:T(8,128)(2,1)S(1)} %collective-permute-done.2) | copy-start | bytes 983044
  35.8 12.7 %collective-permute-start.13 = (bf16[128,1280]{0,1:T(8,128)(2,1)S(1)}, bf16[128,1280]{0,1:T(8,128)(2,1)}, u32[]{:S(2)}, u32[]{:S(2)}) collective-permute-start(bf16[128,1280]{0,1:T(8,128)(2,1)S(1)} %collective-permute-done.12), channel_id=1, source_target_pairs={{0,2},{2,0},{4,6},{6,4},{8,10},{10,8},{12,14},{14,12},{16,18},{18,... | collective-permute-start | bytes 983048 | tf_op jit(solution)/shard_map/ppermute | solution.py:41
  35.8 5.5 %copy-start.16 = (bf16[128,1280]{0,1:T(8,128)(2,1)}, bf16[128,1280]{0,1:T(8,128)(2,1)S(1)}, u32[]{:S(2)}) copy-start(bf16[128,1280]{0,1:T(8,128)(2,1)S(1)} %collective-permute-done.11) | copy-start | bytes 983044
  35.8 16.5 %collective-permute-start.6 = (bf16[128,1280]{0,1:T(8,128)(2,1)}, bf16[128,1280]{0,1:T(8,128)(2,1)}, u32[]{:S(2)}, u32[]{:S(2)}) collective-permute-start(bf16[128,1280]{0,1:T(8,128)(2,1)} %collective-permute-done.5), channel_id=1, source_target_pairs={{0,2},{2,0},{4,6},{6,4},{8,10},{10,8},{12,14},{14,12},{16,18},{18,... | collective-permute-start | bytes 983048 | tf_op jit(solution)/shard_map/ppermute | solution.py:40
  36.3 6.0 %copy-start.18 = (bf16[128,1280]{0,1:T(8,128)(2,1)}, bf16[128,1280]{0,1:T(8,128)(2,1)S(1)}, u32[]{:S(2)}) copy-start(bf16[128,1280]{0,1:T(8,128)(2,1)S(1)} %collective-permute-done.4) | copy-start | bytes 983044
  36.3 17.1 %collective-permute-start.15 = (bf16[128,1280]{0,1:T(8,128)(2,1)S(1)}, bf16[128,1280]{0,1:T(8,128)(2,1)}, u32[]{:S(2)}, u32[]{:S(2)}) collective-permute-start(bf16[128,1280]{0,1:T(8,128)(2,1)S(1)} %collective-permute-done.14), channel_id=1, source_target_pairs={{0,2},{2,0},{4,6},{6,4},{8,10},{10,8},{12,14},{14,12},{16,18},{18,... | collective-permute-start | bytes 983048 | tf_op jit(solution)/shard_map/ppermute | solution.py:41
  40.4 13.9 %collective-permute-start.8 = (bf16[128,1280]{0,1:T(8,128)(2,1)}, bf16[128,1280]{0,1:T(8,128)(2,1)}, u32[]{:S(2)}, u32[]{:S(2)}) collective-permute-start(bf16[128,1280]{0,1:T(8,128)(2,1)} %collective-permute-done.7), channel_id=1, source_target_pairs={{0,2},{2,0},{4,6},{6,4},{8,10},{10,8},{12,14},{14,12},{16,18},{18,... | collective-permute-start | bytes 983048 | tf_op jit(solution)/shard_map/ppermute | solution.py:40
  41.3 13.7 %collective-permute-start.17 = (bf16[128,1280]{0,1:T(8,128)(2,1)}, bf16[128,1280]{0,1:T(8,128)(2,1)}, u32[]{:S(2)}, u32[]{:S(2)}) collective-permute-start(bf16[128,1280]{0,1:T(8,128)(2,1)} %collective-permute-done.16), channel_id=1, source_target_pairs={{0,2},{2,0},{4,6},{6,4},{8,10},{10,8},{12,14},{14,12},{16,18},{18,... | collective-permute-start | bytes 983048 | tf_op jit(solution)/shard_map/ppermute | solution.py:41
  50.7 21.2 %collective-permute-start.18 = (bf16[128,1280]{0,1:T(8,128)(2,1)}, bf16[128,1280]{0,1:T(8,128)(2,1)}, u32[]{:S(2)}, u32[]{:S(2)}) collective-permute-start(bf16[128,1280]{0,1:T(8,128)(2,1)} %collective-permute-done.7), channel_id=1, source_target_pairs={{0,8},{2,10},{8,16},{10,18},{16,24},{18,26},{24,28},{26,30},{28,20... | collective-permute-start | bytes 983048 | tf_op jit(solution)/shard_map/ppermute | solution.py:36
  52.3 23.1 %collective-permute-start.24 = (bf16[128,1280]{0,1:T(8,128)(2,1)}, bf16[128,1280]{0,1:T(8,128)(2,1)}, u32[]{:S(2)}, u32[]{:S(2)}) collective-permute-start(bf16[128,1280]{0,1:T(8,128)(2,1)} %collective-permute-done.16), channel_id=1, source_target_pairs={{8,0},{10,2},{16,8},{18,10},{24,16},{26,18},{28,24},{30,26},{20,28... | collective-permute-start | bytes 983048 | tf_op jit(solution)/shard_map/ppermute | solution.py:37
  68.3 2.0 %copy-start.2 = (bf16[1280,640]{0,1:T(8,128)(2,1)S(1)}, bf16[1280,640]{0,1:T(8,128)(2,1)}, u32[]{:S(2)}) copy-start(bf16[1280,640]{0,1:T(8,128)(2,1)} %get-tuple-element.29) | copy-start | bytes 4915204
  68.3 2.0 %copy-start.4 = (bf16[120,640]{0,1:T(8,128)(2,1)S(1)}, bf16[120,640]{0,1:T(8,128)(2,1)}, u32[]{:S(2)}) copy-start(bf16[120,640]{0,1:T(8,128)(2,1)} %copy.39) | copy-start | bytes 460804
  72.9 13.6 %collective-permute-start.19 = (bf16[128,1280]{0,1:T(8,128)(2,1)}, bf16[128,1280]{0,1:T(8,128)(2,1)S(1)}, u32[]{:S(2)}, u32[]{:S(2)}) collective-permute-start(bf16[128,1280]{0,1:T(8,128)(2,1)} %collective-permute-done.18), channel_id=1, source_target_pairs={{0,2},{2,0},{4,6},{6,4},{8,10},{10,8},{12,14},{14,12},{16,18},{18,... | collective-permute-start | bytes 983048 | tf_op jit(solution)/shard_map/ppermute | solution.py:40
  73.0 10.3 %collective-permute-start.20 = (bf16[128,1280]{0,1:T(8,128)(2,1)}, bf16[128,1280]{0,1:T(8,128)(2,1)S(1)}, u32[]{:S(2)}, u32[]{:S(2)}) collective-permute-start(bf16[128,1280]{0,1:T(8,128)(2,1)} %collective-permute-done.18), channel_id=1, source_target_pairs={{0,8},{2,10},{8,16},{10,18},{16,24},{18,26},{24,28},{26,30},{28,20... | collective-permute-start | bytes 983048 | tf_op jit(solution)/shard_map/ppermute | solution.py:36
  76.4 10.0 %collective-permute-start.26 = (bf16[128,1280]{0,1:T(8,128)(2,1)}, bf16[128,1280]{0,1:T(8,128)(2,1)S(1)}, u32[]{:S(2)}, u32[]{:S(2)}) collective-permute-start(bf16[128,1280]{0,1:T(8,128)(2,1)} %collective-permute-done.24), channel_id=1, source_target_pairs={{8,0},{10,2},{16,8},{18,10},{24,16},{26,18},{28,24},{30,26},{20,28... | collective-permute-start | bytes 983048 | tf_op jit(solution)/shard_map/ppermute | solution.py:37
  77.0 10.1 %collective-permute-start.25 = (bf16[128,1280]{0,1:T(8,128)(2,1)}, bf16[128,1280]{0,1:T(8,128)(2,1)S(1)}, u32[]{:S(2)}, u32[]{:S(2)}) collective-permute-start(bf16[128,1280]{0,1:T(8,128)(2,1)} %collective-permute-done.24), channel_id=1, source_target_pairs={{0,2},{2,0},{4,6},{6,4},{8,10},{10,8},{12,14},{14,12},{16,18},{18,... | collective-permute-start | bytes 983048 | tf_op jit(solution)/shard_map/ppermute | solution.py:41
  83.3 4.0 %collective-permute-start.21 = (bf16[128,1280]{0,1:T(8,128)(2,1)S(1)}, bf16[128,1280]{0,1:T(8,128)(2,1)S(1)}, u32[]{:S(2)}, u32[]{:S(2)}) collective-permute-start(bf16[128,1280]{0,1:T(8,128)(2,1)S(1)} %collective-permute-done.20), channel_id=1, source_target_pairs={{0,2},{2,0},{4,6},{6,4},{8,10},{10,8},{12,14},{14,12},{16,18},{18,... | collective-permute-start | bytes 983048 | tf_op jit(solution)/shard_map/ppermute | solution.py:40
  83.3 10.1 %collective-permute-start.22 = (bf16[128,1280]{0,1:T(8,128)(2,1)S(1)}, bf16[128,1280]{0,1:T(8,128)(2,1)S(1)}, u32[]{:S(2)}, u32[]{:S(2)}) collective-permute-start(bf16[128,1280]{0,1:T(8,128)(2,1)S(1)} %collective-permute-done.20), channel_id=1, source_target_pairs={{0,8},{2,10},{8,16},{10,18},{16,24},{18,26},{24,28},{26,30},{28,20... | collective-permute-start | bytes 983048 | tf_op jit(solution)/shard_map/ppermute | solution.py:36
  86.5 1.6 %collective-permute-start.27 = (bf16[128,1280]{0,1:T(8,128)(2,1)S(1)}, bf16[128,1280]{0,1:T(8,128)(2,1)S(1)}, u32[]{:S(2)}, u32[]{:S(2)}) collective-permute-start(bf16[128,1280]{0,1:T(8,128)(2,1)S(1)} %collective-permute-done.26), channel_id=1, source_target_pairs={{0,2},{2,0},{4,6},{6,4},{8,10},{10,8},{12,14},{14,12},{16,18},{18,... | collective-permute-start | bytes 983048 | tf_op jit(solution)/shard_map/ppermute | solution.py:41
  86.5 10.2 %collective-permute-start.28 = (bf16[128,1280]{0,1:T(8,128)(2,1)S(1)}, bf16[128,1280]{0,1:T(8,128)(2,1)}, u32[]{:S(2)}, u32[]{:S(2)}) collective-permute-start(bf16[128,1280]{0,1:T(8,128)(2,1)S(1)} %collective-permute-done.26), channel_id=1, source_target_pairs={{8,0},{10,2},{16,8},{18,10},{24,16},{26,18},{28,24},{30,26},{20,28... | collective-permute-start | bytes 983048 | tf_op jit(solution)/shard_map/ppermute | solution.py:37
  93.9 4.9 %collective-permute-start.23 = (bf16[128,1280]{0,1:T(8,128)(2,1)S(1)}, bf16[128,1280]{0,1:T(8,128)(2,1)S(1)}, u32[]{:S(2)}, u32[]{:S(2)}) collective-permute-start(bf16[128,1280]{0,1:T(8,128)(2,1)S(1)} %collective-permute-done.22), channel_id=1, source_target_pairs={{0,2},{2,0},{4,6},{6,4},{8,10},{10,8},{12,14},{14,12},{16,18},{18,... | collective-permute-start | bytes 983048 | tf_op jit(solution)/shard_map/ppermute | solution.py:40
  94.4 4.5 %copy-start = (f32[5,120,512]{2,1,0:T(8,128)}, f32[5,120,512]{2,1,0:T(8,128)S(1)}, u32[]{:S(2)}) copy-start(f32[5,120,512]{2,1,0:T(8,128)S(1)} %get-tuple-element.64) | copy-start | bytes 3686404
  96.7 7.0 %collective-permute-start.29 = (bf16[128,1280]{0,1:T(8,128)(2,1)}, bf16[128,1280]{0,1:T(8,128)(2,1)}, u32[]{:S(2)}, u32[]{:S(2)}) collective-permute-start(bf16[128,1280]{0,1:T(8,128)(2,1)} %collective-permute-done.28), channel_id=1, source_target_pairs={{0,2},{2,0},{4,6},{6,4},{8,10},{10,8},{12,14},{14,12},{16,18},{18,... | collective-permute-start | bytes 983048 | tf_op jit(solution)/shard_map/ppermute | solution.py:41
  98.9 1.4 %copy-start.7 = (bf16[1280,640]{0,1:T(8,128)(2,1)S(1)}, bf16[1280,640]{0,1:T(8,128)(2,1)}, u32[]{:S(2)}) copy-start(bf16[1280,640]{0,1:T(8,128)(2,1)} %get-tuple-element.30) | copy-start | bytes 4915204
  105.5 1.9 %copy-start.6 = (bf16[1280,640]{0,1:T(8,128)(2,1)S(1)}, bf16[1280,640]{0,1:T(8,128)(2,1)}, u32[]{:S(2)}) copy-start(bf16[1280,640]{0,1:T(8,128)(2,1)} %get-tuple-element.32) | copy-start | bytes 4915204
  107.4 1.3 copy-start.1
  107.4 1.4 %copy-start.5 = (bf16[512,640]{0,1:T(8,128)(2,1)S(1)}, bf16[512,640]{0,1:T(8,128)(2,1)}, u32[]{:S(2)}) copy-start(bf16[512,640]{0,1:T(8,128)(2,1)} %get-tuple-element.35) | copy-start | bytes 1966084
  121.7 7.2 %collective-permute-start.31 = (bf16[60,1280]{1,0:T(8,128)(2,1)}, bf16[60,1280]{1,0:T(8,128)(2,1)S(1)}, u32[]{:S(2)}, u32[]{:S(2)}) collective-permute-start(bf16[60,1280]{1,0:T(8,128)(2,1)} %bitcast_convert_fusion.2), channel_id=1, source_target_pairs={{0,1},{1,0},{2,3},{3,2},{4,5},{5,4},{6,7},{7,6},{8,9},{9,8},{10,11... | collective-permute-start | bytes 460808 | tf_op jit(solution)/shard_map/ppermute | solution.py:154
  124.0 4.6 %copy-start.19 = (f32[5120]{0:T(1024)S(1)}, f32[5120]{0:T(1024)}, u32[]{:S(2)}) copy-start(f32[5120]{0:T(1024)} %param.14) | copy-start | bytes 61444
  124.0 15.1 %copy-start.8 = (bf16[60,5120]{1,0:T(8,128)(2,1)S(1)}, bf16[60,5120]{1,0:T(8,128)(2,1)}, u32[]{:S(2)}) copy-start(bf16[60,5120]{1,0:T(8,128)(2,1)} %param.10) | copy-start | bytes 1843204
  124.0 8.6 %collective-permute-start.32 = (bf16[60,1280]{1,0:T(8,128)(2,1)}, bf16[60,1280]{1,0:T(8,128)(2,1)}, u32[]{:S(2)}, u32[]{:S(2)}) collective-permute-start(bf16[60,1280]{1,0:T(8,128)(2,1)} %bitcast_convert_fusion.1), channel_id=1, source_target_pairs={{0,1},{1,0},{2,3},{3,2},{4,5},{5,4},{6,7},{7,6},{8,9},{9,8},{10,11... | collective-permute-start | bytes 460808 | tf_op jit(solution)/shard_map/ppermute | solution.py:154
  125.3 10.8 %collective-permute-start.33 = (bf16[60,1280]{1,0:T(8,128)(2,1)}, bf16[60,1280]{1,0:T(8,128)(2,1)}, u32[]{:S(2)}, u32[]{:S(2)}) collective-permute-start(bf16[60,1280]{1,0:T(8,128)(2,1)} %bitcast_convert_fusion), channel_id=1, source_target_pairs={{0,1},{1,0},{2,3},{3,2},{4,5},{5,4},{6,7},{7,6},{8,9},{9,8},{10,11... | collective-permute-start | bytes 460808 | tf_op jit(solution)/shard_map/ppermute | solution.py:154
  127.9 11.1 %collective-permute-start.30 = (bf16[60,1280]{1,0:T(8,128)(2,1)S(1)}, bf16[60,1280]{1,0:T(8,128)(2,1)S(1)}, u32[]{:S(2)}, u32[]{:S(2)}) collective-permute-start(bf16[60,1280]{1,0:T(8,128)(2,1)S(1)} %bitcast_convert_fusion.3), channel_id=1, source_target_pairs={{0,1},{1,0},{2,3},{3,2},{4,5},{5,4},{6,7},{7,6},{8,9},{9,8},{10,11... | collective-permute-start | bytes 460808 | tf_op jit(solution)/shard_map/ppermute | solution.py:154

commit v8 on v6

--- a/solution.py
+++ b/solution.py
@@ -123,6 +123,14 @@
         phases = [(0, known + 1), (known + 1, chips - 1), (chips - 1, chips)]
         phases = [(2 * lo, 2 * hi) for lo, hi in phases if hi > lo]
 
+        anchor = 2 * max(chips - 2, 0)
+        early = 2 * (chips - 1)
+        held_a, held_b, _ = lax.optimization_barrier(
+            (got_a[:early], got_b[:early], (got_a[anchor], got_b[anchor]))
+        )
+        got_a = list(held_a) + got_a[early:]
+        got_b = list(held_b) + got_b[early:]
+
         def half(got, limits, lo, hi):
             width = (hi - lo) * HEAD
             q3 = queries[:, lo * HEAD : hi * HEAD].reshape(rows_dev, hi - lo, HEAD)

time: 141 us -> 134 us (0.950)
  waiting for transfers between devices: 54.1 us -> 51.5 us
  local copies, waits for them, and re-layouts: 40.4 us -> 37.9 us
  other arithmetic: 10.2 us -> 8.55 us
    unnamed x52 -> x50, local copies, waits for them, and re-layouts: 6.75 us -> 14.3 us
    concatenate x6, local copies, waits for them, and re-layouts: 11.6 us -> 4.18 us  [half(): stack = jnp.concatenate(got[first:last], axis=0)]
    slice x2, local copies, waits for them, and re-layouts: 3.28 us -> 1.62 us  [half(): keys = stack[:, :width].reshape(-1, hi - lo, HEAD)]
    concatenate x3 -> x1, other arithmetic: 1.84 us -> 0.27 us  [on_device(): jnp.concatenate([jnp.concatenate([key_rows[:, cut:], value_rows[:, cut:]]...]
  transfers between devices with their start and end apart: 31 -> 31, of which waited for: 11 -> 10; matrix products, arithmetic and copies ran while one was open for 29% -> 28% of each run, Pallas kernels for 0% -> 0%
where the time goes in v8:
time: 134 us; the launch traced here: 133 us
  waiting for transfers between devices  51.5 us (38%)
  local copies, waits for them, and re-layouts  37.9 us (28%)
  starting transfers between devices  19.6 us (15%)
  matrix products  13.1 us (10%)
  other arithmetic  8.55 us (6%)
  between operations  2.34 us (2%)
    ppermute x7, waiting for transfers between devices, gather_ring(): cur_a = lax.ppermute(cur_a, 'seq', forward)  31.7 us
    ppermute x1, waiting for transfers between devices, on_device(): came = lax.ppermute(other, 'tp', [(0, 1), (1, 0)])  15.2 us
    unnamed x50, local copies, waits for them, and re-layouts  14.3 us
    ppermute x7, starting transfers between devices, gather_ring(): cur_a = lax.ppermute(cur_a, 'seq', forward)  12.2 us
    slice x19, local copies, waits for them, and re-layouts, on_device(): g[rows_dev, :2]  8.77 us
    dot_general x1, matrix products, on_device(): partial = jnp.dot(attention, out_weight, preferred_element_type=jnp.float32)  6.64 us
    ppermute x7, waiting for transfers between devices, gather_ring(): cur_b = lax.ppermute(cur_b, 'seq', backward)  4.61 us
    concatenate x6, local copies, waits for them, and re-layouts, half(): stack = jnp.concatenate(got[first:last], axis=0)  4.18 us
  transfers between devices with their start and end apart: 31, of which 10 were waited for; matrix products, arithmetic and copies ran while one was open for 28% of the time, Pallas kernels for 0%

profile of v8, /device:TPU:0, one launch (start us, length us, event | category | flops | bytes accessed | tf_op | source)
XLA Modules:
  0.0 133.1 jit_solution(4337578178064495093)
XLA Ops:
  1.3 1.0 fusion.115
  2.5 1.0 fusion.116
  4.0 0.9 select_convert_fusion
  5.3 3.1 %collective-permute-start.1 = (bf16[128,1280]{0,1:T(8,128)(2,1)S(1)}, bf16[128,1280]{0,1:T(8,128)(2,1)S(1)}, u32[]{:S(2)}, u32[]{:S(2)}) collective-permute-start(bf16[128,1280]{0,1:T(8,128)(2,1)S(1)} %get-tuple-element.34), channel_id=1, source_target_pairs={{0,8},{2,10},{8,16},{10,18},{16,24},{18,26},{24,28},{26,30},{28,20... | collective-permute-start | bytes 983048 | tf_op jit(solution)/shard_map/ppermute | solution.py:36
  8.3 7.6 %collective-permute-done.1 = bf16[128,1280]{0,1:T(8,128)(2,1)S(1)} collective-permute-done((bf16[128,1280]{0,1:T(8,128)(2,1)S(1)}, bf16[128,1280]{0,1:T(8,128)(2,1)S(1)}, u32[]{:S(2)}, u32[]{:S(2)}) %collective-permute-start.1) | collective-permute-done | bytes 327712 | tf_op jit(solution)/shard_map/ppermute | solution.py:36
  16.0 1.8 %collective-permute-start.3 = (bf16[128,1280]{0,1:T(8,128)(2,1)S(1)}, bf16[128,1280]{0,1:T(8,128)(2,1)S(1)}, u32[]{:S(2)}, u32[]{:S(2)}) collective-permute-start(bf16[128,1280]{0,1:T(8,128)(2,1)S(1)} %collective-permute-done.1), channel_id=1, source_target_pairs={{0,8},{2,10},{8,16},{10,18},{16,24},{18,26},{24,28},{26,30},{28,20... | collective-permute-start | bytes 983048 | tf_op jit(solution)/shard_map/ppermute | solution.py:36
  18.5 6.4 %collective-permute-done.3 = bf16[128,1280]{0,1:T(8,128)(2,1)S(1)} collective-permute-done((bf16[128,1280]{0,1:T(8,128)(2,1)S(1)}, bf16[128,1280]{0,1:T(8,128)(2,1)S(1)}, u32[]{:S(2)}, u32[]{:S(2)}) %collective-permute-start.3) | collective-permute-done | bytes 327712 | tf_op jit(solution)/shard_map/ppermute | solution.py:36
  24.9 1.5 %collective-permute-start.5 = (bf16[128,1280]{0,1:T(8,128)(2,1)S(1)}, bf16[128,1280]{0,1:T(8,128)(2,1)}, u32[]{:S(2)}, u32[]{:S(2)}) collective-permute-start(bf16[128,1280]{0,1:T(8,128)(2,1)S(1)} %collective-permute-done.3), channel_id=1, source_target_pairs={{0,8},{2,10},{8,16},{10,18},{16,24},{18,26},{24,28},{26,30},{28,20... | collective-permute-start | bytes 983048 | tf_op jit(solution)/shard_map/ppermute | solution.py:36
  26.4 0.5 collective-permute-start.14
  27.5 5.5 %collective-permute-done.5 = bf16[128,1280]{0,1:T(8,128)(2,1)} collective-permute-done((bf16[128,1280]{0,1:T(8,128)(2,1)S(1)}, bf16[128,1280]{0,1:T(8,128)(2,1)}, u32[]{:S(2)}, u32[]{:S(2)}) %collective-permute-start.5) | collective-permute-done | bytes 327712 | tf_op jit(solution)/shard_map/ppermute | solution.py:36
  33.0 1.2 collective-permute-start.7
  34.1 0.9 collective-permute-start.16
  35.6 4.7 %collective-permute-done.7 = bf16[128,1280]{0,1:T(8,128)(2,1)} collective-permute-done((bf16[128,1280]{0,1:T(8,128)(2,1)}, bf16[128,1280]{0,1:T(8,128)(2,1)}, u32[]{:S(2)}, u32[]{:S(2)}) %collective-permute-start.7) | collective-permute-done | bytes 327712 | tf_op jit(solution)/shard_map/ppermute | solution.py:36
  40.4 1.0 collective-permute-done.16
  41.9 1.0 fusion.114
  43.7 0.8 slice.195
  44.7 0.8 slice.197
  45.5 0.8 slice.200
  46.3 0.8 slice.199
  47.1 0.8 slice.208
  47.8 1.6 %collective-permute-start.18 = (bf16[128,1280]{0,1:T(8,128)(2,1)}, bf16[128,1280]{0,1:T(8,128)(2,1)}, u32[]{:S(2)}, u32[]{:S(2)}) collective-permute-start(bf16[128,1280]{0,1:T(8,128)(2,1)} %collective-permute-done.7), channel_id=1, source_target_pairs={{0,8},{2,10},{8,16},{10,18},{16,24},{18,26},{24,28},{26,30},{28,20... | collective-permute-start | bytes 983048 | tf_op jit(solution)/shard_map/ppermute | solution.py:36
  49.4 0.8 slice.202
  50.2 0.7 slice.211
  51.4 0.7 slice.201
  52.1 0.8 slice.210
  52.9 0.7 slice.203
  53.6 0.7 slice.212
  55.2 2.6 %collective-permute-done.18 = bf16[128,1280]{0,1:T(8,128)(2,1)} collective-permute-done((bf16[128,1280]{0,1:T(8,128)(2,1)}, bf16[128,1280]{0,1:T(8,128)(2,1)}, u32[]{:S(2)}, u32[]{:S(2)}) %collective-permute-start.18) | collective-permute-done | bytes 327712 | tf_op jit(solution)/shard_map/ppermute | solution.py:36
  57.7 1.6 %collective-permute-start.20 = (bf16[128,1280]{0,1:T(8,128)(2,1)}, bf16[128,1280]{0,1:T(8,128)(2,1)S(1)}, u32[]{:S(2)}, u32[]{:S(2)}) collective-permute-start(bf16[128,1280]{0,1:T(8,128)(2,1)} %collective-permute-done.18), channel_id=1, source_target_pairs={{0,8},{2,10},{8,16},{10,18},{16,24},{18,26},{24,28},{26,30},{28,20... | collective-permute-start | bytes 983048 | tf_op jit(solution)/shard_map/ppermute | solution.py:36
  59.4 1.2 collective-permute-done.22
  61.7 5.0 %collective-permute-done.20 = bf16[128,1280]{0,1:T(8,128)(2,1)S(1)} collective-permute-done((bf16[128,1280]{0,1:T(8,128)(2,1)}, bf16[128,1280]{0,1:T(8,128)(2,1)S(1)}, u32[]{:S(2)}, u32[]{:S(2)}) %collective-permute-start.20) | collective-permute-done | bytes 327712 | tf_op jit(solution)/shard_map/ppermute | solution.py:36
  66.7 2.5 %collective-permute-done.24 = bf16[128,1280]{0,1:T(8,128)(2,1)S(1)} collective-permute-done((bf16[128,1280]{0,1:T(8,128)(2,1)}, bf16[128,1280]{0,1:T(8,128)(2,1)S(1)}, u32[]{:S(2)}, u32[]{:S(2)}) %collective-permute-start.24) | collective-permute-done | bytes 327712 | tf_op jit(solution)/shard_map/ppermute | solution.py:37
  69.3 1.6 %collective-permute-start.26 = (bf16[128,1280]{0,1:T(8,128)(2,1)S(1)}, bf16[128,1280]{0,1:T(8,128)(2,1)S(1)}, u32[]{:S(2)}, u32[]{:S(2)}) collective-permute-start(bf16[128,1280]{0,1:T(8,128)(2,1)S(1)} %collective-permute-done.20), channel_id=1, source_target_pairs={{0,8},{2,10},{8,16},{10,18},{16,24},{18,26},{24,28},{26,30},{28,20... | collective-permute-start | bytes 983048 | tf_op jit(solution)/shard_map/ppermute | solution.py:36
  71.4 1.1 constant_dynamic-update-slice_fusion.8
  72.6 1.1 constant_dynamic-update-slice_fusion.6
  73.8 1.1 constant_dynamic-update-slice_fusion.3
  74.9 1.1 constant_dynamic-update-slice_fusion.2
  75.9 1.1 constant_dynamic-update-slice_fusion.1
  77.0 1.1 constant_dynamic-update-slice_fusion
  78.3 1.0 constant_dynamic-update-slice_fusion.13
  80.1 1.1 constant_dynamic-update-slice_fusion.20
  81.2 1.1 constant_dynamic-update-slice_fusion.18
  82.3 1.1 constant_dynamic-update-slice_fusion.17
  83.3 1.1 constant_dynamic-update-slice_fusion.16
  84.4 1.4 %fusion.109 = (bf16[1280,640]{0,1:T(8,128)(2,1)S(1)}, bf16[1280,640]{0,1:T(8,128)(2,1)}) fusion(bf16[1280,1280]{0,1:T(8,128)(2,1)S(1)} %constant_dynamic-update-slice_fusion.16), kind=kLoop, calls=%fused_computation.174 | loop fusion | bytes 6553600 | tf_op jit(solution)/shard_map/slice | solution.py:140
  85.8 1.0 constant_dynamic-update-slice_fusion.29
  87.1 0.9 fusion.111
  88.0 0.8 fusion.120
  90.1 0.6 fusion.4
  90.9 0.8 fusion.117
  91.7 1.7 %constant_dynamic-update-slice_fusion.31 = bf16[256,1280]{0,1:T(8,128)(2,1)} fusion(bf16[128,1280]{0,1:T(8,128)(2,1)} %collective-permute-done.28), kind=kLoop, calls=%fused_computation.119 | loop fusion | bytes 655360
  93.8 0.6 collective-permute-start.29
  94.3 0.6 fusion.6
  95.8 0.8 fusion.42
  97.5 0.8 copy.49
  98.3 1.8 %constant_dynamic-update-slice_fusion.30 = bf16[256,1280]{0,1:T(8,128)(2,1)} fusion(bf16[256,1280]{0,1:T(8,128)(2,1)} %constant_dynamic-update-slice_fusion.31, bf16[128,1280]{0,1:T(8,128)(2,1)} %collective-permute-done.29), kind=kLoop, calls=%fused_computation.118 | loop fusion | bytes 655360 | tf_op jit(solution)/shard_map/concatenate | solution.py:139
  100.2 1.1 fusion.113
  102.0 0.9 fusion.48
  104.1 6.6 %fusion.69 = f32[120,5120]{1,0:T(8,128)S(1)} fusion(bf16[1280,5120]{1,0:T(8,128)(2,1)} %param.15, bf16[120,640]{0,1:T(8,128)(2,1)S(1)} %bitcast.282, bf16[120,640]{0,1:T(8,128)(2,1)S(1)} %bitcast.281), kind=kOutput, calls=%fused_computation.78 | convolution fusion | flops 1573478400 | bytes 15872000 | tf_op jit(solution)/shard_map/dot_general | solution.py:149
  110.8 1.7 %reshape.284 = f32[2,60,5120]{2,1,0:T(8,128)} reshape(f32[120,5120]{1,0:T(8,128)S(1)} %fusion.69) | data formatting | bytes 4915200 | tf_op jit(solution)/shard_map/reshape | solution.py:153
  112.5 1.4 %bitcast_convert_fusion = bf16[60,5120]{1,0:T(8,128)(2,1)S(1)} fusion(f32[2,60,5120]{2,1,0:T(8,128)} %reshape.284, s32[]{:T(128)S(6)} %select_n.279, pred[]{:T(512)S(6)} %and.116), kind=kLoop, calls=%fused_computation.26 | loop fusion | flops 307200 | bytes 1228805 | tf_op jit(solution)/shard_map/convert_element_type | solution.py:155
  113.9 1.6 %collective-permute-start.30 = (bf16[60,5120]{1,0:T(8,128)(2,1)S(1)}, bf16[60,5120]{1,0:T(8,128)(2,1)S(1)}, u32[]{:S(2)}, u32[]{:S(2)}) collective-permute-start(bf16[60,5120]{1,0:T(8,128)(2,1)S(1)} %bitcast_convert_fusion), channel_id=1, source_target_pairs={{0,1},{1,0},{2,3},{3,2},{4,5},{5,4},{6,7},{7,6},{8,9},{9,8},{10,11... | collective-permute-start | bytes 1843208 | tf_op jit(solution)/shard_map/ppermute | solution.py:156
  115.5 15.2 %collective-permute-done.30 = bf16[60,5120]{1,0:T(8,128)(2,1)S(1)} collective-permute-done((bf16[60,5120]{1,0:T(8,128)(2,1)S(1)}, bf16[60,5120]{1,0:T(8,128)(2,1)S(1)}, u32[]{:S(2)}, u32[]{:S(2)}) %collective-permute-start.30) | collective-permute-done | bytes 614432 | tf_op jit(solution)/shard_map/ppermute | solution.py:156
  130.6 2.4 %fusion.24 = bf16[60,5120]{1,0:T(8,128)(2,1)} fusion(f32[2,60,5120]{2,1,0:T(8,128)} %reshape.284, s32[]{:T(128)S(6)} %select_n.277, bf16[60,5120]{1,0:T(8,128)(2,1)S(1)} %collective-permute-done.30, bf16[60,5120]{1,0:T(8,128)(2,1)S(1)} %copy-done.5, f32[5120]{0:T(1024)S(1)} %copy-done.9, pred[]{:T(512)S(6)} %and.115), kind=kLoop, calls=%fused_computation.30 | loop fusion | flops 2150400 | bytes 3092485 | tf_op jit(solution)/shard_map/convert_element_type | solution.py:158
  (132 shorter events, 14.1 us)
Async XLA Ops:
  5.3 10.7 %collective-permute-start.1 = (bf16[128,1280]{0,1:T(8,128)(2,1)S(1)}, bf16[128,1280]{0,1:T(8,128)(2,1)S(1)}, u32[]{:S(2)}, u32[]{:S(2)}) collective-permute-start(bf16[128,1280]{0,1:T(8,128)(2,1)S(1)} %get-tuple-element.34), channel_id=1, source_target_pairs={{0,8},{2,10},{8,16},{10,18},{16,24},{18,26},{24,28},{26,30},{28,20... | collective-permute-start | bytes 983048 | tf_op jit(solution)/shard_map/ppermute | solution.py:36
  8.3 9.5 %collective-permute-start.10 = (bf16[128,1280]{0,1:T(8,128)(2,1)S(1)}, bf16[128,1280]{0,1:T(8,128)(2,1)S(1)}, u32[]{:S(2)}, u32[]{:S(2)}) collective-permute-start(bf16[128,1280]{0,1:T(8,128)(2,1)S(1)} %get-tuple-element.48), channel_id=1, source_target_pairs={{8,0},{10,2},{16,8},{18,10},{24,16},{26,18},{28,24},{30,26},{20,28... | collective-permute-start | bytes 983048 | tf_op jit(solution)/shard_map/ppermute | solution.py:37
  16.0 8.9 %collective-permute-start.3 = (bf16[128,1280]{0,1:T(8,128)(2,1)S(1)}, bf16[128,1280]{0,1:T(8,128)(2,1)S(1)}, u32[]{:S(2)}, u32[]{:S(2)}) collective-permute-start(bf16[128,1280]{0,1:T(8,128)(2,1)S(1)} %collective-permute-done.1), channel_id=1, source_target_pairs={{0,8},{2,10},{8,16},{10,18},{16,24},{18,26},{24,28},{26,30},{28,20... | collective-permute-start | bytes 983048 | tf_op jit(solution)/shard_map/ppermute | solution.py:36
  17.8 8.6 %collective-permute-start.12 = (bf16[128,1280]{0,1:T(8,128)(2,1)S(1)}, bf16[128,1280]{0,1:T(8,128)(2,1)S(1)}, u32[]{:S(2)}, u32[]{:S(2)}) collective-permute-start(bf16[128,1280]{0,1:T(8,128)(2,1)S(1)} %collective-permute-done.10), channel_id=1, source_target_pairs={{8,0},{10,2},{16,8},{18,10},{24,16},{26,18},{28,24},{30,26},{20,28... | collective-permute-start | bytes 983048 | tf_op jit(solution)/shard_map/ppermute | solution.py:37
  18.0 8.9 %collective-permute-start = (bf16[128,1280]{0,1:T(8,128)(2,1)S(1)}, bf16[128,1280]{0,1:T(8,128)(2,1)}, u32[]{:S(2)}, u32[]{:S(2)}) collective-permute-start(bf16[128,1280]{0,1:T(8,128)(2,1)S(1)} %get-tuple-element.34), channel_id=1, source_target_pairs={{0,2},{2,0},{4,6},{6,4},{8,10},{10,8},{12,14},{14,12},{16,18},{18,... | collective-permute-start | bytes 983048 | tf_op jit(solution)/shard_map/ppermute | solution.py:40
  18.0 9.4 %collective-permute-start.9 = (bf16[128,1280]{0,1:T(8,128)(2,1)S(1)}, bf16[128,1280]{0,1:T(8,128)(2,1)S(1)}, u32[]{:S(2)}, u32[]{:S(2)}) collective-permute-start(bf16[128,1280]{0,1:T(8,128)(2,1)S(1)} %get-tuple-element.48), channel_id=1, source_target_pairs={{0,2},{2,0},{4,6},{6,4},{8,10},{10,8},{12,14},{14,12},{16,18},{18,... | collective-permute-start | bytes 983048 | tf_op jit(solution)/shard_map/ppermute | solution.py:41
  24.9 8.1 %collective-permute-start.5 = (bf16[128,1280]{0,1:T(8,128)(2,1)S(1)}, bf16[128,1280]{0,1:T(8,128)(2,1)}, u32[]{:S(2)}, u32[]{:S(2)}) collective-permute-start(bf16[128,1280]{0,1:T(8,128)(2,1)S(1)} %collective-permute-done.3), channel_id=1, source_target_pairs={{0,8},{2,10},{8,16},{10,18},{16,24},{18,26},{24,28},{26,30},{28,20... | collective-permute-start | bytes 983048 | tf_op jit(solution)/shard_map/ppermute | solution.py:36
  26.4 7.8 %collective-permute-start.14 = (bf16[128,1280]{0,1:T(8,128)(2,1)S(1)}, bf16[128,1280]{0,1:T(8,128)(2,1)S(1)}, u32[]{:S(2)}, u32[]{:S(2)}) collective-permute-start(bf16[128,1280]{0,1:T(8,128)(2,1)S(1)} %collective-permute-done.12), channel_id=1, source_target_pairs={{8,0},{10,2},{16,8},{18,10},{24,16},{26,18},{28,24},{30,26},{20,28... | collective-permute-start | bytes 983048 | tf_op jit(solution)/shard_map/ppermute | solution.py:37
  26.9 8.1 %collective-permute-start.11 = (bf16[128,1280]{0,1:T(8,128)(2,1)S(1)}, bf16[128,1280]{0,1:T(8,128)(2,1)S(1)}, u32[]{:S(2)}, u32[]{:S(2)}) collective-permute-start(bf16[128,1280]{0,1:T(8,128)(2,1)S(1)} %collective-permute-done.10), channel_id=1, source_target_pairs={{0,2},{2,0},{4,6},{6,4},{8,10},{10,8},{12,14},{14,12},{16,18},{18,... | collective-permute-start | bytes 983048 | tf_op jit(solution)/shard_map/ppermute | solution.py:41
  26.9 8.1 %collective-permute-start.2 = (bf16[128,1280]{0,1:T(8,128)(2,1)S(1)}, bf16[128,1280]{0,1:T(8,128)(2,1)S(1)}, u32[]{:S(2)}, u32[]{:S(2)}) collective-permute-start(bf16[128,1280]{0,1:T(8,128)(2,1)S(1)} %collective-permute-done.1), channel_id=1, source_target_pairs={{0,2},{2,0},{4,6},{6,4},{8,10},{10,8},{12,14},{14,12},{16,18},{18,... | collective-permute-start | bytes 983048 | tf_op jit(solution)/shard_map/ppermute | solution.py:40
  27.4 8.1 %collective-permute-start.4 = (bf16[128,1280]{0,1:T(8,128)(2,1)S(1)}, bf16[128,1280]{0,1:T(8,128)(2,1)S(1)}, u32[]{:S(2)}, u32[]{:S(2)}) collective-permute-start(bf16[128,1280]{0,1:T(8,128)(2,1)S(1)} %collective-permute-done.3), channel_id=1, source_target_pairs={{0,2},{2,0},{4,6},{6,4},{8,10},{10,8},{12,14},{14,12},{16,18},{18,... | collective-permute-start | bytes 983048 | tf_op jit(solution)/shard_map/ppermute | solution.py:40
  33.0 7.4 %collective-permute-start.7 = (bf16[128,1280]{0,1:T(8,128)(2,1)}, bf16[128,1280]{0,1:T(8,128)(2,1)}, u32[]{:S(2)}, u32[]{:S(2)}) collective-permute-start(bf16[128,1280]{0,1:T(8,128)(2,1)} %collective-permute-done.5), channel_id=1, source_target_pairs={{0,8},{2,10},{8,16},{10,18},{16,24},{18,26},{24,28},{26,30},{28,20... | collective-permute-start | bytes 983048 | tf_op jit(solution)/shard_map/ppermute | solution.py:36
  34.1 7.2 %collective-permute-start.16 = (bf16[128,1280]{0,1:T(8,128)(2,1)S(1)}, bf16[128,1280]{0,1:T(8,128)(2,1)}, u32[]{:S(2)}, u32[]{:S(2)}) collective-permute-start(bf16[128,1280]{0,1:T(8,128)(2,1)S(1)} %collective-permute-done.14), channel_id=1, source_target_pairs={{8,0},{10,2},{16,8},{18,10},{24,16},{26,18},{28,24},{30,26},{20,28... | collective-permute-start | bytes 983048 | tf_op jit(solution)/shard_map/ppermute | solution.py:37
  35.0 12.1 %collective-permute-start.13 = (bf16[128,1280]{0,1:T(8,128)(2,1)S(1)}, bf16[128,1280]{0,1:T(8,128)(2,1)}, u32[]{:S(2)}, u32[]{:S(2)}) collective-permute-start(bf16[128,1280]{0,1:T(8,128)(2,1)S(1)} %collective-permute-done.12), channel_id=1, source_target_pairs={{0,2},{2,0},{4,6},{6,4},{8,10},{10,8},{12,14},{14,12},{16,18},{18,... | collective-permute-start | bytes 983048 | tf_op jit(solution)/shard_map/ppermute | solution.py:41
  35.0 6.3 %copy-start.6 = (bf16[128,1280]{0,1:T(8,128)(2,1)}, bf16[128,1280]{0,1:T(8,128)(2,1)S(1)}, u32[]{:S(2)}) copy-start(bf16[128,1280]{0,1:T(8,128)(2,1)S(1)} %collective-permute-done.2) | copy-start | bytes 983044
  35.0 15.9 %collective-permute-start.6 = (bf16[128,1280]{0,1:T(8,128)(2,1)}, bf16[128,1280]{0,1:T(8,128)(2,1)}, u32[]{:S(2)}, u32[]{:S(2)}) collective-permute-start(bf16[128,1280]{0,1:T(8,128)(2,1)} %collective-permute-done.5), channel_id=1, source_target_pairs={{0,2},{2,0},{4,6},{6,4},{8,10},{10,8},{12,14},{14,12},{16,18},{18,... | collective-permute-start | bytes 983048 | tf_op jit(solution)/shard_map/ppermute | solution.py:40
  35.5 5.8 %copy-start.7 = (bf16[128,1280]{0,1:T(8,128)(2,1)}, bf16[128,1280]{0,1:T(8,128)(2,1)S(1)}, u32[]{:S(2)}) copy-start(bf16[128,1280]{0,1:T(8,128)(2,1)S(1)} %collective-permute-done.4) | copy-start | bytes 983044
  35.5 16.6 %collective-permute-start.15 = (bf16[128,1280]{0,1:T(8,128)(2,1)S(1)}, bf16[128,1280]{0,1:T(8,128)(2,1)}, u32[]{:S(2)}, u32[]{:S(2)}) collective-permute-start(bf16[128,1280]{0,1:T(8,128)(2,1)S(1)} %collective-permute-done.14), channel_id=1, source_target_pairs={{0,2},{2,0},{4,6},{6,4},{8,10},{10,8},{12,14},{14,12},{16,18},{18,... | collective-permute-start | bytes 983048 | tf_op jit(solution)/shard_map/ppermute | solution.py:41
  40.4 12.5 %collective-permute-start.8 = (bf16[128,1280]{0,1:T(8,128)(2,1)}, bf16[128,1280]{0,1:T(8,128)(2,1)}, u32[]{:S(2)}, u32[]{:S(2)}) collective-permute-start(bf16[128,1280]{0,1:T(8,128)(2,1)} %collective-permute-done.7), channel_id=1, source_target_pairs={{0,2},{2,0},{4,6},{6,4},{8,10},{10,8},{12,14},{14,12},{16,18},{18,... | collective-permute-start | bytes 983048 | tf_op jit(solution)/shard_map/ppermute | solution.py:40
  41.3 12.3 %collective-permute-start.17 = (bf16[128,1280]{0,1:T(8,128)(2,1)}, bf16[128,1280]{0,1:T(8,128)(2,1)}, u32[]{:S(2)}, u32[]{:S(2)}) collective-permute-start(bf16[128,1280]{0,1:T(8,128)(2,1)} %collective-permute-done.16), channel_id=1, source_target_pairs={{0,2},{2,0},{4,6},{6,4},{8,10},{10,8},{12,14},{14,12},{16,18},{18,... | collective-permute-start | bytes 983048 | tf_op jit(solution)/shard_map/ppermute | solution.py:41
  47.8 9.9 %collective-permute-start.18 = (bf16[128,1280]{0,1:T(8,128)(2,1)}, bf16[128,1280]{0,1:T(8,128)(2,1)}, u32[]{:S(2)}, u32[]{:S(2)}) collective-permute-start(bf16[128,1280]{0,1:T(8,128)(2,1)} %collective-permute-done.7), channel_id=1, source_target_pairs={{0,8},{2,10},{8,16},{10,18},{16,24},{18,26},{24,28},{26,30},{28,20... | collective-permute-start | bytes 983048 | tf_op jit(solution)/shard_map/ppermute | solution.py:36
  50.9 9.6 %collective-permute-start.22 = (bf16[128,1280]{0,1:T(8,128)(2,1)}, bf16[128,1280]{0,1:T(8,128)(2,1)}, u32[]{:S(2)}, u32[]{:S(2)}) collective-permute-start(bf16[128,1280]{0,1:T(8,128)(2,1)} %collective-permute-done.16), channel_id=1, source_target_pairs={{8,0},{10,2},{16,8},{18,10},{24,16},{26,18},{28,24},{30,26},{20,28... | collective-permute-start | bytes 983048 | tf_op jit(solution)/shard_map/ppermute | solution.py:37
  54.5 19.2 %copy-start.8 = (bf16[128,1280]{0,1:T(8,128)(2,1)S(1)}, bf16[128,1280]{0,1:T(8,128)(2,1)}, u32[]{:S(2)}) copy-start(bf16[128,1280]{0,1:T(8,128)(2,1)} %copy-done.7) | copy-start | bytes 983044
  57.7 8.9 %collective-permute-start.20 = (bf16[128,1280]{0,1:T(8,128)(2,1)}, bf16[128,1280]{0,1:T(8,128)(2,1)S(1)}, u32[]{:S(2)}, u32[]{:S(2)}) collective-permute-start(bf16[128,1280]{0,1:T(8,128)(2,1)} %collective-permute-done.18), channel_id=1, source_target_pairs={{0,8},{2,10},{8,16},{10,18},{16,24},{18,26},{24,28},{26,30},{28,20... | collective-permute-start | bytes 983048 | tf_op jit(solution)/shard_map/ppermute | solution.py:36
  60.5 8.6 %collective-permute-start.24 = (bf16[128,1280]{0,1:T(8,128)(2,1)}, bf16[128,1280]{0,1:T(8,128)(2,1)S(1)}, u32[]{:S(2)}, u32[]{:S(2)}) collective-permute-start(bf16[128,1280]{0,1:T(8,128)(2,1)} %collective-permute-done.22), channel_id=1, source_target_pairs={{8,0},{10,2},{16,8},{18,10},{24,16},{26,18},{28,24},{30,26},{20,28... | collective-permute-start | bytes 983048 | tf_op jit(solution)/shard_map/ppermute | solution.py:37
  61.1 9.8 %collective-permute-start.19 = (bf16[128,1280]{0,1:T(8,128)(2,1)}, bf16[128,1280]{0,1:T(8,128)(2,1)S(1)}, u32[]{:S(2)}, u32[]{:S(2)}) collective-permute-start(bf16[128,1280]{0,1:T(8,128)(2,1)} %collective-permute-done.18), channel_id=1, source_target_pairs={{0,2},{2,0},{4,6},{6,4},{8,10},{10,8},{12,14},{14,12},{16,18},{18,... | collective-permute-start | bytes 983048 | tf_op jit(solution)/shard_map/ppermute | solution.py:40
  61.1 10.2 %collective-permute-start.23 = (bf16[128,1280]{0,1:T(8,128)(2,1)}, bf16[128,1280]{0,1:T(8,128)(2,1)S(1)}, u32[]{:S(2)}, u32[]{:S(2)}) collective-permute-start(bf16[128,1280]{0,1:T(8,128)(2,1)} %collective-permute-done.22), channel_id=1, source_target_pairs={{0,2},{2,0},{4,6},{6,4},{8,10},{10,8},{12,14},{14,12},{16,18},{18,... | collective-permute-start | bytes 983048 | tf_op jit(solution)/shard_map/ppermute | solution.py:41
  66.7 4.7 %collective-permute-start.21 = (bf16[128,1280]{0,1:T(8,128)(2,1)S(1)}, bf16[128,1280]{0,1:T(8,128)(2,1)S(1)}, u32[]{:S(2)}, u32[]{:S(2)}) collective-permute-start(bf16[128,1280]{0,1:T(8,128)(2,1)S(1)} %collective-permute-done.20), channel_id=1, source_target_pairs={{0,2},{2,0},{4,6},{6,4},{8,10},{10,8},{12,14},{14,12},{16,18},{18,... | collective-permute-start | bytes 983048 | tf_op jit(solution)/shard_map/ppermute | solution.py:40
  69.2 2.2 %collective-permute-start.25 = (bf16[128,1280]{0,1:T(8,128)(2,1)S(1)}, bf16[128,1280]{0,1:T(8,128)(2,1)S(1)}, u32[]{:S(2)}, u32[]{:S(2)}) collective-permute-start(bf16[128,1280]{0,1:T(8,128)(2,1)S(1)} %collective-permute-done.24), channel_id=1, source_target_pairs={{0,2},{2,0},{4,6},{6,4},{8,10},{10,8},{12,14},{14,12},{16,18},{18,... | collective-permute-start | bytes 983048 | tf_op jit(solution)/shard_map/ppermute | solution.py:41
  69.3 21.4 %collective-permute-start.26 = (bf16[128,1280]{0,1:T(8,128)(2,1)S(1)}, bf16[128,1280]{0,1:T(8,128)(2,1)S(1)}, u32[]{:S(2)}, u32[]{:S(2)}) collective-permute-start(bf16[128,1280]{0,1:T(8,128)(2,1)S(1)} %collective-permute-done.20), channel_id=1, source_target_pairs={{0,8},{2,10},{8,16},{10,18},{16,24},{18,26},{24,28},{26,30},{28,20... | collective-permute-start | bytes 983048 | tf_op jit(solution)/shard_map/ppermute | solution.py:36
  70.9 20.8 %collective-permute-start.28 = (bf16[128,1280]{0,1:T(8,128)(2,1)S(1)}, bf16[128,1280]{0,1:T(8,128)(2,1)}, u32[]{:S(2)}, u32[]{:S(2)}) collective-permute-start(bf16[128,1280]{0,1:T(8,128)(2,1)S(1)} %collective-permute-done.24), channel_id=1, source_target_pairs={{8,0},{10,2},{16,8},{18,10},{24,16},{26,18},{28,24},{30,26},{20,28... | collective-permute-start | bytes 983048 | tf_op jit(solution)/shard_map/ppermute | solution.py:37
  89.7 3.7 %copy-start = (f32[5,120,512]{2,1,0:T(8,128)}, f32[5,120,512]{2,1,0:T(8,128)S(1)}, u32[]{:S(2)}) copy-start(f32[5,120,512]{2,1,0:T(8,128)S(1)} %get-tuple-element.112) | copy-start | bytes 3686404
  90.8 4.2 %collective-permute-start.27 = (bf16[128,1280]{0,1:T(8,128)(2,1)S(1)}, bf16[128,1280]{0,1:T(8,128)(2,1)S(1)}, u32[]{:S(2)}, u32[]{:S(2)}) collective-permute-start(bf16[128,1280]{0,1:T(8,128)(2,1)S(1)} %collective-permute-done.26), channel_id=1, source_target_pairs={{0,2},{2,0},{4,6},{6,4},{8,10},{10,8},{12,14},{14,12},{16,18},{18,... | collective-permute-start | bytes 983048 | tf_op jit(solution)/shard_map/ppermute | solution.py:40
  93.8 4.5 %collective-permute-start.29 = (bf16[128,1280]{0,1:T(8,128)(2,1)}, bf16[128,1280]{0,1:T(8,128)(2,1)}, u32[]{:S(2)}, u32[]{:S(2)}) collective-permute-start(bf16[128,1280]{0,1:T(8,128)(2,1)} %collective-permute-done.28), channel_id=1, source_target_pairs={{0,2},{2,0},{4,6},{6,4},{8,10},{10,8},{12,14},{14,12},{16,18},{18,... | collective-permute-start | bytes 983048 | tf_op jit(solution)/shard_map/ppermute | solution.py:41
  98.3 3.7 %copy-start.3 = (bf16[1280,640]{0,1:T(8,128)(2,1)S(1)}, bf16[1280,640]{0,1:T(8,128)(2,1)}, u32[]{:S(2)}) copy-start(bf16[1280,640]{0,1:T(8,128)(2,1)} %get-tuple-element.88) | copy-start | bytes 4915204
  101.6 1.3 copy-start.1
  101.7 1.5 %copy-start.2 = (bf16[512,640]{0,1:T(8,128)(2,1)S(1)}, bf16[512,640]{0,1:T(8,128)(2,1)}, u32[]{:S(2)}) copy-start(bf16[512,640]{0,1:T(8,128)(2,1)} %get-tuple-element.91) | copy-start | bytes 1966084
  102.9 1.2 copy-start.4
  110.7 19.9 %copy-start.5 = (bf16[60,5120]{1,0:T(8,128)(2,1)S(1)}, bf16[60,5120]{1,0:T(8,128)(2,1)}, u32[]{:S(2)}) copy-start(bf16[60,5120]{1,0:T(8,128)(2,1)} %param.10) | copy-start | bytes 1843204
  110.8 19.9 %copy-start.9 = (f32[5120]{0:T(1024)S(1)}, f32[5120]{0:T(1024)}, u32[]{:S(2)}) copy-start(f32[5120]{0:T(1024)} %param.14) | copy-start | bytes 61444
  113.9 16.7 %collective-permute-start.30 = (bf16[60,5120]{1,0:T(8,128)(2,1)S(1)}, bf16[60,5120]{1,0:T(8,128)(2,1)S(1)}, u32[]{:S(2)}, u32[]{:S(2)}) collective-permute-start(bf16[60,5120]{1,0:T(8,128)(2,1)S(1)} %bitcast_convert_fusion), channel_id=1, source_target_pairs={{0,1},{1,0},{2,3},{3,2},{4,5},{5,4},{6,7},{7,6},{8,9},{9,8},{10,11... | collective-permute-start | bytes 1843208 | tf_op jit(solution)/shard_map/ppermute | solution.py:156

commit v9 on v8

--- a/solution.py
+++ b/solution.py
@@ -50,7 +50,7 @@
 
 def attend_part(queries_3d, keys, values, keeping, scale_factor):
     scores = (
-        jnp.einsum("qhd,khd->hqk", queries_3d, keys, preferred_element_type=jnp.float32)
+        jnp.einsum("hqd,hkd->hqk", queries_3d, keys, preferred_element_type=jnp.float32)
         * scale_factor
     )
     masked = jnp.where(keeping[None, None, :], scores, neg_large)
@@ -58,7 +58,7 @@
     weights = jnp.where(keeping[None, None, :], jnp.exp(masked - peak), 0.0)
     totals = jnp.sum(weights, axis=2, keepdims=True)
     summed = jnp.einsum(
-        "hqk,khd->hqd", weights.astype(jnp.bfloat16), values, preferred_element_type=jnp.float32
+        "hqk,hkd->hqd", weights.astype(jnp.bfloat16), values, preferred_element_type=jnp.float32
     )
     return peak, totals, summed
 
@@ -91,26 +91,29 @@
         scale_factor = 1.0 / math.sqrt(HEAD)
         me = lax.axis_index("seq")
         rows_pad = (rows_dev + 1 + 7) // 8 * 8
-        row_id = lax.broadcasted_iota(jnp.int32, (rows_pad - rows_dev, 2 * cut), 0)
-        col_id = lax.broadcasted_iota(jnp.int32, (rows_pad - rows_dev, 2 * cut), 1)
+        row_id = lax.broadcasted_iota(jnp.int32, (rows_pad - rows_dev, HEAD), 0)
+        col_id = lax.broadcasted_iota(jnp.int32, (rows_pad - rows_dev, HEAD), 1)
         info = jnp.where(
             (row_id == 0) & (col_id == 0),
             valid_count[0],
             jnp.where((row_id == 0) & (col_id == 1), assignment[0], 0),
         ).astype(jnp.bfloat16)
-        packet_a = jnp.concatenate(
-            [jnp.concatenate([key_rows[:, :cut], value_rows[:, :cut]], axis=1), info], axis=0
-        )
-        packet_b = jnp.concatenate(
-            [jnp.concatenate([key_rows[:, cut:], value_rows[:, cut:]], axis=1), info], axis=0
-        )
+
+        def head_major(lo, hi):
+            both = jnp.concatenate([key_rows[:, lo * HEAD : hi * HEAD], value_rows[:, lo * HEAD : hi * HEAD]], axis=1)
+            both = both.reshape(rows_dev, 2 * (hi - lo), HEAD).transpose(1, 0, 2)
+            pad = jnp.broadcast_to(info[None], (2 * (hi - lo),) + info.shape)
+            return jnp.concatenate([both, pad], axis=1)
+
+        packet_a = head_major(0, heads_a)
+        packet_b = head_major(heads_a, heads_here)
         got_a, got_b, ids_a, ids_b = gather_ring(packet_a, packet_b, me)
         chips = n_seq // 2
         known = chips // 2
         seen = 2 * (known + 1)
         heard = got_a[:seen] + got_b[:seen]
         heard_ids = jnp.concatenate([ids_a[:seen], ids_b[:seen]])
-        extra = jnp.stack([g[rows_dev, :2] for g in heard]).astype(jnp.float32).astype(jnp.int32)
+        extra = jnp.stack([g[0, rows_dev, :2] for g in heard]).astype(jnp.float32).astype(jnp.int32)
         counts_of, blocks_of = extra[:, 0], extra[:, 1]
 
         def limits_for(ids):
@@ -132,13 +135,12 @@
         got_b = list(held_b) + got_b[early:]
 
         def half(got, limits, lo, hi):
-            width = (hi - lo) * HEAD
-            q3 = queries[:, lo * HEAD : hi * HEAD].reshape(rows_dev, hi - lo, HEAD)
+            q3 = queries[:, lo * HEAD : hi * HEAD].reshape(rows_dev, hi - lo, HEAD).transpose(1, 0, 2)
             parts = []
             for first, last in phases:
-                stack = jnp.concatenate(got[first:last], axis=0)
-                keys = stack[:, :width].reshape(-1, hi - lo, HEAD)
-                values = stack[:, width:].reshape(-1, hi - lo, HEAD)
+                stack = jnp.concatenate(got[first:last], axis=1)
+                keys = stack[: hi - lo]
+                values = stack[hi - lo :]
                 keeping = (within[None, :] < limits[first:last, None]).reshape(-1)
                 parts.append(attend_part(q3, keys, values, keeping, scale_factor))
             return combine(parts, rows_dev)

time: 134 us -> 130 us (0.970)
  local copies, waits for them, and re-layouts: 37.9 us -> 33.8 us
  matrix products: 13.1 us -> 16.7 us
  waiting for transfers between devices: 51.5 us -> 49.6 us
    slice x30 -> x6, local copies, waits for them, and re-layouts: 16 us -> 2.45 us  [the longest x1 1.06 us: head_major(): key_rows[:, lo * HEAD:hi * HEAD]]
    another operation x1 -> x37, local copies, waits for them, and re-layouts: 0.11 us -> 5.36 us  [on_device(): jnp.stack([g[0, rows_dev, :2] for g in heard]).astype(jnp.float32)]
    ppermute x7, waiting for transfers between devices: 31.7 us -> 26.6 us  [gather_ring(): cur_a = lax.ppermute(cur_a, 'seq', forward)]
    dot_general x12, matrix products: 6.51 us -> 10.1 us  [the longest x6 6.14 us: attend_part(): jnp.einsum('hqk,hkd->hqd', weights.astype(jnp.bfloat16), values, preferre...]
    ppermute x7, waiting for transfers between devices: 4.61 us -> 7.52 us  [gather_ring(): cur_b = lax.ppermute(cur_b, 'seq', backward)]
    unnamed x50 -> x98, local copies, waits for them, and re-layouts: 14.3 us -> 15.9 us
    reshape x0 -> x4, local copies, waits for them, and re-layouts: none -> 1.43 us  [the longest x2 0.99 us: half(): queries[:, lo * HEAD:hi * HEAD].reshape(rows_dev, hi - lo, HEAD)]
    concatenate x6 -> x8, local copies, waits for them, and re-layouts: 4.18 us -> 4.37 us  [the longest x6 3.93 us: half(): stack = jnp.concatenate(got[first:last], axis=1)]
  transfers between devices with their start and end apart: 31 -> 31, of which waited for: 10 -> 12; matrix products, arithmetic and copies ran while one was open for 28% -> 23% of each run, Pallas kernels for 0% -> 0%
where the time goes in v9:
time: 130 us
  waiting for transfers between devices  49.6 us (38%)
  local copies, waits for them, and re-layouts  33.8 us (26%)
  starting transfers between devices  19.3 us (15%)
  matrix products  16.7 us (13%)
  other arithmetic  7.63 us (6%)
  between operations  2.64 us (2%)
    ppermute x7, waiting for transfers between devices, gather_ring(): cur_a = lax.ppermute(cur_a, 'seq', forward)  26.6 us
    unnamed x98, local copies, waits for them, and re-layouts  15.9 us
    ppermute x1, waiting for transfers between devices, on_device(): came = lax.ppermute(other, 'tp', [(0, 1), (1, 0)])  15.4 us
    ppermute x7, starting transfers between devices, gather_ring(): cur_a = lax.ppermute(cur_a, 'seq', forward)  12.3 us
    ppermute x7, waiting for transfers between devices, gather_ring(): cur_b = lax.ppermute(cur_b, 'seq', backward)  7.52 us
    dot_general x1, matrix products, on_device(): partial = jnp.dot(attention, out_weight, preferred_element_type=jnp.float32)  6.64 us
    dot_general x6, matrix products, attend_part(): jnp.einsum('hqk,hkd->hqd', weights.astype(jnp.bfloat16), values, preferre...  6.14 us
    another operation x37, local copies, waits for them, and re-layouts, on_device(): jnp.stack([g[0, rows_dev, :2] for g in heard]).astype(jnp.float32)  5.36 us
  transfers between devices with their start and end apart: 31, of which 12 were waited for; matrix products, arithmetic and copies ran while one was open for 23% of the time, Pallas kernels for 0%

profile of v9, /device:TPU:0, one launch (start us, length us, event | category | flops | bytes accessed | tf_op | source)
XLA Modules:
  0.0 129.6 jit_solution(8081636067394753499)
XLA Ops:
  0.0 1.1 fusion.129
  1.1 1.0 fusion.130
  4.7 3.1 %collective-permute-start.1 = (bf16[10,128,128]{2,1,0:T(8,128)(2,1)S(1)}, bf16[10,128,128]{2,1,0:T(8,128)(2,1)S(1)}, u32[]{:S(2)}, u32[]{:S(2)}) collective-permute-start(bf16[10,128,128]{2,1,0:T(8,128)(2,1)S(1)} %get-tuple-element.34), channel_id=1, source_target_pairs={{0,8},{2,10},{8,16},{10,18},{16,24},{18,26},{24,28},{26,30},{28,20... | collective-permute-start | bytes 983048 | tf_op jit(solution)/shard_map/ppermute | solution.py:36
  9.0 0.8 copy.72
  10.5 4.9 %collective-permute-done.1 = bf16[10,128,128]{2,1,0:T(8,128)(2,1)S(1)} collective-permute-done((bf16[10,128,128]{2,1,0:T(8,128)(2,1)S(1)}, bf16[10,128,128]{2,1,0:T(8,128)(2,1)S(1)}, u32[]{:S(2)}, u32[]{:S(2)}) %collective-permute-start.1) | collective-permute-done | bytes 327712 | tf_op jit(solution)/shard_map/ppermute | solution.py:36
  15.4 1.8 %collective-permute-start.3 = (bf16[10,128,128]{2,1,0:T(8,128)(2,1)S(1)}, bf16[10,128,128]{2,1,0:T(8,128)(2,1)S(1)}, u32[]{:S(2)}, u32[]{:S(2)}) collective-permute-start(bf16[10,128,128]{2,1,0:T(8,128)(2,1)S(1)} %collective-permute-done.1), channel_id=1, source_target_pairs={{0,8},{2,10},{8,16},{10,18},{16,24},{18,26},{24,28},{26,30},{28,20... | collective-permute-start | bytes 983048 | tf_op jit(solution)/shard_map/ppermute | solution.py:36
  17.2 0.7 collective-permute-done.10
  18.6 0.5 collective-permute-start.2
  19.2 5.2 %collective-permute-done.3 = bf16[10,128,128]{2,1,0:T(8,128)(2,1)S(1)} collective-permute-done((bf16[10,128,128]{2,1,0:T(8,128)(2,1)S(1)}, bf16[10,128,128]{2,1,0:T(8,128)(2,1)S(1)}, u32[]{:S(2)}, u32[]{:S(2)}) %collective-permute-start.3) | collective-permute-done | bytes 327712 | tf_op jit(solution)/shard_map/ppermute | solution.py:36
  24.3 1.5 %collective-permute-start.5 = (bf16[10,128,128]{2,1,0:T(8,128)(2,1)S(1)}, bf16[10,128,128]{2,1,0:T(8,128)(2,1)}, u32[]{:S(2)}, u32[]{:S(2)}) collective-permute-start(bf16[10,128,128]{2,1,0:T(8,128)(2,1)S(1)} %collective-permute-done.3), channel_id=1, source_target_pairs={{0,8},{2,10},{8,16},{10,18},{16,24},{18,26},{24,28},{26,30},{28,20... | collective-permute-start | bytes 983048 | tf_op jit(solution)/shard_map/ppermute | solution.py:36
  25.8 1.4 %collective-permute-done.12 = bf16[10,128,128]{2,1,0:T(8,128)(2,1)S(1)} collective-permute-done((bf16[10,128,128]{2,1,0:T(8,128)(2,1)S(1)}, bf16[10,128,128]{2,1,0:T(8,128)(2,1)S(1)}, u32[]{:S(2)}, u32[]{:S(2)}) %collective-permute-start.12) | collective-permute-done | bytes 327712 | tf_op jit(solution)/shard_map/ppermute | solution.py:37
  27.7 0.7 copy-done.25
  28.4 0.7 copy-done.17
  29.5 0.5 collective-permute-start.4
  30.1 2.3 %collective-permute-done.5 = bf16[10,128,128]{2,1,0:T(8,128)(2,1)} collective-permute-done((bf16[10,128,128]{2,1,0:T(8,128)(2,1)S(1)}, bf16[10,128,128]{2,1,0:T(8,128)(2,1)}, u32[]{:S(2)}, u32[]{:S(2)}) %collective-permute-start.5) | collective-permute-done | bytes 327712 | tf_op jit(solution)/shard_map/ppermute | solution.py:36
  32.4 1.2 collective-permute-start.7
  33.6 0.7 slice_bitcast_fusion.12
  34.3 1.4 %collective-permute-done.14 = bf16[10,128,128]{2,1,0:T(8,128)(2,1)S(1)} collective-permute-done((bf16[10,128,128]{2,1,0:T(8,128)(2,1)S(1)}, bf16[10,128,128]{2,1,0:T(8,128)(2,1)S(1)}, u32[]{:S(2)}, u32[]{:S(2)}) %collective-permute-start.14) | collective-permute-done | bytes 327712 | tf_op jit(solution)/shard_map/ppermute | solution.py:37
  35.7 0.5 collective-permute-start.16
  36.2 0.7 copy-done.29
  37.0 0.7 copy-done.23
  38.1 0.5 collective-permute-start.6
  38.6 1.4 %collective-permute-done.7 = bf16[10,128,128]{2,1,0:T(8,128)(2,1)} collective-permute-done((bf16[10,128,128]{2,1,0:T(8,128)(2,1)}, bf16[10,128,128]{2,1,0:T(8,128)(2,1)}, u32[]{:S(2)}, u32[]{:S(2)}) %collective-permute-start.7) | collective-permute-done | bytes 327712 | tf_op jit(solution)/shard_map/ppermute | solution.py:36
  40.0 0.7 slice_bitcast_fusion.10
  40.7 2.6 %collective-permute-done.16 = bf16[10,128,128]{2,1,0:T(8,128)(2,1)} collective-permute-done((bf16[10,128,128]{2,1,0:T(8,128)(2,1)S(1)}, bf16[10,128,128]{2,1,0:T(8,128)(2,1)}, u32[]{:S(2)}, u32[]{:S(2)}) %collective-permute-start.16) | collective-permute-done | bytes 327712 | tf_op jit(solution)/shard_map/ppermute | solution.py:37
  43.3 0.6 slice_bitcast_fusion.1
  44.0 0.7 copy-done.31
  44.7 0.7 copy-done.27
  45.9 1.6 %collective-permute-start.18 = (bf16[10,128,128]{2,1,0:T(8,128)(2,1)}, bf16[10,128,128]{2,1,0:T(8,128)(2,1)}, u32[]{:S(2)}, u32[]{:S(2)}) collective-permute-start(bf16[10,128,128]{2,1,0:T(8,128)(2,1)} %collective-permute-done.7), channel_id=1, source_target_pairs={{0,8},{2,10},{8,16},{10,18},{16,24},{18,26},{24,28},{26,30},{28,20... | collective-permute-start | bytes 983048 | tf_op jit(solution)/shard_map/ppermute | solution.py:36
  47.9 0.7 slice_bitcast_fusion.9
  48.7 0.6 slice_bitcast_fusion
  50.2 6.1 %collective-permute-done.18 = bf16[10,128,128]{2,1,0:T(8,128)(2,1)} collective-permute-done((bf16[10,128,128]{2,1,0:T(8,128)(2,1)}, bf16[10,128,128]{2,1,0:T(8,128)(2,1)}, u32[]{:S(2)}, u32[]{:S(2)}) %collective-permute-start.18) | collective-permute-done | bytes 327712 | tf_op jit(solution)/shard_map/ppermute | solution.py:36
  56.3 1.6 %collective-permute-start.20 = (bf16[10,128,128]{2,1,0:T(8,128)(2,1)}, bf16[10,128,128]{2,1,0:T(8,128)(2,1)S(1)}, u32[]{:S(2)}, u32[]{:S(2)}) collective-permute-start(bf16[10,128,128]{2,1,0:T(8,128)(2,1)} %collective-permute-done.18), channel_id=1, source_target_pairs={{0,8},{2,10},{8,16},{10,18},{16,24},{18,26},{24,28},{26,30},{28,20... | collective-permute-start | bytes 983048 | tf_op jit(solution)/shard_map/ppermute | solution.py:36
  58.6 0.5 collective-permute-start.23
  59.1 6.7 %collective-permute-done.20 = bf16[10,128,128]{2,1,0:T(8,128)(2,1)S(1)} collective-permute-done((bf16[10,128,128]{2,1,0:T(8,128)(2,1)}, bf16[10,128,128]{2,1,0:T(8,128)(2,1)S(1)}, u32[]{:S(2)}, u32[]{:S(2)}) %collective-permute-start.20) | collective-permute-done | bytes 327712 | tf_op jit(solution)/shard_map/ppermute | solution.py:36
  65.9 1.4 %collective-permute-done.24 = bf16[10,128,128]{2,1,0:T(8,128)(2,1)S(1)} collective-permute-done((bf16[10,128,128]{2,1,0:T(8,128)(2,1)}, bf16[10,128,128]{2,1,0:T(8,128)(2,1)S(1)}, u32[]{:S(2)}, u32[]{:S(2)}) %collective-permute-start.24) | collective-permute-done | bytes 327712 | tf_op jit(solution)/shard_map/ppermute | solution.py:37
  67.4 1.6 %collective-permute-start.26 = (bf16[10,128,128]{2,1,0:T(8,128)(2,1)S(1)}, bf16[10,128,128]{2,1,0:T(8,128)(2,1)S(1)}, u32[]{:S(2)}, u32[]{:S(2)}) collective-permute-start(bf16[10,128,128]{2,1,0:T(8,128)(2,1)S(1)} %collective-permute-done.20), channel_id=1, source_target_pairs={{0,8},{2,10},{8,16},{10,18},{16,24},{18,26},{24,28},{26,30},{28,20... | collective-permute-start | bytes 983048 | tf_op jit(solution)/shard_map/ppermute | solution.py:36
  69.5 1.0 constant_dynamic-update-slice_fusion.13
  70.6 1.0 constant_dynamic-update-slice_fusion.25
  71.6 1.0 constant_dynamic-update-slice_fusion.29
  72.6 1.0 constant_dynamic-update-slice_fusion.8
  73.7 1.0 constant_dynamic-update-slice_fusion.7
  74.9 1.0 constant_dynamic-update-slice_fusion.3
  76.0 1.0 constant_dynamic-update-slice_fusion.1
  77.0 1.0 constant_dynamic-update-slice_fusion
  78.2 0.7 fusion.134
  80.6 1.0 constant_dynamic-update-slice_fusion.17
  81.7 1.0 constant_dynamic-update-slice_fusion.16
  83.7 0.7 fusion.131
  84.6 0.7 fusion.4
  85.2 2.0 %constant_dynamic-update-slice_fusion.31 = bf16[10,256,128]{2,1,0:T(8,128)(2,1)} fusion(bf16[10,128,128]{2,1,0:T(8,128)(2,1)} %collective-permute-done.28), kind=kLoop, calls=%fused_computation.132 | loop fusion | bytes 655360
  87.5 0.6 fusion.6
  88.9 0.9 fusion.56
  90.3 1.0 fusion.61
  91.3 1.7 %copy.73 = bf16[120,5,128]{0,2,1:T(8,128)(2,1)} copy(bf16[120,5,128]{2,0,1:T(8,128)(2,1)} %fusion.61) | data formatting | bytes 307200 | tf_op jit(solution)/shard_map/convert_element_type | solution.py:76
  93.0 1.8 %constant_dynamic-update-slice_fusion.30 = bf16[10,256,128]{2,1,0:T(8,128)(2,1)} fusion(bf16[10,256,128]{2,1,0:T(8,128)(2,1)} %constant_dynamic-update-slice_fusion.31, bf16[10,128,128]{2,1,0:T(8,128)(2,1)} %collective-permute-done.29), kind=kLoop, calls=%fused_computation.131 | loop fusion | bytes 655360 | tf_op jit(solution)/shard_map/concatenate | solution.py:141
  94.7 1.3 %fusion.132 = (f32[5,120]{1,0:T(8,128)S(1)}, f32[5,120,256]{2,1,0:T(8,128)S(1)}) fusion(bf16[10,256,128]{2,1,0:T(8,128)(2,1)} %constant_dynamic-update-slice_fusion.30, bf16[120,5,128]{2,0,1:T(8,128)(2,1)S(1)} %copy.75, pred[256]{0:T(512)(128)(4,1)S(1)} %compare_bitcast_fusion), kind=kOutput, calls=%fused_computation.209 | convolution fusion | flops 39781800 | bytes 1426016 | tf_op jit(solution)/shard_map/hqd,hkd->hqk/dot_general | solution.py:53
  96.4 2.9 %fusion.51 = f32[120,5,128]{2,0,1:T(8,128)S(1)} fusion(bf16[10,1280,128]{2,1,0:T(8,128)(2,1)S(1)} %constant_dynamic-update-slice_fusion.16, f32[5,120,1280]{2,1,0:T(8,128)} %copy-done, f32[5,120]{1,0:T(8,128)S(1)} %get-tuple-element.95, pred[1280]{0:T(1024)(128)(4,1)S(1)} %fusion.102, f32[120,5]{0,1:T(8,128)S(1)} %get-tuple-element.84), kind=kOutput, calls=%fused_computation.57 | convolution fusion | flops 198988800 | bytes 5027840 | tf_op jit(solution)/shard_map/hqk,hkd->hqd/dot_general | solution.py:60
  100.4 6.6 %fusion.83 = f32[120,5120]{1,0:T(8,128)S(1)} fusion(bf16[1280,5120]{1,0:T(8,128)(2,1)} %param.15, bf16[120,640]{0,1:T(8,128)(2,1)S(1)} %bitcast.312, bf16[120,640]{0,1:T(8,128)(2,1)S(1)} %bitcast.311), kind=kOutput, calls=%fused_computation.83 | convolution fusion | flops 1573478400 | bytes 15872000 | tf_op jit(solution)/shard_map/dot_general | solution.py:151
  107.1 1.7 %reshape.294 = f32[2,60,5120]{2,1,0:T(8,128)} reshape(f32[120,5120]{1,0:T(8,128)S(1)} %fusion.83) | data formatting | bytes 4915200 | tf_op jit(solution)/shard_map/reshape | solution.py:155
  108.8 1.4 %bitcast_convert_fusion = bf16[60,5120]{1,0:T(8,128)(2,1)S(1)} fusion(f32[2,60,5120]{2,1,0:T(8,128)} %reshape.294, s32[]{:T(128)S(6)} %select_n.287, pred[]{:T(512)S(6)} %and.124), kind=kLoop, calls=%fused_computation.28 | loop fusion | flops 307200 | bytes 1228805 | tf_op jit(solution)/shard_map/convert_element_type | solution.py:157
  110.2 1.6 %collective-permute-start.30 = (bf16[60,5120]{1,0:T(8,128)(2,1)S(1)}, bf16[60,5120]{1,0:T(8,128)(2,1)S(1)}, u32[]{:S(2)}, u32[]{:S(2)}) collective-permute-start(bf16[60,5120]{1,0:T(8,128)(2,1)S(1)} %bitcast_convert_fusion), channel_id=1, source_target_pairs={{0,1},{1,0},{2,3},{3,2},{4,5},{5,4},{6,7},{7,6},{8,9},{9,8},{10,11... | collective-permute-start | bytes 1843208 | tf_op jit(solution)/shard_map/ppermute | solution.py:158
  111.8 15.4 %collective-permute-done.30 = bf16[60,5120]{1,0:T(8,128)(2,1)S(1)} collective-permute-done((bf16[60,5120]{1,0:T(8,128)(2,1)S(1)}, bf16[60,5120]{1,0:T(8,128)(2,1)S(1)}, u32[]{:S(2)}, u32[]{:S(2)}) %collective-permute-start.30) | collective-permute-done | bytes 614432 | tf_op jit(solution)/shard_map/ppermute | solution.py:158
  127.2 2.4 %fusion.26 = bf16[60,5120]{1,0:T(8,128)(2,1)} fusion(f32[2,60,5120]{2,1,0:T(8,128)} %reshape.294, s32[]{:T(128)S(6)} %select_n.285, bf16[60,5120]{1,0:T(8,128)(2,1)S(1)} %collective-permute-done.30, bf16[60,5120]{1,0:T(8,128)(2,1)S(1)} %copy-done.8, f32[5120]{0:T(1024)S(1)} %copy-done.35, pred[]{:T(512)S(6)} %and.123), kind=kLoop, calls=%fused_computation.32 | loop fusion | flops 2150400 | bytes 3092485 | tf_op jit(solution)/shard_map/convert_element_type | solution.py:160
  (201 shorter events, 13.7 us)
Async XLA Ops:
  0.0 8.3 %copy-start.33 = (bf16[120,1280]{1,0:T(8,128)(2,1)S(1)}, bf16[120,1280]{1,0:T(8,128)(2,1)}, u32[]{:S(2)}) copy-start(bf16[120,1280]{1,0:T(8,128)(2,1)} %param.11) | copy-start | bytes 921604
  4.7 64.8 %copy-start.6 = (bf16[10,128,128]{2,1,0:T(8,128)(2,1)}, bf16[10,128,128]{2,1,0:T(8,128)(2,1)S(1)}, u32[]{:S(2)}) copy-start(bf16[10,128,128]{2,1,0:T(8,128)(2,1)S(1)} %get-tuple-element.48) | copy-start | bytes 983044
  4.7 10.7 %collective-permute-start.1 = (bf16[10,128,128]{2,1,0:T(8,128)(2,1)S(1)}, bf16[10,128,128]{2,1,0:T(8,128)(2,1)S(1)}, u32[]{:S(2)}, u32[]{:S(2)}) collective-permute-start(bf16[10,128,128]{2,1,0:T(8,128)(2,1)S(1)} %get-tuple-element.34), channel_id=1, source_target_pairs={{0,8},{2,10},{8,16},{10,18},{16,24},{18,26},{24,28},{26,30},{28,20... | collective-permute-start | bytes 983048 | tf_op jit(solution)/shard_map/ppermute | solution.py:36
  7.8 10.4 %collective-permute-start = (bf16[10,128,128]{2,1,0:T(8,128)(2,1)S(1)}, bf16[10,128,128]{2,1,0:T(8,128)(2,1)S(1)}, u32[]{:S(2)}, u32[]{:S(2)}) collective-permute-start(bf16[10,128,128]{2,1,0:T(8,128)(2,1)S(1)} %get-tuple-element.34), channel_id=1, source_target_pairs={{0,2},{2,0},{4,6},{6,4},{8,10},{10,8},{12,14},{14,12},{16,18},{18,... | collective-permute-start | bytes 983048 | tf_op jit(solution)/shard_map/ppermute | solution.py:40
  7.8 10.1 %collective-permute-start.10 = (bf16[10,128,128]{2,1,0:T(8,128)(2,1)S(1)}, bf16[10,128,128]{2,1,0:T(8,128)(2,1)S(1)}, u32[]{:S(2)}, u32[]{:S(2)}) collective-permute-start(bf16[10,128,128]{2,1,0:T(8,128)(2,1)S(1)} %get-tuple-element.48), channel_id=1, source_target_pairs={{8,0},{10,2},{16,8},{18,10},{24,16},{26,18},{28,24},{30,26},{20,28... | collective-permute-start | bytes 983048 | tf_op jit(solution)/shard_map/ppermute | solution.py:37
  7.8 10.3 %collective-permute-start.9 = (bf16[10,128,128]{2,1,0:T(8,128)(2,1)S(1)}, bf16[10,128,128]{2,1,0:T(8,128)(2,1)S(1)}, u32[]{:S(2)}, u32[]{:S(2)}) collective-permute-start(bf16[10,128,128]{2,1,0:T(8,128)(2,1)S(1)} %get-tuple-element.48), channel_id=1, source_target_pairs={{0,2},{2,0},{4,6},{6,4},{8,10},{10,8},{12,14},{14,12},{16,18},{18,... | collective-permute-start | bytes 983048 | tf_op jit(solution)/shard_map/ppermute | solution.py:41
  15.4 54.1 %copy-start.13 = (bf16[10,128,128]{2,1,0:T(8,128)(2,1)}, bf16[10,128,128]{2,1,0:T(8,128)(2,1)S(1)}, u32[]{:S(2)}) copy-start(bf16[10,128,128]{2,1,0:T(8,128)(2,1)S(1)} %collective-permute-done.1) | copy-start | bytes 983044
  15.4 8.9 %collective-permute-start.3 = (bf16[10,128,128]{2,1,0:T(8,128)(2,1)S(1)}, bf16[10,128,128]{2,1,0:T(8,128)(2,1)S(1)}, u32[]{:S(2)}, u32[]{:S(2)}) collective-permute-start(bf16[10,128,128]{2,1,0:T(8,128)(2,1)S(1)} %collective-permute-done.1), channel_id=1, source_target_pairs={{0,8},{2,10},{8,16},{10,18},{16,24},{18,26},{24,28},{26,30},{28,20... | collective-permute-start | bytes 983048 | tf_op jit(solution)/shard_map/ppermute | solution.py:36
  17.9 51.6 %copy-start.9 = (bf16[10,128,128]{2,1,0:T(8,128)(2,1)}, bf16[10,128,128]{2,1,0:T(8,128)(2,1)S(1)}, u32[]{:S(2)}) copy-start(bf16[10,128,128]{2,1,0:T(8,128)(2,1)S(1)} %collective-permute-done.10) | copy-start | bytes 983044
  17.9 9.3 %collective-permute-start.12 = (bf16[10,128,128]{2,1,0:T(8,128)(2,1)S(1)}, bf16[10,128,128]{2,1,0:T(8,128)(2,1)S(1)}, u32[]{:S(2)}, u32[]{:S(2)}) collective-permute-start(bf16[10,128,128]{2,1,0:T(8,128)(2,1)S(1)} %collective-permute-done.10), channel_id=1, source_target_pairs={{8,0},{10,2},{16,8},{18,10},{24,16},{26,18},{28,24},{30,26},{20,28... | collective-permute-start | bytes 983048 | tf_op jit(solution)/shard_map/ppermute | solution.py:37
  18.2 51.3 %copy-start.14 = (bf16[10,128,128]{2,1,0:T(8,128)(2,1)}, bf16[10,128,128]{2,1,0:T(8,128)(2,1)S(1)}, u32[]{:S(2)}) copy-start(bf16[10,128,128]{2,1,0:T(8,128)(2,1)S(1)} %collective-permute-done) | copy-start | bytes 983044
  18.2 51.3 %copy-start.11 = (bf16[10,128,128]{2,1,0:T(8,128)(2,1)}, bf16[10,128,128]{2,1,0:T(8,128)(2,1)S(1)}, u32[]{:S(2)}) copy-start(bf16[10,128,128]{2,1,0:T(8,128)(2,1)S(1)} %collective-permute-done.9) | copy-start | bytes 983044
  18.6 9.0 %collective-permute-start.11 = (bf16[10,128,128]{2,1,0:T(8,128)(2,1)S(1)}, bf16[10,128,128]{2,1,0:T(8,128)(2,1)S(1)}, u32[]{:S(2)}, u32[]{:S(2)}) collective-permute-start(bf16[10,128,128]{2,1,0:T(8,128)(2,1)S(1)} %collective-permute-done.10), channel_id=1, source_target_pairs={{0,2},{2,0},{4,6},{6,4},{8,10},{10,8},{12,14},{14,12},{16,18},{18,... | collective-permute-start | bytes 983048 | tf_op jit(solution)/shard_map/ppermute | solution.py:41
  18.6 9.0 %collective-permute-start.2 = (bf16[10,128,128]{2,1,0:T(8,128)(2,1)S(1)}, bf16[10,128,128]{2,1,0:T(8,128)(2,1)S(1)}, u32[]{:S(2)}, u32[]{:S(2)}) collective-permute-start(bf16[10,128,128]{2,1,0:T(8,128)(2,1)S(1)} %collective-permute-done.1), channel_id=1, source_target_pairs={{0,2},{2,0},{4,6},{6,4},{8,10},{10,8},{12,14},{14,12},{16,18},{18,... | collective-permute-start | bytes 983048 | tf_op jit(solution)/shard_map/ppermute | solution.py:40
  24.3 45.2 %copy-start.21 = (bf16[10,128,128]{2,1,0:T(8,128)(2,1)}, bf16[10,128,128]{2,1,0:T(8,128)(2,1)S(1)}, u32[]{:S(2)}) copy-start(bf16[10,128,128]{2,1,0:T(8,128)(2,1)S(1)} %collective-permute-done.3) | copy-start | bytes 983044
  24.3 8.1 %collective-permute-start.5 = (bf16[10,128,128]{2,1,0:T(8,128)(2,1)S(1)}, bf16[10,128,128]{2,1,0:T(8,128)(2,1)}, u32[]{:S(2)}, u32[]{:S(2)}) collective-permute-start(bf16[10,128,128]{2,1,0:T(8,128)(2,1)S(1)} %collective-permute-done.3), channel_id=1, source_target_pairs={{0,8},{2,10},{8,16},{10,18},{16,24},{18,26},{24,28},{26,30},{28,20... | collective-permute-start | bytes 983048 | tf_op jit(solution)/shard_map/ppermute | solution.py:36
  27.2 42.3 %copy-start.15 = (bf16[10,128,128]{2,1,0:T(8,128)(2,1)}, bf16[10,128,128]{2,1,0:T(8,128)(2,1)S(1)}, u32[]{:S(2)}) copy-start(bf16[10,128,128]{2,1,0:T(8,128)(2,1)S(1)} %collective-permute-done.12) | copy-start | bytes 983044
  27.2 8.5 %collective-permute-start.14 = (bf16[10,128,128]{2,1,0:T(8,128)(2,1)S(1)}, bf16[10,128,128]{2,1,0:T(8,128)(2,1)S(1)}, u32[]{:S(2)}, u32[]{:S(2)}) collective-permute-start(bf16[10,128,128]{2,1,0:T(8,128)(2,1)S(1)} %collective-permute-done.12), channel_id=1, source_target_pairs={{8,0},{10,2},{16,8},{18,10},{24,16},{26,18},{28,24},{30,26},{20,28... | collective-permute-start | bytes 983048 | tf_op jit(solution)/shard_map/ppermute | solution.py:37
  27.6 0.7 copy-start.25
  29.5 6.7 %collective-permute-start.13 = (bf16[10,128,128]{2,1,0:T(8,128)(2,1)S(1)}, bf16[10,128,128]{2,1,0:T(8,128)(2,1)S(1)}, u32[]{:S(2)}, u32[]{:S(2)}) collective-permute-start(bf16[10,128,128]{2,1,0:T(8,128)(2,1)S(1)} %collective-permute-done.12), channel_id=1, source_target_pairs={{0,2},{2,0},{4,6},{6,4},{8,10},{10,8},{12,14},{14,12},{16,18},{18,... | collective-permute-start | bytes 983048 | tf_op jit(solution)/shard_map/ppermute | solution.py:41
  29.5 6.7 %collective-permute-start.4 = (bf16[10,128,128]{2,1,0:T(8,128)(2,1)S(1)}, bf16[10,128,128]{2,1,0:T(8,128)(2,1)S(1)}, u32[]{:S(2)}, u32[]{:S(2)}) collective-permute-start(bf16[10,128,128]{2,1,0:T(8,128)(2,1)S(1)} %collective-permute-done.3), channel_id=1, source_target_pairs={{0,2},{2,0},{4,6},{6,4},{8,10},{10,8},{12,14},{14,12},{16,18},{18,... | collective-permute-start | bytes 983048 | tf_op jit(solution)/shard_map/ppermute | solution.py:40
  32.4 7.6 %collective-permute-start.7 = (bf16[10,128,128]{2,1,0:T(8,128)(2,1)}, bf16[10,128,128]{2,1,0:T(8,128)(2,1)}, u32[]{:S(2)}, u32[]{:S(2)}) collective-permute-start(bf16[10,128,128]{2,1,0:T(8,128)(2,1)} %collective-permute-done.5), channel_id=1, source_target_pairs={{0,8},{2,10},{8,16},{10,18},{16,24},{18,26},{24,28},{26,30},{28,20... | collective-permute-start | bytes 983048 | tf_op jit(solution)/shard_map/ppermute | solution.py:36
  35.7 33.8 %copy-start.19 = (bf16[10,128,128]{2,1,0:T(8,128)(2,1)}, bf16[10,128,128]{2,1,0:T(8,128)(2,1)S(1)}, u32[]{:S(2)}) copy-start(bf16[10,128,128]{2,1,0:T(8,128)(2,1)S(1)} %collective-permute-done.14) | copy-start | bytes 983044
  35.7 7.6 %collective-permute-start.16 = (bf16[10,128,128]{2,1,0:T(8,128)(2,1)S(1)}, bf16[10,128,128]{2,1,0:T(8,128)(2,1)}, u32[]{:S(2)}, u32[]{:S(2)}) collective-permute-start(bf16[10,128,128]{2,1,0:T(8,128)(2,1)S(1)} %collective-permute-done.14), channel_id=1, source_target_pairs={{8,0},{10,2},{16,8},{18,10},{24,16},{26,18},{28,24},{30,26},{20,28... | collective-permute-start | bytes 983048 | tf_op jit(solution)/shard_map/ppermute | solution.py:37
  37.0 0.7 copy-start.23
  38.1 5.8 %collective-permute-start.15 = (bf16[10,128,128]{2,1,0:T(8,128)(2,1)S(1)}, bf16[10,128,128]{2,1,0:T(8,128)(2,1)S(1)}, u32[]{:S(2)}, u32[]{:S(2)}) collective-permute-start(bf16[10,128,128]{2,1,0:T(8,128)(2,1)S(1)} %collective-permute-done.14), channel_id=1, source_target_pairs={{0,2},{2,0},{4,6},{6,4},{8,10},{10,8},{12,14},{14,12},{16,18},{18,... | collective-permute-start | bytes 983048 | tf_op jit(solution)/shard_map/ppermute | solution.py:41
  38.1 5.8 %collective-permute-start.6 = (bf16[10,128,128]{2,1,0:T(8,128)(2,1)}, bf16[10,128,128]{2,1,0:T(8,128)(2,1)S(1)}, u32[]{:S(2)}, u32[]{:S(2)}) collective-permute-start(bf16[10,128,128]{2,1,0:T(8,128)(2,1)} %collective-permute-done.5), channel_id=1, source_target_pairs={{0,2},{2,0},{4,6},{6,4},{8,10},{10,8},{12,14},{14,12},{16,18},{18,... | collective-permute-start | bytes 983048 | tf_op jit(solution)/shard_map/ppermute | solution.py:40
  40.0 7.9 %collective-permute-start.8 = (bf16[10,128,128]{2,1,0:T(8,128)(2,1)}, bf16[10,128,128]{2,1,0:T(8,128)(2,1)}, u32[]{:S(2)}, u32[]{:S(2)}) collective-permute-start(bf16[10,128,128]{2,1,0:T(8,128)(2,1)} %collective-permute-done.7), channel_id=1, source_target_pairs={{0,2},{2,0},{4,6},{6,4},{8,10},{10,8},{12,14},{14,12},{16,18},{18,... | collective-permute-start | bytes 983048 | tf_op jit(solution)/shard_map/ppermute | solution.py:40
  43.3 5.4 %collective-permute-start.17 = (bf16[10,128,128]{2,1,0:T(8,128)(2,1)}, bf16[10,128,128]{2,1,0:T(8,128)(2,1)}, u32[]{:S(2)}, u32[]{:S(2)}) collective-permute-start(bf16[10,128,128]{2,1,0:T(8,128)(2,1)} %collective-permute-done.16), channel_id=1, source_target_pairs={{0,2},{2,0},{4,6},{6,4},{8,10},{10,8},{12,14},{14,12},{16,18},{18,... | collective-permute-start | bytes 983048 | tf_op jit(solution)/shard_map/ppermute | solution.py:41
  44.0 0.7 copy-start.31
  45.9 10.4 %collective-permute-start.18 = (bf16[10,128,128]{2,1,0:T(8,128)(2,1)}, bf16[10,128,128]{2,1,0:T(8,128)(2,1)}, u32[]{:S(2)}, u32[]{:S(2)}) collective-permute-start(bf16[10,128,128]{2,1,0:T(8,128)(2,1)} %collective-permute-done.7), channel_id=1, source_target_pairs={{0,8},{2,10},{8,16},{10,18},{16,24},{18,26},{24,28},{26,30},{28,20... | collective-permute-start | bytes 983048 | tf_op jit(solution)/shard_map/ppermute | solution.py:36
  47.4 10.5 %collective-permute-start.22 = (bf16[10,128,128]{2,1,0:T(8,128)(2,1)}, bf16[10,128,128]{2,1,0:T(8,128)(2,1)}, u32[]{:S(2)}, u32[]{:S(2)}) collective-permute-start(bf16[10,128,128]{2,1,0:T(8,128)(2,1)} %collective-permute-done.16), channel_id=1, source_target_pairs={{8,0},{10,2},{16,8},{18,10},{24,16},{26,18},{28,24},{30,26},{20,28... | collective-permute-start | bytes 983048 | tf_op jit(solution)/shard_map/ppermute | solution.py:37
  49.5 25.2 %copy-start.26 = (bf16[10,128,128]{2,1,0:T(8,128)(2,1)S(1)}, bf16[10,128,128]{2,1,0:T(8,128)(2,1)}, u32[]{:S(2)}) copy-start(bf16[10,128,128]{2,1,0:T(8,128)(2,1)} %copy-done.25) | copy-start | bytes 983044
  49.5 25.3 %copy-start.30 = (bf16[10,128,128]{2,1,0:T(8,128)(2,1)S(1)}, bf16[10,128,128]{2,1,0:T(8,128)(2,1)}, u32[]{:S(2)}) copy-start(bf16[10,128,128]{2,1,0:T(8,128)(2,1)} %copy-done.29) | copy-start | bytes 983044
  56.3 9.6 %collective-permute-start.20 = (bf16[10,128,128]{2,1,0:T(8,128)(2,1)}, bf16[10,128,128]{2,1,0:T(8,128)(2,1)S(1)}, u32[]{:S(2)}, u32[]{:S(2)}) collective-permute-start(bf16[10,128,128]{2,1,0:T(8,128)(2,1)} %collective-permute-done.18), channel_id=1, source_target_pairs={{0,8},{2,10},{8,16},{10,18},{16,24},{18,26},{24,28},{26,30},{28,20... | collective-permute-start | bytes 983048 | tf_op jit(solution)/shard_map/ppermute | solution.py:36
  58.0 9.3 %collective-permute-start.24 = (bf16[10,128,128]{2,1,0:T(8,128)(2,1)}, bf16[10,128,128]{2,1,0:T(8,128)(2,1)S(1)}, u32[]{:S(2)}, u32[]{:S(2)}) collective-permute-start(bf16[10,128,128]{2,1,0:T(8,128)(2,1)} %collective-permute-done.22), channel_id=1, source_target_pairs={{8,0},{10,2},{16,8},{18,10},{24,16},{26,18},{28,24},{30,26},{20,28... | collective-permute-start | bytes 983048 | tf_op jit(solution)/shard_map/ppermute | solution.py:37
  58.6 10.4 %collective-permute-start.19 = (bf16[10,128,128]{2,1,0:T(8,128)(2,1)}, bf16[10,128,128]{2,1,0:T(8,128)(2,1)S(1)}, u32[]{:S(2)}, u32[]{:S(2)}) collective-permute-start(bf16[10,128,128]{2,1,0:T(8,128)(2,1)} %collective-permute-done.18), channel_id=1, source_target_pairs={{0,2},{2,0},{4,6},{6,4},{8,10},{10,8},{12,14},{14,12},{16,18},{18,... | collective-permute-start | bytes 983048 | tf_op jit(solution)/shard_map/ppermute | solution.py:40
  58.6 10.9 %collective-permute-start.23 = (bf16[10,128,128]{2,1,0:T(8,128)(2,1)}, bf16[10,128,128]{2,1,0:T(8,128)(2,1)S(1)}, u32[]{:S(2)}, u32[]{:S(2)}) collective-permute-start(bf16[10,128,128]{2,1,0:T(8,128)(2,1)} %collective-permute-done.22), channel_id=1, source_target_pairs={{0,2},{2,0},{4,6},{6,4},{8,10},{10,8},{12,14},{14,12},{16,18},{18,... | collective-permute-start | bytes 983048 | tf_op jit(solution)/shard_map/ppermute | solution.py:41
  65.9 3.6 %collective-permute-start.21 = (bf16[10,128,128]{2,1,0:T(8,128)(2,1)S(1)}, bf16[10,128,128]{2,1,0:T(8,128)(2,1)S(1)}, u32[]{:S(2)}, u32[]{:S(2)}) collective-permute-start(bf16[10,128,128]{2,1,0:T(8,128)(2,1)S(1)} %collective-permute-done.20), channel_id=1, source_target_pairs={{0,2},{2,0},{4,6},{6,4},{8,10},{10,8},{12,14},{14,12},{16,18},{18,... | collective-permute-start | bytes 983048 | tf_op jit(solution)/shard_map/ppermute | solution.py:40
  67.2 2.2 %collective-permute-start.25 = (bf16[10,128,128]{2,1,0:T(8,128)(2,1)S(1)}, bf16[10,128,128]{2,1,0:T(8,128)(2,1)S(1)}, u32[]{:S(2)}, u32[]{:S(2)}) collective-permute-start(bf16[10,128,128]{2,1,0:T(8,128)(2,1)S(1)} %collective-permute-done.24), channel_id=1, source_target_pairs={{0,2},{2,0},{4,6},{6,4},{8,10},{10,8},{12,14},{14,12},{16,18},{18,... | collective-permute-start | bytes 983048 | tf_op jit(solution)/shard_map/ppermute | solution.py:41
  67.4 17.1 %collective-permute-start.26 = (bf16[10,128,128]{2,1,0:T(8,128)(2,1)S(1)}, bf16[10,128,128]{2,1,0:T(8,128)(2,1)S(1)}, u32[]{:S(2)}, u32[]{:S(2)}) collective-permute-start(bf16[10,128,128]{2,1,0:T(8,128)(2,1)S(1)} %collective-permute-done.20), channel_id=1, source_target_pairs={{0,8},{2,10},{8,16},{10,18},{16,24},{18,26},{24,28},{26,30},{28,20... | collective-permute-start | bytes 983048 | tf_op jit(solution)/shard_map/ppermute | solution.py:36
  69.0 16.3 %collective-permute-start.28 = (bf16[10,128,128]{2,1,0:T(8,128)(2,1)S(1)}, bf16[10,128,128]{2,1,0:T(8,128)(2,1)}, u32[]{:S(2)}, u32[]{:S(2)}) collective-permute-start(bf16[10,128,128]{2,1,0:T(8,128)(2,1)S(1)} %collective-permute-done.24), channel_id=1, source_target_pairs={{8,0},{10,2},{16,8},{18,10},{24,16},{26,18},{28,24},{30,26},{20,28... | collective-permute-start | bytes 983048 | tf_op jit(solution)/shard_map/ppermute | solution.py:37
  69.5 6.4 %copy-start.32 = (bf16[10,128,128]{2,1,0:T(8,128)(2,1)S(1)}, bf16[10,128,128]{2,1,0:T(8,128)(2,1)}, u32[]{:S(2)}) copy-start(bf16[10,128,128]{2,1,0:T(8,128)(2,1)} %copy-done.31) | copy-start | bytes 983044
  70.6 4.2 %copy-start.22 = (bf16[10,128,128]{2,1,0:T(8,128)(2,1)S(1)}, bf16[10,128,128]{2,1,0:T(8,128)(2,1)}, u32[]{:S(2)}) copy-start(bf16[10,128,128]{2,1,0:T(8,128)(2,1)} %copy-done.21) | copy-start | bytes 983044
  74.8 3.4 %copy-start.5 = (bf16[120,5,128]{2,0,1:T(8,128)(2,1)S(1)}, bf16[120,5,128]{2,0,1:T(8,128)(2,1)}, u32[]{:S(2)}) copy-start(bf16[120,5,128]{2,0,1:T(8,128)(2,1)} %copy.72) | copy-start | bytes 460804
  78.9 1.0 copy-start.12
  78.9 1.1 copy-start.10
  78.9 1.2 copy-start.18
  78.9 1.2 copy-start.16
  79.0 1.3 %copy-start.24 = (bf16[10,128,128]{2,1,0:T(8,128)(2,1)S(1)}, bf16[10,128,128]{2,1,0:T(8,128)(2,1)}, u32[]{:S(2)}) copy-start(bf16[10,128,128]{2,1,0:T(8,128)(2,1)} %copy-done.23) | copy-start | bytes 983044
  79.4 1.1 copy-start.20
  79.4 1.2 copy-start.28
  82.8 1.6 %copy-start.1 = (bf16[10,512,128]{2,1,0:T(8,128)(2,1)}, bf16[10,512,128]{2,1,0:T(8,128)(2,1)S(1)}, u32[]{:S(2)}) copy-start(bf16[10,512,128]{2,1,0:T(8,128)(2,1)S(1)} %constant_dynamic-update-slice_fusion.26) | copy-start | bytes 3932164
  83.3 1.1 copy-start.3
  84.4 3.7 %copy-start = (f32[5,120,1280]{2,1,0:T(8,128)}, f32[5,120,1280]{2,1,0:T(8,128)S(1)}, u32[]{:S(2)}) copy-start(f32[5,120,1280]{2,1,0:T(8,128)S(1)} %get-tuple-element.96) | copy-start | bytes 9216004
  84.5 3.6 %collective-permute-start.27 = (bf16[10,128,128]{2,1,0:T(8,128)(2,1)S(1)}, bf16[10,128,128]{2,1,0:T(8,128)(2,1)S(1)}, u32[]{:S(2)}, u32[]{:S(2)}) collective-permute-start(bf16[10,128,128]{2,1,0:T(8,128)(2,1)S(1)} %collective-permute-done.26), channel_id=1, source_target_pairs={{0,2},{2,0},{4,6},{6,4},{8,10},{10,8},{12,14},{14,12},{16,18},{18,... | collective-permute-start | bytes 983048 | tf_op jit(solution)/shard_map/ppermute | solution.py:40
  87.2 5.8 %collective-permute-start.29 = (bf16[10,128,128]{2,1,0:T(8,128)(2,1)}, bf16[10,128,128]{2,1,0:T(8,128)(2,1)}, u32[]{:S(2)}, u32[]{:S(2)}) collective-permute-start(bf16[10,128,128]{2,1,0:T(8,128)(2,1)} %collective-permute-done.28), channel_id=1, source_target_pairs={{0,2},{2,0},{4,6},{6,4},{8,10},{10,8},{12,14},{14,12},{16,18},{18,... | collective-permute-start | bytes 983048 | tf_op jit(solution)/shard_map/ppermute | solution.py:41
  96.4 3.0 %copy-start.2 = (bf16[10,512,128]{2,1,0:T(8,128)(2,1)S(1)}, bf16[10,512,128]{2,1,0:T(8,128)(2,1)}, u32[]{:S(2)}) copy-start(bf16[10,512,128]{2,1,0:T(8,128)(2,1)} %copy-done.1) | copy-start | bytes 3932164
  96.4 3.0 %copy-start.4 = (f32[5,120,512]{2,1,0:T(8,128)S(1)}, f32[5,120,512]{2,1,0:T(8,128)}, u32[]{:S(2)}) copy-start(f32[5,120,512]{2,1,0:T(8,128)} %copy-done.3) | copy-start | bytes 3686404
  96.4 3.5 %copy-start.34 = (bf16[10,256,128]{2,1,0:T(8,128)(2,1)S(1)}, bf16[10,256,128]{2,1,0:T(8,128)(2,1)}, u32[]{:S(2)}) copy-start(bf16[10,256,128]{2,1,0:T(8,128)(2,1)} %constant_dynamic-update-slice_fusion.30) | copy-start | bytes 1966084
  99.4 1.0 copy-start.7
  107.0 20.1 %copy-start.8 = (bf16[60,5120]{1,0:T(8,128)(2,1)S(1)}, bf16[60,5120]{1,0:T(8,128)(2,1)}, u32[]{:S(2)}) copy-start(bf16[60,5120]{1,0:T(8,128)(2,1)} %param.10) | copy-start | bytes 1843204
  107.1 20.1 %copy-start.35 = (f32[5120]{0:T(1024)S(1)}, f32[5120]{0:T(1024)}, u32[]{:S(2)}) copy-start(f32[5120]{0:T(1024)} %param.14) | copy-start | bytes 61444
  110.2 17.0 %collective-permute-start.30 = (bf16[60,5120]{1,0:T(8,128)(2,1)S(1)}, bf16[60,5120]{1,0:T(8,128)(2,1)S(1)}, u32[]{:S(2)}, u32[]{:S(2)}) collective-permute-start(bf16[60,5120]{1,0:T(8,128)(2,1)S(1)} %bitcast_convert_fusion), channel_id=1, source_target_pairs={{0,1},{1,0},{2,3},{3,2},{4,5},{5,4},{6,7},{7,6},{8,9},{9,8},{10,11... | collective-permute-start | bytes 1843208 | tf_op jit(solution)/shard_map/ppermute | solution.py:158
  (3 other events, 2.2 us)

commit v10 on v9

--- a/solution.py
+++ b/solution.py
@@ -3,6 +3,7 @@
 import jax
 import jax.numpy as jnp
 from jax import lax
+from jax.experimental import pallas as pl
 from jax.sharding import PartitionSpec as P
 
 HEAD = 128
@@ -63,6 +64,50 @@
     return peak, totals, summed
 
 
+def phase_kernel(count, heads, scale_factor):
+    def kernel(*refs):
+        q_ref, keep_ref = refs[0], refs[1]
+        packets = refs[2 : 2 + count]
+        peak_ref, totals_ref, summed_ref = refs[2 + count :]
+        for head in range(heads):
+            q = q_ref[head]
+            scores = []
+            for p in range(count):
+                s = lax.dot_general(
+                    q, packets[p][head], (((1,), (1,)), ((), ())), preferred_element_type=jnp.float32
+                )
+                scores.append(jnp.where(keep_ref[p] > 0, s * scale_factor, neg_large))
+            peak = jnp.max(scores[0], axis=1, keepdims=True)
+            for s in scores[1:]:
+                peak = jnp.maximum(peak, jnp.max(s, axis=1, keepdims=True))
+            totals = jnp.zeros_like(peak)
+            summed = jnp.zeros((q.shape[0], q.shape[1]), jnp.float32)
+            for p in range(count):
+                weights = jnp.where(keep_ref[p] > 0, jnp.exp(scores[p] - peak), 0.0)
+                totals = totals + jnp.sum(weights, axis=1, keepdims=True)
+                summed = summed + jnp.dot(
+                    weights.astype(jnp.bfloat16), packets[p][heads + head], preferred_element_type=jnp.float32
+                )
+            peak_ref[head] = peak
+            totals_ref[head] = totals
+            summed_ref[head] = summed
+
+    return kernel
+
+
+def attend_packets(q3, packets, keep, scale_factor, interpret=False):
+    heads, rows, width = q3.shape
+    count = len(packets)
+    out_shape = (
+        jax.ShapeDtypeStruct((heads, rows, 1), jnp.float32),
+        jax.ShapeDtypeStruct((heads, rows, 1), jnp.float32),
+        jax.ShapeDtypeStruct((heads, rows, width), jnp.float32),
+    )
+    return pl.pallas_call(
+        phase_kernel(count, heads, scale_factor), out_shape=out_shape, interpret=interpret
+    )(q3, keep, *packets)
+
+
 def combine(parts, rows_dev):
     peak = parts[0][0]
     for part in parts[1:]:
@@ -138,11 +183,8 @@
             q3 = queries[:, lo * HEAD : hi * HEAD].reshape(rows_dev, hi - lo, HEAD).transpose(1, 0, 2)
             parts = []
             for first, last in phases:
-                stack = jnp.concatenate(got[first:last], axis=1)
-                keys = stack[: hi - lo]
-                values = stack[hi - lo :]
-                keeping = (within[None, :] < limits[first:last, None]).reshape(-1)
-                parts.append(attend_part(q3, keys, values, keeping, scale_factor))
+                keep = (within[None, :] < limits[first:last, None]).astype(jnp.float32)[:, None, :]
+                parts.append(attend_packets(q3, got[first:last], keep, scale_factor))
             return combine(parts, rows_dev)
 
         attention = jnp.concatenate(

time: 130 us -> 138 us (1.062)
  Pallas kernels: 0 us -> 25.9 us
  local copies, waits for them, and re-layouts: 33.8 us -> 17.7 us
  matrix products: 16.7 us -> 6.65 us
  other arithmetic: 7.63 us -> 13.5 us
  waiting for transfers between devices: 49.6 us -> 51.3 us
    pallas_call x0 -> x6, Pallas kernels: none -> 25.9 us  [attend_packets(): pl.pallas_call(phase_kernel(count, heads, scale_factor), out_shape=out_sh...]
    ppermute x7, waiting for transfers between devices: 7.52 us -> 21.4 us  [gather_ring(): cur_b = lax.ppermute(cur_b, 'seq', backward)]
    ppermute x7, waiting for transfers between devices: 26.6 us -> 14.6 us  [gather_ring(): cur_a = lax.ppermute(cur_a, 'seq', forward)]
    dot_general x12 -> x0, matrix products: 10.1 us -> none  [the longest x6 6.14 us: attend_part(): jnp.einsum('hqk,hkd->hqd', weights.astype(jnp.bfloat16), values, preferre...]
    unnamed x98 -> x90, local copies, waits for them, and re-layouts: 15.9 us -> 6 us
    convert_element_type x0 -> x6, other arithmetic: none -> 4.02 us  [half(): (within[None, :] < limits[first:last, None]).astype(jnp.float32)[:, None, :]]
    concatenate x6 -> x0, local copies, waits for them, and re-layouts: 3.93 us -> none  [half(): stack = jnp.concatenate(got[first:last], axis=1)]
    exp x0 -> x2, other arithmetic: none -> 3.14 us  [combine(): factor = jnp.exp(part_peak - peak)]
  transfers between devices with their start and end apart: 31 -> 31, of which waited for: 12 -> 13; matrix products, arithmetic and copies ran while one was open for 23% -> 10% of each run, Pallas kernels for 0% -> 16%
where the time goes in v10:
time: 138 us
  waiting for transfers between devices  51.3 us (37%)
  Pallas kernels  25.9 us (19%)
  starting transfers between devices  20.5 us (15%)
  local copies, waits for them, and re-layouts  17.7 us (13%)
  other arithmetic  13.5 us (10%)
  matrix products  6.65 us (5%)
  between operations  2.12 us (2%)
    pallas_call x6, Pallas kernels, attend_packets(): pl.pallas_call(phase_kernel(count, heads, scale_factor), out_shape=out_sh...  25.9 us
    ppermute x7, waiting for transfers between devices, gather_ring(): cur_b = lax.ppermute(cur_b, 'seq', backward)  21.4 us
    ppermute x1, waiting for transfers between devices, on_device(): came = lax.ppermute(other, 'tp', [(0, 1), (1, 0)])  15.2 us
    ppermute x7, waiting for transfers between devices, gather_ring(): cur_a = lax.ppermute(cur_a, 'seq', forward)  14.6 us
    ppermute x7, starting transfers between devices, gather_ring(): cur_a = lax.ppermute(cur_a, 'seq', forward)  12.7 us
    dot_general x1, matrix products, on_device(): partial = jnp.dot(attention, out_weight, preferred_element_type=jnp.float32)  6.65 us
    unnamed x90, local copies, waits for them, and re-layouts  6 us
    another operation x37, local copies, waits for them, and re-layouts, on_device(): jnp.stack([g[0, rows_dev, :2] for g in heard]).astype(jnp.float32)  4.09 us
  transfers between devices with their start and end apart: 31, of which 13 were waited for; matrix products, arithmetic and copies ran while one was open for 10% of the time, Pallas kernels for 16%

profile of v10, /device:TPU:0, one launch (start us, length us, event | category | flops | bytes accessed | tf_op | source)
XLA Modules:
  0.0 137.7 jit_solution(8794152393635364479)
XLA Ops:
  1.5 1.0 fusion.18
  2.5 1.0 fusion.17
  4.6 3.1 %collective-permute-start.1 = (bf16[10,128,128]{2,1,0:T(8,128)(2,1)S(1)}, bf16[10,128,128]{2,1,0:T(8,128)(2,1)S(1)}, u32[]{:S(2)}, u32[]{:S(2)}) collective-permute-start(bf16[10,128,128]{2,1,0:T(8,128)(2,1)S(1)} %get-tuple-element.52.refs_2_), channel_id=1, source_target_pairs={{0,8},{2,10},{8,16},{10,18},{16,24},{18,26},{24,28},{26,30},{28,20... | collective-permute-start | bytes 983048 | tf_op jit(solution)/shard_map/ppermute | solution.py:37
  7.7 0.5 collective-permute-start.9
  8.8 0.8 copy.75
  9.8 0.8 copy.49
  10.9 4.5 %collective-permute-done.1.refs_4_ = bf16[10,128,128]{2,1,0:T(8,128)(2,1)S(1)} collective-permute-done((bf16[10,128,128]{2,1,0:T(8,128)(2,1)S(1)}, bf16[10,128,128]{2,1,0:T(8,128)(2,1)S(1)}, u32[]{:S(2)}, u32[]{:S(2)}) %collective-permute-start.1) | collective-permute-done | bytes 327712 | tf_op jit(solution)/shard_map/ppermute | solution.py:37
  15.4 1.8 %collective-permute-start.3 = (bf16[10,128,128]{2,1,0:T(8,128)(2,1)S(1)}, bf16[10,128,128]{2,1,0:T(8,128)(2,1)S(1)}, u32[]{:S(2)}, u32[]{:S(2)}) collective-permute-start(bf16[10,128,128]{2,1,0:T(8,128)(2,1)S(1)} %collective-permute-done.1.refs_4_), channel_id=1, source_target_pairs={{0,8},{2,10},{8,16},{10,18},{16,24},{18,26},{24,28},{26,30},{28,20... | collective-permute-start | bytes 983048 | tf_op jit(solution)/shard_map/ppermute | solution.py:37
  17.2 0.7 collective-permute-done.10.refs_4_
  18.6 0.5 collective-permute-start.11
  19.1 5.2 %collective-permute-done.3.refs_6_ = bf16[10,128,128]{2,1,0:T(8,128)(2,1)S(1)} collective-permute-done((bf16[10,128,128]{2,1,0:T(8,128)(2,1)S(1)}, bf16[10,128,128]{2,1,0:T(8,128)(2,1)S(1)}, u32[]{:S(2)}, u32[]{:S(2)}) %collective-permute-start.3) | collective-permute-done | bytes 327712 | tf_op jit(solution)/shard_map/ppermute | solution.py:37
  24.3 1.5 %collective-permute-start.5 = (bf16[10,128,128]{2,1,0:T(8,128)(2,1)S(1)}, bf16[10,128,128]{2,1,0:T(8,128)(2,1)S(1)}, u32[]{:S(2)}, u32[]{:S(2)}) collective-permute-start(bf16[10,128,128]{2,1,0:T(8,128)(2,1)S(1)} %collective-permute-done.3.refs_6_), channel_id=1, source_target_pairs={{0,8},{2,10},{8,16},{10,18},{16,24},{18,26},{24,28},{26,30},{28,20... | collective-permute-start | bytes 983048 | tf_op jit(solution)/shard_map/ppermute | solution.py:37
  25.7 0.9 collective-permute-done.12.refs_6_
  26.6 0.6 collective-permute-start.14
  27.2 0.7 copy-done.21
  28.4 0.5 collective-permute-start.13
  28.9 3.4 %collective-permute-done.5.refs_8_ = bf16[10,128,128]{2,1,0:T(8,128)(2,1)S(1)} collective-permute-done((bf16[10,128,128]{2,1,0:T(8,128)(2,1)S(1)}, bf16[10,128,128]{2,1,0:T(8,128)(2,1)S(1)}, u32[]{:S(2)}, u32[]{:S(2)}) %collective-permute-start.5) | collective-permute-done | bytes 327712 | tf_op jit(solution)/shard_map/ppermute | solution.py:37
  32.2 1.4 collective-permute-start.7
  33.6 0.9 collective-permute-done.14.refs_8_
  34.5 0.9 collective-permute-start.16
  35.4 0.7 copy-done.25
  36.1 0.7 copy-done.27
  37.3 0.5 collective-permute-start.15
  37.8 1.6 %collective-permute-done.7.refs_10_ = bf16[10,128,128]{2,1,0:T(8,128)(2,1)S(1)} collective-permute-done((bf16[10,128,128]{2,1,0:T(8,128)(2,1)S(1)}, bf16[10,128,128]{2,1,0:T(8,128)(2,1)S(1)}, u32[]{:S(2)}, u32[]{:S(2)}) %collective-permute-start.7) | collective-permute-done | bytes 327712 | tf_op jit(solution)/shard_map/ppermute | solution.py:37
  39.3 2.3 %collective-permute-done.16.refs_10_ = bf16[10,128,128]{2,1,0:T(8,128)(2,1)} collective-permute-done((bf16[10,128,128]{2,1,0:T(8,128)(2,1)S(1)}, bf16[10,128,128]{2,1,0:T(8,128)(2,1)}, u32[]{:S(2)}, u32[]{:S(2)}) %collective-permute-start.16) | collective-permute-done | bytes 327712 | tf_op jit(solution)/shard_map/ppermute | solution.py:38
  41.7 0.7 slice_bitcast_fusion.1
  42.4 0.7 copy-done.28
  43.1 0.7 copy-done.29
  44.3 1.6 %collective-permute-start.18 = (bf16[10,128,128]{2,1,0:T(8,128)(2,1)S(1)}, bf16[10,128,128]{2,1,0:T(8,128)(2,1)S(1)}, u32[]{:S(2)}, u32[]{:S(2)}) collective-permute-start(bf16[10,128,128]{2,1,0:T(8,128)(2,1)S(1)} %collective-permute-done.7.refs_10_), channel_id=1, source_target_pairs={{0,8},{2,10},{8,16},{10,18},{16,24},{18,26},{24,28},{26,30},{28,20... | collective-permute-start | bytes 983048 | tf_op jit(solution)/shard_map/ppermute | solution.py:37
  45.8 0.4 collective-permute-start.22
  46.3 0.7 slice_bitcast_fusion.9
  47.1 0.7 slice_bitcast_fusion
  48.5 7.4 %collective-permute-done.22.refs_2_ = bf16[10,128,128]{2,1,0:T(8,128)(2,1)S(1)} collective-permute-done((bf16[10,128,128]{2,1,0:T(8,128)(2,1)}, bf16[10,128,128]{2,1,0:T(8,128)(2,1)S(1)}, u32[]{:S(2)}, u32[]{:S(2)}) %collective-permute-start.22) | collective-permute-done | bytes 327712 | tf_op jit(solution)/shard_map/ppermute | solution.py:38
  56.3 0.7 compare_convert_fusion.2.refs_1_
  57.2 1.6 %collective-permute-start.20 = (bf16[10,128,128]{2,1,0:T(8,128)(2,1)S(1)}, bf16[10,128,128]{2,1,0:T(8,128)(2,1)S(1)}, u32[]{:S(2)}, u32[]{:S(2)}) collective-permute-start(bf16[10,128,128]{2,1,0:T(8,128)(2,1)S(1)} %collective-permute-done.18.refs_2_), channel_id=1, source_target_pairs={{0,8},{2,10},{8,16},{10,18},{16,24},{18,26},{24,28},{26,30},{28,20... | collective-permute-start | bytes 983048 | tf_op jit(solution)/shard_map/ppermute | solution.py:37
  58.8 0.7 compare_convert_fusion.3.refs_1_
  59.5 5.4 %collective-permute-done.24.refs_4_ = bf16[10,128,128]{2,1,0:T(8,128)(2,1)S(1)} collective-permute-done((bf16[10,128,128]{2,1,0:T(8,128)(2,1)S(1)}, bf16[10,128,128]{2,1,0:T(8,128)(2,1)S(1)}, u32[]{:S(2)}, u32[]{:S(2)}) %collective-permute-start.24) | collective-permute-done | bytes 327712 | tf_op jit(solution)/shard_map/ppermute | solution.py:38
  64.9 0.4 collective-permute-start.28
  65.4 0.7 compare_convert_fusion.4.refs_1_
  66.1 0.7 compare_convert_fusion.refs_1_
  66.8 0.5 collective-permute-start.25
  67.4 1.8 %collective-permute-start.26 = (bf16[10,128,128]{2,1,0:T(8,128)(2,1)S(1)}, bf16[10,128,128]{2,1,0:T(8,128)(2,1)S(1)}, u32[]{:S(2)}, u32[]{:S(2)}) collective-permute-start(bf16[10,128,128]{2,1,0:T(8,128)(2,1)S(1)} %collective-permute-done.20.refs_4_), channel_id=1, source_target_pairs={{0,8},{2,10},{8,16},{10,18},{16,24},{18,26},{24,28},{26,30},{28,20... | collective-permute-start | bytes 983048 | tf_op jit(solution)/shard_map/ppermute | solution.py:37
  69.2 3.8 %collective-permute-done.28.refs_2_ = bf16[10,128,128]{2,1,0:T(8,128)(2,1)S(1)} collective-permute-done((bf16[10,128,128]{2,1,0:T(8,128)(2,1)S(1)}, bf16[10,128,128]{2,1,0:T(8,128)(2,1)S(1)}, u32[]{:S(2)}, u32[]{:S(2)}) %collective-permute-start.28) | collective-permute-done | bytes 327712 | tf_op jit(solution)/shard_map/ppermute | solution.py:38
  73.0 0.7 compare_convert_fusion.5.refs_1_
  73.7 0.7 compare_convert_fusion.1.refs_1_
  74.4 0.8 copy-done.14
  75.2 3.9 %shard_map.86 = (f32[5,120,1]{2,1,0:T(8,128)}, f32[5,120,1]{2,1,0:T(8,128)}, f32[5,120,128]{2,1,0:T(8,128)}) custom-call(bf16[5,120,128]{2,1,0:T(8,128)(2,1)} %bitcast.101, f32[4,1,128]{2,1,0:T(1,128)} %compare_convert_fusion.2.refs_1_, bf16[10,128,128]{2,1,0:T(8,128)(2,1)} %copy-done.8, bf16[10,128,128]{2,1,0:T(8,128)(2,1)} %copy-done.12, ...), custom_call_target="tpu_custom_call" | custom-call | tf_op jit(solution)/shard_map/pallas_call | solution.py:106
  79.2 3.9 %shard_map.83 = (f32[5,120,1]{2,1,0:T(8,128)}, f32[5,120,1]{2,1,0:T(8,128)}, f32[5,120,128]{2,1,0:T(8,128)}) custom-call(bf16[5,120,128]{2,1,0:T(8,128)(2,1)} %bitcast.104, f32[4,1,128]{2,1,0:T(1,128)} %compare_convert_fusion.3.refs_1_, bf16[10,128,128]{2,1,0:T(8,128)(2,1)} %copy-done.7, bf16[10,128,128]{2,1,0:T(8,128)(2,1)} %copy-done.11, ...), custom_call_target="tpu_custom_call" | custom-call | tf_op jit(solution)/shard_map/pallas_call | solution.py:106
  83.1 5.5 %shard_map.85 = (f32[5,120,1]{2,1,0:T(8,128)}, f32[5,120,1]{2,1,0:T(8,128)}, f32[5,120,128]{2,1,0:T(8,128)}) custom-call(bf16[5,120,128]{2,1,0:T(8,128)(2,1)} %bitcast.102, f32[10,1,128]{2,1,0:T(1,128)} %compare_convert_fusion.refs_1_, bf16[10,128,128]{2,1,0:T(8,128)(2,1)} %copy-done.1, bf16[10,128,128]{2,1,0:T(8,128)(2,1)} %copy-done.17, ...), custom_call_target="tpu_custom_call" | custom-call | tf_op jit(solution)/shard_map/pallas_call | solution.py:106
  88.6 5.6 %shard_map.82 = (f32[5,120,1]{2,1,0:T(8,128)}, f32[5,120,1]{2,1,0:T(8,128)}, f32[5,120,128]{2,1,0:T(8,128)}) custom-call(bf16[5,120,128]{2,1,0:T(8,128)(2,1)} %bitcast.105, f32[10,1,128]{2,1,0:T(1,128)} %compare_convert_fusion.1.refs_1_, bf16[10,128,128]{2,1,0:T(8,128)(2,1)} %copy-done, bf16[10,128,128]{2,1,0:T(8,128)(2,1)} %copy-done.16, ...), custom_call_target="tpu_custom_call" | custom-call | tf_op jit(solution)/shard_map/pallas_call | solution.py:106
  94.3 0.5 collective-permute-start.27
  94.8 0.7 copy-done.5
  95.5 3.5 %shard_map.87 = (f32[5,120,1]{2,1,0:T(8,128)}, f32[5,120,1]{2,1,0:T(8,128)}, f32[5,120,128]{2,1,0:T(8,128)}) custom-call(bf16[5,120,128]{2,1,0:T(8,128)(2,1)} %bitcast.103, f32[2,1,128]{2,1,0:T(1,128)} %compare_convert_fusion.4.refs_1_, bf16[10,128,128]{2,1,0:T(8,128)(2,1)} %copy-done.4, bf16[10,128,128]{2,1,0:T(8,128)(2,1)} %copy-done.5), custom_call_target="tpu_custom_call" | custom-call | tf_op jit(solution)/shard_map/pallas_call | solution.py:106
  99.0 1.6 %fusion.12 = (f32[5,120]{1,0:T(8,128)S(1)}, f32[5,120]{1,0:T(8,128)S(1)}, f32[5,120]{1,0:T(8,128)S(1)}, f32[5,120]{1,0:T(8,128)S(1)}) fusion(f32[5,120,1]{2,1,0:T(8,128)S(1)} %copy-done.36, f32[5,120,1]{2,1,0:T(8,128)} %get-tuple-element.91, f32[5,120,1]{2,1,0:T(8,128)S(1)} %copy-done.34, f32[5,120,1]{2,1,0:T(8,128)} %get-tuple-element.97, ...), kind=kLoop, calls=%fused_computation.30 | loop fusion | flops 6000 | bytes 24000 | tf_op jit(solution)/shard_map/exp | solution.py:118
  100.7 1.4 %fusion.8 = bf16[120,5,128]{2,0,1:T(8,128)(2,1)S(1)} fusion(f32[5,120]{1,0:T(8,128)S(1)} %get-tuple-element.115, f32[5,120,128]{2,1,0:T(8,128)S(1)} %copy-done.42, f32[5,120]{1,0:T(8,128)S(1)} %get-tuple-element.114, f32[5,120,128]{2,1,0:T(8,128)S(1)} %copy-done.41, f32[5,120]{1,0:T(8,128)S(1)} %get-tuple-element.116, f32[5,120,128]{2,1,0:T(8,128)} %get-tuple-element.92, ...), kind=kLoop, calls=%fused_computation.26 | loop fusion | flops 537600 | bytes 1084800 | tf_op jit(solution)/shard_map/transpose | solution.py:122
  102.3 0.7 copy-done.6
  103.0 3.4 %shard_map.84 = (f32[5,120,1]{2,1,0:T(8,128)}, f32[5,120,1]{2,1,0:T(8,128)}, f32[5,120,128]{2,1,0:T(8,128)}) custom-call(bf16[5,120,128]{2,1,0:T(8,128)(2,1)} %bitcast.106, f32[2,1,128]{2,1,0:T(1,128)} %compare_convert_fusion.5.refs_1_, bf16[10,128,128]{2,1,0:T(8,128)(2,1)} %copy-done.3, bf16[10,128,128]{2,1,0:T(8,128)(2,1)} %copy-done.6), custom_call_target="tpu_custom_call" | custom-call | tf_op jit(solution)/shard_map/pallas_call | solution.py:106
  106.5 1.6 %fusion.9 = (f32[5,120]{1,0:T(8,128)S(1)}, f32[5,120]{1,0:T(8,128)S(1)}, f32[5,120]{1,0:T(8,128)S(1)}, f32[5,120]{1,0:T(8,128)S(1)}) fusion(f32[5,120,1]{2,1,0:T(8,128)S(1)} %copy-done.32, f32[5,120,1]{2,1,0:T(8,128)} %get-tuple-element.68, f32[5,120,1]{2,1,0:T(8,128)S(1)} %copy-done.30, f32[5,120,1]{2,1,0:T(8,128)} %get-tuple-element.74, ...), kind=kLoop, calls=%fused_computation.27 | loop fusion | flops 6000 | bytes 24000 | tf_op jit(solution)/shard_map/exp | solution.py:118
  108.7 6.6 %fusion.3 = f32[120,5120]{1,0:T(8,128)S(1)} fusion(bf16[1280,5120]{1,0:T(8,128)(2,1)} %param.15, bf16[120,640]{0,1:T(8,128)(2,1)S(1)} %bitcast.111, bf16[120,640]{0,1:T(8,128)(2,1)S(1)} %bitcast.112), kind=kOutput, calls=%fused_computation.7 | convolution fusion | flops 1573478400 | bytes 15872000 | tf_op jit(solution)/shard_map/dot_general | solution.py:193
  115.3 1.7 %reshape.266 = f32[2,60,5120]{2,1,0:T(8,128)} reshape(f32[120,5120]{1,0:T(8,128)S(1)} %fusion.3) | data formatting | bytes 4915200 | tf_op jit(solution)/shard_map/reshape | solution.py:197
  117.0 1.5 %bitcast_convert_fusion = bf16[60,5120]{1,0:T(8,128)(2,1)S(1)} fusion(f32[2,60,5120]{2,1,0:T(8,128)} %reshape.266, s32[]{:T(128)S(6)} %select_n.212, pred[]{:T(512)S(6)} %and.124), kind=kLoop, calls=%fused_computation | loop fusion | flops 307200 | bytes 1228805 | tf_op jit(solution)/shard_map/convert_element_type | solution.py:199
  118.5 1.6 %collective-permute-start.30 = (bf16[60,5120]{1,0:T(8,128)(2,1)S(1)}, bf16[60,5120]{1,0:T(8,128)(2,1)S(1)}, u32[]{:S(2)}, u32[]{:S(2)}) collective-permute-start(bf16[60,5120]{1,0:T(8,128)(2,1)S(1)} %bitcast_convert_fusion), channel_id=1, source_target_pairs={{0,1},{1,0},{2,3},{3,2},{4,5},{5,4},{6,7},{7,6},{8,9},{9,8},{10,11... | collective-permute-start | bytes 1843208 | tf_op jit(solution)/shard_map/ppermute | solution.py:200
  120.1 15.2 %collective-permute-done.30 = bf16[60,5120]{1,0:T(8,128)(2,1)S(1)} collective-permute-done((bf16[60,5120]{1,0:T(8,128)(2,1)S(1)}, bf16[60,5120]{1,0:T(8,128)(2,1)S(1)}, u32[]{:S(2)}, u32[]{:S(2)}) %collective-permute-start.30) | collective-permute-done | bytes 614432 | tf_op jit(solution)/shard_map/ppermute | solution.py:200
  135.3 2.4 %fusion.2 = bf16[60,5120]{1,0:T(8,128)(2,1)} fusion(f32[2,60,5120]{2,1,0:T(8,128)} %reshape.266, s32[]{:T(128)S(6)} %select_n.210, bf16[60,5120]{1,0:T(8,128)(2,1)S(1)} %collective-permute-done.30, bf16[60,5120]{1,0:T(8,128)(2,1)S(1)} %copy-done.2, f32[5120]{0:T(1024)S(1)} %copy-done.44, pred[]{:T(512)S(6)} %and.123), kind=kLoop, calls=%fused_computation.4 | loop fusion | flops 2150400 | bytes 3092485 | tf_op jit(solution)/shard_map/convert_element_type | solution.py:202
  (177 shorter events, 6.5 us)
Async XLA Ops:
  4.6 6.0 %copy-start = (bf16[10,128,128]{2,1,0:T(8,128)(2,1)}, bf16[10,128,128]{2,1,0:T(8,128)(2,1)S(1)}, u32[]{:S(2)}) copy-start(bf16[10,128,128]{2,1,0:T(8,128)(2,1)S(1)} %get-tuple-element.52.refs_2_) | copy-start | bytes 983044
  4.6 6.0 %copy-start.1 = (bf16[10,128,128]{2,1,0:T(8,128)(2,1)}, bf16[10,128,128]{2,1,0:T(8,128)(2,1)S(1)}, u32[]{:S(2)}) copy-start(bf16[10,128,128]{2,1,0:T(8,128)(2,1)S(1)} %get-tuple-element.75.refs_2_) | copy-start | bytes 983044
  4.6 10.7 %collective-permute-start.1 = (bf16[10,128,128]{2,1,0:T(8,128)(2,1)S(1)}, bf16[10,128,128]{2,1,0:T(8,128)(2,1)S(1)}, u32[]{:S(2)}, u32[]{:S(2)}) collective-permute-start(bf16[10,128,128]{2,1,0:T(8,128)(2,1)S(1)} %get-tuple-element.52.refs_2_), channel_id=1, source_target_pairs={{0,8},{2,10},{8,16},{10,18},{16,24},{18,26},{24,28},{26,30},{28,20... | collective-permute-start | bytes 983048 | tf_op jit(solution)/shard_map/ppermute | solution.py:37
  7.7 10.4 %collective-permute-start = (bf16[10,128,128]{2,1,0:T(8,128)(2,1)S(1)}, bf16[10,128,128]{2,1,0:T(8,128)(2,1)S(1)}, u32[]{:S(2)}, u32[]{:S(2)}) collective-permute-start(bf16[10,128,128]{2,1,0:T(8,128)(2,1)S(1)} %get-tuple-element.52.refs_2_), channel_id=1, source_target_pairs={{0,2},{2,0},{4,6},{6,4},{8,10},{10,8},{12,14},{14,12},{16,18},{18,... | collective-permute-start | bytes 983048 | tf_op jit(solution)/shard_map/ppermute | solution.py:41
  7.7 10.4 %collective-permute-start.9 = (bf16[10,128,128]{2,1,0:T(8,128)(2,1)S(1)}, bf16[10,128,128]{2,1,0:T(8,128)(2,1)S(1)}, u32[]{:S(2)}, u32[]{:S(2)}) collective-permute-start(bf16[10,128,128]{2,1,0:T(8,128)(2,1)S(1)} %get-tuple-element.75.refs_2_), channel_id=1, source_target_pairs={{0,2},{2,0},{4,6},{6,4},{8,10},{10,8},{12,14},{14,12},{16,18},{18,... | collective-permute-start | bytes 983048 | tf_op jit(solution)/shard_map/ppermute | solution.py:42
  8.2 9.6 %collective-permute-start.10 = (bf16[10,128,128]{2,1,0:T(8,128)(2,1)S(1)}, bf16[10,128,128]{2,1,0:T(8,128)(2,1)S(1)}, u32[]{:S(2)}, u32[]{:S(2)}) collective-permute-start(bf16[10,128,128]{2,1,0:T(8,128)(2,1)S(1)} %get-tuple-element.75.refs_2_), channel_id=1, source_target_pairs={{8,0},{10,2},{16,8},{18,10},{24,16},{26,18},{28,24},{30,26},{20,28... | collective-permute-start | bytes 983048 | tf_op jit(solution)/shard_map/ppermute | solution.py:38
  15.4 28.8 %copy-start.15 = (bf16[10,128,128]{2,1,0:T(8,128)(2,1)}, bf16[10,128,128]{2,1,0:T(8,128)(2,1)S(1)}, u32[]{:S(2)}) copy-start(bf16[10,128,128]{2,1,0:T(8,128)(2,1)S(1)} %collective-permute-done.1.refs_4_) | copy-start | bytes 983044
  15.4 8.9 %collective-permute-start.3 = (bf16[10,128,128]{2,1,0:T(8,128)(2,1)S(1)}, bf16[10,128,128]{2,1,0:T(8,128)(2,1)S(1)}, u32[]{:S(2)}, u32[]{:S(2)}) collective-permute-start(bf16[10,128,128]{2,1,0:T(8,128)(2,1)S(1)} %collective-permute-done.1.refs_4_), channel_id=1, source_target_pairs={{0,8},{2,10},{8,16},{10,18},{16,24},{18,26},{24,28},{26,30},{28,20... | collective-permute-start | bytes 983048 | tf_op jit(solution)/shard_map/ppermute | solution.py:37
  17.8 30.6 %copy-start.18 = (bf16[10,128,128]{2,1,0:T(8,128)(2,1)}, bf16[10,128,128]{2,1,0:T(8,128)(2,1)S(1)}, u32[]{:S(2)}) copy-start(bf16[10,128,128]{2,1,0:T(8,128)(2,1)S(1)} %collective-permute-done.10.refs_4_) | copy-start | bytes 983044
  17.8 8.8 %collective-permute-start.12 = (bf16[10,128,128]{2,1,0:T(8,128)(2,1)S(1)}, bf16[10,128,128]{2,1,0:T(8,128)(2,1)S(1)}, u32[]{:S(2)}, u32[]{:S(2)}) collective-permute-start(bf16[10,128,128]{2,1,0:T(8,128)(2,1)S(1)} %collective-permute-done.10.refs_4_), channel_id=1, source_target_pairs={{8,0},{10,2},{16,8},{18,10},{24,16},{26,18},{28,24},{30,26},{20,28... | collective-permute-start | bytes 983048 | tf_op jit(solution)/shard_map/ppermute | solution.py:38
  18.1 26.0 %copy-start.16 = (bf16[10,128,128]{2,1,0:T(8,128)(2,1)}, bf16[10,128,128]{2,1,0:T(8,128)(2,1)S(1)}, u32[]{:S(2)}) copy-start(bf16[10,128,128]{2,1,0:T(8,128)(2,1)S(1)} %collective-permute-done.refs_3_) | copy-start | bytes 983044
  18.1 26.1 %copy-start.17 = (bf16[10,128,128]{2,1,0:T(8,128)(2,1)}, bf16[10,128,128]{2,1,0:T(8,128)(2,1)S(1)}, u32[]{:S(2)}) copy-start(bf16[10,128,128]{2,1,0:T(8,128)(2,1)S(1)} %collective-permute-done.9.refs_3_) | copy-start | bytes 983044
  18.6 8.6 %collective-permute-start.2 = (bf16[10,128,128]{2,1,0:T(8,128)(2,1)S(1)}, bf16[10,128,128]{2,1,0:T(8,128)(2,1)S(1)}, u32[]{:S(2)}, u32[]{:S(2)}) collective-permute-start(bf16[10,128,128]{2,1,0:T(8,128)(2,1)S(1)} %collective-permute-done.1.refs_4_), channel_id=1, source_target_pairs={{0,2},{2,0},{4,6},{6,4},{8,10},{10,8},{12,14},{14,12},{16,18},{18,... | collective-permute-start | bytes 983048 | tf_op jit(solution)/shard_map/ppermute | solution.py:41
  18.6 8.6 %collective-permute-start.11 = (bf16[10,128,128]{2,1,0:T(8,128)(2,1)S(1)}, bf16[10,128,128]{2,1,0:T(8,128)(2,1)S(1)}, u32[]{:S(2)}, u32[]{:S(2)}) collective-permute-start(bf16[10,128,128]{2,1,0:T(8,128)(2,1)S(1)} %collective-permute-done.10.refs_4_), channel_id=1, source_target_pairs={{0,2},{2,0},{4,6},{6,4},{8,10},{10,8},{12,14},{14,12},{16,18},{18,... | collective-permute-start | bytes 983048 | tf_op jit(solution)/shard_map/ppermute | solution.py:42
  24.3 35.2 %copy-start.19 = (bf16[10,128,128]{2,1,0:T(8,128)(2,1)}, bf16[10,128,128]{2,1,0:T(8,128)(2,1)S(1)}, u32[]{:S(2)}) copy-start(bf16[10,128,128]{2,1,0:T(8,128)(2,1)S(1)} %collective-permute-done.3.refs_6_) | copy-start | bytes 983044
  24.3 8.0 %collective-permute-start.5 = (bf16[10,128,128]{2,1,0:T(8,128)(2,1)S(1)}, bf16[10,128,128]{2,1,0:T(8,128)(2,1)S(1)}, u32[]{:S(2)}, u32[]{:S(2)}) collective-permute-start(bf16[10,128,128]{2,1,0:T(8,128)(2,1)S(1)} %collective-permute-done.3.refs_6_), channel_id=1, source_target_pairs={{0,8},{2,10},{8,16},{10,18},{16,24},{18,26},{24,28},{26,30},{28,20... | collective-permute-start | bytes 983048 | tf_op jit(solution)/shard_map/ppermute | solution.py:37
  26.6 21.9 %copy-start.20 = (bf16[10,128,128]{2,1,0:T(8,128)(2,1)}, bf16[10,128,128]{2,1,0:T(8,128)(2,1)S(1)}, u32[]{:S(2)}) copy-start(bf16[10,128,128]{2,1,0:T(8,128)(2,1)S(1)} %collective-permute-done.12.refs_6_) | copy-start | bytes 983044
  26.6 7.9 %collective-permute-start.14 = (bf16[10,128,128]{2,1,0:T(8,128)(2,1)S(1)}, bf16[10,128,128]{2,1,0:T(8,128)(2,1)S(1)}, u32[]{:S(2)}, u32[]{:S(2)}) collective-permute-start(bf16[10,128,128]{2,1,0:T(8,128)(2,1)S(1)} %collective-permute-done.12.refs_6_), channel_id=1, source_target_pairs={{8,0},{10,2},{16,8},{18,10},{24,16},{26,18},{28,24},{30,26},{20,28... | collective-permute-start | bytes 983048 | tf_op jit(solution)/shard_map/ppermute | solution.py:38
  27.9 31.6 %copy-start.23 = (bf16[10,128,128]{2,1,0:T(8,128)(2,1)}, bf16[10,128,128]{2,1,0:T(8,128)(2,1)S(1)}, u32[]{:S(2)}) copy-start(bf16[10,128,128]{2,1,0:T(8,128)(2,1)S(1)} %collective-permute-done.11.refs_5_) | copy-start | bytes 983044
  28.3 7.0 %collective-permute-start.4 = (bf16[10,128,128]{2,1,0:T(8,128)(2,1)S(1)}, bf16[10,128,128]{2,1,0:T(8,128)(2,1)S(1)}, u32[]{:S(2)}, u32[]{:S(2)}) collective-permute-start(bf16[10,128,128]{2,1,0:T(8,128)(2,1)S(1)} %collective-permute-done.3.refs_6_), channel_id=1, source_target_pairs={{0,2},{2,0},{4,6},{6,4},{8,10},{10,8},{12,14},{14,12},{16,18},{18,... | collective-permute-start | bytes 983048 | tf_op jit(solution)/shard_map/ppermute | solution.py:41
  28.4 7.0 %collective-permute-start.13 = (bf16[10,128,128]{2,1,0:T(8,128)(2,1)S(1)}, bf16[10,128,128]{2,1,0:T(8,128)(2,1)S(1)}, u32[]{:S(2)}, u32[]{:S(2)}) collective-permute-start(bf16[10,128,128]{2,1,0:T(8,128)(2,1)S(1)} %collective-permute-done.12.refs_6_), channel_id=1, source_target_pairs={{0,2},{2,0},{4,6},{6,4},{8,10},{10,8},{12,14},{14,12},{16,18},{18,... | collective-permute-start | bytes 983048 | tf_op jit(solution)/shard_map/ppermute | solution.py:42
  32.2 35.1 %copy-start.22 = (bf16[10,128,128]{2,1,0:T(8,128)(2,1)}, bf16[10,128,128]{2,1,0:T(8,128)(2,1)S(1)}, u32[]{:S(2)}) copy-start(bf16[10,128,128]{2,1,0:T(8,128)(2,1)S(1)} %collective-permute-done.5.refs_8_) | copy-start | bytes 983044
  32.2 7.1 %collective-permute-start.7 = (bf16[10,128,128]{2,1,0:T(8,128)(2,1)S(1)}, bf16[10,128,128]{2,1,0:T(8,128)(2,1)S(1)}, u32[]{:S(2)}, u32[]{:S(2)}) collective-permute-start(bf16[10,128,128]{2,1,0:T(8,128)(2,1)S(1)} %collective-permute-done.5.refs_8_), channel_id=1, source_target_pairs={{0,8},{2,10},{8,16},{10,18},{16,24},{18,26},{24,28},{26,30},{28,20... | collective-permute-start | bytes 983048 | tf_op jit(solution)/shard_map/ppermute | solution.py:37
  34.5 22.7 %copy-start.24 = (bf16[10,128,128]{2,1,0:T(8,128)(2,1)}, bf16[10,128,128]{2,1,0:T(8,128)(2,1)S(1)}, u32[]{:S(2)}) copy-start(bf16[10,128,128]{2,1,0:T(8,128)(2,1)S(1)} %collective-permute-done.14.refs_8_) | copy-start | bytes 983044
  34.5 7.2 %collective-permute-start.16 = (bf16[10,128,128]{2,1,0:T(8,128)(2,1)S(1)}, bf16[10,128,128]{2,1,0:T(8,128)(2,1)}, u32[]{:S(2)}, u32[]{:S(2)}) collective-permute-start(bf16[10,128,128]{2,1,0:T(8,128)(2,1)S(1)} %collective-permute-done.14.refs_8_), channel_id=1, source_target_pairs={{8,0},{10,2},{16,8},{18,10},{24,16},{26,18},{28,24},{30,26},{20,28... | collective-permute-start | bytes 983048 | tf_op jit(solution)/shard_map/ppermute | solution.py:38
  37.2 5.1 %collective-permute-start.6 = (bf16[10,128,128]{2,1,0:T(8,128)(2,1)S(1)}, bf16[10,128,128]{2,1,0:T(8,128)(2,1)S(1)}, u32[]{:S(2)}, u32[]{:S(2)}) collective-permute-start(bf16[10,128,128]{2,1,0:T(8,128)(2,1)S(1)} %collective-permute-done.5.refs_8_), channel_id=1, source_target_pairs={{0,2},{2,0},{4,6},{6,4},{8,10},{10,8},{12,14},{14,12},{16,18},{18,... | collective-permute-start | bytes 983048 | tf_op jit(solution)/shard_map/ppermute | solution.py:41
  37.3 5.1 %collective-permute-start.15 = (bf16[10,128,128]{2,1,0:T(8,128)(2,1)S(1)}, bf16[10,128,128]{2,1,0:T(8,128)(2,1)S(1)}, u32[]{:S(2)}, u32[]{:S(2)}) collective-permute-start(bf16[10,128,128]{2,1,0:T(8,128)(2,1)S(1)} %collective-permute-done.14.refs_8_), channel_id=1, source_target_pairs={{0,2},{2,0},{4,6},{6,4},{8,10},{10,8},{12,14},{14,12},{16,18},{18,... | collective-permute-start | bytes 983048 | tf_op jit(solution)/shard_map/ppermute | solution.py:42
  39.3 26.7 %copy-start.26 = (bf16[10,128,128]{2,1,0:T(8,128)(2,1)}, bf16[10,128,128]{2,1,0:T(8,128)(2,1)S(1)}, u32[]{:S(2)}) copy-start(bf16[10,128,128]{2,1,0:T(8,128)(2,1)S(1)} %collective-permute-done.7.refs_10_) | copy-start | bytes 983044
  39.3 7.0 %collective-permute-start.8 = (bf16[10,128,128]{2,1,0:T(8,128)(2,1)S(1)}, bf16[10,128,128]{2,1,0:T(8,128)(2,1)}, u32[]{:S(2)}, u32[]{:S(2)}) collective-permute-start(bf16[10,128,128]{2,1,0:T(8,128)(2,1)S(1)} %collective-permute-done.7.refs_10_), channel_id=1, source_target_pairs={{0,2},{2,0},{4,6},{6,4},{8,10},{10,8},{12,14},{14,12},{16,18},{18,... | collective-permute-start | bytes 983048 | tf_op jit(solution)/shard_map/ppermute | solution.py:41
  42.3 4.7 %collective-permute-start.17 = (bf16[10,128,128]{2,1,0:T(8,128)(2,1)}, bf16[10,128,128]{2,1,0:T(8,128)(2,1)}, u32[]{:S(2)}, u32[]{:S(2)}) collective-permute-start(bf16[10,128,128]{2,1,0:T(8,128)(2,1)} %collective-permute-done.16.refs_10_), channel_id=1, source_target_pairs={{0,2},{2,0},{4,6},{6,4},{8,10},{10,8},{12,14},{14,12},{16,18},{18,... | collective-permute-start | bytes 983048 | tf_op jit(solution)/shard_map/ppermute | solution.py:42
  44.3 12.9 %collective-permute-start.18 = (bf16[10,128,128]{2,1,0:T(8,128)(2,1)S(1)}, bf16[10,128,128]{2,1,0:T(8,128)(2,1)S(1)}, u32[]{:S(2)}, u32[]{:S(2)}) collective-permute-start(bf16[10,128,128]{2,1,0:T(8,128)(2,1)S(1)} %collective-permute-done.7.refs_10_), channel_id=1, source_target_pairs={{0,8},{2,10},{8,16},{10,18},{16,24},{18,26},{24,28},{26,30},{28,20... | collective-permute-start | bytes 983048 | tf_op jit(solution)/shard_map/ppermute | solution.py:37
  45.8 10.1 %collective-permute-start.22 = (bf16[10,128,128]{2,1,0:T(8,128)(2,1)}, bf16[10,128,128]{2,1,0:T(8,128)(2,1)S(1)}, u32[]{:S(2)}, u32[]{:S(2)}) collective-permute-start(bf16[10,128,128]{2,1,0:T(8,128)(2,1)} %collective-permute-done.16.refs_10_), channel_id=1, source_target_pairs={{8,0},{10,2},{16,8},{18,10},{24,16},{26,18},{28,24},{30,26},{20,28... | collective-permute-start | bytes 983048 | tf_op jit(solution)/shard_map/ppermute | solution.py:38
  55.9 19.3 %copy-start.8 = (bf16[10,128,128]{2,1,0:T(8,128)(2,1)}, bf16[10,128,128]{2,1,0:T(8,128)(2,1)S(1)}, u32[]{:S(2)}) copy-start(bf16[10,128,128]{2,1,0:T(8,128)(2,1)S(1)} %collective-permute-done.22.refs_2_) | copy-start | bytes 983044
  55.9 9.0 %collective-permute-start.24 = (bf16[10,128,128]{2,1,0:T(8,128)(2,1)S(1)}, bf16[10,128,128]{2,1,0:T(8,128)(2,1)S(1)}, u32[]{:S(2)}, u32[]{:S(2)}) collective-permute-start(bf16[10,128,128]{2,1,0:T(8,128)(2,1)S(1)} %collective-permute-done.22.refs_2_), channel_id=1, source_target_pairs={{8,0},{10,2},{16,8},{18,10},{24,16},{26,18},{28,24},{30,26},{20,28... | collective-permute-start | bytes 983048 | tf_op jit(solution)/shard_map/ppermute | solution.py:38
  57.2 22.0 %copy-start.7 = (bf16[10,128,128]{2,1,0:T(8,128)(2,1)}, bf16[10,128,128]{2,1,0:T(8,128)(2,1)S(1)}, u32[]{:S(2)}) copy-start(bf16[10,128,128]{2,1,0:T(8,128)(2,1)S(1)} %collective-permute-done.18.refs_2_) | copy-start | bytes 983044
  57.2 10.2 %collective-permute-start.19 = (bf16[10,128,128]{2,1,0:T(8,128)(2,1)S(1)}, bf16[10,128,128]{2,1,0:T(8,128)(2,1)S(1)}, u32[]{:S(2)}, u32[]{:S(2)}) collective-permute-start(bf16[10,128,128]{2,1,0:T(8,128)(2,1)S(1)} %collective-permute-done.18.refs_2_), channel_id=1, source_target_pairs={{0,2},{2,0},{4,6},{6,4},{8,10},{10,8},{12,14},{14,12},{16,18},{18,... | collective-permute-start | bytes 983048 | tf_op jit(solution)/shard_map/ppermute | solution.py:41
  57.2 10.1 %collective-permute-start.20 = (bf16[10,128,128]{2,1,0:T(8,128)(2,1)S(1)}, bf16[10,128,128]{2,1,0:T(8,128)(2,1)S(1)}, u32[]{:S(2)}, u32[]{:S(2)}) collective-permute-start(bf16[10,128,128]{2,1,0:T(8,128)(2,1)S(1)} %collective-permute-done.18.refs_2_), channel_id=1, source_target_pairs={{0,8},{2,10},{8,16},{10,18},{16,24},{18,26},{24,28},{26,30},{28,20... | collective-permute-start | bytes 983048 | tf_op jit(solution)/shard_map/ppermute | solution.py:37
  64.9 10.3 %copy-start.10 = (bf16[10,128,128]{2,1,0:T(8,128)(2,1)}, bf16[10,128,128]{2,1,0:T(8,128)(2,1)S(1)}, u32[]{:S(2)}) copy-start(bf16[10,128,128]{2,1,0:T(8,128)(2,1)S(1)} %collective-permute-done.24.refs_4_) | copy-start | bytes 983044
  64.9 8.1 %collective-permute-start.28 = (bf16[10,128,128]{2,1,0:T(8,128)(2,1)S(1)}, bf16[10,128,128]{2,1,0:T(8,128)(2,1)S(1)}, u32[]{:S(2)}, u32[]{:S(2)}) collective-permute-start(bf16[10,128,128]{2,1,0:T(8,128)(2,1)S(1)} %collective-permute-done.24.refs_4_), channel_id=1, source_target_pairs={{8,0},{10,2},{16,8},{18,10},{24,16},{26,18},{28,24},{30,26},{20,28... | collective-permute-start | bytes 983048 | tf_op jit(solution)/shard_map/ppermute | solution.py:38
  66.1 8.3 %collective-permute-start.23 = (bf16[10,128,128]{2,1,0:T(8,128)(2,1)S(1)}, bf16[10,128,128]{2,1,0:T(8,128)(2,1)S(1)}, u32[]{:S(2)}, u32[]{:S(2)}) collective-permute-start(bf16[10,128,128]{2,1,0:T(8,128)(2,1)S(1)} %collective-permute-done.22.refs_2_), channel_id=1, source_target_pairs={{0,2},{2,0},{4,6},{6,4},{8,10},{10,8},{12,14},{14,12},{16,18},{18,... | collective-permute-start | bytes 983048 | tf_op jit(solution)/shard_map/ppermute | solution.py:42
  66.8 7.7 %collective-permute-start.25 = (bf16[10,128,128]{2,1,0:T(8,128)(2,1)S(1)}, bf16[10,128,128]{2,1,0:T(8,128)(2,1)S(1)}, u32[]{:S(2)}, u32[]{:S(2)}) collective-permute-start(bf16[10,128,128]{2,1,0:T(8,128)(2,1)S(1)} %collective-permute-done.24.refs_4_), channel_id=1, source_target_pairs={{0,2},{2,0},{4,6},{6,4},{8,10},{10,8},{12,14},{14,12},{16,18},{18,... | collective-permute-start | bytes 983048 | tf_op jit(solution)/shard_map/ppermute | solution.py:42
  67.3 11.8 %copy-start.9 = (bf16[10,128,128]{2,1,0:T(8,128)(2,1)}, bf16[10,128,128]{2,1,0:T(8,128)(2,1)S(1)}, u32[]{:S(2)}) copy-start(bf16[10,128,128]{2,1,0:T(8,128)(2,1)S(1)} %collective-permute-done.20.refs_4_) | copy-start | bytes 983044
  67.3 7.1 %collective-permute-start.21 = (bf16[10,128,128]{2,1,0:T(8,128)(2,1)S(1)}, bf16[10,128,128]{2,1,0:T(8,128)(2,1)S(1)}, u32[]{:S(2)}, u32[]{:S(2)}) collective-permute-start(bf16[10,128,128]{2,1,0:T(8,128)(2,1)S(1)} %collective-permute-done.20.refs_4_), channel_id=1, source_target_pairs={{0,2},{2,0},{4,6},{6,4},{8,10},{10,8},{12,14},{14,12},{16,18},{18,... | collective-permute-start | bytes 983048 | tf_op jit(solution)/shard_map/ppermute | solution.py:41
  67.4 11.8 %copy-start.11 = (bf16[10,128,128]{2,1,0:T(8,128)(2,1)}, bf16[10,128,128]{2,1,0:T(8,128)(2,1)S(1)}, u32[]{:S(2)}) copy-start(bf16[10,128,128]{2,1,0:T(8,128)(2,1)S(1)} %collective-permute-done.19.refs_3_) | copy-start | bytes 983044
  67.4 26.9 %collective-permute-start.26 = (bf16[10,128,128]{2,1,0:T(8,128)(2,1)S(1)}, bf16[10,128,128]{2,1,0:T(8,128)(2,1)S(1)}, u32[]{:S(2)}, u32[]{:S(2)}) collective-permute-start(bf16[10,128,128]{2,1,0:T(8,128)(2,1)S(1)} %collective-permute-done.20.refs_4_), channel_id=1, source_target_pairs={{0,8},{2,10},{8,16},{10,18},{16,24},{18,26},{24,28},{26,30},{28,20... | collective-permute-start | bytes 983048 | tf_op jit(solution)/shard_map/ppermute | solution.py:37
  73.0 10.1 %copy-start.4 = (bf16[10,128,128]{2,1,0:T(8,128)(2,1)}, bf16[10,128,128]{2,1,0:T(8,128)(2,1)S(1)}, u32[]{:S(2)}) copy-start(bf16[10,128,128]{2,1,0:T(8,128)(2,1)S(1)} %collective-permute-done.28.refs_2_) | copy-start | bytes 983044
  73.0 21.8 %collective-permute-start.29 = (bf16[10,128,128]{2,1,0:T(8,128)(2,1)S(1)}, bf16[10,128,128]{2,1,0:T(8,128)(2,1)S(1)}, u32[]{:S(2)}, u32[]{:S(2)}) collective-permute-start(bf16[10,128,128]{2,1,0:T(8,128)(2,1)S(1)} %collective-permute-done.28.refs_2_), channel_id=1, source_target_pairs={{0,2},{2,0},{4,6},{6,4},{8,10},{10,8},{12,14},{14,12},{16,18},{18,... | collective-permute-start | bytes 983048 | tf_op jit(solution)/shard_map/ppermute | solution.py:42
  74.4 4.7 %copy-start.13 = (bf16[10,128,128]{2,1,0:T(8,128)(2,1)}, bf16[10,128,128]{2,1,0:T(8,128)(2,1)S(1)}, u32[]{:S(2)}) copy-start(bf16[10,128,128]{2,1,0:T(8,128)(2,1)S(1)} %collective-permute-done.21.refs_5_) | copy-start | bytes 983044
  88.6 10.4 %copy-start.34 = (f32[5,120,1]{2,1,0:T(8,128)S(1)}, f32[5,120,1]{2,1,0:T(8,128)}, u32[]{:S(2)}) copy-start(f32[5,120,1]{2,1,0:T(8,128)} %get-tuple-element.90) | copy-start | bytes 7204
  88.6 10.4 %copy-start.35 = (f32[5,120,1]{2,1,0:T(8,128)S(1)}, f32[5,120,1]{2,1,0:T(8,128)}, u32[]{:S(2)}) copy-start(f32[5,120,1]{2,1,0:T(8,128)} %get-tuple-element.96) | copy-start | bytes 7204
  88.6 10.4 %copy-start.36 = (f32[5,120,1]{2,1,0:T(8,128)S(1)}, f32[5,120,1]{2,1,0:T(8,128)}, u32[]{:S(2)}) copy-start(f32[5,120,1]{2,1,0:T(8,128)} %get-tuple-element.85) | copy-start | bytes 7204
  88.6 10.4 %copy-start.37 = (f32[5,120,1]{2,1,0:T(8,128)S(1)}, f32[5,120,1]{2,1,0:T(8,128)}, u32[]{:S(2)}) copy-start(f32[5,120,1]{2,1,0:T(8,128)} %get-tuple-element.95) | copy-start | bytes 7204
  94.2 6.4 %copy-start.41 = (f32[5,120,128]{2,1,0:T(8,128)S(1)}, f32[5,120,128]{2,1,0:T(8,128)}, u32[]{:S(2)}) copy-start(f32[5,120,128]{2,1,0:T(8,128)} %get-tuple-element.93) | copy-start | bytes 921604
  94.3 6.3 %copy-start.3 = (bf16[10,128,128]{2,1,0:T(8,128)(2,1)}, bf16[10,128,128]{2,1,0:T(8,128)(2,1)S(1)}, u32[]{:S(2)}) copy-start(bf16[10,128,128]{2,1,0:T(8,128)(2,1)S(1)} %collective-permute-done.26.refs_2_) | copy-start | bytes 983044
  94.3 8.0 %collective-permute-start.27 = (bf16[10,128,128]{2,1,0:T(8,128)(2,1)S(1)}, bf16[10,128,128]{2,1,0:T(8,128)(2,1)S(1)}, u32[]{:S(2)}, u32[]{:S(2)}) collective-permute-start(bf16[10,128,128]{2,1,0:T(8,128)(2,1)S(1)} %collective-permute-done.26.refs_2_), channel_id=1, source_target_pairs={{0,2},{2,0},{4,6},{6,4},{8,10},{10,8},{12,14},{14,12},{16,18},{18,... | collective-permute-start | bytes 983048 | tf_op jit(solution)/shard_map/ppermute | solution.py:41
  100.6 5.9 %copy-start.30 = (f32[5,120,1]{2,1,0:T(8,128)S(1)}, f32[5,120,1]{2,1,0:T(8,128)}, u32[]{:S(2)}) copy-start(f32[5,120,1]{2,1,0:T(8,128)} %get-tuple-element.67) | copy-start | bytes 7204
  100.6 5.9 %copy-start.31 = (f32[5,120,1]{2,1,0:T(8,128)S(1)}, f32[5,120,1]{2,1,0:T(8,128)}, u32[]{:S(2)}) copy-start(f32[5,120,1]{2,1,0:T(8,128)} %get-tuple-element.73) | copy-start | bytes 7204
  100.6 5.9 %copy-start.32 = (f32[5,120,1]{2,1,0:T(8,128)S(1)}, f32[5,120,1]{2,1,0:T(8,128)}, u32[]{:S(2)}) copy-start(f32[5,120,1]{2,1,0:T(8,128)} %get-tuple-element.62) | copy-start | bytes 7204
  100.6 5.9 %copy-start.33 = (f32[5,120,1]{2,1,0:T(8,128)S(1)}, f32[5,120,1]{2,1,0:T(8,128)}, u32[]{:S(2)}) copy-start(f32[5,120,1]{2,1,0:T(8,128)} %get-tuple-element.72) | copy-start | bytes 7204
  102.3 5.8 %copy-start.39 = (f32[5,120,128]{2,1,0:T(8,128)S(1)}, f32[5,120,128]{2,1,0:T(8,128)}, u32[]{:S(2)}) copy-start(f32[5,120,128]{2,1,0:T(8,128)} %get-tuple-element.70) | copy-start | bytes 921604
  102.3 5.8 %copy-start.40 = (f32[5,120,128]{2,1,0:T(8,128)S(1)}, f32[5,120,128]{2,1,0:T(8,128)}, u32[]{:S(2)}) copy-start(f32[5,120,128]{2,1,0:T(8,128)} %get-tuple-element.69) | copy-start | bytes 921604
  117.0 18.2 %copy-start.2 = (bf16[60,5120]{1,0:T(8,128)(2,1)S(1)}, bf16[60,5120]{1,0:T(8,128)(2,1)}, u32[]{:S(2)}) copy-start(bf16[60,5120]{1,0:T(8,128)(2,1)} %param.10) | copy-start | bytes 1843204
  117.0 18.2 %copy-start.44 = (f32[5120]{0:T(1024)S(1)}, f32[5120]{0:T(1024)}, u32[]{:S(2)}) copy-start(f32[5120]{0:T(1024)} %param.14) | copy-start | bytes 61444
  118.5 16.8 %collective-permute-start.30 = (bf16[60,5120]{1,0:T(8,128)(2,1)S(1)}, bf16[60,5120]{1,0:T(8,128)(2,1)S(1)}, u32[]{:S(2)}, u32[]{:S(2)}) collective-permute-start(bf16[60,5120]{1,0:T(8,128)(2,1)S(1)} %bitcast_convert_fusion), channel_id=1, source_target_pairs={{0,1},{1,0},{2,3},{3,2},{4,5},{5,4},{6,7},{7,6},{8,9},{9,8},{10,11... | collective-permute-start | bytes 1843208 | tf_op jit(solution)/shard_map/ppermute | solution.py:200
  (12 other events, 14.2 us)

commit v11 on v9

--- a/solution.py
+++ b/solution.py
@@ -134,8 +134,14 @@
         got_a = list(held_a) + got_a[early:]
         got_b = list(held_b) + got_b[early:]
 
-        def half(got, limits, lo, hi):
-            q3 = queries[:, lo * HEAD : hi * HEAD].reshape(rows_dev, hi - lo, HEAD).transpose(1, 0, 2)
+        rows_out = hidden.shape[0]
+        side = lax.axis_index("tp")
+        n_tp = rows_dev // rows_out
+
+        def half(got, limits, lo, hi, which):
+            q3 = queries.reshape(n_tp, rows_out, queries.shape[1])
+            q3 = jnp.take(q3, which, axis=0)[:, lo * HEAD : hi * HEAD]
+            q3 = q3.reshape(rows_out, hi - lo, HEAD).transpose(1, 0, 2)
             parts = []
             for first, last in phases:
                 stack = jnp.concatenate(got[first:last], axis=1)
@@ -143,19 +149,19 @@
                 values = stack[hi - lo :]
                 keeping = (within[None, :] < limits[first:last, None]).reshape(-1)
                 parts.append(attend_part(q3, keys, values, keeping, scale_factor))
-            return combine(parts, rows_dev)
+            return combine(parts, rows_out)
 
-        attention = jnp.concatenate(
-            [half(got_a, limit_a, 0, heads_a), half(got_b, limit_b, heads_a, heads_here)], axis=1
-        )
-        partial = jnp.dot(attention, out_weight, preferred_element_type=jnp.float32)
-        rows_out = hidden.shape[0]
-        side = lax.axis_index("tp")
-        n_tp = rows_dev // rows_out
-        pieces = partial.reshape(n_tp, rows_out, partial.shape[1])
-        own = jnp.take(pieces, side, axis=0)
-        other = jnp.take(pieces, 1 - side, axis=0).astype(jnp.bfloat16)
+        def attention_rows(which):
+            return jnp.concatenate(
+                [half(got_a, limit_a, 0, heads_a, which), half(got_b, limit_b, heads_a, heads_here, which)],
+                axis=1,
+            )
+
+        other = jnp.dot(attention_rows(1 - side), out_weight, preferred_element_type=jnp.float32)
+        other = other.astype(jnp.bfloat16)
         came = lax.ppermute(other, "tp", [(0, 1), (1, 0)])
+        attention_own = attention_rows(side)
+        own = jnp.dot(attention_own, out_weight, preferred_element_type=jnp.float32)
         summed = own + came.astype(jnp.float32)
         return (hidden.astype(jnp.float32) + gate_scale * summed).astype(jnp.bfloat16)
 

time: 130 us -> 116 us (0.89)
  local copies, waits for them, and re-layouts: 33.8 us -> 24.2 us
  other arithmetic: 7.63 us -> 4.04 us
  waiting for transfers between devices: 49.6 us -> 48.3 us
    unnamed x98 -> x68, local copies, waits for them, and re-layouts: 15.9 us -> 11.5 us
    convert_element_type x2 -> x0, other arithmetic: 3.83 us -> none  [the longest x1 2.43 us: on_device(): (hidden.astype(jnp.float32) + gate_scale * summed).astype(jnp.bfloat16)]
    reshape x3 -> x5, local copies, waits for them, and re-layouts: 2.72 us -> 0.48 us  [the longest x4 0.42 us: half(): q3 = q3.reshape(rows_out, hi - lo, HEAD).transpose(1, 0, 2)]
    dot_general x6 -> x12, matrix products: 3.94 us -> 6.1 us  [attend_part(): jnp.einsum('hqd,hkd->hqk', queries_3d, keys, preferred_element_type=jnp.f...]
    ppermute x1, waiting for transfers between devices: 15.4 us -> 13.3 us  [on_device(): came = lax.ppermute(other, 'tp', [(0, 1), (1, 0)])]
    ppermute x7, waiting for transfers between devices: 26.6 us -> 28.6 us  [gather_ring(): cur_a = lax.ppermute(cur_a, 'seq', forward)]
    concatenate x6, local copies, waits for them, and re-layouts: 3.93 us -> 2.22 us  [half(): stack = jnp.concatenate(got[first:last], axis=1)]
    dot_general x6 -> x12, matrix products: 6.14 us -> 4.48 us  [attend_part(): jnp.einsum('hqk,hkd->hqd', weights.astype(jnp.bfloat16), values, preferre...]
where the time goes in v11:
time: 116 us; the launch traced here: 115 us
  waiting for transfers between devices  48.3 us (42%)
  local copies, waits for them, and re-layouts  24.2 us (21%)
  starting transfers between devices  19.6 us (17%)
  matrix products  16.4 us (14%)
  other arithmetic  4.04 us (3%)
  between operations  2.71 us (2%)
    ppermute x7, waiting for transfers between devices, gather_ring(): cur_a = lax.ppermute(cur_a, 'seq', forward)  28.6 us
    ppermute x1, waiting for transfers between devices, on_device(): came = lax.ppermute(other, 'tp', [(0, 1), (1, 0)])  13.3 us
    ppermute x7, starting transfers between devices, gather_ring(): cur_a = lax.ppermute(cur_a, 'seq', forward)  12.2 us
    unnamed x68, local copies, waits for them, and re-layouts  11.5 us
    ppermute x7, waiting for transfers between devices, gather_ring(): cur_b = lax.ppermute(cur_b, 'seq', backward)  6.32 us
    another operation x37, local copies, waits for them, and re-layouts, on_device(): jnp.stack([g[0, rows_dev, :2] for g in heard]).astype(jnp.float32)  6.16 us
    dot_general x12, matrix products, attend_part(): jnp.einsum('hqd,hkd->hqk', queries_3d, keys, preferred_element_type=jnp.f...  6.1 us
    dot_general x12, matrix products, attend_part(): jnp.einsum('hqk,hkd->hqd', weights.astype(jnp.bfloat16), values, preferre...  4.48 us
  transfers between devices with their start and end apart: 31, of which 12 were waited for; matrix products, arithmetic and copies ran while one was open for 23% of the time, Pallas kernels for 0%

profile of v11, /device:TPU:0, one launch (start us, length us, event | category | flops | bytes accessed | tf_op | source)
XLA Modules:
  0.0 115.1 jit_solution(7269398215800438733)
XLA Ops:
  0.0 1.0 fusion.251
  1.0 1.0 fusion.252
  4.6 3.1 %collective-permute-start.1 = (bf16[10,128,128]{2,1,0:T(8,128)(2,1)S(1)}, bf16[10,128,128]{2,1,0:T(8,128)(2,1)S(1)}, u32[]{:S(2)}, u32[]{:S(2)}) collective-permute-start(bf16[10,128,128]{2,1,0:T(8,128)(2,1)S(1)} %get-tuple-element.34), channel_id=1, source_target_pairs={{0,8},{2,10},{8,16},{10,18},{16,24},{18,26},{24,28},{26,30},{28,20... | collective-permute-start | bytes 983048 | tf_op jit(solution)/shard_map/ppermute | solution.py:36
  9.7 5.7 %collective-permute-done.1 = bf16[10,128,128]{2,1,0:T(8,128)(2,1)S(1)} collective-permute-done((bf16[10,128,128]{2,1,0:T(8,128)(2,1)S(1)}, bf16[10,128,128]{2,1,0:T(8,128)(2,1)S(1)}, u32[]{:S(2)}, u32[]{:S(2)}) %collective-permute-start.1) | collective-permute-done | bytes 327712 | tf_op jit(solution)/shard_map/ppermute | solution.py:36
  15.3 1.8 %collective-permute-start.3 = (bf16[10,128,128]{2,1,0:T(8,128)(2,1)S(1)}, bf16[10,128,128]{2,1,0:T(8,128)(2,1)}, u32[]{:S(2)}, u32[]{:S(2)}) collective-permute-start(bf16[10,128,128]{2,1,0:T(8,128)(2,1)S(1)} %collective-permute-done.1), channel_id=1, source_target_pairs={{0,8},{2,10},{8,16},{10,18},{16,24},{18,26},{24,28},{26,30},{28,20... | collective-permute-start | bytes 983048 | tf_op jit(solution)/shard_map/ppermute | solution.py:36
  17.1 0.7 collective-permute-done.10
  18.6 0.5 collective-permute-start.2
  19.1 5.3 %collective-permute-done.3 = bf16[10,128,128]{2,1,0:T(8,128)(2,1)} collective-permute-done((bf16[10,128,128]{2,1,0:T(8,128)(2,1)S(1)}, bf16[10,128,128]{2,1,0:T(8,128)(2,1)}, u32[]{:S(2)}, u32[]{:S(2)}) %collective-permute-start.3) | collective-permute-done | bytes 327712 | tf_op jit(solution)/shard_map/ppermute | solution.py:36
  24.3 1.5 %collective-permute-start.5 = (bf16[10,128,128]{2,1,0:T(8,128)(2,1)}, bf16[10,128,128]{2,1,0:T(8,128)(2,1)}, u32[]{:S(2)}, u32[]{:S(2)}) collective-permute-start(bf16[10,128,128]{2,1,0:T(8,128)(2,1)} %collective-permute-done.3), channel_id=1, source_target_pairs={{0,8},{2,10},{8,16},{10,18},{16,24},{18,26},{24,28},{26,30},{28,20... | collective-permute-start | bytes 983048 | tf_op jit(solution)/shard_map/ppermute | solution.py:36
  25.8 0.7 slice_bitcast_fusion.14
  26.5 0.6 collective-permute-done.12
  27.6 0.7 copy-done.5
  28.7 0.5 collective-permute-start.4
  29.2 3.4 %collective-permute-done.5 = bf16[10,128,128]{2,1,0:T(8,128)(2,1)} collective-permute-done((bf16[10,128,128]{2,1,0:T(8,128)(2,1)}, bf16[10,128,128]{2,1,0:T(8,128)(2,1)}, u32[]{:S(2)}, u32[]{:S(2)}) %collective-permute-start.5) | collective-permute-done | bytes 327712 | tf_op jit(solution)/shard_map/ppermute | solution.py:36
  32.6 1.2 %collective-permute-start.7 = (bf16[10,128,128]{2,1,0:T(8,128)(2,1)}, bf16[10,128,128]{2,1,0:T(8,128)(2,1)}, u32[]{:S(2)}, u32[]{:S(2)}) collective-permute-start(bf16[10,128,128]{2,1,0:T(8,128)(2,1)} %collective-permute-done.5), channel_id=1, source_target_pairs={{0,8},{2,10},{8,16},{10,18},{16,24},{18,26},{24,28},{26,30},{28,20... | collective-permute-start | bytes 983048 | tf_op jit(solution)/shard_map/ppermute | solution.py:36
  33.8 0.7 slice_bitcast_fusion.12
  34.5 1.1 collective-permute-done.14
  35.6 0.5 collective-permute-start.16
  36.2 0.7 copy-done.7
  36.9 0.7 copy-done.1
  38.0 0.5 collective-permute-start.6
  38.5 1.5 %collective-permute-done.7 = bf16[10,128,128]{2,1,0:T(8,128)(2,1)} collective-permute-done((bf16[10,128,128]{2,1,0:T(8,128)(2,1)}, bf16[10,128,128]{2,1,0:T(8,128)(2,1)}, u32[]{:S(2)}, u32[]{:S(2)}) %collective-permute-start.7) | collective-permute-done | bytes 327712 | tf_op jit(solution)/shard_map/ppermute | solution.py:36
  40.0 0.7 slice_bitcast_fusion.10
  40.7 2.5 %collective-permute-done.16 = bf16[10,128,128]{2,1,0:T(8,128)(2,1)} collective-permute-done((bf16[10,128,128]{2,1,0:T(8,128)(2,1)S(1)}, bf16[10,128,128]{2,1,0:T(8,128)(2,1)}, u32[]{:S(2)}, u32[]{:S(2)}) %collective-permute-start.16) | collective-permute-done | bytes 327712 | tf_op jit(solution)/shard_map/ppermute | solution.py:37
  43.2 0.7 slice_bitcast_fusion.1
  43.9 0.7 copy-done.9
  44.6 0.7 copy-done.3
  45.8 1.6 %collective-permute-start.18 = (bf16[10,128,128]{2,1,0:T(8,128)(2,1)}, bf16[10,128,128]{2,1,0:T(8,128)(2,1)}, u32[]{:S(2)}, u32[]{:S(2)}) collective-permute-start(bf16[10,128,128]{2,1,0:T(8,128)(2,1)} %collective-permute-done.7), channel_id=1, source_target_pairs={{0,8},{2,10},{8,16},{10,18},{16,24},{18,26},{24,28},{26,30},{28,20... | collective-permute-start | bytes 983048 | tf_op jit(solution)/shard_map/ppermute | solution.py:36
  47.4 0.4 collective-permute-start.22
  47.9 0.7 slice_bitcast_fusion.9
  48.6 0.7 slice_bitcast_fusion
  50.2 6.0 %collective-permute-done.18 = bf16[10,128,128]{2,1,0:T(8,128)(2,1)} collective-permute-done((bf16[10,128,128]{2,1,0:T(8,128)(2,1)}, bf16[10,128,128]{2,1,0:T(8,128)(2,1)}, u32[]{:S(2)}, u32[]{:S(2)}) %collective-permute-start.18) | collective-permute-done | bytes 327712 | tf_op jit(solution)/shard_map/ppermute | solution.py:36
  56.3 1.6 %collective-permute-start.20 = (bf16[10,128,128]{2,1,0:T(8,128)(2,1)}, bf16[10,128,128]{2,1,0:T(8,128)(2,1)S(1)}, u32[]{:S(2)}, u32[]{:S(2)}) collective-permute-start(bf16[10,128,128]{2,1,0:T(8,128)(2,1)} %collective-permute-done.18), channel_id=1, source_target_pairs={{0,8},{2,10},{8,16},{10,18},{16,24},{18,26},{24,28},{26,30},{28,20... | collective-permute-start | bytes 983048 | tf_op jit(solution)/shard_map/ppermute | solution.py:36
  57.9 0.4 collective-permute-start.24
  58.5 0.5 collective-permute-start.23
  59.1 6.7 %collective-permute-done.20 = bf16[10,128,128]{2,1,0:T(8,128)(2,1)S(1)} collective-permute-done((bf16[10,128,128]{2,1,0:T(8,128)(2,1)}, bf16[10,128,128]{2,1,0:T(8,128)(2,1)S(1)}, u32[]{:S(2)}, u32[]{:S(2)}) %collective-permute-start.20) | collective-permute-done | bytes 327712 | tf_op jit(solution)/shard_map/ppermute | solution.py:36
  65.8 1.4 %collective-permute-done.24 = bf16[10,128,128]{2,1,0:T(8,128)(2,1)S(1)} collective-permute-done((bf16[10,128,128]{2,1,0:T(8,128)(2,1)}, bf16[10,128,128]{2,1,0:T(8,128)(2,1)S(1)}, u32[]{:S(2)}, u32[]{:S(2)}) %collective-permute-start.24) | collective-permute-done | bytes 327712 | tf_op jit(solution)/shard_map/ppermute | solution.py:37
  67.3 1.6 %collective-permute-start.26 = (bf16[10,128,128]{2,1,0:T(8,128)(2,1)S(1)}, bf16[10,128,128]{2,1,0:T(8,128)(2,1)S(1)}, u32[]{:S(2)}, u32[]{:S(2)}) collective-permute-start(bf16[10,128,128]{2,1,0:T(8,128)(2,1)S(1)} %collective-permute-done.20), channel_id=1, source_target_pairs={{0,8},{2,10},{8,16},{10,18},{16,24},{18,26},{24,28},{26,30},{28,20... | collective-permute-start | bytes 983048 | tf_op jit(solution)/shard_map/ppermute | solution.py:36
  68.9 0.5 collective-permute-start.28
  69.6 1.0 constant_dynamic-update-slice_fusion.5
  70.7 1.0 constant_dynamic-update-slice_fusion.3
  71.8 1.0 constant_dynamic-update-slice_fusion.1
  72.8 1.0 constant_dynamic-update-slice_fusion
  73.8 0.8 fusion.266
  74.6 0.8 fusion.265
  75.4 1.0 constant_dynamic-update-slice_fusion.13
  77.0 0.4 fusion.261
  77.4 1.0 constant_dynamic-update-slice_fusion.29
  79.7 0.7 copy-done.2
  80.6 1.0 constant_dynamic-update-slice_fusion.17
  81.6 0.7 fusion.16
  83.1 1.0 constant_dynamic-update-slice_fusion.16
  84.2 0.8 fusion.260
  85.1 0.8 fusion.259
  85.9 0.6 collective-permute-start.29
  86.4 0.7 fusion.18
  90.2 0.5 fusion.47
  91.5 0.5 fusion.65
  92.4 2.4 %convolution_convert_fusion = bf16[60,5120]{1,0:T(8,128)(2,1)S(1)} fusion(bf16[1280,5120]{1,0:T(8,128)(2,1)S(1)} %bitcast.475, bf16[60,640]{1,0:T(8,128)(2,1)S(1)} %bitcast.485, bf16[60,640]{1,0:T(8,128)(2,1)S(1)} %bitcast.484), kind=kOutput, calls=%fused_computation | convolution fusion | flops 787046400 | bytes 13875200 | tf_op jit(solution)/shard_map/dot_general | solution.py:160
  94.8 1.6 %collective-permute-start.30 = (bf16[60,5120]{1,0:T(8,128)(2,1)S(1)}, bf16[60,5120]{1,0:T(8,128)(2,1)S(1)}, u32[]{:S(2)}, u32[]{:S(2)}) collective-permute-start(bf16[60,5120]{1,0:T(8,128)(2,1)S(1)} %convolution_convert_fusion), channel_id=1, source_target_pairs={{0,1},{1,0},{2,3},{3,2},{4,5},{5,4},{6,7},{7,6},{8,9},{9,8},{10,11... | collective-permute-start | bytes 1843208 | tf_op jit(solution)/shard_map/ppermute | solution.py:162
  96.4 0.7 fusion.38
  97.5 0.5 fusion.56
  98.5 13.3 %collective-permute-done.30 = bf16[60,5120]{1,0:T(8,128)(2,1)S(1)} collective-permute-done((bf16[60,5120]{1,0:T(8,128)(2,1)S(1)}, bf16[60,5120]{1,0:T(8,128)(2,1)S(1)}, u32[]{:S(2)}, u32[]{:S(2)}) %collective-permute-start.30) | collective-permute-done | bytes 614432 | tf_op jit(solution)/shard_map/ppermute | solution.py:162
  111.8 3.4 %add_convert_fusion = bf16[60,5120]{1,0:T(8,128)(2,1)} fusion(bf16[60,5120]{1,0:T(8,128)(2,1)S(1)} %collective-permute-done.30, bf16[60,5120]{1,0:T(8,128)(2,1)S(1)} %copy-done, f32[5120]{0:T(1024)S(1)} %copy-done.12, bf16[1280,5120]{1,0:T(8,128)(2,1)S(1)} %bitcast.475, bf16[60,640]{1,0:T(8,128)(2,1)S(1)} %bitcast.487, bf16[60,640]{1,0:T(8,128)(2,1)S(1)} %bitcast.486), kind=kOutput, calls=%fused_computation.33 | convolution fusion | flops 788582400 | bytes 15124480 | tf_op jit(solution)/shard_map/dot_general | solution.py:164
  (188 shorter events, 14.4 us)
Async XLA Ops:
  2.4 5.9 %copy-start.11 = (bf16[120,1280]{1,0:T(8,128)(2,1)S(1)}, bf16[120,1280]{1,0:T(8,128)(2,1)}, u32[]{:S(2)}) copy-start(bf16[120,1280]{1,0:T(8,128)(2,1)} %param.11) | copy-start | bytes 921604
  4.6 10.7 %collective-permute-start.1 = (bf16[10,128,128]{2,1,0:T(8,128)(2,1)S(1)}, bf16[10,128,128]{2,1,0:T(8,128)(2,1)S(1)}, u32[]{:S(2)}, u32[]{:S(2)}) collective-permute-start(bf16[10,128,128]{2,1,0:T(8,128)(2,1)S(1)} %get-tuple-element.34), channel_id=1, source_target_pairs={{0,8},{2,10},{8,16},{10,18},{16,24},{18,26},{24,28},{26,30},{28,20... | collective-permute-start | bytes 983048 | tf_op jit(solution)/shard_map/ppermute | solution.py:36
  7.7 10.4 %collective-permute-start = (bf16[10,128,128]{2,1,0:T(8,128)(2,1)S(1)}, bf16[10,128,128]{2,1,0:T(8,128)(2,1)S(1)}, u32[]{:S(2)}, u32[]{:S(2)}) collective-permute-start(bf16[10,128,128]{2,1,0:T(8,128)(2,1)S(1)} %get-tuple-element.34), channel_id=1, source_target_pairs={{0,2},{2,0},{4,6},{6,4},{8,10},{10,8},{12,14},{14,12},{16,18},{18,... | collective-permute-start | bytes 983048 | tf_op jit(solution)/shard_map/ppermute | solution.py:40
  7.7 10.1 %collective-permute-start.10 = (bf16[10,128,128]{2,1,0:T(8,128)(2,1)S(1)}, bf16[10,128,128]{2,1,0:T(8,128)(2,1)S(1)}, u32[]{:S(2)}, u32[]{:S(2)}) collective-permute-start(bf16[10,128,128]{2,1,0:T(8,128)(2,1)S(1)} %get-tuple-element.48), channel_id=1, source_target_pairs={{8,0},{10,2},{16,8},{18,10},{24,16},{26,18},{28,24},{30,26},{20,28... | collective-permute-start | bytes 983048 | tf_op jit(solution)/shard_map/ppermute | solution.py:37
  7.8 10.3 %collective-permute-start.9 = (bf16[10,128,128]{2,1,0:T(8,128)(2,1)S(1)}, bf16[10,128,128]{2,1,0:T(8,128)(2,1)S(1)}, u32[]{:S(2)}, u32[]{:S(2)}) collective-permute-start(bf16[10,128,128]{2,1,0:T(8,128)(2,1)S(1)} %get-tuple-element.48), channel_id=1, source_target_pairs={{0,2},{2,0},{4,6},{6,4},{8,10},{10,8},{12,14},{14,12},{16,18},{18,... | collective-permute-start | bytes 983048 | tf_op jit(solution)/shard_map/ppermute | solution.py:41
  15.3 9.0 %collective-permute-start.3 = (bf16[10,128,128]{2,1,0:T(8,128)(2,1)S(1)}, bf16[10,128,128]{2,1,0:T(8,128)(2,1)}, u32[]{:S(2)}, u32[]{:S(2)}) collective-permute-start(bf16[10,128,128]{2,1,0:T(8,128)(2,1)S(1)} %collective-permute-done.1), channel_id=1, source_target_pairs={{0,8},{2,10},{8,16},{10,18},{16,24},{18,26},{24,28},{26,30},{28,20... | collective-permute-start | bytes 983048 | tf_op jit(solution)/shard_map/ppermute | solution.py:36
  17.8 9.3 %collective-permute-start.12 = (bf16[10,128,128]{2,1,0:T(8,128)(2,1)S(1)}, bf16[10,128,128]{2,1,0:T(8,128)(2,1)S(1)}, u32[]{:S(2)}, u32[]{:S(2)}) collective-permute-start(bf16[10,128,128]{2,1,0:T(8,128)(2,1)S(1)} %collective-permute-done.10), channel_id=1, source_target_pairs={{8,0},{10,2},{16,8},{18,10},{24,16},{26,18},{28,24},{30,26},{20,28... | collective-permute-start | bytes 983048 | tf_op jit(solution)/shard_map/ppermute | solution.py:37
  18.5 9.0 %collective-permute-start.11 = (bf16[10,128,128]{2,1,0:T(8,128)(2,1)S(1)}, bf16[10,128,128]{2,1,0:T(8,128)(2,1)S(1)}, u32[]{:S(2)}, u32[]{:S(2)}) collective-permute-start(bf16[10,128,128]{2,1,0:T(8,128)(2,1)S(1)} %collective-permute-done.10), channel_id=1, source_target_pairs={{0,2},{2,0},{4,6},{6,4},{8,10},{10,8},{12,14},{14,12},{16,18},{18,... | collective-permute-start | bytes 983048 | tf_op jit(solution)/shard_map/ppermute | solution.py:41
  18.6 9.0 %collective-permute-start.2 = (bf16[10,128,128]{2,1,0:T(8,128)(2,1)S(1)}, bf16[10,128,128]{2,1,0:T(8,128)(2,1)S(1)}, u32[]{:S(2)}, u32[]{:S(2)}) collective-permute-start(bf16[10,128,128]{2,1,0:T(8,128)(2,1)S(1)} %collective-permute-done.1), channel_id=1, source_target_pairs={{0,2},{2,0},{4,6},{6,4},{8,10},{10,8},{12,14},{14,12},{16,18},{18,... | collective-permute-start | bytes 983048 | tf_op jit(solution)/shard_map/ppermute | solution.py:40
  24.3 8.3 %collective-permute-start.5 = (bf16[10,128,128]{2,1,0:T(8,128)(2,1)}, bf16[10,128,128]{2,1,0:T(8,128)(2,1)}, u32[]{:S(2)}, u32[]{:S(2)}) collective-permute-start(bf16[10,128,128]{2,1,0:T(8,128)(2,1)} %collective-permute-done.3), channel_id=1, source_target_pairs={{0,8},{2,10},{8,16},{10,18},{16,24},{18,26},{24,28},{26,30},{28,20... | collective-permute-start | bytes 983048 | tf_op jit(solution)/shard_map/ppermute | solution.py:36
  27.2 8.5 %collective-permute-start.14 = (bf16[10,128,128]{2,1,0:T(8,128)(2,1)S(1)}, bf16[10,128,128]{2,1,0:T(8,128)(2,1)S(1)}, u32[]{:S(2)}, u32[]{:S(2)}) collective-permute-start(bf16[10,128,128]{2,1,0:T(8,128)(2,1)S(1)} %collective-permute-done.12), channel_id=1, source_target_pairs={{8,0},{10,2},{16,8},{18,10},{24,16},{26,18},{28,24},{30,26},{20,28... | collective-permute-start | bytes 983048 | tf_op jit(solution)/shard_map/ppermute | solution.py:37
  27.6 0.7 copy-start.5
  28.7 7.4 %collective-permute-start.13 = (bf16[10,128,128]{2,1,0:T(8,128)(2,1)S(1)}, bf16[10,128,128]{2,1,0:T(8,128)(2,1)S(1)}, u32[]{:S(2)}, u32[]{:S(2)}) collective-permute-start(bf16[10,128,128]{2,1,0:T(8,128)(2,1)S(1)} %collective-permute-done.12), channel_id=1, source_target_pairs={{0,2},{2,0},{4,6},{6,4},{8,10},{10,8},{12,14},{14,12},{16,18},{18,... | collective-permute-start | bytes 983048 | tf_op jit(solution)/shard_map/ppermute | solution.py:41
  28.7 7.4 %collective-permute-start.4 = (bf16[10,128,128]{2,1,0:T(8,128)(2,1)}, bf16[10,128,128]{2,1,0:T(8,128)(2,1)S(1)}, u32[]{:S(2)}, u32[]{:S(2)}) collective-permute-start(bf16[10,128,128]{2,1,0:T(8,128)(2,1)} %collective-permute-done.3), channel_id=1, source_target_pairs={{0,2},{2,0},{4,6},{6,4},{8,10},{10,8},{12,14},{14,12},{16,18},{18,... | collective-permute-start | bytes 983048 | tf_op jit(solution)/shard_map/ppermute | solution.py:40
  32.6 7.4 %collective-permute-start.7 = (bf16[10,128,128]{2,1,0:T(8,128)(2,1)}, bf16[10,128,128]{2,1,0:T(8,128)(2,1)}, u32[]{:S(2)}, u32[]{:S(2)}) collective-permute-start(bf16[10,128,128]{2,1,0:T(8,128)(2,1)} %collective-permute-done.5), channel_id=1, source_target_pairs={{0,8},{2,10},{8,16},{10,18},{16,24},{18,26},{24,28},{26,30},{28,20... | collective-permute-start | bytes 983048 | tf_op jit(solution)/shard_map/ppermute | solution.py:36
  35.6 7.6 %collective-permute-start.16 = (bf16[10,128,128]{2,1,0:T(8,128)(2,1)S(1)}, bf16[10,128,128]{2,1,0:T(8,128)(2,1)}, u32[]{:S(2)}, u32[]{:S(2)}) collective-permute-start(bf16[10,128,128]{2,1,0:T(8,128)(2,1)S(1)} %collective-permute-done.14), channel_id=1, source_target_pairs={{8,0},{10,2},{16,8},{18,10},{24,16},{26,18},{28,24},{30,26},{20,28... | collective-permute-start | bytes 983048 | tf_op jit(solution)/shard_map/ppermute | solution.py:37
  36.2 0.7 copy-start.7
  36.9 0.7 copy-start.1
  38.0 5.9 %collective-permute-start.15 = (bf16[10,128,128]{2,1,0:T(8,128)(2,1)S(1)}, bf16[10,128,128]{2,1,0:T(8,128)(2,1)S(1)}, u32[]{:S(2)}, u32[]{:S(2)}) collective-permute-start(bf16[10,128,128]{2,1,0:T(8,128)(2,1)S(1)} %collective-permute-done.14), channel_id=1, source_target_pairs={{0,2},{2,0},{4,6},{6,4},{8,10},{10,8},{12,14},{14,12},{16,18},{18,... | collective-permute-start | bytes 983048 | tf_op jit(solution)/shard_map/ppermute | solution.py:41
  38.0 5.9 %collective-permute-start.6 = (bf16[10,128,128]{2,1,0:T(8,128)(2,1)}, bf16[10,128,128]{2,1,0:T(8,128)(2,1)S(1)}, u32[]{:S(2)}, u32[]{:S(2)}) collective-permute-start(bf16[10,128,128]{2,1,0:T(8,128)(2,1)} %collective-permute-done.5), channel_id=1, source_target_pairs={{0,2},{2,0},{4,6},{6,4},{8,10},{10,8},{12,14},{14,12},{16,18},{18,... | collective-permute-start | bytes 983048 | tf_op jit(solution)/shard_map/ppermute | solution.py:40
  40.0 7.8 %collective-permute-start.8 = (bf16[10,128,128]{2,1,0:T(8,128)(2,1)}, bf16[10,128,128]{2,1,0:T(8,128)(2,1)}, u32[]{:S(2)}, u32[]{:S(2)}) collective-permute-start(bf16[10,128,128]{2,1,0:T(8,128)(2,1)} %collective-permute-done.7), channel_id=1, source_target_pairs={{0,2},{2,0},{4,6},{6,4},{8,10},{10,8},{12,14},{14,12},{16,18},{18,... | collective-permute-start | bytes 983048 | tf_op jit(solution)/shard_map/ppermute | solution.py:40
  43.2 5.4 %collective-permute-start.17 = (bf16[10,128,128]{2,1,0:T(8,128)(2,1)}, bf16[10,128,128]{2,1,0:T(8,128)(2,1)}, u32[]{:S(2)}, u32[]{:S(2)}) collective-permute-start(bf16[10,128,128]{2,1,0:T(8,128)(2,1)} %collective-permute-done.16), channel_id=1, source_target_pairs={{0,2},{2,0},{4,6},{6,4},{8,10},{10,8},{12,14},{14,12},{16,18},{18,... | collective-permute-start | bytes 983048 | tf_op jit(solution)/shard_map/ppermute | solution.py:41
  43.9 0.7 copy-start.9
  44.6 0.7 copy-start.3
  45.8 10.4 %collective-permute-start.18 = (bf16[10,128,128]{2,1,0:T(8,128)(2,1)}, bf16[10,128,128]{2,1,0:T(8,128)(2,1)}, u32[]{:S(2)}, u32[]{:S(2)}) collective-permute-start(bf16[10,128,128]{2,1,0:T(8,128)(2,1)} %collective-permute-done.7), channel_id=1, source_target_pairs={{0,8},{2,10},{8,16},{10,18},{16,24},{18,26},{24,28},{26,30},{28,20... | collective-permute-start | bytes 983048 | tf_op jit(solution)/shard_map/ppermute | solution.py:36
  47.4 10.5 %collective-permute-start.22 = (bf16[10,128,128]{2,1,0:T(8,128)(2,1)}, bf16[10,128,128]{2,1,0:T(8,128)(2,1)}, u32[]{:S(2)}, u32[]{:S(2)}) collective-permute-start(bf16[10,128,128]{2,1,0:T(8,128)(2,1)} %collective-permute-done.16), channel_id=1, source_target_pairs={{8,0},{10,2},{16,8},{18,10},{24,16},{26,18},{28,24},{30,26},{20,28... | collective-permute-start | bytes 983048 | tf_op jit(solution)/shard_map/ppermute | solution.py:37
  49.5 20.0 %copy-start.6 = (bf16[10,128,128]{2,1,0:T(8,128)(2,1)S(1)}, bf16[10,128,128]{2,1,0:T(8,128)(2,1)}, u32[]{:S(2)}) copy-start(bf16[10,128,128]{2,1,0:T(8,128)(2,1)} %copy-done.5) | copy-start | bytes 983044
  56.3 9.6 %collective-permute-start.20 = (bf16[10,128,128]{2,1,0:T(8,128)(2,1)}, bf16[10,128,128]{2,1,0:T(8,128)(2,1)S(1)}, u32[]{:S(2)}, u32[]{:S(2)}) collective-permute-start(bf16[10,128,128]{2,1,0:T(8,128)(2,1)} %collective-permute-done.18), channel_id=1, source_target_pairs={{0,8},{2,10},{8,16},{10,18},{16,24},{18,26},{24,28},{26,30},{28,20... | collective-permute-start | bytes 983048 | tf_op jit(solution)/shard_map/ppermute | solution.py:36
  57.9 9.3 %collective-permute-start.24 = (bf16[10,128,128]{2,1,0:T(8,128)(2,1)}, bf16[10,128,128]{2,1,0:T(8,128)(2,1)S(1)}, u32[]{:S(2)}, u32[]{:S(2)}) collective-permute-start(bf16[10,128,128]{2,1,0:T(8,128)(2,1)} %collective-permute-done.22), channel_id=1, source_target_pairs={{8,0},{10,2},{16,8},{18,10},{24,16},{26,18},{28,24},{30,26},{20,28... | collective-permute-start | bytes 983048 | tf_op jit(solution)/shard_map/ppermute | solution.py:37
  58.5 10.4 %collective-permute-start.19 = (bf16[10,128,128]{2,1,0:T(8,128)(2,1)}, bf16[10,128,128]{2,1,0:T(8,128)(2,1)S(1)}, u32[]{:S(2)}, u32[]{:S(2)}) collective-permute-start(bf16[10,128,128]{2,1,0:T(8,128)(2,1)} %collective-permute-done.18), channel_id=1, source_target_pairs={{0,2},{2,0},{4,6},{6,4},{8,10},{10,8},{12,14},{14,12},{16,18},{18,... | collective-permute-start | bytes 983048 | tf_op jit(solution)/shard_map/ppermute | solution.py:40
  58.5 10.9 %collective-permute-start.23 = (bf16[10,128,128]{2,1,0:T(8,128)(2,1)}, bf16[10,128,128]{2,1,0:T(8,128)(2,1)S(1)}, u32[]{:S(2)}, u32[]{:S(2)}) collective-permute-start(bf16[10,128,128]{2,1,0:T(8,128)(2,1)} %collective-permute-done.22), channel_id=1, source_target_pairs={{0,2},{2,0},{4,6},{6,4},{8,10},{10,8},{12,14},{14,12},{16,18},{18,... | collective-permute-start | bytes 983048 | tf_op jit(solution)/shard_map/ppermute | solution.py:41
  65.8 3.6 %collective-permute-start.21 = (bf16[10,128,128]{2,1,0:T(8,128)(2,1)S(1)}, bf16[10,128,128]{2,1,0:T(8,128)(2,1)S(1)}, u32[]{:S(2)}, u32[]{:S(2)}) collective-permute-start(bf16[10,128,128]{2,1,0:T(8,128)(2,1)S(1)} %collective-permute-done.20), channel_id=1, source_target_pairs={{0,2},{2,0},{4,6},{6,4},{8,10},{10,8},{12,14},{14,12},{16,18},{18,... | collective-permute-start | bytes 983048 | tf_op jit(solution)/shard_map/ppermute | solution.py:40
  67.2 2.2 %collective-permute-start.25 = (bf16[10,128,128]{2,1,0:T(8,128)(2,1)S(1)}, bf16[10,128,128]{2,1,0:T(8,128)(2,1)S(1)}, u32[]{:S(2)}, u32[]{:S(2)}) collective-permute-start(bf16[10,128,128]{2,1,0:T(8,128)(2,1)S(1)} %collective-permute-done.24), channel_id=1, source_target_pairs={{0,2},{2,0},{4,6},{6,4},{8,10},{10,8},{12,14},{14,12},{16,18},{18,... | collective-permute-start | bytes 983048 | tf_op jit(solution)/shard_map/ppermute | solution.py:41
  67.3 3.3 %copy-start.8 = (bf16[10,128,128]{2,1,0:T(8,128)(2,1)S(1)}, bf16[10,128,128]{2,1,0:T(8,128)(2,1)}, u32[]{:S(2)}) copy-start(bf16[10,128,128]{2,1,0:T(8,128)(2,1)} %copy-done.7) | copy-start | bytes 983044
  67.3 17.6 %collective-permute-start.26 = (bf16[10,128,128]{2,1,0:T(8,128)(2,1)S(1)}, bf16[10,128,128]{2,1,0:T(8,128)(2,1)S(1)}, u32[]{:S(2)}, u32[]{:S(2)}) collective-permute-start(bf16[10,128,128]{2,1,0:T(8,128)(2,1)S(1)} %collective-permute-done.20), channel_id=1, source_target_pairs={{0,8},{2,10},{8,16},{10,18},{16,24},{18,26},{24,28},{26,30},{28,20... | collective-permute-start | bytes 983048 | tf_op jit(solution)/shard_map/ppermute | solution.py:36
  68.9 16.9 %collective-permute-start.28 = (bf16[10,128,128]{2,1,0:T(8,128)(2,1)S(1)}, bf16[10,128,128]{2,1,0:T(8,128)(2,1)S(1)}, u32[]{:S(2)}, u32[]{:S(2)}) collective-permute-start(bf16[10,128,128]{2,1,0:T(8,128)(2,1)S(1)} %collective-permute-done.24), channel_id=1, source_target_pairs={{8,0},{10,2},{16,8},{18,10},{24,16},{26,18},{28,24},{30,26},{20,28... | collective-permute-start | bytes 983048 | tf_op jit(solution)/shard_map/ppermute | solution.py:37
  69.5 2.2 %copy-start.10 = (bf16[10,128,128]{2,1,0:T(8,128)(2,1)S(1)}, bf16[10,128,128]{2,1,0:T(8,128)(2,1)}, u32[]{:S(2)}) copy-start(bf16[10,128,128]{2,1,0:T(8,128)(2,1)} %copy-done.9) | copy-start | bytes 983044
  79.4 1.0 copy-start.2
  79.5 1.0 copy-start.4
  85.0 2.2 %collective-permute-start.27 = (bf16[10,128,128]{2,1,0:T(8,128)(2,1)S(1)}, bf16[10,128,128]{2,1,0:T(8,128)(2,1)S(1)}, u32[]{:S(2)}, u32[]{:S(2)}) collective-permute-start(bf16[10,128,128]{2,1,0:T(8,128)(2,1)S(1)} %collective-permute-done.26), channel_id=1, source_target_pairs={{0,2},{2,0},{4,6},{6,4},{8,10},{10,8},{12,14},{14,12},{16,18},{18,... | collective-permute-start | bytes 983048 | tf_op jit(solution)/shard_map/ppermute | solution.py:40
  85.1 7.3 %slice-start = ((s8[13107200]{0:T(1024)(128)(4,1)}), s8[4194304]{0:T(1024)(128)(4,1)S(1)}, s32[]{:S(2)}) async-start(s8[13107200]{0:T(1024)(128)(4,1)} %bitcast.474), calls=%async_computation | async-start | bytes 8388608
  85.9 2.0 %collective-permute-start.29 = (bf16[10,128,128]{2,1,0:T(8,128)(2,1)S(1)}, bf16[10,128,128]{2,1,0:T(8,128)(2,1)S(1)}, u32[]{:S(2)}, u32[]{:S(2)}) collective-permute-start(bf16[10,128,128]{2,1,0:T(8,128)(2,1)S(1)} %collective-permute-done.28), channel_id=1, source_target_pairs={{0,2},{2,0},{4,6},{6,4},{8,10},{10,8},{12,14},{14,12},{16,18},{18,... | collective-permute-start | bytes 983048 | tf_op jit(solution)/shard_map/ppermute | solution.py:41
  87.2 5.2 %slice-start.1 = ((s8[13107200]{0:T(1024)(128)(4,1)}), s8[4194304]{0:T(1024)(128)(4,1)S(1)}, s32[]{:S(2)}) async-start(s8[13107200]{0:T(1024)(128)(4,1)} %bitcast.474), calls=%async_computation.1 | async-start | bytes 8388608
  89.6 2.8 %slice-start.2 = ((s8[13107200]{0:T(1024)(128)(4,1)}), s8[4194304]{0:T(1024)(128)(4,1)S(1)}, s32[]{:S(2)}) async-start(s8[13107200]{0:T(1024)(128)(4,1)} %bitcast.474), calls=%async_computation.2 | async-start | bytes 8388608
  91.1 1.3 %slice-start.3 = ((s8[13107200]{0:T(1024)(128)(4,1)}), s8[524288]{0:T(1024)(128)(4,1)S(1)}, s32[]{:S(2)}) async-start(s8[13107200]{0:T(1024)(128)(4,1)} %bitcast.474), calls=%async_computation.3 | async-start | bytes 1048576
  94.8 16.9 %collective-permute-start.30 = (bf16[60,5120]{1,0:T(8,128)(2,1)S(1)}, bf16[60,5120]{1,0:T(8,128)(2,1)S(1)}, u32[]{:S(2)}, u32[]{:S(2)}) collective-permute-start(bf16[60,5120]{1,0:T(8,128)(2,1)S(1)} %convolution_convert_fusion), channel_id=1, source_target_pairs={{0,1},{1,0},{2,3},{3,2},{4,5},{5,4},{6,7},{7,6},{8,9},{9,8},{10,11... | collective-permute-start | bytes 1843208 | tf_op jit(solution)/shard_map/ppermute | solution.py:162
  98.0 13.7 %copy-start = (bf16[60,5120]{1,0:T(8,128)(2,1)S(1)}, bf16[60,5120]{1,0:T(8,128)(2,1)}, u32[]{:S(2)}) copy-start(bf16[60,5120]{1,0:T(8,128)(2,1)} %param.10) | copy-start | bytes 1843204
  98.0 13.7 %copy-start.12 = (f32[5120]{0:T(1024)S(1)}, f32[5120]{0:T(1024)}, u32[]{:S(2)}) copy-start(f32[5120]{0:T(1024)} %param.14) | copy-start | bytes 61444

commit v12 on v11

--- a/solution.py
+++ b/solution.py
@@ -3,6 +3,8 @@
 import jax
 import jax.numpy as jnp
 from jax import lax
+from jax.experimental import pallas as pl
+from jax.experimental.pallas import tpu as pltpu
 from jax.sharding import PartitionSpec as P
 
 HEAD = 128
@@ -63,6 +65,31 @@
     return peak, totals, summed
 
 
+def join_packets(packets, interpret=False):
+    count = len(packets)
+    heads, rows, width = packets[0].shape
+
+    def kernel(*refs):
+        sources, target, sems = refs[:count], refs[count], refs[count + 1]
+        copies = [
+            pltpu.make_async_copy(sources[i], target.at[:, i * rows : (i + 1) * rows, :], sems.at[i])
+            for i in range(count)
+        ]
+        for copy in copies:
+            copy.start()
+        for copy in copies:
+            copy.wait()
+
+    return pl.pallas_call(
+        kernel,
+        out_shape=jax.ShapeDtypeStruct((heads, count * rows, width), packets[0].dtype),
+        in_specs=[pl.BlockSpec(memory_space=pl.ANY)] * count,
+        out_specs=pl.BlockSpec(memory_space=pl.ANY),
+        scratch_shapes=[pltpu.SemaphoreType.DMA((count,))],
+        interpret=interpret,
+    )(*packets)
+
+
 def combine(parts, rows_dev):
     peak = parts[0][0]
     for part in parts[1:]:
@@ -138,13 +165,15 @@
         side = lax.axis_index("tp")
         n_tp = rows_dev // rows_out
 
-        def half(got, limits, lo, hi, which):
+        stacks_a = [join_packets(got_a[first:last]) for first, last in phases]
+        stacks_b = [join_packets(got_b[first:last]) for first, last in phases]
+
+        def half(stacks, limits, lo, hi, which):
             q3 = queries.reshape(n_tp, rows_out, queries.shape[1])
             q3 = jnp.take(q3, which, axis=0)[:, lo * HEAD : hi * HEAD]
             q3 = q3.reshape(rows_out, hi - lo, HEAD).transpose(1, 0, 2)
             parts = []
-            for first, last in phases:
-                stack = jnp.concatenate(got[first:last], axis=1)
+            for (first, last), stack in zip(phases, stacks):
                 keys = stack[: hi - lo]
                 values = stack[hi - lo :]
                 keeping = (within[None, :] < limits[first:last, None]).reshape(-1)
@@ -153,7 +182,7 @@
 
         def attention_rows(which):
             return jnp.concatenate(
-                [half(got_a, limit_a, 0, heads_a, which), half(got_b, limit_b, heads_a, heads_here, which)],
+                [half(stacks_a, limit_a, 0, heads_a, which), half(stacks_b, limit_b, heads_a, heads_here, which)],
                 axis=1,
             )
 

time: 116 us -> 470 us (4.05)
  Pallas kernels: 0 us -> 325 us
  matrix products: 16.4 us -> 39 us
  local copies, waits for them, and re-layouts: 24.2 us -> 40.2 us
  waiting for transfers between devices: 48.3 us -> 35.2 us
    pallas_call x0 -> x6, Pallas kernels: none -> 325 us  [join_packets(): pl.pallas_call(kernel, out_shape=jax.ShapeDtypeStruct((heads, count * row...]
    ppermute x7, waiting for transfers between devices: 28.6 us -> 5.2 us  [gather_ring(): cur_a = lax.ppermute(cur_a, 'seq', forward)]
    another operation x37, local copies, waits for them, and re-layouts: 6.16 us -> 26 us  [on_device(): jnp.stack([g[0, rows_dev, :2] for g in heard]).astype(jnp.float32)]
    dot_general x12, matrix products: 6.1 us -> 23.8 us  [attend_part(): jnp.einsum('hqd,hkd->hqk', queries_3d, keys, preferred_element_type=jnp.f...]
    ppermute x7, waiting for transfers between devices: 6.32 us -> 17.4 us  [gather_ring(): cur_b = lax.ppermute(cur_b, 'seq', backward)]
    ppermute x7, starting transfers between devices: 12.2 us -> 2.82 us  [gather_ring(): cur_a = lax.ppermute(cur_a, 'seq', forward)]
    ppermute x7, starting transfers between devices: 2.66 us -> 11.8 us  [gather_ring(): cur_b = lax.ppermute(cur_b, 'seq', backward)]
    dot_general x1, matrix products: 2.43 us -> 7.26 us  [on_device(): jnp.dot(attention_rows(1 - side), out_weight, preferred_element_type=jnp....]
  transfers between devices with their start and end apart: 31 -> 31, of which waited for: 12 -> 9; matrix products, arithmetic and copies ran while one was open for 23% -> 12% of each run, Pallas kernels for 0% -> 65%
where the time goes in v12:
time: 470 us
  Pallas kernels  325 us (69%)
  local copies, waits for them, and re-layouts  40.2 us (9%)
  matrix products  39 us (8%)
  waiting for transfers between devices  35.2 us (7%)
  starting transfers between devices  19.1 us (4%)
  other arithmetic  8.63 us (2%)
    pallas_call x6, Pallas kernels, join_packets(): pl.pallas_call(kernel, out_shape=jax.ShapeDtypeStruct((heads, count * row...  325 us
    another operation x37, local copies, waits for them, and re-layouts, on_device(): jnp.stack([g[0, rows_dev, :2] for g in heard]).astype(jnp.float32)  26 us
    dot_general x12, matrix products, attend_part(): jnp.einsum('hqd,hkd->hqk', queries_3d, keys, preferred_element_type=jnp.f...  23.8 us
    ppermute x7, waiting for transfers between devices, gather_ring(): cur_b = lax.ppermute(cur_b, 'seq', backward)  17.4 us
    ppermute x1, waiting for transfers between devices, on_device(): came = lax.ppermute(other, 'tp', [(0, 1), (1, 0)])  12.6 us
    ppermute x7, starting transfers between devices, gather_ring(): cur_b = lax.ppermute(cur_b, 'seq', backward)  11.8 us
  transfers between devices with their start and end apart: 31, of which 9 were waited for; matrix products, arithmetic and copies ran while one was open for 12% of the time, Pallas kernels for 65%

profile of v12, /device:TPU:0, one launch (start us, length us, event | category | flops | bytes accessed | tf_op | source)
XLA Modules:
  0.0 469.6 jit_solution(11477691410715428554)
XLA Ops:
  1.5 1.0 fusion.251
  2.5 1.0 fusion.252
  4.6 3.0 collective-permute-start.10
  9.0 0.8 reshape.426
  9.7 0.8 reshape.430
  10.9 4.5 collective-permute-done.10.refs_2_
  15.4 1.7 collective-permute-start.12
  19.0 5.3 %collective-permute-done.12.refs_4_ = bf16[10,128,128]{2,1,0:T(8,128)(2,1)S(1)} collective-permute-done((bf16[10,128,128]{2,1,0:T(8,128)(2,1)S(1)}, bf16[10,128,128]{2,1,0:T(8,128)(2,1)S(1)}, u32[]{:S(2)}, u32[]{:S(2)}) %collective-permute-start.12) | collective-permute-done | bytes 327712 | tf_op jit(solution)/shard_map/ppermute | solution.py:39
  24.3 1.4 collective-permute-start.14
  25.7 1.4 collective-permute-done.3.refs_4_
  30.7 1.6 collective-permute-done.14.refs_6_
  32.9 1.0 collective-permute-start.16
  33.9 1.8 collective-permute-done.5.refs_6_
  35.7 1.3 slice_bitcast_fusion.12
  39.2 1.2 copy.71
  40.4 1.2 copy.70
  41.6 1.2 copy.62
  42.9 1.2 copy.61
  44.6 1.2 slice_bitcast_fusion.1
  45.9 1.2 slice_bitcast_fusion.10
  48.9 0.8 copy-done.40
  50.2 1.2 copy.73
  51.5 1.3 copy.72
  52.8 1.3 copy.64
  54.1 1.3 copy.63
  55.4 1.5 collective-permute-start.22
  57.4 1.2 slice_bitcast_fusion
  58.6 1.3 copy.74
  59.9 1.3 slice_bitcast_fusion.9
  61.2 1.3 copy.65
  62.4 1.4 stack.126
  65.7 1.5 collective-permute-start.24
  69.1 6.0 %collective-permute-done.24.refs_2_ = bf16[10,128,128]{2,1,0:T(8,128)(2,1)} collective-permute-done((bf16[10,128,128]{2,1,0:T(8,128)(2,1)}, bf16[10,128,128]{2,1,0:T(8,128)(2,1)}, u32[]{:S(2)}, u32[]{:S(2)}) %collective-permute-start.24) | collective-permute-done | bytes 327712 | tf_op jit(solution)/shard_map/ppermute | solution.py:39
  75.1 1.3 collective-permute-done.20.refs_2_
  76.5 1.6 collective-permute-start.28
  78.6 40.8 %shard_map.83 = bf16[10,512,128]{2,1,0:T(8,128)(2,1)} custom-call(bf16[10,128,128]{2,1,0:T(8,128)(2,1)} %collective-permute-done.18.refs_0_, bf16[10,128,128]{2,1,0:T(8,128)(2,1)} %collective-permute-done.19.refs_1_, bf16[10,128,128]{2,1,0:T(8,128)(2,1)} %collective-permute-done.20.refs_2_, bf16[10,128,128]{2,1,0:T(8,128)(2,1)} %collective-permute-done.21.refs_3_), custom_call_target="tpu_custom_call" | custom-call | tf_op jit(solution)/shard_map/pallas_call | solution.py:83
  119.4 2.3 fusion.261
  121.8 2.3 fusion.264
  124.1 100.5 %shard_map.82 = bf16[10,1280,128]{2,1,0:T(8,128)(2,1)} custom-call(bf16[10,128,128]{2,1,0:T(8,128)(2,1)} %copy-done.23, bf16[10,128,128]{2,1,0:T(8,128)(2,1)} %copy-done.31, bf16[10,128,128]{2,1,0:T(8,128)(2,1)} %copy-done.30, bf16[10,128,128]{2,1,0:T(8,128)(2,1)} %copy-done.36, bf16[10,128,128]{2,1,0:T(8,128)(2,1)} %copy-done.34, ...), custom_call_target="tpu_custom_call" | custom-call | tf_op jit(solution)/shard_map/pallas_call | solution.py:83
  224.6 3.5 fusion.265
  228.1 1.9 fusion.266
  230.0 40.8 %shard_map.86 = bf16[10,512,128]{2,1,0:T(8,128)(2,1)} custom-call(bf16[10,128,128]{2,1,0:T(8,128)(2,1)} %collective-permute-done.22.refs_0_, bf16[10,128,128]{2,1,0:T(8,128)(2,1)} %collective-permute-done.23.refs_1_, bf16[10,128,128]{2,1,0:T(8,128)(2,1)} %collective-permute-done.24.refs_2_, bf16[10,128,128]{2,1,0:T(8,128)(2,1)} %collective-permute-done.25.refs_3_), custom_call_target="tpu_custom_call" | custom-call | tf_op jit(solution)/shard_map/pallas_call | solution.py:83
  270.8 2.4 fusion.255
  273.2 100.5 %shard_map.85 = bf16[10,1280,128]{2,1,0:T(8,128)(2,1)} custom-call(bf16[10,128,128]{2,1,0:T(8,128)(2,1)} %copy-done.22, bf16[10,128,128]{2,1,0:T(8,128)(2,1)} %copy-done.29, bf16[10,128,128]{2,1,0:T(8,128)(2,1)} %copy-done.28, bf16[10,128,128]{2,1,0:T(8,128)(2,1)} %copy-done.33, bf16[10,128,128]{2,1,0:T(8,128)(2,1)} %copy-done.32, ...), custom_call_target="tpu_custom_call" | custom-call | tf_op jit(solution)/shard_map/pallas_call | solution.py:83
  373.7 2.4 fusion.260
  376.2 1.3 fusion.16
  377.9 0.8 copy-done.1
  378.8 0.8 fusion.259
  380.3 1.0 fusion.112
  381.3 1.0 fusion.114
  382.3 1.3 fusion.18
  383.6 21.0 %shard_map.87 = bf16[10,256,128]{2,1,0:T(8,128)(2,1)} custom-call(bf16[10,128,128]{2,1,0:T(8,128)(2,1)} %collective-permute-done.28.refs_0_, bf16[10,128,128]{2,1,0:T(8,128)(2,1)} %collective-permute-done.29.refs_1_), custom_call_target="tpu_custom_call" | custom-call | tf_op jit(solution)/shard_map/pallas_call | solution.py:83
  404.6 2.6 fusion.257
  407.1 2.6 fusion.256
  409.7 21.0 %shard_map.84 = bf16[10,256,128]{2,1,0:T(8,128)(2,1)} custom-call(bf16[10,128,128]{2,1,0:T(8,128)(2,1)} %collective-permute-done.26.refs_0_, bf16[10,128,128]{2,1,0:T(8,128)(2,1)} %collective-permute-done.27.refs_1_), custom_call_target="tpu_custom_call" | custom-call | tf_op jit(solution)/shard_map/pallas_call | solution.py:83
  430.7 1.4 fusion.263
  432.2 1.4 fusion.262
  433.5 0.9 fusion.144
  438.9 1.3 copy-done.2
  441.7 7.3 %convolution_convert_fusion = bf16[60,5120]{1,0:T(8,128)(2,1)S(1)} fusion(bf16[1280,5120]{1,0:T(8,128)(2,1)} %param.15, bf16[60,640]{1,0:T(8,128)(2,1)S(1)} %bitcast.485, bf16[60,640]{1,0:T(8,128)(2,1)S(1)} %bitcast.484), kind=kOutput, calls=%fused_computation | convolution fusion | flops 787046400 | bytes 13875200 | tf_op jit(solution)/shard_map/dot_general | solution.py:189
  449.0 1.5 collective-permute-start.30
  451.4 1.0 copy-done.6
  453.6 12.6 %collective-permute-done.30 = bf16[60,5120]{1,0:T(8,128)(2,1)S(1)} collective-permute-done((bf16[60,5120]{1,0:T(8,128)(2,1)S(1)}, bf16[60,5120]{1,0:T(8,128)(2,1)S(1)}, u32[]{:S(2)}, u32[]{:S(2)}) %collective-permute-start.30) | collective-permute-done | bytes 614432 | tf_op jit(solution)/shard_map/ppermute | solution.py:191
  466.2 3.4 add_convert_fusion
  (272 shorter events, 27.2 us)
Async XLA Ops:
  3.8 4.3 copy-start.43
  4.6 5.9 %copy-start.22 = (bf16[10,128,128]{2,1,0:T(8,128)(2,1)}, bf16[10,128,128]{2,1,0:T(8,128)(2,1)S(1)}, u32[]{:S(2)}) copy-start(bf16[10,128,128]{2,1,0:T(8,128)(2,1)S(1)} %get-tuple-element.48.refs_0_) | copy-start | bytes 983044
  4.6 5.9 %copy-start.23 = (bf16[10,128,128]{2,1,0:T(8,128)(2,1)}, bf16[10,128,128]{2,1,0:T(8,128)(2,1)S(1)}, u32[]{:S(2)}) copy-start(bf16[10,128,128]{2,1,0:T(8,128)(2,1)S(1)} %get-tuple-element.34.refs_0_) | copy-start | bytes 983044
  4.6 10.8 %collective-permute-start.10 = (bf16[10,128,128]{2,1,0:T(8,128)(2,1)S(1)}, bf16[10,128,128]{2,1,0:T(8,128)(2,1)S(1)}, u32[]{:S(2)}, u32[]{:S(2)}) collective-permute-start(bf16[10,128,128]{2,1,0:T(8,128)(2,1)S(1)} %get-tuple-element.48.refs_0_), channel_id=1, source_target_pairs={{8,0},{10,2},{16,8},{18,10},{24,16},{26,18},{28,24},{30,26},{20,28... | collective-permute-start | bytes 983048 | tf_op jit(solution)/shard_map/ppermute | solution.py:39
  7.6 10.4 %collective-permute-start.9 = (bf16[10,128,128]{2,1,0:T(8,128)(2,1)S(1)}, bf16[10,128,128]{2,1,0:T(8,128)(2,1)S(1)}, u32[]{:S(2)}, u32[]{:S(2)}) collective-permute-start(bf16[10,128,128]{2,1,0:T(8,128)(2,1)S(1)} %get-tuple-element.48.refs_0_), channel_id=1, source_target_pairs={{0,2},{2,0},{4,6},{6,4},{8,10},{10,8},{12,14},{14,12},{16,18},{18,... | collective-permute-start | bytes 983048 | tf_op jit(solution)/shard_map/ppermute | solution.py:43
  7.7 10.1 %collective-permute-start.1 = (bf16[10,128,128]{2,1,0:T(8,128)(2,1)S(1)}, bf16[10,128,128]{2,1,0:T(8,128)(2,1)S(1)}, u32[]{:S(2)}, u32[]{:S(2)}) collective-permute-start(bf16[10,128,128]{2,1,0:T(8,128)(2,1)S(1)} %get-tuple-element.34.refs_0_), channel_id=1, source_target_pairs={{0,8},{2,10},{8,16},{10,18},{16,24},{18,26},{24,28},{26,30},{28,20... | collective-permute-start | bytes 983048 | tf_op jit(solution)/shard_map/ppermute | solution.py:38
  7.8 10.2 %collective-permute-start = (bf16[10,128,128]{2,1,0:T(8,128)(2,1)S(1)}, bf16[10,128,128]{2,1,0:T(8,128)(2,1)S(1)}, u32[]{:S(2)}, u32[]{:S(2)}) collective-permute-start(bf16[10,128,128]{2,1,0:T(8,128)(2,1)S(1)} %get-tuple-element.34.refs_0_), channel_id=1, source_target_pairs={{0,2},{2,0},{4,6},{6,4},{8,10},{10,8},{12,14},{14,12},{16,18},{18,... | collective-permute-start | bytes 983048 | tf_op jit(solution)/shard_map/ppermute | solution.py:42
  15.4 106.3 %copy-start.28 = (bf16[10,128,128]{2,1,0:T(8,128)(2,1)}, bf16[10,128,128]{2,1,0:T(8,128)(2,1)S(1)}, u32[]{:S(2)}) copy-start(bf16[10,128,128]{2,1,0:T(8,128)(2,1)S(1)} %collective-permute-done.10.refs_2_) | copy-start | bytes 983044
  15.4 8.9 %collective-permute-start.12 = (bf16[10,128,128]{2,1,0:T(8,128)(2,1)S(1)}, bf16[10,128,128]{2,1,0:T(8,128)(2,1)S(1)}, u32[]{:S(2)}, u32[]{:S(2)}) collective-permute-start(bf16[10,128,128]{2,1,0:T(8,128)(2,1)S(1)} %collective-permute-done.10.refs_2_), channel_id=1, source_target_pairs={{8,0},{10,2},{16,8},{18,10},{24,16},{26,18},{28,24},{30,26},{20,28... | collective-permute-start | bytes 983048 | tf_op jit(solution)/shard_map/ppermute | solution.py:39
  17.8 104.0 %copy-start.30 = (bf16[10,128,128]{2,1,0:T(8,128)(2,1)}, bf16[10,128,128]{2,1,0:T(8,128)(2,1)S(1)}, u32[]{:S(2)}) copy-start(bf16[10,128,128]{2,1,0:T(8,128)(2,1)S(1)} %collective-permute-done.1.refs_2_) | copy-start | bytes 983044
  17.8 9.3 %collective-permute-start.3 = (bf16[10,128,128]{2,1,0:T(8,128)(2,1)S(1)}, bf16[10,128,128]{2,1,0:T(8,128)(2,1)S(1)}, u32[]{:S(2)}, u32[]{:S(2)}) collective-permute-start(bf16[10,128,128]{2,1,0:T(8,128)(2,1)S(1)} %collective-permute-done.1.refs_2_), channel_id=1, source_target_pairs={{0,8},{2,10},{8,16},{10,18},{16,24},{18,26},{24,28},{26,30},{28,20... | collective-permute-start | bytes 983048 | tf_op jit(solution)/shard_map/ppermute | solution.py:38
  18.1 103.7 %copy-start.29 = (bf16[10,128,128]{2,1,0:T(8,128)(2,1)}, bf16[10,128,128]{2,1,0:T(8,128)(2,1)S(1)}, u32[]{:S(2)}) copy-start(bf16[10,128,128]{2,1,0:T(8,128)(2,1)S(1)} %collective-permute-done.9.refs_1_) | copy-start | bytes 983044
  18.1 103.7 %copy-start.31 = (bf16[10,128,128]{2,1,0:T(8,128)(2,1)}, bf16[10,128,128]{2,1,0:T(8,128)(2,1)S(1)}, u32[]{:S(2)}) copy-start(bf16[10,128,128]{2,1,0:T(8,128)(2,1)S(1)} %collective-permute-done.refs_1_) | copy-start | bytes 983044
  18.5 9.0 %collective-permute-start.11 = (bf16[10,128,128]{2,1,0:T(8,128)(2,1)S(1)}, bf16[10,128,128]{2,1,0:T(8,128)(2,1)S(1)}, u32[]{:S(2)}, u32[]{:S(2)}) collective-permute-start(bf16[10,128,128]{2,1,0:T(8,128)(2,1)S(1)} %collective-permute-done.10.refs_2_), channel_id=1, source_target_pairs={{0,2},{2,0},{4,6},{6,4},{8,10},{10,8},{12,14},{14,12},{16,18},{18,... | collective-permute-start | bytes 983048 | tf_op jit(solution)/shard_map/ppermute | solution.py:43
  18.5 9.0 %collective-permute-start.2 = (bf16[10,128,128]{2,1,0:T(8,128)(2,1)S(1)}, bf16[10,128,128]{2,1,0:T(8,128)(2,1)S(1)}, u32[]{:S(2)}, u32[]{:S(2)}) collective-permute-start(bf16[10,128,128]{2,1,0:T(8,128)(2,1)S(1)} %collective-permute-done.1.refs_2_), channel_id=1, source_target_pairs={{0,2},{2,0},{4,6},{6,4},{8,10},{10,8},{12,14},{14,12},{16,18},{18,... | collective-permute-start | bytes 983048 | tf_op jit(solution)/shard_map/ppermute | solution.py:42
  24.3 97.4 %copy-start.32 = (bf16[10,128,128]{2,1,0:T(8,128)(2,1)}, bf16[10,128,128]{2,1,0:T(8,128)(2,1)S(1)}, u32[]{:S(2)}) copy-start(bf16[10,128,128]{2,1,0:T(8,128)(2,1)S(1)} %collective-permute-done.12.refs_4_) | copy-start | bytes 983044
  24.3 8.0 %collective-permute-start.14 = (bf16[10,128,128]{2,1,0:T(8,128)(2,1)S(1)}, bf16[10,128,128]{2,1,0:T(8,128)(2,1)S(1)}, u32[]{:S(2)}, u32[]{:S(2)}) collective-permute-start(bf16[10,128,128]{2,1,0:T(8,128)(2,1)S(1)} %collective-permute-done.12.refs_4_), channel_id=1, source_target_pairs={{8,0},{10,2},{16,8},{18,10},{24,16},{26,18},{28,24},{30,26},{20,28... | collective-permute-start | bytes 983048 | tf_op jit(solution)/shard_map/ppermute | solution.py:39
  27.1 94.6 %copy-start.34 = (bf16[10,128,128]{2,1,0:T(8,128)(2,1)}, bf16[10,128,128]{2,1,0:T(8,128)(2,1)S(1)}, u32[]{:S(2)}) copy-start(bf16[10,128,128]{2,1,0:T(8,128)(2,1)S(1)} %collective-permute-done.3.refs_4_) | copy-start | bytes 983044
  27.1 8.6 %collective-permute-start.5 = (bf16[10,128,128]{2,1,0:T(8,128)(2,1)S(1)}, bf16[10,128,128]{2,1,0:T(8,128)(2,1)}, u32[]{:S(2)}, u32[]{:S(2)}) collective-permute-start(bf16[10,128,128]{2,1,0:T(8,128)(2,1)S(1)} %collective-permute-done.3.refs_4_), channel_id=1, source_target_pairs={{0,8},{2,10},{8,16},{10,18},{16,24},{18,26},{24,28},{26,30},{28,20... | collective-permute-start | bytes 983048 | tf_op jit(solution)/shard_map/ppermute | solution.py:38
  27.5 94.3 %copy-start.33 = (bf16[10,128,128]{2,1,0:T(8,128)(2,1)}, bf16[10,128,128]{2,1,0:T(8,128)(2,1)S(1)}, u32[]{:S(2)}) copy-start(bf16[10,128,128]{2,1,0:T(8,128)(2,1)S(1)} %collective-permute-done.11.refs_3_) | copy-start | bytes 983044
  27.5 94.3 %copy-start.36 = (bf16[10,128,128]{2,1,0:T(8,128)(2,1)}, bf16[10,128,128]{2,1,0:T(8,128)(2,1)S(1)}, u32[]{:S(2)}) copy-start(bf16[10,128,128]{2,1,0:T(8,128)(2,1)S(1)} %collective-permute-done.2.refs_3_) | copy-start | bytes 983044
  30.2 7.2 %collective-permute-start.13 = (bf16[10,128,128]{2,1,0:T(8,128)(2,1)S(1)}, bf16[10,128,128]{2,1,0:T(8,128)(2,1)S(1)}, u32[]{:S(2)}, u32[]{:S(2)}) collective-permute-start(bf16[10,128,128]{2,1,0:T(8,128)(2,1)S(1)} %collective-permute-done.12.refs_4_), channel_id=1, source_target_pairs={{0,2},{2,0},{4,6},{6,4},{8,10},{10,8},{12,14},{14,12},{16,18},{18,... | collective-permute-start | bytes 983048 | tf_op jit(solution)/shard_map/ppermute | solution.py:43
  30.2 7.8 %collective-permute-start.4 = (bf16[10,128,128]{2,1,0:T(8,128)(2,1)S(1)}, bf16[10,128,128]{2,1,0:T(8,128)(2,1)S(1)}, u32[]{:S(2)}, u32[]{:S(2)}) collective-permute-start(bf16[10,128,128]{2,1,0:T(8,128)(2,1)S(1)} %collective-permute-done.3.refs_4_), channel_id=1, source_target_pairs={{0,2},{2,0},{4,6},{6,4},{8,10},{10,8},{12,14},{14,12},{16,18},{18,... | collective-permute-start | bytes 983048 | tf_op jit(solution)/shard_map/ppermute | solution.py:42
  32.3 89.5 %copy-start.35 = (bf16[10,128,128]{2,1,0:T(8,128)(2,1)}, bf16[10,128,128]{2,1,0:T(8,128)(2,1)S(1)}, u32[]{:S(2)}) copy-start(bf16[10,128,128]{2,1,0:T(8,128)(2,1)S(1)} %collective-permute-done.14.refs_6_) | copy-start | bytes 983044
  32.9 11.7 %collective-permute-start.16 = (bf16[10,128,128]{2,1,0:T(8,128)(2,1)S(1)}, bf16[10,128,128]{2,1,0:T(8,128)(2,1)}, u32[]{:S(2)}, u32[]{:S(2)}) collective-permute-start(bf16[10,128,128]{2,1,0:T(8,128)(2,1)S(1)} %collective-permute-done.14.refs_6_), channel_id=1, source_target_pairs={{8,0},{10,2},{16,8},{18,10},{24,16},{26,18},{28,24},{30,26},{20,28... | collective-permute-start | bytes 983048 | tf_op jit(solution)/shard_map/ppermute | solution.py:39
  36.9 9.0 %collective-permute-start.7 = (bf16[10,128,128]{2,1,0:T(8,128)(2,1)}, bf16[10,128,128]{2,1,0:T(8,128)(2,1)}, u32[]{:S(2)}, u32[]{:S(2)}) collective-permute-start(bf16[10,128,128]{2,1,0:T(8,128)(2,1)} %collective-permute-done.5.refs_6_), channel_id=1, source_target_pairs={{0,8},{2,10},{8,16},{10,18},{16,24},{18,26},{24,28},{26,30},{28,20... | collective-permute-start | bytes 983048 | tf_op jit(solution)/shard_map/ppermute | solution.py:38
  37.4 84.4 %copy-start.37 = (bf16[10,128,128]{2,1,0:T(8,128)(2,1)}, bf16[10,128,128]{2,1,0:T(8,128)(2,1)S(1)}, u32[]{:S(2)}) copy-start(bf16[10,128,128]{2,1,0:T(8,128)(2,1)S(1)} %collective-permute-done.13.refs_5_) | copy-start | bytes 983044
  44.1 3.5 collective-permute-start.15
  44.1 4.8 %collective-permute-start.6 = (bf16[10,128,128]{2,1,0:T(8,128)(2,1)}, bf16[10,128,128]{2,1,0:T(8,128)(2,1)S(1)}, u32[]{:S(2)}, u32[]{:S(2)}) collective-permute-start(bf16[10,128,128]{2,1,0:T(8,128)(2,1)} %collective-permute-done.5.refs_6_), channel_id=1, source_target_pairs={{0,2},{2,0},{4,6},{6,4},{8,10},{10,8},{12,14},{14,12},{16,18},{18,... | collective-permute-start | bytes 983048 | tf_op jit(solution)/shard_map/ppermute | solution.py:42
  45.9 11.5 %collective-permute-start.17 = (bf16[10,128,128]{2,1,0:T(8,128)(2,1)}, bf16[10,128,128]{2,1,0:T(8,128)(2,1)}, u32[]{:S(2)}, u32[]{:S(2)}) collective-permute-start(bf16[10,128,128]{2,1,0:T(8,128)(2,1)} %collective-permute-done.16.refs_8_), channel_id=1, source_target_pairs={{0,2},{2,0},{4,6},{6,4},{8,10},{10,8},{12,14},{14,12},{16,18},{18,... | collective-permute-start | bytes 983048 | tf_op jit(solution)/shard_map/ppermute | solution.py:43
  47.1 12.8 %collective-permute-start.8 = (bf16[10,128,128]{2,1,0:T(8,128)(2,1)}, bf16[10,128,128]{2,1,0:T(8,128)(2,1)}, u32[]{:S(2)}, u32[]{:S(2)}) collective-permute-start(bf16[10,128,128]{2,1,0:T(8,128)(2,1)} %collective-permute-done.7.refs_8_), channel_id=1, source_target_pairs={{0,2},{2,0},{4,6},{6,4},{8,10},{10,8},{12,14},{14,12},{16,18},{18,... | collective-permute-start | bytes 983048 | tf_op jit(solution)/shard_map/ppermute | solution.py:42
  55.4 10.3 %collective-permute-start.22 = (bf16[10,128,128]{2,1,0:T(8,128)(2,1)}, bf16[10,128,128]{2,1,0:T(8,128)(2,1)}, u32[]{:S(2)}, u32[]{:S(2)}) collective-permute-start(bf16[10,128,128]{2,1,0:T(8,128)(2,1)} %collective-permute-done.16.refs_8_), channel_id=1, source_target_pairs={{8,0},{10,2},{16,8},{18,10},{24,16},{26,18},{28,24},{30,26},{20,28... | collective-permute-start | bytes 983048 | tf_op jit(solution)/shard_map/ppermute | solution.py:39
  56.9 10.4 %collective-permute-start.18 = (bf16[10,128,128]{2,1,0:T(8,128)(2,1)}, bf16[10,128,128]{2,1,0:T(8,128)(2,1)}, u32[]{:S(2)}, u32[]{:S(2)}) collective-permute-start(bf16[10,128,128]{2,1,0:T(8,128)(2,1)} %collective-permute-done.7.refs_8_), channel_id=1, source_target_pairs={{0,8},{2,10},{8,16},{10,18},{16,24},{18,26},{24,28},{26,30},{28,20... | collective-permute-start | bytes 983048 | tf_op jit(solution)/shard_map/ppermute | solution.py:38
  65.7 9.4 %collective-permute-start.24 = (bf16[10,128,128]{2,1,0:T(8,128)(2,1)}, bf16[10,128,128]{2,1,0:T(8,128)(2,1)}, u32[]{:S(2)}, u32[]{:S(2)}) collective-permute-start(bf16[10,128,128]{2,1,0:T(8,128)(2,1)} %collective-permute-done.22.refs_0_), channel_id=1, source_target_pairs={{8,0},{10,2},{16,8},{18,10},{24,16},{26,18},{28,24},{30,26},{20,28... | collective-permute-start | bytes 983048 | tf_op jit(solution)/shard_map/ppermute | solution.py:39
  67.3 54.5 %copy-start.63 = (pred[512]{0:T(512)(128)(4,1)}, pred[512]{0:T(512)(128)(4,1)S(1)}, u32[]{:S(2)}) copy-start(pred[512]{0:T(512)(128)(4,1)S(1)} %fusion.223) | copy-start | bytes 1540
  67.3 9.1 %collective-permute-start.20 = (bf16[10,128,128]{2,1,0:T(8,128)(2,1)}, bf16[10,128,128]{2,1,0:T(8,128)(2,1)}, u32[]{:S(2)}, u32[]{:S(2)}) collective-permute-start(bf16[10,128,128]{2,1,0:T(8,128)(2,1)} %collective-permute-done.18.refs_0_), channel_id=1, source_target_pairs={{0,8},{2,10},{8,16},{10,18},{16,24},{18,26},{24,28},{26,30},{28,20... | collective-permute-start | bytes 983048 | tf_op jit(solution)/shard_map/ppermute | solution.py:38
  68.5 9.7 %collective-permute-start.23 = (bf16[10,128,128]{2,1,0:T(8,128)(2,1)}, bf16[10,128,128]{2,1,0:T(8,128)(2,1)}, u32[]{:S(2)}, u32[]{:S(2)}) collective-permute-start(bf16[10,128,128]{2,1,0:T(8,128)(2,1)} %collective-permute-done.22.refs_0_), channel_id=1, source_target_pairs={{0,2},{2,0},{4,6},{6,4},{8,10},{10,8},{12,14},{14,12},{16,18},{18,... | collective-permute-start | bytes 983048 | tf_op jit(solution)/shard_map/ppermute | solution.py:43
  68.5 10.1 %collective-permute-start.19 = (bf16[10,128,128]{2,1,0:T(8,128)(2,1)}, bf16[10,128,128]{2,1,0:T(8,128)(2,1)}, u32[]{:S(2)}, u32[]{:S(2)}) collective-permute-start(bf16[10,128,128]{2,1,0:T(8,128)(2,1)} %collective-permute-done.18.refs_0_), channel_id=1, source_target_pairs={{0,2},{2,0},{4,6},{6,4},{8,10},{10,8},{12,14},{14,12},{16,18},{18,... | collective-permute-start | bytes 983048 | tf_op jit(solution)/shard_map/ppermute | solution.py:42
  69.1 304.6 %copy-start.44 = (pred[1280]{0:T(1024)(128)(4,1)}, pred[1280]{0:T(1024)(128)(4,1)S(1)}, u32[]{:S(2)}) copy-start(pred[1280]{0:T(1024)(128)(4,1)S(1)} %fusion.202) | copy-start | bytes 3844
  75.0 3.5 collective-permute-start.25
  76.4 2.2 collective-permute-start.21
  76.5 194.3 %copy-start.60 = (pred[512]{0:T(512)(128)(4,1)}, pred[512]{0:T(512)(128)(4,1)S(1)}, u32[]{:S(2)}) copy-start(pred[512]{0:T(512)(128)(4,1)S(1)} %fusion.224) | copy-start | bytes 1540
  76.5 299.6 %copy-start.47 = (pred[1280]{0:T(1024)(128)(4,1)}, pred[1280]{0:T(1024)(128)(4,1)S(1)}, u32[]{:S(2)}) copy-start(pred[1280]{0:T(1024)(128)(4,1)S(1)} %fusion.201) | copy-start | bytes 3844
  76.5 303.0 %collective-permute-start.28 = (bf16[10,128,128]{2,1,0:T(8,128)(2,1)}, bf16[10,128,128]{2,1,0:T(8,128)(2,1)}, u32[]{:S(2)}, u32[]{:S(2)}) collective-permute-start(bf16[10,128,128]{2,1,0:T(8,128)(2,1)} %collective-permute-done.24.refs_2_), channel_id=1, source_target_pairs={{8,0},{10,2},{16,8},{18,10},{24,16},{26,18},{28,24},{30,26},{20,28... | collective-permute-start | bytes 983048 | tf_op jit(solution)/shard_map/ppermute | solution.py:39
  78.1 304.1 %collective-permute-start.26 = (bf16[10,128,128]{2,1,0:T(8,128)(2,1)}, bf16[10,128,128]{2,1,0:T(8,128)(2,1)}, u32[]{:S(2)}, u32[]{:S(2)}) collective-permute-start(bf16[10,128,128]{2,1,0:T(8,128)(2,1)} %collective-permute-done.20.refs_2_), channel_id=1, source_target_pairs={{0,8},{2,10},{8,16},{10,18},{16,24},{18,26},{24,28},{26,30},{28,20... | collective-permute-start | bytes 983048 | tf_op jit(solution)/shard_map/ppermute | solution.py:38
  373.7 3.8 copy-start.11
  373.7 3.8 copy-start.24
  373.7 3.8 copy-start.61
  376.1 6.2 %copy-start.7 = (f32[5,60,1280]{2,1,0:T(8,128)}, f32[5,60,1280]{2,1,0:T(8,128)S(1)}, u32[]{:S(2)}) copy-start(f32[5,60,1280]{2,1,0:T(8,128)S(1)} %get-tuple-element.130) | copy-start | bytes 4608004
  379.5 4.0 copy-start.5
  379.6 4.0 collective-permute-start.29
  382.3 27.4 %collective-permute-start.27 = (bf16[10,128,128]{2,1,0:T(8,128)(2,1)}, bf16[10,128,128]{2,1,0:T(8,128)(2,1)}, u32[]{:S(2)}, u32[]{:S(2)}) collective-permute-start(bf16[10,128,128]{2,1,0:T(8,128)(2,1)} %collective-permute-done.26.refs_0_), channel_id=1, source_target_pairs={{0,2},{2,0},{4,6},{6,4},{8,10},{10,8},{12,14},{14,12},{16,18},{18,... | collective-permute-start | bytes 983048 | tf_op jit(solution)/shard_map/ppermute | solution.py:42
  430.7 3.8 copy-start.57
  430.7 3.8 copy-start.13
  430.7 3.8 copy-start.21
  430.7 3.8 copy-start.65
  441.7 8.9 %copy-start.4 = (f32[5,60,1280]{2,1,0:T(8,128)S(1)}, f32[5,60,1280]{2,1,0:T(8,128)}, u32[]{:S(2)}) copy-start(f32[5,60,1280]{2,1,0:T(8,128)} %get-tuple-element.140) | copy-start | bytes 4608004
  441.7 24.5 %slice-start = ((s8[13107200]{0:T(1024)(128)(4,1)}), s8[4194304]{0:T(1024)(128)(4,1)S(1)}, s32[]{:S(2)}) async-start(s8[13107200]{0:T(1024)(128)(4,1)} %bitcast.474), calls=%async_computation | async-start | bytes 8388608
  441.7 24.5 %slice-start.1 = ((s8[13107200]{0:T(1024)(128)(4,1)}), s8[4194304]{0:T(1024)(128)(4,1)S(1)}, s32[]{:S(2)}) async-start(s8[13107200]{0:T(1024)(128)(4,1)} %bitcast.474), calls=%async_computation.1 | async-start | bytes 8388608
  441.7 24.5 %slice-start.2 = ((s8[13107200]{0:T(1024)(128)(4,1)}), s8[4194304]{0:T(1024)(128)(4,1)S(1)}, s32[]{:S(2)}) async-start(s8[13107200]{0:T(1024)(128)(4,1)} %bitcast.474), calls=%async_computation.2 | async-start | bytes 8388608
  449.0 17.2 %collective-permute-start.30 = (bf16[60,5120]{1,0:T(8,128)(2,1)S(1)}, bf16[60,5120]{1,0:T(8,128)(2,1)S(1)}, u32[]{:S(2)}, u32[]{:S(2)}) collective-permute-start(bf16[60,5120]{1,0:T(8,128)(2,1)S(1)} %convolution_convert_fusion), channel_id=1, source_target_pairs={{0,1},{1,0},{2,3},{3,2},{4,5},{5,4},{6,7},{7,6},{8,9},{9,8},{10,11... | collective-permute-start | bytes 1843208 | tf_op jit(solution)/shard_map/ppermute | solution.py:191
  451.0 15.2 %slice-start.3 = ((s8[13107200]{0:T(1024)(128)(4,1)}), s8[524288]{0:T(1024)(128)(4,1)S(1)}, s32[]{:S(2)}) async-start(s8[13107200]{0:T(1024)(128)(4,1)} %bitcast.474), calls=%async_computation.3 | async-start | bytes 1048576
  453.2 13.0 %copy-start.25 = (bf16[60,5120]{1,0:T(8,128)(2,1)S(1)}, bf16[60,5120]{1,0:T(8,128)(2,1)}, u32[]{:S(2)}) copy-start(bf16[60,5120]{1,0:T(8,128)(2,1)} %param.10) | copy-start | bytes 1843204
  453.2 13.0 %copy-start.49 = (f32[5120]{0:T(1024)S(1)}, f32[5120]{0:T(1024)}, u32[]{:S(2)}) copy-start(f32[5120]{0:T(1024)} %param.14) | copy-start | bytes 61444
  (39 other events, 69.6 us)

commit v13 on v11

--- a/solution.py
+++ b/solution.py
@@ -126,8 +126,8 @@
         phases = [(0, known + 1), (known + 1, chips - 1), (chips - 1, chips)]
         phases = [(2 * lo, 2 * hi) for lo, hi in phases if hi > lo]
 
-        anchor = 2 * max(chips - 2, 0)
-        early = 2 * (chips - 1)
+        anchor = 2 * min(known + 1, chips - 1)
+        early = 2 * (known + 1)
         held_a, held_b, _ = lax.optimization_barrier(
             (got_a[:early], got_b[:early], (got_a[anchor], got_b[anchor]))
         )

time: 116 us -> 120 us (1.034)
  waiting for transfers between devices: 48.3 us -> 53.4 us
    ppermute x7, waiting for transfers between devices: 28.6 us -> 31.5 us  [gather_ring(): cur_a = lax.ppermute(cur_a, 'seq', forward)]
    ppermute x7, waiting for transfers between devices: 6.32 us -> 8.15 us  [gather_ring(): cur_b = lax.ppermute(cur_b, 'seq', backward)]
  transfers between devices with their start and end apart: 31 -> 31, of which waited for: 12 -> 17; matrix products, arithmetic and copies ran while one was open for 23% -> 13% of each run, Pallas kernels for 0% -> 0%
where the time goes in v13:
time: 120 us
  waiting for transfers between devices  53.4 us (44%)
  local copies, waits for them, and re-layouts  24.2 us (20%)
  starting transfers between devices  19 us (16%)
  matrix products  16.2 us (14%)
  other arithmetic  4.01 us (3%)
  between operations  2.66 us (2%)
    ppermute x7, waiting for transfers between devices, gather_ring(): cur_a = lax.ppermute(cur_a, 'seq', forward)  31.5 us
    ppermute x1, waiting for transfers between devices, on_device(): came = lax.ppermute(other, 'tp', [(0, 1), (1, 0)])  12.8 us
    ppermute x7, starting transfers between devices, gather_ring(): cur_a = lax.ppermute(cur_a, 'seq', forward)  12.1 us
    unnamed x68, local copies, waits for them, and re-layouts  11.5 us
    ppermute x7, waiting for transfers between devices, gather_ring(): cur_b = lax.ppermute(cur_b, 'seq', backward)  8.15 us
    another operation x37, local copies, waits for them, and re-layouts, on_device(): jnp.stack([g[0, rows_dev, :2] for g in heard]).astype(jnp.float32)  6.17 us
    dot_general x12, matrix products, attend_part(): jnp.einsum('hqd,hkd->hqk', queries_3d, keys, preferred_element_type=jnp.f...  6.09 us
    dot_general x12, matrix products, attend_part(): jnp.einsum('hqk,hkd->hqd', weights.astype(jnp.bfloat16), values, preferre...  4.29 us
  transfers between devices with their start and end apart: 31, of which 17 were waited for; matrix products, arithmetic and copies ran while one was open for 13% of the time, Pallas kernels for 0%

profile of v13, /device:TPU:0, one launch (start us, length us, event | category | flops | bytes accessed | tf_op | source)
XLA Modules:
  0.0 119.5 jit_solution(15795050274912155004)
XLA Ops:
  1.5 1.0 fusion.244
  2.5 1.0 fusion.243
  4.6 0.5 collective-permute-start
  5.1 2.6 %collective-permute-start.1 = (bf16[10,128,128]{2,1,0:T(8,128)(2,1)S(1)}, bf16[10,128,128]{2,1,0:T(8,128)(2,1)S(1)}, u32[]{:S(2)}, u32[]{:S(2)}) collective-permute-start(bf16[10,128,128]{2,1,0:T(8,128)(2,1)S(1)} %get-tuple-element.26), channel_id=1, source_target_pairs={{0,8},{2,10},{8,16},{10,18},{16,24},{18,26},{24,28},{26,30},{28,20... | collective-permute-start | bytes 983048 | tf_op jit(solution)/shard_map/ppermute | solution.py:36
  9.6 6.4 %collective-permute-done.1 = bf16[10,128,128]{2,1,0:T(8,128)(2,1)S(1)} collective-permute-done((bf16[10,128,128]{2,1,0:T(8,128)(2,1)S(1)}, bf16[10,128,128]{2,1,0:T(8,128)(2,1)S(1)}, u32[]{:S(2)}, u32[]{:S(2)}) %collective-permute-start.1) | collective-permute-done | bytes 327712 | tf_op jit(solution)/shard_map/ppermute | solution.py:36
  16.0 1.8 %collective-permute-start.3 = (bf16[10,128,128]{2,1,0:T(8,128)(2,1)S(1)}, bf16[10,128,128]{2,1,0:T(8,128)(2,1)S(1)}, u32[]{:S(2)}, u32[]{:S(2)}) collective-permute-start(bf16[10,128,128]{2,1,0:T(8,128)(2,1)S(1)} %collective-permute-done.1), channel_id=1, source_target_pairs={{0,8},{2,10},{8,16},{10,18},{16,24},{18,26},{24,28},{26,30},{28,20... | collective-permute-start | bytes 983048 | tf_op jit(solution)/shard_map/ppermute | solution.py:36
  18.6 0.5 collective-permute-start.11
  19.1 6.4 %collective-permute-done.3 = bf16[10,128,128]{2,1,0:T(8,128)(2,1)S(1)} collective-permute-done((bf16[10,128,128]{2,1,0:T(8,128)(2,1)S(1)}, bf16[10,128,128]{2,1,0:T(8,128)(2,1)S(1)}, u32[]{:S(2)}, u32[]{:S(2)}) %collective-permute-start.3) | collective-permute-done | bytes 327712 | tf_op jit(solution)/shard_map/ppermute | solution.py:36
  25.5 1.6 %collective-permute-start.5 = (bf16[10,128,128]{2,1,0:T(8,128)(2,1)S(1)}, bf16[10,128,128]{2,1,0:T(8,128)(2,1)S(1)}, u32[]{:S(2)}, u32[]{:S(2)}) collective-permute-start(bf16[10,128,128]{2,1,0:T(8,128)(2,1)S(1)} %collective-permute-done.3), channel_id=1, source_target_pairs={{0,8},{2,10},{8,16},{10,18},{16,24},{18,26},{24,28},{26,30},{28,20... | collective-permute-start | bytes 983048 | tf_op jit(solution)/shard_map/ppermute | solution.py:36
  27.5 0.7 slice_bitcast_fusion.5
  28.3 0.7 copy-done.3
  29.4 0.5 collective-permute-start.13
  29.9 4.3 %collective-permute-done.5 = bf16[10,128,128]{2,1,0:T(8,128)(2,1)S(1)} collective-permute-done((bf16[10,128,128]{2,1,0:T(8,128)(2,1)S(1)}, bf16[10,128,128]{2,1,0:T(8,128)(2,1)S(1)}, u32[]{:S(2)}, u32[]{:S(2)}) %collective-permute-start.5) | collective-permute-done | bytes 327712 | tf_op jit(solution)/shard_map/ppermute | solution.py:36
  34.2 1.4 %collective-permute-start.7 = (bf16[10,128,128]{2,1,0:T(8,128)(2,1)S(1)}, bf16[10,128,128]{2,1,0:T(8,128)(2,1)}, u32[]{:S(2)}, u32[]{:S(2)}) collective-permute-start(bf16[10,128,128]{2,1,0:T(8,128)(2,1)S(1)} %collective-permute-done.5), channel_id=1, source_target_pairs={{0,8},{2,10},{8,16},{10,18},{16,24},{18,26},{24,28},{26,30},{28,20... | collective-permute-start | bytes 983048 | tf_op jit(solution)/shard_map/ppermute | solution.py:36
  35.7 0.6 collective-permute-start.16
  36.3 0.7 slice_bitcast_fusion.3
  37.0 0.7 copy-done.1
  37.7 0.7 copy-done.7
  38.9 0.5 collective-permute-start.15
  39.4 2.8 %collective-permute-done.7 = bf16[10,128,128]{2,1,0:T(8,128)(2,1)} collective-permute-done((bf16[10,128,128]{2,1,0:T(8,128)(2,1)S(1)}, bf16[10,128,128]{2,1,0:T(8,128)(2,1)}, u32[]{:S(2)}, u32[]{:S(2)}) %collective-permute-start.7) | collective-permute-done | bytes 327712 | tf_op jit(solution)/shard_map/ppermute | solution.py:36
  42.2 0.7 slice_bitcast_fusion.10
  42.9 0.5 collective-permute-done.16
  43.4 0.7 slice_bitcast_fusion.1
  44.1 0.7 copy-done.5
  44.8 0.7 copy-done.9
  46.0 1.5 %collective-permute-start.18 = (bf16[10,128,128]{2,1,0:T(8,128)(2,1)}, bf16[10,128,128]{2,1,0:T(8,128)(2,1)}, u32[]{:S(2)}, u32[]{:S(2)}) collective-permute-start(bf16[10,128,128]{2,1,0:T(8,128)(2,1)} %collective-permute-done.7), channel_id=1, source_target_pairs={{0,8},{2,10},{8,16},{10,18},{16,24},{18,26},{24,28},{26,30},{28,20... | collective-permute-start | bytes 983048 | tf_op jit(solution)/shard_map/ppermute | solution.py:36
  47.5 0.5 collective-permute-start.19
  48.0 0.7 slice_bitcast_fusion.9
  48.8 0.7 slice_bitcast_fusion
  50.4 6.0 %collective-permute-done.18 = bf16[10,128,128]{2,1,0:T(8,128)(2,1)} collective-permute-done((bf16[10,128,128]{2,1,0:T(8,128)(2,1)}, bf16[10,128,128]{2,1,0:T(8,128)(2,1)}, u32[]{:S(2)}, u32[]{:S(2)}) %collective-permute-start.18) | collective-permute-done | bytes 327712 | tf_op jit(solution)/shard_map/ppermute | solution.py:36
  56.4 1.3 %collective-permute-done.19 = bf16[10,128,128]{2,1,0:T(8,128)(2,1)} collective-permute-done((bf16[10,128,128]{2,1,0:T(8,128)(2,1)}, bf16[10,128,128]{2,1,0:T(8,128)(2,1)}, u32[]{:S(2)}, u32[]{:S(2)}) %collective-permute-start.19) | collective-permute-done | bytes 327712 | tf_op jit(solution)/shard_map/ppermute | solution.py:37
  58.1 1.0 constant_dynamic-update-slice_fusion.21
  59.2 1.0 constant_dynamic-update-slice_fusion.19
  60.3 1.0 constant_dynamic-update-slice_fusion.17
  61.3 1.0 constant_dynamic-update-slice_fusion.16
  62.3 0.8 fusion.247
  63.1 0.8 fusion.252
  64.3 0.6 copy-done.2
  65.1 1.0 constant_dynamic-update-slice_fusion.1
  66.2 1.0 constant_dynamic-update-slice_fusion
  67.2 0.8 fusion.253
  68.0 0.8 fusion.258
  68.7 0.7 fusion.18
  69.4 0.7 fusion.16
  70.1 0.5 collective-permute-start.26
  70.6 1.0 constant_dynamic-update-slice_fusion.29
  71.7 1.6 %collective-permute-start.21 = (bf16[10,128,128]{2,1,0:T(8,128)(2,1)}, bf16[10,128,128]{2,1,0:T(8,128)(2,1)S(1)}, u32[]{:S(2)}, u32[]{:S(2)}) collective-permute-start(bf16[10,128,128]{2,1,0:T(8,128)(2,1)} %collective-permute-done.18), channel_id=1, source_target_pairs={{0,8},{2,10},{8,16},{10,18},{16,24},{18,26},{24,28},{26,30},{28,20... | collective-permute-start | bytes 983048 | tf_op jit(solution)/shard_map/ppermute | solution.py:36
  73.6 1.0 constant_dynamic-update-slice_fusion.13
  74.6 4.8 %collective-permute-done.26 = bf16[10,128,128]{2,1,0:T(8,128)(2,1)S(1)} collective-permute-done((bf16[10,128,128]{2,1,0:T(8,128)(2,1)}, bf16[10,128,128]{2,1,0:T(8,128)(2,1)S(1)}, u32[]{:S(2)}, u32[]{:S(2)}) %collective-permute-start.26) | collective-permute-done | bytes 327712 | tf_op jit(solution)/shard_map/ppermute | solution.py:37
  79.8 2.2 %collective-permute-done.21 = bf16[10,128,128]{2,1,0:T(8,128)(2,1)S(1)} collective-permute-done((bf16[10,128,128]{2,1,0:T(8,128)(2,1)}, bf16[10,128,128]{2,1,0:T(8,128)(2,1)S(1)}, u32[]{:S(2)}, u32[]{:S(2)}) %collective-permute-start.21) | collective-permute-done | bytes 327712 | tf_op jit(solution)/shard_map/ppermute | solution.py:36
  82.1 1.6 %collective-permute-start.23 = (bf16[10,128,128]{2,1,0:T(8,128)(2,1)S(1)}, bf16[10,128,128]{2,1,0:T(8,128)(2,1)S(1)}, u32[]{:S(2)}, u32[]{:S(2)}) collective-permute-start(bf16[10,128,128]{2,1,0:T(8,128)(2,1)S(1)} %collective-permute-done.21), channel_id=1, source_target_pairs={{0,8},{2,10},{8,16},{10,18},{16,24},{18,26},{24,28},{26,30},{28,20... | collective-permute-start | bytes 983048 | tf_op jit(solution)/shard_map/ppermute | solution.py:36
  83.9 0.4 fusion.250
  84.8 0.5 collective-permute-done.22
  86.2 1.3 %collective-permute-done.28 = bf16[10,128,128]{2,1,0:T(8,128)(2,1)S(1)} collective-permute-done((bf16[10,128,128]{2,1,0:T(8,128)(2,1)S(1)}, bf16[10,128,128]{2,1,0:T(8,128)(2,1)S(1)}, u32[]{:S(2)}, u32[]{:S(2)}) %collective-permute-start.28) | collective-permute-done | bytes 327712 | tf_op jit(solution)/shard_map/ppermute | solution.py:37
  88.0 3.4 %collective-permute-done.23 = bf16[10,128,128]{2,1,0:T(8,128)(2,1)S(1)} collective-permute-done((bf16[10,128,128]{2,1,0:T(8,128)(2,1)S(1)}, bf16[10,128,128]{2,1,0:T(8,128)(2,1)S(1)}, u32[]{:S(2)}, u32[]{:S(2)}) %collective-permute-start.23) | collective-permute-done | bytes 327712 | tf_op jit(solution)/shard_map/ppermute | solution.py:36
  92.5 0.5 collective-permute-done.24
  94.0 0.5 fusion.53
  95.6 0.5 fusion.41
  96.8 2.4 %convolution_convert_fusion = bf16[60,5120]{1,0:T(8,128)(2,1)S(1)} fusion(bf16[1280,5120]{1,0:T(8,128)(2,1)S(1)} %bitcast.475, bf16[60,640]{1,0:T(8,128)(2,1)S(1)} %bitcast.484, bf16[60,640]{1,0:T(8,128)(2,1)S(1)} %bitcast.485), kind=kOutput, calls=%fused_computation | convolution fusion | flops 787046400 | bytes 13875200 | tf_op jit(solution)/shard_map/dot_general | solution.py:160
  99.3 1.6 %collective-permute-start.30 = (bf16[60,5120]{1,0:T(8,128)(2,1)S(1)}, bf16[60,5120]{1,0:T(8,128)(2,1)S(1)}, u32[]{:S(2)}, u32[]{:S(2)}) collective-permute-start(bf16[60,5120]{1,0:T(8,128)(2,1)S(1)} %convolution_convert_fusion), channel_id=1, source_target_pairs={{0,1},{1,0},{2,3},{3,2},{4,5},{5,4},{6,7},{7,6},{8,9},{9,8},{10,11... | collective-permute-start | bytes 1843208 | tf_op jit(solution)/shard_map/ppermute | solution.py:162
  100.8 0.5 fusion.47
  101.3 0.5 fusion.35
  103.3 12.8 %collective-permute-done.30 = bf16[60,5120]{1,0:T(8,128)(2,1)S(1)} collective-permute-done((bf16[60,5120]{1,0:T(8,128)(2,1)S(1)}, bf16[60,5120]{1,0:T(8,128)(2,1)S(1)}, u32[]{:S(2)}, u32[]{:S(2)}) %collective-permute-start.30) | collective-permute-done | bytes 614432 | tf_op jit(solution)/shard_map/ppermute | solution.py:162
  116.1 3.4 %add_convert_fusion = bf16[60,5120]{1,0:T(8,128)(2,1)} fusion(bf16[60,5120]{1,0:T(8,128)(2,1)S(1)} %collective-permute-done.30, bf16[60,5120]{1,0:T(8,128)(2,1)S(1)} %copy-done, f32[5120]{0:T(1024)S(1)} %copy-done.12, bf16[1280,5120]{1,0:T(8,128)(2,1)S(1)} %bitcast.475, bf16[60,640]{1,0:T(8,128)(2,1)S(1)} %bitcast.486, bf16[60,640]{1,0:T(8,128)(2,1)S(1)} %bitcast.487), kind=kOutput, calls=%fused_computation.33 | convolution fusion | flops 788582400 | bytes 15124480 | tf_op jit(solution)/shard_map/dot_general | solution.py:164
  (188 shorter events, 15.3 us)
Async XLA Ops:
  3.8 4.3 %copy-start.11 = (bf16[120,1280]{1,0:T(8,128)(2,1)S(1)}, bf16[120,1280]{1,0:T(8,128)(2,1)}, u32[]{:S(2)}) copy-start(bf16[120,1280]{1,0:T(8,128)(2,1)} %param.11) | copy-start | bytes 921604
  4.6 13.6 %collective-permute-start = (bf16[10,128,128]{2,1,0:T(8,128)(2,1)S(1)}, bf16[10,128,128]{2,1,0:T(8,128)(2,1)S(1)}, u32[]{:S(2)}, u32[]{:S(2)}) collective-permute-start(bf16[10,128,128]{2,1,0:T(8,128)(2,1)S(1)} %get-tuple-element.26), channel_id=1, source_target_pairs={{0,2},{2,0},{4,6},{6,4},{8,10},{10,8},{12,14},{14,12},{16,18},{18,... | collective-permute-start | bytes 983048 | tf_op jit(solution)/shard_map/ppermute | solution.py:40
  5.1 10.9 %collective-permute-start.1 = (bf16[10,128,128]{2,1,0:T(8,128)(2,1)S(1)}, bf16[10,128,128]{2,1,0:T(8,128)(2,1)S(1)}, u32[]{:S(2)}, u32[]{:S(2)}) collective-permute-start(bf16[10,128,128]{2,1,0:T(8,128)(2,1)S(1)} %get-tuple-element.26), channel_id=1, source_target_pairs={{0,8},{2,10},{8,16},{10,18},{16,24},{18,26},{24,28},{26,30},{28,20... | collective-permute-start | bytes 983048 | tf_op jit(solution)/shard_map/ppermute | solution.py:36
  7.8 10.4 %collective-permute-start.9 = (bf16[10,128,128]{2,1,0:T(8,128)(2,1)S(1)}, bf16[10,128,128]{2,1,0:T(8,128)(2,1)S(1)}, u32[]{:S(2)}, u32[]{:S(2)}) collective-permute-start(bf16[10,128,128]{2,1,0:T(8,128)(2,1)S(1)} %get-tuple-element.36), channel_id=1, source_target_pairs={{0,2},{2,0},{4,6},{6,4},{8,10},{10,8},{12,14},{14,12},{16,18},{18,... | collective-permute-start | bytes 983048 | tf_op jit(solution)/shard_map/ppermute | solution.py:41
  7.9 10.0 %collective-permute-start.10 = (bf16[10,128,128]{2,1,0:T(8,128)(2,1)S(1)}, bf16[10,128,128]{2,1,0:T(8,128)(2,1)S(1)}, u32[]{:S(2)}, u32[]{:S(2)}) collective-permute-start(bf16[10,128,128]{2,1,0:T(8,128)(2,1)S(1)} %get-tuple-element.36), channel_id=1, source_target_pairs={{8,0},{10,2},{16,8},{18,10},{24,16},{26,18},{28,24},{30,26},{20,28... | collective-permute-start | bytes 983048 | tf_op jit(solution)/shard_map/ppermute | solution.py:37
  16.0 9.5 %collective-permute-start.3 = (bf16[10,128,128]{2,1,0:T(8,128)(2,1)S(1)}, bf16[10,128,128]{2,1,0:T(8,128)(2,1)S(1)}, u32[]{:S(2)}, u32[]{:S(2)}) collective-permute-start(bf16[10,128,128]{2,1,0:T(8,128)(2,1)S(1)} %collective-permute-done.1), channel_id=1, source_target_pairs={{0,8},{2,10},{8,16},{10,18},{16,24},{18,26},{24,28},{26,30},{28,20... | collective-permute-start | bytes 983048 | tf_op jit(solution)/shard_map/ppermute | solution.py:36
  17.9 9.3 %collective-permute-start.12 = (bf16[10,128,128]{2,1,0:T(8,128)(2,1)S(1)}, bf16[10,128,128]{2,1,0:T(8,128)(2,1)}, u32[]{:S(2)}, u32[]{:S(2)}) collective-permute-start(bf16[10,128,128]{2,1,0:T(8,128)(2,1)S(1)} %collective-permute-done.10), channel_id=1, source_target_pairs={{8,0},{10,2},{16,8},{18,10},{24,16},{26,18},{28,24},{30,26},{20,28... | collective-permute-start | bytes 983048 | tf_op jit(solution)/shard_map/ppermute | solution.py:37
  18.6 9.6 %collective-permute-start.2 = (bf16[10,128,128]{2,1,0:T(8,128)(2,1)S(1)}, bf16[10,128,128]{2,1,0:T(8,128)(2,1)S(1)}, u32[]{:S(2)}, u32[]{:S(2)}) collective-permute-start(bf16[10,128,128]{2,1,0:T(8,128)(2,1)S(1)} %collective-permute-done.1), channel_id=1, source_target_pairs={{0,2},{2,0},{4,6},{6,4},{8,10},{10,8},{12,14},{14,12},{16,18},{18,... | collective-permute-start | bytes 983048 | tf_op jit(solution)/shard_map/ppermute | solution.py:40
  18.6 9.6 %collective-permute-start.11 = (bf16[10,128,128]{2,1,0:T(8,128)(2,1)S(1)}, bf16[10,128,128]{2,1,0:T(8,128)(2,1)S(1)}, u32[]{:S(2)}, u32[]{:S(2)}) collective-permute-start(bf16[10,128,128]{2,1,0:T(8,128)(2,1)S(1)} %collective-permute-done.10), channel_id=1, source_target_pairs={{0,2},{2,0},{4,6},{6,4},{8,10},{10,8},{12,14},{14,12},{16,18},{18,... | collective-permute-start | bytes 983048 | tf_op jit(solution)/shard_map/ppermute | solution.py:41
  25.5 8.7 %collective-permute-start.5 = (bf16[10,128,128]{2,1,0:T(8,128)(2,1)S(1)}, bf16[10,128,128]{2,1,0:T(8,128)(2,1)S(1)}, u32[]{:S(2)}, u32[]{:S(2)}) collective-permute-start(bf16[10,128,128]{2,1,0:T(8,128)(2,1)S(1)} %collective-permute-done.3), channel_id=1, source_target_pairs={{0,8},{2,10},{8,16},{10,18},{16,24},{18,26},{24,28},{26,30},{28,20... | collective-permute-start | bytes 983048 | tf_op jit(solution)/shard_map/ppermute | solution.py:36
  27.2 8.6 %collective-permute-start.14 = (bf16[10,128,128]{2,1,0:T(8,128)(2,1)}, bf16[10,128,128]{2,1,0:T(8,128)(2,1)}, u32[]{:S(2)}, u32[]{:S(2)}) collective-permute-start(bf16[10,128,128]{2,1,0:T(8,128)(2,1)} %collective-permute-done.12), channel_id=1, source_target_pairs={{8,0},{10,2},{16,8},{18,10},{24,16},{26,18},{28,24},{30,26},{20,28... | collective-permute-start | bytes 983048 | tf_op jit(solution)/shard_map/ppermute | solution.py:37
  28.2 0.7 copy-start.3
  29.4 7.6 %collective-permute-start.4 = (bf16[10,128,128]{2,1,0:T(8,128)(2,1)S(1)}, bf16[10,128,128]{2,1,0:T(8,128)(2,1)S(1)}, u32[]{:S(2)}, u32[]{:S(2)}) collective-permute-start(bf16[10,128,128]{2,1,0:T(8,128)(2,1)S(1)} %collective-permute-done.3), channel_id=1, source_target_pairs={{0,2},{2,0},{4,6},{6,4},{8,10},{10,8},{12,14},{14,12},{16,18},{18,... | collective-permute-start | bytes 983048 | tf_op jit(solution)/shard_map/ppermute | solution.py:40
  29.4 8.3 %collective-permute-start.13 = (bf16[10,128,128]{2,1,0:T(8,128)(2,1)}, bf16[10,128,128]{2,1,0:T(8,128)(2,1)S(1)}, u32[]{:S(2)}, u32[]{:S(2)}) collective-permute-start(bf16[10,128,128]{2,1,0:T(8,128)(2,1)} %collective-permute-done.12), channel_id=1, source_target_pairs={{0,2},{2,0},{4,6},{6,4},{8,10},{10,8},{12,14},{14,12},{16,18},{18,... | collective-permute-start | bytes 983048 | tf_op jit(solution)/shard_map/ppermute | solution.py:41
  34.2 8.0 %collective-permute-start.7 = (bf16[10,128,128]{2,1,0:T(8,128)(2,1)S(1)}, bf16[10,128,128]{2,1,0:T(8,128)(2,1)}, u32[]{:S(2)}, u32[]{:S(2)}) collective-permute-start(bf16[10,128,128]{2,1,0:T(8,128)(2,1)S(1)} %collective-permute-done.5), channel_id=1, source_target_pairs={{0,8},{2,10},{8,16},{10,18},{16,24},{18,26},{24,28},{26,30},{28,20... | collective-permute-start | bytes 983048 | tf_op jit(solution)/shard_map/ppermute | solution.py:36
  35.7 7.6 %collective-permute-start.16 = (bf16[10,128,128]{2,1,0:T(8,128)(2,1)}, bf16[10,128,128]{2,1,0:T(8,128)(2,1)}, u32[]{:S(2)}, u32[]{:S(2)}) collective-permute-start(bf16[10,128,128]{2,1,0:T(8,128)(2,1)} %collective-permute-done.14), channel_id=1, source_target_pairs={{8,0},{10,2},{16,8},{18,10},{24,16},{26,18},{28,24},{30,26},{20,28... | collective-permute-start | bytes 983048 | tf_op jit(solution)/shard_map/ppermute | solution.py:37
  37.0 0.7 copy-start.1
  37.7 0.7 copy-start.7
  38.9 5.2 %collective-permute-start.6 = (bf16[10,128,128]{2,1,0:T(8,128)(2,1)S(1)}, bf16[10,128,128]{2,1,0:T(8,128)(2,1)S(1)}, u32[]{:S(2)}, u32[]{:S(2)}) collective-permute-start(bf16[10,128,128]{2,1,0:T(8,128)(2,1)S(1)} %collective-permute-done.5), channel_id=1, source_target_pairs={{0,2},{2,0},{4,6},{6,4},{8,10},{10,8},{12,14},{14,12},{16,18},{18,... | collective-permute-start | bytes 983048 | tf_op jit(solution)/shard_map/ppermute | solution.py:40
  38.9 5.9 %collective-permute-start.15 = (bf16[10,128,128]{2,1,0:T(8,128)(2,1)}, bf16[10,128,128]{2,1,0:T(8,128)(2,1)S(1)}, u32[]{:S(2)}, u32[]{:S(2)}) collective-permute-start(bf16[10,128,128]{2,1,0:T(8,128)(2,1)} %collective-permute-done.14), channel_id=1, source_target_pairs={{0,2},{2,0},{4,6},{6,4},{8,10},{10,8},{12,14},{14,12},{16,18},{18,... | collective-permute-start | bytes 983048 | tf_op jit(solution)/shard_map/ppermute | solution.py:41
  42.2 5.8 %collective-permute-start.8 = (bf16[10,128,128]{2,1,0:T(8,128)(2,1)}, bf16[10,128,128]{2,1,0:T(8,128)(2,1)}, u32[]{:S(2)}, u32[]{:S(2)}) collective-permute-start(bf16[10,128,128]{2,1,0:T(8,128)(2,1)} %collective-permute-done.7), channel_id=1, source_target_pairs={{0,2},{2,0},{4,6},{6,4},{8,10},{10,8},{12,14},{14,12},{16,18},{18,... | collective-permute-start | bytes 983048 | tf_op jit(solution)/shard_map/ppermute | solution.py:40
  43.4 5.4 %collective-permute-start.17 = (bf16[10,128,128]{2,1,0:T(8,128)(2,1)}, bf16[10,128,128]{2,1,0:T(8,128)(2,1)}, u32[]{:S(2)}, u32[]{:S(2)}) collective-permute-start(bf16[10,128,128]{2,1,0:T(8,128)(2,1)} %collective-permute-done.16), channel_id=1, source_target_pairs={{0,2},{2,0},{4,6},{6,4},{8,10},{10,8},{12,14},{14,12},{16,18},{18,... | collective-permute-start | bytes 983048 | tf_op jit(solution)/shard_map/ppermute | solution.py:41
  44.1 0.7 copy-start.5
  44.8 0.7 copy-start.9
  46.0 10.4 %collective-permute-start.18 = (bf16[10,128,128]{2,1,0:T(8,128)(2,1)}, bf16[10,128,128]{2,1,0:T(8,128)(2,1)}, u32[]{:S(2)}, u32[]{:S(2)}) collective-permute-start(bf16[10,128,128]{2,1,0:T(8,128)(2,1)} %collective-permute-done.7), channel_id=1, source_target_pairs={{0,8},{2,10},{8,16},{10,18},{16,24},{18,26},{24,28},{26,30},{28,20... | collective-permute-start | bytes 983048 | tf_op jit(solution)/shard_map/ppermute | solution.py:36
  47.5 10.2 %collective-permute-start.19 = (bf16[10,128,128]{2,1,0:T(8,128)(2,1)}, bf16[10,128,128]{2,1,0:T(8,128)(2,1)}, u32[]{:S(2)}, u32[]{:S(2)}) collective-permute-start(bf16[10,128,128]{2,1,0:T(8,128)(2,1)} %collective-permute-done.16), channel_id=1, source_target_pairs={{8,0},{10,2},{16,8},{18,10},{24,16},{26,18},{28,24},{30,26},{20,28... | collective-permute-start | bytes 983048 | tf_op jit(solution)/shard_map/ppermute | solution.py:37
  49.7 8.3 %copy-start.4 = (bf16[10,128,128]{2,1,0:T(8,128)(2,1)S(1)}, bf16[10,128,128]{2,1,0:T(8,128)(2,1)}, u32[]{:S(2)}) copy-start(bf16[10,128,128]{2,1,0:T(8,128)(2,1)} %copy-done.3) | copy-start | bytes 983044
  50.4 8.7 %copy-start.8 = (bf16[10,128,128]{2,1,0:T(8,128)(2,1)S(1)}, bf16[10,128,128]{2,1,0:T(8,128)(2,1)}, u32[]{:S(2)}) copy-start(bf16[10,128,128]{2,1,0:T(8,128)(2,1)} %copy-done.7) | copy-start | bytes 983044
  58.0 2.2 %copy-start.10 = (bf16[10,128,128]{2,1,0:T(8,128)(2,1)S(1)}, bf16[10,128,128]{2,1,0:T(8,128)(2,1)}, u32[]{:S(2)}) copy-start(bf16[10,128,128]{2,1,0:T(8,128)(2,1)} %copy-done.9) | copy-start | bytes 983044
  63.9 1.0 copy-start.2
  64.1 1.0 copy-start.6
  70.1 9.3 %collective-permute-start.26 = (bf16[10,128,128]{2,1,0:T(8,128)(2,1)}, bf16[10,128,128]{2,1,0:T(8,128)(2,1)S(1)}, u32[]{:S(2)}, u32[]{:S(2)}) collective-permute-start(bf16[10,128,128]{2,1,0:T(8,128)(2,1)} %collective-permute-done.19), channel_id=1, source_target_pairs={{8,0},{10,2},{16,8},{18,10},{24,16},{26,18},{28,24},{30,26},{20,28... | collective-permute-start | bytes 983048 | tf_op jit(solution)/shard_map/ppermute | solution.py:37
  71.7 12.0 %collective-permute-start.25 = (bf16[10,128,128]{2,1,0:T(8,128)(2,1)}, bf16[10,128,128]{2,1,0:T(8,128)(2,1)S(1)}, u32[]{:S(2)}, u32[]{:S(2)}) collective-permute-start(bf16[10,128,128]{2,1,0:T(8,128)(2,1)} %collective-permute-done.19), channel_id=1, source_target_pairs={{0,2},{2,0},{4,6},{6,4},{8,10},{10,8},{12,14},{14,12},{16,18},{18,... | collective-permute-start | bytes 983048 | tf_op jit(solution)/shard_map/ppermute | solution.py:41
  71.7 10.3 %collective-permute-start.21 = (bf16[10,128,128]{2,1,0:T(8,128)(2,1)}, bf16[10,128,128]{2,1,0:T(8,128)(2,1)S(1)}, u32[]{:S(2)}, u32[]{:S(2)}) collective-permute-start(bf16[10,128,128]{2,1,0:T(8,128)(2,1)} %collective-permute-done.18), channel_id=1, source_target_pairs={{0,8},{2,10},{8,16},{10,18},{16,24},{18,26},{24,28},{26,30},{28,20... | collective-permute-start | bytes 983048 | tf_op jit(solution)/shard_map/ppermute | solution.py:36
  73.4 10.4 %collective-permute-start.20 = (bf16[10,128,128]{2,1,0:T(8,128)(2,1)}, bf16[10,128,128]{2,1,0:T(8,128)(2,1)S(1)}, u32[]{:S(2)}, u32[]{:S(2)}) collective-permute-start(bf16[10,128,128]{2,1,0:T(8,128)(2,1)} %collective-permute-done.18), channel_id=1, source_target_pairs={{0,2},{2,0},{4,6},{6,4},{8,10},{10,8},{12,14},{14,12},{16,18},{18,... | collective-permute-start | bytes 983048 | tf_op jit(solution)/shard_map/ppermute | solution.py:40
  79.4 8.1 %collective-permute-start.28 = (bf16[10,128,128]{2,1,0:T(8,128)(2,1)S(1)}, bf16[10,128,128]{2,1,0:T(8,128)(2,1)S(1)}, u32[]{:S(2)}, u32[]{:S(2)}) collective-permute-start(bf16[10,128,128]{2,1,0:T(8,128)(2,1)S(1)} %collective-permute-done.26), channel_id=1, source_target_pairs={{8,0},{10,2},{16,8},{18,10},{24,16},{26,18},{28,24},{30,26},{20,28... | collective-permute-start | bytes 983048 | tf_op jit(solution)/shard_map/ppermute | solution.py:37
  79.8 4.1 %collective-permute-start.27 = (bf16[10,128,128]{2,1,0:T(8,128)(2,1)S(1)}, bf16[10,128,128]{2,1,0:T(8,128)(2,1)S(1)}, u32[]{:S(2)}, u32[]{:S(2)}) collective-permute-start(bf16[10,128,128]{2,1,0:T(8,128)(2,1)S(1)} %collective-permute-done.26), channel_id=1, source_target_pairs={{0,2},{2,0},{4,6},{6,4},{8,10},{10,8},{12,14},{14,12},{16,18},{18,... | collective-permute-start | bytes 983048 | tf_op jit(solution)/shard_map/ppermute | solution.py:41
  82.1 9.3 %collective-permute-start.23 = (bf16[10,128,128]{2,1,0:T(8,128)(2,1)S(1)}, bf16[10,128,128]{2,1,0:T(8,128)(2,1)S(1)}, u32[]{:S(2)}, u32[]{:S(2)}) collective-permute-start(bf16[10,128,128]{2,1,0:T(8,128)(2,1)S(1)} %collective-permute-done.21), channel_id=1, source_target_pairs={{0,8},{2,10},{8,16},{10,18},{16,24},{18,26},{24,28},{26,30},{28,20... | collective-permute-start | bytes 983048 | tf_op jit(solution)/shard_map/ppermute | solution.py:36
  83.7 1.6 %collective-permute-start.22 = (bf16[10,128,128]{2,1,0:T(8,128)(2,1)S(1)}, bf16[10,128,128]{2,1,0:T(8,128)(2,1)S(1)}, u32[]{:S(2)}, u32[]{:S(2)}) collective-permute-start(bf16[10,128,128]{2,1,0:T(8,128)(2,1)S(1)} %collective-permute-done.21), channel_id=1, source_target_pairs={{0,2},{2,0},{4,6},{6,4},{8,10},{10,8},{12,14},{14,12},{16,18},{18,... | collective-permute-start | bytes 983048 | tf_op jit(solution)/shard_map/ppermute | solution.py:40
  84.4 12.4 %slice-start = ((s8[13107200]{0:T(1024)(128)(4,1)}), s8[4194304]{0:T(1024)(128)(4,1)S(1)}, s32[]{:S(2)}) async-start(s8[13107200]{0:T(1024)(128)(4,1)} %bitcast.474), calls=%async_computation | async-start | bytes 8388608
  87.5 4.3 %collective-permute-start.29 = (bf16[10,128,128]{2,1,0:T(8,128)(2,1)S(1)}, bf16[10,128,128]{2,1,0:T(8,128)(2,1)S(1)}, u32[]{:S(2)}, u32[]{:S(2)}) collective-permute-start(bf16[10,128,128]{2,1,0:T(8,128)(2,1)S(1)} %collective-permute-done.28), channel_id=1, source_target_pairs={{0,2},{2,0},{4,6},{6,4},{8,10},{10,8},{12,14},{14,12},{16,18},{18,... | collective-permute-start | bytes 983048 | tf_op jit(solution)/shard_map/ppermute | solution.py:41
  91.3 1.6 %collective-permute-start.24 = (bf16[10,128,128]{2,1,0:T(8,128)(2,1)S(1)}, bf16[10,128,128]{2,1,0:T(8,128)(2,1)S(1)}, u32[]{:S(2)}, u32[]{:S(2)}) collective-permute-start(bf16[10,128,128]{2,1,0:T(8,128)(2,1)S(1)} %collective-permute-done.23), channel_id=1, source_target_pairs={{0,2},{2,0},{4,6},{6,4},{8,10},{10,8},{12,14},{14,12},{16,18},{18,... | collective-permute-start | bytes 983048 | tf_op jit(solution)/shard_map/ppermute | solution.py:40
  91.4 5.4 %slice-start.1 = ((s8[13107200]{0:T(1024)(128)(4,1)}), s8[4194304]{0:T(1024)(128)(4,1)S(1)}, s32[]{:S(2)}) async-start(s8[13107200]{0:T(1024)(128)(4,1)} %bitcast.474), calls=%async_computation.1 | async-start | bytes 8388608
  94.0 2.8 %slice-start.2 = ((s8[13107200]{0:T(1024)(128)(4,1)}), s8[4194304]{0:T(1024)(128)(4,1)S(1)}, s32[]{:S(2)}) async-start(s8[13107200]{0:T(1024)(128)(4,1)} %bitcast.474), calls=%async_computation.2 | async-start | bytes 8388608
  95.6 1.3 %slice-start.3 = ((s8[13107200]{0:T(1024)(128)(4,1)}), s8[524288]{0:T(1024)(128)(4,1)S(1)}, s32[]{:S(2)}) async-start(s8[13107200]{0:T(1024)(128)(4,1)} %bitcast.474), calls=%async_computation.3 | async-start | bytes 1048576
  99.3 16.8 %collective-permute-start.30 = (bf16[60,5120]{1,0:T(8,128)(2,1)S(1)}, bf16[60,5120]{1,0:T(8,128)(2,1)S(1)}, u32[]{:S(2)}, u32[]{:S(2)}) collective-permute-start(bf16[60,5120]{1,0:T(8,128)(2,1)S(1)} %convolution_convert_fusion), channel_id=1, source_target_pairs={{0,1},{1,0},{2,3},{3,2},{4,5},{5,4},{6,7},{7,6},{8,9},{9,8},{10,11... | collective-permute-start | bytes 1843208 | tf_op jit(solution)/shard_map/ppermute | solution.py:162
  102.6 13.5 %copy-start = (bf16[60,5120]{1,0:T(8,128)(2,1)S(1)}, bf16[60,5120]{1,0:T(8,128)(2,1)}, u32[]{:S(2)}) copy-start(bf16[60,5120]{1,0:T(8,128)(2,1)} %param.10) | copy-start | bytes 1843204
  102.6 13.5 %copy-start.12 = (f32[5120]{0:T(1024)S(1)}, f32[5120]{0:T(1024)}, u32[]{:S(2)}) copy-start(f32[5120]{0:T(1024)} %param.14) | copy-start | bytes 61444

commit v14 on v11

--- a/solution.py
+++ b/solution.py
@@ -162,6 +162,7 @@
         came = lax.ppermute(other, "tp", [(0, 1), (1, 0)])
         attention_own = attention_rows(side)
         own = jnp.dot(attention_own, out_weight, preferred_element_type=jnp.float32)
+        own = lax.optimization_barrier(own)
         summed = own + came.astype(jnp.float32)
         return (hidden.astype(jnp.float32) + gate_scale * summed).astype(jnp.bfloat16)
 

time: 116 us -> 113 us (0.974)
  waiting for transfers between devices: 48.3 us -> 45.3 us
    ppermute x1, waiting for transfers between devices: 13.3 us -> 10.3 us  [on_device(): came = lax.ppermute(other, 'tp', [(0, 1), (1, 0)])]
  transfers between devices with their start and end apart: 31 -> 31, of which waited for: 12 -> 12; matrix products, arithmetic and copies ran while one was open for 23% -> 27% of each run, Pallas kernels for 0% -> 0%
where the time goes in v14:
time: 113 us; the launch traced here: 112 us
  waiting for transfers between devices  45.3 us (40%)
  local copies, waits for them, and re-layouts  24.2 us (21%)
  starting transfers between devices  19.6 us (17%)
  matrix products  15.4 us (14%)
  other arithmetic  5.11 us (5%)
  between operations  2.69 us (2%)
    ppermute x7, waiting for transfers between devices, gather_ring(): cur_a = lax.ppermute(cur_a, 'seq', forward)  28.6 us
    ppermute x7, starting transfers between devices, gather_ring(): cur_a = lax.ppermute(cur_a, 'seq', forward)  12.2 us
    unnamed x68, local copies, waits for them, and re-layouts  11.5 us
    ppermute x1, waiting for transfers between devices, on_device(): came = lax.ppermute(other, 'tp', [(0, 1), (1, 0)])  10.3 us
    ppermute x7, waiting for transfers between devices, gather_ring(): cur_b = lax.ppermute(cur_b, 'seq', backward)  6.32 us
    another operation x37, local copies, waits for them, and re-layouts, on_device(): jnp.stack([g[0, rows_dev, :2] for g in heard]).astype(jnp.float32)  6.16 us
    dot_general x12, matrix products, attend_part(): jnp.einsum('hqd,hkd->hqk', queries_3d, keys, preferred_element_type=jnp.f...  6.1 us
    dot_general x12, matrix products, attend_part(): jnp.einsum('hqk,hkd->hqd', weights.astype(jnp.bfloat16), values, preferre...  4.5 us
  transfers between devices with their start and end apart: 31, of which 12 were waited for; matrix products, arithmetic and copies ran while one was open for 27% of the time, Pallas kernels for 0%

profile of v14, /device:TPU:0, one launch (start us, length us, event | category | flops | bytes accessed | tf_op | source)
XLA Modules:
  0.0 112.2 jit_solution(1574031710557864245)
XLA Ops:
  0.0 1.0 fusion.249
  1.0 1.0 fusion.250
  4.6 3.1 %collective-permute-start.1 = (bf16[10,128,128]{2,1,0:T(8,128)(2,1)S(1)}, bf16[10,128,128]{2,1,0:T(8,128)(2,1)S(1)}, u32[]{:S(2)}, u32[]{:S(2)}) collective-permute-start(bf16[10,128,128]{2,1,0:T(8,128)(2,1)S(1)} %get-tuple-element.34), channel_id=1, source_target_pairs={{0,8},{2,10},{8,16},{10,18},{16,24},{18,26},{24,28},{26,30},{28,20... | collective-permute-start | bytes 983048 | tf_op jit(solution)/shard_map/ppermute | solution.py:36
  9.7 5.7 %collective-permute-done.1 = bf16[10,128,128]{2,1,0:T(8,128)(2,1)S(1)} collective-permute-done((bf16[10,128,128]{2,1,0:T(8,128)(2,1)S(1)}, bf16[10,128,128]{2,1,0:T(8,128)(2,1)S(1)}, u32[]{:S(2)}, u32[]{:S(2)}) %collective-permute-start.1) | collective-permute-done | bytes 327712 | tf_op jit(solution)/shard_map/ppermute | solution.py:36
  15.3 1.8 %collective-permute-start.3 = (bf16[10,128,128]{2,1,0:T(8,128)(2,1)S(1)}, bf16[10,128,128]{2,1,0:T(8,128)(2,1)}, u32[]{:S(2)}, u32[]{:S(2)}) collective-permute-start(bf16[10,128,128]{2,1,0:T(8,128)(2,1)S(1)} %collective-permute-done.1), channel_id=1, source_target_pairs={{0,8},{2,10},{8,16},{10,18},{16,24},{18,26},{24,28},{26,30},{28,20... | collective-permute-start | bytes 983048 | tf_op jit(solution)/shard_map/ppermute | solution.py:36
  17.1 0.7 collective-permute-done.10
  18.6 0.5 collective-permute-start.2
  19.1 5.3 %collective-permute-done.3 = bf16[10,128,128]{2,1,0:T(8,128)(2,1)} collective-permute-done((bf16[10,128,128]{2,1,0:T(8,128)(2,1)S(1)}, bf16[10,128,128]{2,1,0:T(8,128)(2,1)}, u32[]{:S(2)}, u32[]{:S(2)}) %collective-permute-start.3) | collective-permute-done | bytes 327712 | tf_op jit(solution)/shard_map/ppermute | solution.py:36
  24.3 1.5 %collective-permute-start.5 = (bf16[10,128,128]{2,1,0:T(8,128)(2,1)}, bf16[10,128,128]{2,1,0:T(8,128)(2,1)}, u32[]{:S(2)}, u32[]{:S(2)}) collective-permute-start(bf16[10,128,128]{2,1,0:T(8,128)(2,1)} %collective-permute-done.3), channel_id=1, source_target_pairs={{0,8},{2,10},{8,16},{10,18},{16,24},{18,26},{24,28},{26,30},{28,20... | collective-permute-start | bytes 983048 | tf_op jit(solution)/shard_map/ppermute | solution.py:36
  25.8 0.7 slice_bitcast_fusion.14
  26.5 0.6 collective-permute-done.12
  27.6 0.7 copy-done.5
  28.7 0.5 collective-permute-start.4
  29.2 3.4 %collective-permute-done.5 = bf16[10,128,128]{2,1,0:T(8,128)(2,1)} collective-permute-done((bf16[10,128,128]{2,1,0:T(8,128)(2,1)}, bf16[10,128,128]{2,1,0:T(8,128)(2,1)}, u32[]{:S(2)}, u32[]{:S(2)}) %collective-permute-start.5) | collective-permute-done | bytes 327712 | tf_op jit(solution)/shard_map/ppermute | solution.py:36
  32.6 1.2 %collective-permute-start.7 = (bf16[10,128,128]{2,1,0:T(8,128)(2,1)}, bf16[10,128,128]{2,1,0:T(8,128)(2,1)}, u32[]{:S(2)}, u32[]{:S(2)}) collective-permute-start(bf16[10,128,128]{2,1,0:T(8,128)(2,1)} %collective-permute-done.5), channel_id=1, source_target_pairs={{0,8},{2,10},{8,16},{10,18},{16,24},{18,26},{24,28},{26,30},{28,20... | collective-permute-start | bytes 983048 | tf_op jit(solution)/shard_map/ppermute | solution.py:36
  33.8 0.7 slice_bitcast_fusion.12
  34.5 1.1 collective-permute-done.14
  35.6 0.5 collective-permute-start.16
  36.2 0.7 copy-done.7
  36.9 0.7 copy-done.1
  38.0 0.5 collective-permute-start.6
  38.5 1.5 %collective-permute-done.7 = bf16[10,128,128]{2,1,0:T(8,128)(2,1)} collective-permute-done((bf16[10,128,128]{2,1,0:T(8,128)(2,1)}, bf16[10,128,128]{2,1,0:T(8,128)(2,1)}, u32[]{:S(2)}, u32[]{:S(2)}) %collective-permute-start.7) | collective-permute-done | bytes 327712 | tf_op jit(solution)/shard_map/ppermute | solution.py:36
  40.0 0.7 slice_bitcast_fusion.10
  40.7 2.5 %collective-permute-done.16 = bf16[10,128,128]{2,1,0:T(8,128)(2,1)} collective-permute-done((bf16[10,128,128]{2,1,0:T(8,128)(2,1)S(1)}, bf16[10,128,128]{2,1,0:T(8,128)(2,1)}, u32[]{:S(2)}, u32[]{:S(2)}) %collective-permute-start.16) | collective-permute-done | bytes 327712 | tf_op jit(solution)/shard_map/ppermute | solution.py:37
  43.2 0.7 slice_bitcast_fusion.1
  43.9 0.7 copy-done.9
  44.6 0.7 copy-done.3
  45.8 1.6 %collective-permute-start.18 = (bf16[10,128,128]{2,1,0:T(8,128)(2,1)}, bf16[10,128,128]{2,1,0:T(8,128)(2,1)}, u32[]{:S(2)}, u32[]{:S(2)}) collective-permute-start(bf16[10,128,128]{2,1,0:T(8,128)(2,1)} %collective-permute-done.7), channel_id=1, source_target_pairs={{0,8},{2,10},{8,16},{10,18},{16,24},{18,26},{24,28},{26,30},{28,20... | collective-permute-start | bytes 983048 | tf_op jit(solution)/shard_map/ppermute | solution.py:36
  47.4 0.4 collective-permute-start.22
  47.9 0.7 slice_bitcast_fusion.9
  48.6 0.7 slice_bitcast_fusion
  50.2 6.0 %collective-permute-done.18 = bf16[10,128,128]{2,1,0:T(8,128)(2,1)} collective-permute-done((bf16[10,128,128]{2,1,0:T(8,128)(2,1)}, bf16[10,128,128]{2,1,0:T(8,128)(2,1)}, u32[]{:S(2)}, u32[]{:S(2)}) %collective-permute-start.18) | collective-permute-done | bytes 327712 | tf_op jit(solution)/shard_map/ppermute | solution.py:36
  56.3 1.6 %collective-permute-start.20 = (bf16[10,128,128]{2,1,0:T(8,128)(2,1)}, bf16[10,128,128]{2,1,0:T(8,128)(2,1)S(1)}, u32[]{:S(2)}, u32[]{:S(2)}) collective-permute-start(bf16[10,128,128]{2,1,0:T(8,128)(2,1)} %collective-permute-done.18), channel_id=1, source_target_pairs={{0,8},{2,10},{8,16},{10,18},{16,24},{18,26},{24,28},{26,30},{28,20... | collective-permute-start | bytes 983048 | tf_op jit(solution)/shard_map/ppermute | solution.py:36
  57.9 0.4 collective-permute-start.24
  58.5 0.5 collective-permute-start.23
  59.1 6.7 %collective-permute-done.20 = bf16[10,128,128]{2,1,0:T(8,128)(2,1)S(1)} collective-permute-done((bf16[10,128,128]{2,1,0:T(8,128)(2,1)}, bf16[10,128,128]{2,1,0:T(8,128)(2,1)S(1)}, u32[]{:S(2)}, u32[]{:S(2)}) %collective-permute-start.20) | collective-permute-done | bytes 327712 | tf_op jit(solution)/shard_map/ppermute | solution.py:36
  65.8 1.4 %collective-permute-done.24 = bf16[10,128,128]{2,1,0:T(8,128)(2,1)S(1)} collective-permute-done((bf16[10,128,128]{2,1,0:T(8,128)(2,1)}, bf16[10,128,128]{2,1,0:T(8,128)(2,1)S(1)}, u32[]{:S(2)}, u32[]{:S(2)}) %collective-permute-start.24) | collective-permute-done | bytes 327712 | tf_op jit(solution)/shard_map/ppermute | solution.py:37
  67.3 1.6 %collective-permute-start.26 = (bf16[10,128,128]{2,1,0:T(8,128)(2,1)S(1)}, bf16[10,128,128]{2,1,0:T(8,128)(2,1)S(1)}, u32[]{:S(2)}, u32[]{:S(2)}) collective-permute-start(bf16[10,128,128]{2,1,0:T(8,128)(2,1)S(1)} %collective-permute-done.20), channel_id=1, source_target_pairs={{0,8},{2,10},{8,16},{10,18},{16,24},{18,26},{24,28},{26,30},{28,20... | collective-permute-start | bytes 983048 | tf_op jit(solution)/shard_map/ppermute | solution.py:36
  68.9 0.5 collective-permute-start.28
  69.6 1.0 constant_dynamic-update-slice_fusion.5
  70.7 1.0 constant_dynamic-update-slice_fusion.3
  71.8 1.0 constant_dynamic-update-slice_fusion.1
  72.8 1.0 constant_dynamic-update-slice_fusion
  73.8 0.8 fusion.264
  74.6 0.8 fusion.263
  75.4 1.0 constant_dynamic-update-slice_fusion.13
  77.4 1.0 constant_dynamic-update-slice_fusion.29
  79.7 0.7 copy-done.2
  80.6 1.0 constant_dynamic-update-slice_fusion.17
  81.6 0.7 fusion.20
  83.1 1.0 constant_dynamic-update-slice_fusion.16
  84.2 0.8 fusion.258
  85.1 0.8 fusion.257
  85.9 0.6 collective-permute-start.29
  86.5 0.7 fusion.22
  89.2 0.5 fusion.47
  90.8 0.5 fusion.65
  91.8 2.4 %convolution_convert_fusion = bf16[60,5120]{1,0:T(8,128)(2,1)S(1)} fusion(bf16[1280,5120]{1,0:T(8,128)(2,1)S(1)} %bitcast.475, bf16[60,640]{1,0:T(8,128)(2,1)S(1)} %bitcast.486, bf16[60,640]{1,0:T(8,128)(2,1)S(1)} %bitcast.485), kind=kOutput, calls=%fused_computation | convolution fusion | flops 787046400 | bytes 13875200 | tf_op jit(solution)/shard_map/dot_general | solution.py:160
  94.2 1.6 %collective-permute-start.30 = (bf16[60,5120]{1,0:T(8,128)(2,1)S(1)}, bf16[60,5120]{1,0:T(8,128)(2,1)S(1)}, u32[]{:S(2)}, u32[]{:S(2)}) collective-permute-start(bf16[60,5120]{1,0:T(8,128)(2,1)S(1)} %convolution_convert_fusion), channel_id=1, source_target_pairs={{0,1},{1,0},{2,3},{3,2},{4,5},{5,4},{6,7},{7,6},{8,9},{9,8},{10,11... | collective-permute-start | bytes 1843208 | tf_op jit(solution)/shard_map/ppermute | solution.py:162
  96.0 0.7 fusion.38
  97.5 0.5 fusion.56
  98.4 2.4 %fusion.156 = f32[60,5120]{1,0:T(8,128)S(1)} fusion(bf16[1280,5120]{1,0:T(8,128)(2,1)S(1)} %bitcast.475, bf16[60,640]{1,0:T(8,128)(2,1)S(1)} %bitcast.487, bf16[60,640]{1,0:T(8,128)(2,1)S(1)} %bitcast.484), kind=kOutput, calls=%fused_computation.158 | convolution fusion | flops 786739200 | bytes 14489600 | tf_op jit(solution)/shard_map/dot_general | solution.py:164
  100.8 10.3 %collective-permute-done.30 = bf16[60,5120]{1,0:T(8,128)(2,1)S(1)} collective-permute-done((bf16[60,5120]{1,0:T(8,128)(2,1)S(1)}, bf16[60,5120]{1,0:T(8,128)(2,1)S(1)}, u32[]{:S(2)}, u32[]{:S(2)}) %collective-permute-start.30) | collective-permute-done | bytes 614432 | tf_op jit(solution)/shard_map/ppermute | solution.py:162
  111.1 1.1 add_convert_fusion
  (189 shorter events, 14.9 us)
Async XLA Ops:
  2.4 5.9 %copy-start.11 = (bf16[120,1280]{1,0:T(8,128)(2,1)S(1)}, bf16[120,1280]{1,0:T(8,128)(2,1)}, u32[]{:S(2)}) copy-start(bf16[120,1280]{1,0:T(8,128)(2,1)} %param.11) | copy-start | bytes 921604
  4.6 10.7 %collective-permute-start.1 = (bf16[10,128,128]{2,1,0:T(8,128)(2,1)S(1)}, bf16[10,128,128]{2,1,0:T(8,128)(2,1)S(1)}, u32[]{:S(2)}, u32[]{:S(2)}) collective-permute-start(bf16[10,128,128]{2,1,0:T(8,128)(2,1)S(1)} %get-tuple-element.34), channel_id=1, source_target_pairs={{0,8},{2,10},{8,16},{10,18},{16,24},{18,26},{24,28},{26,30},{28,20... | collective-permute-start | bytes 983048 | tf_op jit(solution)/shard_map/ppermute | solution.py:36
  7.7 10.4 %collective-permute-start = (bf16[10,128,128]{2,1,0:T(8,128)(2,1)S(1)}, bf16[10,128,128]{2,1,0:T(8,128)(2,1)S(1)}, u32[]{:S(2)}, u32[]{:S(2)}) collective-permute-start(bf16[10,128,128]{2,1,0:T(8,128)(2,1)S(1)} %get-tuple-element.34), channel_id=1, source_target_pairs={{0,2},{2,0},{4,6},{6,4},{8,10},{10,8},{12,14},{14,12},{16,18},{18,... | collective-permute-start | bytes 983048 | tf_op jit(solution)/shard_map/ppermute | solution.py:40
  7.7 10.1 %collective-permute-start.10 = (bf16[10,128,128]{2,1,0:T(8,128)(2,1)S(1)}, bf16[10,128,128]{2,1,0:T(8,128)(2,1)S(1)}, u32[]{:S(2)}, u32[]{:S(2)}) collective-permute-start(bf16[10,128,128]{2,1,0:T(8,128)(2,1)S(1)} %get-tuple-element.48), channel_id=1, source_target_pairs={{8,0},{10,2},{16,8},{18,10},{24,16},{26,18},{28,24},{30,26},{20,28... | collective-permute-start | bytes 983048 | tf_op jit(solution)/shard_map/ppermute | solution.py:37
  7.8 10.3 %collective-permute-start.9 = (bf16[10,128,128]{2,1,0:T(8,128)(2,1)S(1)}, bf16[10,128,128]{2,1,0:T(8,128)(2,1)S(1)}, u32[]{:S(2)}, u32[]{:S(2)}) collective-permute-start(bf16[10,128,128]{2,1,0:T(8,128)(2,1)S(1)} %get-tuple-element.48), channel_id=1, source_target_pairs={{0,2},{2,0},{4,6},{6,4},{8,10},{10,8},{12,14},{14,12},{16,18},{18,... | collective-permute-start | bytes 983048 | tf_op jit(solution)/shard_map/ppermute | solution.py:41
  15.3 9.0 %collective-permute-start.3 = (bf16[10,128,128]{2,1,0:T(8,128)(2,1)S(1)}, bf16[10,128,128]{2,1,0:T(8,128)(2,1)}, u32[]{:S(2)}, u32[]{:S(2)}) collective-permute-start(bf16[10,128,128]{2,1,0:T(8,128)(2,1)S(1)} %collective-permute-done.1), channel_id=1, source_target_pairs={{0,8},{2,10},{8,16},{10,18},{16,24},{18,26},{24,28},{26,30},{28,20... | collective-permute-start | bytes 983048 | tf_op jit(solution)/shard_map/ppermute | solution.py:36
  17.8 9.3 %collective-permute-start.12 = (bf16[10,128,128]{2,1,0:T(8,128)(2,1)S(1)}, bf16[10,128,128]{2,1,0:T(8,128)(2,1)S(1)}, u32[]{:S(2)}, u32[]{:S(2)}) collective-permute-start(bf16[10,128,128]{2,1,0:T(8,128)(2,1)S(1)} %collective-permute-done.10), channel_id=1, source_target_pairs={{8,0},{10,2},{16,8},{18,10},{24,16},{26,18},{28,24},{30,26},{20,28... | collective-permute-start | bytes 983048 | tf_op jit(solution)/shard_map/ppermute | solution.py:37
  18.5 9.0 %collective-permute-start.11 = (bf16[10,128,128]{2,1,0:T(8,128)(2,1)S(1)}, bf16[10,128,128]{2,1,0:T(8,128)(2,1)S(1)}, u32[]{:S(2)}, u32[]{:S(2)}) collective-permute-start(bf16[10,128,128]{2,1,0:T(8,128)(2,1)S(1)} %collective-permute-done.10), channel_id=1, source_target_pairs={{0,2},{2,0},{4,6},{6,4},{8,10},{10,8},{12,14},{14,12},{16,18},{18,... | collective-permute-start | bytes 983048 | tf_op jit(solution)/shard_map/ppermute | solution.py:41
  18.6 9.0 %collective-permute-start.2 = (bf16[10,128,128]{2,1,0:T(8,128)(2,1)S(1)}, bf16[10,128,128]{2,1,0:T(8,128)(2,1)S(1)}, u32[]{:S(2)}, u32[]{:S(2)}) collective-permute-start(bf16[10,128,128]{2,1,0:T(8,128)(2,1)S(1)} %collective-permute-done.1), channel_id=1, source_target_pairs={{0,2},{2,0},{4,6},{6,4},{8,10},{10,8},{12,14},{14,12},{16,18},{18,... | collective-permute-start | bytes 983048 | tf_op jit(solution)/shard_map/ppermute | solution.py:40
  24.3 8.3 %collective-permute-start.5 = (bf16[10,128,128]{2,1,0:T(8,128)(2,1)}, bf16[10,128,128]{2,1,0:T(8,128)(2,1)}, u32[]{:S(2)}, u32[]{:S(2)}) collective-permute-start(bf16[10,128,128]{2,1,0:T(8,128)(2,1)} %collective-permute-done.3), channel_id=1, source_target_pairs={{0,8},{2,10},{8,16},{10,18},{16,24},{18,26},{24,28},{26,30},{28,20... | collective-permute-start | bytes 983048 | tf_op jit(solution)/shard_map/ppermute | solution.py:36
  27.2 8.5 %collective-permute-start.14 = (bf16[10,128,128]{2,1,0:T(8,128)(2,1)S(1)}, bf16[10,128,128]{2,1,0:T(8,128)(2,1)S(1)}, u32[]{:S(2)}, u32[]{:S(2)}) collective-permute-start(bf16[10,128,128]{2,1,0:T(8,128)(2,1)S(1)} %collective-permute-done.12), channel_id=1, source_target_pairs={{8,0},{10,2},{16,8},{18,10},{24,16},{26,18},{28,24},{30,26},{20,28... | collective-permute-start | bytes 983048 | tf_op jit(solution)/shard_map/ppermute | solution.py:37
  27.6 0.7 copy-start.5
  28.7 7.4 %collective-permute-start.13 = (bf16[10,128,128]{2,1,0:T(8,128)(2,1)S(1)}, bf16[10,128,128]{2,1,0:T(8,128)(2,1)S(1)}, u32[]{:S(2)}, u32[]{:S(2)}) collective-permute-start(bf16[10,128,128]{2,1,0:T(8,128)(2,1)S(1)} %collective-permute-done.12), channel_id=1, source_target_pairs={{0,2},{2,0},{4,6},{6,4},{8,10},{10,8},{12,14},{14,12},{16,18},{18,... | collective-permute-start | bytes 983048 | tf_op jit(solution)/shard_map/ppermute | solution.py:41
  28.7 7.4 %collective-permute-start.4 = (bf16[10,128,128]{2,1,0:T(8,128)(2,1)}, bf16[10,128,128]{2,1,0:T(8,128)(2,1)S(1)}, u32[]{:S(2)}, u32[]{:S(2)}) collective-permute-start(bf16[10,128,128]{2,1,0:T(8,128)(2,1)} %collective-permute-done.3), channel_id=1, source_target_pairs={{0,2},{2,0},{4,6},{6,4},{8,10},{10,8},{12,14},{14,12},{16,18},{18,... | collective-permute-start | bytes 983048 | tf_op jit(solution)/shard_map/ppermute | solution.py:40
  32.6 7.4 %collective-permute-start.7 = (bf16[10,128,128]{2,1,0:T(8,128)(2,1)}, bf16[10,128,128]{2,1,0:T(8,128)(2,1)}, u32[]{:S(2)}, u32[]{:S(2)}) collective-permute-start(bf16[10,128,128]{2,1,0:T(8,128)(2,1)} %collective-permute-done.5), channel_id=1, source_target_pairs={{0,8},{2,10},{8,16},{10,18},{16,24},{18,26},{24,28},{26,30},{28,20... | collective-permute-start | bytes 983048 | tf_op jit(solution)/shard_map/ppermute | solution.py:36
  35.6 7.6 %collective-permute-start.16 = (bf16[10,128,128]{2,1,0:T(8,128)(2,1)S(1)}, bf16[10,128,128]{2,1,0:T(8,128)(2,1)}, u32[]{:S(2)}, u32[]{:S(2)}) collective-permute-start(bf16[10,128,128]{2,1,0:T(8,128)(2,1)S(1)} %collective-permute-done.14), channel_id=1, source_target_pairs={{8,0},{10,2},{16,8},{18,10},{24,16},{26,18},{28,24},{30,26},{20,28... | collective-permute-start | bytes 983048 | tf_op jit(solution)/shard_map/ppermute | solution.py:37
  36.2 0.7 copy-start.7
  36.9 0.7 copy-start.1
  38.0 5.9 %collective-permute-start.15 = (bf16[10,128,128]{2,1,0:T(8,128)(2,1)S(1)}, bf16[10,128,128]{2,1,0:T(8,128)(2,1)S(1)}, u32[]{:S(2)}, u32[]{:S(2)}) collective-permute-start(bf16[10,128,128]{2,1,0:T(8,128)(2,1)S(1)} %collective-permute-done.14), channel_id=1, source_target_pairs={{0,2},{2,0},{4,6},{6,4},{8,10},{10,8},{12,14},{14,12},{16,18},{18,... | collective-permute-start | bytes 983048 | tf_op jit(solution)/shard_map/ppermute | solution.py:41
  38.0 5.9 %collective-permute-start.6 = (bf16[10,128,128]{2,1,0:T(8,128)(2,1)}, bf16[10,128,128]{2,1,0:T(8,128)(2,1)S(1)}, u32[]{:S(2)}, u32[]{:S(2)}) collective-permute-start(bf16[10,128,128]{2,1,0:T(8,128)(2,1)} %collective-permute-done.5), channel_id=1, source_target_pairs={{0,2},{2,0},{4,6},{6,4},{8,10},{10,8},{12,14},{14,12},{16,18},{18,... | collective-permute-start | bytes 983048 | tf_op jit(solution)/shard_map/ppermute | solution.py:40
  40.0 7.8 %collective-permute-start.8 = (bf16[10,128,128]{2,1,0:T(8,128)(2,1)}, bf16[10,128,128]{2,1,0:T(8,128)(2,1)}, u32[]{:S(2)}, u32[]{:S(2)}) collective-permute-start(bf16[10,128,128]{2,1,0:T(8,128)(2,1)} %collective-permute-done.7), channel_id=1, source_target_pairs={{0,2},{2,0},{4,6},{6,4},{8,10},{10,8},{12,14},{14,12},{16,18},{18,... | collective-permute-start | bytes 983048 | tf_op jit(solution)/shard_map/ppermute | solution.py:40
  43.2 5.4 %collective-permute-start.17 = (bf16[10,128,128]{2,1,0:T(8,128)(2,1)}, bf16[10,128,128]{2,1,0:T(8,128)(2,1)}, u32[]{:S(2)}, u32[]{:S(2)}) collective-permute-start(bf16[10,128,128]{2,1,0:T(8,128)(2,1)} %collective-permute-done.16), channel_id=1, source_target_pairs={{0,2},{2,0},{4,6},{6,4},{8,10},{10,8},{12,14},{14,12},{16,18},{18,... | collective-permute-start | bytes 983048 | tf_op jit(solution)/shard_map/ppermute | solution.py:41
  43.9 0.7 copy-start.9
  44.6 0.7 copy-start.3
  45.8 10.4 %collective-permute-start.18 = (bf16[10,128,128]{2,1,0:T(8,128)(2,1)}, bf16[10,128,128]{2,1,0:T(8,128)(2,1)}, u32[]{:S(2)}, u32[]{:S(2)}) collective-permute-start(bf16[10,128,128]{2,1,0:T(8,128)(2,1)} %collective-permute-done.7), channel_id=1, source_target_pairs={{0,8},{2,10},{8,16},{10,18},{16,24},{18,26},{24,28},{26,30},{28,20... | collective-permute-start | bytes 983048 | tf_op jit(solution)/shard_map/ppermute | solution.py:36
  47.4 10.5 %collective-permute-start.22 = (bf16[10,128,128]{2,1,0:T(8,128)(2,1)}, bf16[10,128,128]{2,1,0:T(8,128)(2,1)}, u32[]{:S(2)}, u32[]{:S(2)}) collective-permute-start(bf16[10,128,128]{2,1,0:T(8,128)(2,1)} %collective-permute-done.16), channel_id=1, source_target_pairs={{8,0},{10,2},{16,8},{18,10},{24,16},{26,18},{28,24},{30,26},{20,28... | collective-permute-start | bytes 983048 | tf_op jit(solution)/shard_map/ppermute | solution.py:37
  49.5 20.0 %copy-start.6 = (bf16[10,128,128]{2,1,0:T(8,128)(2,1)S(1)}, bf16[10,128,128]{2,1,0:T(8,128)(2,1)}, u32[]{:S(2)}) copy-start(bf16[10,128,128]{2,1,0:T(8,128)(2,1)} %copy-done.5) | copy-start | bytes 983044
  56.3 9.6 %collective-permute-start.20 = (bf16[10,128,128]{2,1,0:T(8,128)(2,1)}, bf16[10,128,128]{2,1,0:T(8,128)(2,1)S(1)}, u32[]{:S(2)}, u32[]{:S(2)}) collective-permute-start(bf16[10,128,128]{2,1,0:T(8,128)(2,1)} %collective-permute-done.18), channel_id=1, source_target_pairs={{0,8},{2,10},{8,16},{10,18},{16,24},{18,26},{24,28},{26,30},{28,20... | collective-permute-start | bytes 983048 | tf_op jit(solution)/shard_map/ppermute | solution.py:36
  57.9 9.3 %collective-permute-start.24 = (bf16[10,128,128]{2,1,0:T(8,128)(2,1)}, bf16[10,128,128]{2,1,0:T(8,128)(2,1)S(1)}, u32[]{:S(2)}, u32[]{:S(2)}) collective-permute-start(bf16[10,128,128]{2,1,0:T(8,128)(2,1)} %collective-permute-done.22), channel_id=1, source_target_pairs={{8,0},{10,2},{16,8},{18,10},{24,16},{26,18},{28,24},{30,26},{20,28... | collective-permute-start | bytes 983048 | tf_op jit(solution)/shard_map/ppermute | solution.py:37
  58.5 10.4 %collective-permute-start.19 = (bf16[10,128,128]{2,1,0:T(8,128)(2,1)}, bf16[10,128,128]{2,1,0:T(8,128)(2,1)S(1)}, u32[]{:S(2)}, u32[]{:S(2)}) collective-permute-start(bf16[10,128,128]{2,1,0:T(8,128)(2,1)} %collective-permute-done.18), channel_id=1, source_target_pairs={{0,2},{2,0},{4,6},{6,4},{8,10},{10,8},{12,14},{14,12},{16,18},{18,... | collective-permute-start | bytes 983048 | tf_op jit(solution)/shard_map/ppermute | solution.py:40
  58.5 10.9 %collective-permute-start.23 = (bf16[10,128,128]{2,1,0:T(8,128)(2,1)}, bf16[10,128,128]{2,1,0:T(8,128)(2,1)S(1)}, u32[]{:S(2)}, u32[]{:S(2)}) collective-permute-start(bf16[10,128,128]{2,1,0:T(8,128)(2,1)} %collective-permute-done.22), channel_id=1, source_target_pairs={{0,2},{2,0},{4,6},{6,4},{8,10},{10,8},{12,14},{14,12},{16,18},{18,... | collective-permute-start | bytes 983048 | tf_op jit(solution)/shard_map/ppermute | solution.py:41
  65.8 3.6 %collective-permute-start.21 = (bf16[10,128,128]{2,1,0:T(8,128)(2,1)S(1)}, bf16[10,128,128]{2,1,0:T(8,128)(2,1)S(1)}, u32[]{:S(2)}, u32[]{:S(2)}) collective-permute-start(bf16[10,128,128]{2,1,0:T(8,128)(2,1)S(1)} %collective-permute-done.20), channel_id=1, source_target_pairs={{0,2},{2,0},{4,6},{6,4},{8,10},{10,8},{12,14},{14,12},{16,18},{18,... | collective-permute-start | bytes 983048 | tf_op jit(solution)/shard_map/ppermute | solution.py:40
  67.2 2.2 %collective-permute-start.25 = (bf16[10,128,128]{2,1,0:T(8,128)(2,1)S(1)}, bf16[10,128,128]{2,1,0:T(8,128)(2,1)S(1)}, u32[]{:S(2)}, u32[]{:S(2)}) collective-permute-start(bf16[10,128,128]{2,1,0:T(8,128)(2,1)S(1)} %collective-permute-done.24), channel_id=1, source_target_pairs={{0,2},{2,0},{4,6},{6,4},{8,10},{10,8},{12,14},{14,12},{16,18},{18,... | collective-permute-start | bytes 983048 | tf_op jit(solution)/shard_map/ppermute | solution.py:41
  67.3 3.3 %copy-start.8 = (bf16[10,128,128]{2,1,0:T(8,128)(2,1)S(1)}, bf16[10,128,128]{2,1,0:T(8,128)(2,1)}, u32[]{:S(2)}) copy-start(bf16[10,128,128]{2,1,0:T(8,128)(2,1)} %copy-done.7) | copy-start | bytes 983044
  67.3 17.6 %collective-permute-start.26 = (bf16[10,128,128]{2,1,0:T(8,128)(2,1)S(1)}, bf16[10,128,128]{2,1,0:T(8,128)(2,1)S(1)}, u32[]{:S(2)}, u32[]{:S(2)}) collective-permute-start(bf16[10,128,128]{2,1,0:T(8,128)(2,1)S(1)} %collective-permute-done.20), channel_id=1, source_target_pairs={{0,8},{2,10},{8,16},{10,18},{16,24},{18,26},{24,28},{26,30},{28,20... | collective-permute-start | bytes 983048 | tf_op jit(solution)/shard_map/ppermute | solution.py:36
  68.9 16.9 %collective-permute-start.28 = (bf16[10,128,128]{2,1,0:T(8,128)(2,1)S(1)}, bf16[10,128,128]{2,1,0:T(8,128)(2,1)S(1)}, u32[]{:S(2)}, u32[]{:S(2)}) collective-permute-start(bf16[10,128,128]{2,1,0:T(8,128)(2,1)S(1)} %collective-permute-done.24), channel_id=1, source_target_pairs={{8,0},{10,2},{16,8},{18,10},{24,16},{26,18},{28,24},{30,26},{20,28... | collective-permute-start | bytes 983048 | tf_op jit(solution)/shard_map/ppermute | solution.py:37
  69.5 2.2 %copy-start.10 = (bf16[10,128,128]{2,1,0:T(8,128)(2,1)S(1)}, bf16[10,128,128]{2,1,0:T(8,128)(2,1)}, u32[]{:S(2)}) copy-start(bf16[10,128,128]{2,1,0:T(8,128)(2,1)} %copy-done.9) | copy-start | bytes 983044
  79.4 1.0 copy-start.2
  79.5 1.0 copy-start.4
  84.2 7.6 %slice-start = ((s8[13107200]{0:T(1024)(128)(4,1)}), s8[4194304]{0:T(1024)(128)(4,1)S(1)}, s32[]{:S(2)}) async-start(s8[13107200]{0:T(1024)(128)(4,1)} %bitcast.474), calls=%async_computation | async-start | bytes 8388608
  85.0 2.1 %collective-permute-start.27 = (bf16[10,128,128]{2,1,0:T(8,128)(2,1)S(1)}, bf16[10,128,128]{2,1,0:T(8,128)(2,1)S(1)}, u32[]{:S(2)}, u32[]{:S(2)}) collective-permute-start(bf16[10,128,128]{2,1,0:T(8,128)(2,1)S(1)} %collective-permute-done.26), channel_id=1, source_target_pairs={{0,2},{2,0},{4,6},{6,4},{8,10},{10,8},{12,14},{14,12},{16,18},{18,... | collective-permute-start | bytes 983048 | tf_op jit(solution)/shard_map/ppermute | solution.py:40
  85.9 2.0 %collective-permute-start.29 = (bf16[10,128,128]{2,1,0:T(8,128)(2,1)S(1)}, bf16[10,128,128]{2,1,0:T(8,128)(2,1)S(1)}, u32[]{:S(2)}, u32[]{:S(2)}) collective-permute-start(bf16[10,128,128]{2,1,0:T(8,128)(2,1)S(1)} %collective-permute-done.28), channel_id=1, source_target_pairs={{0,2},{2,0},{4,6},{6,4},{8,10},{10,8},{12,14},{14,12},{16,18},{18,... | collective-permute-start | bytes 983048 | tf_op jit(solution)/shard_map/ppermute | solution.py:41
  86.4 5.3 %slice-start.1 = ((s8[13107200]{0:T(1024)(128)(4,1)}), s8[4194304]{0:T(1024)(128)(4,1)S(1)}, s32[]{:S(2)}) async-start(s8[13107200]{0:T(1024)(128)(4,1)} %bitcast.474), calls=%async_computation.1 | async-start | bytes 8388608
  88.9 2.8 %slice-start.2 = ((s8[13107200]{0:T(1024)(128)(4,1)}), s8[4194304]{0:T(1024)(128)(4,1)S(1)}, s32[]{:S(2)}) async-start(s8[13107200]{0:T(1024)(128)(4,1)} %bitcast.474), calls=%async_computation.2 | async-start | bytes 8388608
  90.2 1.6 %slice-start.3 = ((s8[13107200]{0:T(1024)(128)(4,1)}), s8[524288]{0:T(1024)(128)(4,1)S(1)}, s32[]{:S(2)}) async-start(s8[13107200]{0:T(1024)(128)(4,1)} %bitcast.474), calls=%async_computation.3 | async-start | bytes 1048576
  94.2 16.9 %collective-permute-start.30 = (bf16[60,5120]{1,0:T(8,128)(2,1)S(1)}, bf16[60,5120]{1,0:T(8,128)(2,1)S(1)}, u32[]{:S(2)}, u32[]{:S(2)}) collective-permute-start(bf16[60,5120]{1,0:T(8,128)(2,1)S(1)} %convolution_convert_fusion), channel_id=1, source_target_pairs={{0,1},{1,0},{2,3},{3,2},{4,5},{5,4},{6,7},{7,6},{8,9},{9,8},{10,11... | collective-permute-start | bytes 1843208 | tf_op jit(solution)/shard_map/ppermute | solution.py:162
  98.4 12.7 %copy-start = (bf16[60,5120]{1,0:T(8,128)(2,1)S(1)}, bf16[60,5120]{1,0:T(8,128)(2,1)}, u32[]{:S(2)}) copy-start(bf16[60,5120]{1,0:T(8,128)(2,1)} %param.10) | copy-start | bytes 1843204
  98.4 12.7 %copy-start.12 = (f32[5120]{0:T(1024)S(1)}, f32[5120]{0:T(1024)}, u32[]{:S(2)}) copy-start(f32[5120]{0:T(1024)} %param.14) | copy-start | bytes 61444

commit v15 on v14

--- a/solution.py
+++ b/solution.py
@@ -50,15 +50,15 @@
 
 def attend_part(queries_3d, keys, values, keeping, scale_factor):
     scores = (
-        jnp.einsum("hqd,hkd->hqk", queries_3d, keys, preferred_element_type=jnp.float32)
+        jnp.einsum("hqd,nhkd->hqnk", queries_3d, keys, preferred_element_type=jnp.float32)
         * scale_factor
     )
-    masked = jnp.where(keeping[None, None, :], scores, neg_large)
-    peak = jnp.max(masked, axis=2, keepdims=True)
-    weights = jnp.where(keeping[None, None, :], jnp.exp(masked - peak), 0.0)
-    totals = jnp.sum(weights, axis=2, keepdims=True)
+    masked = jnp.where(keeping[None, None], scores, neg_large)
+    peak = jnp.max(masked, axis=(2, 3))[:, :, None]
+    weights = jnp.where(keeping[None, None], jnp.exp(masked - peak[:, :, :, None]), 0.0)
+    totals = jnp.sum(weights, axis=(2, 3))[:, :, None]
     summed = jnp.einsum(
-        "hqk,hkd->hqd", weights.astype(jnp.bfloat16), values, preferred_element_type=jnp.float32
+        "hqnk,nhkd->hqd", weights.astype(jnp.bfloat16), values, preferred_element_type=jnp.float32
     )
     return peak, totals, summed
 
@@ -144,10 +144,10 @@
             q3 = q3.reshape(rows_out, hi - lo, HEAD).transpose(1, 0, 2)
             parts = []
             for first, last in phases:
-                stack = jnp.concatenate(got[first:last], axis=1)
-                keys = stack[: hi - lo]
-                values = stack[hi - lo :]
-                keeping = (within[None, :] < limits[first:last, None]).reshape(-1)
+                stack = jnp.stack(got[first:last])
+                keys = stack[:, : hi - lo]
+                values = stack[:, hi - lo :]
+                keeping = within[None, :] < limits[first:last, None]
                 parts.append(attend_part(q3, keys, values, keeping, scale_factor))
             return combine(parts, rows_out)
 

time: 113 us -> 111 us (0.982)
  local copies, waits for them, and re-layouts: 24.2 us -> 22.1 us
    concatenate x6 -> x0, local copies, waits for them, and re-layouts: 2.22 us -> none  [half(): stack = jnp.concatenate(got[first:last], axis=1)]
    unnamed x68, local copies, waits for them, and re-layouts: 11.5 us -> 9.42 us
    another operation x0 -> x2, local copies, waits for them, and re-layouts: none -> 2.03 us  [half(): stack = jnp.stack(got[first:last])]
  transfers between devices with their start and end apart: 31 -> 31, of which waited for: 12 -> 12; matrix products, arithmetic and copies ran while one was open for 27% -> 25% of each run, Pallas kernels for 0% -> 0%
where the time goes in v15:
time: 111 us; the launch traced here: 110 us
  waiting for transfers between devices  44.9 us (40%)
  local copies, waits for them, and re-layouts  22.1 us (20%)
  starting transfers between devices  19.6 us (18%)
  matrix products  15.4 us (14%)
  other arithmetic  5.57 us (5%)
  between operations  2.62 us (2%)
    ppermute x7, waiting for transfers between devices, gather_ring(): cur_a = lax.ppermute(cur_a, 'seq', forward)  28.2 us
    ppermute x7, starting transfers between devices, gather_ring(): cur_a = lax.ppermute(cur_a, 'seq', forward)  12.2 us
    ppermute x1, waiting for transfers between devices, on_device(): came = lax.ppermute(other, 'tp', [(0, 1), (1, 0)])  10.3 us
    unnamed x68, local copies, waits for them, and re-layouts  9.42 us
    ppermute x7, waiting for transfers between devices, gather_ring(): cur_b = lax.ppermute(cur_b, 'seq', backward)  6.34 us
    dot_general x12, matrix products, attend_part(): jnp.einsum('hqd,nhkd->hqnk', queries_3d, keys, preferred_element_type=jnp...  6.13 us
    another operation x37, local copies, waits for them, and re-layouts, on_device(): jnp.stack([g[0, rows_dev, :2] for g in heard]).astype(jnp.float32)  6.11 us
    dot_general x12, matrix products, attend_part(): jnp.einsum('hqnk,nhkd->hqd', weights.astype(jnp.bfloat16), values, prefer...  4.5 us
  transfers between devices with their start and end apart: 31, of which 12 were waited for; matrix products, arithmetic and copies ran while one was open for 25% of the time, Pallas kernels for 0%

profile of v15, /device:TPU:0, one launch (start us, length us, event | category | flops | bytes accessed | tf_op | source)
XLA Modules:
  0.0 110.1 jit_solution(5451325908188959168)
XLA Ops:
  0.0 1.0 fusion.237
  1.0 1.0 fusion.238
  4.6 3.1 %collective-permute-start.1 = (bf16[10,128,128]{2,1,0:T(8,128)(2,1)S(1)}, bf16[10,128,128]{2,1,0:T(8,128)(2,1)S(1)}, u32[]{:S(2)}, u32[]{:S(2)}) collective-permute-start(bf16[10,128,128]{2,1,0:T(8,128)(2,1)S(1)} %get-tuple-element.34), channel_id=1, source_target_pairs={{0,8},{2,10},{8,16},{10,18},{16,24},{18,26},{24,28},{26,30},{28,20... | collective-permute-start | bytes 983048 | tf_op jit(solution)/shard_map/ppermute | solution.py:36
  9.7 5.7 %collective-permute-done.1 = bf16[10,128,128]{2,1,0:T(8,128)(2,1)S(1)} collective-permute-done((bf16[10,128,128]{2,1,0:T(8,128)(2,1)S(1)}, bf16[10,128,128]{2,1,0:T(8,128)(2,1)S(1)}, u32[]{:S(2)}, u32[]{:S(2)}) %collective-permute-start.1) | collective-permute-done | bytes 327712 | tf_op jit(solution)/shard_map/ppermute | solution.py:36
  15.3 1.8 %collective-permute-start.3 = (bf16[10,128,128]{2,1,0:T(8,128)(2,1)S(1)}, bf16[10,128,128]{2,1,0:T(8,128)(2,1)}, u32[]{:S(2)}, u32[]{:S(2)}) collective-permute-start(bf16[10,128,128]{2,1,0:T(8,128)(2,1)S(1)} %collective-permute-done.1), channel_id=1, source_target_pairs={{0,8},{2,10},{8,16},{10,18},{16,24},{18,26},{24,28},{26,30},{28,20... | collective-permute-start | bytes 983048 | tf_op jit(solution)/shard_map/ppermute | solution.py:36
  17.1 0.7 collective-permute-done.10
  18.5 0.5 collective-permute-start.2
  19.1 5.3 %collective-permute-done.3 = bf16[10,128,128]{2,1,0:T(8,128)(2,1)} collective-permute-done((bf16[10,128,128]{2,1,0:T(8,128)(2,1)S(1)}, bf16[10,128,128]{2,1,0:T(8,128)(2,1)}, u32[]{:S(2)}, u32[]{:S(2)}) %collective-permute-start.3) | collective-permute-done | bytes 327712 | tf_op jit(solution)/shard_map/ppermute | solution.py:36
  24.3 1.5 %collective-permute-start.5 = (bf16[10,128,128]{2,1,0:T(8,128)(2,1)}, bf16[10,128,128]{2,1,0:T(8,128)(2,1)}, u32[]{:S(2)}, u32[]{:S(2)}) collective-permute-start(bf16[10,128,128]{2,1,0:T(8,128)(2,1)} %collective-permute-done.3), channel_id=1, source_target_pairs={{0,8},{2,10},{8,16},{10,18},{16,24},{18,26},{24,28},{26,30},{28,20... | collective-permute-start | bytes 983048 | tf_op jit(solution)/shard_map/ppermute | solution.py:36
  25.8 0.7 slice_bitcast_fusion.14
  26.5 0.6 collective-permute-done.12
  27.6 0.7 copy-done.7
  28.8 0.5 collective-permute-start.4
  29.3 3.4 %collective-permute-done.5 = bf16[10,128,128]{2,1,0:T(8,128)(2,1)} collective-permute-done((bf16[10,128,128]{2,1,0:T(8,128)(2,1)}, bf16[10,128,128]{2,1,0:T(8,128)(2,1)}, u32[]{:S(2)}, u32[]{:S(2)}) %collective-permute-start.5) | collective-permute-done | bytes 327712 | tf_op jit(solution)/shard_map/ppermute | solution.py:36
  32.6 1.2 %collective-permute-start.7 = (bf16[10,128,128]{2,1,0:T(8,128)(2,1)}, bf16[10,128,128]{2,1,0:T(8,128)(2,1)}, u32[]{:S(2)}, u32[]{:S(2)}) collective-permute-start(bf16[10,128,128]{2,1,0:T(8,128)(2,1)} %collective-permute-done.5), channel_id=1, source_target_pairs={{0,8},{2,10},{8,16},{10,18},{16,24},{18,26},{24,28},{26,30},{28,20... | collective-permute-start | bytes 983048 | tf_op jit(solution)/shard_map/ppermute | solution.py:36
  33.8 0.7 slice_bitcast_fusion.12
  34.5 1.1 %collective-permute-done.14 = bf16[10,128,128]{2,1,0:T(8,128)(2,1)S(1)} collective-permute-done((bf16[10,128,128]{2,1,0:T(8,128)(2,1)S(1)}, bf16[10,128,128]{2,1,0:T(8,128)(2,1)S(1)}, u32[]{:S(2)}, u32[]{:S(2)}) %collective-permute-start.14) | collective-permute-done | bytes 327712 | tf_op jit(solution)/shard_map/ppermute | solution.py:37
  35.6 0.5 collective-permute-start.16
  36.2 0.7 copy-done.11
  36.9 0.8 copy-done.5
  38.1 0.5 collective-permute-start.6
  38.6 1.4 %collective-permute-done.7 = bf16[10,128,128]{2,1,0:T(8,128)(2,1)} collective-permute-done((bf16[10,128,128]{2,1,0:T(8,128)(2,1)}, bf16[10,128,128]{2,1,0:T(8,128)(2,1)}, u32[]{:S(2)}, u32[]{:S(2)}) %collective-permute-start.7) | collective-permute-done | bytes 327712 | tf_op jit(solution)/shard_map/ppermute | solution.py:36
  40.0 0.7 slice_bitcast_fusion.10
  40.7 2.5 %collective-permute-done.16 = bf16[10,128,128]{2,1,0:T(8,128)(2,1)} collective-permute-done((bf16[10,128,128]{2,1,0:T(8,128)(2,1)S(1)}, bf16[10,128,128]{2,1,0:T(8,128)(2,1)}, u32[]{:S(2)}, u32[]{:S(2)}) %collective-permute-start.16) | collective-permute-done | bytes 327712 | tf_op jit(solution)/shard_map/ppermute | solution.py:37
  43.2 0.7 slice_bitcast_fusion.1
  43.9 0.7 copy-done.13
  44.6 0.7 copy-done.9
  45.8 1.6 %collective-permute-start.18 = (bf16[10,128,128]{2,1,0:T(8,128)(2,1)}, bf16[10,128,128]{2,1,0:T(8,128)(2,1)S(1)}, u32[]{:S(2)}, u32[]{:S(2)}) collective-permute-start(bf16[10,128,128]{2,1,0:T(8,128)(2,1)} %collective-permute-done.7), channel_id=1, source_target_pairs={{0,8},{2,10},{8,16},{10,18},{16,24},{18,26},{24,28},{26,30},{28,20... | collective-permute-start | bytes 983048 | tf_op jit(solution)/shard_map/ppermute | solution.py:36
  47.4 0.4 collective-permute-start.22
  47.8 0.7 slice_bitcast_fusion.9
  48.6 0.7 slice_bitcast_fusion
  50.2 6.0 %collective-permute-done.18 = bf16[10,128,128]{2,1,0:T(8,128)(2,1)S(1)} collective-permute-done((bf16[10,128,128]{2,1,0:T(8,128)(2,1)}, bf16[10,128,128]{2,1,0:T(8,128)(2,1)S(1)}, u32[]{:S(2)}, u32[]{:S(2)}) %collective-permute-start.18) | collective-permute-done | bytes 327712 | tf_op jit(solution)/shard_map/ppermute | solution.py:36
  56.1 1.6 %collective-permute-start.20 = (bf16[10,128,128]{2,1,0:T(8,128)(2,1)S(1)}, bf16[10,128,128]{2,1,0:T(8,128)(2,1)S(1)}, u32[]{:S(2)}, u32[]{:S(2)}) collective-permute-start(bf16[10,128,128]{2,1,0:T(8,128)(2,1)S(1)} %collective-permute-done.18), channel_id=1, source_target_pairs={{0,8},{2,10},{8,16},{10,18},{16,24},{18,26},{24,28},{26,30},{28,20... | collective-permute-start | bytes 983048 | tf_op jit(solution)/shard_map/ppermute | solution.py:36
  57.8 0.4 collective-permute-start.24
  58.4 0.5 collective-permute-start.23
  59.0 6.5 %collective-permute-done.20 = bf16[10,128,128]{2,1,0:T(8,128)(2,1)S(1)} collective-permute-done((bf16[10,128,128]{2,1,0:T(8,128)(2,1)S(1)}, bf16[10,128,128]{2,1,0:T(8,128)(2,1)S(1)}, u32[]{:S(2)}, u32[]{:S(2)}) %collective-permute-start.20) | collective-permute-done | bytes 327712 | tf_op jit(solution)/shard_map/ppermute | solution.py:36
  65.5 1.4 %collective-permute-done.24 = bf16[10,128,128]{2,1,0:T(8,128)(2,1)S(1)} collective-permute-done((bf16[10,128,128]{2,1,0:T(8,128)(2,1)S(1)}, bf16[10,128,128]{2,1,0:T(8,128)(2,1)S(1)}, u32[]{:S(2)}, u32[]{:S(2)}) %collective-permute-start.24) | collective-permute-done | bytes 327712 | tf_op jit(solution)/shard_map/ppermute | solution.py:37
  67.0 1.6 %collective-permute-start.26 = (bf16[10,128,128]{2,1,0:T(8,128)(2,1)S(1)}, bf16[10,128,128]{2,1,0:T(8,128)(2,1)S(1)}, u32[]{:S(2)}, u32[]{:S(2)}) collective-permute-start(bf16[10,128,128]{2,1,0:T(8,128)(2,1)S(1)} %collective-permute-done.20), channel_id=1, source_target_pairs={{0,8},{2,10},{8,16},{10,18},{16,24},{18,26},{24,28},{26,30},{28,20... | collective-permute-start | bytes 983048 | tf_op jit(solution)/shard_map/ppermute | solution.py:36
  68.6 0.5 collective-permute-start.28
  69.3 1.0 bitcast_dynamic-update-slice_fusion.13
  70.3 1.0 bitcast_dynamic-update-slice_fusion.11
  71.4 1.0 bitcast_dynamic-update-slice_fusion.9
  72.5 1.0 bitcast_dynamic-update-slice_fusion.19
  73.5 0.8 fusion.252
  74.3 0.8 fusion.251
  75.7 0.4 fusion.249
  76.7 0.7 copy-done.2
  77.8 1.0 bitcast_dynamic-update-slice_fusion
  78.8 1.0 bitcast_dynamic-update-slice_fusion.18
  79.8 0.8 fusion.246
  80.6 0.4 fusion.244
  81.0 0.7 fusion.16
  82.2 0.8 fusion.245
  83.9 0.5 collective-permute-start.29
  84.4 0.7 fusion.18
  86.9 0.5 fusion.66
  88.5 0.5 fusion.60
  89.8 2.4 %convolution_convert_fusion = bf16[60,5120]{1,0:T(8,128)(2,1)S(1)} fusion(bf16[1280,5120]{1,0:T(8,128)(2,1)S(1)} %bitcast.603, bf16[60,640]{1,0:T(8,128)(2,1)S(1)} %bitcast.614, bf16[60,640]{1,0:T(8,128)(2,1)S(1)} %bitcast.613), kind=kOutput, calls=%fused_computation | convolution fusion | flops 787046400 | bytes 13875200 | tf_op jit(solution)/shard_map/dot_general | solution.py:160
  92.2 1.6 %collective-permute-start.30 = (bf16[60,5120]{1,0:T(8,128)(2,1)S(1)}, bf16[60,5120]{1,0:T(8,128)(2,1)S(1)}, u32[]{:S(2)}, u32[]{:S(2)}) collective-permute-start(bf16[60,5120]{1,0:T(8,128)(2,1)S(1)} %convolution_convert_fusion), channel_id=1, source_target_pairs={{0,1},{1,0},{2,3},{3,2},{4,5},{5,4},{6,7},{7,6},{8,9},{9,8},{10,11... | collective-permute-start | bytes 1843208 | tf_op jit(solution)/shard_map/ppermute | solution.py:162
  93.7 0.7 fusion.69
  95.2 0.5 fusion.63
  96.4 2.4 %fusion.146 = f32[60,5120]{1,0:T(8,128)S(1)} fusion(bf16[1280,5120]{1,0:T(8,128)(2,1)S(1)} %bitcast.603, bf16[60,640]{1,0:T(8,128)(2,1)S(1)} %bitcast.615, bf16[60,640]{1,0:T(8,128)(2,1)S(1)} %bitcast.612), kind=kOutput, calls=%fused_computation.184 | convolution fusion | flops 786739200 | bytes 14489600 | tf_op jit(solution)/shard_map/dot_general | solution.py:164
  98.8 10.3 %collective-permute-done.30 = bf16[60,5120]{1,0:T(8,128)(2,1)S(1)} collective-permute-done((bf16[60,5120]{1,0:T(8,128)(2,1)S(1)}, bf16[60,5120]{1,0:T(8,128)(2,1)S(1)}, u32[]{:S(2)}, u32[]{:S(2)}) %collective-permute-start.30) | collective-permute-done | bytes 614432 | tf_op jit(solution)/shard_map/ppermute | solution.py:162
  109.1 1.1 add_convert_fusion
  (191 shorter events, 14.4 us)
Async XLA Ops:
  2.3 5.9 %copy-start.15 = (bf16[120,1280]{1,0:T(8,128)(2,1)S(1)}, bf16[120,1280]{1,0:T(8,128)(2,1)}, u32[]{:S(2)}) copy-start(bf16[120,1280]{1,0:T(8,128)(2,1)} %param.11) | copy-start | bytes 921604
  4.6 10.7 %collective-permute-start.1 = (bf16[10,128,128]{2,1,0:T(8,128)(2,1)S(1)}, bf16[10,128,128]{2,1,0:T(8,128)(2,1)S(1)}, u32[]{:S(2)}, u32[]{:S(2)}) collective-permute-start(bf16[10,128,128]{2,1,0:T(8,128)(2,1)S(1)} %get-tuple-element.34), channel_id=1, source_target_pairs={{0,8},{2,10},{8,16},{10,18},{16,24},{18,26},{24,28},{26,30},{28,20... | collective-permute-start | bytes 983048 | tf_op jit(solution)/shard_map/ppermute | solution.py:36
  7.7 10.4 %collective-permute-start = (bf16[10,128,128]{2,1,0:T(8,128)(2,1)S(1)}, bf16[10,128,128]{2,1,0:T(8,128)(2,1)S(1)}, u32[]{:S(2)}, u32[]{:S(2)}) collective-permute-start(bf16[10,128,128]{2,1,0:T(8,128)(2,1)S(1)} %get-tuple-element.34), channel_id=1, source_target_pairs={{0,2},{2,0},{4,6},{6,4},{8,10},{10,8},{12,14},{14,12},{16,18},{18,... | collective-permute-start | bytes 983048 | tf_op jit(solution)/shard_map/ppermute | solution.py:40
  7.7 10.1 %collective-permute-start.10 = (bf16[10,128,128]{2,1,0:T(8,128)(2,1)S(1)}, bf16[10,128,128]{2,1,0:T(8,128)(2,1)S(1)}, u32[]{:S(2)}, u32[]{:S(2)}) collective-permute-start(bf16[10,128,128]{2,1,0:T(8,128)(2,1)S(1)} %get-tuple-element.48), channel_id=1, source_target_pairs={{8,0},{10,2},{16,8},{18,10},{24,16},{26,18},{28,24},{30,26},{20,28... | collective-permute-start | bytes 983048 | tf_op jit(solution)/shard_map/ppermute | solution.py:37
  7.8 10.3 %collective-permute-start.9 = (bf16[10,128,128]{2,1,0:T(8,128)(2,1)S(1)}, bf16[10,128,128]{2,1,0:T(8,128)(2,1)S(1)}, u32[]{:S(2)}, u32[]{:S(2)}) collective-permute-start(bf16[10,128,128]{2,1,0:T(8,128)(2,1)S(1)} %get-tuple-element.48), channel_id=1, source_target_pairs={{0,2},{2,0},{4,6},{6,4},{8,10},{10,8},{12,14},{14,12},{16,18},{18,... | collective-permute-start | bytes 983048 | tf_op jit(solution)/shard_map/ppermute | solution.py:41
  15.3 9.0 %collective-permute-start.3 = (bf16[10,128,128]{2,1,0:T(8,128)(2,1)S(1)}, bf16[10,128,128]{2,1,0:T(8,128)(2,1)}, u32[]{:S(2)}, u32[]{:S(2)}) collective-permute-start(bf16[10,128,128]{2,1,0:T(8,128)(2,1)S(1)} %collective-permute-done.1), channel_id=1, source_target_pairs={{0,8},{2,10},{8,16},{10,18},{16,24},{18,26},{24,28},{26,30},{28,20... | collective-permute-start | bytes 983048 | tf_op jit(solution)/shard_map/ppermute | solution.py:36
  17.8 9.3 %collective-permute-start.12 = (bf16[10,128,128]{2,1,0:T(8,128)(2,1)S(1)}, bf16[10,128,128]{2,1,0:T(8,128)(2,1)S(1)}, u32[]{:S(2)}, u32[]{:S(2)}) collective-permute-start(bf16[10,128,128]{2,1,0:T(8,128)(2,1)S(1)} %collective-permute-done.10), channel_id=1, source_target_pairs={{8,0},{10,2},{16,8},{18,10},{24,16},{26,18},{28,24},{30,26},{20,28... | collective-permute-start | bytes 983048 | tf_op jit(solution)/shard_map/ppermute | solution.py:37
  18.5 9.0 %collective-permute-start.11 = (bf16[10,128,128]{2,1,0:T(8,128)(2,1)S(1)}, bf16[10,128,128]{2,1,0:T(8,128)(2,1)S(1)}, u32[]{:S(2)}, u32[]{:S(2)}) collective-permute-start(bf16[10,128,128]{2,1,0:T(8,128)(2,1)S(1)} %collective-permute-done.10), channel_id=1, source_target_pairs={{0,2},{2,0},{4,6},{6,4},{8,10},{10,8},{12,14},{14,12},{16,18},{18,... | collective-permute-start | bytes 983048 | tf_op jit(solution)/shard_map/ppermute | solution.py:41
  18.5 9.0 %collective-permute-start.2 = (bf16[10,128,128]{2,1,0:T(8,128)(2,1)S(1)}, bf16[10,128,128]{2,1,0:T(8,128)(2,1)S(1)}, u32[]{:S(2)}, u32[]{:S(2)}) collective-permute-start(bf16[10,128,128]{2,1,0:T(8,128)(2,1)S(1)} %collective-permute-done.1), channel_id=1, source_target_pairs={{0,2},{2,0},{4,6},{6,4},{8,10},{10,8},{12,14},{14,12},{16,18},{18,... | collective-permute-start | bytes 983048 | tf_op jit(solution)/shard_map/ppermute | solution.py:40
  24.3 8.3 %collective-permute-start.5 = (bf16[10,128,128]{2,1,0:T(8,128)(2,1)}, bf16[10,128,128]{2,1,0:T(8,128)(2,1)}, u32[]{:S(2)}, u32[]{:S(2)}) collective-permute-start(bf16[10,128,128]{2,1,0:T(8,128)(2,1)} %collective-permute-done.3), channel_id=1, source_target_pairs={{0,8},{2,10},{8,16},{10,18},{16,24},{18,26},{24,28},{26,30},{28,20... | collective-permute-start | bytes 983048 | tf_op jit(solution)/shard_map/ppermute | solution.py:36
  27.2 8.5 %collective-permute-start.14 = (bf16[10,128,128]{2,1,0:T(8,128)(2,1)S(1)}, bf16[10,128,128]{2,1,0:T(8,128)(2,1)S(1)}, u32[]{:S(2)}, u32[]{:S(2)}) collective-permute-start(bf16[10,128,128]{2,1,0:T(8,128)(2,1)S(1)} %collective-permute-done.12), channel_id=1, source_target_pairs={{8,0},{10,2},{16,8},{18,10},{24,16},{26,18},{28,24},{30,26},{20,28... | collective-permute-start | bytes 983048 | tf_op jit(solution)/shard_map/ppermute | solution.py:37
  27.6 0.8 copy-start.7
  28.3 17.5 %copy-start.1 = (bf16[10,128,128]{2,1,0:T(8,128)(2,1)}, bf16[10,128,128]{2,1,0:T(8,128)(2,1)S(1)}, u32[]{:S(2)}) copy-start(bf16[10,128,128]{2,1,0:T(8,128)(2,1)S(1)} %collective-permute-done.11) | copy-start | bytes 983044
  28.7 7.4 %collective-permute-start.13 = (bf16[10,128,128]{2,1,0:T(8,128)(2,1)S(1)}, bf16[10,128,128]{2,1,0:T(8,128)(2,1)S(1)}, u32[]{:S(2)}, u32[]{:S(2)}) collective-permute-start(bf16[10,128,128]{2,1,0:T(8,128)(2,1)S(1)} %collective-permute-done.12), channel_id=1, source_target_pairs={{0,2},{2,0},{4,6},{6,4},{8,10},{10,8},{12,14},{14,12},{16,18},{18,... | collective-permute-start | bytes 983048 | tf_op jit(solution)/shard_map/ppermute | solution.py:41
  28.8 7.4 %collective-permute-start.4 = (bf16[10,128,128]{2,1,0:T(8,128)(2,1)}, bf16[10,128,128]{2,1,0:T(8,128)(2,1)S(1)}, u32[]{:S(2)}, u32[]{:S(2)}) collective-permute-start(bf16[10,128,128]{2,1,0:T(8,128)(2,1)} %collective-permute-done.3), channel_id=1, source_target_pairs={{0,2},{2,0},{4,6},{6,4},{8,10},{10,8},{12,14},{14,12},{16,18},{18,... | collective-permute-start | bytes 983048 | tf_op jit(solution)/shard_map/ppermute | solution.py:40
  32.6 7.4 %collective-permute-start.7 = (bf16[10,128,128]{2,1,0:T(8,128)(2,1)}, bf16[10,128,128]{2,1,0:T(8,128)(2,1)}, u32[]{:S(2)}, u32[]{:S(2)}) collective-permute-start(bf16[10,128,128]{2,1,0:T(8,128)(2,1)} %collective-permute-done.5), channel_id=1, source_target_pairs={{0,8},{2,10},{8,16},{10,18},{16,24},{18,26},{24,28},{26,30},{28,20... | collective-permute-start | bytes 983048 | tf_op jit(solution)/shard_map/ppermute | solution.py:36
  35.6 10.1 %copy-start.3 = (bf16[10,128,128]{2,1,0:T(8,128)(2,1)}, bf16[10,128,128]{2,1,0:T(8,128)(2,1)S(1)}, u32[]{:S(2)}) copy-start(bf16[10,128,128]{2,1,0:T(8,128)(2,1)S(1)} %collective-permute-done.14) | copy-start | bytes 983044
  35.6 7.6 %collective-permute-start.16 = (bf16[10,128,128]{2,1,0:T(8,128)(2,1)S(1)}, bf16[10,128,128]{2,1,0:T(8,128)(2,1)}, u32[]{:S(2)}, u32[]{:S(2)}) collective-permute-start(bf16[10,128,128]{2,1,0:T(8,128)(2,1)S(1)} %collective-permute-done.14), channel_id=1, source_target_pairs={{8,0},{10,2},{16,8},{18,10},{24,16},{26,18},{28,24},{30,26},{20,28... | collective-permute-start | bytes 983048 | tf_op jit(solution)/shard_map/ppermute | solution.py:37
  36.2 0.7 copy-start.11
  36.9 0.8 copy-start.5
  38.1 5.9 %collective-permute-start.15 = (bf16[10,128,128]{2,1,0:T(8,128)(2,1)S(1)}, bf16[10,128,128]{2,1,0:T(8,128)(2,1)S(1)}, u32[]{:S(2)}, u32[]{:S(2)}) collective-permute-start(bf16[10,128,128]{2,1,0:T(8,128)(2,1)S(1)} %collective-permute-done.14), channel_id=1, source_target_pairs={{0,2},{2,0},{4,6},{6,4},{8,10},{10,8},{12,14},{14,12},{16,18},{18,... | collective-permute-start | bytes 983048 | tf_op jit(solution)/shard_map/ppermute | solution.py:41
  38.1 5.9 %collective-permute-start.6 = (bf16[10,128,128]{2,1,0:T(8,128)(2,1)}, bf16[10,128,128]{2,1,0:T(8,128)(2,1)S(1)}, u32[]{:S(2)}, u32[]{:S(2)}) collective-permute-start(bf16[10,128,128]{2,1,0:T(8,128)(2,1)} %collective-permute-done.5), channel_id=1, source_target_pairs={{0,2},{2,0},{4,6},{6,4},{8,10},{10,8},{12,14},{14,12},{16,18},{18,... | collective-permute-start | bytes 983048 | tf_op jit(solution)/shard_map/ppermute | solution.py:40
  40.0 7.8 %collective-permute-start.8 = (bf16[10,128,128]{2,1,0:T(8,128)(2,1)}, bf16[10,128,128]{2,1,0:T(8,128)(2,1)}, u32[]{:S(2)}, u32[]{:S(2)}) collective-permute-start(bf16[10,128,128]{2,1,0:T(8,128)(2,1)} %collective-permute-done.7), channel_id=1, source_target_pairs={{0,2},{2,0},{4,6},{6,4},{8,10},{10,8},{12,14},{14,12},{16,18},{18,... | collective-permute-start | bytes 983048 | tf_op jit(solution)/shard_map/ppermute | solution.py:40
  43.2 5.4 %collective-permute-start.17 = (bf16[10,128,128]{2,1,0:T(8,128)(2,1)}, bf16[10,128,128]{2,1,0:T(8,128)(2,1)}, u32[]{:S(2)}, u32[]{:S(2)}) collective-permute-start(bf16[10,128,128]{2,1,0:T(8,128)(2,1)} %collective-permute-done.16), channel_id=1, source_target_pairs={{0,2},{2,0},{4,6},{6,4},{8,10},{10,8},{12,14},{14,12},{16,18},{18,... | collective-permute-start | bytes 983048 | tf_op jit(solution)/shard_map/ppermute | solution.py:41
  43.9 0.7 copy-start.13
  44.6 0.7 copy-start.9
  45.8 10.3 %collective-permute-start.18 = (bf16[10,128,128]{2,1,0:T(8,128)(2,1)}, bf16[10,128,128]{2,1,0:T(8,128)(2,1)S(1)}, u32[]{:S(2)}, u32[]{:S(2)}) collective-permute-start(bf16[10,128,128]{2,1,0:T(8,128)(2,1)} %collective-permute-done.7), channel_id=1, source_target_pairs={{0,8},{2,10},{8,16},{10,18},{16,24},{18,26},{24,28},{26,30},{28,20... | collective-permute-start | bytes 983048 | tf_op jit(solution)/shard_map/ppermute | solution.py:36
  47.4 10.4 %collective-permute-start.22 = (bf16[10,128,128]{2,1,0:T(8,128)(2,1)}, bf16[10,128,128]{2,1,0:T(8,128)(2,1)S(1)}, u32[]{:S(2)}, u32[]{:S(2)}) collective-permute-start(bf16[10,128,128]{2,1,0:T(8,128)(2,1)} %collective-permute-done.16), channel_id=1, source_target_pairs={{8,0},{10,2},{16,8},{18,10},{24,16},{26,18},{28,24},{30,26},{20,28... | collective-permute-start | bytes 983048 | tf_op jit(solution)/shard_map/ppermute | solution.py:37
  49.5 19.7 %copy-start.8 = (bf16[10,128,128]{2,1,0:T(8,128)(2,1)S(1)}, bf16[10,128,128]{2,1,0:T(8,128)(2,1)}, u32[]{:S(2)}) copy-start(bf16[10,128,128]{2,1,0:T(8,128)(2,1)} %copy-done.7) | copy-start | bytes 983044
  56.1 9.3 %collective-permute-start.20 = (bf16[10,128,128]{2,1,0:T(8,128)(2,1)S(1)}, bf16[10,128,128]{2,1,0:T(8,128)(2,1)S(1)}, u32[]{:S(2)}, u32[]{:S(2)}) collective-permute-start(bf16[10,128,128]{2,1,0:T(8,128)(2,1)S(1)} %collective-permute-done.18), channel_id=1, source_target_pairs={{0,8},{2,10},{8,16},{10,18},{16,24},{18,26},{24,28},{26,30},{28,20... | collective-permute-start | bytes 983048 | tf_op jit(solution)/shard_map/ppermute | solution.py:36
  57.8 9.1 %collective-permute-start.24 = (bf16[10,128,128]{2,1,0:T(8,128)(2,1)S(1)}, bf16[10,128,128]{2,1,0:T(8,128)(2,1)S(1)}, u32[]{:S(2)}, u32[]{:S(2)}) collective-permute-start(bf16[10,128,128]{2,1,0:T(8,128)(2,1)S(1)} %collective-permute-done.22), channel_id=1, source_target_pairs={{8,0},{10,2},{16,8},{18,10},{24,16},{26,18},{28,24},{30,26},{20,28... | collective-permute-start | bytes 983048 | tf_op jit(solution)/shard_map/ppermute | solution.py:37
  58.4 10.2 %collective-permute-start.19 = (bf16[10,128,128]{2,1,0:T(8,128)(2,1)S(1)}, bf16[10,128,128]{2,1,0:T(8,128)(2,1)S(1)}, u32[]{:S(2)}, u32[]{:S(2)}) collective-permute-start(bf16[10,128,128]{2,1,0:T(8,128)(2,1)S(1)} %collective-permute-done.18), channel_id=1, source_target_pairs={{0,2},{2,0},{4,6},{6,4},{8,10},{10,8},{12,14},{14,12},{16,18},{18,... | collective-permute-start | bytes 983048 | tf_op jit(solution)/shard_map/ppermute | solution.py:40
  58.4 10.7 %collective-permute-start.23 = (bf16[10,128,128]{2,1,0:T(8,128)(2,1)S(1)}, bf16[10,128,128]{2,1,0:T(8,128)(2,1)S(1)}, u32[]{:S(2)}, u32[]{:S(2)}) collective-permute-start(bf16[10,128,128]{2,1,0:T(8,128)(2,1)S(1)} %collective-permute-done.22), channel_id=1, source_target_pairs={{0,2},{2,0},{4,6},{6,4},{8,10},{10,8},{12,14},{14,12},{16,18},{18,... | collective-permute-start | bytes 983048 | tf_op jit(solution)/shard_map/ppermute | solution.py:41
  65.5 3.6 %collective-permute-start.21 = (bf16[10,128,128]{2,1,0:T(8,128)(2,1)S(1)}, bf16[10,128,128]{2,1,0:T(8,128)(2,1)S(1)}, u32[]{:S(2)}, u32[]{:S(2)}) collective-permute-start(bf16[10,128,128]{2,1,0:T(8,128)(2,1)S(1)} %collective-permute-done.20), channel_id=1, source_target_pairs={{0,2},{2,0},{4,6},{6,4},{8,10},{10,8},{12,14},{14,12},{16,18},{18,... | collective-permute-start | bytes 983048 | tf_op jit(solution)/shard_map/ppermute | solution.py:40
  66.9 2.2 %collective-permute-start.25 = (bf16[10,128,128]{2,1,0:T(8,128)(2,1)S(1)}, bf16[10,128,128]{2,1,0:T(8,128)(2,1)S(1)}, u32[]{:S(2)}, u32[]{:S(2)}) collective-permute-start(bf16[10,128,128]{2,1,0:T(8,128)(2,1)S(1)} %collective-permute-done.24), channel_id=1, source_target_pairs={{0,2},{2,0},{4,6},{6,4},{8,10},{10,8},{12,14},{14,12},{16,18},{18,... | collective-permute-start | bytes 983048 | tf_op jit(solution)/shard_map/ppermute | solution.py:41
  67.0 3.3 %copy-start.12 = (bf16[10,128,128]{2,1,0:T(8,128)(2,1)S(1)}, bf16[10,128,128]{2,1,0:T(8,128)(2,1)}, u32[]{:S(2)}) copy-start(bf16[10,128,128]{2,1,0:T(8,128)(2,1)} %copy-done.11) | copy-start | bytes 983044
  67.0 15.9 %collective-permute-start.26 = (bf16[10,128,128]{2,1,0:T(8,128)(2,1)S(1)}, bf16[10,128,128]{2,1,0:T(8,128)(2,1)S(1)}, u32[]{:S(2)}, u32[]{:S(2)}) collective-permute-start(bf16[10,128,128]{2,1,0:T(8,128)(2,1)S(1)} %collective-permute-done.20), channel_id=1, source_target_pairs={{0,8},{2,10},{8,16},{10,18},{16,24},{18,26},{24,28},{26,30},{28,20... | collective-permute-start | bytes 983048 | tf_op jit(solution)/shard_map/ppermute | solution.py:36
  68.6 15.3 %collective-permute-start.28 = (bf16[10,128,128]{2,1,0:T(8,128)(2,1)S(1)}, bf16[10,128,128]{2,1,0:T(8,128)(2,1)S(1)}, u32[]{:S(2)}, u32[]{:S(2)}) collective-permute-start(bf16[10,128,128]{2,1,0:T(8,128)(2,1)S(1)} %collective-permute-done.24), channel_id=1, source_target_pairs={{8,0},{10,2},{16,8},{18,10},{24,16},{26,18},{28,24},{30,26},{20,28... | collective-permute-start | bytes 983048 | tf_op jit(solution)/shard_map/ppermute | solution.py:37
  69.1 2.2 %copy-start.14 = (bf16[10,128,128]{2,1,0:T(8,128)(2,1)S(1)}, bf16[10,128,128]{2,1,0:T(8,128)(2,1)}, u32[]{:S(2)}) copy-start(bf16[10,128,128]{2,1,0:T(8,128)(2,1)} %copy-done.13) | copy-start | bytes 983044
  76.4 1.0 copy-start.2
  76.5 1.0 copy-start.6
  76.5 1.1 copy-start.4
  76.6 1.1 %copy-start.10 = (bf16[10,128,128]{2,1,0:T(8,128)(2,1)S(1)}, bf16[10,128,128]{2,1,0:T(8,128)(2,1)}, u32[]{:S(2)}) copy-start(bf16[10,128,128]{2,1,0:T(8,128)(2,1)} %copy-done.9) | copy-start | bytes 983044
  83.0 2.2 %collective-permute-start.27 = (bf16[10,128,128]{2,1,0:T(8,128)(2,1)S(1)}, bf16[10,128,128]{2,1,0:T(8,128)(2,1)S(1)}, u32[]{:S(2)}, u32[]{:S(2)}) collective-permute-start(bf16[10,128,128]{2,1,0:T(8,128)(2,1)S(1)} %collective-permute-done.26), channel_id=1, source_target_pairs={{0,2},{2,0},{4,6},{6,4},{8,10},{10,8},{12,14},{14,12},{16,18},{18,... | collective-permute-start | bytes 983048 | tf_op jit(solution)/shard_map/ppermute | solution.py:40
  83.0 6.7 %slice-start = ((s8[13107200]{0:T(1024)(128)(4,1)}), s8[4194304]{0:T(1024)(128)(4,1)S(1)}, s32[]{:S(2)}) async-start(s8[13107200]{0:T(1024)(128)(4,1)} %bitcast.602), calls=%async_computation | async-start | bytes 8388608
  83.9 2.0 %collective-permute-start.29 = (bf16[10,128,128]{2,1,0:T(8,128)(2,1)S(1)}, bf16[10,128,128]{2,1,0:T(8,128)(2,1)S(1)}, u32[]{:S(2)}, u32[]{:S(2)}) collective-permute-start(bf16[10,128,128]{2,1,0:T(8,128)(2,1)S(1)} %collective-permute-done.28), channel_id=1, source_target_pairs={{0,2},{2,0},{4,6},{6,4},{8,10},{10,8},{12,14},{14,12},{16,18},{18,... | collective-permute-start | bytes 983048 | tf_op jit(solution)/shard_map/ppermute | solution.py:41
  85.1 4.6 %slice-start.1 = ((s8[13107200]{0:T(1024)(128)(4,1)}), s8[4194304]{0:T(1024)(128)(4,1)S(1)}, s32[]{:S(2)}) async-start(s8[13107200]{0:T(1024)(128)(4,1)} %bitcast.602), calls=%async_computation.1 | async-start | bytes 8388608
  86.9 2.8 %slice-start.2 = ((s8[13107200]{0:T(1024)(128)(4,1)}), s8[4194304]{0:T(1024)(128)(4,1)S(1)}, s32[]{:S(2)}) async-start(s8[13107200]{0:T(1024)(128)(4,1)} %bitcast.602), calls=%async_computation.2 | async-start | bytes 8388608
  88.5 1.3 %slice-start.3 = ((s8[13107200]{0:T(1024)(128)(4,1)}), s8[524288]{0:T(1024)(128)(4,1)S(1)}, s32[]{:S(2)}) async-start(s8[13107200]{0:T(1024)(128)(4,1)} %bitcast.602), calls=%async_computation.3 | async-start | bytes 1048576
  92.2 16.9 %collective-permute-start.30 = (bf16[60,5120]{1,0:T(8,128)(2,1)S(1)}, bf16[60,5120]{1,0:T(8,128)(2,1)S(1)}, u32[]{:S(2)}, u32[]{:S(2)}) collective-permute-start(bf16[60,5120]{1,0:T(8,128)(2,1)S(1)} %convolution_convert_fusion), channel_id=1, source_target_pairs={{0,1},{1,0},{2,3},{3,2},{4,5},{5,4},{6,7},{7,6},{8,9},{9,8},{10,11... | collective-permute-start | bytes 1843208 | tf_op jit(solution)/shard_map/ppermute | solution.py:162
  96.4 12.7 %copy-start = (bf16[60,5120]{1,0:T(8,128)(2,1)S(1)}, bf16[60,5120]{1,0:T(8,128)(2,1)}, u32[]{:S(2)}) copy-start(bf16[60,5120]{1,0:T(8,128)(2,1)} %param.10) | copy-start | bytes 1843204
  96.4 12.7 %copy-start.16 = (f32[5120]{0:T(1024)S(1)}, f32[5120]{0:T(1024)}, u32[]{:S(2)}) copy-start(f32[5120]{0:T(1024)} %param.14) | copy-start | bytes 61444

commit v16 on v15

--- a/solution.py
+++ b/solution.py
@@ -125,6 +125,7 @@
         within = jnp.arange(rows_pad, dtype=jnp.int32)
         phases = [(0, known + 1), (known + 1, chips - 1), (chips - 1, chips)]
         phases = [(2 * lo, 2 * hi) for lo, hi in phases if hi > lo]
+        phases = phases[:-1] + [(phases[-1][0], phases[-1][0] + 1), (phases[-1][0] + 1, phases[-1][1])]
 
         anchor = 2 * max(chips - 2, 0)
         early = 2 * (chips - 1)

time: 111 us -> 120 us (1.081)
  waiting for transfers between devices: 44.9 us -> 47.8 us
  other arithmetic: 5.57 us -> 8.42 us
  matrix products: 15.4 us -> 17.6 us
  local copies, waits for them, and re-layouts: 22.1 us -> 23.6 us
    ppermute x1, waiting for transfers between devices: 10.3 us -> 13 us  [on_device(): came = lax.ppermute(other, 'tp', [(0, 1), (1, 0)])]
    lt x6 -> x8, other arithmetic: 0.44 us -> 2.79 us  [half(): keeping = within[None, :] < limits[first:last, None]]
    ppermute x7, waiting for transfers between devices: 28.2 us -> 30.5 us  [gather_ring(): cur_a = lax.ppermute(cur_a, 'seq', forward)]
    ppermute x7, waiting for transfers between devices: 6.34 us -> 4.29 us  [gather_ring(): cur_b = lax.ppermute(cur_b, 'seq', backward)]
    dot_general x12 -> x16, matrix products: 6.13 us -> 7.36 us  [attend_part(): jnp.einsum('hqd,nhkd->hqnk', queries_3d, keys, preferred_element_type=jnp...]
    dot_general x12 -> x16, matrix products: 4.5 us -> 5.49 us  [attend_part(): jnp.einsum('hqnk,nhkd->hqd', weights.astype(jnp.bfloat16), values, prefer...]
    reduce_sum x6 -> x8, other arithmetic: 2.83 us -> 3.46 us  [attend_part(): totals = jnp.sum(weights, axis=(2, 3))[:, :, None]]
  transfers between devices with their start and end apart: 31 -> 31, of which waited for: 12 -> 13; matrix products, arithmetic and copies ran while one was open for 25% -> 19% of each run, Pallas kernels for 0% -> 0%
where the time goes in v16:
time: 120 us
  waiting for transfers between devices  47.8 us (40%)
  local copies, waits for them, and re-layouts  23.6 us (20%)
  starting transfers between devices  19.6 us (16%)
  matrix products  17.6 us (15%)
  other arithmetic  8.42 us (7%)
  between operations  2.68 us (2%)
    ppermute x7, waiting for transfers between devices, gather_ring(): cur_a = lax.ppermute(cur_a, 'seq', forward)  30.5 us
    ppermute x1, waiting for transfers between devices, on_device(): came = lax.ppermute(other, 'tp', [(0, 1), (1, 0)])  13 us
    ppermute x7, starting transfers between devices, gather_ring(): cur_a = lax.ppermute(cur_a, 'seq', forward)  12.1 us
    unnamed x68, local copies, waits for them, and re-layouts  9.79 us
    dot_general x16, matrix products, attend_part(): jnp.einsum('hqd,nhkd->hqnk', queries_3d, keys, preferred_element_type=jnp...  7.36 us
    another operation x37, local copies, waits for them, and re-layouts, on_device(): jnp.stack([g[0, rows_dev, :2] for g in heard]).astype(jnp.float32)  6.13 us
    dot_general x16, matrix products, attend_part(): jnp.einsum('hqnk,nhkd->hqd', weights.astype(jnp.bfloat16), values, prefer...  5.49 us
    ppermute x7, waiting for transfers between devices, gather_ring(): cur_b = lax.ppermute(cur_b, 'seq', backward)  4.29 us
  transfers between devices with their start and end apart: 31, of which 13 were waited for; matrix products, arithmetic and copies ran while one was open for 19% of the time, Pallas kernels for 0%

profile of v16, /device:TPU:0, one launch (start us, length us, event | category | flops | bytes accessed | tf_op | source)
XLA Modules:
  0.0 119.8 jit_solution(14256189127372413745)
XLA Ops:
  1.5 1.0 fusion.288
  2.5 1.0 fusion.287
  4.6 0.5 collective-permute-start
  5.1 2.6 %collective-permute-start.1 = (bf16[10,128,128]{2,1,0:T(8,128)(2,1)S(1)}, bf16[10,128,128]{2,1,0:T(8,128)(2,1)S(1)}, u32[]{:S(2)}, u32[]{:S(2)}) collective-permute-start(bf16[10,128,128]{2,1,0:T(8,128)(2,1)S(1)} %get-tuple-element.34), channel_id=1, source_target_pairs={{0,8},{2,10},{8,16},{10,18},{16,24},{18,26},{24,28},{26,30},{28,20... | collective-permute-start | bytes 983048 | tf_op jit(solution)/shard_map/ppermute | solution.py:36
  9.6 6.4 %collective-permute-done.1 = bf16[10,128,128]{2,1,0:T(8,128)(2,1)S(1)} collective-permute-done((bf16[10,128,128]{2,1,0:T(8,128)(2,1)S(1)}, bf16[10,128,128]{2,1,0:T(8,128)(2,1)S(1)}, u32[]{:S(2)}, u32[]{:S(2)}) %collective-permute-start.1) | collective-permute-done | bytes 327712 | tf_op jit(solution)/shard_map/ppermute | solution.py:36
  16.0 1.8 %collective-permute-start.3 = (bf16[10,128,128]{2,1,0:T(8,128)(2,1)S(1)}, bf16[10,128,128]{2,1,0:T(8,128)(2,1)S(1)}, u32[]{:S(2)}, u32[]{:S(2)}) collective-permute-start(bf16[10,128,128]{2,1,0:T(8,128)(2,1)S(1)} %collective-permute-done.1), channel_id=1, source_target_pairs={{0,8},{2,10},{8,16},{10,18},{16,24},{18,26},{24,28},{26,30},{28,20... | collective-permute-start | bytes 983048 | tf_op jit(solution)/shard_map/ppermute | solution.py:36
  18.6 0.5 collective-permute-start.11
  19.1 6.4 %collective-permute-done.3 = bf16[10,128,128]{2,1,0:T(8,128)(2,1)S(1)} collective-permute-done((bf16[10,128,128]{2,1,0:T(8,128)(2,1)S(1)}, bf16[10,128,128]{2,1,0:T(8,128)(2,1)S(1)}, u32[]{:S(2)}, u32[]{:S(2)}) %collective-permute-start.3) | collective-permute-done | bytes 327712 | tf_op jit(solution)/shard_map/ppermute | solution.py:36
  25.5 1.6 %collective-permute-start.5 = (bf16[10,128,128]{2,1,0:T(8,128)(2,1)S(1)}, bf16[10,128,128]{2,1,0:T(8,128)(2,1)S(1)}, u32[]{:S(2)}, u32[]{:S(2)}) collective-permute-start(bf16[10,128,128]{2,1,0:T(8,128)(2,1)S(1)} %collective-permute-done.3), channel_id=1, source_target_pairs={{0,8},{2,10},{8,16},{10,18},{16,24},{18,26},{24,28},{26,30},{28,20... | collective-permute-start | bytes 983048 | tf_op jit(solution)/shard_map/ppermute | solution.py:36
  27.5 0.7 slice_bitcast_fusion.29
  28.3 0.7 copy-done.9
  29.4 0.5 collective-permute-start.13
  29.9 4.3 %collective-permute-done.5 = bf16[10,128,128]{2,1,0:T(8,128)(2,1)S(1)} collective-permute-done((bf16[10,128,128]{2,1,0:T(8,128)(2,1)S(1)}, bf16[10,128,128]{2,1,0:T(8,128)(2,1)S(1)}, u32[]{:S(2)}, u32[]{:S(2)}) %collective-permute-start.5) | collective-permute-done | bytes 327712 | tf_op jit(solution)/shard_map/ppermute | solution.py:36
  34.2 1.4 %collective-permute-start.7 = (bf16[10,128,128]{2,1,0:T(8,128)(2,1)S(1)}, bf16[10,128,128]{2,1,0:T(8,128)(2,1)}, u32[]{:S(2)}, u32[]{:S(2)}) collective-permute-start(bf16[10,128,128]{2,1,0:T(8,128)(2,1)S(1)} %collective-permute-done.5), channel_id=1, source_target_pairs={{0,8},{2,10},{8,16},{10,18},{16,24},{18,26},{24,28},{26,30},{28,20... | collective-permute-start | bytes 983048 | tf_op jit(solution)/shard_map/ppermute | solution.py:36
  35.7 0.6 collective-permute-start.16
  36.3 0.7 slice_bitcast_fusion.27
  37.0 0.7 copy-done.5
  37.7 0.7 copy-done.11
  38.9 0.5 collective-permute-start.15
  39.4 2.8 %collective-permute-done.7 = bf16[10,128,128]{2,1,0:T(8,128)(2,1)} collective-permute-done((bf16[10,128,128]{2,1,0:T(8,128)(2,1)S(1)}, bf16[10,128,128]{2,1,0:T(8,128)(2,1)}, u32[]{:S(2)}, u32[]{:S(2)}) %collective-permute-start.7) | collective-permute-done | bytes 327712 | tf_op jit(solution)/shard_map/ppermute | solution.py:36
  42.2 0.7 slice_bitcast_fusion.34
  42.9 0.5 collective-permute-done.16
  43.4 0.7 slice_bitcast_fusion.25
  44.1 0.7 copy-done.7
  44.8 0.7 copy-done.13
  46.0 1.5 %collective-permute-start.18 = (bf16[10,128,128]{2,1,0:T(8,128)(2,1)}, bf16[10,128,128]{2,1,0:T(8,128)(2,1)S(1)}, u32[]{:S(2)}, u32[]{:S(2)}) collective-permute-start(bf16[10,128,128]{2,1,0:T(8,128)(2,1)} %collective-permute-done.7), channel_id=1, source_target_pairs={{0,8},{2,10},{8,16},{10,18},{16,24},{18,26},{24,28},{26,30},{28,20... | collective-permute-start | bytes 983048 | tf_op jit(solution)/shard_map/ppermute | solution.py:36
  47.5 0.5 collective-permute-start.22
  48.0 0.7 slice_bitcast_fusion.33
  48.8 0.6 slice_bitcast_fusion.24
  50.1 0.6 fusion.292
  50.8 0.6 fusion.291
  51.5 0.6 iota_compare_fusion.4
  52.1 4.1 %collective-permute-done.18 = bf16[10,128,128]{2,1,0:T(8,128)(2,1)S(1)} collective-permute-done((bf16[10,128,128]{2,1,0:T(8,128)(2,1)}, bf16[10,128,128]{2,1,0:T(8,128)(2,1)S(1)}, u32[]{:S(2)}, u32[]{:S(2)}) %collective-permute-start.18) | collective-permute-done | bytes 327712 | tf_op jit(solution)/shard_map/ppermute | solution.py:36
  56.3 1.6 %collective-permute-start.20 = (bf16[10,128,128]{2,1,0:T(8,128)(2,1)S(1)}, bf16[10,128,128]{2,1,0:T(8,128)(2,1)S(1)}, u32[]{:S(2)}, u32[]{:S(2)}) collective-permute-start(bf16[10,128,128]{2,1,0:T(8,128)(2,1)S(1)} %collective-permute-done.18), channel_id=1, source_target_pairs={{0,8},{2,10},{8,16},{10,18},{16,24},{18,26},{24,28},{26,30},{28,20... | collective-permute-start | bytes 983048 | tf_op jit(solution)/shard_map/ppermute | solution.py:36
  57.8 0.6 iota_compare_fusion.5
  59.3 0.6 iota_compare_fusion.6
  59.9 6.4 %collective-permute-done.20 = bf16[10,128,128]{2,1,0:T(8,128)(2,1)S(1)} collective-permute-done((bf16[10,128,128]{2,1,0:T(8,128)(2,1)S(1)}, bf16[10,128,128]{2,1,0:T(8,128)(2,1)S(1)}, u32[]{:S(2)}, u32[]{:S(2)}) %collective-permute-start.20) | collective-permute-done | bytes 327712 | tf_op jit(solution)/shard_map/ppermute | solution.py:36
  66.4 2.3 %collective-permute-done.24 = bf16[10,128,128]{2,1,0:T(8,128)(2,1)S(1)} collective-permute-done((bf16[10,128,128]{2,1,0:T(8,128)(2,1)S(1)}, bf16[10,128,128]{2,1,0:T(8,128)(2,1)S(1)}, u32[]{:S(2)}, u32[]{:S(2)}) %collective-permute-start.24) | collective-permute-done | bytes 327712 | tf_op jit(solution)/shard_map/ppermute | solution.py:37
  68.7 0.6 iota_compare_fusion.7
  69.4 0.5 collective-permute-start.28
  69.9 1.6 %collective-permute-start.26 = (bf16[10,128,128]{2,1,0:T(8,128)(2,1)S(1)}, bf16[10,128,128]{2,1,0:T(8,128)(2,1)S(1)}, u32[]{:S(2)}, u32[]{:S(2)}) collective-permute-start(bf16[10,128,128]{2,1,0:T(8,128)(2,1)S(1)} %collective-permute-done.20), channel_id=1, source_target_pairs={{0,8},{2,10},{8,16},{10,18},{16,24},{18,26},{24,28},{26,30},{28,20... | collective-permute-start | bytes 983048 | tf_op jit(solution)/shard_map/ppermute | solution.py:36
  73.3 1.0 bitcast_dynamic-update-slice_fusion.4
  74.4 1.0 bitcast_dynamic-update-slice_fusion.2
  75.4 1.0 bitcast_dynamic-update-slice_fusion
  76.5 1.0 bitcast_dynamic-update-slice_fusion.18
  77.5 0.8 fusion.293
  78.3 1.3 %collective-permute-done.28 = bf16[10,128,128]{2,1,0:T(8,128)(2,1)S(1)} collective-permute-done((bf16[10,128,128]{2,1,0:T(8,128)(2,1)S(1)}, bf16[10,128,128]{2,1,0:T(8,128)(2,1)S(1)}, u32[]{:S(2)}, u32[]{:S(2)}) %collective-permute-start.28) | collective-permute-done | bytes 327712 | tf_op jit(solution)/shard_map/ppermute | solution.py:37
  80.2 0.8 fusion.300
  84.0 1.0 bitcast_dynamic-update-slice_fusion.9
  85.0 1.0 bitcast_dynamic-update-slice_fusion.19
  86.1 0.8 fusion.301
  86.8 0.8 fusion.308
  88.4 0.7 fusion.18
  89.9 0.6 collective-permute-start.27
  90.4 0.7 fusion.16
  92.8 0.5 fusion.75
  94.6 0.5 fusion.81
  96.1 0.5 fusion.72
  97.6 0.7 fusion.78
  99.4 2.4 %convolution_convert_fusion = bf16[60,5120]{1,0:T(8,128)(2,1)S(1)} fusion(bf16[1280,5120]{1,0:T(8,128)(2,1)S(1)} %bitcast.643, bf16[60,640]{1,0:T(8,128)(2,1)S(1)} %bitcast.654, bf16[60,640]{1,0:T(8,128)(2,1)S(1)} %bitcast.655), kind=kOutput, calls=%fused_computation | convolution fusion | flops 787046400 | bytes 13875200 | tf_op jit(solution)/shard_map/dot_general | solution.py:161
  101.8 1.6 %collective-permute-start.30 = (bf16[60,5120]{1,0:T(8,128)(2,1)S(1)}, bf16[60,5120]{1,0:T(8,128)(2,1)S(1)}, u32[]{:S(2)}, u32[]{:S(2)}) collective-permute-start(bf16[60,5120]{1,0:T(8,128)(2,1)S(1)} %convolution_convert_fusion), channel_id=1, source_target_pairs={{0,1},{1,0},{2,3},{3,2},{4,5},{5,4},{6,7},{7,6},{8,9},{9,8},{10,11... | collective-permute-start | bytes 1843208 | tf_op jit(solution)/shard_map/ppermute | solution.py:163
  103.3 2.4 %fusion.136 = f32[60,5120]{1,0:T(8,128)S(1)} fusion(bf16[1280,5120]{1,0:T(8,128)(2,1)S(1)} %bitcast.643, bf16[60,640]{1,0:T(8,128)(2,1)S(1)} %bitcast.652, bf16[60,640]{1,0:T(8,128)(2,1)S(1)} %bitcast.653), kind=kOutput, calls=%fused_computation.184 | convolution fusion | flops 786739200 | bytes 14489600 | tf_op jit(solution)/shard_map/dot_general | solution.py:165
  105.7 13.0 %collective-permute-done.30 = bf16[60,5120]{1,0:T(8,128)(2,1)S(1)} collective-permute-done((bf16[60,5120]{1,0:T(8,128)(2,1)S(1)}, bf16[60,5120]{1,0:T(8,128)(2,1)S(1)}, u32[]{:S(2)}, u32[]{:S(2)}) %collective-permute-start.30) | collective-permute-done | bytes 614432 | tf_op jit(solution)/shard_map/ppermute | solution.py:163
  118.7 1.1 add_convert_fusion
  (201 shorter events, 19.7 us)
Async XLA Ops:
  3.8 4.3 %copy-start.15 = (bf16[120,1280]{1,0:T(8,128)(2,1)S(1)}, bf16[120,1280]{1,0:T(8,128)(2,1)}, u32[]{:S(2)}) copy-start(bf16[120,1280]{1,0:T(8,128)(2,1)} %param.11) | copy-start | bytes 921604
  4.6 13.6 %collective-permute-start = (bf16[10,128,128]{2,1,0:T(8,128)(2,1)S(1)}, bf16[10,128,128]{2,1,0:T(8,128)(2,1)S(1)}, u32[]{:S(2)}, u32[]{:S(2)}) collective-permute-start(bf16[10,128,128]{2,1,0:T(8,128)(2,1)S(1)} %get-tuple-element.34), channel_id=1, source_target_pairs={{0,2},{2,0},{4,6},{6,4},{8,10},{10,8},{12,14},{14,12},{16,18},{18,... | collective-permute-start | bytes 983048 | tf_op jit(solution)/shard_map/ppermute | solution.py:40
  5.1 10.9 %collective-permute-start.1 = (bf16[10,128,128]{2,1,0:T(8,128)(2,1)S(1)}, bf16[10,128,128]{2,1,0:T(8,128)(2,1)S(1)}, u32[]{:S(2)}, u32[]{:S(2)}) collective-permute-start(bf16[10,128,128]{2,1,0:T(8,128)(2,1)S(1)} %get-tuple-element.34), channel_id=1, source_target_pairs={{0,8},{2,10},{8,16},{10,18},{16,24},{18,26},{24,28},{26,30},{28,20... | collective-permute-start | bytes 983048 | tf_op jit(solution)/shard_map/ppermute | solution.py:36
  7.8 10.4 %collective-permute-start.9 = (bf16[10,128,128]{2,1,0:T(8,128)(2,1)S(1)}, bf16[10,128,128]{2,1,0:T(8,128)(2,1)S(1)}, u32[]{:S(2)}, u32[]{:S(2)}) collective-permute-start(bf16[10,128,128]{2,1,0:T(8,128)(2,1)S(1)} %get-tuple-element.48), channel_id=1, source_target_pairs={{0,2},{2,0},{4,6},{6,4},{8,10},{10,8},{12,14},{14,12},{16,18},{18,... | collective-permute-start | bytes 983048 | tf_op jit(solution)/shard_map/ppermute | solution.py:41
  7.9 10.0 %collective-permute-start.10 = (bf16[10,128,128]{2,1,0:T(8,128)(2,1)S(1)}, bf16[10,128,128]{2,1,0:T(8,128)(2,1)S(1)}, u32[]{:S(2)}, u32[]{:S(2)}) collective-permute-start(bf16[10,128,128]{2,1,0:T(8,128)(2,1)S(1)} %get-tuple-element.48), channel_id=1, source_target_pairs={{8,0},{10,2},{16,8},{18,10},{24,16},{26,18},{28,24},{30,26},{20,28... | collective-permute-start | bytes 983048 | tf_op jit(solution)/shard_map/ppermute | solution.py:37
  16.0 9.5 %collective-permute-start.3 = (bf16[10,128,128]{2,1,0:T(8,128)(2,1)S(1)}, bf16[10,128,128]{2,1,0:T(8,128)(2,1)S(1)}, u32[]{:S(2)}, u32[]{:S(2)}) collective-permute-start(bf16[10,128,128]{2,1,0:T(8,128)(2,1)S(1)} %collective-permute-done.1), channel_id=1, source_target_pairs={{0,8},{2,10},{8,16},{10,18},{16,24},{18,26},{24,28},{26,30},{28,20... | collective-permute-start | bytes 983048 | tf_op jit(solution)/shard_map/ppermute | solution.py:36
  17.9 9.3 %collective-permute-start.12 = (bf16[10,128,128]{2,1,0:T(8,128)(2,1)S(1)}, bf16[10,128,128]{2,1,0:T(8,128)(2,1)}, u32[]{:S(2)}, u32[]{:S(2)}) collective-permute-start(bf16[10,128,128]{2,1,0:T(8,128)(2,1)S(1)} %collective-permute-done.10), channel_id=1, source_target_pairs={{8,0},{10,2},{16,8},{18,10},{24,16},{26,18},{28,24},{30,26},{20,28... | collective-permute-start | bytes 983048 | tf_op jit(solution)/shard_map/ppermute | solution.py:37
  18.6 9.6 %collective-permute-start.2 = (bf16[10,128,128]{2,1,0:T(8,128)(2,1)S(1)}, bf16[10,128,128]{2,1,0:T(8,128)(2,1)S(1)}, u32[]{:S(2)}, u32[]{:S(2)}) collective-permute-start(bf16[10,128,128]{2,1,0:T(8,128)(2,1)S(1)} %collective-permute-done.1), channel_id=1, source_target_pairs={{0,2},{2,0},{4,6},{6,4},{8,10},{10,8},{12,14},{14,12},{16,18},{18,... | collective-permute-start | bytes 983048 | tf_op jit(solution)/shard_map/ppermute | solution.py:40
  18.6 9.6 %collective-permute-start.11 = (bf16[10,128,128]{2,1,0:T(8,128)(2,1)S(1)}, bf16[10,128,128]{2,1,0:T(8,128)(2,1)S(1)}, u32[]{:S(2)}, u32[]{:S(2)}) collective-permute-start(bf16[10,128,128]{2,1,0:T(8,128)(2,1)S(1)} %collective-permute-done.10), channel_id=1, source_target_pairs={{0,2},{2,0},{4,6},{6,4},{8,10},{10,8},{12,14},{14,12},{16,18},{18,... | collective-permute-start | bytes 983048 | tf_op jit(solution)/shard_map/ppermute | solution.py:41
  25.5 8.7 %collective-permute-start.5 = (bf16[10,128,128]{2,1,0:T(8,128)(2,1)S(1)}, bf16[10,128,128]{2,1,0:T(8,128)(2,1)S(1)}, u32[]{:S(2)}, u32[]{:S(2)}) collective-permute-start(bf16[10,128,128]{2,1,0:T(8,128)(2,1)S(1)} %collective-permute-done.3), channel_id=1, source_target_pairs={{0,8},{2,10},{8,16},{10,18},{16,24},{18,26},{24,28},{26,30},{28,20... | collective-permute-start | bytes 983048 | tf_op jit(solution)/shard_map/ppermute | solution.py:36
  27.2 8.6 %collective-permute-start.14 = (bf16[10,128,128]{2,1,0:T(8,128)(2,1)}, bf16[10,128,128]{2,1,0:T(8,128)(2,1)}, u32[]{:S(2)}, u32[]{:S(2)}) collective-permute-start(bf16[10,128,128]{2,1,0:T(8,128)(2,1)} %collective-permute-done.12), channel_id=1, source_target_pairs={{8,0},{10,2},{16,8},{18,10},{24,16},{26,18},{28,24},{30,26},{20,28... | collective-permute-start | bytes 983048 | tf_op jit(solution)/shard_map/ppermute | solution.py:37
  28.2 17.6 %copy-start.1 = (bf16[10,128,128]{2,1,0:T(8,128)(2,1)}, bf16[10,128,128]{2,1,0:T(8,128)(2,1)S(1)}, u32[]{:S(2)}) copy-start(bf16[10,128,128]{2,1,0:T(8,128)(2,1)S(1)} %collective-permute-done.2) | copy-start | bytes 983044
  28.3 0.8 copy-start.9
  29.4 7.6 %collective-permute-start.4 = (bf16[10,128,128]{2,1,0:T(8,128)(2,1)S(1)}, bf16[10,128,128]{2,1,0:T(8,128)(2,1)S(1)}, u32[]{:S(2)}, u32[]{:S(2)}) collective-permute-start(bf16[10,128,128]{2,1,0:T(8,128)(2,1)S(1)} %collective-permute-done.3), channel_id=1, source_target_pairs={{0,2},{2,0},{4,6},{6,4},{8,10},{10,8},{12,14},{14,12},{16,18},{18,... | collective-permute-start | bytes 983048 | tf_op jit(solution)/shard_map/ppermute | solution.py:40
  29.4 8.3 %collective-permute-start.13 = (bf16[10,128,128]{2,1,0:T(8,128)(2,1)}, bf16[10,128,128]{2,1,0:T(8,128)(2,1)S(1)}, u32[]{:S(2)}, u32[]{:S(2)}) collective-permute-start(bf16[10,128,128]{2,1,0:T(8,128)(2,1)} %collective-permute-done.12), channel_id=1, source_target_pairs={{0,2},{2,0},{4,6},{6,4},{8,10},{10,8},{12,14},{14,12},{16,18},{18,... | collective-permute-start | bytes 983048 | tf_op jit(solution)/shard_map/ppermute | solution.py:41
  34.2 11.8 %copy-start.3 = (bf16[10,128,128]{2,1,0:T(8,128)(2,1)}, bf16[10,128,128]{2,1,0:T(8,128)(2,1)S(1)}, u32[]{:S(2)}) copy-start(bf16[10,128,128]{2,1,0:T(8,128)(2,1)S(1)} %collective-permute-done.5) | copy-start | bytes 983044
  34.2 8.0 %collective-permute-start.7 = (bf16[10,128,128]{2,1,0:T(8,128)(2,1)S(1)}, bf16[10,128,128]{2,1,0:T(8,128)(2,1)}, u32[]{:S(2)}, u32[]{:S(2)}) collective-permute-start(bf16[10,128,128]{2,1,0:T(8,128)(2,1)S(1)} %collective-permute-done.5), channel_id=1, source_target_pairs={{0,8},{2,10},{8,16},{10,18},{16,24},{18,26},{24,28},{26,30},{28,20... | collective-permute-start | bytes 983048 | tf_op jit(solution)/shard_map/ppermute | solution.py:36
  35.7 7.6 %collective-permute-start.16 = (bf16[10,128,128]{2,1,0:T(8,128)(2,1)}, bf16[10,128,128]{2,1,0:T(8,128)(2,1)}, u32[]{:S(2)}, u32[]{:S(2)}) collective-permute-start(bf16[10,128,128]{2,1,0:T(8,128)(2,1)} %collective-permute-done.14), channel_id=1, source_target_pairs={{8,0},{10,2},{16,8},{18,10},{24,16},{26,18},{28,24},{30,26},{20,28... | collective-permute-start | bytes 983048 | tf_op jit(solution)/shard_map/ppermute | solution.py:37
  37.0 0.7 copy-start.5
  37.7 0.7 copy-start.11
  38.9 5.2 %collective-permute-start.6 = (bf16[10,128,128]{2,1,0:T(8,128)(2,1)S(1)}, bf16[10,128,128]{2,1,0:T(8,128)(2,1)S(1)}, u32[]{:S(2)}, u32[]{:S(2)}) collective-permute-start(bf16[10,128,128]{2,1,0:T(8,128)(2,1)S(1)} %collective-permute-done.5), channel_id=1, source_target_pairs={{0,2},{2,0},{4,6},{6,4},{8,10},{10,8},{12,14},{14,12},{16,18},{18,... | collective-permute-start | bytes 983048 | tf_op jit(solution)/shard_map/ppermute | solution.py:40
  38.9 5.9 %collective-permute-start.15 = (bf16[10,128,128]{2,1,0:T(8,128)(2,1)}, bf16[10,128,128]{2,1,0:T(8,128)(2,1)S(1)}, u32[]{:S(2)}, u32[]{:S(2)}) collective-permute-start(bf16[10,128,128]{2,1,0:T(8,128)(2,1)} %collective-permute-done.14), channel_id=1, source_target_pairs={{0,2},{2,0},{4,6},{6,4},{8,10},{10,8},{12,14},{14,12},{16,18},{18,... | collective-permute-start | bytes 983048 | tf_op jit(solution)/shard_map/ppermute | solution.py:41
  42.2 5.8 %collective-permute-start.8 = (bf16[10,128,128]{2,1,0:T(8,128)(2,1)}, bf16[10,128,128]{2,1,0:T(8,128)(2,1)}, u32[]{:S(2)}, u32[]{:S(2)}) collective-permute-start(bf16[10,128,128]{2,1,0:T(8,128)(2,1)} %collective-permute-done.7), channel_id=1, source_target_pairs={{0,2},{2,0},{4,6},{6,4},{8,10},{10,8},{12,14},{14,12},{16,18},{18,... | collective-permute-start | bytes 983048 | tf_op jit(solution)/shard_map/ppermute | solution.py:40
  43.4 5.4 %collective-permute-start.17 = (bf16[10,128,128]{2,1,0:T(8,128)(2,1)}, bf16[10,128,128]{2,1,0:T(8,128)(2,1)}, u32[]{:S(2)}, u32[]{:S(2)}) collective-permute-start(bf16[10,128,128]{2,1,0:T(8,128)(2,1)} %collective-permute-done.16), channel_id=1, source_target_pairs={{0,2},{2,0},{4,6},{6,4},{8,10},{10,8},{12,14},{14,12},{16,18},{18,... | collective-permute-start | bytes 983048 | tf_op jit(solution)/shard_map/ppermute | solution.py:41
  44.1 0.7 copy-start.7
  44.8 0.7 copy-start.13
  46.0 10.3 %collective-permute-start.18 = (bf16[10,128,128]{2,1,0:T(8,128)(2,1)}, bf16[10,128,128]{2,1,0:T(8,128)(2,1)S(1)}, u32[]{:S(2)}, u32[]{:S(2)}) collective-permute-start(bf16[10,128,128]{2,1,0:T(8,128)(2,1)} %collective-permute-done.7), channel_id=1, source_target_pairs={{0,8},{2,10},{8,16},{10,18},{16,24},{18,26},{24,28},{26,30},{28,20... | collective-permute-start | bytes 983048 | tf_op jit(solution)/shard_map/ppermute | solution.py:36
  47.5 11.1 %collective-permute-start.22 = (bf16[10,128,128]{2,1,0:T(8,128)(2,1)}, bf16[10,128,128]{2,1,0:T(8,128)(2,1)S(1)}, u32[]{:S(2)}, u32[]{:S(2)}) collective-permute-start(bf16[10,128,128]{2,1,0:T(8,128)(2,1)} %collective-permute-done.16), channel_id=1, source_target_pairs={{8,0},{10,2},{16,8},{18,10},{24,16},{26,18},{28,24},{30,26},{20,28... | collective-permute-start | bytes 983048 | tf_op jit(solution)/shard_map/ppermute | solution.py:37
  56.3 13.6 %collective-permute-start.19 = (bf16[10,128,128]{2,1,0:T(8,128)(2,1)S(1)}, bf16[10,128,128]{2,1,0:T(8,128)(2,1)S(1)}, u32[]{:S(2)}, u32[]{:S(2)}) collective-permute-start(bf16[10,128,128]{2,1,0:T(8,128)(2,1)S(1)} %collective-permute-done.18), channel_id=1, source_target_pairs={{0,2},{2,0},{4,6},{6,4},{8,10},{10,8},{12,14},{14,12},{16,18},{18,... | collective-permute-start | bytes 983048 | tf_op jit(solution)/shard_map/ppermute | solution.py:40
  56.3 10.1 %collective-permute-start.20 = (bf16[10,128,128]{2,1,0:T(8,128)(2,1)S(1)}, bf16[10,128,128]{2,1,0:T(8,128)(2,1)S(1)}, u32[]{:S(2)}, u32[]{:S(2)}) collective-permute-start(bf16[10,128,128]{2,1,0:T(8,128)(2,1)S(1)} %collective-permute-done.18), channel_id=1, source_target_pairs={{0,8},{2,10},{8,16},{10,18},{16,24},{18,26},{24,28},{26,30},{28,20... | collective-permute-start | bytes 983048 | tf_op jit(solution)/shard_map/ppermute | solution.py:36
  58.6 12.9 %collective-permute-start.23 = (bf16[10,128,128]{2,1,0:T(8,128)(2,1)S(1)}, bf16[10,128,128]{2,1,0:T(8,128)(2,1)S(1)}, u32[]{:S(2)}, u32[]{:S(2)}) collective-permute-start(bf16[10,128,128]{2,1,0:T(8,128)(2,1)S(1)} %collective-permute-done.22), channel_id=1, source_target_pairs={{0,2},{2,0},{4,6},{6,4},{8,10},{10,8},{12,14},{14,12},{16,18},{18,... | collective-permute-start | bytes 983048 | tf_op jit(solution)/shard_map/ppermute | solution.py:41
  58.8 9.9 %collective-permute-start.24 = (bf16[10,128,128]{2,1,0:T(8,128)(2,1)S(1)}, bf16[10,128,128]{2,1,0:T(8,128)(2,1)S(1)}, u32[]{:S(2)}, u32[]{:S(2)}) collective-permute-start(bf16[10,128,128]{2,1,0:T(8,128)(2,1)S(1)} %collective-permute-done.22), channel_id=1, source_target_pairs={{8,0},{10,2},{16,8},{18,10},{24,16},{26,18},{28,24},{30,26},{20,28... | collective-permute-start | bytes 983048 | tf_op jit(solution)/shard_map/ppermute | solution.py:37
  66.4 5.1 %collective-permute-start.21 = (bf16[10,128,128]{2,1,0:T(8,128)(2,1)S(1)}, bf16[10,128,128]{2,1,0:T(8,128)(2,1)S(1)}, u32[]{:S(2)}, u32[]{:S(2)}) collective-permute-start(bf16[10,128,128]{2,1,0:T(8,128)(2,1)S(1)} %collective-permute-done.20), channel_id=1, source_target_pairs={{0,2},{2,0},{4,6},{6,4},{8,10},{10,8},{12,14},{14,12},{16,18},{18,... | collective-permute-start | bytes 983048 | tf_op jit(solution)/shard_map/ppermute | solution.py:40
  68.7 2.8 %collective-permute-start.25 = (bf16[10,128,128]{2,1,0:T(8,128)(2,1)S(1)}, bf16[10,128,128]{2,1,0:T(8,128)(2,1)S(1)}, u32[]{:S(2)}, u32[]{:S(2)}) collective-permute-start(bf16[10,128,128]{2,1,0:T(8,128)(2,1)S(1)} %collective-permute-done.24), channel_id=1, source_target_pairs={{0,2},{2,0},{4,6},{6,4},{8,10},{10,8},{12,14},{14,12},{16,18},{18,... | collective-permute-start | bytes 983048 | tf_op jit(solution)/shard_map/ppermute | solution.py:41
  69.4 10.1 %collective-permute-start.28 = (bf16[10,128,128]{2,1,0:T(8,128)(2,1)S(1)}, bf16[10,128,128]{2,1,0:T(8,128)(2,1)S(1)}, u32[]{:S(2)}, u32[]{:S(2)}) collective-permute-start(bf16[10,128,128]{2,1,0:T(8,128)(2,1)S(1)} %collective-permute-done.24), channel_id=1, source_target_pairs={{8,0},{10,2},{16,8},{18,10},{24,16},{26,18},{28,24},{30,26},{20,28... | collective-permute-start | bytes 983048 | tf_op jit(solution)/shard_map/ppermute | solution.py:37
  69.9 11.1 %collective-permute-start.26 = (bf16[10,128,128]{2,1,0:T(8,128)(2,1)S(1)}, bf16[10,128,128]{2,1,0:T(8,128)(2,1)S(1)}, u32[]{:S(2)}, u32[]{:S(2)}) collective-permute-start(bf16[10,128,128]{2,1,0:T(8,128)(2,1)S(1)} %collective-permute-done.20), channel_id=1, source_target_pairs={{0,8},{2,10},{8,16},{10,18},{16,24},{18,26},{24,28},{26,30},{28,20... | collective-permute-start | bytes 983048 | tf_op jit(solution)/shard_map/ppermute | solution.py:36
  72.2 1.0 copy-start.10
  72.7 1.6 %copy-start.12 = (bf16[10,128,128]{2,1,0:T(8,128)(2,1)S(1)}, bf16[10,128,128]{2,1,0:T(8,128)(2,1)}, u32[]{:S(2)}) copy-start(bf16[10,128,128]{2,1,0:T(8,128)(2,1)} %copy-done.11) | copy-start | bytes 983044
  72.8 2.6 %copy-start.14 = (bf16[10,128,128]{2,1,0:T(8,128)(2,1)S(1)}, bf16[10,128,128]{2,1,0:T(8,128)(2,1)}, u32[]{:S(2)}) copy-start(bf16[10,128,128]{2,1,0:T(8,128)(2,1)} %copy-done.13) | copy-start | bytes 983044
  82.3 1.0 copy-start.2
  82.8 1.0 copy-start.6
  82.8 1.1 copy-start.4
  82.9 1.1 copy-start.8
  89.5 1.7 %collective-permute-start.29 = (bf16[10,128,128]{2,1,0:T(8,128)(2,1)S(1)}, bf16[10,128,128]{2,1,0:T(8,128)(2,1)S(1)}, u32[]{:S(2)}, u32[]{:S(2)}) collective-permute-start(bf16[10,128,128]{2,1,0:T(8,128)(2,1)S(1)} %collective-permute-done.28), channel_id=1, source_target_pairs={{0,2},{2,0},{4,6},{6,4},{8,10},{10,8},{12,14},{14,12},{16,18},{18,... | collective-permute-start | bytes 983048 | tf_op jit(solution)/shard_map/ppermute | solution.py:41
  89.9 1.9 %collective-permute-start.27 = (bf16[10,128,128]{2,1,0:T(8,128)(2,1)S(1)}, bf16[10,128,128]{2,1,0:T(8,128)(2,1)S(1)}, u32[]{:S(2)}, u32[]{:S(2)}) collective-permute-start(bf16[10,128,128]{2,1,0:T(8,128)(2,1)S(1)} %collective-permute-done.26), channel_id=1, source_target_pairs={{0,2},{2,0},{4,6},{6,4},{8,10},{10,8},{12,14},{14,12},{16,18},{18,... | collective-permute-start | bytes 983048 | tf_op jit(solution)/shard_map/ppermute | solution.py:40
  93.3 6.0 %slice-start = ((s8[13107200]{0:T(1024)(128)(4,1)}), s8[4194304]{0:T(1024)(128)(4,1)S(1)}, s32[]{:S(2)}) async-start(s8[13107200]{0:T(1024)(128)(4,1)} %bitcast.642), calls=%async_computation | async-start | bytes 8388608
  94.6 4.7 %slice-start.1 = ((s8[13107200]{0:T(1024)(128)(4,1)}), s8[4194304]{0:T(1024)(128)(4,1)S(1)}, s32[]{:S(2)}) async-start(s8[13107200]{0:T(1024)(128)(4,1)} %bitcast.642), calls=%async_computation.1 | async-start | bytes 8388608
  96.1 3.2 %slice-start.2 = ((s8[13107200]{0:T(1024)(128)(4,1)}), s8[4194304]{0:T(1024)(128)(4,1)S(1)}, s32[]{:S(2)}) async-start(s8[13107200]{0:T(1024)(128)(4,1)} %bitcast.642), calls=%async_computation.2 | async-start | bytes 8388608
  97.6 1.7 %slice-start.3 = ((s8[13107200]{0:T(1024)(128)(4,1)}), s8[524288]{0:T(1024)(128)(4,1)S(1)}, s32[]{:S(2)}) async-start(s8[13107200]{0:T(1024)(128)(4,1)} %bitcast.642), calls=%async_computation.3 | async-start | bytes 1048576
  101.8 16.9 %collective-permute-start.30 = (bf16[60,5120]{1,0:T(8,128)(2,1)S(1)}, bf16[60,5120]{1,0:T(8,128)(2,1)S(1)}, u32[]{:S(2)}, u32[]{:S(2)}) collective-permute-start(bf16[60,5120]{1,0:T(8,128)(2,1)S(1)} %convolution_convert_fusion), channel_id=1, source_target_pairs={{0,1},{1,0},{2,3},{3,2},{4,5},{5,4},{6,7},{7,6},{8,9},{9,8},{10,11... | collective-permute-start | bytes 1843208 | tf_op jit(solution)/shard_map/ppermute | solution.py:163
  103.3 15.4 %copy-start = (bf16[60,5120]{1,0:T(8,128)(2,1)S(1)}, bf16[60,5120]{1,0:T(8,128)(2,1)}, u32[]{:S(2)}) copy-start(bf16[60,5120]{1,0:T(8,128)(2,1)} %param.10) | copy-start | bytes 1843204
  103.3 15.4 %copy-start.16 = (f32[5120]{0:T(1024)S(1)}, f32[5120]{0:T(1024)}, u32[]{:S(2)}) copy-start(f32[5120]{0:T(1024)} %param.14) | copy-start | bytes 61444

commit v17 on v15

--- a/solution.py
+++ b/solution.py
@@ -29,18 +29,20 @@
         chip = me // 2
         core = me % 2
         pos = jnp.where(chip % 2 == 0, chip // 2, chips - 1 - chip // 2)
+        ring_a, ring_b = [packet_a], [packet_b]
+        for step in range(1, chips):
+            ring_a.append(lax.ppermute(ring_a[-1], "seq", forward))
+            ring_b.append(lax.ppermute(ring_b[-1], "seq", backward))
         got_a, got_b, ids_a, ids_b = [], [], [], []
-        cur_a, cur_b = packet_a, packet_b
         for step in range(chips):
-            if step > 0:
-                cur_a = lax.ppermute(cur_a, "seq", forward)
-                cur_b = lax.ppermute(cur_b, "seq", backward)
+            cur_a, cur_b = ring_a[step], ring_b[step]
+            if step + 1 < chips:
+                cur_a, _ = lax.optimization_barrier((cur_a, ring_a[step + 1]))
+                cur_b, _ = lax.optimization_barrier((cur_b, ring_b[step + 1]))
             src_a = chip_at((pos - step) % chips) * 2 + core
             src_b = chip_at((pos + step) % chips) * 2 + core
-            mate_a = lax.ppermute(cur_a, "seq", swap)
-            mate_b = lax.ppermute(cur_b, "seq", swap)
-            got_a += [cur_a, mate_a]
-            got_b += [cur_b, mate_b]
+            got_a += [ring_a[step], lax.ppermute(cur_a, "seq", swap)]
+            got_b += [ring_b[step], lax.ppermute(cur_b, "seq", swap)]
             ids_a += [src_a, src_a ^ 1]
             ids_b += [src_b, src_b ^ 1]
         return got_a, got_b, jnp.stack(ids_a), jnp.stack(ids_b)

time: 111 us -> 135 us (1.22)
  waiting for transfers between devices: 44.9 us -> 63.9 us
  local copies, waits for them, and re-layouts: 22.1 us -> 26.6 us
    ppermute x30, waiting for transfers between devices: 34.6 us -> 53.7 us  [the longest x7 33.7 us: gather_ring(): ring_b.append(lax.ppermute(ring_b[-1], 'seq', backward))]
    another operation x37, local copies, waits for them, and re-layouts: 6.11 us -> 9.54 us  [on_device(): jnp.stack([g[0, rows_dev, :2] for g in heard]).astype(jnp.float32)]
    unnamed x68 -> x56, local copies, waits for them, and re-layouts: 9.42 us -> 10.4 us
  transfers between devices with their start and end apart: 31 -> 31, of which waited for: 12 -> 13; matrix products, arithmetic and copies ran while one was open for 25% -> 25% of each run, Pallas kernels for 0% -> 0%
where the time goes in v17:
time: 135 us; the launch traced here: 134 us
  waiting for transfers between devices  63.9 us (47%)
  local copies, waits for them, and re-layouts  26.6 us (20%)
  starting transfers between devices  20.1 us (15%)
  matrix products  15.4 us (11%)
  other arithmetic  5.56 us (4%)
  between operations  2.54 us (2%)
    ppermute x7, waiting for transfers between devices, gather_ring(): ring_b.append(lax.ppermute(ring_b[-1], 'seq', backward))  33.7 us
    ppermute x7, waiting for transfers between devices, gather_ring(): ring_a.append(lax.ppermute(ring_a[-1], 'seq', forward))  19.1 us
    unnamed x56, local copies, waits for them, and re-layouts  10.4 us
    ppermute x1, waiting for transfers between devices, on_device(): came = lax.ppermute(other, 'tp', [(0, 1), (1, 0)])  10.2 us
    another operation x37, local copies, waits for them, and re-layouts, on_device(): jnp.stack([g[0, rows_dev, :2] for g in heard]).astype(jnp.float32)  9.54 us
    ppermute x7, starting transfers between devices, gather_ring(): ring_a.append(lax.ppermute(ring_a[-1], 'seq', forward))  9.1 us
    ppermute x7, starting transfers between devices, gather_ring(): ring_b.append(lax.ppermute(ring_b[-1], 'seq', backward))  6.19 us
    dot_general x12, matrix products, attend_part(): jnp.einsum('hqd,nhkd->hqnk', queries_3d, keys, preferred_element_type=jnp...  6.13 us
  transfers between devices with their start and end apart: 31, of which 13 were waited for; matrix products, arithmetic and copies ran while one was open for 25% of the time, Pallas kernels for 0%

profile of v17, /device:TPU:0, one launch (start us, length us, event | category | flops | bytes accessed | tf_op | source)
XLA Modules:
  0.0 134.1 jit_solution(16286176705351961513)
XLA Ops:
  0.0 1.0 fusion.237
  1.0 1.0 fusion.238
  4.6 3.1 %collective-permute-start = (bf16[10,128,128]{2,1,0:T(8,128)(2,1)S(1)}, bf16[10,128,128]{2,1,0:T(8,128)(2,1)S(1)}, u32[]{:S(2)}, u32[]{:S(2)}) collective-permute-start(bf16[10,128,128]{2,1,0:T(8,128)(2,1)S(1)} %get-tuple-element.62), channel_id=1, source_target_pairs={{0,8},{2,10},{8,16},{10,18},{16,24},{18,26},{24,28},{26,30},{28,20... | collective-permute-start | bytes 983048 | tf_op jit(solution)/shard_map/ppermute | solution.py:34
  9.1 6.2 %collective-permute-done = bf16[10,128,128]{2,1,0:T(8,128)(2,1)S(1)} collective-permute-done((bf16[10,128,128]{2,1,0:T(8,128)(2,1)S(1)}, bf16[10,128,128]{2,1,0:T(8,128)(2,1)S(1)}, u32[]{:S(2)}, u32[]{:S(2)}) %collective-permute-start) | collective-permute-done | bytes 327712 | tf_op jit(solution)/shard_map/ppermute | solution.py:34
  15.3 1.5 %collective-permute-done.10 = bf16[10,128,128]{2,1,0:T(8,128)(2,1)S(1)} collective-permute-done((bf16[10,128,128]{2,1,0:T(8,128)(2,1)S(1)}, bf16[10,128,128]{2,1,0:T(8,128)(2,1)S(1)}, u32[]{:S(2)}, u32[]{:S(2)}) %collective-permute-start.10) | collective-permute-done | bytes 327712 | tf_op jit(solution)/shard_map/ppermute | solution.py:35
  16.9 1.6 %collective-permute-start.2 = (bf16[10,128,128]{2,1,0:T(8,128)(2,1)S(1)}, bf16[10,128,128]{2,1,0:T(8,128)(2,1)}, u32[]{:S(2)}, u32[]{:S(2)}) collective-permute-start(bf16[10,128,128]{2,1,0:T(8,128)(2,1)S(1)} %collective-permute-done), channel_id=1, source_target_pairs={{0,8},{2,10},{8,16},{10,18},{16,24},{18,26},{24,28},{26,30},{28,20... | collective-permute-start | bytes 983048 | tf_op jit(solution)/shard_map/ppermute | solution.py:34
  19.1 9.2 %collective-permute-done.12 = bf16[10,128,128]{2,1,0:T(8,128)(2,1)S(1)} collective-permute-done((bf16[10,128,128]{2,1,0:T(8,128)(2,1)S(1)}, bf16[10,128,128]{2,1,0:T(8,128)(2,1)S(1)}, u32[]{:S(2)}, u32[]{:S(2)}) %collective-permute-start.12) | collective-permute-done | bytes 327712 | tf_op jit(solution)/shard_map/ppermute | solution.py:35
  28.3 0.5 collective-permute-start.3
  28.8 1.6 %collective-permute-start.4 = (bf16[10,128,128]{2,1,0:T(8,128)(2,1)}, bf16[10,128,128]{2,1,0:T(8,128)(2,1)}, u32[]{:S(2)}, u32[]{:S(2)}) collective-permute-start(bf16[10,128,128]{2,1,0:T(8,128)(2,1)} %collective-permute-done.2), channel_id=1, source_target_pairs={{0,8},{2,10},{8,16},{10,18},{16,24},{18,26},{24,28},{26,30},{28,20... | collective-permute-start | bytes 983048 | tf_op jit(solution)/shard_map/ppermute | solution.py:34
  30.4 0.7 slice_bitcast_fusion.14
  31.1 0.5 collective-permute-start.14
  32.0 8.4 %collective-permute-done.14 = bf16[10,128,128]{2,1,0:T(8,128)(2,1)S(1)} collective-permute-done((bf16[10,128,128]{2,1,0:T(8,128)(2,1)S(1)}, bf16[10,128,128]{2,1,0:T(8,128)(2,1)S(1)}, u32[]{:S(2)}, u32[]{:S(2)}) %collective-permute-start.14) | collective-permute-done | bytes 327712 | tf_op jit(solution)/shard_map/ppermute | solution.py:35
  40.5 0.5 collective-permute-start.5
  41.0 1.5 %collective-permute-start.6 = (bf16[10,128,128]{2,1,0:T(8,128)(2,1)}, bf16[10,128,128]{2,1,0:T(8,128)(2,1)}, u32[]{:S(2)}, u32[]{:S(2)}) collective-permute-start(bf16[10,128,128]{2,1,0:T(8,128)(2,1)} %collective-permute-done.4), channel_id=1, source_target_pairs={{0,8},{2,10},{8,16},{10,18},{16,24},{18,26},{24,28},{26,30},{28,20... | collective-permute-start | bytes 983048 | tf_op jit(solution)/shard_map/ppermute | solution.py:34
  42.5 0.7 slice_bitcast_fusion.12
  43.2 0.5 collective-permute-start.16
  43.7 0.7 slice_bitcast_fusion.15
  44.8 7.9 %collective-permute-done.16 = bf16[10,128,128]{2,1,0:T(8,128)(2,1)} collective-permute-done((bf16[10,128,128]{2,1,0:T(8,128)(2,1)S(1)}, bf16[10,128,128]{2,1,0:T(8,128)(2,1)}, u32[]{:S(2)}, u32[]{:S(2)}) %collective-permute-start.16) | collective-permute-done | bytes 327712 | tf_op jit(solution)/shard_map/ppermute | solution.py:35
  52.8 0.5 collective-permute-start.7
  53.3 0.5 collective-permute-start.8
  53.7 0.7 slice_bitcast_fusion.10
  54.4 0.7 slice_bitcast_fusion.1
  55.1 1.6 %collective-permute-start.18 = (bf16[10,128,128]{2,1,0:T(8,128)(2,1)}, bf16[10,128,128]{2,1,0:T(8,128)(2,1)S(1)}, u32[]{:S(2)}, u32[]{:S(2)}) collective-permute-start(bf16[10,128,128]{2,1,0:T(8,128)(2,1)} %collective-permute-done.16), channel_id=1, source_target_pairs={{8,0},{10,2},{16,8},{18,10},{24,16},{26,18},{28,24},{30,26},{20,28... | collective-permute-start | bytes 983048 | tf_op jit(solution)/shard_map/ppermute | solution.py:35
  56.7 0.7 slice_bitcast_fusion.13
  57.3 0.7 slice_bitcast_fusion.4
  58.4 6.3 %collective-permute-done.18 = bf16[10,128,128]{2,1,0:T(8,128)(2,1)S(1)} collective-permute-done((bf16[10,128,128]{2,1,0:T(8,128)(2,1)}, bf16[10,128,128]{2,1,0:T(8,128)(2,1)S(1)}, u32[]{:S(2)}, u32[]{:S(2)}) %collective-permute-start.18) | collective-permute-done | bytes 327712 | tf_op jit(solution)/shard_map/ppermute | solution.py:35
  64.7 0.5 collective-permute-start.9
  65.2 0.7 slice_bitcast_fusion.11
  65.9 0.7 slice_bitcast_fusion.2
  66.8 0.4 collective-permute-start.20
  67.3 1.6 %collective-permute-start.24 = (bf16[10,128,128]{2,1,0:T(8,128)(2,1)S(1)}, bf16[10,128,128]{2,1,0:T(8,128)(2,1)S(1)}, u32[]{:S(2)}, u32[]{:S(2)}) collective-permute-start(bf16[10,128,128]{2,1,0:T(8,128)(2,1)S(1)} %collective-permute-done.18), channel_id=1, source_target_pairs={{8,0},{10,2},{16,8},{18,10},{24,16},{26,18},{28,24},{30,26},{20,28... | collective-permute-start | bytes 983048 | tf_op jit(solution)/shard_map/ppermute | solution.py:35
  68.8 0.7 slice_bitcast_fusion.9
  69.6 0.7 slice_bitcast_fusion
  71.1 5.4 %collective-permute-done.20 = bf16[10,128,128]{2,1,0:T(8,128)(2,1)S(1)} collective-permute-done((bf16[10,128,128]{2,1,0:T(8,128)(2,1)S(1)}, bf16[10,128,128]{2,1,0:T(8,128)(2,1)S(1)}, u32[]{:S(2)}, u32[]{:S(2)}) %collective-permute-start.20) | collective-permute-done | bytes 327712 | tf_op jit(solution)/shard_map/ppermute | solution.py:34
  77.6 1.6 %collective-permute-start.26 = (bf16[10,128,128]{2,1,0:T(8,128)(2,1)S(1)}, bf16[10,128,128]{2,1,0:T(8,128)(2,1)S(1)}, u32[]{:S(2)}, u32[]{:S(2)}) collective-permute-start(bf16[10,128,128]{2,1,0:T(8,128)(2,1)S(1)} %collective-permute-done.24), channel_id=1, source_target_pairs={{8,0},{10,2},{16,8},{18,10},{24,16},{26,18},{28,24},{30,26},{20,28... | collective-permute-start | bytes 983048 | tf_op jit(solution)/shard_map/ppermute | solution.py:35
  79.4 7.5 %collective-permute-done.22 = bf16[10,128,128]{2,1,0:T(8,128)(2,1)S(1)} collective-permute-done((bf16[10,128,128]{2,1,0:T(8,128)(2,1)S(1)}, bf16[10,128,128]{2,1,0:T(8,128)(2,1)S(1)}, u32[]{:S(2)}, u32[]{:S(2)}) %collective-permute-start.22) | collective-permute-done | bytes 327712 | tf_op jit(solution)/shard_map/ppermute | solution.py:34
  88.6 0.5 collective-permute-done.27
  91.7 1.0 bitcast_dynamic-update-slice_fusion.14
  92.7 1.0 bitcast_dynamic-update-slice_fusion.13
  93.7 1.0 bitcast_dynamic-update-slice_fusion.12
  94.7 1.0 bitcast_dynamic-update-slice_fusion.11
  95.7 1.0 bitcast_dynamic-update-slice_fusion.10
  96.8 1.0 bitcast_dynamic-update-slice_fusion.9
  97.8 1.0 bitcast_dynamic-update-slice_fusion.19
  98.8 0.8 fusion.252
  99.6 0.8 fusion.251
  100.8 0.6 copy-done.2
  101.6 1.0 bitcast_dynamic-update-slice_fusion.3
  102.7 1.0 bitcast_dynamic-update-slice_fusion.1
  103.7 1.0 bitcast_dynamic-update-slice_fusion
  104.7 1.0 bitcast_dynamic-update-slice_fusion.18
  105.8 0.8 fusion.246
  106.9 0.8 fusion.245
  108.4 0.7 fusion.16
  109.8 0.5 fusion.66
  111.0 0.7 fusion.18
  112.5 0.5 fusion.60
  113.8 2.4 %convolution_convert_fusion = bf16[60,5120]{1,0:T(8,128)(2,1)S(1)} fusion(bf16[1280,5120]{1,0:T(8,128)(2,1)S(1)} %bitcast.603, bf16[60,640]{1,0:T(8,128)(2,1)S(1)} %bitcast.614, bf16[60,640]{1,0:T(8,128)(2,1)S(1)} %bitcast.612), kind=kOutput, calls=%fused_computation | convolution fusion | flops 787046400 | bytes 13875200 | tf_op jit(solution)/shard_map/dot_general | solution.py:162
  116.2 1.6 %collective-permute-start.30 = (bf16[60,5120]{1,0:T(8,128)(2,1)S(1)}, bf16[60,5120]{1,0:T(8,128)(2,1)S(1)}, u32[]{:S(2)}, u32[]{:S(2)}) collective-permute-start(bf16[60,5120]{1,0:T(8,128)(2,1)S(1)} %convolution_convert_fusion), channel_id=1, source_target_pairs={{0,1},{1,0},{2,3},{3,2},{4,5},{5,4},{6,7},{7,6},{8,9},{9,8},{10,11... | collective-permute-start | bytes 1843208 | tf_op jit(solution)/shard_map/ppermute | solution.py:164
  117.7 0.7 fusion.69
  119.2 0.5 fusion.63
  120.4 2.4 %fusion.146 = f32[60,5120]{1,0:T(8,128)S(1)} fusion(bf16[1280,5120]{1,0:T(8,128)(2,1)S(1)} %bitcast.603, bf16[60,640]{1,0:T(8,128)(2,1)S(1)} %bitcast.615, bf16[60,640]{1,0:T(8,128)(2,1)S(1)} %bitcast.613), kind=kOutput, calls=%fused_computation.184 | convolution fusion | flops 786739200 | bytes 14489600 | tf_op jit(solution)/shard_map/dot_general | solution.py:166
  122.8 10.2 %collective-permute-done.30 = bf16[60,5120]{1,0:T(8,128)(2,1)S(1)} collective-permute-done((bf16[60,5120]{1,0:T(8,128)(2,1)S(1)}, bf16[60,5120]{1,0:T(8,128)(2,1)S(1)}, u32[]{:S(2)}, u32[]{:S(2)}) %collective-permute-start.30) | collective-permute-done | bytes 614432 | tf_op jit(solution)/shard_map/ppermute | solution.py:164
  133.0 1.1 add_convert_fusion
  (179 shorter events, 16.7 us)
Async XLA Ops:
  2.3 5.3 %copy-start.9 = (bf16[120,1280]{1,0:T(8,128)(2,1)S(1)}, bf16[120,1280]{1,0:T(8,128)(2,1)}, u32[]{:S(2)}) copy-start(bf16[120,1280]{1,0:T(8,128)(2,1)} %param.11) | copy-start | bytes 921604
  4.6 10.7 %collective-permute-start = (bf16[10,128,128]{2,1,0:T(8,128)(2,1)S(1)}, bf16[10,128,128]{2,1,0:T(8,128)(2,1)S(1)}, u32[]{:S(2)}, u32[]{:S(2)}) collective-permute-start(bf16[10,128,128]{2,1,0:T(8,128)(2,1)S(1)} %get-tuple-element.62), channel_id=1, source_target_pairs={{0,8},{2,10},{8,16},{10,18},{16,24},{18,26},{24,28},{26,30},{28,20... | collective-permute-start | bytes 983048 | tf_op jit(solution)/shard_map/ppermute | solution.py:34
  7.7 9.2 %collective-permute-start.10 = (bf16[10,128,128]{2,1,0:T(8,128)(2,1)S(1)}, bf16[10,128,128]{2,1,0:T(8,128)(2,1)S(1)}, u32[]{:S(2)}, u32[]{:S(2)}) collective-permute-start(bf16[10,128,128]{2,1,0:T(8,128)(2,1)S(1)} %get-tuple-element.76), channel_id=1, source_target_pairs={{8,0},{10,2},{16,8},{18,10},{24,16},{26,18},{28,24},{30,26},{20,28... | collective-permute-start | bytes 983048 | tf_op jit(solution)/shard_map/ppermute | solution.py:35
  15.3 15.8 %collective-permute-start.1 = (bf16[10,128,128]{2,1,0:T(8,128)(2,1)S(1)}, bf16[10,128,128]{2,1,0:T(8,128)(2,1)S(1)}, u32[]{:S(2)}, u32[]{:S(2)}) collective-permute-start(bf16[10,128,128]{2,1,0:T(8,128)(2,1)S(1)} %get-tuple-element.62), channel_id=1, source_target_pairs={{0,2},{2,0},{4,6},{6,4},{8,10},{10,8},{12,14},{14,12},{16,18},{18,... | collective-permute-start | bytes 983048 | tf_op jit(solution)/shard_map/ppermute | solution.py:44
  16.9 14.7 %collective-permute-start.11 = (bf16[10,128,128]{2,1,0:T(8,128)(2,1)S(1)}, bf16[10,128,128]{2,1,0:T(8,128)(2,1)S(1)}, u32[]{:S(2)}, u32[]{:S(2)}) collective-permute-start(bf16[10,128,128]{2,1,0:T(8,128)(2,1)S(1)} %get-tuple-element.76), channel_id=1, source_target_pairs={{0,2},{2,0},{4,6},{6,4},{8,10},{10,8},{12,14},{14,12},{16,18},{18,... | collective-permute-start | bytes 983048 | tf_op jit(solution)/shard_map/ppermute | solution.py:45
  16.9 11.4 %collective-permute-start.2 = (bf16[10,128,128]{2,1,0:T(8,128)(2,1)S(1)}, bf16[10,128,128]{2,1,0:T(8,128)(2,1)}, u32[]{:S(2)}, u32[]{:S(2)}) collective-permute-start(bf16[10,128,128]{2,1,0:T(8,128)(2,1)S(1)} %collective-permute-done), channel_id=1, source_target_pairs={{0,8},{2,10},{8,16},{10,18},{16,24},{18,26},{24,28},{26,30},{28,20... | collective-permute-start | bytes 983048 | tf_op jit(solution)/shard_map/ppermute | solution.py:34
  18.4 9.8 %collective-permute-start.12 = (bf16[10,128,128]{2,1,0:T(8,128)(2,1)S(1)}, bf16[10,128,128]{2,1,0:T(8,128)(2,1)S(1)}, u32[]{:S(2)}, u32[]{:S(2)}) collective-permute-start(bf16[10,128,128]{2,1,0:T(8,128)(2,1)S(1)} %collective-permute-done.10), channel_id=1, source_target_pairs={{8,0},{10,2},{16,8},{18,10},{24,16},{26,18},{28,24},{30,26},{20,28... | collective-permute-start | bytes 983048 | tf_op jit(solution)/shard_map/ppermute | solution.py:35
  28.3 16.1 %collective-permute-start.13 = (bf16[10,128,128]{2,1,0:T(8,128)(2,1)S(1)}, bf16[10,128,128]{2,1,0:T(8,128)(2,1)S(1)}, u32[]{:S(2)}, u32[]{:S(2)}) collective-permute-start(bf16[10,128,128]{2,1,0:T(8,128)(2,1)S(1)} %collective-permute-done.10), channel_id=1, source_target_pairs={{0,2},{2,0},{4,6},{6,4},{8,10},{10,8},{12,14},{14,12},{16,18},{18,... | collective-permute-start | bytes 983048 | tf_op jit(solution)/shard_map/ppermute | solution.py:45
  28.3 14.9 %collective-permute-start.3 = (bf16[10,128,128]{2,1,0:T(8,128)(2,1)S(1)}, bf16[10,128,128]{2,1,0:T(8,128)(2,1)}, u32[]{:S(2)}, u32[]{:S(2)}) collective-permute-start(bf16[10,128,128]{2,1,0:T(8,128)(2,1)S(1)} %collective-permute-done), channel_id=1, source_target_pairs={{0,2},{2,0},{4,6},{6,4},{8,10},{10,8},{12,14},{14,12},{16,18},{18,... | collective-permute-start | bytes 983048 | tf_op jit(solution)/shard_map/ppermute | solution.py:44
  28.8 11.7 %collective-permute-start.4 = (bf16[10,128,128]{2,1,0:T(8,128)(2,1)}, bf16[10,128,128]{2,1,0:T(8,128)(2,1)}, u32[]{:S(2)}, u32[]{:S(2)}) collective-permute-start(bf16[10,128,128]{2,1,0:T(8,128)(2,1)} %collective-permute-done.2), channel_id=1, source_target_pairs={{0,8},{2,10},{8,16},{10,18},{16,24},{18,26},{24,28},{26,30},{28,20... | collective-permute-start | bytes 983048 | tf_op jit(solution)/shard_map/ppermute | solution.py:34
  31.1 35.6 %copy-start.7 = (bf16[10,128,128]{2,1,0:T(8,128)(2,1)}, bf16[10,128,128]{2,1,0:T(8,128)(2,1)S(1)}, u32[]{:S(2)}) copy-start(bf16[10,128,128]{2,1,0:T(8,128)(2,1)S(1)} %collective-permute-done.1) | copy-start | bytes 983044
  31.1 9.4 %collective-permute-start.14 = (bf16[10,128,128]{2,1,0:T(8,128)(2,1)S(1)}, bf16[10,128,128]{2,1,0:T(8,128)(2,1)S(1)}, u32[]{:S(2)}, u32[]{:S(2)}) collective-permute-start(bf16[10,128,128]{2,1,0:T(8,128)(2,1)S(1)} %collective-permute-done.12), channel_id=1, source_target_pairs={{8,0},{10,2},{16,8},{18,10},{24,16},{26,18},{28,24},{30,26},{20,28... | collective-permute-start | bytes 983048 | tf_op jit(solution)/shard_map/ppermute | solution.py:35
  31.6 23.5 %copy-start.1 = (bf16[10,128,128]{2,1,0:T(8,128)(2,1)}, bf16[10,128,128]{2,1,0:T(8,128)(2,1)S(1)}, u32[]{:S(2)}) copy-start(bf16[10,128,128]{2,1,0:T(8,128)(2,1)S(1)} %collective-permute-done.11) | copy-start | bytes 983044
  40.5 26.3 %copy-start.5 = (bf16[10,128,128]{2,1,0:T(8,128)(2,1)}, bf16[10,128,128]{2,1,0:T(8,128)(2,1)S(1)}, u32[]{:S(2)}) copy-start(bf16[10,128,128]{2,1,0:T(8,128)(2,1)S(1)} %collective-permute-done.14) | copy-start | bytes 983044
  40.5 16.9 %collective-permute-start.15 = (bf16[10,128,128]{2,1,0:T(8,128)(2,1)S(1)}, bf16[10,128,128]{2,1,0:T(8,128)(2,1)}, u32[]{:S(2)}, u32[]{:S(2)}) collective-permute-start(bf16[10,128,128]{2,1,0:T(8,128)(2,1)S(1)} %collective-permute-done.12), channel_id=1, source_target_pairs={{0,2},{2,0},{4,6},{6,4},{8,10},{10,8},{12,14},{14,12},{16,18},{18,... | collective-permute-start | bytes 983048 | tf_op jit(solution)/shard_map/ppermute | solution.py:45
  40.5 14.6 %collective-permute-start.5 = (bf16[10,128,128]{2,1,0:T(8,128)(2,1)}, bf16[10,128,128]{2,1,0:T(8,128)(2,1)}, u32[]{:S(2)}, u32[]{:S(2)}) collective-permute-start(bf16[10,128,128]{2,1,0:T(8,128)(2,1)} %collective-permute-done.2), channel_id=1, source_target_pairs={{0,2},{2,0},{4,6},{6,4},{8,10},{10,8},{12,14},{14,12},{16,18},{18,... | collective-permute-start | bytes 983048 | tf_op jit(solution)/shard_map/ppermute | solution.py:44
  41.0 11.7 %collective-permute-start.6 = (bf16[10,128,128]{2,1,0:T(8,128)(2,1)}, bf16[10,128,128]{2,1,0:T(8,128)(2,1)}, u32[]{:S(2)}, u32[]{:S(2)}) collective-permute-start(bf16[10,128,128]{2,1,0:T(8,128)(2,1)} %collective-permute-done.4), channel_id=1, source_target_pairs={{0,8},{2,10},{8,16},{10,18},{16,24},{18,26},{24,28},{26,30},{28,20... | collective-permute-start | bytes 983048 | tf_op jit(solution)/shard_map/ppermute | solution.py:34
  43.2 9.5 %collective-permute-start.16 = (bf16[10,128,128]{2,1,0:T(8,128)(2,1)S(1)}, bf16[10,128,128]{2,1,0:T(8,128)(2,1)}, u32[]{:S(2)}, u32[]{:S(2)}) collective-permute-start(bf16[10,128,128]{2,1,0:T(8,128)(2,1)S(1)} %collective-permute-done.14), channel_id=1, source_target_pairs={{8,0},{10,2},{16,8},{18,10},{24,16},{26,18},{28,24},{30,26},{20,28... | collective-permute-start | bytes 983048 | tf_op jit(solution)/shard_map/ppermute | solution.py:35
  44.4 8.3 %copy-start.3 = (bf16[10,128,128]{2,1,0:T(8,128)(2,1)}, bf16[10,128,128]{2,1,0:T(8,128)(2,1)S(1)}, u32[]{:S(2)}) copy-start(bf16[10,128,128]{2,1,0:T(8,128)(2,1)S(1)} %collective-permute-done.13) | copy-start | bytes 983044
  52.7 13.2 %collective-permute-start.17 = (bf16[10,128,128]{2,1,0:T(8,128)(2,1)S(1)}, bf16[10,128,128]{2,1,0:T(8,128)(2,1)}, u32[]{:S(2)}, u32[]{:S(2)}) collective-permute-start(bf16[10,128,128]{2,1,0:T(8,128)(2,1)S(1)} %collective-permute-done.14), channel_id=1, source_target_pairs={{0,2},{2,0},{4,6},{6,4},{8,10},{10,8},{12,14},{14,12},{16,18},{18,... | collective-permute-start | bytes 983048 | tf_op jit(solution)/shard_map/ppermute | solution.py:45
  52.8 12.5 %collective-permute-start.7 = (bf16[10,128,128]{2,1,0:T(8,128)(2,1)}, bf16[10,128,128]{2,1,0:T(8,128)(2,1)}, u32[]{:S(2)}, u32[]{:S(2)}) collective-permute-start(bf16[10,128,128]{2,1,0:T(8,128)(2,1)} %collective-permute-done.4), channel_id=1, source_target_pairs={{0,2},{2,0},{4,6},{6,4},{8,10},{10,8},{12,14},{14,12},{16,18},{18,... | collective-permute-start | bytes 983048 | tf_op jit(solution)/shard_map/ppermute | solution.py:44
  53.3 11.5 %collective-permute-start.8 = (bf16[10,128,128]{2,1,0:T(8,128)(2,1)}, bf16[10,128,128]{2,1,0:T(8,128)(2,1)S(1)}, u32[]{:S(2)}, u32[]{:S(2)}) collective-permute-start(bf16[10,128,128]{2,1,0:T(8,128)(2,1)} %collective-permute-done.6), channel_id=1, source_target_pairs={{0,8},{2,10},{8,16},{10,18},{16,24},{18,26},{24,28},{26,30},{28,20... | collective-permute-start | bytes 983048 | tf_op jit(solution)/shard_map/ppermute | solution.py:34
  55.1 9.6 %collective-permute-start.18 = (bf16[10,128,128]{2,1,0:T(8,128)(2,1)}, bf16[10,128,128]{2,1,0:T(8,128)(2,1)S(1)}, u32[]{:S(2)}, u32[]{:S(2)}) collective-permute-start(bf16[10,128,128]{2,1,0:T(8,128)(2,1)} %collective-permute-done.16), channel_id=1, source_target_pairs={{8,0},{10,2},{16,8},{18,10},{24,16},{26,18},{28,24},{30,26},{20,28... | collective-permute-start | bytes 983048 | tf_op jit(solution)/shard_map/ppermute | solution.py:35
  64.7 4.9 %collective-permute-start.19 = (bf16[10,128,128]{2,1,0:T(8,128)(2,1)}, bf16[10,128,128]{2,1,0:T(8,128)(2,1)}, u32[]{:S(2)}, u32[]{:S(2)}) collective-permute-start(bf16[10,128,128]{2,1,0:T(8,128)(2,1)} %collective-permute-done.16), channel_id=1, source_target_pairs={{0,2},{2,0},{4,6},{6,4},{8,10},{10,8},{12,14},{14,12},{16,18},{18,... | collective-permute-start | bytes 983048 | tf_op jit(solution)/shard_map/ppermute | solution.py:45
  64.7 4.1 %collective-permute-start.9 = (bf16[10,128,128]{2,1,0:T(8,128)(2,1)}, bf16[10,128,128]{2,1,0:T(8,128)(2,1)}, u32[]{:S(2)}, u32[]{:S(2)}) collective-permute-start(bf16[10,128,128]{2,1,0:T(8,128)(2,1)} %collective-permute-done.6), channel_id=1, source_target_pairs={{0,2},{2,0},{4,6},{6,4},{8,10},{10,8},{12,14},{14,12},{16,18},{18,... | collective-permute-start | bytes 983048 | tf_op jit(solution)/shard_map/ppermute | solution.py:44
  66.8 9.6 %collective-permute-start.20 = (bf16[10,128,128]{2,1,0:T(8,128)(2,1)S(1)}, bf16[10,128,128]{2,1,0:T(8,128)(2,1)S(1)}, u32[]{:S(2)}, u32[]{:S(2)}) collective-permute-start(bf16[10,128,128]{2,1,0:T(8,128)(2,1)S(1)} %collective-permute-done.8), channel_id=1, source_target_pairs={{0,8},{2,10},{8,16},{10,18},{16,24},{18,26},{24,28},{26,30},{28,20... | collective-permute-start | bytes 983048 | tf_op jit(solution)/shard_map/ppermute | solution.py:34
  67.3 9.3 %collective-permute-start.24 = (bf16[10,128,128]{2,1,0:T(8,128)(2,1)S(1)}, bf16[10,128,128]{2,1,0:T(8,128)(2,1)S(1)}, u32[]{:S(2)}, u32[]{:S(2)}) collective-permute-start(bf16[10,128,128]{2,1,0:T(8,128)(2,1)S(1)} %collective-permute-done.18), channel_id=1, source_target_pairs={{8,0},{10,2},{16,8},{18,10},{24,16},{26,18},{28,24},{30,26},{20,28... | collective-permute-start | bytes 983048 | tf_op jit(solution)/shard_map/ppermute | solution.py:35
  76.4 11.4 %collective-permute-start.21 = (bf16[10,128,128]{2,1,0:T(8,128)(2,1)S(1)}, bf16[10,128,128]{2,1,0:T(8,128)(2,1)S(1)}, u32[]{:S(2)}, u32[]{:S(2)}) collective-permute-start(bf16[10,128,128]{2,1,0:T(8,128)(2,1)S(1)} %collective-permute-done.8), channel_id=1, source_target_pairs={{0,2},{2,0},{4,6},{6,4},{8,10},{10,8},{12,14},{14,12},{16,18},{18,... | collective-permute-start | bytes 983048 | tf_op jit(solution)/shard_map/ppermute | solution.py:44
  76.6 11.5 %collective-permute-start.25 = (bf16[10,128,128]{2,1,0:T(8,128)(2,1)S(1)}, bf16[10,128,128]{2,1,0:T(8,128)(2,1)S(1)}, u32[]{:S(2)}, u32[]{:S(2)}) collective-permute-start(bf16[10,128,128]{2,1,0:T(8,128)(2,1)S(1)} %collective-permute-done.18), channel_id=1, source_target_pairs={{0,2},{2,0},{4,6},{6,4},{8,10},{10,8},{12,14},{14,12},{16,18},{18,... | collective-permute-start | bytes 983048 | tf_op jit(solution)/shard_map/ppermute | solution.py:45
  77.2 9.8 %collective-permute-start.22 = (bf16[10,128,128]{2,1,0:T(8,128)(2,1)S(1)}, bf16[10,128,128]{2,1,0:T(8,128)(2,1)S(1)}, u32[]{:S(2)}, u32[]{:S(2)}) collective-permute-start(bf16[10,128,128]{2,1,0:T(8,128)(2,1)S(1)} %collective-permute-done.20), channel_id=1, source_target_pairs={{0,8},{2,10},{8,16},{10,18},{16,24},{18,26},{24,28},{26,30},{28,20... | collective-permute-start | bytes 983048 | tf_op jit(solution)/shard_map/ppermute | solution.py:34
  77.6 9.5 %collective-permute-start.26 = (bf16[10,128,128]{2,1,0:T(8,128)(2,1)S(1)}, bf16[10,128,128]{2,1,0:T(8,128)(2,1)S(1)}, u32[]{:S(2)}, u32[]{:S(2)}) collective-permute-start(bf16[10,128,128]{2,1,0:T(8,128)(2,1)S(1)} %collective-permute-done.24), channel_id=1, source_target_pairs={{8,0},{10,2},{16,8},{18,10},{24,16},{26,18},{28,24},{30,26},{20,28... | collective-permute-start | bytes 983048 | tf_op jit(solution)/shard_map/ppermute | solution.py:35
  86.9 1.6 %collective-permute-start.23 = (bf16[10,128,128]{2,1,0:T(8,128)(2,1)S(1)}, bf16[10,128,128]{2,1,0:T(8,128)(2,1)S(1)}, u32[]{:S(2)}, u32[]{:S(2)}) collective-permute-start(bf16[10,128,128]{2,1,0:T(8,128)(2,1)S(1)} %collective-permute-done.20), channel_id=1, source_target_pairs={{0,2},{2,0},{4,6},{6,4},{8,10},{10,8},{12,14},{14,12},{16,18},{18,... | collective-permute-start | bytes 983048 | tf_op jit(solution)/shard_map/ppermute | solution.py:44
  87.1 1.9 %collective-permute-start.27 = (bf16[10,128,128]{2,1,0:T(8,128)(2,1)S(1)}, bf16[10,128,128]{2,1,0:T(8,128)(2,1)S(1)}, u32[]{:S(2)}, u32[]{:S(2)}) collective-permute-start(bf16[10,128,128]{2,1,0:T(8,128)(2,1)S(1)} %collective-permute-done.24), channel_id=1, source_target_pairs={{0,2},{2,0},{4,6},{6,4},{8,10},{10,8},{12,14},{14,12},{16,18},{18,... | collective-permute-start | bytes 983048 | tf_op jit(solution)/shard_map/ppermute | solution.py:45
  87.6 12.8 %collective-permute-start.28 = (bf16[10,128,128]{2,1,0:T(8,128)(2,1)S(1)}, bf16[10,128,128]{2,1,0:T(8,128)(2,1)S(1)}, u32[]{:S(2)}, u32[]{:S(2)}) collective-permute-start(bf16[10,128,128]{2,1,0:T(8,128)(2,1)S(1)} %collective-permute-done.22), channel_id=1, source_target_pairs={{0,2},{2,0},{4,6},{6,4},{8,10},{10,8},{12,14},{14,12},{16,18},{18,... | collective-permute-start | bytes 983048 | tf_op jit(solution)/shard_map/ppermute | solution.py:44
  87.8 19.8 %collective-permute-start.29 = (bf16[10,128,128]{2,1,0:T(8,128)(2,1)S(1)}, bf16[10,128,128]{2,1,0:T(8,128)(2,1)S(1)}, u32[]{:S(2)}, u32[]{:S(2)}) collective-permute-start(bf16[10,128,128]{2,1,0:T(8,128)(2,1)S(1)} %collective-permute-done.26), channel_id=1, source_target_pairs={{0,2},{2,0},{4,6},{6,4},{8,10},{10,8},{12,14},{14,12},{16,18},{18,... | collective-permute-start | bytes 983048 | tf_op jit(solution)/shard_map/ppermute | solution.py:45
  90.6 1.0 copy-start.8
  100.4 1.0 copy-start.2
  100.4 1.1 copy-start.4
  101.4 1.2 copy-start.6
  107.6 6.1 %slice-start = ((s8[13107200]{0:T(1024)(128)(4,1)}), s8[4194304]{0:T(1024)(128)(4,1)S(1)}, s32[]{:S(2)}) async-start(s8[13107200]{0:T(1024)(128)(4,1)} %bitcast.602), calls=%async_computation | async-start | bytes 8388608
  109.1 4.7 %slice-start.1 = ((s8[13107200]{0:T(1024)(128)(4,1)}), s8[4194304]{0:T(1024)(128)(4,1)S(1)}, s32[]{:S(2)}) async-start(s8[13107200]{0:T(1024)(128)(4,1)} %bitcast.602), calls=%async_computation.1 | async-start | bytes 8388608
  110.6 3.2 %slice-start.2 = ((s8[13107200]{0:T(1024)(128)(4,1)}), s8[4194304]{0:T(1024)(128)(4,1)S(1)}, s32[]{:S(2)}) async-start(s8[13107200]{0:T(1024)(128)(4,1)} %bitcast.602), calls=%async_computation.2 | async-start | bytes 8388608
  112.5 1.3 slice-start.3
  116.2 16.8 %collective-permute-start.30 = (bf16[60,5120]{1,0:T(8,128)(2,1)S(1)}, bf16[60,5120]{1,0:T(8,128)(2,1)S(1)}, u32[]{:S(2)}, u32[]{:S(2)}) collective-permute-start(bf16[60,5120]{1,0:T(8,128)(2,1)S(1)} %convolution_convert_fusion), channel_id=1, source_target_pairs={{0,1},{1,0},{2,3},{3,2},{4,5},{5,4},{6,7},{7,6},{8,9},{9,8},{10,11... | collective-permute-start | bytes 1843208 | tf_op jit(solution)/shard_map/ppermute | solution.py:164
  120.4 12.6 %copy-start = (bf16[60,5120]{1,0:T(8,128)(2,1)S(1)}, bf16[60,5120]{1,0:T(8,128)(2,1)}, u32[]{:S(2)}) copy-start(bf16[60,5120]{1,0:T(8,128)(2,1)} %param.10) | copy-start | bytes 1843204
  120.4 12.6 %copy-start.10 = (f32[5120]{0:T(1024)S(1)}, f32[5120]{0:T(1024)}, u32[]{:S(2)}) copy-start(f32[5120]{0:T(1024)} %param.14) | copy-start | bytes 61444

commit v18 on v17

--- a/solution.py
+++ b/solution.py
@@ -36,9 +36,8 @@
         got_a, got_b, ids_a, ids_b = [], [], [], []
         for step in range(chips):
             cur_a, cur_b = ring_a[step], ring_b[step]
-            if step + 1 < chips:
-                cur_a, _ = lax.optimization_barrier((cur_a, ring_a[step + 1]))
-                cur_b, _ = lax.optimization_barrier((cur_b, ring_b[step + 1]))
+            if step == 0 and chips > 1:
+                cur_a, cur_b, _ = lax.optimization_barrier((cur_a, cur_b, (ring_a[1], ring_b[1])))
             src_a = chip_at((pos - step) % chips) * 2 + core
             src_b = chip_at((pos + step) % chips) * 2 + core
             got_a += [ring_a[step], lax.ppermute(cur_a, "seq", swap)]

time: 135 us -> 116 us (0.86)
  waiting for transfers between devices: 63.9 us -> 49.2 us
  local copies, waits for them, and re-layouts: 26.6 us -> 22 us
    ppermute x7, waiting for transfers between devices: 33.7 us -> 6.12 us  [gather_ring(): ring_b.append(lax.ppermute(ring_b[-1], 'seq', backward))]
    ppermute x7, waiting for transfers between devices: 19.1 us -> 32.7 us  [gather_ring(): ring_a.append(lax.ppermute(ring_a[-1], 'seq', forward))]
    ppermute x7, starting transfers between devices: 9.1 us -> 14.5 us  [gather_ring(): ring_a.append(lax.ppermute(ring_a[-1], 'seq', forward))]
    ppermute x7, starting transfers between devices: 6.19 us -> 1.65 us  [gather_ring(): ring_b.append(lax.ppermute(ring_b[-1], 'seq', backward))]
    another operation x37, local copies, waits for them, and re-layouts: 9.54 us -> 6.08 us  [on_device(): jnp.stack([g[0, rows_dev, :2] for g in heard]).astype(jnp.float32)]
    unnamed x56 -> x68, local copies, waits for them, and re-layouts: 10.4 us -> 9.35 us
  transfers between devices with their start and end apart: 31 -> 31, of which waited for: 13 -> 11; matrix products, arithmetic and copies ran while one was open for 25% -> 24% of each run, Pallas kernels for 0% -> 0%
where the time goes in v18:
time: 116 us; the launch traced here: 115 us
  waiting for transfers between devices  49.2 us (42%)
  local copies, waits for them, and re-layouts  22 us (19%)
  starting transfers between devices  20.4 us (18%)
  matrix products  15.4 us (13%)
  other arithmetic  5.57 us (5%)
  between operations  2.64 us (2%)
    ppermute x7, waiting for transfers between devices, gather_ring(): ring_a.append(lax.ppermute(ring_a[-1], 'seq', forward))  32.7 us
    ppermute x7, starting transfers between devices, gather_ring(): ring_a.append(lax.ppermute(ring_a[-1], 'seq', forward))  14.5 us
    ppermute x1, waiting for transfers between devices, on_device(): came = lax.ppermute(other, 'tp', [(0, 1), (1, 0)])  10.3 us
    unnamed x68, local copies, waits for them, and re-layouts  9.35 us
    dot_general x12, matrix products, attend_part(): jnp.einsum('hqd,nhkd->hqnk', queries_3d, keys, preferred_element_type=jnp...  6.13 us
    ppermute x7, waiting for transfers between devices, gather_ring(): ring_b.append(lax.ppermute(ring_b[-1], 'seq', backward))  6.12 us
    another operation x37, local copies, waits for them, and re-layouts, on_device(): jnp.stack([g[0, rows_dev, :2] for g in heard]).astype(jnp.float32)  6.08 us
    dot_general x12, matrix products, attend_part(): jnp.einsum('hqnk,nhkd->hqd', weights.astype(jnp.bfloat16), values, prefer...  4.51 us
  transfers between devices with their start and end apart: 31, of which 11 were waited for; matrix products, arithmetic and copies ran while one was open for 24% of the time, Pallas kernels for 0%

profile of v18, /device:TPU:0, one launch (start us, length us, event | category | flops | bytes accessed | tf_op | source)
XLA Modules:
  0.0 115.1 jit_solution(4472906833598384583)
XLA Ops:
  0.0 1.0 fusion.237
  1.0 1.0 fusion.238
  4.6 3.1 %collective-permute-start = (bf16[10,128,128]{2,1,0:T(8,128)(2,1)S(1)}, bf16[10,128,128]{2,1,0:T(8,128)(2,1)S(1)}, u32[]{:S(2)}, u32[]{:S(2)}) collective-permute-start(bf16[10,128,128]{2,1,0:T(8,128)(2,1)S(1)} %get-tuple-element.38), channel_id=1, source_target_pairs={{0,8},{2,10},{8,16},{10,18},{16,24},{18,26},{24,28},{26,30},{28,20... | collective-permute-start | bytes 983048 | tf_op jit(solution)/shard_map/ppermute | solution.py:34
  9.1 6.2 %collective-permute-done = bf16[10,128,128]{2,1,0:T(8,128)(2,1)S(1)} collective-permute-done((bf16[10,128,128]{2,1,0:T(8,128)(2,1)S(1)}, bf16[10,128,128]{2,1,0:T(8,128)(2,1)S(1)}, u32[]{:S(2)}, u32[]{:S(2)}) %collective-permute-start) | collective-permute-done | bytes 327712 | tf_op jit(solution)/shard_map/ppermute | solution.py:34
  15.3 1.5 %collective-permute-done.1 = bf16[10,128,128]{2,1,0:T(8,128)(2,1)S(1)} collective-permute-done((bf16[10,128,128]{2,1,0:T(8,128)(2,1)S(1)}, bf16[10,128,128]{2,1,0:T(8,128)(2,1)S(1)}, u32[]{:S(2)}, u32[]{:S(2)}) %collective-permute-start.1) | collective-permute-done | bytes 327712 | tf_op jit(solution)/shard_map/ppermute | solution.py:35
  16.9 0.5 collective-permute-start.2
  17.4 1.6 %collective-permute-start.4 = (bf16[10,128,128]{2,1,0:T(8,128)(2,1)S(1)}, bf16[10,128,128]{2,1,0:T(8,128)(2,1)S(1)}, u32[]{:S(2)}, u32[]{:S(2)}) collective-permute-start(bf16[10,128,128]{2,1,0:T(8,128)(2,1)S(1)} %collective-permute-done), channel_id=1, source_target_pairs={{0,8},{2,10},{8,16},{10,18},{16,24},{18,26},{24,28},{26,30},{28,20... | collective-permute-start | bytes 983048 | tf_op jit(solution)/shard_map/ppermute | solution.py:34
  18.9 0.4 collective-permute-start.12
  19.6 7.4 %collective-permute-done.4 = bf16[10,128,128]{2,1,0:T(8,128)(2,1)S(1)} collective-permute-done((bf16[10,128,128]{2,1,0:T(8,128)(2,1)S(1)}, bf16[10,128,128]{2,1,0:T(8,128)(2,1)S(1)}, u32[]{:S(2)}, u32[]{:S(2)}) %collective-permute-start.4) | collective-permute-done | bytes 327712 | tf_op jit(solution)/shard_map/ppermute | solution.py:34
  27.0 1.3 %collective-permute-done.12 = bf16[10,128,128]{2,1,0:T(8,128)(2,1)S(1)} collective-permute-done((bf16[10,128,128]{2,1,0:T(8,128)(2,1)S(1)}, bf16[10,128,128]{2,1,0:T(8,128)(2,1)S(1)}, u32[]{:S(2)}, u32[]{:S(2)}) %collective-permute-start.12) | collective-permute-done | bytes 327712 | tf_op jit(solution)/shard_map/ppermute | solution.py:35
  28.3 1.6 %collective-permute-start.6 = (bf16[10,128,128]{2,1,0:T(8,128)(2,1)S(1)}, bf16[10,128,128]{2,1,0:T(8,128)(2,1)}, u32[]{:S(2)}, u32[]{:S(2)}) collective-permute-start(bf16[10,128,128]{2,1,0:T(8,128)(2,1)S(1)} %collective-permute-done.4), channel_id=1, source_target_pairs={{0,8},{2,10},{8,16},{10,18},{16,24},{18,26},{24,28},{26,30},{28,20... | collective-permute-start | bytes 983048 | tf_op jit(solution)/shard_map/ppermute | solution.py:34
  29.9 0.5 collective-permute-start.14
  30.3 0.7 slice_bitcast_fusion.17
  31.0 0.7 copy-done.7
  32.4 0.5 collective-permute-start.5
  32.9 4.3 %collective-permute-done.6 = bf16[10,128,128]{2,1,0:T(8,128)(2,1)} collective-permute-done((bf16[10,128,128]{2,1,0:T(8,128)(2,1)S(1)}, bf16[10,128,128]{2,1,0:T(8,128)(2,1)}, u32[]{:S(2)}, u32[]{:S(2)}) %collective-permute-start.6) | collective-permute-done | bytes 327712 | tf_op jit(solution)/shard_map/ppermute | solution.py:34
  37.2 1.6 %collective-permute-start.8 = (bf16[10,128,128]{2,1,0:T(8,128)(2,1)}, bf16[10,128,128]{2,1,0:T(8,128)(2,1)}, u32[]{:S(2)}, u32[]{:S(2)}) collective-permute-start(bf16[10,128,128]{2,1,0:T(8,128)(2,1)} %collective-permute-done.6), channel_id=1, source_target_pairs={{0,8},{2,10},{8,16},{10,18},{16,24},{18,26},{24,28},{26,30},{28,20... | collective-permute-start | bytes 983048 | tf_op jit(solution)/shard_map/ppermute | solution.py:34
  38.8 0.7 slice_bitcast_fusion.12
  39.5 0.4 collective-permute-start.16
  40.0 0.7 copy-done.11
  40.7 0.7 copy-done.5
  41.8 0.5 collective-permute-start.7
  42.4 3.1 %collective-permute-done.8 = bf16[10,128,128]{2,1,0:T(8,128)(2,1)} collective-permute-done((bf16[10,128,128]{2,1,0:T(8,128)(2,1)}, bf16[10,128,128]{2,1,0:T(8,128)(2,1)}, u32[]{:S(2)}, u32[]{:S(2)}) %collective-permute-start.8) | collective-permute-done | bytes 327712 | tf_op jit(solution)/shard_map/ppermute | solution.py:34
  45.5 0.7 slice_bitcast_fusion.10
  46.1 1.1 collective-permute-done.16
  47.3 0.7 slice_bitcast_fusion.1
  48.0 0.7 copy-done.13
  48.7 0.7 copy-done.9
  49.8 2.6 %collective-permute-start.18 = (bf16[10,128,128]{2,1,0:T(8,128)(2,1)}, bf16[10,128,128]{2,1,0:T(8,128)(2,1)S(1)}, u32[]{:S(2)}, u32[]{:S(2)}) collective-permute-start(bf16[10,128,128]{2,1,0:T(8,128)(2,1)} %collective-permute-done.8), channel_id=1, source_target_pairs={{0,8},{2,10},{8,16},{10,18},{16,24},{18,26},{24,28},{26,30},{28,20... | collective-permute-start | bytes 983048 | tf_op jit(solution)/shard_map/ppermute | solution.py:34
  52.4 0.7 slice_bitcast_fusion.9
  53.2 0.7 slice_bitcast_fusion
  54.8 5.6 %collective-permute-done.18 = bf16[10,128,128]{2,1,0:T(8,128)(2,1)S(1)} collective-permute-done((bf16[10,128,128]{2,1,0:T(8,128)(2,1)}, bf16[10,128,128]{2,1,0:T(8,128)(2,1)S(1)}, u32[]{:S(2)}, u32[]{:S(2)}) %collective-permute-start.18) | collective-permute-done | bytes 327712 | tf_op jit(solution)/shard_map/ppermute | solution.py:34
  60.4 2.4 %collective-permute-start.20 = (bf16[10,128,128]{2,1,0:T(8,128)(2,1)S(1)}, bf16[10,128,128]{2,1,0:T(8,128)(2,1)S(1)}, u32[]{:S(2)}, u32[]{:S(2)}) collective-permute-start(bf16[10,128,128]{2,1,0:T(8,128)(2,1)S(1)} %collective-permute-done.18), channel_id=1, source_target_pairs={{0,8},{2,10},{8,16},{10,18},{16,24},{18,26},{24,28},{26,30},{28,20... | collective-permute-start | bytes 983048 | tf_op jit(solution)/shard_map/ppermute | solution.py:34
  63.0 0.5 collective-permute-start.23
  63.6 6.2 %collective-permute-done.20 = bf16[10,128,128]{2,1,0:T(8,128)(2,1)S(1)} collective-permute-done((bf16[10,128,128]{2,1,0:T(8,128)(2,1)S(1)}, bf16[10,128,128]{2,1,0:T(8,128)(2,1)S(1)}, u32[]{:S(2)}, u32[]{:S(2)}) %collective-permute-start.20) | collective-permute-done | bytes 327712 | tf_op jit(solution)/shard_map/ppermute | solution.py:34
  69.7 2.2 %collective-permute-done.24 = bf16[10,128,128]{2,1,0:T(8,128)(2,1)S(1)} collective-permute-done((bf16[10,128,128]{2,1,0:T(8,128)(2,1)S(1)}, bf16[10,128,128]{2,1,0:T(8,128)(2,1)S(1)}, u32[]{:S(2)}, u32[]{:S(2)}) %collective-permute-start.24) | collective-permute-done | bytes 327712 | tf_op jit(solution)/shard_map/ppermute | solution.py:35
  72.0 1.7 %collective-permute-start.26 = (bf16[10,128,128]{2,1,0:T(8,128)(2,1)S(1)}, bf16[10,128,128]{2,1,0:T(8,128)(2,1)S(1)}, u32[]{:S(2)}, u32[]{:S(2)}) collective-permute-start(bf16[10,128,128]{2,1,0:T(8,128)(2,1)S(1)} %collective-permute-done.20), channel_id=1, source_target_pairs={{0,8},{2,10},{8,16},{10,18},{16,24},{18,26},{24,28},{26,30},{28,20... | collective-permute-start | bytes 983048 | tf_op jit(solution)/shard_map/ppermute | solution.py:34
  74.1 1.0 bitcast_dynamic-update-slice_fusion.16
  75.4 1.0 bitcast_dynamic-update-slice_fusion.11
  76.5 1.0 bitcast_dynamic-update-slice_fusion.9
  77.5 1.0 bitcast_dynamic-update-slice_fusion.19
  78.5 0.8 fusion.252
  79.3 0.8 fusion.251
  80.3 0.4 fusion.250
  80.8 0.4 fusion.249
  81.8 0.7 copy-done.6
  82.8 1.0 bitcast_dynamic-update-slice_fusion
  83.8 1.0 bitcast_dynamic-update-slice_fusion.18
  84.8 0.8 fusion.246
  85.6 0.4 fusion.244
  86.0 0.7 fusion.16
  86.7 0.4 fusion.243
  87.2 0.8 fusion.245
  88.9 0.5 collective-permute-start.29
  89.4 0.7 fusion.18
  91.9 0.5 fusion.66
  93.5 0.5 fusion.60
  94.8 2.4 %convolution_convert_fusion = bf16[60,5120]{1,0:T(8,128)(2,1)S(1)} fusion(bf16[1280,5120]{1,0:T(8,128)(2,1)S(1)} %bitcast.603, bf16[60,640]{1,0:T(8,128)(2,1)S(1)} %bitcast.614, bf16[60,640]{1,0:T(8,128)(2,1)S(1)} %bitcast.613), kind=kOutput, calls=%fused_computation | convolution fusion | flops 787046400 | bytes 13875200 | tf_op jit(solution)/shard_map/dot_general | solution.py:161
  97.2 1.6 %collective-permute-start.30 = (bf16[60,5120]{1,0:T(8,128)(2,1)S(1)}, bf16[60,5120]{1,0:T(8,128)(2,1)S(1)}, u32[]{:S(2)}, u32[]{:S(2)}) collective-permute-start(bf16[60,5120]{1,0:T(8,128)(2,1)S(1)} %convolution_convert_fusion), channel_id=1, source_target_pairs={{0,1},{1,0},{2,3},{3,2},{4,5},{5,4},{6,7},{7,6},{8,9},{9,8},{10,11... | collective-permute-start | bytes 1843208 | tf_op jit(solution)/shard_map/ppermute | solution.py:163
  98.7 0.7 fusion.69
  100.2 0.5 fusion.63
  101.4 2.4 %fusion.146 = f32[60,5120]{1,0:T(8,128)S(1)} fusion(bf16[1280,5120]{1,0:T(8,128)(2,1)S(1)} %bitcast.603, bf16[60,640]{1,0:T(8,128)(2,1)S(1)} %bitcast.615, bf16[60,640]{1,0:T(8,128)(2,1)S(1)} %bitcast.612), kind=kOutput, calls=%fused_computation.184 | convolution fusion | flops 786739200 | bytes 14489600 | tf_op jit(solution)/shard_map/dot_general | solution.py:165
  103.8 10.3 %collective-permute-done.30 = bf16[60,5120]{1,0:T(8,128)(2,1)S(1)} collective-permute-done((bf16[60,5120]{1,0:T(8,128)(2,1)S(1)}, bf16[60,5120]{1,0:T(8,128)(2,1)S(1)}, u32[]{:S(2)}, u32[]{:S(2)}) %collective-permute-start.30) | collective-permute-done | bytes 614432 | tf_op jit(solution)/shard_map/ppermute | solution.py:163
  114.1 1.1 add_convert_fusion
  (191 shorter events, 12.6 us)
Async XLA Ops:
  2.3 5.3 %copy-start.15 = (bf16[120,1280]{1,0:T(8,128)(2,1)S(1)}, bf16[120,1280]{1,0:T(8,128)(2,1)}, u32[]{:S(2)}) copy-start(bf16[120,1280]{1,0:T(8,128)(2,1)} %param.11) | copy-start | bytes 921604
  4.6 10.7 %collective-permute-start = (bf16[10,128,128]{2,1,0:T(8,128)(2,1)S(1)}, bf16[10,128,128]{2,1,0:T(8,128)(2,1)S(1)}, u32[]{:S(2)}, u32[]{:S(2)}) collective-permute-start(bf16[10,128,128]{2,1,0:T(8,128)(2,1)S(1)} %get-tuple-element.38), channel_id=1, source_target_pairs={{0,8},{2,10},{8,16},{10,18},{16,24},{18,26},{24,28},{26,30},{28,20... | collective-permute-start | bytes 983048 | tf_op jit(solution)/shard_map/ppermute | solution.py:34
  7.7 9.2 %collective-permute-start.1 = (bf16[10,128,128]{2,1,0:T(8,128)(2,1)S(1)}, bf16[10,128,128]{2,1,0:T(8,128)(2,1)S(1)}, u32[]{:S(2)}, u32[]{:S(2)}) collective-permute-start(bf16[10,128,128]{2,1,0:T(8,128)(2,1)S(1)} %get-tuple-element.52), channel_id=1, source_target_pairs={{8,0},{10,2},{16,8},{18,10},{24,16},{26,18},{28,24},{30,26},{20,28... | collective-permute-start | bytes 983048 | tf_op jit(solution)/shard_map/ppermute | solution.py:35
  16.9 14.1 %collective-permute-start.10 = (bf16[10,128,128]{2,1,0:T(8,128)(2,1)S(1)}, bf16[10,128,128]{2,1,0:T(8,128)(2,1)S(1)}, u32[]{:S(2)}, u32[]{:S(2)}) collective-permute-start(bf16[10,128,128]{2,1,0:T(8,128)(2,1)S(1)} %get-tuple-element.52), channel_id=1, source_target_pairs={{0,2},{2,0},{4,6},{6,4},{8,10},{10,8},{12,14},{14,12},{16,18},{18,... | collective-permute-start | bytes 983048 | tf_op jit(solution)/shard_map/ppermute | solution.py:44
  16.9 13.0 %collective-permute-start.2 = (bf16[10,128,128]{2,1,0:T(8,128)(2,1)S(1)}, bf16[10,128,128]{2,1,0:T(8,128)(2,1)}, u32[]{:S(2)}, u32[]{:S(2)}) collective-permute-start(bf16[10,128,128]{2,1,0:T(8,128)(2,1)S(1)} %get-tuple-element.38), channel_id=1, source_target_pairs={{0,2},{2,0},{4,6},{6,4},{8,10},{10,8},{12,14},{14,12},{16,18},{18,... | collective-permute-start | bytes 983048 | tf_op jit(solution)/shard_map/ppermute | solution.py:43
  17.4 9.6 %collective-permute-start.4 = (bf16[10,128,128]{2,1,0:T(8,128)(2,1)S(1)}, bf16[10,128,128]{2,1,0:T(8,128)(2,1)S(1)}, u32[]{:S(2)}, u32[]{:S(2)}) collective-permute-start(bf16[10,128,128]{2,1,0:T(8,128)(2,1)S(1)} %collective-permute-done), channel_id=1, source_target_pairs={{0,8},{2,10},{8,16},{10,18},{16,24},{18,26},{24,28},{26,30},{28,20... | collective-permute-start | bytes 983048 | tf_op jit(solution)/shard_map/ppermute | solution.py:34
  18.9 9.3 %collective-permute-start.12 = (bf16[10,128,128]{2,1,0:T(8,128)(2,1)S(1)}, bf16[10,128,128]{2,1,0:T(8,128)(2,1)S(1)}, u32[]{:S(2)}, u32[]{:S(2)}) collective-permute-start(bf16[10,128,128]{2,1,0:T(8,128)(2,1)S(1)} %collective-permute-done.1), channel_id=1, source_target_pairs={{8,0},{10,2},{16,8},{18,10},{24,16},{26,18},{28,24},{30,26},{20,28... | collective-permute-start | bytes 983048 | tf_op jit(solution)/shard_map/ppermute | solution.py:35
  19.6 11.4 %collective-permute-start.11 = (bf16[10,128,128]{2,1,0:T(8,128)(2,1)S(1)}, bf16[10,128,128]{2,1,0:T(8,128)(2,1)S(1)}, u32[]{:S(2)}, u32[]{:S(2)}) collective-permute-start(bf16[10,128,128]{2,1,0:T(8,128)(2,1)S(1)} %collective-permute-done.1), channel_id=1, source_target_pairs={{0,2},{2,0},{4,6},{6,4},{8,10},{10,8},{12,14},{14,12},{16,18},{18,... | collective-permute-start | bytes 983048 | tf_op jit(solution)/shard_map/ppermute | solution.py:44
  27.0 22.7 %copy-start.3 = (bf16[10,128,128]{2,1,0:T(8,128)(2,1)}, bf16[10,128,128]{2,1,0:T(8,128)(2,1)S(1)}, u32[]{:S(2)}) copy-start(bf16[10,128,128]{2,1,0:T(8,128)(2,1)S(1)} %collective-permute-done.4) | copy-start | bytes 983044
  27.0 4.0 %collective-permute-start.3 = (bf16[10,128,128]{2,1,0:T(8,128)(2,1)S(1)}, bf16[10,128,128]{2,1,0:T(8,128)(2,1)S(1)}, u32[]{:S(2)}, u32[]{:S(2)}) collective-permute-start(bf16[10,128,128]{2,1,0:T(8,128)(2,1)S(1)} %collective-permute-done), channel_id=1, source_target_pairs={{0,2},{2,0},{4,6},{6,4},{8,10},{10,8},{12,14},{14,12},{16,18},{18,... | collective-permute-start | bytes 983048 | tf_op jit(solution)/shard_map/ppermute | solution.py:43
  28.3 8.9 %collective-permute-start.6 = (bf16[10,128,128]{2,1,0:T(8,128)(2,1)S(1)}, bf16[10,128,128]{2,1,0:T(8,128)(2,1)}, u32[]{:S(2)}, u32[]{:S(2)}) collective-permute-start(bf16[10,128,128]{2,1,0:T(8,128)(2,1)S(1)} %collective-permute-done.4), channel_id=1, source_target_pairs={{0,8},{2,10},{8,16},{10,18},{16,24},{18,26},{24,28},{26,30},{28,20... | collective-permute-start | bytes 983048 | tf_op jit(solution)/shard_map/ppermute | solution.py:34
  29.9 9.6 %collective-permute-start.14 = (bf16[10,128,128]{2,1,0:T(8,128)(2,1)S(1)}, bf16[10,128,128]{2,1,0:T(8,128)(2,1)S(1)}, u32[]{:S(2)}, u32[]{:S(2)}) collective-permute-start(bf16[10,128,128]{2,1,0:T(8,128)(2,1)S(1)} %collective-permute-done.12), channel_id=1, source_target_pairs={{8,0},{10,2},{16,8},{18,10},{24,16},{26,18},{28,24},{30,26},{20,28... | collective-permute-start | bytes 983048 | tf_op jit(solution)/shard_map/ppermute | solution.py:35
  31.0 0.8 copy-start.7
  32.4 7.6 %collective-permute-start.13 = (bf16[10,128,128]{2,1,0:T(8,128)(2,1)S(1)}, bf16[10,128,128]{2,1,0:T(8,128)(2,1)S(1)}, u32[]{:S(2)}, u32[]{:S(2)}) collective-permute-start(bf16[10,128,128]{2,1,0:T(8,128)(2,1)S(1)} %collective-permute-done.12), channel_id=1, source_target_pairs={{0,2},{2,0},{4,6},{6,4},{8,10},{10,8},{12,14},{14,12},{16,18},{18,... | collective-permute-start | bytes 983048 | tf_op jit(solution)/shard_map/ppermute | solution.py:44
  32.4 7.6 %collective-permute-start.5 = (bf16[10,128,128]{2,1,0:T(8,128)(2,1)S(1)}, bf16[10,128,128]{2,1,0:T(8,128)(2,1)S(1)}, u32[]{:S(2)}, u32[]{:S(2)}) collective-permute-start(bf16[10,128,128]{2,1,0:T(8,128)(2,1)S(1)} %collective-permute-done.4), channel_id=1, source_target_pairs={{0,2},{2,0},{4,6},{6,4},{8,10},{10,8},{12,14},{14,12},{16,18},{18,... | collective-permute-start | bytes 983048 | tf_op jit(solution)/shard_map/ppermute | solution.py:43
  37.2 8.2 %collective-permute-start.8 = (bf16[10,128,128]{2,1,0:T(8,128)(2,1)}, bf16[10,128,128]{2,1,0:T(8,128)(2,1)}, u32[]{:S(2)}, u32[]{:S(2)}) collective-permute-start(bf16[10,128,128]{2,1,0:T(8,128)(2,1)} %collective-permute-done.6), channel_id=1, source_target_pairs={{0,8},{2,10},{8,16},{10,18},{16,24},{18,26},{24,28},{26,30},{28,20... | collective-permute-start | bytes 983048 | tf_op jit(solution)/shard_map/ppermute | solution.py:34
  39.5 10.3 %copy-start.1 = (bf16[10,128,128]{2,1,0:T(8,128)(2,1)}, bf16[10,128,128]{2,1,0:T(8,128)(2,1)S(1)}, u32[]{:S(2)}) copy-start(bf16[10,128,128]{2,1,0:T(8,128)(2,1)S(1)} %collective-permute-done.14) | copy-start | bytes 983044
  39.5 7.8 %collective-permute-start.16 = (bf16[10,128,128]{2,1,0:T(8,128)(2,1)S(1)}, bf16[10,128,128]{2,1,0:T(8,128)(2,1)}, u32[]{:S(2)}, u32[]{:S(2)}) collective-permute-start(bf16[10,128,128]{2,1,0:T(8,128)(2,1)S(1)} %collective-permute-done.14), channel_id=1, source_target_pairs={{8,0},{10,2},{16,8},{18,10},{24,16},{26,18},{28,24},{30,26},{20,28... | collective-permute-start | bytes 983048 | tf_op jit(solution)/shard_map/ppermute | solution.py:35
  40.0 0.7 copy-start.11
  40.7 0.7 copy-start.5
  41.8 6.1 %collective-permute-start.15 = (bf16[10,128,128]{2,1,0:T(8,128)(2,1)S(1)}, bf16[10,128,128]{2,1,0:T(8,128)(2,1)S(1)}, u32[]{:S(2)}, u32[]{:S(2)}) collective-permute-start(bf16[10,128,128]{2,1,0:T(8,128)(2,1)S(1)} %collective-permute-done.14), channel_id=1, source_target_pairs={{0,2},{2,0},{4,6},{6,4},{8,10},{10,8},{12,14},{14,12},{16,18},{18,... | collective-permute-start | bytes 983048 | tf_op jit(solution)/shard_map/ppermute | solution.py:44
  41.8 6.1 %collective-permute-start.7 = (bf16[10,128,128]{2,1,0:T(8,128)(2,1)}, bf16[10,128,128]{2,1,0:T(8,128)(2,1)S(1)}, u32[]{:S(2)}, u32[]{:S(2)}) collective-permute-start(bf16[10,128,128]{2,1,0:T(8,128)(2,1)} %collective-permute-done.6), channel_id=1, source_target_pairs={{0,2},{2,0},{4,6},{6,4},{8,10},{10,8},{12,14},{14,12},{16,18},{18,... | collective-permute-start | bytes 983048 | tf_op jit(solution)/shard_map/ppermute | solution.py:43
  45.5 7.0 %collective-permute-start.9 = (bf16[10,128,128]{2,1,0:T(8,128)(2,1)}, bf16[10,128,128]{2,1,0:T(8,128)(2,1)}, u32[]{:S(2)}, u32[]{:S(2)}) collective-permute-start(bf16[10,128,128]{2,1,0:T(8,128)(2,1)} %collective-permute-done.8), channel_id=1, source_target_pairs={{0,2},{2,0},{4,6},{6,4},{8,10},{10,8},{12,14},{14,12},{16,18},{18,... | collective-permute-start | bytes 983048 | tf_op jit(solution)/shard_map/ppermute | solution.py:43
  47.3 5.9 %collective-permute-start.17 = (bf16[10,128,128]{2,1,0:T(8,128)(2,1)}, bf16[10,128,128]{2,1,0:T(8,128)(2,1)}, u32[]{:S(2)}, u32[]{:S(2)}) collective-permute-start(bf16[10,128,128]{2,1,0:T(8,128)(2,1)} %collective-permute-done.16), channel_id=1, source_target_pairs={{0,2},{2,0},{4,6},{6,4},{8,10},{10,8},{12,14},{14,12},{16,18},{18,... | collective-permute-start | bytes 983048 | tf_op jit(solution)/shard_map/ppermute | solution.py:44
  47.9 0.7 copy-start.13
  48.7 0.7 copy-start.9
  49.8 10.5 %collective-permute-start.18 = (bf16[10,128,128]{2,1,0:T(8,128)(2,1)}, bf16[10,128,128]{2,1,0:T(8,128)(2,1)S(1)}, u32[]{:S(2)}, u32[]{:S(2)}) collective-permute-start(bf16[10,128,128]{2,1,0:T(8,128)(2,1)} %collective-permute-done.8), channel_id=1, source_target_pairs={{0,8},{2,10},{8,16},{10,18},{16,24},{18,26},{24,28},{26,30},{28,20... | collective-permute-start | bytes 983048 | tf_op jit(solution)/shard_map/ppermute | solution.py:34
  52.4 10.4 %collective-permute-start.22 = (bf16[10,128,128]{2,1,0:T(8,128)(2,1)}, bf16[10,128,128]{2,1,0:T(8,128)(2,1)S(1)}, u32[]{:S(2)}, u32[]{:S(2)}) collective-permute-start(bf16[10,128,128]{2,1,0:T(8,128)(2,1)} %collective-permute-done.16), channel_id=1, source_target_pairs={{8,0},{10,2},{16,8},{18,10},{24,16},{26,18},{28,24},{30,26},{20,28... | collective-permute-start | bytes 983048 | tf_op jit(solution)/shard_map/ppermute | solution.py:35
  54.1 21.1 %copy-start.8 = (bf16[10,128,128]{2,1,0:T(8,128)(2,1)S(1)}, bf16[10,128,128]{2,1,0:T(8,128)(2,1)}, u32[]{:S(2)}) copy-start(bf16[10,128,128]{2,1,0:T(8,128)(2,1)} %copy-done.7) | copy-start | bytes 983044
  54.1 21.2 %copy-start.4 = (bf16[10,128,128]{2,1,0:T(8,128)(2,1)S(1)}, bf16[10,128,128]{2,1,0:T(8,128)(2,1)}, u32[]{:S(2)}) copy-start(bf16[10,128,128]{2,1,0:T(8,128)(2,1)} %copy-done.3) | copy-start | bytes 983044
  60.4 9.3 %collective-permute-start.20 = (bf16[10,128,128]{2,1,0:T(8,128)(2,1)S(1)}, bf16[10,128,128]{2,1,0:T(8,128)(2,1)S(1)}, u32[]{:S(2)}, u32[]{:S(2)}) collective-permute-start(bf16[10,128,128]{2,1,0:T(8,128)(2,1)S(1)} %collective-permute-done.18), channel_id=1, source_target_pairs={{0,8},{2,10},{8,16},{10,18},{16,24},{18,26},{24,28},{26,30},{28,20... | collective-permute-start | bytes 983048 | tf_op jit(solution)/shard_map/ppermute | solution.py:34
  62.8 9.1 %collective-permute-start.24 = (bf16[10,128,128]{2,1,0:T(8,128)(2,1)S(1)}, bf16[10,128,128]{2,1,0:T(8,128)(2,1)S(1)}, u32[]{:S(2)}, u32[]{:S(2)}) collective-permute-start(bf16[10,128,128]{2,1,0:T(8,128)(2,1)S(1)} %collective-permute-done.22), channel_id=1, source_target_pairs={{8,0},{10,2},{16,8},{18,10},{24,16},{26,18},{28,24},{30,26},{20,28... | collective-permute-start | bytes 983048 | tf_op jit(solution)/shard_map/ppermute | solution.py:35
  63.0 10.8 %collective-permute-start.19 = (bf16[10,128,128]{2,1,0:T(8,128)(2,1)S(1)}, bf16[10,128,128]{2,1,0:T(8,128)(2,1)S(1)}, u32[]{:S(2)}, u32[]{:S(2)}) collective-permute-start(bf16[10,128,128]{2,1,0:T(8,128)(2,1)S(1)} %collective-permute-done.18), channel_id=1, source_target_pairs={{0,2},{2,0},{4,6},{6,4},{8,10},{10,8},{12,14},{14,12},{16,18},{18,... | collective-permute-start | bytes 983048 | tf_op jit(solution)/shard_map/ppermute | solution.py:43
  63.0 11.1 %collective-permute-start.23 = (bf16[10,128,128]{2,1,0:T(8,128)(2,1)S(1)}, bf16[10,128,128]{2,1,0:T(8,128)(2,1)S(1)}, u32[]{:S(2)}, u32[]{:S(2)}) collective-permute-start(bf16[10,128,128]{2,1,0:T(8,128)(2,1)S(1)} %collective-permute-done.22), channel_id=1, source_target_pairs={{0,2},{2,0},{4,6},{6,4},{8,10},{10,8},{12,14},{14,12},{16,18},{18,... | collective-permute-start | bytes 983048 | tf_op jit(solution)/shard_map/ppermute | solution.py:44
  69.7 4.4 %collective-permute-start.21 = (bf16[10,128,128]{2,1,0:T(8,128)(2,1)S(1)}, bf16[10,128,128]{2,1,0:T(8,128)(2,1)S(1)}, u32[]{:S(2)}, u32[]{:S(2)}) collective-permute-start(bf16[10,128,128]{2,1,0:T(8,128)(2,1)S(1)} %collective-permute-done.20), channel_id=1, source_target_pairs={{0,2},{2,0},{4,6},{6,4},{8,10},{10,8},{12,14},{14,12},{16,18},{18,... | collective-permute-start | bytes 983048 | tf_op jit(solution)/shard_map/ppermute | solution.py:43
  71.9 2.2 %collective-permute-start.25 = (bf16[10,128,128]{2,1,0:T(8,128)(2,1)S(1)}, bf16[10,128,128]{2,1,0:T(8,128)(2,1)S(1)}, u32[]{:S(2)}, u32[]{:S(2)}) collective-permute-start(bf16[10,128,128]{2,1,0:T(8,128)(2,1)S(1)} %collective-permute-done.24), channel_id=1, source_target_pairs={{0,2},{2,0},{4,6},{6,4},{8,10},{10,8},{12,14},{14,12},{16,18},{18,... | collective-permute-start | bytes 983048 | tf_op jit(solution)/shard_map/ppermute | solution.py:44
  72.0 3.3 %copy-start.12 = (bf16[10,128,128]{2,1,0:T(8,128)(2,1)S(1)}, bf16[10,128,128]{2,1,0:T(8,128)(2,1)}, u32[]{:S(2)}) copy-start(bf16[10,128,128]{2,1,0:T(8,128)(2,1)} %copy-done.11) | copy-start | bytes 983044
  72.0 15.9 %collective-permute-start.26 = (bf16[10,128,128]{2,1,0:T(8,128)(2,1)S(1)}, bf16[10,128,128]{2,1,0:T(8,128)(2,1)S(1)}, u32[]{:S(2)}, u32[]{:S(2)}) collective-permute-start(bf16[10,128,128]{2,1,0:T(8,128)(2,1)S(1)} %collective-permute-done.20), channel_id=1, source_target_pairs={{0,8},{2,10},{8,16},{10,18},{16,24},{18,26},{24,28},{26,30},{28,20... | collective-permute-start | bytes 983048 | tf_op jit(solution)/shard_map/ppermute | solution.py:34
  73.8 15.1 %collective-permute-start.28 = (bf16[10,128,128]{2,1,0:T(8,128)(2,1)S(1)}, bf16[10,128,128]{2,1,0:T(8,128)(2,1)S(1)}, u32[]{:S(2)}, u32[]{:S(2)}) collective-permute-start(bf16[10,128,128]{2,1,0:T(8,128)(2,1)S(1)} %collective-permute-done.24), channel_id=1, source_target_pairs={{8,0},{10,2},{16,8},{18,10},{24,16},{26,18},{28,24},{30,26},{20,28... | collective-permute-start | bytes 983048 | tf_op jit(solution)/shard_map/ppermute | solution.py:35
  75.1 1.3 %copy-start.14 = (bf16[10,128,128]{2,1,0:T(8,128)(2,1)S(1)}, bf16[10,128,128]{2,1,0:T(8,128)(2,1)}, u32[]{:S(2)}) copy-start(bf16[10,128,128]{2,1,0:T(8,128)(2,1)} %copy-done.13) | copy-start | bytes 983044
  81.5 1.0 copy-start.6
  81.6 1.1 copy-start.2
  81.6 1.1 copy-start.10
  88.0 2.2 %collective-permute-start.27 = (bf16[10,128,128]{2,1,0:T(8,128)(2,1)S(1)}, bf16[10,128,128]{2,1,0:T(8,128)(2,1)S(1)}, u32[]{:S(2)}, u32[]{:S(2)}) collective-permute-start(bf16[10,128,128]{2,1,0:T(8,128)(2,1)S(1)} %collective-permute-done.26), channel_id=1, source_target_pairs={{0,2},{2,0},{4,6},{6,4},{8,10},{10,8},{12,14},{14,12},{16,18},{18,... | collective-permute-start | bytes 983048 | tf_op jit(solution)/shard_map/ppermute | solution.py:43
  88.0 6.7 %slice-start = ((s8[13107200]{0:T(1024)(128)(4,1)}), s8[4194304]{0:T(1024)(128)(4,1)S(1)}, s32[]{:S(2)}) async-start(s8[13107200]{0:T(1024)(128)(4,1)} %bitcast.602), calls=%async_computation | async-start | bytes 8388608
  88.9 2.0 %collective-permute-start.29 = (bf16[10,128,128]{2,1,0:T(8,128)(2,1)S(1)}, bf16[10,128,128]{2,1,0:T(8,128)(2,1)S(1)}, u32[]{:S(2)}, u32[]{:S(2)}) collective-permute-start(bf16[10,128,128]{2,1,0:T(8,128)(2,1)S(1)} %collective-permute-done.28), channel_id=1, source_target_pairs={{0,2},{2,0},{4,6},{6,4},{8,10},{10,8},{12,14},{14,12},{16,18},{18,... | collective-permute-start | bytes 983048 | tf_op jit(solution)/shard_map/ppermute | solution.py:44
  90.1 4.6 %slice-start.1 = ((s8[13107200]{0:T(1024)(128)(4,1)}), s8[4194304]{0:T(1024)(128)(4,1)S(1)}, s32[]{:S(2)}) async-start(s8[13107200]{0:T(1024)(128)(4,1)} %bitcast.602), calls=%async_computation.1 | async-start | bytes 8388608
  91.9 2.8 %slice-start.2 = ((s8[13107200]{0:T(1024)(128)(4,1)}), s8[4194304]{0:T(1024)(128)(4,1)S(1)}, s32[]{:S(2)}) async-start(s8[13107200]{0:T(1024)(128)(4,1)} %bitcast.602), calls=%async_computation.2 | async-start | bytes 8388608
  93.5 1.3 %slice-start.3 = ((s8[13107200]{0:T(1024)(128)(4,1)}), s8[524288]{0:T(1024)(128)(4,1)S(1)}, s32[]{:S(2)}) async-start(s8[13107200]{0:T(1024)(128)(4,1)} %bitcast.602), calls=%async_computation.3 | async-start | bytes 1048576
  97.2 16.9 %collective-permute-start.30 = (bf16[60,5120]{1,0:T(8,128)(2,1)S(1)}, bf16[60,5120]{1,0:T(8,128)(2,1)S(1)}, u32[]{:S(2)}, u32[]{:S(2)}) collective-permute-start(bf16[60,5120]{1,0:T(8,128)(2,1)S(1)} %convolution_convert_fusion), channel_id=1, source_target_pairs={{0,1},{1,0},{2,3},{3,2},{4,5},{5,4},{6,7},{7,6},{8,9},{9,8},{10,11... | collective-permute-start | bytes 1843208 | tf_op jit(solution)/shard_map/ppermute | solution.py:163
  101.4 12.7 %copy-start = (bf16[60,5120]{1,0:T(8,128)(2,1)S(1)}, bf16[60,5120]{1,0:T(8,128)(2,1)}, u32[]{:S(2)}) copy-start(bf16[60,5120]{1,0:T(8,128)(2,1)} %param.10) | copy-start | bytes 1843204
  101.4 12.7 %copy-start.16 = (f32[5120]{0:T(1024)S(1)}, f32[5120]{0:T(1024)}, u32[]{:S(2)}) copy-start(f32[5120]{0:T(1024)} %param.14) | copy-start | bytes 61444

commit v19 on v15

--- a/solution.py
+++ b/solution.py
@@ -123,7 +123,7 @@
         limit_a = limits_for(ids_a)
         limit_b = limits_for(ids_b)
         within = jnp.arange(rows_pad, dtype=jnp.int32)
-        phases = [(0, known + 1), (known + 1, chips - 1), (chips - 1, chips)]
+        phases = [(0, known + 1), (known + 1, chips)]
         phases = [(2 * lo, 2 * hi) for lo, hi in phases if hi > lo]
 
         anchor = 2 * max(chips - 2, 0)

time: 111 us -> 114 us (1.027)
  local copies, waits for them, and re-layouts: 22.1 us -> 25 us
  waiting for transfers between devices: 44.9 us -> 47.8 us
  matrix products: 15.4 us -> 13.9 us
    ppermute x7, waiting for transfers between devices: 28.2 us -> 32.9 us  [gather_ring(): cur_a = lax.ppermute(cur_a, 'seq', forward)]
    ppermute x7, waiting for transfers between devices: 6.34 us -> 2.07 us  [gather_ring(): cur_b = lax.ppermute(cur_b, 'seq', backward)]
    unnamed x68 -> x70, local copies, waits for them, and re-layouts: 9.42 us -> 12.2 us
    ppermute x1, waiting for transfers between devices: 10.3 us -> 12.8 us  [on_device(): came = lax.ppermute(other, 'tp', [(0, 1), (1, 0)])]
    dot_general x12 -> x8, matrix products: 4.5 us -> 3.58 us  [attend_part(): jnp.einsum('hqnk,nhkd->hqd', weights.astype(jnp.bfloat16), values, prefer...]
    dot_general x12 -> x8, matrix products: 6.13 us -> 5.29 us  [attend_part(): jnp.einsum('hqd,nhkd->hqnk', queries_3d, keys, preferred_element_type=jnp...]
    reduce_sum x6 -> x4, other arithmetic: 2.83 us -> 2.46 us  [attend_part(): totals = jnp.sum(weights, axis=(2, 3))[:, :, None]]
  transfers between devices with their start and end apart: 31 -> 31, of which waited for: 12 -> 12; matrix products, arithmetic and copies ran while one was open for 25% -> 22% of each run, Pallas kernels for 0% -> 0%
where the time goes in v19:
time: 114 us
  waiting for transfers between devices  47.8 us (42%)
  local copies, waits for them, and re-layouts  25 us (22%)
  starting transfers between devices  19.9 us (17%)
  matrix products  13.9 us (12%)
  other arithmetic  4.56 us (4%)
  between operations  2.6 us (2%)
    ppermute x7, waiting for transfers between devices, gather_ring(): cur_a = lax.ppermute(cur_a, 'seq', forward)  32.9 us
    ppermute x1, waiting for transfers between devices, on_device(): came = lax.ppermute(other, 'tp', [(0, 1), (1, 0)])  12.8 us
    unnamed x70, local copies, waits for them, and re-layouts  12.2 us
    ppermute x7, starting transfers between devices, gather_ring(): cur_a = lax.ppermute(cur_a, 'seq', forward)  12.1 us
    another operation x37, local copies, waits for them, and re-layouts, on_device(): jnp.stack([g[0, rows_dev, :2] for g in heard]).astype(jnp.float32)  6.14 us
    dot_general x8, matrix products, attend_part(): jnp.einsum('hqd,nhkd->hqnk', queries_3d, keys, preferred_element_type=jnp...  5.29 us
    dot_general x8, matrix products, attend_part(): jnp.einsum('hqnk,nhkd->hqd', weights.astype(jnp.bfloat16), values, prefer...  3.58 us
    ppermute x7, starting transfers between devices, gather_ring(): cur_b = lax.ppermute(cur_b, 'seq', backward)  2.8 us
  transfers between devices with their start and end apart: 31, of which 12 were waited for; matrix products, arithmetic and copies ran while one was open for 22% of the time, Pallas kernels for 0%

profile of v19, /device:TPU:0, one launch (start us, length us, event | category | flops | bytes accessed | tf_op | source)
XLA Modules:
  0.0 113.7 jit_solution(2378079272783551001)
XLA Ops:
  1.5 1.0 fusion.168
  2.5 1.0 fusion.167
  4.6 0.5 collective-permute-start
  5.1 2.6 %collective-permute-start.1 = (bf16[10,128,128]{2,1,0:T(8,128)(2,1)S(1)}, bf16[10,128,128]{2,1,0:T(8,128)(2,1)S(1)}, u32[]{:S(2)}, u32[]{:S(2)}) collective-permute-start(bf16[10,128,128]{2,1,0:T(8,128)(2,1)S(1)} %get-tuple-element.34), channel_id=1, source_target_pairs={{0,8},{2,10},{8,16},{10,18},{16,24},{18,26},{24,28},{26,30},{28,20... | collective-permute-start | bytes 983048 | tf_op jit(solution)/shard_map/ppermute | solution.py:36
  9.6 6.4 %collective-permute-done.1 = bf16[10,128,128]{2,1,0:T(8,128)(2,1)S(1)} collective-permute-done((bf16[10,128,128]{2,1,0:T(8,128)(2,1)S(1)}, bf16[10,128,128]{2,1,0:T(8,128)(2,1)S(1)}, u32[]{:S(2)}, u32[]{:S(2)}) %collective-permute-start.1) | collective-permute-done | bytes 327712 | tf_op jit(solution)/shard_map/ppermute | solution.py:36
  16.0 1.8 %collective-permute-start.3 = (bf16[10,128,128]{2,1,0:T(8,128)(2,1)S(1)}, bf16[10,128,128]{2,1,0:T(8,128)(2,1)S(1)}, u32[]{:S(2)}, u32[]{:S(2)}) collective-permute-start(bf16[10,128,128]{2,1,0:T(8,128)(2,1)S(1)} %collective-permute-done.1), channel_id=1, source_target_pairs={{0,8},{2,10},{8,16},{10,18},{16,24},{18,26},{24,28},{26,30},{28,20... | collective-permute-start | bytes 983048 | tf_op jit(solution)/shard_map/ppermute | solution.py:36
  18.6 0.5 collective-permute-start.11
  19.1 6.4 %collective-permute-done.3 = bf16[10,128,128]{2,1,0:T(8,128)(2,1)S(1)} collective-permute-done((bf16[10,128,128]{2,1,0:T(8,128)(2,1)S(1)}, bf16[10,128,128]{2,1,0:T(8,128)(2,1)S(1)}, u32[]{:S(2)}, u32[]{:S(2)}) %collective-permute-start.3) | collective-permute-done | bytes 327712 | tf_op jit(solution)/shard_map/ppermute | solution.py:36
  25.5 1.6 %collective-permute-start.5 = (bf16[10,128,128]{2,1,0:T(8,128)(2,1)S(1)}, bf16[10,128,128]{2,1,0:T(8,128)(2,1)S(1)}, u32[]{:S(2)}, u32[]{:S(2)}) collective-permute-start(bf16[10,128,128]{2,1,0:T(8,128)(2,1)S(1)} %collective-permute-done.3), channel_id=1, source_target_pairs={{0,8},{2,10},{8,16},{10,18},{16,24},{18,26},{24,28},{26,30},{28,20... | collective-permute-start | bytes 983048 | tf_op jit(solution)/shard_map/ppermute | solution.py:36
  27.5 0.7 slice_bitcast_fusion.5
  28.3 0.7 copy-done.3
  29.4 0.5 collective-permute-start.13
  29.9 4.3 %collective-permute-done.5 = bf16[10,128,128]{2,1,0:T(8,128)(2,1)S(1)} collective-permute-done((bf16[10,128,128]{2,1,0:T(8,128)(2,1)S(1)}, bf16[10,128,128]{2,1,0:T(8,128)(2,1)S(1)}, u32[]{:S(2)}, u32[]{:S(2)}) %collective-permute-start.5) | collective-permute-done | bytes 327712 | tf_op jit(solution)/shard_map/ppermute | solution.py:36
  34.2 1.4 %collective-permute-start.7 = (bf16[10,128,128]{2,1,0:T(8,128)(2,1)S(1)}, bf16[10,128,128]{2,1,0:T(8,128)(2,1)}, u32[]{:S(2)}, u32[]{:S(2)}) collective-permute-start(bf16[10,128,128]{2,1,0:T(8,128)(2,1)S(1)} %collective-permute-done.5), channel_id=1, source_target_pairs={{0,8},{2,10},{8,16},{10,18},{16,24},{18,26},{24,28},{26,30},{28,20... | collective-permute-start | bytes 983048 | tf_op jit(solution)/shard_map/ppermute | solution.py:36
  35.7 0.6 collective-permute-start.16
  36.3 0.7 slice_bitcast_fusion.3
  37.0 0.7 copy-done.1
  37.8 0.7 copy-done.7
  38.9 0.5 collective-permute-start.15
  39.4 2.8 %collective-permute-done.7 = bf16[10,128,128]{2,1,0:T(8,128)(2,1)} collective-permute-done((bf16[10,128,128]{2,1,0:T(8,128)(2,1)S(1)}, bf16[10,128,128]{2,1,0:T(8,128)(2,1)}, u32[]{:S(2)}, u32[]{:S(2)}) %collective-permute-start.7) | collective-permute-done | bytes 327712 | tf_op jit(solution)/shard_map/ppermute | solution.py:36
  42.2 0.7 slice_bitcast_fusion.10
  43.4 0.7 slice_bitcast_fusion.1
  44.1 0.7 copy-done.5
  44.8 0.7 copy-done.9
  46.0 1.5 %collective-permute-start.18 = (bf16[10,128,128]{2,1,0:T(8,128)(2,1)}, bf16[10,128,128]{2,1,0:T(8,128)(2,1)}, u32[]{:S(2)}, u32[]{:S(2)}) collective-permute-start(bf16[10,128,128]{2,1,0:T(8,128)(2,1)} %collective-permute-done.7), channel_id=1, source_target_pairs={{0,8},{2,10},{8,16},{10,18},{16,24},{18,26},{24,28},{26,30},{28,20... | collective-permute-start | bytes 983048 | tf_op jit(solution)/shard_map/ppermute | solution.py:36
  48.0 0.7 slice_bitcast_fusion.9
  48.8 0.7 slice_bitcast_fusion
  50.2 6.2 %collective-permute-done.18 = bf16[10,128,128]{2,1,0:T(8,128)(2,1)} collective-permute-done((bf16[10,128,128]{2,1,0:T(8,128)(2,1)}, bf16[10,128,128]{2,1,0:T(8,128)(2,1)}, u32[]{:S(2)}, u32[]{:S(2)}) %collective-permute-start.18) | collective-permute-done | bytes 327712 | tf_op jit(solution)/shard_map/ppermute | solution.py:36
  56.4 1.6 %collective-permute-start.20 = (bf16[10,128,128]{2,1,0:T(8,128)(2,1)}, bf16[10,128,128]{2,1,0:T(8,128)(2,1)S(1)}, u32[]{:S(2)}, u32[]{:S(2)}) collective-permute-start(bf16[10,128,128]{2,1,0:T(8,128)(2,1)} %collective-permute-done.18), channel_id=1, source_target_pairs={{0,8},{2,10},{8,16},{10,18},{16,24},{18,26},{24,28},{26,30},{28,20... | collective-permute-start | bytes 983048 | tf_op jit(solution)/shard_map/ppermute | solution.py:36
  59.1 6.7 %collective-permute-done.20 = bf16[10,128,128]{2,1,0:T(8,128)(2,1)S(1)} collective-permute-done((bf16[10,128,128]{2,1,0:T(8,128)(2,1)}, bf16[10,128,128]{2,1,0:T(8,128)(2,1)S(1)}, u32[]{:S(2)}, u32[]{:S(2)}) %collective-permute-start.20) | collective-permute-done | bytes 327712 | tf_op jit(solution)/shard_map/ppermute | solution.py:36
  65.9 1.3 %collective-permute-done.24 = bf16[10,128,128]{2,1,0:T(8,128)(2,1)S(1)} collective-permute-done((bf16[10,128,128]{2,1,0:T(8,128)(2,1)}, bf16[10,128,128]{2,1,0:T(8,128)(2,1)S(1)}, u32[]{:S(2)}, u32[]{:S(2)}) %collective-permute-start.24) | collective-permute-done | bytes 327712 | tf_op jit(solution)/shard_map/ppermute | solution.py:37
  67.8 1.6 %collective-permute-start.26 = (bf16[10,128,128]{2,1,0:T(8,128)(2,1)S(1)}, bf16[10,128,128]{2,1,0:T(8,128)(2,1)S(1)}, u32[]{:S(2)}, u32[]{:S(2)}) collective-permute-start(bf16[10,128,128]{2,1,0:T(8,128)(2,1)S(1)} %collective-permute-done.20), channel_id=1, source_target_pairs={{0,8},{2,10},{8,16},{10,18},{16,24},{18,26},{24,28},{26,30},{28,20... | collective-permute-start | bytes 983048 | tf_op jit(solution)/shard_map/ppermute | solution.py:36
  69.5 1.0 bitcast_dynamic-update-slice_fusion.23
  70.6 1.0 bitcast_dynamic-update-slice_fusion.4
  71.7 1.0 bitcast_dynamic-update-slice_fusion.2
  72.8 1.0 bitcast_dynamic-update-slice_fusion
  73.8 1.0 bitcast_dynamic-update-slice_fusion.24
  74.9 0.8 fusion.171
  75.6 0.8 fusion.174
  76.4 1.0 bitcast_dynamic-update-slice_fusion.30
  77.8 0.6 copy-done.2
  78.7 1.0 bitcast_dynamic-update-slice_fusion.9
  79.7 1.0 bitcast_dynamic-update-slice_fusion.31
  80.8 0.7 fusion.22
  81.6 0.8 fusion.175
  82.5 0.8 fusion.178
  83.3 0.6 collective-permute-start.27
  83.9 0.7 fusion.20
  84.8 0.5 fusion.172
  85.4 0.6 fusion.173
  86.1 0.5 fusion.176
  86.7 0.5 fusion.177
  87.2 0.5 fusion.94
  87.8 0.5 fusion.51
  88.8 0.5 fusion.92
  89.4 0.5 fusion.57
  90.5 0.5 fusion.48
  91.5 0.5 fusion.54
  92.6 0.5 slice-done.2
  93.3 2.6 %convolution_convert_fusion = bf16[60,5120]{1,0:T(8,128)(2,1)S(1)} fusion(bf16[1280,5120]{1,0:T(8,128)(2,1)S(1)} %bitcast.403, bf16[60,640]{1,0:T(8,128)(2,1)S(1)} %bitcast.414, bf16[60,640]{1,0:T(8,128)(2,1)S(1)} %bitcast.415), kind=kOutput, calls=%fused_computation | convolution fusion | flops 787046400 | bytes 13875200 | tf_op jit(solution)/shard_map/dot_general | solution.py:160
  95.9 1.6 %collective-permute-start.30 = (bf16[60,5120]{1,0:T(8,128)(2,1)S(1)}, bf16[60,5120]{1,0:T(8,128)(2,1)S(1)}, u32[]{:S(2)}, u32[]{:S(2)}) collective-permute-start(bf16[60,5120]{1,0:T(8,128)(2,1)S(1)} %convolution_convert_fusion), channel_id=1, source_target_pairs={{0,1},{1,0},{2,3},{3,2},{4,5},{5,4},{6,7},{7,6},{8,9},{9,8},{10,11... | collective-permute-start | bytes 1843208 | tf_op jit(solution)/shard_map/ppermute | solution.py:162
  97.4 2.4 %fusion.112 = f32[60,5120]{1,0:T(8,128)S(1)} fusion(bf16[1280,5120]{1,0:T(8,128)(2,1)S(1)} %bitcast.403, bf16[60,640]{1,0:T(8,128)(2,1)S(1)} %bitcast.412, bf16[60,640]{1,0:T(8,128)(2,1)S(1)} %bitcast.413), kind=kOutput, calls=%fused_computation.146 | convolution fusion | flops 786739200 | bytes 14489600 | tf_op jit(solution)/shard_map/dot_general | solution.py:164
  99.8 12.8 %collective-permute-done.30 = bf16[60,5120]{1,0:T(8,128)(2,1)S(1)} collective-permute-done((bf16[60,5120]{1,0:T(8,128)(2,1)S(1)}, bf16[60,5120]{1,0:T(8,128)(2,1)S(1)}, u32[]{:S(2)}, u32[]{:S(2)}) %collective-permute-start.30) | collective-permute-done | bytes 614432 | tf_op jit(solution)/shard_map/ppermute | solution.py:162
  112.6 1.1 add_convert_fusion
  (177 shorter events, 12.3 us)
Async XLA Ops:
  3.6 4.5 %copy-start.11 = (bf16[120,1280]{1,0:T(8,128)(2,1)S(1)}, bf16[120,1280]{1,0:T(8,128)(2,1)}, u32[]{:S(2)}) copy-start(bf16[120,1280]{1,0:T(8,128)(2,1)} %param.11) | copy-start | bytes 921604
  4.6 13.6 %collective-permute-start = (bf16[10,128,128]{2,1,0:T(8,128)(2,1)S(1)}, bf16[10,128,128]{2,1,0:T(8,128)(2,1)S(1)}, u32[]{:S(2)}, u32[]{:S(2)}) collective-permute-start(bf16[10,128,128]{2,1,0:T(8,128)(2,1)S(1)} %get-tuple-element.34), channel_id=1, source_target_pairs={{0,2},{2,0},{4,6},{6,4},{8,10},{10,8},{12,14},{14,12},{16,18},{18,... | collective-permute-start | bytes 983048 | tf_op jit(solution)/shard_map/ppermute | solution.py:40
  5.1 10.9 %collective-permute-start.1 = (bf16[10,128,128]{2,1,0:T(8,128)(2,1)S(1)}, bf16[10,128,128]{2,1,0:T(8,128)(2,1)S(1)}, u32[]{:S(2)}, u32[]{:S(2)}) collective-permute-start(bf16[10,128,128]{2,1,0:T(8,128)(2,1)S(1)} %get-tuple-element.34), channel_id=1, source_target_pairs={{0,8},{2,10},{8,16},{10,18},{16,24},{18,26},{24,28},{26,30},{28,20... | collective-permute-start | bytes 983048 | tf_op jit(solution)/shard_map/ppermute | solution.py:36
  7.8 10.4 %collective-permute-start.9 = (bf16[10,128,128]{2,1,0:T(8,128)(2,1)S(1)}, bf16[10,128,128]{2,1,0:T(8,128)(2,1)S(1)}, u32[]{:S(2)}, u32[]{:S(2)}) collective-permute-start(bf16[10,128,128]{2,1,0:T(8,128)(2,1)S(1)} %get-tuple-element.48), channel_id=1, source_target_pairs={{0,2},{2,0},{4,6},{6,4},{8,10},{10,8},{12,14},{14,12},{16,18},{18,... | collective-permute-start | bytes 983048 | tf_op jit(solution)/shard_map/ppermute | solution.py:41
  7.9 10.0 %collective-permute-start.10 = (bf16[10,128,128]{2,1,0:T(8,128)(2,1)S(1)}, bf16[10,128,128]{2,1,0:T(8,128)(2,1)S(1)}, u32[]{:S(2)}, u32[]{:S(2)}) collective-permute-start(bf16[10,128,128]{2,1,0:T(8,128)(2,1)S(1)} %get-tuple-element.48), channel_id=1, source_target_pairs={{8,0},{10,2},{16,8},{18,10},{24,16},{26,18},{28,24},{30,26},{20,28... | collective-permute-start | bytes 983048 | tf_op jit(solution)/shard_map/ppermute | solution.py:37
  16.0 9.5 %collective-permute-start.3 = (bf16[10,128,128]{2,1,0:T(8,128)(2,1)S(1)}, bf16[10,128,128]{2,1,0:T(8,128)(2,1)S(1)}, u32[]{:S(2)}, u32[]{:S(2)}) collective-permute-start(bf16[10,128,128]{2,1,0:T(8,128)(2,1)S(1)} %collective-permute-done.1), channel_id=1, source_target_pairs={{0,8},{2,10},{8,16},{10,18},{16,24},{18,26},{24,28},{26,30},{28,20... | collective-permute-start | bytes 983048 | tf_op jit(solution)/shard_map/ppermute | solution.py:36
  17.9 9.3 %collective-permute-start.12 = (bf16[10,128,128]{2,1,0:T(8,128)(2,1)S(1)}, bf16[10,128,128]{2,1,0:T(8,128)(2,1)}, u32[]{:S(2)}, u32[]{:S(2)}) collective-permute-start(bf16[10,128,128]{2,1,0:T(8,128)(2,1)S(1)} %collective-permute-done.10), channel_id=1, source_target_pairs={{8,0},{10,2},{16,8},{18,10},{24,16},{26,18},{28,24},{30,26},{20,28... | collective-permute-start | bytes 983048 | tf_op jit(solution)/shard_map/ppermute | solution.py:37
  18.6 9.6 %collective-permute-start.2 = (bf16[10,128,128]{2,1,0:T(8,128)(2,1)S(1)}, bf16[10,128,128]{2,1,0:T(8,128)(2,1)S(1)}, u32[]{:S(2)}, u32[]{:S(2)}) collective-permute-start(bf16[10,128,128]{2,1,0:T(8,128)(2,1)S(1)} %collective-permute-done.1), channel_id=1, source_target_pairs={{0,2},{2,0},{4,6},{6,4},{8,10},{10,8},{12,14},{14,12},{16,18},{18,... | collective-permute-start | bytes 983048 | tf_op jit(solution)/shard_map/ppermute | solution.py:40
  18.6 9.6 %collective-permute-start.11 = (bf16[10,128,128]{2,1,0:T(8,128)(2,1)S(1)}, bf16[10,128,128]{2,1,0:T(8,128)(2,1)S(1)}, u32[]{:S(2)}, u32[]{:S(2)}) collective-permute-start(bf16[10,128,128]{2,1,0:T(8,128)(2,1)S(1)} %collective-permute-done.10), channel_id=1, source_target_pairs={{0,2},{2,0},{4,6},{6,4},{8,10},{10,8},{12,14},{14,12},{16,18},{18,... | collective-permute-start | bytes 983048 | tf_op jit(solution)/shard_map/ppermute | solution.py:41
  25.5 8.7 %collective-permute-start.5 = (bf16[10,128,128]{2,1,0:T(8,128)(2,1)S(1)}, bf16[10,128,128]{2,1,0:T(8,128)(2,1)S(1)}, u32[]{:S(2)}, u32[]{:S(2)}) collective-permute-start(bf16[10,128,128]{2,1,0:T(8,128)(2,1)S(1)} %collective-permute-done.3), channel_id=1, source_target_pairs={{0,8},{2,10},{8,16},{10,18},{16,24},{18,26},{24,28},{26,30},{28,20... | collective-permute-start | bytes 983048 | tf_op jit(solution)/shard_map/ppermute | solution.py:36
  27.2 8.6 %collective-permute-start.14 = (bf16[10,128,128]{2,1,0:T(8,128)(2,1)}, bf16[10,128,128]{2,1,0:T(8,128)(2,1)}, u32[]{:S(2)}, u32[]{:S(2)}) collective-permute-start(bf16[10,128,128]{2,1,0:T(8,128)(2,1)} %collective-permute-done.12), channel_id=1, source_target_pairs={{8,0},{10,2},{16,8},{18,10},{24,16},{26,18},{28,24},{30,26},{20,28... | collective-permute-start | bytes 983048 | tf_op jit(solution)/shard_map/ppermute | solution.py:37
  28.3 0.7 copy-start.3
  29.4 7.6 %collective-permute-start.4 = (bf16[10,128,128]{2,1,0:T(8,128)(2,1)S(1)}, bf16[10,128,128]{2,1,0:T(8,128)(2,1)S(1)}, u32[]{:S(2)}, u32[]{:S(2)}) collective-permute-start(bf16[10,128,128]{2,1,0:T(8,128)(2,1)S(1)} %collective-permute-done.3), channel_id=1, source_target_pairs={{0,2},{2,0},{4,6},{6,4},{8,10},{10,8},{12,14},{14,12},{16,18},{18,... | collective-permute-start | bytes 983048 | tf_op jit(solution)/shard_map/ppermute | solution.py:40
  29.4 8.3 %collective-permute-start.13 = (bf16[10,128,128]{2,1,0:T(8,128)(2,1)}, bf16[10,128,128]{2,1,0:T(8,128)(2,1)S(1)}, u32[]{:S(2)}, u32[]{:S(2)}) collective-permute-start(bf16[10,128,128]{2,1,0:T(8,128)(2,1)} %collective-permute-done.12), channel_id=1, source_target_pairs={{0,2},{2,0},{4,6},{6,4},{8,10},{10,8},{12,14},{14,12},{16,18},{18,... | collective-permute-start | bytes 983048 | tf_op jit(solution)/shard_map/ppermute | solution.py:41
  34.2 8.0 %collective-permute-start.7 = (bf16[10,128,128]{2,1,0:T(8,128)(2,1)S(1)}, bf16[10,128,128]{2,1,0:T(8,128)(2,1)}, u32[]{:S(2)}, u32[]{:S(2)}) collective-permute-start(bf16[10,128,128]{2,1,0:T(8,128)(2,1)S(1)} %collective-permute-done.5), channel_id=1, source_target_pairs={{0,8},{2,10},{8,16},{10,18},{16,24},{18,26},{24,28},{26,30},{28,20... | collective-permute-start | bytes 983048 | tf_op jit(solution)/shard_map/ppermute | solution.py:36
  35.7 7.6 %collective-permute-start.16 = (bf16[10,128,128]{2,1,0:T(8,128)(2,1)}, bf16[10,128,128]{2,1,0:T(8,128)(2,1)}, u32[]{:S(2)}, u32[]{:S(2)}) collective-permute-start(bf16[10,128,128]{2,1,0:T(8,128)(2,1)} %collective-permute-done.14), channel_id=1, source_target_pairs={{8,0},{10,2},{16,8},{18,10},{24,16},{26,18},{28,24},{30,26},{20,28... | collective-permute-start | bytes 983048 | tf_op jit(solution)/shard_map/ppermute | solution.py:37
  37.0 0.7 copy-start.1
  37.7 0.7 copy-start.7
  38.9 5.2 %collective-permute-start.6 = (bf16[10,128,128]{2,1,0:T(8,128)(2,1)S(1)}, bf16[10,128,128]{2,1,0:T(8,128)(2,1)S(1)}, u32[]{:S(2)}, u32[]{:S(2)}) collective-permute-start(bf16[10,128,128]{2,1,0:T(8,128)(2,1)S(1)} %collective-permute-done.5), channel_id=1, source_target_pairs={{0,2},{2,0},{4,6},{6,4},{8,10},{10,8},{12,14},{14,12},{16,18},{18,... | collective-permute-start | bytes 983048 | tf_op jit(solution)/shard_map/ppermute | solution.py:40
  38.9 5.9 %collective-permute-start.15 = (bf16[10,128,128]{2,1,0:T(8,128)(2,1)}, bf16[10,128,128]{2,1,0:T(8,128)(2,1)S(1)}, u32[]{:S(2)}, u32[]{:S(2)}) collective-permute-start(bf16[10,128,128]{2,1,0:T(8,128)(2,1)} %collective-permute-done.14), channel_id=1, source_target_pairs={{0,2},{2,0},{4,6},{6,4},{8,10},{10,8},{12,14},{14,12},{16,18},{18,... | collective-permute-start | bytes 983048 | tf_op jit(solution)/shard_map/ppermute | solution.py:41
  42.2 5.8 %collective-permute-start.8 = (bf16[10,128,128]{2,1,0:T(8,128)(2,1)}, bf16[10,128,128]{2,1,0:T(8,128)(2,1)}, u32[]{:S(2)}, u32[]{:S(2)}) collective-permute-start(bf16[10,128,128]{2,1,0:T(8,128)(2,1)} %collective-permute-done.7), channel_id=1, source_target_pairs={{0,2},{2,0},{4,6},{6,4},{8,10},{10,8},{12,14},{14,12},{16,18},{18,... | collective-permute-start | bytes 983048 | tf_op jit(solution)/shard_map/ppermute | solution.py:40
  43.4 5.4 %collective-permute-start.17 = (bf16[10,128,128]{2,1,0:T(8,128)(2,1)}, bf16[10,128,128]{2,1,0:T(8,128)(2,1)}, u32[]{:S(2)}, u32[]{:S(2)}) collective-permute-start(bf16[10,128,128]{2,1,0:T(8,128)(2,1)} %collective-permute-done.16), channel_id=1, source_target_pairs={{0,2},{2,0},{4,6},{6,4},{8,10},{10,8},{12,14},{14,12},{16,18},{18,... | collective-permute-start | bytes 983048 | tf_op jit(solution)/shard_map/ppermute | solution.py:41
  44.1 0.7 copy-start.5
  44.8 0.7 copy-start.9
  46.0 10.4 %collective-permute-start.18 = (bf16[10,128,128]{2,1,0:T(8,128)(2,1)}, bf16[10,128,128]{2,1,0:T(8,128)(2,1)}, u32[]{:S(2)}, u32[]{:S(2)}) collective-permute-start(bf16[10,128,128]{2,1,0:T(8,128)(2,1)} %collective-permute-done.7), channel_id=1, source_target_pairs={{0,8},{2,10},{8,16},{10,18},{16,24},{18,26},{24,28},{26,30},{28,20... | collective-permute-start | bytes 983048 | tf_op jit(solution)/shard_map/ppermute | solution.py:36
  47.5 10.4 %collective-permute-start.22 = (bf16[10,128,128]{2,1,0:T(8,128)(2,1)}, bf16[10,128,128]{2,1,0:T(8,128)(2,1)}, u32[]{:S(2)}, u32[]{:S(2)}) collective-permute-start(bf16[10,128,128]{2,1,0:T(8,128)(2,1)} %collective-permute-done.16), channel_id=1, source_target_pairs={{8,0},{10,2},{16,8},{18,10},{24,16},{26,18},{28,24},{30,26},{20,28... | collective-permute-start | bytes 983048 | tf_op jit(solution)/shard_map/ppermute | solution.py:37
  49.7 20.9 %copy-start.4 = (bf16[10,128,128]{2,1,0:T(8,128)(2,1)S(1)}, bf16[10,128,128]{2,1,0:T(8,128)(2,1)}, u32[]{:S(2)}) copy-start(bf16[10,128,128]{2,1,0:T(8,128)(2,1)} %copy-done.3) | copy-start | bytes 983044
  56.4 9.5 %collective-permute-start.20 = (bf16[10,128,128]{2,1,0:T(8,128)(2,1)}, bf16[10,128,128]{2,1,0:T(8,128)(2,1)S(1)}, u32[]{:S(2)}, u32[]{:S(2)}) collective-permute-start(bf16[10,128,128]{2,1,0:T(8,128)(2,1)} %collective-permute-done.18), channel_id=1, source_target_pairs={{0,8},{2,10},{8,16},{10,18},{16,24},{18,26},{24,28},{26,30},{28,20... | collective-permute-start | bytes 983048 | tf_op jit(solution)/shard_map/ppermute | solution.py:36
  58.0 9.3 %collective-permute-start.24 = (bf16[10,128,128]{2,1,0:T(8,128)(2,1)}, bf16[10,128,128]{2,1,0:T(8,128)(2,1)S(1)}, u32[]{:S(2)}, u32[]{:S(2)}) collective-permute-start(bf16[10,128,128]{2,1,0:T(8,128)(2,1)} %collective-permute-done.22), channel_id=1, source_target_pairs={{8,0},{10,2},{16,8},{18,10},{24,16},{26,18},{28,24},{30,26},{20,28... | collective-permute-start | bytes 983048 | tf_op jit(solution)/shard_map/ppermute | solution.py:37
  58.5 9.2 %collective-permute-start.19 = (bf16[10,128,128]{2,1,0:T(8,128)(2,1)}, bf16[10,128,128]{2,1,0:T(8,128)(2,1)S(1)}, u32[]{:S(2)}, u32[]{:S(2)}) collective-permute-start(bf16[10,128,128]{2,1,0:T(8,128)(2,1)} %collective-permute-done.18), channel_id=1, source_target_pairs={{0,2},{2,0},{4,6},{6,4},{8,10},{10,8},{12,14},{14,12},{16,18},{18,... | collective-permute-start | bytes 983048 | tf_op jit(solution)/shard_map/ppermute | solution.py:40
  58.6 10.9 %collective-permute-start.23 = (bf16[10,128,128]{2,1,0:T(8,128)(2,1)}, bf16[10,128,128]{2,1,0:T(8,128)(2,1)S(1)}, u32[]{:S(2)}, u32[]{:S(2)}) collective-permute-start(bf16[10,128,128]{2,1,0:T(8,128)(2,1)} %collective-permute-done.22), channel_id=1, source_target_pairs={{0,2},{2,0},{4,6},{6,4},{8,10},{10,8},{12,14},{14,12},{16,18},{18,... | collective-permute-start | bytes 983048 | tf_op jit(solution)/shard_map/ppermute | solution.py:41
  65.9 3.5 %collective-permute-start.21 = (bf16[10,128,128]{2,1,0:T(8,128)(2,1)S(1)}, bf16[10,128,128]{2,1,0:T(8,128)(2,1)S(1)}, u32[]{:S(2)}, u32[]{:S(2)}) collective-permute-start(bf16[10,128,128]{2,1,0:T(8,128)(2,1)S(1)} %collective-permute-done.20), channel_id=1, source_target_pairs={{0,2},{2,0},{4,6},{6,4},{8,10},{10,8},{12,14},{14,12},{16,18},{18,... | collective-permute-start | bytes 983048 | tf_op jit(solution)/shard_map/ppermute | solution.py:40
  67.2 2.2 %collective-permute-start.25 = (bf16[10,128,128]{2,1,0:T(8,128)(2,1)S(1)}, bf16[10,128,128]{2,1,0:T(8,128)(2,1)S(1)}, u32[]{:S(2)}, u32[]{:S(2)}) collective-permute-start(bf16[10,128,128]{2,1,0:T(8,128)(2,1)S(1)} %collective-permute-done.24), channel_id=1, source_target_pairs={{0,2},{2,0},{4,6},{6,4},{8,10},{10,8},{12,14},{14,12},{16,18},{18,... | collective-permute-start | bytes 983048 | tf_op jit(solution)/shard_map/ppermute | solution.py:41
  67.4 4.3 %copy-start.8 = (bf16[10,128,128]{2,1,0:T(8,128)(2,1)S(1)}, bf16[10,128,128]{2,1,0:T(8,128)(2,1)}, u32[]{:S(2)}) copy-start(bf16[10,128,128]{2,1,0:T(8,128)(2,1)} %copy-done.7) | copy-start | bytes 983044
  67.4 15.0 %collective-permute-start.28 = (bf16[10,128,128]{2,1,0:T(8,128)(2,1)S(1)}, bf16[10,128,128]{2,1,0:T(8,128)(2,1)S(1)}, u32[]{:S(2)}, u32[]{:S(2)}) collective-permute-start(bf16[10,128,128]{2,1,0:T(8,128)(2,1)S(1)} %collective-permute-done.24), channel_id=1, source_target_pairs={{8,0},{10,2},{16,8},{18,10},{24,16},{26,18},{28,24},{30,26},{20,28... | collective-permute-start | bytes 983048 | tf_op jit(solution)/shard_map/ppermute | solution.py:37
  67.8 15.5 %collective-permute-start.26 = (bf16[10,128,128]{2,1,0:T(8,128)(2,1)S(1)}, bf16[10,128,128]{2,1,0:T(8,128)(2,1)S(1)}, u32[]{:S(2)}, u32[]{:S(2)}) collective-permute-start(bf16[10,128,128]{2,1,0:T(8,128)(2,1)S(1)} %collective-permute-done.20), channel_id=1, source_target_pairs={{0,8},{2,10},{8,16},{10,18},{16,24},{18,26},{24,28},{26,30},{28,20... | collective-permute-start | bytes 983048 | tf_op jit(solution)/shard_map/ppermute | solution.py:36
  70.5 2.3 %copy-start.10 = (bf16[10,128,128]{2,1,0:T(8,128)(2,1)S(1)}, bf16[10,128,128]{2,1,0:T(8,128)(2,1)}, u32[]{:S(2)}) copy-start(bf16[10,128,128]{2,1,0:T(8,128)(2,1)} %copy-done.9) | copy-start | bytes 983044
  77.5 1.0 copy-start.2
  77.6 1.0 copy-start.6
  82.3 2.2 %collective-permute-start.29 = (bf16[10,128,128]{2,1,0:T(8,128)(2,1)S(1)}, bf16[10,128,128]{2,1,0:T(8,128)(2,1)S(1)}, u32[]{:S(2)}, u32[]{:S(2)}) collective-permute-start(bf16[10,128,128]{2,1,0:T(8,128)(2,1)S(1)} %collective-permute-done.28), channel_id=1, source_target_pairs={{0,2},{2,0},{4,6},{6,4},{8,10},{10,8},{12,14},{14,12},{16,18},{18,... | collective-permute-start | bytes 983048 | tf_op jit(solution)/shard_map/ppermute | solution.py:41
  83.3 2.6 %collective-permute-start.27 = (bf16[10,128,128]{2,1,0:T(8,128)(2,1)S(1)}, bf16[10,128,128]{2,1,0:T(8,128)(2,1)S(1)}, u32[]{:S(2)}, u32[]{:S(2)}) collective-permute-start(bf16[10,128,128]{2,1,0:T(8,128)(2,1)S(1)} %collective-permute-done.26), channel_id=1, source_target_pairs={{0,2},{2,0},{4,6},{6,4},{8,10},{10,8},{12,14},{14,12},{16,18},{18,... | collective-permute-start | bytes 983048 | tf_op jit(solution)/shard_map/ppermute | solution.py:40
  88.3 4.3 %slice-start = ((s8[13107200]{0:T(1024)(128)(4,1)}), s8[4194304]{0:T(1024)(128)(4,1)S(1)}, s32[]{:S(2)}) async-start(s8[13107200]{0:T(1024)(128)(4,1)} %bitcast.402), calls=%async_computation | async-start | bytes 8388608
  89.4 3.2 %slice-start.1 = ((s8[13107200]{0:T(1024)(128)(4,1)}), s8[4194304]{0:T(1024)(128)(4,1)S(1)}, s32[]{:S(2)}) async-start(s8[13107200]{0:T(1024)(128)(4,1)} %bitcast.402), calls=%async_computation.1 | async-start | bytes 8388608
  90.5 2.7 %slice-start.2 = ((s8[13107200]{0:T(1024)(128)(4,1)}), s8[4194304]{0:T(1024)(128)(4,1)S(1)}, s32[]{:S(2)}) async-start(s8[13107200]{0:T(1024)(128)(4,1)} %bitcast.402), calls=%async_computation.2 | async-start | bytes 8388608
  91.5 1.7 %slice-start.3 = ((s8[13107200]{0:T(1024)(128)(4,1)}), s8[524288]{0:T(1024)(128)(4,1)S(1)}, s32[]{:S(2)}) async-start(s8[13107200]{0:T(1024)(128)(4,1)} %bitcast.402), calls=%async_computation.3 | async-start | bytes 1048576
  95.9 16.7 %collective-permute-start.30 = (bf16[60,5120]{1,0:T(8,128)(2,1)S(1)}, bf16[60,5120]{1,0:T(8,128)(2,1)S(1)}, u32[]{:S(2)}, u32[]{:S(2)}) collective-permute-start(bf16[60,5120]{1,0:T(8,128)(2,1)S(1)} %convolution_convert_fusion), channel_id=1, source_target_pairs={{0,1},{1,0},{2,3},{3,2},{4,5},{5,4},{6,7},{7,6},{8,9},{9,8},{10,11... | collective-permute-start | bytes 1843208 | tf_op jit(solution)/shard_map/ppermute | solution.py:162
  97.4 15.2 %copy-start = (bf16[60,5120]{1,0:T(8,128)(2,1)S(1)}, bf16[60,5120]{1,0:T(8,128)(2,1)}, u32[]{:S(2)}) copy-start(bf16[60,5120]{1,0:T(8,128)(2,1)} %param.10) | copy-start | bytes 1843204
  97.4 15.2 %copy-start.12 = (f32[5120]{0:T(1024)S(1)}, f32[5120]{0:T(1024)}, u32[]{:S(2)}) copy-start(f32[5120]{0:T(1024)} %param.14) | copy-start | bytes 61444

commit v20 on v15

--- a/solution.py
+++ b/solution.py
@@ -157,9 +157,17 @@
                 axis=1,
             )
 
-        other = jnp.dot(attention_rows(1 - side), out_weight, preferred_element_type=jnp.float32)
-        other = other.astype(jnp.bfloat16)
-        came = lax.ppermute(other, "tp", [(0, 1), (1, 0)])
+        attention_other = attention_rows(1 - side)
+        width_all = out_weight.shape[1]
+        n_cols = 2 if width_all % (2 * HEAD) == 0 else 1
+        width = width_all // n_cols
+        came = []
+        for i in range(n_cols):
+            other = jnp.dot(
+                attention_other, out_weight[:, i * width : (i + 1) * width], preferred_element_type=jnp.float32
+            ).astype(jnp.bfloat16)
+            came.append(lax.ppermute(other, "tp", [(0, 1), (1, 0)]))
+        came = jnp.concatenate(came, axis=1)
         attention_own = attention_rows(side)
         own = jnp.dot(attention_own, out_weight, preferred_element_type=jnp.float32)
         own = lax.optimization_barrier(own)

time: 111 us -> 112 us (level)
    ppermute x7, waiting for transfers between devices: 6.34 us -> 9.45 us  [gather_ring(): cur_b = lax.ppermute(cur_b, 'seq', backward)]
    ppermute x7, waiting for transfers between devices: 28.2 us -> 25.7 us  [gather_ring(): cur_a = lax.ppermute(cur_a, 'seq', forward)]
    ppermute x1 -> x2, waiting for transfers between devices: 10.3 us -> 9.67 us  [on_device(): came.append(lax.ppermute(other, 'tp', [(0, 1), (1, 0)]))]
    dot_general x1 -> x2, matrix products: 2.38 us -> 2.53 us  [on_device(): jnp.dot(attention_other, out_weight[:, i * width:(i + 1) * width], prefer...]
    unnamed x68 -> x69, local copies, waits for them, and re-layouts: 9.42 us -> 9.45 us
  transfers between devices with their start and end apart: 31 -> 32, of which waited for: 12 -> 13; matrix products, arithmetic and copies ran while one was open for 25% -> 25% of each run, Pallas kernels for 0% -> 0%
where the time goes in v20:
time: 112 us; the launch traced here: 111 us
  waiting for transfers between devices  44.9 us (40%)
  local copies, waits for them, and re-layouts  22.2 us (20%)
  starting transfers between devices  20.1 us (18%)
  matrix products  15.6 us (14%)
  other arithmetic  5.61 us (5%)
  between operations  2.63 us (2%)
    ppermute x7, waiting for transfers between devices, gather_ring(): cur_a = lax.ppermute(cur_a, 'seq', forward)  25.7 us
    ppermute x7, starting transfers between devices, gather_ring(): cur_a = lax.ppermute(cur_a, 'seq', forward)  12.2 us
    ppermute x2, waiting for transfers between devices, on_device(): came.append(lax.ppermute(other, 'tp', [(0, 1), (1, 0)]))  9.67 us
    unnamed x69, local copies, waits for them, and re-layouts  9.45 us
    ppermute x7, waiting for transfers between devices, gather_ring(): cur_b = lax.ppermute(cur_b, 'seq', backward)  9.45 us
    another operation x37, local copies, waits for them, and re-layouts, on_device(): jnp.stack([g[0, rows_dev, :2] for g in heard]).astype(jnp.float32)  6.16 us
    dot_general x12, matrix products, attend_part(): jnp.einsum('hqd,nhkd->hqnk', queries_3d, keys, preferred_element_type=jnp...  6.12 us
    dot_general x12, matrix products, attend_part(): jnp.einsum('hqnk,nhkd->hqd', weights.astype(jnp.bfloat16), values, prefer...  4.58 us
  transfers between devices with their start and end apart: 32, of which 13 were waited for; matrix products, arithmetic and copies ran while one was open for 25% of the time, Pallas kernels for 0%

profile of v20, /device:TPU:0, one launch (start us, length us, event | category | flops | bytes accessed | tf_op | source)
XLA Modules:
  0.0 111.0 jit_solution(8117908618321145679)
XLA Ops:
  0.0 1.0 fusion.243
  1.0 1.0 fusion.244
  4.6 3.1 %collective-permute-start.1 = (bf16[10,128,128]{2,1,0:T(8,128)(2,1)S(1)}, bf16[10,128,128]{2,1,0:T(8,128)(2,1)S(1)}, u32[]{:S(2)}, u32[]{:S(2)}) collective-permute-start(bf16[10,128,128]{2,1,0:T(8,128)(2,1)S(1)} %get-tuple-element.34), channel_id=1, source_target_pairs={{0,8},{2,10},{8,16},{10,18},{16,24},{18,26},{24,28},{26,30},{28,20... | collective-permute-start | bytes 983048 | tf_op jit(solution)/shard_map/ppermute | solution.py:36
  9.7 5.7 %collective-permute-done.1 = bf16[10,128,128]{2,1,0:T(8,128)(2,1)S(1)} collective-permute-done((bf16[10,128,128]{2,1,0:T(8,128)(2,1)S(1)}, bf16[10,128,128]{2,1,0:T(8,128)(2,1)S(1)}, u32[]{:S(2)}, u32[]{:S(2)}) %collective-permute-start.1) | collective-permute-done | bytes 327712 | tf_op jit(solution)/shard_map/ppermute | solution.py:36
  15.3 1.8 %collective-permute-start.3 = (bf16[10,128,128]{2,1,0:T(8,128)(2,1)S(1)}, bf16[10,128,128]{2,1,0:T(8,128)(2,1)S(1)}, u32[]{:S(2)}, u32[]{:S(2)}) collective-permute-start(bf16[10,128,128]{2,1,0:T(8,128)(2,1)S(1)} %collective-permute-done.1), channel_id=1, source_target_pairs={{0,8},{2,10},{8,16},{10,18},{16,24},{18,26},{24,28},{26,30},{28,20... | collective-permute-start | bytes 983048 | tf_op jit(solution)/shard_map/ppermute | solution.py:36
  17.1 0.7 collective-permute-done.10
  18.5 0.5 collective-permute-start.2
  19.1 5.2 %collective-permute-done.3 = bf16[10,128,128]{2,1,0:T(8,128)(2,1)S(1)} collective-permute-done((bf16[10,128,128]{2,1,0:T(8,128)(2,1)S(1)}, bf16[10,128,128]{2,1,0:T(8,128)(2,1)S(1)}, u32[]{:S(2)}, u32[]{:S(2)}) %collective-permute-start.3) | collective-permute-done | bytes 327712 | tf_op jit(solution)/shard_map/ppermute | solution.py:36
  24.2 1.5 %collective-permute-start.5 = (bf16[10,128,128]{2,1,0:T(8,128)(2,1)S(1)}, bf16[10,128,128]{2,1,0:T(8,128)(2,1)S(1)}, u32[]{:S(2)}, u32[]{:S(2)}) collective-permute-start(bf16[10,128,128]{2,1,0:T(8,128)(2,1)S(1)} %collective-permute-done.3), channel_id=1, source_target_pairs={{0,8},{2,10},{8,16},{10,18},{16,24},{18,26},{24,28},{26,30},{28,20... | collective-permute-start | bytes 983048 | tf_op jit(solution)/shard_map/ppermute | solution.py:36
  25.7 1.5 %collective-permute-done.12 = bf16[10,128,128]{2,1,0:T(8,128)(2,1)} collective-permute-done((bf16[10,128,128]{2,1,0:T(8,128)(2,1)S(1)}, bf16[10,128,128]{2,1,0:T(8,128)(2,1)}, u32[]{:S(2)}, u32[]{:S(2)}) %collective-permute-start.12) | collective-permute-done | bytes 327712 | tf_op jit(solution)/shard_map/ppermute | solution.py:37
  27.7 0.7 slice_bitcast_fusion.5
  28.4 0.8 copy-done.7
  29.6 0.5 collective-permute-start.4
  30.1 2.2 %collective-permute-done.5 = bf16[10,128,128]{2,1,0:T(8,128)(2,1)S(1)} collective-permute-done((bf16[10,128,128]{2,1,0:T(8,128)(2,1)S(1)}, bf16[10,128,128]{2,1,0:T(8,128)(2,1)S(1)}, u32[]{:S(2)}, u32[]{:S(2)}) %collective-permute-start.5) | collective-permute-done | bytes 327712 | tf_op jit(solution)/shard_map/ppermute | solution.py:36
  32.3 1.2 %collective-permute-start.7 = (bf16[10,128,128]{2,1,0:T(8,128)(2,1)S(1)}, bf16[10,128,128]{2,1,0:T(8,128)(2,1)}, u32[]{:S(2)}, u32[]{:S(2)}) collective-permute-start(bf16[10,128,128]{2,1,0:T(8,128)(2,1)S(1)} %collective-permute-done.5), channel_id=1, source_target_pairs={{0,8},{2,10},{8,16},{10,18},{16,24},{18,26},{24,28},{26,30},{28,20... | collective-permute-start | bytes 983048 | tf_op jit(solution)/shard_map/ppermute | solution.py:36
  33.5 2.5 %collective-permute-done.14 = bf16[10,128,128]{2,1,0:T(8,128)(2,1)} collective-permute-done((bf16[10,128,128]{2,1,0:T(8,128)(2,1)}, bf16[10,128,128]{2,1,0:T(8,128)(2,1)}, u32[]{:S(2)}, u32[]{:S(2)}) %collective-permute-start.14) | collective-permute-done | bytes 327712 | tf_op jit(solution)/shard_map/ppermute | solution.py:37
  36.0 0.5 collective-permute-start.16
  36.6 0.7 slice_bitcast_fusion.3
  37.3 0.7 copy-done.5
  38.0 0.7 copy-done.11
  39.2 0.5 collective-permute-start.6
  39.9 0.7 slice_bitcast_fusion.10
  40.6 3.3 %collective-permute-done.16 = bf16[10,128,128]{2,1,0:T(8,128)(2,1)} collective-permute-done((bf16[10,128,128]{2,1,0:T(8,128)(2,1)}, bf16[10,128,128]{2,1,0:T(8,128)(2,1)}, u32[]{:S(2)}, u32[]{:S(2)}) %collective-permute-start.16) | collective-permute-done | bytes 327712 | tf_op jit(solution)/shard_map/ppermute | solution.py:37
  43.9 0.7 slice_bitcast_fusion.1
  44.5 0.7 copy-done.9
  45.3 0.7 copy-done.13
  46.4 1.6 %collective-permute-start.18 = (bf16[10,128,128]{2,1,0:T(8,128)(2,1)}, bf16[10,128,128]{2,1,0:T(8,128)(2,1)S(1)}, u32[]{:S(2)}, u32[]{:S(2)}) collective-permute-start(bf16[10,128,128]{2,1,0:T(8,128)(2,1)} %collective-permute-done.7), channel_id=1, source_target_pairs={{0,8},{2,10},{8,16},{10,18},{16,24},{18,26},{24,28},{26,30},{28,20... | collective-permute-start | bytes 983048 | tf_op jit(solution)/shard_map/ppermute | solution.py:36
  48.0 0.4 collective-permute-start.22
  48.5 0.7 slice_bitcast_fusion.9
  49.3 0.7 slice_bitcast_fusion
  50.9 5.9 %collective-permute-done.18 = bf16[10,128,128]{2,1,0:T(8,128)(2,1)S(1)} collective-permute-done((bf16[10,128,128]{2,1,0:T(8,128)(2,1)}, bf16[10,128,128]{2,1,0:T(8,128)(2,1)S(1)}, u32[]{:S(2)}, u32[]{:S(2)}) %collective-permute-start.18) | collective-permute-done | bytes 327712 | tf_op jit(solution)/shard_map/ppermute | solution.py:36
  56.8 1.6 %collective-permute-start.20 = (bf16[10,128,128]{2,1,0:T(8,128)(2,1)S(1)}, bf16[10,128,128]{2,1,0:T(8,128)(2,1)S(1)}, u32[]{:S(2)}, u32[]{:S(2)}) collective-permute-start(bf16[10,128,128]{2,1,0:T(8,128)(2,1)S(1)} %collective-permute-done.18), channel_id=1, source_target_pairs={{0,8},{2,10},{8,16},{10,18},{16,24},{18,26},{24,28},{26,30},{28,20... | collective-permute-start | bytes 983048 | tf_op jit(solution)/shard_map/ppermute | solution.py:36
  58.4 0.4 collective-permute-start.24
  59.0 0.5 collective-permute-start.23
  59.6 6.5 %collective-permute-done.20 = bf16[10,128,128]{2,1,0:T(8,128)(2,1)S(1)} collective-permute-done((bf16[10,128,128]{2,1,0:T(8,128)(2,1)S(1)}, bf16[10,128,128]{2,1,0:T(8,128)(2,1)S(1)}, u32[]{:S(2)}, u32[]{:S(2)}) %collective-permute-start.20) | collective-permute-done | bytes 327712 | tf_op jit(solution)/shard_map/ppermute | solution.py:36
  66.1 1.4 %collective-permute-done.24 = bf16[10,128,128]{2,1,0:T(8,128)(2,1)S(1)} collective-permute-done((bf16[10,128,128]{2,1,0:T(8,128)(2,1)S(1)}, bf16[10,128,128]{2,1,0:T(8,128)(2,1)S(1)}, u32[]{:S(2)}, u32[]{:S(2)}) %collective-permute-start.24) | collective-permute-done | bytes 327712 | tf_op jit(solution)/shard_map/ppermute | solution.py:37
  67.7 0.5 collective-permute-start.28
  68.1 1.6 %collective-permute-start.26 = (bf16[10,128,128]{2,1,0:T(8,128)(2,1)S(1)}, bf16[10,128,128]{2,1,0:T(8,128)(2,1)S(1)}, u32[]{:S(2)}, u32[]{:S(2)}) collective-permute-start(bf16[10,128,128]{2,1,0:T(8,128)(2,1)S(1)} %collective-permute-done.20), channel_id=1, source_target_pairs={{0,8},{2,10},{8,16},{10,18},{16,24},{18,26},{24,28},{26,30},{28,20... | collective-permute-start | bytes 983048 | tf_op jit(solution)/shard_map/ppermute | solution.py:36
  69.9 1.0 bitcast_dynamic-update-slice_fusion.4
  71.0 1.0 bitcast_dynamic-update-slice_fusion.2
  72.1 1.0 bitcast_dynamic-update-slice_fusion
  73.1 1.0 bitcast_dynamic-update-slice_fusion.18
  74.1 0.8 fusion.252
  74.9 0.8 fusion.251
  77.3 0.7 copy-done.4
  78.4 1.0 bitcast_dynamic-update-slice_fusion.9
  79.4 1.0 bitcast_dynamic-update-slice_fusion.19
  80.5 0.8 fusion.258
  81.7 0.7 fusion.28
  82.8 0.8 fusion.257
  84.6 0.5 collective-permute-start.27
  85.1 0.7 fusion.26
  87.6 0.5 fusion.70
  89.2 0.5 fusion.76
  90.5 1.3 %fusion.4 = bf16[60,2560]{1,0:T(8,128)(2,1)S(1)} fusion(bf16[60,1280]{1,0:T(8,128)(2,1)S(1)} %constant_dynamic-update-slice_fusion, bf16[1280,5120]{1,0:T(8,128)(2,1)S(1)} %bitcast.604), kind=kOutput, calls=%fused_computation.4 | convolution fusion | flops 393369600 | bytes 7024640 | tf_op jit(solution)/shard_map/dot_general | solution.py:166
  91.8 1.3 %fusion.7 = bf16[60,2560]{1,0:T(8,128)(2,1)S(1)} fusion(bf16[60,1280]{1,0:T(8,128)(2,1)S(1)} %constant_dynamic-update-slice_fusion, bf16[1280,5120]{1,0:T(8,128)(2,1)S(1)} %bitcast.604), kind=kOutput, calls=%fused_computation.5 | convolution fusion | flops 393369600 | bytes 7024640 | tf_op jit(solution)/shard_map/dot_general | solution.py:166
  93.0 1.6 %collective-permute-start.30 = (bf16[60,2560]{1,0:T(8,128)(2,1)S(1)}, bf16[60,2560]{1,0:T(8,128)(2,1)S(1)}, u32[]{:S(2)}, u32[]{:S(2)}) collective-permute-start(bf16[60,2560]{1,0:T(8,128)(2,1)S(1)} %fusion.4), channel_id=1, source_target_pairs={{0,1},{1,0},{2,3},{3,2},{4,5},{5,4},{6,7},{7,6},{8,9},{9,8},{10,11... | collective-permute-start | bytes 921608 | tf_op jit(solution)/shard_map/ppermute | solution.py:169
  94.6 0.5 collective-permute-start.31
  95.1 0.7 fusion.79
  96.6 0.5 fusion.73
  97.9 2.4 %fusion.156 = f32[60,5120]{1,0:T(8,128)S(1)} fusion(bf16[1280,5120]{1,0:T(8,128)(2,1)S(1)} %bitcast.604, bf16[60,640]{1,0:T(8,128)(2,1)S(1)} %bitcast.614, bf16[60,640]{1,0:T(8,128)(2,1)S(1)} %bitcast.613), kind=kOutput, calls=%fused_computation.189 | convolution fusion | flops 786739200 | bytes 14489600 | tf_op jit(solution)/shard_map/dot_general | solution.py:172
  100.2 3.4 %collective-permute-done.30 = bf16[60,2560]{1,0:T(8,128)(2,1)S(1)} collective-permute-done((bf16[60,2560]{1,0:T(8,128)(2,1)S(1)}, bf16[60,2560]{1,0:T(8,128)(2,1)S(1)}, u32[]{:S(2)}, u32[]{:S(2)}) %collective-permute-start.30) | collective-permute-done | bytes 307232 | tf_op jit(solution)/shard_map/ppermute | solution.py:169
  103.6 6.3 %collective-permute-done.31 = bf16[60,2560]{1,0:T(8,128)(2,1)S(1)} collective-permute-done((bf16[60,2560]{1,0:T(8,128)(2,1)S(1)}, bf16[60,2560]{1,0:T(8,128)(2,1)S(1)}, u32[]{:S(2)}, u32[]{:S(2)}) %collective-permute-start.31) | collective-permute-done | bytes 307232 | tf_op jit(solution)/shard_map/ppermute | solution.py:169
  109.9 1.1 add_convert_fusion
  (196 shorter events, 15.6 us)
Async XLA Ops:
  2.3 5.9 %copy-start.15 = (bf16[120,1280]{1,0:T(8,128)(2,1)S(1)}, bf16[120,1280]{1,0:T(8,128)(2,1)}, u32[]{:S(2)}) copy-start(bf16[120,1280]{1,0:T(8,128)(2,1)} %param.11) | copy-start | bytes 921604
  4.6 10.7 %collective-permute-start.1 = (bf16[10,128,128]{2,1,0:T(8,128)(2,1)S(1)}, bf16[10,128,128]{2,1,0:T(8,128)(2,1)S(1)}, u32[]{:S(2)}, u32[]{:S(2)}) collective-permute-start(bf16[10,128,128]{2,1,0:T(8,128)(2,1)S(1)} %get-tuple-element.34), channel_id=1, source_target_pairs={{0,8},{2,10},{8,16},{10,18},{16,24},{18,26},{24,28},{26,30},{28,20... | collective-permute-start | bytes 983048 | tf_op jit(solution)/shard_map/ppermute | solution.py:36
  7.7 10.4 %collective-permute-start = (bf16[10,128,128]{2,1,0:T(8,128)(2,1)S(1)}, bf16[10,128,128]{2,1,0:T(8,128)(2,1)S(1)}, u32[]{:S(2)}, u32[]{:S(2)}) collective-permute-start(bf16[10,128,128]{2,1,0:T(8,128)(2,1)S(1)} %get-tuple-element.34), channel_id=1, source_target_pairs={{0,2},{2,0},{4,6},{6,4},{8,10},{10,8},{12,14},{14,12},{16,18},{18,... | collective-permute-start | bytes 983048 | tf_op jit(solution)/shard_map/ppermute | solution.py:40
  7.7 10.1 %collective-permute-start.10 = (bf16[10,128,128]{2,1,0:T(8,128)(2,1)S(1)}, bf16[10,128,128]{2,1,0:T(8,128)(2,1)S(1)}, u32[]{:S(2)}, u32[]{:S(2)}) collective-permute-start(bf16[10,128,128]{2,1,0:T(8,128)(2,1)S(1)} %get-tuple-element.48), channel_id=1, source_target_pairs={{8,0},{10,2},{16,8},{18,10},{24,16},{26,18},{28,24},{30,26},{20,28... | collective-permute-start | bytes 983048 | tf_op jit(solution)/shard_map/ppermute | solution.py:37
  7.8 10.3 %collective-permute-start.9 = (bf16[10,128,128]{2,1,0:T(8,128)(2,1)S(1)}, bf16[10,128,128]{2,1,0:T(8,128)(2,1)S(1)}, u32[]{:S(2)}, u32[]{:S(2)}) collective-permute-start(bf16[10,128,128]{2,1,0:T(8,128)(2,1)S(1)} %get-tuple-element.48), channel_id=1, source_target_pairs={{0,2},{2,0},{4,6},{6,4},{8,10},{10,8},{12,14},{14,12},{16,18},{18,... | collective-permute-start | bytes 983048 | tf_op jit(solution)/shard_map/ppermute | solution.py:41
  15.3 8.9 %collective-permute-start.3 = (bf16[10,128,128]{2,1,0:T(8,128)(2,1)S(1)}, bf16[10,128,128]{2,1,0:T(8,128)(2,1)S(1)}, u32[]{:S(2)}, u32[]{:S(2)}) collective-permute-start(bf16[10,128,128]{2,1,0:T(8,128)(2,1)S(1)} %collective-permute-done.1), channel_id=1, source_target_pairs={{0,8},{2,10},{8,16},{10,18},{16,24},{18,26},{24,28},{26,30},{28,20... | collective-permute-start | bytes 983048 | tf_op jit(solution)/shard_map/ppermute | solution.py:36
  17.8 9.4 %collective-permute-start.12 = (bf16[10,128,128]{2,1,0:T(8,128)(2,1)S(1)}, bf16[10,128,128]{2,1,0:T(8,128)(2,1)}, u32[]{:S(2)}, u32[]{:S(2)}) collective-permute-start(bf16[10,128,128]{2,1,0:T(8,128)(2,1)S(1)} %collective-permute-done.10), channel_id=1, source_target_pairs={{8,0},{10,2},{16,8},{18,10},{24,16},{26,18},{28,24},{30,26},{20,28... | collective-permute-start | bytes 983048 | tf_op jit(solution)/shard_map/ppermute | solution.py:37
  18.5 9.8 %collective-permute-start.11 = (bf16[10,128,128]{2,1,0:T(8,128)(2,1)S(1)}, bf16[10,128,128]{2,1,0:T(8,128)(2,1)S(1)}, u32[]{:S(2)}, u32[]{:S(2)}) collective-permute-start(bf16[10,128,128]{2,1,0:T(8,128)(2,1)S(1)} %collective-permute-done.10), channel_id=1, source_target_pairs={{0,2},{2,0},{4,6},{6,4},{8,10},{10,8},{12,14},{14,12},{16,18},{18,... | collective-permute-start | bytes 983048 | tf_op jit(solution)/shard_map/ppermute | solution.py:41
  18.5 9.8 %collective-permute-start.2 = (bf16[10,128,128]{2,1,0:T(8,128)(2,1)S(1)}, bf16[10,128,128]{2,1,0:T(8,128)(2,1)S(1)}, u32[]{:S(2)}, u32[]{:S(2)}) collective-permute-start(bf16[10,128,128]{2,1,0:T(8,128)(2,1)S(1)} %collective-permute-done.1), channel_id=1, source_target_pairs={{0,2},{2,0},{4,6},{6,4},{8,10},{10,8},{12,14},{14,12},{16,18},{18,... | collective-permute-start | bytes 983048 | tf_op jit(solution)/shard_map/ppermute | solution.py:40
  24.2 8.1 %collective-permute-start.5 = (bf16[10,128,128]{2,1,0:T(8,128)(2,1)S(1)}, bf16[10,128,128]{2,1,0:T(8,128)(2,1)S(1)}, u32[]{:S(2)}, u32[]{:S(2)}) collective-permute-start(bf16[10,128,128]{2,1,0:T(8,128)(2,1)S(1)} %collective-permute-done.3), channel_id=1, source_target_pairs={{0,8},{2,10},{8,16},{10,18},{16,24},{18,26},{24,28},{26,30},{28,20... | collective-permute-start | bytes 983048 | tf_op jit(solution)/shard_map/ppermute | solution.py:36
  27.3 8.8 %collective-permute-start.14 = (bf16[10,128,128]{2,1,0:T(8,128)(2,1)}, bf16[10,128,128]{2,1,0:T(8,128)(2,1)}, u32[]{:S(2)}, u32[]{:S(2)}) collective-permute-start(bf16[10,128,128]{2,1,0:T(8,128)(2,1)} %collective-permute-done.12), channel_id=1, source_target_pairs={{8,0},{10,2},{16,8},{18,10},{24,16},{26,18},{28,24},{30,26},{20,28... | collective-permute-start | bytes 983048 | tf_op jit(solution)/shard_map/ppermute | solution.py:37
  28.4 18.1 %copy-start.3 = (bf16[10,128,128]{2,1,0:T(8,128)(2,1)}, bf16[10,128,128]{2,1,0:T(8,128)(2,1)S(1)}, u32[]{:S(2)}) copy-start(bf16[10,128,128]{2,1,0:T(8,128)(2,1)S(1)} %collective-permute-done.2) | copy-start | bytes 983044
  28.4 0.8 copy-start.7
  29.6 8.4 %collective-permute-start.13 = (bf16[10,128,128]{2,1,0:T(8,128)(2,1)}, bf16[10,128,128]{2,1,0:T(8,128)(2,1)S(1)}, u32[]{:S(2)}, u32[]{:S(2)}) collective-permute-start(bf16[10,128,128]{2,1,0:T(8,128)(2,1)} %collective-permute-done.12), channel_id=1, source_target_pairs={{0,2},{2,0},{4,6},{6,4},{8,10},{10,8},{12,14},{14,12},{16,18},{18,... | collective-permute-start | bytes 983048 | tf_op jit(solution)/shard_map/ppermute | solution.py:41
  29.6 7.7 %collective-permute-start.4 = (bf16[10,128,128]{2,1,0:T(8,128)(2,1)S(1)}, bf16[10,128,128]{2,1,0:T(8,128)(2,1)S(1)}, u32[]{:S(2)}, u32[]{:S(2)}) collective-permute-start(bf16[10,128,128]{2,1,0:T(8,128)(2,1)S(1)} %collective-permute-done.3), channel_id=1, source_target_pairs={{0,2},{2,0},{4,6},{6,4},{8,10},{10,8},{12,14},{14,12},{16,18},{18,... | collective-permute-start | bytes 983048 | tf_op jit(solution)/shard_map/ppermute | solution.py:40
  32.3 14.0 %copy-start.1 = (bf16[10,128,128]{2,1,0:T(8,128)(2,1)}, bf16[10,128,128]{2,1,0:T(8,128)(2,1)S(1)}, u32[]{:S(2)}) copy-start(bf16[10,128,128]{2,1,0:T(8,128)(2,1)S(1)} %collective-permute-done.5) | copy-start | bytes 983044
  32.3 7.6 %collective-permute-start.7 = (bf16[10,128,128]{2,1,0:T(8,128)(2,1)S(1)}, bf16[10,128,128]{2,1,0:T(8,128)(2,1)}, u32[]{:S(2)}, u32[]{:S(2)}) collective-permute-start(bf16[10,128,128]{2,1,0:T(8,128)(2,1)S(1)} %collective-permute-done.5), channel_id=1, source_target_pairs={{0,8},{2,10},{8,16},{10,18},{16,24},{18,26},{24,28},{26,30},{28,20... | collective-permute-start | bytes 983048 | tf_op jit(solution)/shard_map/ppermute | solution.py:36
  36.0 7.8 %collective-permute-start.16 = (bf16[10,128,128]{2,1,0:T(8,128)(2,1)}, bf16[10,128,128]{2,1,0:T(8,128)(2,1)}, u32[]{:S(2)}, u32[]{:S(2)}) collective-permute-start(bf16[10,128,128]{2,1,0:T(8,128)(2,1)} %collective-permute-done.14), channel_id=1, source_target_pairs={{8,0},{10,2},{16,8},{18,10},{24,16},{26,18},{28,24},{30,26},{20,28... | collective-permute-start | bytes 983048 | tf_op jit(solution)/shard_map/ppermute | solution.py:37
  37.3 0.7 copy-start.5
  38.0 0.7 copy-start.11
  39.2 6.1 %collective-permute-start.15 = (bf16[10,128,128]{2,1,0:T(8,128)(2,1)}, bf16[10,128,128]{2,1,0:T(8,128)(2,1)S(1)}, u32[]{:S(2)}, u32[]{:S(2)}) collective-permute-start(bf16[10,128,128]{2,1,0:T(8,128)(2,1)} %collective-permute-done.14), channel_id=1, source_target_pairs={{0,2},{2,0},{4,6},{6,4},{8,10},{10,8},{12,14},{14,12},{16,18},{18,... | collective-permute-start | bytes 983048 | tf_op jit(solution)/shard_map/ppermute | solution.py:41
  39.2 5.4 %collective-permute-start.6 = (bf16[10,128,128]{2,1,0:T(8,128)(2,1)S(1)}, bf16[10,128,128]{2,1,0:T(8,128)(2,1)S(1)}, u32[]{:S(2)}, u32[]{:S(2)}) collective-permute-start(bf16[10,128,128]{2,1,0:T(8,128)(2,1)S(1)} %collective-permute-done.5), channel_id=1, source_target_pairs={{0,2},{2,0},{4,6},{6,4},{8,10},{10,8},{12,14},{14,12},{16,18},{18,... | collective-permute-start | bytes 983048 | tf_op jit(solution)/shard_map/ppermute | solution.py:40
  39.9 8.6 %collective-permute-start.8 = (bf16[10,128,128]{2,1,0:T(8,128)(2,1)}, bf16[10,128,128]{2,1,0:T(8,128)(2,1)}, u32[]{:S(2)}, u32[]{:S(2)}) collective-permute-start(bf16[10,128,128]{2,1,0:T(8,128)(2,1)} %collective-permute-done.7), channel_id=1, source_target_pairs={{0,2},{2,0},{4,6},{6,4},{8,10},{10,8},{12,14},{14,12},{16,18},{18,... | collective-permute-start | bytes 983048 | tf_op jit(solution)/shard_map/ppermute | solution.py:40
  43.9 5.4 %collective-permute-start.17 = (bf16[10,128,128]{2,1,0:T(8,128)(2,1)}, bf16[10,128,128]{2,1,0:T(8,128)(2,1)}, u32[]{:S(2)}, u32[]{:S(2)}) collective-permute-start(bf16[10,128,128]{2,1,0:T(8,128)(2,1)} %collective-permute-done.16), channel_id=1, source_target_pairs={{0,2},{2,0},{4,6},{6,4},{8,10},{10,8},{12,14},{14,12},{16,18},{18,... | collective-permute-start | bytes 983048 | tf_op jit(solution)/shard_map/ppermute | solution.py:41
  44.5 0.7 copy-start.9
  45.3 0.7 copy-start.13
  46.4 10.3 %collective-permute-start.18 = (bf16[10,128,128]{2,1,0:T(8,128)(2,1)}, bf16[10,128,128]{2,1,0:T(8,128)(2,1)S(1)}, u32[]{:S(2)}, u32[]{:S(2)}) collective-permute-start(bf16[10,128,128]{2,1,0:T(8,128)(2,1)} %collective-permute-done.7), channel_id=1, source_target_pairs={{0,8},{2,10},{8,16},{10,18},{16,24},{18,26},{24,28},{26,30},{28,20... | collective-permute-start | bytes 983048 | tf_op jit(solution)/shard_map/ppermute | solution.py:36
  48.0 10.4 %collective-permute-start.22 = (bf16[10,128,128]{2,1,0:T(8,128)(2,1)}, bf16[10,128,128]{2,1,0:T(8,128)(2,1)S(1)}, u32[]{:S(2)}, u32[]{:S(2)}) collective-permute-start(bf16[10,128,128]{2,1,0:T(8,128)(2,1)} %collective-permute-done.16), channel_id=1, source_target_pairs={{8,0},{10,2},{16,8},{18,10},{24,16},{26,18},{28,24},{30,26},{20,28... | collective-permute-start | bytes 983048 | tf_op jit(solution)/shard_map/ppermute | solution.py:37
  50.2 19.7 %copy-start.8 = (bf16[10,128,128]{2,1,0:T(8,128)(2,1)S(1)}, bf16[10,128,128]{2,1,0:T(8,128)(2,1)}, u32[]{:S(2)}) copy-start(bf16[10,128,128]{2,1,0:T(8,128)(2,1)} %copy-done.7) | copy-start | bytes 983044
  56.8 9.3 %collective-permute-start.20 = (bf16[10,128,128]{2,1,0:T(8,128)(2,1)S(1)}, bf16[10,128,128]{2,1,0:T(8,128)(2,1)S(1)}, u32[]{:S(2)}, u32[]{:S(2)}) collective-permute-start(bf16[10,128,128]{2,1,0:T(8,128)(2,1)S(1)} %collective-permute-done.18), channel_id=1, source_target_pairs={{0,8},{2,10},{8,16},{10,18},{16,24},{18,26},{24,28},{26,30},{28,20... | collective-permute-start | bytes 983048 | tf_op jit(solution)/shard_map/ppermute | solution.py:36
  58.4 9.1 %collective-permute-start.24 = (bf16[10,128,128]{2,1,0:T(8,128)(2,1)S(1)}, bf16[10,128,128]{2,1,0:T(8,128)(2,1)S(1)}, u32[]{:S(2)}, u32[]{:S(2)}) collective-permute-start(bf16[10,128,128]{2,1,0:T(8,128)(2,1)S(1)} %collective-permute-done.22), channel_id=1, source_target_pairs={{8,0},{10,2},{16,8},{18,10},{24,16},{26,18},{28,24},{30,26},{20,28... | collective-permute-start | bytes 983048 | tf_op jit(solution)/shard_map/ppermute | solution.py:37
  59.0 9.1 %collective-permute-start.19 = (bf16[10,128,128]{2,1,0:T(8,128)(2,1)S(1)}, bf16[10,128,128]{2,1,0:T(8,128)(2,1)S(1)}, u32[]{:S(2)}, u32[]{:S(2)}) collective-permute-start(bf16[10,128,128]{2,1,0:T(8,128)(2,1)S(1)} %collective-permute-done.18), channel_id=1, source_target_pairs={{0,2},{2,0},{4,6},{6,4},{8,10},{10,8},{12,14},{14,12},{16,18},{18,... | collective-permute-start | bytes 983048 | tf_op jit(solution)/shard_map/ppermute | solution.py:40
  59.0 10.7 %collective-permute-start.23 = (bf16[10,128,128]{2,1,0:T(8,128)(2,1)S(1)}, bf16[10,128,128]{2,1,0:T(8,128)(2,1)S(1)}, u32[]{:S(2)}, u32[]{:S(2)}) collective-permute-start(bf16[10,128,128]{2,1,0:T(8,128)(2,1)S(1)} %collective-permute-done.22), channel_id=1, source_target_pairs={{0,2},{2,0},{4,6},{6,4},{8,10},{10,8},{12,14},{14,12},{16,18},{18,... | collective-permute-start | bytes 983048 | tf_op jit(solution)/shard_map/ppermute | solution.py:41
  66.1 3.6 %collective-permute-start.21 = (bf16[10,128,128]{2,1,0:T(8,128)(2,1)S(1)}, bf16[10,128,128]{2,1,0:T(8,128)(2,1)S(1)}, u32[]{:S(2)}, u32[]{:S(2)}) collective-permute-start(bf16[10,128,128]{2,1,0:T(8,128)(2,1)S(1)} %collective-permute-done.20), channel_id=1, source_target_pairs={{0,2},{2,0},{4,6},{6,4},{8,10},{10,8},{12,14},{14,12},{16,18},{18,... | collective-permute-start | bytes 983048 | tf_op jit(solution)/shard_map/ppermute | solution.py:40
  67.5 2.2 %collective-permute-start.25 = (bf16[10,128,128]{2,1,0:T(8,128)(2,1)S(1)}, bf16[10,128,128]{2,1,0:T(8,128)(2,1)S(1)}, u32[]{:S(2)}, u32[]{:S(2)}) collective-permute-start(bf16[10,128,128]{2,1,0:T(8,128)(2,1)S(1)} %collective-permute-done.24), channel_id=1, source_target_pairs={{0,2},{2,0},{4,6},{6,4},{8,10},{10,8},{12,14},{14,12},{16,18},{18,... | collective-permute-start | bytes 983048 | tf_op jit(solution)/shard_map/ppermute | solution.py:41
  67.6 3.3 %copy-start.12 = (bf16[10,128,128]{2,1,0:T(8,128)(2,1)S(1)}, bf16[10,128,128]{2,1,0:T(8,128)(2,1)}, u32[]{:S(2)}) copy-start(bf16[10,128,128]{2,1,0:T(8,128)(2,1)} %copy-done.11) | copy-start | bytes 983044
  67.7 15.9 %collective-permute-start.28 = (bf16[10,128,128]{2,1,0:T(8,128)(2,1)S(1)}, bf16[10,128,128]{2,1,0:T(8,128)(2,1)S(1)}, u32[]{:S(2)}, u32[]{:S(2)}) collective-permute-start(bf16[10,128,128]{2,1,0:T(8,128)(2,1)S(1)} %collective-permute-done.24), channel_id=1, source_target_pairs={{8,0},{10,2},{16,8},{18,10},{24,16},{26,18},{28,24},{30,26},{20,28... | collective-permute-start | bytes 983048 | tf_op jit(solution)/shard_map/ppermute | solution.py:37
  68.1 16.4 %collective-permute-start.26 = (bf16[10,128,128]{2,1,0:T(8,128)(2,1)S(1)}, bf16[10,128,128]{2,1,0:T(8,128)(2,1)S(1)}, u32[]{:S(2)}, u32[]{:S(2)}) collective-permute-start(bf16[10,128,128]{2,1,0:T(8,128)(2,1)S(1)} %collective-permute-done.20), channel_id=1, source_target_pairs={{0,8},{2,10},{8,16},{10,18},{16,24},{18,26},{24,28},{26,30},{28,20... | collective-permute-start | bytes 983048 | tf_op jit(solution)/shard_map/ppermute | solution.py:36
  69.8 2.2 %copy-start.14 = (bf16[10,128,128]{2,1,0:T(8,128)(2,1)S(1)}, bf16[10,128,128]{2,1,0:T(8,128)(2,1)}, u32[]{:S(2)}) copy-start(bf16[10,128,128]{2,1,0:T(8,128)(2,1)} %copy-done.13) | copy-start | bytes 983044
  77.0 1.0 copy-start.4
  77.2 1.0 copy-start.6
  77.2 1.1 copy-start.2
  77.2 1.1 %copy-start.10 = (bf16[10,128,128]{2,1,0:T(8,128)(2,1)S(1)}, bf16[10,128,128]{2,1,0:T(8,128)(2,1)}, u32[]{:S(2)}) copy-start(bf16[10,128,128]{2,1,0:T(8,128)(2,1)} %copy-done.9) | copy-start | bytes 983044
  83.6 2.2 %collective-permute-start.29 = (bf16[10,128,128]{2,1,0:T(8,128)(2,1)S(1)}, bf16[10,128,128]{2,1,0:T(8,128)(2,1)S(1)}, u32[]{:S(2)}, u32[]{:S(2)}) collective-permute-start(bf16[10,128,128]{2,1,0:T(8,128)(2,1)S(1)} %collective-permute-done.28), channel_id=1, source_target_pairs={{0,2},{2,0},{4,6},{6,4},{8,10},{10,8},{12,14},{14,12},{16,18},{18,... | collective-permute-start | bytes 983048 | tf_op jit(solution)/shard_map/ppermute | solution.py:41
  83.7 6.8 %slice-start = ((s8[13107200]{0:T(1024)(128)(4,1)}), s8[4194304]{0:T(1024)(128)(4,1)S(1)}, s32[]{:S(2)}) async-start(s8[13107200]{0:T(1024)(128)(4,1)} %bitcast.603), calls=%async_computation | async-start | bytes 8388608
  84.6 2.0 %collective-permute-start.27 = (bf16[10,128,128]{2,1,0:T(8,128)(2,1)S(1)}, bf16[10,128,128]{2,1,0:T(8,128)(2,1)S(1)}, u32[]{:S(2)}, u32[]{:S(2)}) collective-permute-start(bf16[10,128,128]{2,1,0:T(8,128)(2,1)S(1)} %collective-permute-done.26), channel_id=1, source_target_pairs={{0,2},{2,0},{4,6},{6,4},{8,10},{10,8},{12,14},{14,12},{16,18},{18,... | collective-permute-start | bytes 983048 | tf_op jit(solution)/shard_map/ppermute | solution.py:40
  85.8 4.7 %slice-start.1 = ((s8[13107200]{0:T(1024)(128)(4,1)}), s8[4194304]{0:T(1024)(128)(4,1)S(1)}, s32[]{:S(2)}) async-start(s8[13107200]{0:T(1024)(128)(4,1)} %bitcast.603), calls=%async_computation.1 | async-start | bytes 8388608
  87.6 2.9 %slice-start.2 = ((s8[13107200]{0:T(1024)(128)(4,1)}), s8[4194304]{0:T(1024)(128)(4,1)S(1)}, s32[]{:S(2)}) async-start(s8[13107200]{0:T(1024)(128)(4,1)} %bitcast.603), calls=%async_computation.2 | async-start | bytes 8388608
  89.2 1.3 %slice-start.3 = ((s8[13107200]{0:T(1024)(128)(4,1)}), s8[524288]{0:T(1024)(128)(4,1)S(1)}, s32[]{:S(2)}) async-start(s8[13107200]{0:T(1024)(128)(4,1)} %bitcast.603), calls=%async_computation.3 | async-start | bytes 1048576
  93.0 10.6 %collective-permute-start.30 = (bf16[60,2560]{1,0:T(8,128)(2,1)S(1)}, bf16[60,2560]{1,0:T(8,128)(2,1)S(1)}, u32[]{:S(2)}, u32[]{:S(2)}) collective-permute-start(bf16[60,2560]{1,0:T(8,128)(2,1)S(1)} %fusion.4), channel_id=1, source_target_pairs={{0,1},{1,0},{2,3},{3,2},{4,5},{5,4},{6,7},{7,6},{8,9},{9,8},{10,11... | collective-permute-start | bytes 921608 | tf_op jit(solution)/shard_map/ppermute | solution.py:169
  94.6 15.3 %collective-permute-start.31 = (bf16[60,2560]{1,0:T(8,128)(2,1)S(1)}, bf16[60,2560]{1,0:T(8,128)(2,1)S(1)}, u32[]{:S(2)}, u32[]{:S(2)}) collective-permute-start(bf16[60,2560]{1,0:T(8,128)(2,1)S(1)} %fusion.7), channel_id=1, source_target_pairs={{0,1},{1,0},{2,3},{3,2},{4,5},{5,4},{6,7},{7,6},{8,9},{9,8},{10,11... | collective-permute-start | bytes 921608 | tf_op jit(solution)/shard_map/ppermute | solution.py:169
  97.8 12.1 %copy-start = (bf16[60,5120]{1,0:T(8,128)(2,1)S(1)}, bf16[60,5120]{1,0:T(8,128)(2,1)}, u32[]{:S(2)}) copy-start(bf16[60,5120]{1,0:T(8,128)(2,1)} %param.10) | copy-start | bytes 1843204
  97.8 12.1 %copy-start.16 = (f32[5120]{0:T(1024)S(1)}, f32[5120]{0:T(1024)}, u32[]{:S(2)}) copy-start(f32[5120]{0:T(1024)} %param.14) | copy-start | bytes 61444
